TPU v7x, 32 devices: a whole 2x2x4 slice. The times are simulated.
32 devices in a mesh: grp: 2 (over y), ctx: 8 (over z, x), pair: 2 (over core).
Axes of the slice: x: 2, y: 2, z: 4, core: 2. Of those that a mesh axis runs over, the one named last changes fastest.
Arguments:
- normed_input: bfloat16 [4, 1024, 2688], P(('grp', 'pair'), 'ctx'), parts along dimension 0, may hold values from -6 to 6
- queries: bfloat16 [4, 1024, 2048], P(('grp', 'pair'), 'ctx'), parts along dimension 0, may hold values from -64 to 64
- keys: bfloat16 [4, 1024, 1024], P(('grp', 'pair'), 'ctx'), parts along dimension 0, may hold values from -64 to 64
- value_projection: bfloat16 [2688, 1024], P('ctx'), may hold values from -0.125 to 0.125
- adapter_down: bfloat16 [2688, 16], replicated, may hold values from -0.125 to 0.125
- adapter_up: bfloat16 [16, 1024], replicated, may hold values from -1.5 to 1.5
- output_gradient: bfloat16 [4, 1024, 2048], P(('grp', 'pair'), 'ctx'), parts along dimension 0, may hold values from -6 to 6
- policy_logprob: float32 [4, 1024], P(('grp', 'pair'), 'ctx'), parts along dimension 0, may hold values from -6 to 0
- reference_logprob: float32 [4, 1024], P(('grp', 'pair'), 'ctx'), parts along dimension 0, may hold values from -8 to 0
- token_pair_index: int32 [4, 1024], P(('grp', 'pair'), 'ctx'), parts along dimension 0, may hold values from 0 to 7, never falling along the last dimension, each value on 1 to 1017 neighbouring positions
Outputs:
- input_grad: bfloat16 [4, 1024, 2688], P(('grp', 'pair'), 'ctx'), parts along dimension 0
- query_grad: bfloat16 [4, 1024, 2048], P(('grp', 'pair'), 'ctx'), parts along dimension 0
- key_grad: bfloat16 [4, 1024, 1024], P(('grp', 'pair'), 'ctx'), parts along dimension 0
- down_gradient: float32 [5376, 16], P('grp'), parts along dimension 0
- up_gradient: float32 [32, 1024], P('grp'), parts along dimension 0
There are 2 independent parts, one for each index of `grp`. A program takes and returns all parts, laid end to end along the dimension named above; an argument that names none is the same for every part. Nothing has to cross between parts.
Inputs may be any that keep to these rules, and one draw needn't show every extreme that they name: `token_pair_index`: along each sequence the ids never fall; both sequences hold every id, each segment at most 1017 tokens and one exactly 1017.
All inputs are finite; a program needn't handle non-finite values.
Results may differ from a plain program's by a relative error of at most 0.03.
Values may be sent and summed in bfloat16 or wider, within the bound.
No kernel may reach another device: no remote copies, remote signals or barrier semaphores. Data moves between devices by JAX's collectives and lax.ppermute only.
A program may use at most 128 MiB of HBM per device.

v0:
```python
import jax
import jax.numpy as jnp
from jax import lax
from jax.sharding import PartitionSpec as P

HEAD_SIZE = 128
WINDOW = 1024
SEGS = 8


DPO_BETA = 0.1
LOSS_SCALE = 256.0
ADAPTER_SCALE = 2.0
ATTN_SCALE = 168.0 ** (-0.5)
NEG_FILL = -1e30


def from_partner(shard, axis, stride):
    return lax.ppermute(shard, axis, [(i, i ^ 1 << stride) for i in range(lax.axis_size(axis))])


def shifted(block, axis, distance):
    devices = range(lax.axis_size(axis))
    route = [(i - distance, i) for i in devices if i - distance in devices]
    return lax.ppermute(block, axis, route)


def shards(
    normed_input,
    queries,
    keys,
    value_projection,
    adapter_down,
    adapter_up,
    output_gradient,
    policy_logprob,
    reference_logprob,
    token_pair_index,
):
    tok_rows = normed_input.shape[1]
    width_kv = keys.shape[2]
    kv_heads = width_kv // HEAD_SIZE
    group_size = queries.shape[2] // width_kv
    hidden_rows = normed_input[0]
    own_keys = keys[0]
    pair_index = lax.axis_index("pair")
    ctx_index = lax.axis_index("ctx")
    half_cols = width_kv // 2
    own_half = lax.dynamic_slice_in_dim(value_projection, pair_index * half_cols, half_cols, 1)
    rows_half = lax.all_gather(own_half, "ctx", axis=0, tiled=True)
    full_weight = lax.all_gather(rows_half, "pair", axis=1, tiled=True)
    rank_projection = jnp.dot(hidden_rows, adapter_down, preferred_element_type=jnp.float32).astype(
        jnp.bfloat16
    )
    values = (
        jnp.dot(hidden_rows, full_weight, preferred_element_type=jnp.float32)
        + ADAPTER_SCALE * jnp.dot(rank_projection, adapter_up, preferred_element_type=jnp.float32)
    ).astype(jnp.bfloat16)
    segment_labels = token_pair_index[0]
    seg_table = (segment_labels[:, None] == jnp.arange(SEGS, dtype=jnp.int32)[None, :]).astype(
        jnp.float32
    )
    log_gap = policy_logprob[0] - reference_logprob[0]
    part_diff = jnp.sum(seg_table * log_gap[:, None], 0)
    part_count = jnp.sum(seg_table, 0)
    own_diff, counts = lax.psum((part_diff, part_count), "ctx")
    other_diff = from_partner(own_diff, "pair", 0)
    direction = 1.0 - 2.0 * pair_index.astype(jnp.float32)
    margin = DPO_BETA * (direction * (own_diff - other_diff))
    coef = -direction * DPO_BETA * LOSS_SCALE * jax.nn.sigmoid(-margin)
    starts = jnp.cumsum(counts) - counts
    tok_start = jnp.sum(seg_table * starts[None, :], 1).astype(jnp.int32)
    token_coefficient = jnp.sum(seg_table * coef[None, :], 1)
    halo_blocks = WINDOW // tok_rows
    key_blocks = []
    value_blocks = []
    for distance in range(halo_blocks, 0, -1):
        got_keys, got_values = shifted((own_keys, values), "ctx", distance)
        key_blocks.append(got_keys)
        value_blocks.append(got_values)
    all_keys = jnp.concatenate(key_blocks + [own_keys], 0)
    all_values = jnp.concatenate(value_blocks + [values], 0)
    span = all_keys.shape[0]
    tpos = ctx_index * tok_rows + jnp.arange(tok_rows, dtype=jnp.int32)
    upos = ctx_index * tok_rows - WINDOW + jnp.arange(span, dtype=jnp.int32)
    allowed = (
        (upos[None, :] <= tpos[:, None])
        & (upos[None, :] > tpos[:, None] - WINDOW)
        & (upos[None, :] >= tok_start[:, None])
    )
    coef_rows = token_coefficient[None, :, None]
    query_heads = (
        queries[0].reshape(tok_rows, kv_heads, group_size, HEAD_SIZE).transpose(1, 0, 2, 3)
    )
    grad_heads = (
        output_gradient[0].reshape(tok_rows, kv_heads, group_size, HEAD_SIZE).transpose(1, 0, 2, 3)
    )
    key_heads = all_keys.reshape(span, kv_heads, HEAD_SIZE).transpose(1, 0, 2)
    value_heads = all_values.reshape(span, kv_heads, HEAD_SIZE).transpose(1, 0, 2)

    def per_head(operands):
        query_head, key_head, value_head, grad_head = operands
        scores = ATTN_SCALE * jnp.einsum(
            "tgd,ld->gtl", query_head, key_head, preferred_element_type=jnp.float32
        )
        masked = jnp.where(allowed[None], scores, NEG_FILL)
        row_max = jnp.max(masked, -1, keepdims=True)
        weights_exp = jnp.where(allowed[None], jnp.exp(masked - row_max), 0.0)
        attn_probs = weights_exp / jnp.sum(weights_exp, -1, keepdims=True)
        prob_grad = coef_rows * jnp.einsum(
            "tgd,ld->gtl", grad_head, value_head, preferred_element_type=jnp.float32
        )
        row_delta = jnp.sum(attn_probs * prob_grad, -1, keepdims=True)
        score_grad = (ATTN_SCALE * attn_probs * (prob_grad - row_delta)).astype(jnp.bfloat16)
        head_qgrad = jnp.einsum(
            "gtl,ld->tgd", score_grad, key_head, preferred_element_type=jnp.float32
        ).astype(jnp.bfloat16)
        head_kgrad = jnp.einsum(
            "gtl,tgd->ld", score_grad, query_head, preferred_element_type=jnp.float32
        )
        weighted = (attn_probs * coef_rows).astype(jnp.bfloat16)
        head_vgrad = jnp.einsum(
            "gtl,tgd->ld", weighted, grad_head, preferred_element_type=jnp.float32
        )
        return (head_qgrad, head_kgrad, head_vgrad)

    query_stack, key_stack, value_stack = lax.map(
        per_head, (query_heads, key_heads, value_heads, grad_heads)
    )
    query_grad = query_stack.transpose(1, 0, 2, 3).reshape(
        tok_rows, kv_heads * group_size * HEAD_SIZE
    )
    key_parts = key_stack.transpose(1, 0, 2).reshape(span, width_kv)
    value_parts = value_stack.transpose(1, 0, 2).reshape(span, width_kv)
    key_total = key_parts[WINDOW:]
    value_total = value_parts[WINDOW:]
    for distance in range(1, halo_blocks + 1):
        block_start = (halo_blocks - distance) * tok_rows
        send_keys = key_parts[block_start : block_start + tok_rows].astype(jnp.bfloat16)
        send_values = value_parts[block_start : block_start + tok_rows].astype(jnp.bfloat16)
        back_keys, back_values = shifted((send_keys, send_values), "ctx", -distance)
        key_total = key_total + back_keys.astype(jnp.float32)
        value_total = value_total + back_values.astype(jnp.float32)
    key_grad = key_total.astype(jnp.bfloat16)
    value_gradient = value_total.astype(jnp.bfloat16)
    rank_middle = jnp.einsum(
        "sj,zj->sz", value_gradient, adapter_up, preferred_element_type=jnp.float32
    ).astype(jnp.bfloat16)
    input_grad = (
        jnp.einsum("tk,dk->td", value_gradient, full_weight, preferred_element_type=jnp.float32)
        + ADAPTER_SCALE
        * jnp.einsum("pb,wb->pw", rank_middle, adapter_down, preferred_element_type=jnp.float32)
    ).astype(jnp.bfloat16)
    up_factor = ADAPTER_SCALE * jnp.einsum(
        "tr,tk->rk", rank_projection, value_gradient, preferred_element_type=jnp.float32
    )
    down_factor = ADAPTER_SCALE * jnp.einsum(
        "td,tr->dr", hidden_rows, rank_middle, preferred_element_type=jnp.float32
    )
    down_gradient, up_gradient = lax.psum((down_factor, up_factor), ("ctx", "pair"))
    return (input_grad[None], query_grad[None], key_grad[None], down_gradient, up_gradient)


def solution(mesh):
    return jax.shard_map(
        shards,
        mesh=mesh,
        in_specs=(
            P(("grp", "pair"), "ctx", None),
            P(("grp", "pair"), "ctx", None),
            P(("grp", "pair"), "ctx", None),
            P("ctx", None),
            P(),
            P(),
            P(("grp", "pair"), "ctx", None),
            P(("grp", "pair"), "ctx"),
            P(("grp", "pair"), "ctx"),
            P(("grp", "pair"), "ctx"),
        ),
        out_specs=(
            P(("grp", "pair"), "ctx", None),
            P(("grp", "pair"), "ctx", None),
            P(("grp", "pair"), "ctx", None),
            P("grp", None),
            P("grp", None),
        ),
        check_vma=False,
    )
```

profile of v0, /device:TPU:0, one launch (start us, length us, event | category | flops | bytes accessed | tf_op | source)
XLA Modules:
  0.0 454.8 jit_solution(16031757888208835869)
XLA Ops:
  7.3 1.8 constant_dynamic-slice_fusion
  9.2 60.4 %all-gather.3.cloned.1.call-done = bf16[2688,512]{1,0:T(8,128)(2,1)} async-done(((bf16[336,512]{1,0:T(8,128)(2,1)}), bf16[2688,512]{1,0:T(8,128)(2,1)}) %all-gather.3.cloned.1.call-update) | async-done | bytes 2752528 | tf_op jit(solution)/shard_map/all_gather | solution.py:50
  69.9 2.5 collective-permute-start.7
  72.3 3.4 collective-permute-start.6
  75.7 1.7 collective-permute-start.2
  77.5 2.0 collective-permute-start.1
  79.6 26.4 %all-reduce.1 = (f32[8]{0:T(128)S(1)}, f32[8]{0:T(128)S(1)}) all-reduce(f32[8]{0:T(128)S(1)} %get-tuple-element.122, f32[8]{0:T(128)S(1)} %get-tuple-element.123), channel_id=1, replica_groups=mesh['grp'=2,'ctx'=8,'pair'=2] {'ctx'}, use_global_device_ids=true, to_apply=%region_1.0 | all-reduce | flops 16 | bytes 128 | tf_op jit(solution)/shard_map/psum | solution.py:66
  113.1 2.8 collective-permute-start.5
  117.4 4.3 collective-permute-done.4
  122.4 4.6 %collective-permute-done.5 = bf16[128,1024]{0,1:T(8,128)(2,1)S(1)} collective-permute-done((bf16[128,1024]{0,1:T(8,128)(2,1)S(1)}, bf16[128,1024]{0,1:T(8,128)(2,1)S(1)}, u32[]{:S(2)}, u32[]{:S(2)}) %collective-permute-start.5) | collective-permute-done | bytes 262176 | tf_op jit(solution)/shard_map/ppermute | solution.py:25
  127.8 3.5 convolution_bitcast_fusion.2
  133.0 12.6 %collective-permute-start.10 = (bf16[128,1024]{1,0:T(8,128)(2,1)S(1)}, bf16[128,1024]{1,0:T(8,128)(2,1)S(1)}, u32[]{:S(2)}, u32[]{:S(2)}) collective-permute-start(bf16[128,1024]{1,0:T(8,128)(2,1)S(1)} %fusion.60), channel_id=1, source_target_pairs={{0,14},{1,15},{16,30},{17,31}} | collective-permute-start | bytes 786440 | tf_op jit(solution)/shard_map/ppermute | solution.py:25
  146.4 5.5 %collective-permute-start.11 = (bf16[128,1024]{1,0:T(8,128)(2,1)S(1)}, bf16[128,1024]{1,0:T(8,128)(2,1)S(1)}, u32[]{:S(2)}, u32[]{:S(2)}) collective-permute-start(bf16[128,1024]{1,0:T(8,128)(2,1)S(1)} %fusion.60), channel_id=1, source_target_pairs={{0,12},{2,14},{1,13},{3,15},{16,28},{18,30},{17,29},{19,31}} | collective-permute-start | bytes 786440 | tf_op jit(solution)/shard_map/ppermute | solution.py:25
  155.2 4.0 collective-permute-start.12
  161.9 7.9 %collective-permute-done.12 = bf16[128,1024]{1,0:T(8,128)(2,1)S(1)} collective-permute-done((bf16[128,1024]{1,0:T(8,128)(2,1)S(1)}, bf16[128,1024]{1,0:T(8,128)(2,1)S(1)}, u32[]{:S(2)}, u32[]{:S(2)}) %collective-permute-start.12) | collective-permute-done | bytes 262176 | tf_op jit(solution)/shard_map/ppermute | solution.py:25
  169.8 5.6 %collective-permute-done.13 = bf16[128,1024]{1,0:T(8,128)(2,1)S(1)} collective-permute-done((bf16[128,1024]{1,0:T(8,128)(2,1)S(1)}, bf16[128,1024]{1,0:T(8,128)(2,1)S(1)}, u32[]{:S(2)}, u32[]{:S(2)}) %collective-permute-start.13) | collective-permute-done | bytes 262176 | tf_op jit(solution)/shard_map/ppermute | solution.py:25
  175.5 4.7 %collective-permute-done.14 = bf16[128,1024]{1,0:T(8,128)(2,1)S(1)} collective-permute-done((bf16[128,1024]{1,0:T(8,128)(2,1)S(1)}, bf16[128,1024]{1,0:T(8,128)(2,1)S(1)}, u32[]{:S(2)}, u32[]{:S(2)}) %collective-permute-start.14) | collective-permute-done | bytes 262176 | tf_op jit(solution)/shard_map/ppermute | solution.py:25
  180.3 1.8 bitcast_bitcast_fusion
  182.1 75.4 %while.15 = (s32[]{:T(128)}, bf16[8,128,2,128]{1,3,2,0:T(8,128)(2,1)}, f32[8,1152,128]{2,1,0:T(8,128)}, f32[8,1152,128]{1,2,0:T(8,128)}, bf16[8,1152,128]{1,2,0:...) while((s32[]{:T(128)}, ...), condition=%wide.region_11.12_spmd.clone, body=%wide.region_7.11_spmd.clone.sunk | while | flops 459950336 | bytes 11177101 | solution.py:127
  185.7 1.9 fusion.126
  188.7 2.9 fusion.128
  195.1 1.9 fusion.126
  198.1 2.8 fusion.128
  204.5 1.9 fusion.126
  207.5 2.9 fusion.128
  213.9 1.9 fusion.126
  216.9 2.9 fusion.128
  223.3 1.9 fusion.126
  226.4 2.9 fusion.128
  232.8 1.9 fusion.126
  235.9 2.8 fusion.128
  242.3 1.9 fusion.126
  245.3 2.8 fusion.128
  251.7 1.9 fusion.126
  254.7 2.8 fusion.128
  257.5 2.7 bitcast_convert_fusion.1
  265.6 2.7 bitcast_convert_fusion
  268.3 2.0 copy.72
  276.7 15.1 %collective-permute-done.23 = bf16[128,1024]{0,1:T(8,128)(2,1)} collective-permute-done((bf16[128,1024]{0,1:T(8,128)(2,1)}, bf16[128,1024]{0,1:T(8,128)(2,1)}, u32[]{:S(2)}, u32[]{:S(2)}) %collective-permute-start.23) | collective-permute-done | bytes 262176 | tf_op jit(solution)/shard_map/ppermute | solution.py:25
  293.9 3.9 collective-permute-done.22
  299.1 15.2 %collective-permute-done.21 = bf16[128,1024]{0,1:T(8,128)(2,1)S(1)} collective-permute-done((bf16[128,1024]{0,1:T(8,128)(2,1)}, bf16[128,1024]{0,1:T(8,128)(2,1)S(1)}, u32[]{:S(2)}, u32[]{:S(2)}) %collective-permute-start.21) | collective-permute-done | bytes 262176 | tf_op jit(solution)/shard_map/ppermute | solution.py:25
  315.6 4.0 collective-permute-done.20
  328.4 2.6 collective-permute-done.27
  331.7 38.9 %collective-permute-done.28 = bf16[128,1024]{1,0:T(8,128)(2,1)} collective-permute-done((bf16[128,1024]{1,0:T(8,128)(2,1)S(1)}, bf16[128,1024]{1,0:T(8,128)(2,1)}, u32[]{:S(2)}, u32[]{:S(2)}) %collective-permute-start.28) | collective-permute-done | bytes 262176 | tf_op jit(solution)/shard_map/ppermute | solution.py:25
  371.9 5.4 %fusion.57 = bf16[1,128,2688]{2,1,0:T(8,128)(2,1)} fusion(f32[128,2688]{1,0:T(8,128)S(1)} %convolution_multiply_fusion.2, bf16[128,1024]{0,1:T(8,128)(2,1)S(1)} %fusion.79, bf16[2688,1024]{1,0:T(8,128)(2,1)} %all-gather.5.cloned.1.call-done), kind=kOutput, calls=%fused_computation.51 | convolution fusion | flops 705331200 | bytes 7831552 | tf_op jit(solution)/shard_map/tk,dk->td/dot_general | solution.py:150
  377.5 5.3 %collective-permute-done.25 = bf16[128,1024]{1,0:T(8,128)(2,1)S(1)} collective-permute-done((bf16[128,1024]{1,0:T(8,128)(2,1)S(1)}, bf16[128,1024]{1,0:T(8,128)(2,1)S(1)}, u32[]{:S(2)}, u32[]{:S(2)}) %collective-permute-start.25) | collective-permute-done | bytes 262176 | tf_op jit(solution)/shard_map/ppermute | solution.py:25
  382.7 2.5 fusion.80
  385.2 60.0 %all-reduce.4.cloned.1.call-done = (f32[2688,16]{0,1:T(8,128)}, f32[16,1024]{1,0:T(8,128)}) async-done(((f32[2688,16]{0,1:T(8,128)}, f32[16,1024]{1,0:T(8,128)}), (f32[2688,16]{0,1:T(8,128)}, f32[16,1024]{1,0:T(8,128)})) %all-reduce.4.cloned.1.call-update) | async-done | bytes 237584 | tf_op jit(solution)/shard_map/psum | solution.py:160
  (164 shorter events, 86.8 us)
Async XLA Ops:
  7.2 99.7 %copy-start = (bf16[1,128,2688]{2,1,0:T(8,128)(2,1)S(1)}, bf16[1,128,2688]{2,1,0:T(8,128)(2,1)}, u32[]{:S(2)}) copy-start(bf16[1,128,2688]{2,1,0:T(8,128)(2,1)} %param.12) | copy-start | bytes 2064388
  7.2 62.5 %copy-start.4 = (bf16[1,128,1024]{2,1,0:T(8,128)(2,1)S(1)}, bf16[1,128,1024]{2,1,0:T(8,128)(2,1)}, u32[]{:S(2)}) copy-start(bf16[1,128,1024]{2,1,0:T(8,128)(2,1)} %param.14) | copy-start | bytes 786436
  7.2 72.3 %copy-start.8 = (f32[1,128]{1,0:T(1,128)S(1)}, f32[1,128]{1,0:T(1,128)}, u32[]{:S(2)}) copy-start(f32[1,128]{1,0:T(1,128)} %param.20) | copy-start | bytes 1540
  7.2 72.3 %copy-start.7 = (f32[1,128]{1,0:T(1,128)S(1)}, f32[1,128]{1,0:T(1,128)}, u32[]{:S(2)}) copy-start(f32[1,128]{1,0:T(1,128)} %param.19) | copy-start | bytes 1540
  7.2 72.3 %copy-start.6 = (s32[1,128]{1,0:T(1,128)S(1)}, s32[1,128]{1,0:T(1,128)}, u32[]{:S(2)}) copy-start(s32[1,128]{1,0:T(1,128)} %param.21) | copy-start | bytes 1540
  7.2 98.9 %copy-start.1 = (bf16[1,128,2048]{2,1,0:T(8,128)(2,1)S(1)}, bf16[1,128,2048]{2,1,0:T(8,128)(2,1)}, u32[]{:S(2)}) copy-start(bf16[1,128,2048]{2,1,0:T(8,128)(2,1)} %param.13) | copy-start | bytes 1572868
  7.2 62.4 %all-gather.3.cloned.1.call-start = ((), (), s32[]{:S(2)}) async-start(), calls=%async_computation | async-start | bytes 3096576 | tf_op jit(solution)/shard_map/all_gather | solution.py:50
  9.1 97.3 %copy-start.2 = (bf16[1,128,2048]{2,1,0:T(8,128)(2,1)S(1)}, bf16[1,128,2048]{2,1,0:T(8,128)(2,1)}, u32[]{:S(2)}) copy-start(bf16[1,128,2048]{2,1,0:T(8,128)(2,1)} %param.18) | copy-start | bytes 1572868
  9.2 118.7 %all-gather.5.cloned.1.call-start = ((), (), s32[]{:S(2)}) async-start(), calls=%async_computation.1 | async-start | bytes 8257536 | tf_op jit(solution)/shard_map/all_gather | solution.py:51
  69.6 37.3 %copy-start.3 = (bf16[2688,16]{0,1:T(8,128)(2,1)S(1)}, bf16[2688,16]{0,1:T(8,128)(2,1)}, u32[]{:S(2)}) copy-start(bf16[2688,16]{0,1:T(8,128)(2,1)} %param.16) | copy-start | bytes 258052
  69.6 375.6 %all-reduce.4.cloned.1.call-start = ((), (), s32[]{:S(2)}) async-start(), calls=%async_computation.2 | async-start | bytes 475136 | tf_op jit(solution)/shard_map/psum | solution.py:160
  69.9 75.7 %collective-permute-start.7 = (bf16[128,1024]{0,1:T(8,128)(2,1)S(1)}, bf16[128,1024]{0,1:T(8,128)(2,1)S(1)}, u32[]{:S(2)}, u32[]{:S(2)}) collective-permute-start(bf16[128,1024]{0,1:T(8,128)(2,1)S(1)} %bitcast.280), channel_id=1, source_target_pairs={{0,2},{2,4},{4,6},{6,8},{8,10},{10,12},{12,14},{1,3},{3,5},{5,7},{... | collective-permute-start | bytes 786440 | tf_op jit(solution)/shard_map/ppermute | solution.py:25
  72.3 59.9 %collective-permute-start.6 = (bf16[128,1024]{0,1:T(8,128)(2,1)S(1)}, bf16[128,1024]{0,1:T(8,128)(2,1)S(1)}, u32[]{:S(2)}, u32[]{:S(2)}) collective-permute-start(bf16[128,1024]{0,1:T(8,128)(2,1)S(1)} %bitcast.281), channel_id=1, source_target_pairs={{0,4},{2,6},{4,8},{6,10},{8,12},{10,14},{1,5},{3,7},{5,9},{7,11},{... | collective-permute-start | bytes 786440 | tf_op jit(solution)/shard_map/ppermute | solution.py:25
  75.7 37.4 %collective-permute-start.2 = (bf16[128,1024]{0,1:T(8,128)(2,1)S(1)}, bf16[128,1024]{0,1:T(8,128)(2,1)S(1)}, u32[]{:S(2)}, u32[]{:S(2)}) collective-permute-start(bf16[128,1024]{0,1:T(8,128)(2,1)S(1)} %bitcast.282), channel_id=1, source_target_pairs={{0,12},{2,14},{1,13},{3,15},{16,28},{18,30},{17,29},{19,31}} | collective-permute-start | bytes 786440 | tf_op jit(solution)/shard_map/ppermute | solution.py:25
  77.5 32.6 %collective-permute-start.1 = (bf16[128,1024]{0,1:T(8,128)(2,1)S(1)}, bf16[128,1024]{0,1:T(8,128)(2,1)}, u32[]{:S(2)}, u32[]{:S(2)}) collective-permute-start(bf16[128,1024]{0,1:T(8,128)(2,1)S(1)} %bitcast.283), channel_id=1, source_target_pairs={{0,14},{1,15},{16,30},{17,31}} | collective-permute-start | bytes 786440 | tf_op jit(solution)/shard_map/ppermute | solution.py:25
  106.0 1.2 collective-permute-start.8
  107.2 0.8 collective-permute-start
  108.0 8.6 %collective-permute-start.3 = (bf16[128,1024]{0,1:T(8,128)(2,1)S(1)}, bf16[128,1024]{0,1:T(8,128)(2,1)S(1)}, u32[]{:S(2)}, u32[]{:S(2)}) collective-permute-start(bf16[128,1024]{0,1:T(8,128)(2,1)S(1)} %bitcast.285), channel_id=1, source_target_pairs={{0,10},{2,12},{4,14},{1,11},{3,13},{5,15},{16,26},{18,28},{20,30},... | collective-permute-start | bytes 786440 | tf_op jit(solution)/shard_map/ppermute | solution.py:25
  110.1 11.6 %collective-permute-start.4 = (bf16[128,1024]{0,1:T(8,128)(2,1)S(1)}, bf16[128,1024]{0,1:T(8,128)(2,1)S(1)}, u32[]{:S(2)}, u32[]{:S(2)}) collective-permute-start(bf16[128,1024]{0,1:T(8,128)(2,1)S(1)} %bitcast.286), channel_id=1, source_target_pairs={{0,8},{2,10},{4,12},{6,14},{1,9},{3,11},{5,13},{7,15},{16,24},{18,... | collective-permute-start | bytes 786440 | tf_op jit(solution)/shard_map/ppermute | solution.py:25
  113.1 13.9 %collective-permute-start.5 = (bf16[128,1024]{0,1:T(8,128)(2,1)S(1)}, bf16[128,1024]{0,1:T(8,128)(2,1)S(1)}, u32[]{:S(2)}, u32[]{:S(2)}) collective-permute-start(bf16[128,1024]{0,1:T(8,128)(2,1)S(1)} %bitcast.287), channel_id=1, source_target_pairs={{0,6},{2,8},{4,10},{6,12},{8,14},{1,7},{3,9},{5,11},{7,13},{9,15},... | collective-permute-start | bytes 786440 | tf_op jit(solution)/shard_map/ppermute | solution.py:25
  127.8 3.5 copy-start.5
  131.6 23.7 %collective-permute-start.9 = (bf16[128,1024]{1,0:T(8,128)(2,1)S(1)}, bf16[128,1024]{1,0:T(8,128)(2,1)S(1)}, u32[]{:S(2)}, u32[]{:S(2)}) collective-permute-start(bf16[128,1024]{1,0:T(8,128)(2,1)S(1)} %fusion.60), channel_id=1, source_target_pairs={} | collective-permute-start | bytes 786440 | tf_op jit(solution)/shard_map/ppermute | solution.py:25
  133.0 26.2 %collective-permute-start.10 = (bf16[128,1024]{1,0:T(8,128)(2,1)S(1)}, bf16[128,1024]{1,0:T(8,128)(2,1)S(1)}, u32[]{:S(2)}, u32[]{:S(2)}) collective-permute-start(bf16[128,1024]{1,0:T(8,128)(2,1)S(1)} %fusion.60), channel_id=1, source_target_pairs={{0,14},{1,15},{16,30},{17,31}} | collective-permute-start | bytes 786440 | tf_op jit(solution)/shard_map/ppermute | solution.py:25
  146.4 14.2 %collective-permute-start.11 = (bf16[128,1024]{1,0:T(8,128)(2,1)S(1)}, bf16[128,1024]{1,0:T(8,128)(2,1)S(1)}, u32[]{:S(2)}, u32[]{:S(2)}) collective-permute-start(bf16[128,1024]{1,0:T(8,128)(2,1)S(1)} %fusion.60), channel_id=1, source_target_pairs={{0,12},{2,14},{1,13},{3,15},{16,28},{18,30},{17,29},{19,31}} | collective-permute-start | bytes 786440 | tf_op jit(solution)/shard_map/ppermute | solution.py:25
  152.6 27.6 %collective-permute-start.16 = (bf16[128,1024]{1,0:T(8,128)(2,1)S(1)}, bf16[128,1024]{1,0:T(8,128)(2,1)S(1)}, u32[]{:S(2)}, u32[]{:S(2)}) collective-permute-start(bf16[128,1024]{1,0:T(8,128)(2,1)S(1)} %fusion.60), channel_id=1, source_target_pairs={{0,2},{2,4},{4,6},{6,8},{8,10},{10,12},{12,14},{1,3},{3,5},{5,7},{... | collective-permute-start | bytes 786440 | tf_op jit(solution)/shard_map/ppermute | solution.py:25
  153.9 26.3 %collective-permute-start.15 = (bf16[128,1024]{1,0:T(8,128)(2,1)S(1)}, bf16[128,1024]{1,0:T(8,128)(2,1)S(1)}, u32[]{:S(2)}, u32[]{:S(2)}) collective-permute-start(bf16[128,1024]{1,0:T(8,128)(2,1)S(1)} %fusion.60), channel_id=1, source_target_pairs={{0,4},{2,6},{4,8},{6,10},{8,12},{10,14},{1,5},{3,7},{5,9},{7,11},{... | collective-permute-start | bytes 786440 | tf_op jit(solution)/shard_map/ppermute | solution.py:25
  155.2 14.6 %collective-permute-start.12 = (bf16[128,1024]{1,0:T(8,128)(2,1)S(1)}, bf16[128,1024]{1,0:T(8,128)(2,1)S(1)}, u32[]{:S(2)}, u32[]{:S(2)}) collective-permute-start(bf16[128,1024]{1,0:T(8,128)(2,1)S(1)} %fusion.60), channel_id=1, source_target_pairs={{0,10},{2,12},{4,14},{1,11},{3,13},{5,15},{16,26},{18,28},{20,30},... | collective-permute-start | bytes 786440 | tf_op jit(solution)/shard_map/ppermute | solution.py:25
  159.3 16.2 %collective-permute-start.13 = (bf16[128,1024]{1,0:T(8,128)(2,1)S(1)}, bf16[128,1024]{1,0:T(8,128)(2,1)S(1)}, u32[]{:S(2)}, u32[]{:S(2)}) collective-permute-start(bf16[128,1024]{1,0:T(8,128)(2,1)S(1)} %fusion.60), channel_id=1, source_target_pairs={{0,8},{2,10},{4,12},{6,14},{1,9},{3,11},{5,13},{7,15},{16,24},{18,... | collective-permute-start | bytes 786440 | tf_op jit(solution)/shard_map/ppermute | solution.py:25
  160.6 19.6 %collective-permute-start.14 = (bf16[128,1024]{1,0:T(8,128)(2,1)S(1)}, bf16[128,1024]{1,0:T(8,128)(2,1)S(1)}, u32[]{:S(2)}, u32[]{:S(2)}) collective-permute-start(bf16[128,1024]{1,0:T(8,128)(2,1)S(1)} %fusion.60), channel_id=1, source_target_pairs={{0,6},{2,8},{4,10},{6,12},{8,14},{1,7},{3,9},{5,11},{7,13},{9,15},... | collective-permute-start | bytes 786440 | tf_op jit(solution)/shard_map/ppermute | solution.py:25
  261.7 12.4 %collective-permute-start.24 = (bf16[128,1024]{0,1:T(8,128)(2,1)}, bf16[128,1024]{0,1:T(8,128)(2,1)}, u32[]{:S(2)}, u32[]{:S(2)}) collective-permute-start(bf16[128,1024]{0,1:T(8,128)(2,1)} %bitcast.32), channel_id=1, source_target_pairs={} | collective-permute-start | bytes 786440 | tf_op jit(solution)/shard_map/ppermute | solution.py:25
  263.0 12.3 %collective-permute-start.17 = (bf16[128,1024]{0,1:T(8,128)(2,1)}, bf16[128,1024]{0,1:T(8,128)(2,1)}, u32[]{:S(2)}, u32[]{:S(2)}) collective-permute-start(bf16[128,1024]{0,1:T(8,128)(2,1)} %bitcast.25), channel_id=1, source_target_pairs={{2,0},{4,2},{6,4},{8,6},{10,8},{12,10},{14,12},{3,1},{5,3},{7,5},{... | collective-permute-start | bytes 786440 | tf_op jit(solution)/shard_map/ppermute | solution.py:25
  264.3 27.5 %collective-permute-start.23 = (bf16[128,1024]{0,1:T(8,128)(2,1)}, bf16[128,1024]{0,1:T(8,128)(2,1)}, u32[]{:S(2)}, u32[]{:S(2)}) collective-permute-start(bf16[128,1024]{0,1:T(8,128)(2,1)} %bitcast.31), channel_id=1, source_target_pairs={{14,0},{15,1},{30,16},{31,17}} | collective-permute-start | bytes 786440 | tf_op jit(solution)/shard_map/ppermute | solution.py:25
  271.5 26.4 %collective-permute-start.22 = (bf16[128,1024]{0,1:T(8,128)(2,1)}, bf16[128,1024]{0,1:T(8,128)(2,1)S(1)}, u32[]{:S(2)}, u32[]{:S(2)}) collective-permute-start(bf16[128,1024]{0,1:T(8,128)(2,1)} %bitcast.294), channel_id=1, source_target_pairs={{12,0},{14,2},{13,1},{15,3},{28,16},{30,18},{29,17},{31,19}} | collective-permute-start | bytes 786440 | tf_op jit(solution)/shard_map/ppermute | solution.py:25
  272.8 41.5 %collective-permute-start.21 = (bf16[128,1024]{0,1:T(8,128)(2,1)}, bf16[128,1024]{0,1:T(8,128)(2,1)S(1)}, u32[]{:S(2)}, u32[]{:S(2)}) collective-permute-start(bf16[128,1024]{0,1:T(8,128)(2,1)} %bitcast.293), channel_id=1, source_target_pairs={{10,0},{12,2},{14,4},{11,1},{13,3},{15,5},{26,16},{28,18},{30,20},... | collective-permute-start | bytes 786440 | tf_op jit(solution)/shard_map/ppermute | solution.py:25
  274.1 45.5 %collective-permute-start.20 = (bf16[128,1024]{0,1:T(8,128)(2,1)}, bf16[128,1024]{0,1:T(8,128)(2,1)S(1)}, u32[]{:S(2)}, u32[]{:S(2)}) collective-permute-start(bf16[128,1024]{0,1:T(8,128)(2,1)} %bitcast.292), channel_id=1, source_target_pairs={{8,0},{10,2},{12,4},{14,6},{9,1},{11,3},{13,5},{15,7},{24,16},{26,... | collective-permute-start | bytes 786440 | tf_op jit(solution)/shard_map/ppermute | solution.py:25
  275.4 45.5 %collective-permute-start.19 = (bf16[128,1024]{0,1:T(8,128)(2,1)}, bf16[128,1024]{0,1:T(8,128)(2,1)S(1)}, u32[]{:S(2)}, u32[]{:S(2)}) collective-permute-start(bf16[128,1024]{0,1:T(8,128)(2,1)} %bitcast.291), channel_id=1, source_target_pairs={{6,0},{8,2},{10,4},{12,6},{14,8},{7,1},{9,3},{11,5},{13,7},{15,9},... | collective-permute-start | bytes 786440 | tf_op jit(solution)/shard_map/ppermute | solution.py:25
  291.8 30.4 %collective-permute-start.18 = (bf16[128,1024]{0,1:T(8,128)(2,1)S(1)}, bf16[128,1024]{0,1:T(8,128)(2,1)S(1)}, u32[]{:S(2)}, u32[]{:S(2)}) collective-permute-start(bf16[128,1024]{0,1:T(8,128)(2,1)S(1)} %bitcast.290), channel_id=1, source_target_pairs={{4,0},{6,2},{8,4},{10,6},{12,8},{14,10},{5,1},{7,3},{9,5},{11,7},{... | collective-permute-start | bytes 786440 | tf_op jit(solution)/shard_map/ppermute | solution.py:25
  297.8 29.3 %collective-permute-start.26 = (bf16[128,1024]{1,0:T(8,128)(2,1)S(1)}, bf16[128,1024]{1,0:T(8,128)(2,1)S(1)}, u32[]{:S(2)}, u32[]{:S(2)}) collective-permute-start(bf16[128,1024]{1,0:T(8,128)(2,1)S(1)} %bitcast.305), channel_id=1, source_target_pairs={{4,0},{6,2},{8,4},{10,6},{12,8},{14,10},{5,1},{7,3},{9,5},{11,7},{... | collective-permute-start | bytes 786440 | tf_op jit(solution)/shard_map/ppermute | solution.py:25
  314.3 16.8 %collective-permute-start.27 = (bf16[128,1024]{1,0:T(8,128)(2,1)S(1)}, bf16[128,1024]{1,0:T(8,128)(2,1)}, u32[]{:S(2)}, u32[]{:S(2)}) collective-permute-start(bf16[128,1024]{1,0:T(8,128)(2,1)S(1)} %bitcast.304), channel_id=1, source_target_pairs={{6,0},{8,2},{10,4},{12,6},{14,8},{7,1},{9,3},{11,5},{13,7},{15,9},... | collective-permute-start | bytes 786440 | tf_op jit(solution)/shard_map/ppermute | solution.py:25
  319.6 51.1 %collective-permute-start.28 = (bf16[128,1024]{1,0:T(8,128)(2,1)S(1)}, bf16[128,1024]{1,0:T(8,128)(2,1)}, u32[]{:S(2)}, u32[]{:S(2)}) collective-permute-start(bf16[128,1024]{1,0:T(8,128)(2,1)S(1)} %bitcast.303), channel_id=1, source_target_pairs={{8,0},{10,2},{12,4},{14,6},{9,1},{11,3},{13,5},{15,7},{24,16},{26,... | collective-permute-start | bytes 786440 | tf_op jit(solution)/shard_map/ppermute | solution.py:25
  320.9 56.6 %collective-permute-start.29 = (bf16[128,1024]{1,0:T(8,128)(2,1)S(1)}, bf16[128,1024]{1,0:T(8,128)(2,1)}, u32[]{:S(2)}, u32[]{:S(2)}) collective-permute-start(bf16[128,1024]{1,0:T(8,128)(2,1)S(1)} %bitcast.302), channel_id=1, source_target_pairs={{10,0},{12,2},{14,4},{11,1},{13,3},{15,5},{26,16},{28,18},{30,20},... | collective-permute-start | bytes 786440 | tf_op jit(solution)/shard_map/ppermute | solution.py:25
  322.2 55.3 %collective-permute-start.30 = (bf16[128,1024]{1,0:T(8,128)(2,1)S(1)}, bf16[128,1024]{1,0:T(8,128)(2,1)}, u32[]{:S(2)}, u32[]{:S(2)}) collective-permute-start(bf16[128,1024]{1,0:T(8,128)(2,1)S(1)} %bitcast.300), channel_id=1, source_target_pairs={{12,0},{14,2},{13,1},{15,3},{28,16},{30,18},{29,17},{31,19}} | collective-permute-start | bytes 786440 | tf_op jit(solution)/shard_map/ppermute | solution.py:25
  327.1 50.3 %collective-permute-start.31 = (bf16[128,1024]{1,0:T(8,128)(2,1)S(1)}, bf16[128,1024]{1,0:T(8,128)(2,1)S(1)}, u32[]{:S(2)}, u32[]{:S(2)}) collective-permute-start(bf16[128,1024]{1,0:T(8,128)(2,1)S(1)} %bitcast.299), channel_id=1, source_target_pairs={{14,0},{15,1},{30,16},{31,17}} | collective-permute-start | bytes 786440 | tf_op jit(solution)/shard_map/ppermute | solution.py:25
  331.0 46.4 %collective-permute-start.32 = (bf16[128,1024]{1,0:T(8,128)(2,1)S(1)}, bf16[128,1024]{1,0:T(8,128)(2,1)S(1)}, u32[]{:S(2)}, u32[]{:S(2)}) collective-permute-start(bf16[128,1024]{1,0:T(8,128)(2,1)S(1)} %bitcast.298), channel_id=1, source_target_pairs={} | collective-permute-start | bytes 786440 | tf_op jit(solution)/shard_map/ppermute | solution.py:25
  370.6 12.1 %collective-permute-start.25 = (bf16[128,1024]{1,0:T(8,128)(2,1)S(1)}, bf16[128,1024]{1,0:T(8,128)(2,1)S(1)}, u32[]{:S(2)}, u32[]{:S(2)}) collective-permute-start(bf16[128,1024]{1,0:T(8,128)(2,1)S(1)} %bitcast.297), channel_id=1, source_target_pairs={{2,0},{4,2},{6,4},{8,6},{10,8},{12,10},{14,12},{3,1},{5,3},{7,5},{... | collective-permute-start | bytes 786440 | tf_op jit(solution)/shard_map/ppermute | solution.py:25
Sparse Core Ops, SparseCore 0:
  10.8 58.7 all-gather.2
  71.1 14.1 all-gather.4
  326.9 118.2 all-reduce.3
where the time goes:
time: 457 us; the launch traced here: 455 us
  waiting for transfers between devices  233 us (51%)
  matrix products  83.5 us (18%)
  starting transfers between devices  63.8 us (14%)
  blocking collectives  26.4 us (6%)
  local copies, waits for them, and re-layouts  20.7 us (5%)
  between operations  14.5 us (3%)
  other arithmetic  13.1 us (3%)
    ppermute x32, waiting for transfers between devices, shifted(): return lax.ppermute(block, axis, route)  112 us
    ppermute x32, starting transfers between devices, shifted(): return lax.ppermute(block, axis, route)  63.7 us
    all_gather x1, waiting for transfers between devices, shards(): rows_half = lax.all_gather(own_half, 'ctx', axis=0, tiled=True)  60.4 us
    psum x1, waiting for transfers between devices, shards(): lax.psum((down_factor, up_factor), ('ctx', 'pair'))  60 us
    psum x1, blocking collectives, shards(): own_diff, counts = lax.psum((part_diff, part_count), 'ctx')  26.4 us
    dot_general x8, matrix products, per_head(): jnp.einsum('gtl,tgd->ld', weighted, grad_head, preferred_element_type=jnp...  22.8 us
    dot_general x8, matrix products, per_head(): jnp.einsum('gtl,ld->tgd', score_grad, key_head, preferred_element_type=jn...  14.9 us
    sub x8, matrix products, per_head(): weights_exp = jnp.where(allowed[None], jnp.exp(masked - row_max), 0.0)  13.8 us
  transfers between devices with their start and end apart: 36, of which 15 were waited for; matrix products, arithmetic and copies ran while one was open for 7% of the time, Pallas kernels for 0%

commit v1 on v0

--- a/solution.py
+++ b/solution.py
@@ -71,7 +71,7 @@
     starts = jnp.cumsum(counts) - counts
     tok_start = jnp.sum(seg_table * starts[None, :], 1).astype(jnp.int32)
     token_coefficient = jnp.sum(seg_table * coef[None, :], 1)
-    halo_blocks = WINDOW // tok_rows
+    halo_blocks = min(WINDOW // tok_rows, lax.axis_size("ctx") - 1)
     key_blocks = []
     value_blocks = []
     for distance in range(halo_blocks, 0, -1):
@@ -82,58 +82,41 @@
     all_values = jnp.concatenate(value_blocks + [values], 0)
     span = all_keys.shape[0]
     tpos = ctx_index * tok_rows + jnp.arange(tok_rows, dtype=jnp.int32)
-    upos = ctx_index * tok_rows - WINDOW + jnp.arange(span, dtype=jnp.int32)
+    upos = ctx_index * tok_rows - halo_blocks * tok_rows + jnp.arange(span, dtype=jnp.int32)
     allowed = (
         (upos[None, :] <= tpos[:, None])
         & (upos[None, :] > tpos[:, None] - WINDOW)
         & (upos[None, :] >= tok_start[:, None])
     )
     coef_rows = token_coefficient[None, :, None]
-    query_heads = (
-        queries[0].reshape(tok_rows, kv_heads, group_size, HEAD_SIZE).transpose(1, 0, 2, 3)
+    query_rows = queries[0].reshape(tok_rows, kv_heads, group_size, HEAD_SIZE)
+    grad_rows = output_gradient[0].reshape(tok_rows, kv_heads, group_size, HEAD_SIZE)
+    key_rows = all_keys.reshape(span, kv_heads, HEAD_SIZE)
+    value_rows = all_values.reshape(span, kv_heads, HEAD_SIZE)
+    scores = ATTN_SCALE * jnp.einsum(
+        "tjgd,ljd->jgtl", query_rows, key_rows, preferred_element_type=jnp.float32
     )
-    grad_heads = (
-        output_gradient[0].reshape(tok_rows, kv_heads, group_size, HEAD_SIZE).transpose(1, 0, 2, 3)
+    masked = jnp.where(allowed[None, None], scores, NEG_FILL)
+    row_max = jnp.max(masked, -1, keepdims=True)
+    weights_exp = jnp.where(allowed[None, None], jnp.exp(masked - row_max), 0.0)
+    attn_probs = weights_exp / jnp.sum(weights_exp, -1, keepdims=True)
+    prob_grad = coef_rows[None] * jnp.einsum(
+        "tjgd,ljd->jgtl", grad_rows, value_rows, preferred_element_type=jnp.float32
     )
-    key_heads = all_keys.reshape(span, kv_heads, HEAD_SIZE).transpose(1, 0, 2)
-    value_heads = all_values.reshape(span, kv_heads, HEAD_SIZE).transpose(1, 0, 2)
-
-    def per_head(operands):
-        query_head, key_head, value_head, grad_head = operands
-        scores = ATTN_SCALE * jnp.einsum(
-            "tgd,ld->gtl", query_head, key_head, preferred_element_type=jnp.float32
-        )
-        masked = jnp.where(allowed[None], scores, NEG_FILL)
-        row_max = jnp.max(masked, -1, keepdims=True)
-        weights_exp = jnp.where(allowed[None], jnp.exp(masked - row_max), 0.0)
-        attn_probs = weights_exp / jnp.sum(weights_exp, -1, keepdims=True)
-        prob_grad = coef_rows * jnp.einsum(
-            "tgd,ld->gtl", grad_head, value_head, preferred_element_type=jnp.float32
-        )
-        row_delta = jnp.sum(attn_probs * prob_grad, -1, keepdims=True)
-        score_grad = (ATTN_SCALE * attn_probs * (prob_grad - row_delta)).astype(jnp.bfloat16)
-        head_qgrad = jnp.einsum(
-            "gtl,ld->tgd", score_grad, key_head, preferred_element_type=jnp.float32
-        ).astype(jnp.bfloat16)
-        head_kgrad = jnp.einsum(
-            "gtl,tgd->ld", score_grad, query_head, preferred_element_type=jnp.float32
-        )
-        weighted = (attn_probs * coef_rows).astype(jnp.bfloat16)
-        head_vgrad = jnp.einsum(
-            "gtl,tgd->ld", weighted, grad_head, preferred_element_type=jnp.float32
-        )
-        return (head_qgrad, head_kgrad, head_vgrad)
-
-    query_stack, key_stack, value_stack = lax.map(
-        per_head, (query_heads, key_heads, value_heads, grad_heads)
-    )
-    query_grad = query_stack.transpose(1, 0, 2, 3).reshape(
-        tok_rows, kv_heads * group_size * HEAD_SIZE
-    )
-    key_parts = key_stack.transpose(1, 0, 2).reshape(span, width_kv)
-    value_parts = value_stack.transpose(1, 0, 2).reshape(span, width_kv)
-    key_total = key_parts[WINDOW:]
-    value_total = value_parts[WINDOW:]
+    row_delta = jnp.sum(attn_probs * prob_grad, -1, keepdims=True)
+    score_grad = (ATTN_SCALE * attn_probs * (prob_grad - row_delta)).astype(jnp.bfloat16)
+    query_grad = jnp.einsum(
+        "jgtl,ljd->tjgd", score_grad, key_rows, preferred_element_type=jnp.float32
+    ).astype(jnp.bfloat16).reshape(tok_rows, kv_heads * group_size * HEAD_SIZE)
+    key_parts = jnp.einsum(
+        "jgtl,tjgd->ljd", score_grad, query_rows, preferred_element_type=jnp.float32
+    ).reshape(span, width_kv)
+    weighted = (attn_probs * coef_rows[None]).astype(jnp.bfloat16)
+    value_parts = jnp.einsum(
+        "jgtl,tjgd->ljd", weighted, grad_rows, preferred_element_type=jnp.float32
+    ).reshape(span, width_kv)
+    key_total = key_parts[halo_blocks * tok_rows :]
+    value_total = value_parts[halo_blocks * tok_rows :]
     for distance in range(1, halo_blocks + 1):
         block_start = (halo_blocks - distance) * tok_rows
         send_keys = key_parts[block_start : block_start + tok_rows].astype(jnp.bfloat16)

time: 457 us -> 305 us (0.67)
  waiting for transfers between devices: 233 us -> 96.3 us
  matrix products: 83.5 us -> 28 us
  local copies, waits for them, and re-layouts: 20.7 us -> 39.9 us
  blocking collectives: 26.4 us -> 43.1 us
  starting transfers between devices: 63.8 us -> 68.5 us
    ppermute x32 -> x28, waiting for transfers between devices: 112 us -> 62.8 us  [shifted(): return lax.ppermute(block, axis, route)]
    psum x1, waiting for transfers between devices: 60 us -> 11.7 us  [shards(): lax.psum((down_factor, up_factor), ('ctx', 'pair'))]
    dot_general x32 -> x5, matrix products: 58 us -> 14.2 us  [the longest x1 4.83 us: shards(): jnp.einsum('tjgd,ljd->jgtl', grad_rows, value_rows, preferred_element_typ...]
    all_gather x1, waiting for transfers between devices: 60.4 us -> 21.7 us  [shards(): rows_half = lax.all_gather(own_half, 'ctx', axis=0, tiled=True)]
    psum x1, blocking collectives: 26.4 us -> 43.1 us  [shards(): own_diff, counts = lax.psum((part_diff, part_count), 'ctx')]
    sub x8 -> x0, matrix products: 13.8 us -> none  [per_head(): weights_exp = jnp.where(allowed[None], jnp.exp(masked - row_max), 0.0)]
    convert_element_type x8 -> x7, local copies, waits for them, and re-layouts: 0.5 us -> 9.73 us  [shards(): key_parts[block_start:block_start + tok_rows].astype(jnp.bfloat16)]
    concatenate x1 -> x9, local copies, waits for them, and re-layouts: 0.76 us -> 6.83 us  [shards(): all_keys = jnp.concatenate(key_blocks + [own_keys], 0)]
  transfers between devices with their start and end apart: 36 -> 32, of which waited for: 15 -> 11; matrix products, arithmetic and copies ran while one was open for 7% -> 22% of each run, Pallas kernels for 0% -> 0%
where the time goes in v1:
time: 305 us; the launch traced here: 303 us
  waiting for transfers between devices  96.3 us (32%)
  starting transfers between devices  68.5 us (22%)
  blocking collectives  43.1 us (14%)
  local copies, waits for them, and re-layouts  39.9 us (13%)
  matrix products  28 us (9%)
  between operations  16.2 us (5%)
  other arithmetic  10.7 us (4%)
    ppermute x28, starting transfers between devices, shifted(): return lax.ppermute(block, axis, route)  68.3 us
    ppermute x28, waiting for transfers between devices, shifted(): return lax.ppermute(block, axis, route)  62.8 us
    psum x1, blocking collectives, shards(): own_diff, counts = lax.psum((part_diff, part_count), 'ctx')  43.1 us
    all_gather x1, waiting for transfers between devices, shards(): rows_half = lax.all_gather(own_half, 'ctx', axis=0, tiled=True)  21.7 us
    unnamed x57, local copies, waits for them, and re-layouts  14.7 us
    psum x1, waiting for transfers between devices, shards(): lax.psum((down_factor, up_factor), ('ctx', 'pair'))  11.7 us
    convert_element_type x7, local copies, waits for them, and re-layouts, shards(): key_parts[block_start:block_start + tok_rows].astype(jnp.bfloat16)  9.73 us
    concatenate x9, local copies, waits for them, and re-layouts, shards(): all_keys = jnp.concatenate(key_blocks + [own_keys], 0)  6.83 us
  transfers between devices with their start and end apart: 32, of which 11 were waited for; matrix products, arithmetic and copies ran while one was open for 22% of the time, Pallas kernels for 0%

profile of v1, /device:TPU:0, one launch (start us, length us, event | category | flops | bytes accessed | tf_op | source)
XLA Modules:
  0.0 302.7 jit_solution(10808703439121389320)
XLA Ops:
  8.1 1.8 constant_dynamic-slice_fusion
  11.1 7.9 %collective-permute-start = (bf16[128,1024]{0,1:T(8,128)(2,1)S(1)}, bf16[128,1024]{0,1:T(8,128)(2,1)S(1)}, u32[]{:S(2)}, u32[]{:S(2)}) collective-permute-start(bf16[128,1024]{0,1:T(8,128)(2,1)S(1)} %bitcast.143), channel_id=1, source_target_pairs={{0,14},{1,15},{16,30},{17,31}} | collective-permute-start | bytes 786440 | tf_op jit(solution)/shard_map/ppermute | solution.py:25
  19.0 1.3 collective-permute-start.1
  20.3 1.3 collective-permute-start.2
  21.6 1.3 collective-permute-start.3
  24.4 43.1 %all-reduce.1 = (f32[8]{0:T(128)S(1)}, f32[8]{0:T(128)S(1)}) all-reduce(f32[8]{0:T(128)S(1)} %get-tuple-element.22, f32[8]{0:T(128)S(1)} %get-tuple-element.23), channel_id=1, replica_groups=mesh['grp'=2,'ctx'=8,'pair'=2] {'ctx'}, use_global_device_ids=true, to_apply=%region_1.0 | all-reduce | flops 16 | bytes 128 | tf_op jit(solution)/shard_map/psum | solution.py:66
  67.8 2.2 reshape_squeeze.7
  71.1 21.7 %all-gather.3.cloned.1.call-done = bf16[2688,512]{1,0:T(8,128)(2,1)} async-done(((bf16[336,512]{1,0:T(8,128)(2,1)}), bf16[2688,512]{1,0:T(8,128)(2,1)}) %all-gather.3.cloned.1.call-update) | async-done | bytes 2752528 | tf_op jit(solution)/shard_map/all_gather | solution.py:50
  92.9 3.4 %collective-permute-start.4 = (bf16[128,1024]{0,1:T(8,128)(2,1)S(1)}, bf16[128,1024]{0,1:T(8,128)(2,1)S(1)}, u32[]{:S(2)}, u32[]{:S(2)}) collective-permute-start(bf16[128,1024]{0,1:T(8,128)(2,1)S(1)} %bitcast.148), channel_id=1, source_target_pairs={{0,6},{2,8},{4,10},{6,12},{8,14},{1,7},{3,9},{5,11},{7,13},{9,15},... | collective-permute-start | bytes 786440 | tf_op jit(solution)/shard_map/ppermute | solution.py:25
  96.4 2.9 collective-permute-start.5
  99.3 3.3 %collective-permute-start.6 = (bf16[128,1024]{0,1:T(8,128)(2,1)S(1)}, bf16[128,1024]{0,1:T(8,128)(2,1)S(1)}, u32[]{:S(2)}, u32[]{:S(2)}) collective-permute-start(bf16[128,1024]{0,1:T(8,128)(2,1)S(1)} %bitcast.150), channel_id=1, source_target_pairs={{0,2},{2,4},{4,6},{6,8},{8,10},{10,12},{12,14},{1,3},{3,5},{5,7},{... | collective-permute-start | bytes 786440 | tf_op jit(solution)/shard_map/ppermute | solution.py:25
  114.4 4.3 %fusion.42 = (f32[8,2,128]{2,1,0:T(2,128)S(1)}, f32[8,2,128,1024]{2,3,1,0:T(8,128)S(1)}) fusion(f32[8,1024,128,2]{2,1,3,0:T(8,128)S(1)} %fusion.16, pred[128,1024]{0,1:T(8,128)(4,1)S(1)} %compare_and_fusion), kind=kOutput, calls=%fused_computation.86 | output fusion | flops 14681087 | bytes 16916480 | tf_op jit(solution)/shard_map/sub | solution.py:101
  118.8 1.5 fusion.43
  120.3 1.7 copy-done.3
  122.6 1.3 collective-permute-start.14
  129.1 6.2 %collective-permute-done.14 = bf16[128,1024]{0,1:T(8,128)(2,1)S(1)} collective-permute-done((bf16[128,1024]{0,1:T(8,128)(2,1)S(1)}, bf16[128,1024]{0,1:T(8,128)(2,1)S(1)}, u32[]{:S(2)}, u32[]{:S(2)}) %collective-permute-start.14) | collective-permute-done | bytes 262176 | tf_op jit(solution)/shard_map/ppermute | solution.py:25
  136.6 4.6 %collective-permute-done.13 = bf16[128,1024]{0,1:T(8,128)(2,1)S(1)} collective-permute-done((bf16[128,1024]{0,1:T(8,128)(2,1)S(1)}, bf16[128,1024]{0,1:T(8,128)(2,1)S(1)}, u32[]{:S(2)}, u32[]{:S(2)}) %collective-permute-start.13) | collective-permute-done | bytes 262176 | tf_op jit(solution)/shard_map/ppermute | solution.py:25
  141.1 1.6 collective-permute-start.8
  143.1 13.9 %collective-permute-done.12 = bf16[128,1024]{0,1:T(8,128)(2,1)S(1)} collective-permute-done((bf16[128,1024]{0,1:T(8,128)(2,1)S(1)}, bf16[128,1024]{0,1:T(8,128)(2,1)S(1)}, u32[]{:S(2)}, u32[]{:S(2)}) %collective-permute-start.12) | collective-permute-done | bytes 262176 | tf_op jit(solution)/shard_map/ppermute | solution.py:25
  157.1 5.0 %collective-permute-done.11 = bf16[128,1024]{0,1:T(8,128)(2,1)S(1)} collective-permute-done((bf16[128,1024]{0,1:T(8,128)(2,1)S(1)}, bf16[128,1024]{0,1:T(8,128)(2,1)S(1)}, u32[]{:S(2)}, u32[]{:S(2)}) %collective-permute-start.11) | collective-permute-done | bytes 262176 | tf_op jit(solution)/shard_map/ppermute | solution.py:25
  163.2 1.5 convolution_multiply_fusion
  164.7 3.5 %convolution_bitcast_fusion.1 = f32[128,1024]{1,0:T(8,128)S(1)} fusion(bf16[2688,1024]{1,0:T(8,128)(2,1)} %all-gather.5.cloned.1.call-done, bf16[1,128,2688]{2,1,0:T(8,128)(2,1)S(1)} %copy-done), kind=kOutput, calls=%fused_computation.31 | convolution fusion | flops 704643072 | bytes 6717440 | tf_op jit(solution)/shard_map/dot_general | solution.py:56
  169.2 2.6 collective-permute-start.15
  172.7 5.8 %collective-permute-start.16 = (bf16[128,1024]{1,0:T(8,128)(2,1)}, bf16[128,1024]{1,0:T(8,128)(2,1)S(1)}, u32[]{:S(2)}, u32[]{:S(2)}) collective-permute-start(bf16[128,1024]{1,0:T(8,128)(2,1)} %fusion.24), channel_id=1, source_target_pairs={{0,12},{2,14},{1,13},{3,15},{16,28},{18,30},{17,29},{19,31}} | collective-permute-start | bytes 786440 | tf_op jit(solution)/shard_map/ppermute | solution.py:25
  178.4 6.8 %collective-permute-start.17 = (bf16[128,1024]{1,0:T(8,128)(2,1)}, bf16[128,1024]{1,0:T(8,128)(2,1)S(1)}, u32[]{:S(2)}, u32[]{:S(2)}) collective-permute-start(bf16[128,1024]{1,0:T(8,128)(2,1)} %fusion.24), channel_id=1, source_target_pairs={{0,10},{2,12},{4,14},{1,11},{3,13},{5,15},{16,26},{18,28},{20,30},... | collective-permute-start | bytes 786440 | tf_op jit(solution)/shard_map/ppermute | solution.py:25
  186.1 5.8 %collective-permute-start.18 = (bf16[128,1024]{1,0:T(8,128)(2,1)}, bf16[128,1024]{1,0:T(8,128)(2,1)S(1)}, u32[]{:S(2)}, u32[]{:S(2)}) collective-permute-start(bf16[128,1024]{1,0:T(8,128)(2,1)} %fusion.24), channel_id=1, source_target_pairs={{0,8},{2,10},{4,12},{6,14},{1,9},{3,11},{5,13},{7,15},{16,24},{18,... | collective-permute-start | bytes 786440 | tf_op jit(solution)/shard_map/ppermute | solution.py:25
  191.9 3.2 %collective-permute-start.19 = (bf16[128,1024]{1,0:T(8,128)(2,1)}, bf16[128,1024]{1,0:T(8,128)(2,1)S(1)}, u32[]{:S(2)}, u32[]{:S(2)}) collective-permute-start(bf16[128,1024]{1,0:T(8,128)(2,1)} %fusion.24), channel_id=1, source_target_pairs={{0,6},{2,8},{4,10},{6,12},{8,14},{1,7},{3,9},{5,11},{7,13},{9,15},... | collective-permute-start | bytes 786440 | tf_op jit(solution)/shard_map/ppermute | solution.py:25
  195.1 1.3 collective-permute-start.20
  197.4 3.1 %collective-permute-start.21 = (bf16[128,1024]{1,0:T(8,128)(2,1)}, bf16[128,1024]{1,0:T(8,128)(2,1)S(1)}, u32[]{:S(2)}, u32[]{:S(2)}) collective-permute-start(bf16[128,1024]{1,0:T(8,128)(2,1)} %fusion.24), channel_id=1, source_target_pairs={{0,2},{2,4},{4,6},{6,8},{8,10},{10,12},{12,14},{1,3},{3,5},{5,7},{... | collective-permute-start | bytes 786440 | tf_op jit(solution)/shard_map/ppermute | solution.py:25
  200.6 4.7 %collective-permute-done.19 = bf16[128,1024]{1,0:T(8,128)(2,1)S(1)} collective-permute-done((bf16[128,1024]{1,0:T(8,128)(2,1)}, bf16[128,1024]{1,0:T(8,128)(2,1)S(1)}, u32[]{:S(2)}, u32[]{:S(2)}) %collective-permute-start.19) | collective-permute-done | bytes 262176 | tf_op jit(solution)/shard_map/ppermute | solution.py:25
  205.4 5.1 %collective-permute-done.20 = bf16[128,1024]{1,0:T(8,128)(2,1)S(1)} collective-permute-done((bf16[128,1024]{1,0:T(8,128)(2,1)}, bf16[128,1024]{1,0:T(8,128)(2,1)S(1)}, u32[]{:S(2)}, u32[]{:S(2)}) %collective-permute-start.20) | collective-permute-done | bytes 262176 | tf_op jit(solution)/shard_map/ppermute | solution.py:25
  212.6 4.8 %fusion.1 = (f32[8,2,128]{2,1,0:T(2,128)S(1)}, f32[8,1024,128,2]{2,1,3,0:T(8,128)S(1)}) fusion(f32[128]{0:T(128)S(1)} %get-tuple-element.21, f32[8,2,128,1024]{2,3,1,0:T(8,128)} %copy-done.3, f32[8,2,128]{2,1,0:T(2,128)S(1)} %get-tuple-element.42, bf16[128,8,2,128]{3,2,1,0:T(2,128)(2,1)S(1)} %copy-done.13, bf16[1024,8,128,1]{2,1,0,3:T(8,128)(2,1)S(1)} %bitcast.134), kind=kOutput, calls=%fused_computation.3 | convolution fusion | flops 545257472 | bytes 19415552 | tf_op jit(solution)/shard_map/tjgd,ljd->jgtl/dot_general | solution.py:103
  218.2 1.7 fusion.3
  219.9 3.5 %fusion.44 = (bf16[1024,8,128]{0,2,1:T(8,128)(2,1)S(1)}, f32[1024,8,128]{0,2,1:T(8,128)}) fusion(bf16[8,2,128,1024]{2,3,1,0:T(8,128)(2,1)S(1)} %fusion.3, bf16[128,8,2,128]{0,3,2,1:T(8,128)(2,1)S(1)} %bitcast.131), kind=kOutput, calls=%fused_computation.88 | convolution fusion | flops 537919488 | bytes 11010048 | tf_op jit(solution)/shard_map/jgtl,tjgd->ljd/dot_general | solution.py:111
  223.4 1.3 fusion.40
  224.8 1.8 copy.87
  227.9 1.8 copy.86
  231.0 5.7 %fusion.11 = bf16[1,128,2688]{2,1,0:T(8,128)(2,1)} fusion(f32[128,2688]{1,0:T(8,128)} %convolution_multiply_fusion, bf16[128,1024]{0,1:T(8,128)(2,1)S(1)} %copy-done.6, bf16[2688,1024]{1,0:T(8,128)(2,1)} %all-gather.5.cloned.1.call-done), kind=kOutput, calls=%fused_computation.19 | convolution fusion | flops 705331200 | bytes 7831552 | tf_op jit(solution)/shard_map/tk,dk->td/dot_general | solution.py:133
  236.7 1.8 copy.85
  239.8 1.8 copy.84
  249.3 3.1 %fusion.20 = bf16[8,128,2,128]{3,1,2,0:T(8,128)(2,1)S(1)} fusion(bf16[8,2,128,1024]{2,3,1,0:T(8,128)(2,1)} %copy-done.2, bf16[1024,8,128]{2,0,1:T(8,128)(2,1)S(1)} %constant_dynamic-update-slice_fusion), kind=kOutput, calls=%fused_computation.30 | convolution fusion | flops 537133056 | bytes 6815744 | tf_op jit(solution)/shard_map/jgtl,ljd->tjgd/dot_general | solution.py:108
  254.8 17.4 %collective-permute-done.26 = bf16[128,1024]{1,0:T(8,128)(2,1)} collective-permute-done((bf16[128,1024]{1,0:T(8,128)(2,1)}, bf16[128,1024]{1,0:T(8,128)(2,1)}, u32[]{:S(2)}, u32[]{:S(2)}) %collective-permute-start.26) | collective-permute-done | bytes 262176 | tf_op jit(solution)/shard_map/ppermute | solution.py:25
  272.1 4.2 %collective-permute-done.25 = bf16[128,1024]{1,0:T(8,128)(2,1)} collective-permute-done((bf16[128,1024]{1,0:T(8,128)(2,1)}, bf16[128,1024]{1,0:T(8,128)(2,1)}, u32[]{:S(2)}, u32[]{:S(2)}) %collective-permute-start.25) | collective-permute-done | bytes 262176 | tf_op jit(solution)/shard_map/ppermute | solution.py:25
  276.4 1.6 collective-permute-done.24
  278.0 2.5 fusion.37
  280.4 11.7 %all-reduce.4.cloned.1.call-done = (f32[2688,16]{0,1:T(8,128)}, f32[16,1024]{1,0:T(8,128)}) async-done(((f32[2688,16]{0,1:T(8,128)}, f32[16,1024]{1,0:T(8,128)}), (f32[2688,16]{0,1:T(8,128)}, f32[16,1024]{1,0:T(8,128)})) %all-reduce.4.cloned.1.call-update) | async-done | bytes 237584 | tf_op jit(solution)/shard_map/psum | solution.py:143
  292.1 1.6 copy.131
  293.7 1.5 copy.132
  (130 shorter events, 44.8 us)
Async XLA Ops:
  8.0 134.7 %copy-start = (bf16[1,128,2688]{2,1,0:T(8,128)(2,1)S(1)}, bf16[1,128,2688]{2,1,0:T(8,128)(2,1)}, u32[]{:S(2)}) copy-start(bf16[1,128,2688]{2,1,0:T(8,128)(2,1)} %param.10) | copy-start | bytes 2064388
  8.0 62.0 %copy-start.11 = (bf16[1,128,2048]{2,1,0:T(8,128)(2,1)S(1)}, bf16[1,128,2048]{2,1,0:T(8,128)(2,1)}, u32[]{:S(2)}) copy-start(bf16[1,128,2048]{2,1,0:T(8,128)(2,1)} %param.11) | copy-start | bytes 1572868
  8.0 84.8 %all-gather.3.cloned.1.call-start = ((), (), s32[]{:S(2)}) async-start(), calls=%async_computation | async-start | bytes 3096576 | tf_op jit(solution)/shard_map/all_gather | solution.py:50
  9.9 154.8 %all-gather.5.cloned.1.call-start = ((), (), s32[]{:S(2)}) async-start(), calls=%async_computation.1 | async-start | bytes 8257536 | tf_op jit(solution)/shard_map/all_gather | solution.py:51
  11.1 85.2 %collective-permute-start = (bf16[128,1024]{0,1:T(8,128)(2,1)S(1)}, bf16[128,1024]{0,1:T(8,128)(2,1)S(1)}, u32[]{:S(2)}, u32[]{:S(2)}) collective-permute-start(bf16[128,1024]{0,1:T(8,128)(2,1)S(1)} %bitcast.143), channel_id=1, source_target_pairs={{0,14},{1,15},{16,30},{17,31}} | collective-permute-start | bytes 786440 | tf_op jit(solution)/shard_map/ppermute | solution.py:25
  19.0 80.3 %collective-permute-start.1 = (bf16[128,1024]{0,1:T(8,128)(2,1)S(1)}, bf16[128,1024]{0,1:T(8,128)(2,1)S(1)}, u32[]{:S(2)}, u32[]{:S(2)}) collective-permute-start(bf16[128,1024]{0,1:T(8,128)(2,1)S(1)} %bitcast.144), channel_id=1, source_target_pairs={{0,12},{2,14},{1,13},{3,15},{16,28},{18,30},{17,29},{19,31}} | collective-permute-start | bytes 786440 | tf_op jit(solution)/shard_map/ppermute | solution.py:25
  20.3 84.3 %collective-permute-start.2 = (bf16[128,1024]{0,1:T(8,128)(2,1)S(1)}, bf16[128,1024]{0,1:T(8,128)(2,1)S(1)}, u32[]{:S(2)}, u32[]{:S(2)}) collective-permute-start(bf16[128,1024]{0,1:T(8,128)(2,1)S(1)} %bitcast.145), channel_id=1, source_target_pairs={{0,10},{2,12},{4,14},{1,11},{3,13},{5,15},{16,26},{18,28},{20,30},... | collective-permute-start | bytes 786440 | tf_op jit(solution)/shard_map/ppermute | solution.py:25
  21.6 83.9 %collective-permute-start.3 = (bf16[128,1024]{0,1:T(8,128)(2,1)S(1)}, bf16[128,1024]{0,1:T(8,128)(2,1)S(1)}, u32[]{:S(2)}, u32[]{:S(2)}) collective-permute-start(bf16[128,1024]{0,1:T(8,128)(2,1)S(1)} %bitcast.146), channel_id=1, source_target_pairs={{0,8},{2,10},{4,12},{6,14},{1,9},{3,11},{5,13},{7,15},{16,24},{18,... | collective-permute-start | bytes 786440 | tf_op jit(solution)/shard_map/ppermute | solution.py:25
  67.5 25.4 %collective-permute-start.7 = (f32[8]{0:T(128)S(1)}, f32[8]{0:T(128)S(1)}, u32[]{:S(2)}, u32[]{:S(2)}) collective-permute-start(f32[8]{0:T(128)S(1)} %get-tuple-element.27), channel_id=1, source_target_pairs={{0,1},{1,0},{2,3},{3,2},{4,5},{5,4},{6,7},{7,6},{8,9},{9,8},{10,11... | collective-permute-start | bytes 104 | tf_op jit(solution)/shard_map/ppermute | solution.py:19
  70.0 32.7 %copy-start.16 = (s32[1,128]{1,0:T(1,128)S(1)}, s32[1,128]{1,0:T(1,128)}, u32[]{:S(2)}) copy-start(s32[1,128]{1,0:T(1,128)} %param.19) | copy-start | bytes 1540
  92.9 199.3 %all-reduce.4.cloned.1.call-start = ((), (), s32[]{:S(2)}) async-start(), calls=%async_computation.2 | async-start | bytes 475136 | tf_op jit(solution)/shard_map/psum | solution.py:143
  92.9 13.5 %collective-permute-start.4 = (bf16[128,1024]{0,1:T(8,128)(2,1)S(1)}, bf16[128,1024]{0,1:T(8,128)(2,1)S(1)}, u32[]{:S(2)}, u32[]{:S(2)}) collective-permute-start(bf16[128,1024]{0,1:T(8,128)(2,1)S(1)} %bitcast.148), channel_id=1, source_target_pairs={{0,6},{2,8},{4,10},{6,12},{8,14},{1,7},{3,9},{5,11},{7,13},{9,15},... | collective-permute-start | bytes 786440 | tf_op jit(solution)/shard_map/ppermute | solution.py:25
  96.4 10.9 %collective-permute-start.5 = (bf16[128,1024]{0,1:T(8,128)(2,1)S(1)}, bf16[128,1024]{0,1:T(8,128)(2,1)S(1)}, u32[]{:S(2)}, u32[]{:S(2)}) collective-permute-start(bf16[128,1024]{0,1:T(8,128)(2,1)S(1)} %bitcast.149), channel_id=1, source_target_pairs={{0,4},{2,6},{4,8},{6,10},{8,12},{10,14},{1,5},{3,7},{5,9},{7,11},{... | collective-permute-start | bytes 786440 | tf_op jit(solution)/shard_map/ppermute | solution.py:25
  99.3 8.8 %collective-permute-start.6 = (bf16[128,1024]{0,1:T(8,128)(2,1)S(1)}, bf16[128,1024]{0,1:T(8,128)(2,1)S(1)}, u32[]{:S(2)}, u32[]{:S(2)}) collective-permute-start(bf16[128,1024]{0,1:T(8,128)(2,1)S(1)} %bitcast.150), channel_id=1, source_target_pairs={{0,2},{2,4},{4,6},{6,8},{8,10},{10,12},{12,14},{1,3},{3,5},{5,7},{... | collective-permute-start | bytes 786440 | tf_op jit(solution)/shard_map/ppermute | solution.py:25
  108.9 4.0 %copy-start.8 = (bf16[128,8,128]{2,0,1:T(8,128)(2,1)S(1)}, bf16[128,8,128]{2,0,1:T(8,128)(2,1)}, u32[]{:S(2)}) copy-start(bf16[128,8,128]{2,0,1:T(8,128)(2,1)} %copy.67) | copy-start | bytes 786436
  108.9 4.1 %copy-start.9 = (bf16[128,8,128]{2,0,1:T(8,128)(2,1)S(1)}, bf16[128,8,128]{2,0,1:T(8,128)(2,1)}, u32[]{:S(2)}) copy-start(bf16[128,8,128]{2,0,1:T(8,128)(2,1)} %copy.68) | copy-start | bytes 786436
  108.9 4.2 %copy-start.10 = (bf16[128,8,128]{2,0,1:T(8,128)(2,1)S(1)}, bf16[128,8,128]{2,0,1:T(8,128)(2,1)}, u32[]{:S(2)}) copy-start(bf16[128,8,128]{2,0,1:T(8,128)(2,1)} %copy.69) | copy-start | bytes 786436
  108.9 4.2 %copy-start.7 = (bf16[128,8,128]{2,0,1:T(8,128)(2,1)S(1)}, bf16[128,8,128]{2,0,1:T(8,128)(2,1)}, u32[]{:S(2)}) copy-start(bf16[128,8,128]{2,0,1:T(8,128)(2,1)} %copy.70) | copy-start | bytes 786436
  114.4 4.3 %copy-start.12 = (bf16[128,8,2,128]{3,2,1,0:T(2,128)(2,1)S(1)}, bf16[128,8,2,128]{3,2,1,0:T(2,128)(2,1)}, u32[]{:S(2)}) copy-start(bf16[128,8,2,128]{3,2,1,0:T(2,128)(2,1)} %reshape_squeeze.7) | copy-start | bytes 1572868
  122.1 20.7 %copy-start.14 = (bf16[2688,16]{0,1:T(8,128)(2,1)S(1)}, bf16[2688,16]{0,1:T(8,128)(2,1)}, u32[]{:S(2)}) copy-start(bf16[2688,16]{0,1:T(8,128)(2,1)} %param.14) | copy-start | bytes 258052
  122.6 12.7 %collective-permute-start.14 = (bf16[128,1024]{0,1:T(8,128)(2,1)S(1)}, bf16[128,1024]{0,1:T(8,128)(2,1)S(1)}, u32[]{:S(2)}, u32[]{:S(2)}) collective-permute-start(bf16[128,1024]{0,1:T(8,128)(2,1)S(1)} %bitcast.157), channel_id=1, source_target_pairs={{14,0},{15,1},{30,16},{31,17}} | collective-permute-start | bytes 786440 | tf_op jit(solution)/shard_map/ppermute | solution.py:25
  123.9 17.3 %collective-permute-start.13 = (bf16[128,1024]{0,1:T(8,128)(2,1)S(1)}, bf16[128,1024]{0,1:T(8,128)(2,1)S(1)}, u32[]{:S(2)}, u32[]{:S(2)}) collective-permute-start(bf16[128,1024]{0,1:T(8,128)(2,1)S(1)} %bitcast.156), channel_id=1, source_target_pairs={{12,0},{14,2},{13,1},{15,3},{28,16},{30,18},{29,17},{31,19}} | collective-permute-start | bytes 786440 | tf_op jit(solution)/shard_map/ppermute | solution.py:25
  125.2 31.9 %collective-permute-start.12 = (bf16[128,1024]{0,1:T(8,128)(2,1)S(1)}, bf16[128,1024]{0,1:T(8,128)(2,1)S(1)}, u32[]{:S(2)}, u32[]{:S(2)}) collective-permute-start(bf16[128,1024]{0,1:T(8,128)(2,1)S(1)} %bitcast.155), channel_id=1, source_target_pairs={{10,0},{12,2},{14,4},{11,1},{13,3},{15,5},{26,16},{28,18},{30,20},... | collective-permute-start | bytes 786440 | tf_op jit(solution)/shard_map/ppermute | solution.py:25
  126.5 35.6 %collective-permute-start.11 = (bf16[128,1024]{0,1:T(8,128)(2,1)S(1)}, bf16[128,1024]{0,1:T(8,128)(2,1)S(1)}, u32[]{:S(2)}, u32[]{:S(2)}) collective-permute-start(bf16[128,1024]{0,1:T(8,128)(2,1)S(1)} %bitcast.154), channel_id=1, source_target_pairs={{8,0},{10,2},{12,4},{14,6},{9,1},{11,3},{13,5},{15,7},{24,16},{26,... | collective-permute-start | bytes 786440 | tf_op jit(solution)/shard_map/ppermute | solution.py:25
  127.8 34.3 %collective-permute-start.10 = (bf16[128,1024]{0,1:T(8,128)(2,1)S(1)}, bf16[128,1024]{0,1:T(8,128)(2,1)S(1)}, u32[]{:S(2)}, u32[]{:S(2)}) collective-permute-start(bf16[128,1024]{0,1:T(8,128)(2,1)S(1)} %bitcast.153), channel_id=1, source_target_pairs={{6,0},{8,2},{10,4},{12,6},{14,8},{7,1},{9,3},{11,5},{13,7},{15,9},... | collective-permute-start | bytes 786440 | tf_op jit(solution)/shard_map/ppermute | solution.py:25
  135.3 26.8 %collective-permute-start.9 = (bf16[128,1024]{0,1:T(8,128)(2,1)S(1)}, bf16[128,1024]{0,1:T(8,128)(2,1)S(1)}, u32[]{:S(2)}, u32[]{:S(2)}) collective-permute-start(bf16[128,1024]{0,1:T(8,128)(2,1)S(1)} %bitcast.152), channel_id=1, source_target_pairs={{4,0},{6,2},{8,4},{10,6},{12,8},{14,10},{5,1},{7,3},{9,5},{11,7},{... | collective-permute-start | bytes 786440 | tf_op jit(solution)/shard_map/ppermute | solution.py:25
  141.1 22.0 %copy-start.15 = (bf16[16,1024]{1,0:T(8,128)(2,1)S(1)}, bf16[16,1024]{1,0:T(8,128)(2,1)}, u32[]{:S(2)}) copy-start(bf16[16,1024]{1,0:T(8,128)(2,1)} %param.15) | copy-start | bytes 98308
  141.1 21.0 %collective-permute-start.8 = (bf16[128,1024]{0,1:T(8,128)(2,1)S(1)}, bf16[128,1024]{0,1:T(8,128)(2,1)S(1)}, u32[]{:S(2)}, u32[]{:S(2)}) collective-permute-start(bf16[128,1024]{0,1:T(8,128)(2,1)S(1)} %bitcast.151), channel_id=1, source_target_pairs={{2,0},{4,2},{6,4},{8,6},{10,8},{12,10},{14,12},{3,1},{5,3},{7,5},{... | collective-permute-start | bytes 786440 | tf_op jit(solution)/shard_map/ppermute | solution.py:25
  164.7 20.5 %copy-start.5 = (bf16[128,1024]{0,1:T(8,128)(2,1)S(1)}, bf16[128,1024]{0,1:T(8,128)(2,1)}, u32[]{:S(2)}) copy-start(bf16[128,1024]{0,1:T(8,128)(2,1)} %copy-done.4) | copy-start | bytes 786436
  169.2 25.9 %collective-permute-start.15 = (bf16[128,1024]{1,0:T(8,128)(2,1)}, bf16[128,1024]{1,0:T(8,128)(2,1)}, u32[]{:S(2)}, u32[]{:S(2)}) collective-permute-start(bf16[128,1024]{1,0:T(8,128)(2,1)} %fusion.24), channel_id=1, source_target_pairs={{0,14},{1,15},{16,30},{17,31}} | collective-permute-start | bytes 786440 | tf_op jit(solution)/shard_map/ppermute | solution.py:25
  172.7 24.7 %collective-permute-start.16 = (bf16[128,1024]{1,0:T(8,128)(2,1)}, bf16[128,1024]{1,0:T(8,128)(2,1)S(1)}, u32[]{:S(2)}, u32[]{:S(2)}) collective-permute-start(bf16[128,1024]{1,0:T(8,128)(2,1)} %fusion.24), channel_id=1, source_target_pairs={{0,12},{2,14},{1,13},{3,15},{16,28},{18,30},{17,29},{19,31}} | collective-permute-start | bytes 786440 | tf_op jit(solution)/shard_map/ppermute | solution.py:25
  178.4 22.1 %collective-permute-start.17 = (bf16[128,1024]{1,0:T(8,128)(2,1)}, bf16[128,1024]{1,0:T(8,128)(2,1)S(1)}, u32[]{:S(2)}, u32[]{:S(2)}) collective-permute-start(bf16[128,1024]{1,0:T(8,128)(2,1)} %fusion.24), channel_id=1, source_target_pairs={{0,10},{2,12},{4,14},{1,11},{3,13},{5,15},{16,26},{18,28},{20,30},... | collective-permute-start | bytes 786440 | tf_op jit(solution)/shard_map/ppermute | solution.py:25
  186.1 14.5 %collective-permute-start.18 = (bf16[128,1024]{1,0:T(8,128)(2,1)}, bf16[128,1024]{1,0:T(8,128)(2,1)S(1)}, u32[]{:S(2)}, u32[]{:S(2)}) collective-permute-start(bf16[128,1024]{1,0:T(8,128)(2,1)} %fusion.24), channel_id=1, source_target_pairs={{0,8},{2,10},{4,12},{6,14},{1,9},{3,11},{5,13},{7,15},{16,24},{18,... | collective-permute-start | bytes 786440 | tf_op jit(solution)/shard_map/ppermute | solution.py:25
  191.9 13.5 %collective-permute-start.19 = (bf16[128,1024]{1,0:T(8,128)(2,1)}, bf16[128,1024]{1,0:T(8,128)(2,1)S(1)}, u32[]{:S(2)}, u32[]{:S(2)}) collective-permute-start(bf16[128,1024]{1,0:T(8,128)(2,1)} %fusion.24), channel_id=1, source_target_pairs={{0,6},{2,8},{4,10},{6,12},{8,14},{1,7},{3,9},{5,11},{7,13},{9,15},... | collective-permute-start | bytes 786440 | tf_op jit(solution)/shard_map/ppermute | solution.py:25
  195.1 15.4 %collective-permute-start.20 = (bf16[128,1024]{1,0:T(8,128)(2,1)}, bf16[128,1024]{1,0:T(8,128)(2,1)S(1)}, u32[]{:S(2)}, u32[]{:S(2)}) collective-permute-start(bf16[128,1024]{1,0:T(8,128)(2,1)} %fusion.24), channel_id=1, source_target_pairs={{0,4},{2,6},{4,8},{6,10},{8,12},{10,14},{1,5},{3,7},{5,9},{7,11},{... | collective-permute-start | bytes 786440 | tf_op jit(solution)/shard_map/ppermute | solution.py:25
  197.4 13.1 %collective-permute-start.21 = (bf16[128,1024]{1,0:T(8,128)(2,1)}, bf16[128,1024]{1,0:T(8,128)(2,1)S(1)}, u32[]{:S(2)}, u32[]{:S(2)}) collective-permute-start(bf16[128,1024]{1,0:T(8,128)(2,1)} %fusion.24), channel_id=1, source_target_pairs={{0,2},{2,4},{4,6},{6,8},{8,10},{10,12},{12,14},{1,3},{3,5},{5,7},{... | collective-permute-start | bytes 786440 | tf_op jit(solution)/shard_map/ppermute | solution.py:25
  212.1 5.3 %slice-start = ((s8[8388608]{0:T(1024)(128)(4,1)}), s8[4194304]{0:T(1024)(128)(4,1)S(1)}, s32[]{:S(2)}) async-start(s8[8388608]{0:T(1024)(128)(4,1)} %bitcast.128), calls=%async_computation.3 | async-start | bytes 8388608
  212.5 5.6 %slice-start.1 = ((s8[8388608]{0:T(1024)(128)(4,1)}), s8[4194304]{0:T(1024)(128)(4,1)S(1)}, s32[]{:S(2)}) async-start(s8[8388608]{0:T(1024)(128)(4,1)} %bitcast.128), calls=%async_computation.4 | async-start | bytes 8388608
  219.9 3.5 %copy-start.2 = (bf16[8,2,128,1024]{2,3,1,0:T(8,128)(2,1)}, bf16[8,2,128,1024]{2,3,1,0:T(8,128)(2,1)S(1)}, u32[]{:S(2)}) copy-start(bf16[8,2,128,1024]{2,3,1,0:T(8,128)(2,1)S(1)} %fusion.3) | copy-start | bytes 12582916
  223.4 7.5 %copy-start.6 = (bf16[128,1024]{0,1:T(8,128)(2,1)S(1)}, bf16[128,1024]{0,1:T(8,128)(2,1)}, u32[]{:S(2)}) copy-start(bf16[128,1024]{0,1:T(8,128)(2,1)} %copy-done.4) | copy-start | bytes 786436
  226.6 20.1 %collective-permute-start.28 = (bf16[128,1024]{1,0:T(8,128)(2,1)}, bf16[128,1024]{1,0:T(8,128)(2,1)}, u32[]{:S(2)}, u32[]{:S(2)}) collective-permute-start(bf16[128,1024]{1,0:T(8,128)(2,1)} %copy.87), channel_id=1, source_target_pairs={{14,0},{15,1},{30,16},{31,17}} | collective-permute-start | bytes 786440 | tf_op jit(solution)/shard_map/ppermute | solution.py:25
  229.7 18.4 %collective-permute-start.27 = (bf16[128,1024]{1,0:T(8,128)(2,1)}, bf16[128,1024]{1,0:T(8,128)(2,1)}, u32[]{:S(2)}, u32[]{:S(2)}) collective-permute-start(bf16[128,1024]{1,0:T(8,128)(2,1)} %copy.86), channel_id=1, source_target_pairs={{12,0},{14,2},{13,1},{15,3},{28,16},{30,18},{29,17},{31,19}} | collective-permute-start | bytes 786440 | tf_op jit(solution)/shard_map/ppermute | solution.py:25
  238.5 33.7 %collective-permute-start.26 = (bf16[128,1024]{1,0:T(8,128)(2,1)}, bf16[128,1024]{1,0:T(8,128)(2,1)}, u32[]{:S(2)}, u32[]{:S(2)}) collective-permute-start(bf16[128,1024]{1,0:T(8,128)(2,1)} %copy.85), channel_id=1, source_target_pairs={{10,0},{12,2},{14,4},{11,1},{13,3},{15,5},{26,16},{28,18},{30,20},... | collective-permute-start | bytes 786440 | tf_op jit(solution)/shard_map/ppermute | solution.py:25
  241.6 34.8 %collective-permute-start.25 = (bf16[128,1024]{1,0:T(8,128)(2,1)}, bf16[128,1024]{1,0:T(8,128)(2,1)}, u32[]{:S(2)}, u32[]{:S(2)}) collective-permute-start(bf16[128,1024]{1,0:T(8,128)(2,1)} %copy.84), channel_id=1, source_target_pairs={{8,0},{10,2},{12,4},{14,6},{9,1},{11,3},{13,5},{15,7},{24,16},{26,... | collective-permute-start | bytes 786440 | tf_op jit(solution)/shard_map/ppermute | solution.py:25
  243.7 34.2 %collective-permute-start.24 = (bf16[128,1024]{1,0:T(8,128)(2,1)}, bf16[128,1024]{1,0:T(8,128)(2,1)}, u32[]{:S(2)}, u32[]{:S(2)}) collective-permute-start(bf16[128,1024]{1,0:T(8,128)(2,1)} %copy.83), channel_id=1, source_target_pairs={{6,0},{8,2},{10,4},{12,6},{14,8},{7,1},{9,3},{11,5},{13,7},{15,9},... | collective-permute-start | bytes 786440 | tf_op jit(solution)/shard_map/ppermute | solution.py:25
  246.7 31.3 %collective-permute-start.23 = (bf16[128,1024]{1,0:T(8,128)(2,1)}, bf16[128,1024]{1,0:T(8,128)(2,1)}, u32[]{:S(2)}, u32[]{:S(2)}) collective-permute-start(bf16[128,1024]{1,0:T(8,128)(2,1)} %copy.82), channel_id=1, source_target_pairs={{4,0},{6,2},{8,4},{10,6},{12,8},{14,10},{5,1},{7,3},{9,5},{11,7},{... | collective-permute-start | bytes 786440 | tf_op jit(solution)/shard_map/ppermute | solution.py:25
  248.0 30.0 %collective-permute-start.22 = (bf16[128,1024]{1,0:T(8,128)(2,1)}, bf16[128,1024]{1,0:T(8,128)(2,1)}, u32[]{:S(2)}, u32[]{:S(2)}) collective-permute-start(bf16[128,1024]{1,0:T(8,128)(2,1)} %copy.80), channel_id=1, source_target_pairs={{2,0},{4,2},{6,4},{8,6},{10,8},{12,10},{14,12},{3,1},{5,3},{7,5},{... | collective-permute-start | bytes 786440 | tf_op jit(solution)/shard_map/ppermute | solution.py:25
  253.4 41.8 %copy-start.1 = (bf16[1,128,2688]{2,1,0:T(8,128)(2,1)S(1)}, bf16[1,128,2688]{2,1,0:T(8,128)(2,1)}, u32[]{:S(2)}) copy-start(bf16[1,128,2688]{2,1,0:T(8,128)(2,1)} %param.10) | copy-start | bytes 2064388
  (3 other events, 5.0 us)
Sparse Core Ops, SparseCore 0:
  11.6 81.1 all-gather.2
  94.4 14.1 all-gather.4
Sparse Core Ops, SparseCore 1:
  186.2 105.9 all-reduce.3

commit v2 on v1

--- a/solution.py
+++ b/solution.py
@@ -75,11 +75,11 @@
     key_blocks = []
     value_blocks = []
     for distance in range(halo_blocks, 0, -1):
-        got_keys, got_values = shifted((own_keys, values), "ctx", distance)
-        key_blocks.append(got_keys)
-        value_blocks.append(got_values)
+        key_blocks.append(shifted(own_keys, "ctx", distance))
+        value_blocks.append(shifted(values, "ctx", distance))
     all_keys = jnp.concatenate(key_blocks + [own_keys], 0)
-    all_values = jnp.concatenate(value_blocks + [values], 0)
+    all_keys, own_values = lax.optimization_barrier((all_keys, values))
+    all_values = jnp.concatenate(value_blocks + [own_values], 0)
     span = all_keys.shape[0]
     tpos = ctx_index * tok_rows + jnp.arange(tok_rows, dtype=jnp.int32)
     upos = ctx_index * tok_rows - halo_blocks * tok_rows + jnp.arange(span, dtype=jnp.int32)

time: 305 us -> 363 us (1.19)
  waiting for transfers between devices: 96.3 us -> 181 us
  blocking collectives: 43.1 us -> 31.5 us
  starting transfers between devices: 68.5 us -> 59.2 us
  other arithmetic: 10.7 us -> 5.3 us
  matrix products: 28 us -> 32 us
    psum x1, waiting for transfers between devices: 11.7 us -> 81.7 us  [shards(): lax.psum((down_factor, up_factor), ('ctx', 'pair'))]
    all_gather x1, waiting for transfers between devices: 21.7 us -> 60.4 us  [shards(): rows_half = lax.all_gather(own_half, 'ctx', axis=0, tiled=True)]
    ppermute x28, waiting for transfers between devices: 62.8 us -> 38.7 us  [shifted(): return lax.ppermute(block, axis, route)]
    psum x1, blocking collectives: 43.1 us -> 31.5 us  [shards(): own_diff, counts = lax.psum((part_diff, part_count), 'ctx')]
    ppermute x28, starting transfers between devices: 68.3 us -> 59.1 us  [shifted(): return lax.ppermute(block, axis, route)]
    sub x0 -> x1, matrix products: none -> 6.9 us  [shards(): weights_exp = jnp.where(allowed[None, None], jnp.exp(masked - row_max), 0.0)]
    concatenate x9 -> x1, local copies, waits for them, and re-layouts: 6.83 us -> 0.97 us  [shards(): all_keys = jnp.concatenate(key_blocks + [own_keys], 0)]
    sub x1 -> x0, other arithmetic: 4.31 us -> none  [shards(): weights_exp = jnp.where(allowed[None, None], jnp.exp(masked - row_max), 0.0)]
  transfers between devices with their start and end apart: 32 -> 32, of which waited for: 11 -> 9; matrix products, arithmetic and copies ran while one was open for 22% -> 16% of each run, Pallas kernels for 0% -> 0%
where the time goes in v2:
time: 363 us; the launch traced here: 361 us
  waiting for transfers between devices  181 us (50%)
  starting transfers between devices  59.2 us (16%)
  local copies, waits for them, and re-layouts  37.7 us (10%)
  matrix products  32 us (9%)
  blocking collectives  31.5 us (9%)
  between operations  14.4 us (4%)
  other arithmetic  5.3 us (1%)
    psum x1, waiting for transfers between devices, shards(): lax.psum((down_factor, up_factor), ('ctx', 'pair'))  81.7 us
    all_gather x1, waiting for transfers between devices, shards(): rows_half = lax.all_gather(own_half, 'ctx', axis=0, tiled=True)  60.4 us
    ppermute x28, starting transfers between devices, shifted(): return lax.ppermute(block, axis, route)  59.1 us
    ppermute x28, waiting for transfers between devices, shifted(): return lax.ppermute(block, axis, route)  38.7 us
    psum x1, blocking collectives, shards(): own_diff, counts = lax.psum((part_diff, part_count), 'ctx')  31.5 us
    unnamed x48, local copies, waits for them, and re-layouts  17.1 us
    convert_element_type x7, local copies, waits for them, and re-layouts, shards(): key_parts[block_start:block_start + tok_rows].astype(jnp.bfloat16)  8.84 us
  transfers between devices with their start and end apart: 32, of which 9 were waited for; matrix products, arithmetic and copies ran while one was open for 16% of the time, Pallas kernels for 0%

profile of v2, /device:TPU:0, one launch (start us, length us, event | category | flops | bytes accessed | tf_op | source)
XLA Modules:
  0.0 361.0 jit_solution(16586474015925666652)
XLA Ops:
  7.3 1.8 constant_dynamic-slice_fusion
  9.2 60.4 %all-gather.3.cloned.1.call-done = bf16[2688,512]{1,0:T(8,128)(2,1)} async-done(((bf16[336,512]{1,0:T(8,128)(2,1)}), bf16[2688,512]{1,0:T(8,128)(2,1)}) %all-gather.3.cloned.1.call-update) | async-done | bytes 2752528 | tf_op jit(solution)/shard_map/all_gather | solution.py:50
  69.7 3.8 %collective-permute-start = (bf16[128,1024]{1,0:T(8,128)(2,1)}, bf16[128,1024]{1,0:T(8,128)(2,1)S(1)}, u32[]{:S(2)}, u32[]{:S(2)}) collective-permute-start(bf16[128,1024]{1,0:T(8,128)(2,1)} %bitcast.3), channel_id=1, source_target_pairs={{0,14},{1,15},{16,30},{17,31}} | collective-permute-start | bytes 786440 | tf_op jit(solution)/shard_map/ppermute | solution.py:25
  73.5 2.0 collective-permute-start.1
  75.5 2.0 collective-permute-start.2
  77.5 2.0 collective-permute-start.3
  79.7 31.5 %all-reduce.1 = (f32[8]{0:T(128)S(1)}, f32[8]{0:T(128)S(1)}) all-reduce(f32[8]{0:T(128)S(1)} %get-tuple-element.21, f32[8]{0:T(128)S(1)} %get-tuple-element.22), channel_id=1, replica_groups=mesh['grp'=2,'ctx'=8,'pair'=2] {'ctx'}, use_global_device_ids=true, to_apply=%region_1.0 | all-reduce | flops 16 | bytes 128 | tf_op jit(solution)/shard_map/psum | solution.py:66
  113.1 1.4 collective-permute-start.4
  116.2 2.1 collective-permute-start.5
  119.3 3.0 collective-permute-start.6
  125.3 1.6 collective-permute-done.5
  126.9 1.3 collective-permute-done.6
  129.3 4.2 %convolution_bitcast_fusion.1 = f32[128,1024]{0,1:T(8,128)S(1)} fusion(bf16[2688,1024]{1,0:T(8,128)(2,1)} %all-gather.5.cloned.1.call-done, bf16[1,128,2688]{2,1,0:T(8,128)(2,1)S(1)} %copy-done), kind=kOutput, calls=%fused_computation.26 | convolution fusion | flops 704643072 | bytes 6717440 | tf_op jit(solution)/shard_map/dot_general | solution.py:56
  134.5 7.0 %collective-permute-start.15 = (bf16[128,1024]{0,1:T(8,128)(2,1)}, bf16[128,1024]{0,1:T(8,128)(2,1)}, u32[]{:S(2)}, u32[]{:S(2)}) collective-permute-start(bf16[128,1024]{0,1:T(8,128)(2,1)} %fusion.15), channel_id=1, source_target_pairs={{0,14},{1,15},{16,30},{17,31}} | collective-permute-start | bytes 786440 | tf_op jit(solution)/shard_map/ppermute | solution.py:25
  141.5 6.5 %collective-permute-start.16 = (bf16[128,1024]{0,1:T(8,128)(2,1)}, bf16[128,1024]{0,1:T(8,128)(2,1)}, u32[]{:S(2)}, u32[]{:S(2)}) collective-permute-start(bf16[128,1024]{0,1:T(8,128)(2,1)} %fusion.15), channel_id=1, source_target_pairs={{0,12},{2,14},{1,13},{3,15},{16,28},{18,30},{17,29},{19,31}} | collective-permute-start | bytes 786440 | tf_op jit(solution)/shard_map/ppermute | solution.py:25
  148.0 2.0 collective-permute-start.17
  150.0 2.9 collective-permute-start.18
  152.9 2.0 collective-permute-start.19
  154.9 2.0 copy.71
  156.9 3.2 copy.60
  160.1 6.9 %fusion.36 = (f32[8,2,128]{2,1,0:T(2,128)S(1)}, f32[8,2,128,1024]{2,3,1,0:T(8,128)}) fusion(pred[128,1024]{0,1:T(8,128)(4,1)} %compare_and_fusion, bf16[1024,8,128,1]{0,2,3,1:T(8,128)(2,1)S(1)} %copy.60, bf16[128,8,2,128]{0,3,2,1:T(8,128)(2,1)S(1)} %bitcast.126), kind=kOutput, calls=%fused_computation.82 | convolution fusion | flops 547357696 | bytes 11149312 | tf_op jit(solution)/shard_map/sub | solution.py:101
  167.0 5.1 %fusion.37 = (bf16[1024,8,128]{0,2,1:T(8,128)(2,1)S(1)}, f32[1024,8,128]{0,2,1:T(8,128)S(1)}) fusion(bf16[128,8,2,128]{3,2,1,0:T(2,128)(2,1)} %reshape_squeeze.7, f32[128]{0:T(128)S(1)} %get-tuple-element.20, f32[8,2,128,1024]{2,3,1,0:T(8,128)} %get-tuple-element.42, f32[8,2,128]{2,1,0:T(2,128)S(1)} %get-tuple-element.41), kind=kOutput, calls=%fused_computation.83 | convolution fusion | flops 544210944 | bytes 15213056 | tf_op jit(solution)/shard_map/jgtl,tjgd->ljd/dot_general | solution.py:115
  172.8 1.4 collective-permute-start.20
  175.2 2.7 collective-permute-start.21
  179.0 1.3 collective-permute-start.14
  181.3 1.3 collective-permute-start.13
  183.7 1.3 collective-permute-start.12
  187.4 1.5 collective-permute-start.10
  190.1 1.9 fusion.1
  192.0 1.7 fusion.3
  193.8 1.6 convolution_convert_fusion
  198.0 3.5 fusion.38
  201.5 12.4 %collective-permute-done.12 = bf16[128,1024]{0,1:T(8,128)(2,1)S(1)} collective-permute-done((bf16[128,1024]{0,1:T(8,128)(2,1)S(1)}, bf16[128,1024]{0,1:T(8,128)(2,1)S(1)}, u32[]{:S(2)}, u32[]{:S(2)}) %collective-permute-start.12) | collective-permute-done | bytes 262176 | tf_op jit(solution)/shard_map/ppermute | solution.py:25
  213.9 1.5 collective-permute-done.11
  216.7 2.0 copy.54
  218.7 1.4 fusion.34
  220.1 1.9 copy.53
  223.3 1.8 copy.52
  226.4 1.8 copy.51
  239.3 1.3 collective-permute-start.22
  240.6 5.3 %fusion.11 = bf16[1,128,2688]{2,1,0:T(8,128)(2,1)} fusion(f32[128,2688]{1,0:T(8,128)S(1)} %convolution_multiply_fusion, bf16[128,1024]{0,1:T(8,128)(2,1)S(1)} %fusion.27, bf16[2688,1024]{1,0:T(8,128)(2,1)} %all-gather.5.cloned.1.call-done), kind=kOutput, calls=%fused_computation.19 | convolution fusion | flops 705331200 | bytes 7831552 | tf_op jit(solution)/shard_map/tk,dk->td/dot_general | solution.py:133
  246.0 10.0 %collective-permute-done.26 = bf16[128,1024]{1,0:T(8,128)(2,1)S(1)} collective-permute-done((bf16[128,1024]{1,0:T(8,128)(2,1)}, bf16[128,1024]{1,0:T(8,128)(2,1)S(1)}, u32[]{:S(2)}, u32[]{:S(2)}) %collective-permute-start.26) | collective-permute-done | bytes 262176 | tf_op jit(solution)/shard_map/ppermute | solution.py:25
  256.0 3.9 %collective-permute-done.25 = bf16[128,1024]{1,0:T(8,128)(2,1)S(1)} collective-permute-done((bf16[128,1024]{1,0:T(8,128)(2,1)}, bf16[128,1024]{1,0:T(8,128)(2,1)S(1)}, u32[]{:S(2)}, u32[]{:S(2)}) %collective-permute-start.25) | collective-permute-done | bytes 262176 | tf_op jit(solution)/shard_map/ppermute | solution.py:25
  260.0 7.8 %collective-permute-done.24 = bf16[128,1024]{1,0:T(8,128)(2,1)} collective-permute-done((bf16[128,1024]{1,0:T(8,128)(2,1)}, bf16[128,1024]{1,0:T(8,128)(2,1)}, u32[]{:S(2)}, u32[]{:S(2)}) %collective-permute-start.24) | collective-permute-done | bytes 262176 | tf_op jit(solution)/shard_map/ppermute | solution.py:25
  267.8 2.0 fusion.31
  269.7 81.7 %all-reduce.4.cloned.1.call-done = (f32[2688,16]{0,1:T(8,128)}, f32[16,1024]{1,0:T(8,128)}) async-done(((f32[2688,16]{0,1:T(8,128)}, f32[16,1024]{1,0:T(8,128)}), (f32[2688,16]{0,1:T(8,128)}, f32[16,1024]{1,0:T(8,128)})) %all-reduce.4.cloned.1.call-update) | async-done | bytes 237584 | tf_op jit(solution)/shard_map/psum | solution.py:143
  351.4 1.6 copy.96
  353.0 1.5 copy.97
  (113 shorter events, 35.6 us)
Async XLA Ops:
  7.2 105.7 %copy-start = (bf16[1,128,2688]{2,1,0:T(8,128)(2,1)S(1)}, bf16[1,128,2688]{2,1,0:T(8,128)(2,1)}, u32[]{:S(2)}) copy-start(bf16[1,128,2688]{2,1,0:T(8,128)(2,1)} %param.10) | copy-start | bytes 2064388
  7.2 72.3 %copy-start.11 = (f32[1,128]{1,0:T(1,128)S(1)}, f32[1,128]{1,0:T(1,128)}, u32[]{:S(2)}) copy-start(f32[1,128]{1,0:T(1,128)} %param.17) | copy-start | bytes 1540
  7.2 72.3 %copy-start.12 = (f32[1,128]{1,0:T(1,128)S(1)}, f32[1,128]{1,0:T(1,128)}, u32[]{:S(2)}) copy-start(f32[1,128]{1,0:T(1,128)} %param.18) | copy-start | bytes 1540
  7.2 72.3 %copy-start.10 = (s32[1,128]{1,0:T(1,128)S(1)}, s32[1,128]{1,0:T(1,128)}, u32[]{:S(2)}) copy-start(s32[1,128]{1,0:T(1,128)} %param.19) | copy-start | bytes 1540
  7.2 104.0 %copy-start.4 = (bf16[1,128,2048]{2,1,0:T(8,128)(2,1)S(1)}, bf16[1,128,2048]{2,1,0:T(8,128)(2,1)}, u32[]{:S(2)}) copy-start(bf16[1,128,2048]{2,1,0:T(8,128)(2,1)} %param.16) | copy-start | bytes 1572868
  7.2 62.4 %all-gather.3.cloned.1.call-start = ((), (), s32[]{:S(2)}) async-start(), calls=%async_computation | async-start | bytes 3096576 | tf_op jit(solution)/shard_map/all_gather | solution.py:50
  9.1 103.3 %copy-start.5 = (bf16[1,128,2048]{2,1,0:T(8,128)(2,1)S(1)}, bf16[1,128,2048]{2,1,0:T(8,128)(2,1)}, u32[]{:S(2)}) copy-start(bf16[1,128,2048]{2,1,0:T(8,128)(2,1)} %param.11) | copy-start | bytes 1572868
  9.1 120.1 %all-gather.5.cloned.1.call-start = ((), (), s32[]{:S(2)}) async-start(), calls=%async_computation.1 | async-start | bytes 8257536 | tf_op jit(solution)/shard_map/all_gather | solution.py:51
  69.6 43.3 %copy-start.7 = (bf16[2688,16]{0,1:T(8,128)(2,1)S(1)}, bf16[2688,16]{0,1:T(8,128)(2,1)}, u32[]{:S(2)}) copy-start(bf16[2688,16]{0,1:T(8,128)(2,1)} %param.14) | copy-start | bytes 258052
  69.6 281.8 %all-reduce.4.cloned.1.call-start = ((), (), s32[]{:S(2)}) async-start(), calls=%async_computation.2 | async-start | bytes 475136 | tf_op jit(solution)/shard_map/psum | solution.py:143
  69.7 45.8 %collective-permute-start = (bf16[128,1024]{1,0:T(8,128)(2,1)}, bf16[128,1024]{1,0:T(8,128)(2,1)S(1)}, u32[]{:S(2)}, u32[]{:S(2)}) collective-permute-start(bf16[128,1024]{1,0:T(8,128)(2,1)} %bitcast.3), channel_id=1, source_target_pairs={{0,14},{1,15},{16,30},{17,31}} | collective-permute-start | bytes 786440 | tf_op jit(solution)/shard_map/ppermute | solution.py:25
  73.5 45.8 %collective-permute-start.1 = (bf16[128,1024]{1,0:T(8,128)(2,1)}, bf16[128,1024]{1,0:T(8,128)(2,1)}, u32[]{:S(2)}, u32[]{:S(2)}) collective-permute-start(bf16[128,1024]{1,0:T(8,128)(2,1)} %bitcast.3), channel_id=1, source_target_pairs={{0,12},{2,14},{1,13},{3,15},{16,28},{18,30},{17,29},{19,31}} | collective-permute-start | bytes 786440 | tf_op jit(solution)/shard_map/ppermute | solution.py:25
  75.5 47.8 %collective-permute-start.2 = (bf16[128,1024]{1,0:T(8,128)(2,1)}, bf16[128,1024]{1,0:T(8,128)(2,1)}, u32[]{:S(2)}, u32[]{:S(2)}) collective-permute-start(bf16[128,1024]{1,0:T(8,128)(2,1)} %bitcast.3), channel_id=1, source_target_pairs={{0,10},{2,12},{4,14},{1,11},{3,13},{5,15},{16,26},{18,28},{20,30},... | collective-permute-start | bytes 786440 | tf_op jit(solution)/shard_map/ppermute | solution.py:25
  77.5 46.8 %collective-permute-start.3 = (bf16[128,1024]{1,0:T(8,128)(2,1)}, bf16[128,1024]{1,0:T(8,128)(2,1)}, u32[]{:S(2)}, u32[]{:S(2)}) collective-permute-start(bf16[128,1024]{1,0:T(8,128)(2,1)} %bitcast.3), channel_id=1, source_target_pairs={{0,8},{2,10},{4,12},{6,14},{1,9},{3,11},{5,13},{7,15},{16,24},{18,... | collective-permute-start | bytes 786440 | tf_op jit(solution)/shard_map/ppermute | solution.py:25
  111.1 2.0 collective-permute-start.7
  113.1 12.1 %collective-permute-start.4 = (bf16[128,1024]{1,0:T(8,128)(2,1)}, bf16[128,1024]{1,0:T(8,128)(2,1)S(1)}, u32[]{:S(2)}, u32[]{:S(2)}) collective-permute-start(bf16[128,1024]{1,0:T(8,128)(2,1)} %bitcast.3), channel_id=1, source_target_pairs={{0,6},{2,8},{4,10},{6,12},{8,14},{1,7},{3,9},{5,11},{7,13},{9,15},... | collective-permute-start | bytes 786440 | tf_op jit(solution)/shard_map/ppermute | solution.py:25
  115.5 0.7 copy-start.8
  116.2 10.7 %collective-permute-start.5 = (bf16[128,1024]{1,0:T(8,128)(2,1)}, bf16[128,1024]{1,0:T(8,128)(2,1)S(1)}, u32[]{:S(2)}, u32[]{:S(2)}) collective-permute-start(bf16[128,1024]{1,0:T(8,128)(2,1)} %bitcast.3), channel_id=1, source_target_pairs={{0,4},{2,6},{4,8},{6,10},{8,12},{10,14},{1,5},{3,7},{5,9},{7,11},{... | collective-permute-start | bytes 786440 | tf_op jit(solution)/shard_map/ppermute | solution.py:25
  119.3 9.0 %collective-permute-start.6 = (bf16[128,1024]{1,0:T(8,128)(2,1)}, bf16[128,1024]{1,0:T(8,128)(2,1)S(1)}, u32[]{:S(2)}, u32[]{:S(2)}) collective-permute-start(bf16[128,1024]{1,0:T(8,128)(2,1)} %bitcast.3), channel_id=1, source_target_pairs={{0,2},{2,4},{4,6},{6,8},{8,10},{10,12},{12,14},{1,3},{3,5},{5,7},{... | collective-permute-start | bytes 786440 | tf_op jit(solution)/shard_map/ppermute | solution.py:25
  129.2 4.2 %copy-start.9 = (bf16[16,1024]{1,0:T(8,128)(2,1)S(1)}, bf16[16,1024]{1,0:T(8,128)(2,1)}, u32[]{:S(2)}) copy-start(bf16[16,1024]{1,0:T(8,128)(2,1)} %param.15) | copy-start | bytes 98308
  134.5 38.3 %collective-permute-start.15 = (bf16[128,1024]{0,1:T(8,128)(2,1)}, bf16[128,1024]{0,1:T(8,128)(2,1)}, u32[]{:S(2)}, u32[]{:S(2)}) collective-permute-start(bf16[128,1024]{0,1:T(8,128)(2,1)} %fusion.15), channel_id=1, source_target_pairs={{0,14},{1,15},{16,30},{17,31}} | collective-permute-start | bytes 786440 | tf_op jit(solution)/shard_map/ppermute | solution.py:25
  141.5 33.7 %collective-permute-start.16 = (bf16[128,1024]{0,1:T(8,128)(2,1)}, bf16[128,1024]{0,1:T(8,128)(2,1)}, u32[]{:S(2)}, u32[]{:S(2)}) collective-permute-start(bf16[128,1024]{0,1:T(8,128)(2,1)} %fusion.15), channel_id=1, source_target_pairs={{0,12},{2,14},{1,13},{3,15},{16,28},{18,30},{17,29},{19,31}} | collective-permute-start | bytes 786440 | tf_op jit(solution)/shard_map/ppermute | solution.py:25
  148.0 30.9 %collective-permute-start.17 = (bf16[128,1024]{0,1:T(8,128)(2,1)}, bf16[128,1024]{0,1:T(8,128)(2,1)}, u32[]{:S(2)}, u32[]{:S(2)}) collective-permute-start(bf16[128,1024]{0,1:T(8,128)(2,1)} %fusion.15), channel_id=1, source_target_pairs={{0,10},{2,12},{4,14},{1,11},{3,13},{5,15},{16,26},{18,28},{20,30},... | collective-permute-start | bytes 786440 | tf_op jit(solution)/shard_map/ppermute | solution.py:25
  150.0 31.3 %collective-permute-start.18 = (bf16[128,1024]{0,1:T(8,128)(2,1)}, bf16[128,1024]{0,1:T(8,128)(2,1)}, u32[]{:S(2)}, u32[]{:S(2)}) collective-permute-start(bf16[128,1024]{0,1:T(8,128)(2,1)} %fusion.15), channel_id=1, source_target_pairs={{0,8},{2,10},{4,12},{6,14},{1,9},{3,11},{5,13},{7,15},{16,24},{18,... | collective-permute-start | bytes 786440 | tf_op jit(solution)/shard_map/ppermute | solution.py:25
  152.9 30.8 %collective-permute-start.19 = (bf16[128,1024]{0,1:T(8,128)(2,1)}, bf16[128,1024]{0,1:T(8,128)(2,1)}, u32[]{:S(2)}, u32[]{:S(2)}) collective-permute-start(bf16[128,1024]{0,1:T(8,128)(2,1)} %fusion.15), channel_id=1, source_target_pairs={{0,6},{2,8},{4,10},{6,12},{8,14},{1,7},{3,9},{5,11},{7,13},{9,15},... | collective-permute-start | bytes 786440 | tf_op jit(solution)/shard_map/ppermute | solution.py:25
  167.0 23.0 %slice-start = ((s8[8388608]{0:T(1024)(128)(4,1)}), s8[4194304]{0:T(1024)(128)(4,1)S(1)}, s32[]{:S(2)}) async-start(s8[8388608]{0:T(1024)(128)(4,1)} %bitcast.121), calls=%async_computation.3 | async-start | bytes 8388608
  167.0 23.0 %slice-start.1 = ((s8[8388608]{0:T(1024)(128)(4,1)}), s8[4194304]{0:T(1024)(128)(4,1)S(1)}, s32[]{:S(2)}) async-start(s8[8388608]{0:T(1024)(128)(4,1)} %bitcast.121), calls=%async_computation.4 | async-start | bytes 8388608
  172.7 17.3 %copy-start.6 = (bf16[128,8,2,128]{3,2,1,0:T(2,128)(2,1)S(1)}, bf16[128,8,2,128]{3,2,1,0:T(2,128)(2,1)}, u32[]{:S(2)}) copy-start(bf16[128,8,2,128]{3,2,1,0:T(2,128)(2,1)} %reshape_squeeze.7) | copy-start | bytes 1572868
  172.8 13.3 %collective-permute-start.20 = (bf16[128,1024]{0,1:T(8,128)(2,1)}, bf16[128,1024]{0,1:T(8,128)(2,1)S(1)}, u32[]{:S(2)}, u32[]{:S(2)}) collective-permute-start(bf16[128,1024]{0,1:T(8,128)(2,1)} %fusion.15), channel_id=1, source_target_pairs={{0,4},{2,6},{4,8},{6,10},{8,12},{10,14},{1,5},{3,7},{5,9},{7,11},{... | collective-permute-start | bytes 786440 | tf_op jit(solution)/shard_map/ppermute | solution.py:25
  175.2 12.2 %collective-permute-start.21 = (bf16[128,1024]{0,1:T(8,128)(2,1)}, bf16[128,1024]{0,1:T(8,128)(2,1)S(1)}, u32[]{:S(2)}, u32[]{:S(2)}) collective-permute-start(bf16[128,1024]{0,1:T(8,128)(2,1)} %fusion.15), channel_id=1, source_target_pairs={{0,2},{2,4},{4,6},{6,8},{8,10},{10,12},{12,14},{1,3},{3,5},{5,7},{... | collective-permute-start | bytes 786440 | tf_op jit(solution)/shard_map/ppermute | solution.py:25
  179.0 16.4 %collective-permute-start.14 = (bf16[128,1024]{0,1:T(8,128)(2,1)S(1)}, bf16[128,1024]{0,1:T(8,128)(2,1)S(1)}, u32[]{:S(2)}, u32[]{:S(2)}) collective-permute-start(bf16[128,1024]{0,1:T(8,128)(2,1)S(1)} %bitcast.141), channel_id=1, source_target_pairs={{14,0},{15,1},{30,16},{31,17}} | collective-permute-start | bytes 786440 | tf_op jit(solution)/shard_map/ppermute | solution.py:25
  181.3 15.4 %collective-permute-start.13 = (bf16[128,1024]{0,1:T(8,128)(2,1)S(1)}, bf16[128,1024]{0,1:T(8,128)(2,1)S(1)}, u32[]{:S(2)}, u32[]{:S(2)}) collective-permute-start(bf16[128,1024]{0,1:T(8,128)(2,1)S(1)} %bitcast.140), channel_id=1, source_target_pairs={{12,0},{14,2},{13,1},{15,3},{28,16},{30,18},{29,17},{31,19}} | collective-permute-start | bytes 786440 | tf_op jit(solution)/shard_map/ppermute | solution.py:25
  183.7 30.2 %collective-permute-start.12 = (bf16[128,1024]{0,1:T(8,128)(2,1)S(1)}, bf16[128,1024]{0,1:T(8,128)(2,1)S(1)}, u32[]{:S(2)}, u32[]{:S(2)}) collective-permute-start(bf16[128,1024]{0,1:T(8,128)(2,1)S(1)} %bitcast.139), channel_id=1, source_target_pairs={{10,0},{12,2},{14,4},{11,1},{13,3},{15,5},{26,16},{28,18},{30,20},... | collective-permute-start | bytes 786440 | tf_op jit(solution)/shard_map/ppermute | solution.py:25
  186.0 29.4 %collective-permute-start.11 = (bf16[128,1024]{0,1:T(8,128)(2,1)S(1)}, bf16[128,1024]{0,1:T(8,128)(2,1)S(1)}, u32[]{:S(2)}, u32[]{:S(2)}) collective-permute-start(bf16[128,1024]{0,1:T(8,128)(2,1)S(1)} %bitcast.138), channel_id=1, source_target_pairs={{8,0},{10,2},{12,4},{14,6},{9,1},{11,3},{13,5},{15,7},{24,16},{26,... | collective-permute-start | bytes 786440 | tf_op jit(solution)/shard_map/ppermute | solution.py:25
  187.4 28.0 %collective-permute-start.10 = (bf16[128,1024]{0,1:T(8,128)(2,1)S(1)}, bf16[128,1024]{0,1:T(8,128)(2,1)S(1)}, u32[]{:S(2)}, u32[]{:S(2)}) collective-permute-start(bf16[128,1024]{0,1:T(8,128)(2,1)S(1)} %bitcast.137), channel_id=1, source_target_pairs={{6,0},{8,2},{10,4},{12,6},{14,8},{7,1},{9,3},{11,5},{13,7},{15,9},... | collective-permute-start | bytes 786440 | tf_op jit(solution)/shard_map/ppermute | solution.py:25
  195.4 20.0 %collective-permute-start.9 = (bf16[128,1024]{0,1:T(8,128)(2,1)S(1)}, bf16[128,1024]{0,1:T(8,128)(2,1)S(1)}, u32[]{:S(2)}, u32[]{:S(2)}) collective-permute-start(bf16[128,1024]{0,1:T(8,128)(2,1)S(1)} %bitcast.136), channel_id=1, source_target_pairs={{4,0},{6,2},{8,4},{10,6},{12,8},{14,10},{5,1},{7,3},{9,5},{11,7},{... | collective-permute-start | bytes 786440 | tf_op jit(solution)/shard_map/ppermute | solution.py:25
  196.7 18.7 %collective-permute-start.8 = (bf16[128,1024]{0,1:T(8,128)(2,1)S(1)}, bf16[128,1024]{0,1:T(8,128)(2,1)S(1)}, u32[]{:S(2)}, u32[]{:S(2)}) collective-permute-start(bf16[128,1024]{0,1:T(8,128)(2,1)S(1)} %bitcast.135), channel_id=1, source_target_pairs={{2,0},{4,2},{6,4},{8,6},{10,8},{12,10},{14,12},{3,1},{5,3},{7,5},{... | collective-permute-start | bytes 786440 | tf_op jit(solution)/shard_map/ppermute | solution.py:25
  220.1 10.2 %copy-start.3 = (bf16[128,8,128]{0,2,1:T(8,128)(2,1)S(1)}, bf16[128,8,128]{0,2,1:T(8,128)(2,1)}, u32[]{:S(2)}) copy-start(bf16[128,8,128]{0,2,1:T(8,128)(2,1)} %get-tuple-element.31) | copy-start | bytes 786436
  220.1 12.4 %copy-start.2 = (bf16[128,8,128]{0,2,1:T(8,128)(2,1)S(1)}, bf16[128,8,128]{0,2,1:T(8,128)(2,1)}, u32[]{:S(2)}) copy-start(bf16[128,8,128]{0,2,1:T(8,128)(2,1)} %get-tuple-element.32) | copy-start | bytes 786436
  220.1 14.5 %copy-start.1 = (bf16[128,8,128]{0,2,1:T(8,128)(2,1)S(1)}, bf16[128,8,128]{0,2,1:T(8,128)(2,1)}, u32[]{:S(2)}) copy-start(bf16[128,8,128]{0,2,1:T(8,128)(2,1)} %get-tuple-element.33) | copy-start | bytes 786436
  222.0 16.0 %collective-permute-start.28 = (bf16[128,1024]{1,0:T(8,128)(2,1)}, bf16[128,1024]{1,0:T(8,128)(2,1)S(1)}, u32[]{:S(2)}, u32[]{:S(2)}) collective-permute-start(bf16[128,1024]{1,0:T(8,128)(2,1)} %copy.53), channel_id=1, source_target_pairs={{14,0},{15,1},{30,16},{31,17}} | collective-permute-start | bytes 786440 | tf_op jit(solution)/shard_map/ppermute | solution.py:25
  225.1 14.2 %collective-permute-start.27 = (bf16[128,1024]{1,0:T(8,128)(2,1)}, bf16[128,1024]{1,0:T(8,128)(2,1)S(1)}, u32[]{:S(2)}, u32[]{:S(2)}) collective-permute-start(bf16[128,1024]{1,0:T(8,128)(2,1)} %copy.52), channel_id=1, source_target_pairs={{12,0},{14,2},{13,1},{15,3},{28,16},{30,18},{29,17},{31,19}} | collective-permute-start | bytes 786440 | tf_op jit(solution)/shard_map/ppermute | solution.py:25
  228.2 27.8 %collective-permute-start.26 = (bf16[128,1024]{1,0:T(8,128)(2,1)}, bf16[128,1024]{1,0:T(8,128)(2,1)S(1)}, u32[]{:S(2)}, u32[]{:S(2)}) collective-permute-start(bf16[128,1024]{1,0:T(8,128)(2,1)} %copy.51), channel_id=1, source_target_pairs={{10,0},{12,2},{14,4},{11,1},{13,3},{15,5},{26,16},{28,18},{30,20},... | collective-permute-start | bytes 786440 | tf_op jit(solution)/shard_map/ppermute | solution.py:25
  231.2 28.7 %collective-permute-start.25 = (bf16[128,1024]{1,0:T(8,128)(2,1)}, bf16[128,1024]{1,0:T(8,128)(2,1)S(1)}, u32[]{:S(2)}, u32[]{:S(2)}) collective-permute-start(bf16[128,1024]{1,0:T(8,128)(2,1)} %copy.50), channel_id=1, source_target_pairs={{8,0},{10,2},{12,4},{14,6},{9,1},{11,3},{13,5},{15,7},{24,16},{26,... | collective-permute-start | bytes 786440 | tf_op jit(solution)/shard_map/ppermute | solution.py:25
  233.4 34.4 %collective-permute-start.24 = (bf16[128,1024]{1,0:T(8,128)(2,1)}, bf16[128,1024]{1,0:T(8,128)(2,1)}, u32[]{:S(2)}, u32[]{:S(2)}) collective-permute-start(bf16[128,1024]{1,0:T(8,128)(2,1)} %copy.49), channel_id=1, source_target_pairs={{6,0},{8,2},{10,4},{12,6},{14,8},{7,1},{9,3},{11,5},{13,7},{15,9},... | collective-permute-start | bytes 786440 | tf_op jit(solution)/shard_map/ppermute | solution.py:25
  238.0 29.7 %collective-permute-start.23 = (bf16[128,1024]{1,0:T(8,128)(2,1)}, bf16[128,1024]{1,0:T(8,128)(2,1)S(1)}, u32[]{:S(2)}, u32[]{:S(2)}) collective-permute-start(bf16[128,1024]{1,0:T(8,128)(2,1)} %copy.48), channel_id=1, source_target_pairs={{4,0},{6,2},{8,4},{10,6},{12,8},{14,10},{5,1},{7,3},{9,5},{11,7},{... | collective-permute-start | bytes 786440 | tf_op jit(solution)/shard_map/ppermute | solution.py:25
  239.3 28.4 %collective-permute-start.22 = (bf16[128,1024]{1,0:T(8,128)(2,1)}, bf16[128,1024]{1,0:T(8,128)(2,1)S(1)}, u32[]{:S(2)}, u32[]{:S(2)}) collective-permute-start(bf16[128,1024]{1,0:T(8,128)(2,1)} %copy.46), channel_id=1, source_target_pairs={{2,0},{4,2},{6,4},{8,6},{10,8},{12,10},{14,12},{3,1},{5,3},{7,5},{... | collective-permute-start | bytes 786440 | tf_op jit(solution)/shard_map/ppermute | solution.py:25
Sparse Core Ops, SparseCore 0:
  10.8 58.7 all-gather.2
  71.1 14.1 all-gather.4
  237.8 113.6 all-reduce.3

commit v3 on v2

--- a/solution.py
+++ b/solution.py
@@ -17,6 +17,20 @@
 
 def from_partner(shard, axis, stride):
     return lax.ppermute(shard, axis, [(i, i ^ 1 << stride) for i in range(lax.axis_size(axis))])
+
+
+def butterfly_sum(parts, axes):
+    for axis in axes:
+        size = lax.axis_size(axis)
+        if size & (size - 1):
+            parts = lax.psum(parts, axis)
+            continue
+        stride = 0
+        while 1 << stride < size:
+            got = from_partner(parts, axis, stride)
+            parts = jax.tree.map(jnp.add, parts, got)
+            stride += 1
+    return parts
 
 
 def shifted(block, axis, distance):
@@ -63,7 +77,7 @@
     log_gap = policy_logprob[0] - reference_logprob[0]
     part_diff = jnp.sum(seg_table * log_gap[:, None], 0)
     part_count = jnp.sum(seg_table, 0)
-    own_diff, counts = lax.psum((part_diff, part_count), "ctx")
+    own_diff, counts = butterfly_sum((part_diff, part_count), ("ctx",))
     other_diff = from_partner(own_diff, "pair", 0)
     direction = 1.0 - 2.0 * pair_index.astype(jnp.float32)
     margin = DPO_BETA * (direction * (own_diff - other_diff))
@@ -140,7 +154,7 @@
     down_factor = ADAPTER_SCALE * jnp.einsum(
         "td,tr->dr", hidden_rows, rank_middle, preferred_element_type=jnp.float32
     )
-    down_gradient, up_gradient = lax.psum((down_factor, up_factor), ("ctx", "pair"))
+    down_gradient, up_gradient = butterfly_sum((down_factor, up_factor), ("pair", "ctx"))
     return (input_grad[None], query_grad[None], key_grad[None], down_gradient, up_gradient)
 
 

time: 363 us -> 316 us (0.87)
  waiting for transfers between devices: 181 us -> 141 us
  blocking collectives: 31.5 us -> 0 us
  starting transfers between devices: 59.2 us -> 88.4 us
  local copies, waits for them, and re-layouts: 37.7 us -> 32.6 us
    psum x1 -> x0, waiting for transfers between devices: 81.7 us -> none  [shards(): lax.psum((down_factor, up_factor), ('ctx', 'pair'))]
    ppermute x1 -> x15, waiting for transfers between devices: 0.01 us -> 44.8 us  [from_partner(): lax.ppermute(shard, axis, [(i, i ^ 1 << stride) for i in range(lax.axis_s...]
    psum x1 -> x0, blocking collectives: 31.5 us -> none  [shards(): own_diff, counts = lax.psum((part_diff, part_count), 'ctx')]
    ppermute x1 -> x15, starting transfers between devices: 0.05 us -> 19.6 us  [from_partner(): lax.ppermute(shard, axis, [(i, i ^ 1 << stride) for i in range(lax.axis_s...]
    ppermute x28, starting transfers between devices: 59.1 us -> 68.7 us  [shifted(): return lax.ppermute(block, axis, route)]
    unnamed x48 -> x44, local copies, waits for them, and re-layouts: 17.1 us -> 9.34 us
  transfers between devices with their start and end apart: 32 -> 45, of which waited for: 9 -> 20; matrix products, arithmetic and copies ran while one was open for 16% -> 18% of each run, Pallas kernels for 0% -> 0%
where the time goes in v3:
time: 316 us; the launch traced here: 315 us
  waiting for transfers between devices  141 us (45%)
  starting transfers between devices  88.4 us (28%)
  local copies, waits for them, and re-layouts  32.6 us (10%)
  matrix products  30.5 us (10%)
  between operations  14.8 us (5%)
  other arithmetic  7.78 us (2%)
    ppermute x28, starting transfers between devices, shifted(): return lax.ppermute(block, axis, route)  68.7 us
    all_gather x1, waiting for transfers between devices, shards(): rows_half = lax.all_gather(own_half, 'ctx', axis=0, tiled=True)  60.4 us
    ppermute x15, waiting for transfers between devices, from_partner(): lax.ppermute(shard, axis, [(i, i ^ 1 << stride) for i in range(lax.axis_s...  44.8 us
    ppermute x28, waiting for transfers between devices, shifted(): return lax.ppermute(block, axis, route)  35.7 us
    ppermute x15, starting transfers between devices, from_partner(): lax.ppermute(shard, axis, [(i, i ^ 1 << stride) for i in range(lax.axis_s...  19.6 us
    convert_element_type x7, local copies, waits for them, and re-layouts, shards(): key_parts[block_start:block_start + tok_rows].astype(jnp.bfloat16)  9.81 us
    unnamed x44, local copies, waits for them, and re-layouts  9.34 us
    sub x1, matrix products, shards(): weights_exp = jnp.where(allowed[None, None], jnp.exp(masked - row_max), 0.0)  6.9 us
  transfers between devices with their start and end apart: 45, of which 20 were waited for; matrix products, arithmetic and copies ran while one was open for 18% of the time, Pallas kernels for 0%

profile of v3, /device:TPU:0, one launch (start us, length us, event | category | flops | bytes accessed | tf_op | source)
XLA Modules:
  0.0 315.0 jit_solution(13265718489556357328)
XLA Ops:
  7.3 1.8 constant_dynamic-slice_fusion
  9.2 60.4 %all-gather.3.cloned.1.call-done = bf16[2688,512]{1,0:T(8,128)(2,1)} async-done(((bf16[336,512]{1,0:T(8,128)(2,1)}), bf16[2688,512]{1,0:T(8,128)(2,1)}) %all-gather.3.cloned.1.call-update) | async-done | bytes 2752528 | tf_op jit(solution)/shard_map/all_gather | solution.py:64
  69.6 4.0 %collective-permute-start.3 = (bf16[128,1024]{1,0:T(8,128)(2,1)}, bf16[128,1024]{1,0:T(8,128)(2,1)S(1)}, u32[]{:S(2)}, u32[]{:S(2)}) collective-permute-start(bf16[128,1024]{1,0:T(8,128)(2,1)} %bitcast.3), channel_id=1, source_target_pairs={{0,14},{1,15},{16,30},{17,31}} | collective-permute-start | bytes 786440 | tf_op jit(solution)/shard_map/ppermute | solution.py:39
  73.6 2.0 collective-permute-start.4
  75.6 2.0 collective-permute-start.5
  77.6 2.0 collective-permute-start.6
  83.9 3.0 collective-permute-done
  86.9 9.5 %collective-permute-done.11 = f32[8]{0:T(128)S(1)} collective-permute-done((f32[8]{0:T(128)S(1)}, f32[8]{0:T(128)S(1)}, u32[]{:S(2)}, u32[]{:S(2)}) %collective-permute-start.11) | collective-permute-done | bytes 64 | tf_op jit(solution)/shard_map/ppermute | solution.py:19
  96.3 2.4 collective-permute-start.1
  98.7 1.5 collective-permute-done.1
  100.2 4.4 %collective-permute-done.12 = f32[8]{0:T(128)S(1)} collective-permute-done((f32[8]{0:T(128)S(1)}, f32[8]{0:T(128)S(1)}, u32[]{:S(2)}, u32[]{:S(2)}) %collective-permute-start.12) | collective-permute-done | bytes 64 | tf_op jit(solution)/shard_map/ppermute | solution.py:19
  104.7 4.4 %collective-permute-done.2 = f32[8]{0:T(128)S(1)} collective-permute-done((f32[8]{0:T(128)S(1)}, f32[8]{0:T(128)S(1)}, u32[]{:S(2)}, u32[]{:S(2)}) %collective-permute-start.2) | collective-permute-done | bytes 64 | tf_op jit(solution)/shard_map/ppermute | solution.py:19
  113.2 6.7 %collective-permute-start.8 = (bf16[128,1024]{1,0:T(8,128)(2,1)}, bf16[128,1024]{1,0:T(8,128)(2,1)S(1)}, u32[]{:S(2)}, u32[]{:S(2)}) collective-permute-start(bf16[128,1024]{1,0:T(8,128)(2,1)} %bitcast.3), channel_id=1, source_target_pairs={{0,4},{2,6},{4,8},{6,10},{8,12},{10,14},{1,5},{3,7},{5,9},{7,11},{... | collective-permute-start | bytes 786440 | tf_op jit(solution)/shard_map/ppermute | solution.py:39
  120.9 6.9 %collective-permute-start.9 = (bf16[128,1024]{1,0:T(8,128)(2,1)}, bf16[128,1024]{1,0:T(8,128)(2,1)S(1)}, u32[]{:S(2)}, u32[]{:S(2)}) collective-permute-start(bf16[128,1024]{1,0:T(8,128)(2,1)} %bitcast.3), channel_id=1, source_target_pairs={{0,2},{2,4},{4,6},{6,8},{8,10},{10,12},{12,14},{1,3},{3,5},{5,7},{... | collective-permute-start | bytes 786440 | tf_op jit(solution)/shard_map/ppermute | solution.py:39
  130.9 2.6 collective-permute-done.9
  134.6 4.2 %convolution_bitcast_fusion.1 = f32[128,1024]{0,1:T(8,128)S(1)} fusion(bf16[2688,1024]{1,0:T(8,128)(2,1)} %all-gather.5.cloned.1.call-done, bf16[1,128,2688]{2,1,0:T(8,128)(2,1)S(1)} %copy-done), kind=kOutput, calls=%fused_computation.26 | convolution fusion | flops 704643072 | bytes 6717440 | tf_op jit(solution)/shard_map/dot_general | solution.py:70
  139.7 2.0 collective-permute-start.21
  141.7 2.0 copy.71
  143.7 3.2 %copy.60 = bf16[1024,8,128,1]{0,2,3,1:T(8,128)(2,1)S(1)} copy(bf16[1024,8,128,1]{2,1,0,3:T(8,128)(2,1)} %bitcast.120) | data formatting | bytes 4194304 | tf_op jit(solution)/shard_map/reshape | solution.py:108
  146.9 6.9 %fusion.36 = (f32[8,2,128]{2,1,0:T(2,128)S(1)}, f32[8,2,128,1024]{2,3,1,0:T(8,128)}) fusion(pred[128,1024]{0,1:T(8,128)(4,1)} %compare_and_fusion, bf16[1024,8,128,1]{0,2,3,1:T(8,128)(2,1)S(1)} %copy.60, bf16[128,8,2,128]{0,3,2,1:T(8,128)(2,1)S(1)} %bitcast.124), kind=kOutput, calls=%fused_computation.82 | convolution fusion | flops 547357696 | bytes 11149312 | tf_op jit(solution)/shard_map/sub | solution.py:115
  153.8 5.0 %fusion.37 = (bf16[1024,8,128]{0,2,1:T(8,128)(2,1)S(1)}, f32[1024,8,128]{0,2,1:T(8,128)S(1)}) fusion(bf16[128,8,2,128]{3,2,1,0:T(2,128)(2,1)} %reshape_squeeze.7, f32[128]{0:T(128)S(1)} %get-tuple-element.20, f32[8,2,128,1024]{2,3,1,0:T(8,128)} %get-tuple-element.38, f32[8,2,128]{2,1,0:T(2,128)S(1)} %get-tuple-element.37), kind=kOutput, calls=%fused_computation.83 | convolution fusion | flops 544210944 | bytes 15213056 | tf_op jit(solution)/shard_map/jgtl,tjgd->ljd/dot_general | solution.py:129
  161.8 6.4 %collective-permute-start.22 = (bf16[128,1024]{0,1:T(8,128)(2,1)}, bf16[128,1024]{0,1:T(8,128)(2,1)S(1)}, u32[]{:S(2)}, u32[]{:S(2)}) collective-permute-start(bf16[128,1024]{0,1:T(8,128)(2,1)} %fusion.15), channel_id=1, source_target_pairs={{0,12},{2,14},{1,13},{3,15},{16,28},{18,30},{17,29},{19,31}} | collective-permute-start | bytes 786440 | tf_op jit(solution)/shard_map/ppermute | solution.py:39
  177.1 3.8 %collective-permute-done.23 = bf16[128,1024]{0,1:T(8,128)(2,1)S(1)} collective-permute-done((bf16[128,1024]{0,1:T(8,128)(2,1)}, bf16[128,1024]{0,1:T(8,128)(2,1)S(1)}, u32[]{:S(2)}, u32[]{:S(2)}) %collective-permute-start.23) | collective-permute-done | bytes 262176 | tf_op jit(solution)/shard_map/ppermute | solution.py:39
  182.2 2.4 collective-permute-done.24
  186.2 9.3 %collective-permute-done.18 = bf16[128,1024]{0,1:T(8,128)(2,1)S(1)} collective-permute-done((bf16[128,1024]{0,1:T(8,128)(2,1)S(1)}, bf16[128,1024]{0,1:T(8,128)(2,1)S(1)}, u32[]{:S(2)}, u32[]{:S(2)}) %collective-permute-start.18) | collective-permute-done | bytes 262176 | tf_op jit(solution)/shard_map/ppermute | solution.py:39
  195.6 7.3 %collective-permute-start.25 = (bf16[128,1024]{0,1:T(8,128)(2,1)}, bf16[128,1024]{0,1:T(8,128)(2,1)S(1)}, u32[]{:S(2)}, u32[]{:S(2)}) collective-permute-start(bf16[128,1024]{0,1:T(8,128)(2,1)} %fusion.15), channel_id=1, source_target_pairs={{0,6},{2,8},{4,10},{6,12},{8,14},{1,7},{3,9},{5,11},{7,13},{9,15},... | collective-permute-start | bytes 786440 | tf_op jit(solution)/shard_map/ppermute | solution.py:39
  204.2 6.1 %collective-permute-start.27 = (bf16[128,1024]{0,1:T(8,128)(2,1)}, bf16[128,1024]{0,1:T(8,128)(2,1)S(1)}, u32[]{:S(2)}, u32[]{:S(2)}) collective-permute-start(bf16[128,1024]{0,1:T(8,128)(2,1)} %fusion.15), channel_id=1, source_target_pairs={{0,2},{2,4},{4,6},{6,8},{8,10},{10,12},{12,14},{1,3},{3,5},{5,7},{... | collective-permute-start | bytes 786440 | tf_op jit(solution)/shard_map/ppermute | solution.py:39
  210.9 3.4 %collective-permute-done.26 = bf16[128,1024]{0,1:T(8,128)(2,1)S(1)} collective-permute-done((bf16[128,1024]{0,1:T(8,128)(2,1)}, bf16[128,1024]{0,1:T(8,128)(2,1)S(1)}, u32[]{:S(2)}, u32[]{:S(2)}) %collective-permute-start.26) | collective-permute-done | bytes 262176 | tf_op jit(solution)/shard_map/ppermute | solution.py:39
  214.5 5.8 %collective-permute-done.27 = bf16[128,1024]{0,1:T(8,128)(2,1)S(1)} collective-permute-done((bf16[128,1024]{0,1:T(8,128)(2,1)}, bf16[128,1024]{0,1:T(8,128)(2,1)S(1)}, u32[]{:S(2)}, u32[]{:S(2)}) %collective-permute-start.27) | collective-permute-done | bytes 262176 | tf_op jit(solution)/shard_map/ppermute | solution.py:39
  221.5 1.9 fusion.1
  223.4 1.7 fusion.3
  225.1 1.7 convolution_convert_fusion
  228.1 2.4 collective-permute-start.40
  230.5 3.4 %fusion.38 = (bf16[1024,8,128]{0,2,1:T(8,128)(2,1)S(1)}, f32[1024,8,128]{0,2,1:T(8,128)}) fusion(bf16[8,2,128,1024]{2,3,1,0:T(8,128)(2,1)S(1)} %fusion.3, bf16[128,8,2,128]{0,3,2,1:T(8,128)(2,1)S(1)} %bitcast.125), kind=kOutput, calls=%fused_computation.84 | convolution fusion | flops 537919488 | bytes 11010048 | tf_op jit(solution)/shard_map/jgtl,tjgd->ljd/dot_general | solution.py:125
  234.0 2.2 collective-permute-start.41
  242.8 3.4 %collective-permute-start.42 = (f32[16,1024]{1,0:T(8,128)S(1)}, f32[16,1024]{1,0:T(8,128)S(1)}, u32[]{:S(2)}, u32[]{:S(2)}) collective-permute-start(f32[16,1024]{1,0:T(8,128)S(1)} %add.160), channel_id=1, source_target_pairs={{0,8},{2,10},{4,12},{6,14},{8,0},{10,2},{12,4},{14,6},{1,9},{3,11}... | collective-permute-start | bytes 196616 | tf_op jit(solution)/shard_map/ppermute | solution.py:19
  246.2 2.5 collective-permute-start.37
  250.0 1.8 copy.51
  253.1 1.8 copy.50
  254.9 1.8 copy.49
  256.7 1.8 copy.48
  258.5 1.9 slice.108
  267.7 5.3 %fusion.11 = bf16[1,128,2688]{2,1,0:T(8,128)(2,1)} fusion(f32[128,2688]{1,0:T(8,128)S(1)} %convolution_multiply_fusion, bf16[128,1024]{0,1:T(8,128)(2,1)S(1)} %fusion.27, bf16[2688,1024]{1,0:T(8,128)(2,1)} %all-gather.5.cloned.1.call-done), kind=kOutput, calls=%fused_computation.19 | convolution fusion | flops 705331200 | bytes 7831552 | tf_op jit(solution)/shard_map/tk,dk->td/dot_general | solution.py:147
  274.6 2.4 collective-permute-done.32
  277.0 4.1 %collective-permute-start.38 = (f32[2688,16]{0,1:T(8,128)S(1)}, f32[2688,16]{0,1:T(8,128)S(1)}, u32[]{:S(2)}, u32[]{:S(2)}) collective-permute-start(f32[2688,16]{0,1:T(8,128)S(1)} %add.156), channel_id=1, source_target_pairs={{0,8},{2,10},{4,12},{6,14},{8,0},{10,2},{12,4},{14,6},{1,9},{3,11}... | collective-permute-start | bytes 516104 | tf_op jit(solution)/shard_map/ppermute | solution.py:19
  281.1 4.9 %collective-permute-done.31 = bf16[128,1024]{1,0:T(8,128)(2,1)S(1)} collective-permute-done((bf16[128,1024]{1,0:T(8,128)(2,1)}, bf16[128,1024]{1,0:T(8,128)(2,1)S(1)}, u32[]{:S(2)}, u32[]{:S(2)}) %collective-permute-start.31) | collective-permute-done | bytes 262176 | tf_op jit(solution)/shard_map/ppermute | solution.py:39
  286.0 2.2 fusion.31
  288.1 19.3 %collective-permute-done.38 = f32[2688,16]{0,1:T(8,128)S(1)} collective-permute-done((f32[2688,16]{0,1:T(8,128)S(1)}, f32[2688,16]{0,1:T(8,128)S(1)}, u32[]{:S(2)}, u32[]{:S(2)}) %collective-permute-start.38) | collective-permute-done | bytes 172064 | tf_op jit(solution)/shard_map/ppermute | solution.py:19
  (146 shorter events, 52.3 us)
Async XLA Ops:
  7.2 74.7 %copy-start = (bf16[1,128,2688]{2,1,0:T(8,128)(2,1)S(1)}, bf16[1,128,2688]{2,1,0:T(8,128)(2,1)}, u32[]{:S(2)}) copy-start(bf16[1,128,2688]{2,1,0:T(8,128)(2,1)} %param.10) | copy-start | bytes 2064388
  7.2 73.1 %copy-start.5 = (bf16[1,128,2048]{2,1,0:T(8,128)(2,1)S(1)}, bf16[1,128,2048]{2,1,0:T(8,128)(2,1)}, u32[]{:S(2)}) copy-start(bf16[1,128,2048]{2,1,0:T(8,128)(2,1)} %param.16) | copy-start | bytes 1572868
  7.2 62.4 %all-gather.3.cloned.1.call-start = ((), (), s32[]{:S(2)}) async-start(), calls=%async_computation | async-start | bytes 3096576 | tf_op jit(solution)/shard_map/all_gather | solution.py:64
  9.1 72.4 %copy-start.6 = (bf16[1,128,2048]{2,1,0:T(8,128)(2,1)S(1)}, bf16[1,128,2048]{2,1,0:T(8,128)(2,1)}, u32[]{:S(2)}) copy-start(bf16[1,128,2048]{2,1,0:T(8,128)(2,1)} %param.11) | copy-start | bytes 1572868
  9.1 125.4 %all-gather.5.cloned.1.call-start = ((), (), s32[]{:S(2)}) async-start(), calls=%async_computation.1 | async-start | bytes 8257536 | tf_op jit(solution)/shard_map/all_gather | solution.py:65
  69.6 42.9 %collective-permute-start.3 = (bf16[128,1024]{1,0:T(8,128)(2,1)}, bf16[128,1024]{1,0:T(8,128)(2,1)S(1)}, u32[]{:S(2)}, u32[]{:S(2)}) collective-permute-start(bf16[128,1024]{1,0:T(8,128)(2,1)} %bitcast.3), channel_id=1, source_target_pairs={{0,14},{1,15},{16,30},{17,31}} | collective-permute-start | bytes 786440 | tf_op jit(solution)/shard_map/ppermute | solution.py:39
  73.6 47.3 %collective-permute-start.4 = (bf16[128,1024]{1,0:T(8,128)(2,1)}, bf16[128,1024]{1,0:T(8,128)(2,1)}, u32[]{:S(2)}, u32[]{:S(2)}) collective-permute-start(bf16[128,1024]{1,0:T(8,128)(2,1)} %bitcast.3), channel_id=1, source_target_pairs={{0,12},{2,14},{1,13},{3,15},{16,28},{18,30},{17,29},{19,31}} | collective-permute-start | bytes 786440 | tf_op jit(solution)/shard_map/ppermute | solution.py:39
  75.6 53.2 %collective-permute-start.5 = (bf16[128,1024]{1,0:T(8,128)(2,1)}, bf16[128,1024]{1,0:T(8,128)(2,1)}, u32[]{:S(2)}, u32[]{:S(2)}) collective-permute-start(bf16[128,1024]{1,0:T(8,128)(2,1)} %bitcast.3), channel_id=1, source_target_pairs={{0,10},{2,12},{4,14},{1,11},{3,13},{5,15},{16,26},{18,28},{20,30},... | collective-permute-start | bytes 786440 | tf_op jit(solution)/shard_map/ppermute | solution.py:39
  77.6 52.2 %collective-permute-start.6 = (bf16[128,1024]{1,0:T(8,128)(2,1)}, bf16[128,1024]{1,0:T(8,128)(2,1)}, u32[]{:S(2)}, u32[]{:S(2)}) collective-permute-start(bf16[128,1024]{1,0:T(8,128)(2,1)} %bitcast.3), channel_id=1, source_target_pairs={{0,8},{2,10},{4,12},{6,14},{1,9},{3,11},{5,13},{7,15},{16,24},{18,... | collective-permute-start | bytes 786440 | tf_op jit(solution)/shard_map/ppermute | solution.py:39
  79.7 3.6 %collective-permute-start.10 = (f32[8]{0:T(128)S(1)}, f32[8]{0:T(128)S(1)}, u32[]{:S(2)}, u32[]{:S(2)}) collective-permute-start(f32[8]{0:T(128)S(1)} %get-tuple-element.22), channel_id=1, source_target_pairs={{0,2},{2,0},{4,6},{6,4},{8,10},{10,8},{12,14},{14,12},{1,3},{3,1},... | collective-permute-start | bytes 104 | tf_op jit(solution)/shard_map/ppermute | solution.py:19
  83.3 3.5 %collective-permute-start = (f32[8]{0:T(128)S(1)}, f32[8]{0:T(128)S(1)}, u32[]{:S(2)}, u32[]{:S(2)}) collective-permute-start(f32[8]{0:T(128)S(1)} %get-tuple-element.21), channel_id=1, source_target_pairs={{0,2},{2,0},{4,6},{6,4},{8,10},{10,8},{12,14},{14,12},{1,3},{3,1},... | collective-permute-start | bytes 104 | tf_op jit(solution)/shard_map/ppermute | solution.py:19
  86.9 9.5 %collective-permute-start.11 = (f32[8]{0:T(128)S(1)}, f32[8]{0:T(128)S(1)}, u32[]{:S(2)}, u32[]{:S(2)}) collective-permute-start(f32[8]{0:T(128)S(1)} %add.135), channel_id=1, source_target_pairs={{0,4},{2,6},{4,0},{6,2},{8,12},{10,14},{12,8},{14,10},{1,5},{3,7},... | collective-permute-start | bytes 104 | tf_op jit(solution)/shard_map/ppermute | solution.py:19
  96.3 3.9 %collective-permute-start.1 = (f32[8]{0:T(128)S(1)}, f32[8]{0:T(128)S(1)}, u32[]{:S(2)}, u32[]{:S(2)}) collective-permute-start(f32[8]{0:T(128)S(1)} %add.130), channel_id=1, source_target_pairs={{0,4},{2,6},{4,0},{6,2},{8,12},{10,14},{12,8},{14,10},{1,5},{3,7},... | collective-permute-start | bytes 104 | tf_op jit(solution)/shard_map/ppermute | solution.py:19
  100.2 4.4 %collective-permute-start.12 = (f32[8]{0:T(128)S(1)}, f32[8]{0:T(128)S(1)}, u32[]{:S(2)}, u32[]{:S(2)}) collective-permute-start(f32[8]{0:T(128)S(1)} %add.136), channel_id=1, source_target_pairs={{0,8},{2,10},{4,12},{6,14},{8,0},{10,2},{12,4},{14,6},{1,9},{3,11}... | collective-permute-start | bytes 104 | tf_op jit(solution)/shard_map/ppermute | solution.py:19
  104.7 4.4 %collective-permute-start.2 = (f32[8]{0:T(128)S(1)}, f32[8]{0:T(128)S(1)}, u32[]{:S(2)}, u32[]{:S(2)}) collective-permute-start(f32[8]{0:T(128)S(1)} %add.131), channel_id=1, source_target_pairs={{0,8},{2,10},{4,12},{6,14},{8,0},{10,2},{12,4},{14,6},{1,9},{3,11}... | collective-permute-start | bytes 104 | tf_op jit(solution)/shard_map/ppermute | solution.py:19
  109.1 1.1 collective-permute-start.13
  110.2 20.6 %collective-permute-start.7 = (bf16[128,1024]{1,0:T(8,128)(2,1)}, bf16[128,1024]{1,0:T(8,128)(2,1)S(1)}, u32[]{:S(2)}, u32[]{:S(2)}) collective-permute-start(bf16[128,1024]{1,0:T(8,128)(2,1)} %bitcast.3), channel_id=1, source_target_pairs={{0,6},{2,8},{4,10},{6,12},{8,14},{1,7},{3,9},{5,11},{7,13},{9,15},... | collective-permute-start | bytes 786440 | tf_op jit(solution)/shard_map/ppermute | solution.py:39
  113.2 17.6 %collective-permute-start.8 = (bf16[128,1024]{1,0:T(8,128)(2,1)}, bf16[128,1024]{1,0:T(8,128)(2,1)S(1)}, u32[]{:S(2)}, u32[]{:S(2)}) collective-permute-start(bf16[128,1024]{1,0:T(8,128)(2,1)} %bitcast.3), channel_id=1, source_target_pairs={{0,4},{2,6},{4,8},{6,10},{8,12},{10,14},{1,5},{3,7},{5,9},{7,11},{... | collective-permute-start | bytes 786440 | tf_op jit(solution)/shard_map/ppermute | solution.py:39
  120.9 12.6 %collective-permute-start.9 = (bf16[128,1024]{1,0:T(8,128)(2,1)}, bf16[128,1024]{1,0:T(8,128)(2,1)S(1)}, u32[]{:S(2)}, u32[]{:S(2)}) collective-permute-start(bf16[128,1024]{1,0:T(8,128)(2,1)} %bitcast.3), channel_id=1, source_target_pairs={{0,2},{2,4},{4,6},{6,8},{8,10},{10,12},{12,14},{1,3},{3,5},{5,7},{... | collective-permute-start | bytes 786440 | tf_op jit(solution)/shard_map/ppermute | solution.py:39
  139.7 29.8 %collective-permute-start.21 = (bf16[128,1024]{0,1:T(8,128)(2,1)}, bf16[128,1024]{0,1:T(8,128)(2,1)}, u32[]{:S(2)}, u32[]{:S(2)}) collective-permute-start(bf16[128,1024]{0,1:T(8,128)(2,1)} %fusion.15), channel_id=1, source_target_pairs={{0,14},{1,15},{16,30},{17,31}} | collective-permute-start | bytes 786440 | tf_op jit(solution)/shard_map/ppermute | solution.py:39
  159.2 13.8 %collective-permute-start.20 = (bf16[128,1024]{0,1:T(8,128)(2,1)S(1)}, bf16[128,1024]{0,1:T(8,128)(2,1)S(1)}, u32[]{:S(2)}, u32[]{:S(2)}) collective-permute-start(bf16[128,1024]{0,1:T(8,128)(2,1)S(1)} %bitcast.139), channel_id=1, source_target_pairs={{14,0},{15,1},{30,16},{31,17}} | collective-permute-start | bytes 786440 | tf_op jit(solution)/shard_map/ppermute | solution.py:39
  160.5 14.0 %collective-permute-start.19 = (bf16[128,1024]{0,1:T(8,128)(2,1)S(1)}, bf16[128,1024]{0,1:T(8,128)(2,1)S(1)}, u32[]{:S(2)}, u32[]{:S(2)}) collective-permute-start(bf16[128,1024]{0,1:T(8,128)(2,1)S(1)} %bitcast.138), channel_id=1, source_target_pairs={{12,0},{14,2},{13,1},{15,3},{28,16},{30,18},{29,17},{31,19}} | collective-permute-start | bytes 786440 | tf_op jit(solution)/shard_map/ppermute | solution.py:39
  161.8 14.0 %collective-permute-start.22 = (bf16[128,1024]{0,1:T(8,128)(2,1)}, bf16[128,1024]{0,1:T(8,128)(2,1)S(1)}, u32[]{:S(2)}, u32[]{:S(2)}) collective-permute-start(bf16[128,1024]{0,1:T(8,128)(2,1)} %fusion.15), channel_id=1, source_target_pairs={{0,12},{2,14},{1,13},{3,15},{16,28},{18,30},{17,29},{19,31}} | collective-permute-start | bytes 786440 | tf_op jit(solution)/shard_map/ppermute | solution.py:39
  168.2 12.7 %collective-permute-start.23 = (bf16[128,1024]{0,1:T(8,128)(2,1)}, bf16[128,1024]{0,1:T(8,128)(2,1)S(1)}, u32[]{:S(2)}, u32[]{:S(2)}) collective-permute-start(bf16[128,1024]{0,1:T(8,128)(2,1)} %fusion.15), channel_id=1, source_target_pairs={{0,10},{2,12},{4,14},{1,11},{3,13},{5,15},{16,26},{18,28},{20,30},... | collective-permute-start | bytes 786440 | tf_op jit(solution)/shard_map/ppermute | solution.py:39
  169.5 15.1 %collective-permute-start.24 = (bf16[128,1024]{0,1:T(8,128)(2,1)}, bf16[128,1024]{0,1:T(8,128)(2,1)S(1)}, u32[]{:S(2)}, u32[]{:S(2)}) collective-permute-start(bf16[128,1024]{0,1:T(8,128)(2,1)} %fusion.15), channel_id=1, source_target_pairs={{0,8},{2,10},{4,12},{6,14},{1,9},{3,11},{5,13},{7,15},{16,24},{18,... | collective-permute-start | bytes 786440 | tf_op jit(solution)/shard_map/ppermute | solution.py:39
  173.1 22.5 %collective-permute-start.18 = (bf16[128,1024]{0,1:T(8,128)(2,1)S(1)}, bf16[128,1024]{0,1:T(8,128)(2,1)S(1)}, u32[]{:S(2)}, u32[]{:S(2)}) collective-permute-start(bf16[128,1024]{0,1:T(8,128)(2,1)S(1)} %bitcast.137), channel_id=1, source_target_pairs={{10,0},{12,2},{14,4},{11,1},{13,3},{15,5},{26,16},{28,18},{30,20},... | collective-permute-start | bytes 786440 | tf_op jit(solution)/shard_map/ppermute | solution.py:39
  174.5 28.4 %collective-permute-start.17 = (bf16[128,1024]{0,1:T(8,128)(2,1)S(1)}, bf16[128,1024]{0,1:T(8,128)(2,1)S(1)}, u32[]{:S(2)}, u32[]{:S(2)}) collective-permute-start(bf16[128,1024]{0,1:T(8,128)(2,1)S(1)} %bitcast.136), channel_id=1, source_target_pairs={{8,0},{10,2},{12,4},{14,6},{9,1},{11,3},{13,5},{15,7},{24,16},{26,... | collective-permute-start | bytes 786440 | tf_op jit(solution)/shard_map/ppermute | solution.py:39
  175.8 28.4 %collective-permute-start.16 = (bf16[128,1024]{0,1:T(8,128)(2,1)S(1)}, bf16[128,1024]{0,1:T(8,128)(2,1)S(1)}, u32[]{:S(2)}, u32[]{:S(2)}) collective-permute-start(bf16[128,1024]{0,1:T(8,128)(2,1)S(1)} %bitcast.135), channel_id=1, source_target_pairs={{6,0},{8,2},{10,4},{12,6},{14,8},{7,1},{9,3},{11,5},{13,7},{15,9},... | collective-permute-start | bytes 786440 | tf_op jit(solution)/shard_map/ppermute | solution.py:39
  180.9 29.4 %collective-permute-start.15 = (bf16[128,1024]{0,1:T(8,128)(2,1)S(1)}, bf16[128,1024]{0,1:T(8,128)(2,1)S(1)}, u32[]{:S(2)}, u32[]{:S(2)}) collective-permute-start(bf16[128,1024]{0,1:T(8,128)(2,1)S(1)} %bitcast.134), channel_id=1, source_target_pairs={{4,0},{6,2},{8,4},{10,6},{12,8},{14,10},{5,1},{7,3},{9,5},{11,7},{... | collective-permute-start | bytes 786440 | tf_op jit(solution)/shard_map/ppermute | solution.py:39
  184.7 25.7 %collective-permute-start.14 = (bf16[128,1024]{0,1:T(8,128)(2,1)S(1)}, bf16[128,1024]{0,1:T(8,128)(2,1)S(1)}, u32[]{:S(2)}, u32[]{:S(2)}) collective-permute-start(bf16[128,1024]{0,1:T(8,128)(2,1)S(1)} %bitcast.133), channel_id=1, source_target_pairs={{2,0},{4,2},{6,4},{8,6},{10,8},{12,10},{14,12},{3,1},{5,3},{7,5},{... | collective-permute-start | bytes 786440 | tf_op jit(solution)/shard_map/ppermute | solution.py:39
  195.6 15.1 %collective-permute-start.25 = (bf16[128,1024]{0,1:T(8,128)(2,1)}, bf16[128,1024]{0,1:T(8,128)(2,1)S(1)}, u32[]{:S(2)}, u32[]{:S(2)}) collective-permute-start(bf16[128,1024]{0,1:T(8,128)(2,1)} %fusion.15), channel_id=1, source_target_pairs={{0,6},{2,8},{4,10},{6,12},{8,14},{1,7},{3,9},{5,11},{7,13},{9,15},... | collective-permute-start | bytes 786440 | tf_op jit(solution)/shard_map/ppermute | solution.py:39
  202.9 11.4 %collective-permute-start.26 = (bf16[128,1024]{0,1:T(8,128)(2,1)}, bf16[128,1024]{0,1:T(8,128)(2,1)S(1)}, u32[]{:S(2)}, u32[]{:S(2)}) collective-permute-start(bf16[128,1024]{0,1:T(8,128)(2,1)} %fusion.15), channel_id=1, source_target_pairs={{0,4},{2,6},{4,8},{6,10},{8,12},{10,14},{1,5},{3,7},{5,9},{7,11},{... | collective-permute-start | bytes 786440 | tf_op jit(solution)/shard_map/ppermute | solution.py:39
  204.2 16.1 %collective-permute-start.27 = (bf16[128,1024]{0,1:T(8,128)(2,1)}, bf16[128,1024]{0,1:T(8,128)(2,1)S(1)}, u32[]{:S(2)}, u32[]{:S(2)}) collective-permute-start(bf16[128,1024]{0,1:T(8,128)(2,1)} %fusion.15), channel_id=1, source_target_pairs={{0,2},{2,4},{4,6},{6,8},{8,10},{10,12},{12,14},{1,3},{3,5},{5,7},{... | collective-permute-start | bytes 786440 | tf_op jit(solution)/shard_map/ppermute | solution.py:39
  226.8 1.3 collective-permute-start.39
  227.0 9.1 %collective-permute-start.35 = (f32[2688,16]{0,1:T(8,128)S(1)}, f32[2688,16]{0,1:T(8,128)S(1)}, u32[]{:S(2)}, u32[]{:S(2)}) collective-permute-start(f32[2688,16]{0,1:T(8,128)S(1)} %fusion.12), channel_id=1, source_target_pairs={{0,1},{1,0},{2,3},{3,2},{4,5},{5,4},{6,7},{7,6},{8,9},{9,8},{10,11... | collective-permute-start | bytes 516104 | tf_op jit(solution)/shard_map/ppermute | solution.py:19
  228.1 5.9 %collective-permute-start.40 = (f32[16,1024]{1,0:T(8,128)S(1)}, f32[16,1024]{1,0:T(8,128)S(1)}, u32[]{:S(2)}, u32[]{:S(2)}) collective-permute-start(f32[16,1024]{1,0:T(8,128)S(1)} %add.158), channel_id=1, source_target_pairs={{0,2},{2,0},{4,6},{6,4},{8,10},{10,8},{12,14},{14,12},{1,3},{3,1},... | collective-permute-start | bytes 196616 | tf_op jit(solution)/shard_map/ppermute | solution.py:19
  234.0 8.8 %collective-permute-start.41 = (f32[16,1024]{1,0:T(8,128)S(1)}, f32[16,1024]{1,0:T(8,128)S(1)}, u32[]{:S(2)}, u32[]{:S(2)}) collective-permute-start(f32[16,1024]{1,0:T(8,128)S(1)} %add.159), channel_id=1, source_target_pairs={{0,4},{2,6},{4,0},{6,2},{8,12},{10,14},{12,8},{14,10},{1,5},{3,7},... | collective-permute-start | bytes 196616 | tf_op jit(solution)/shard_map/ppermute | solution.py:19
  236.2 9.9 %collective-permute-start.36 = (f32[2688,16]{0,1:T(8,128)S(1)}, f32[2688,16]{0,1:T(8,128)S(1)}, u32[]{:S(2)}, u32[]{:S(2)}) collective-permute-start(f32[2688,16]{0,1:T(8,128)S(1)} %add.154), channel_id=1, source_target_pairs={{0,2},{2,0},{4,6},{6,4},{8,10},{10,8},{12,14},{14,12},{1,3},{3,1},... | collective-permute-start | bytes 516104 | tf_op jit(solution)/shard_map/ppermute | solution.py:19
  239.3 23.2 %collective-permute-start.34 = (bf16[128,1024]{1,0:T(8,128)(2,1)}, bf16[128,1024]{1,0:T(8,128)(2,1)}, u32[]{:S(2)}, u32[]{:S(2)}) collective-permute-start(bf16[128,1024]{1,0:T(8,128)(2,1)} %copy.53), channel_id=1, source_target_pairs={{14,0},{15,1},{30,16},{31,17}} | collective-permute-start | bytes 786440 | tf_op jit(solution)/shard_map/ppermute | solution.py:39
  241.4 22.3 %collective-permute-start.33 = (bf16[128,1024]{1,0:T(8,128)(2,1)}, bf16[128,1024]{1,0:T(8,128)(2,1)}, u32[]{:S(2)}, u32[]{:S(2)}) collective-permute-start(bf16[128,1024]{1,0:T(8,128)(2,1)} %copy.52), channel_id=1, source_target_pairs={{12,0},{14,2},{13,1},{15,3},{28,16},{30,18},{29,17},{31,19}} | collective-permute-start | bytes 786440 | tf_op jit(solution)/shard_map/ppermute | solution.py:39
  242.8 22.3 %collective-permute-start.42 = (f32[16,1024]{1,0:T(8,128)S(1)}, f32[16,1024]{1,0:T(8,128)S(1)}, u32[]{:S(2)}, u32[]{:S(2)}) collective-permute-start(f32[16,1024]{1,0:T(8,128)S(1)} %add.160), channel_id=1, source_target_pairs={{0,8},{2,10},{4,12},{6,14},{8,0},{10,2},{12,4},{14,6},{1,9},{3,11}... | collective-permute-start | bytes 196616 | tf_op jit(solution)/shard_map/ppermute | solution.py:19
  246.2 20.3 %collective-permute-start.37 = (f32[2688,16]{0,1:T(8,128)S(1)}, f32[2688,16]{0,1:T(8,128)}, u32[]{:S(2)}, u32[]{:S(2)}) collective-permute-start(f32[2688,16]{0,1:T(8,128)S(1)} %add.155), channel_id=1, source_target_pairs={{0,4},{2,6},{4,0},{6,2},{8,12},{10,14},{12,8},{14,10},{1,5},{3,7},... | collective-permute-start | bytes 516104 | tf_op jit(solution)/shard_map/ppermute | solution.py:19
  251.8 25.1 %collective-permute-start.32 = (bf16[128,1024]{1,0:T(8,128)(2,1)}, bf16[128,1024]{1,0:T(8,128)(2,1)}, u32[]{:S(2)}, u32[]{:S(2)}) collective-permute-start(bf16[128,1024]{1,0:T(8,128)(2,1)} %copy.51), channel_id=1, source_target_pairs={{10,0},{12,2},{14,4},{11,1},{13,3},{15,5},{26,16},{28,18},{30,20},... | collective-permute-start | bytes 786440 | tf_op jit(solution)/shard_map/ppermute | solution.py:39
  262.5 23.5 %collective-permute-start.31 = (bf16[128,1024]{1,0:T(8,128)(2,1)}, bf16[128,1024]{1,0:T(8,128)(2,1)S(1)}, u32[]{:S(2)}, u32[]{:S(2)}) collective-permute-start(bf16[128,1024]{1,0:T(8,128)(2,1)} %copy.50), channel_id=1, source_target_pairs={{8,0},{10,2},{12,4},{14,6},{9,1},{11,3},{13,5},{15,7},{24,16},{26,... | collective-permute-start | bytes 786440 | tf_op jit(solution)/shard_map/ppermute | solution.py:39
  263.8 22.2 %collective-permute-start.30 = (bf16[128,1024]{1,0:T(8,128)(2,1)}, bf16[128,1024]{1,0:T(8,128)(2,1)S(1)}, u32[]{:S(2)}, u32[]{:S(2)}) collective-permute-start(bf16[128,1024]{1,0:T(8,128)(2,1)} %copy.49), channel_id=1, source_target_pairs={{6,0},{8,2},{10,4},{12,6},{14,8},{7,1},{9,3},{11,5},{13,7},{15,9},... | collective-permute-start | bytes 786440 | tf_op jit(solution)/shard_map/ppermute | solution.py:39
  265.1 20.9 %collective-permute-start.29 = (bf16[128,1024]{1,0:T(8,128)(2,1)}, bf16[128,1024]{1,0:T(8,128)(2,1)S(1)}, u32[]{:S(2)}, u32[]{:S(2)}) collective-permute-start(bf16[128,1024]{1,0:T(8,128)(2,1)} %copy.48), channel_id=1, source_target_pairs={{4,0},{6,2},{8,4},{10,6},{12,8},{14,10},{5,1},{7,3},{9,5},{11,7},{... | collective-permute-start | bytes 786440 | tf_op jit(solution)/shard_map/ppermute | solution.py:39
  266.4 19.6 %collective-permute-start.28 = (bf16[128,1024]{1,0:T(8,128)(2,1)}, bf16[128,1024]{1,0:T(8,128)(2,1)S(1)}, u32[]{:S(2)}, u32[]{:S(2)}) collective-permute-start(bf16[128,1024]{1,0:T(8,128)(2,1)} %copy.46), channel_id=1, source_target_pairs={{2,0},{4,2},{6,4},{8,6},{10,8},{12,10},{14,12},{3,1},{5,3},{7,5},{... | collective-permute-start | bytes 786440 | tf_op jit(solution)/shard_map/ppermute | solution.py:39
  277.0 30.5 %collective-permute-start.38 = (f32[2688,16]{0,1:T(8,128)S(1)}, f32[2688,16]{0,1:T(8,128)S(1)}, u32[]{:S(2)}, u32[]{:S(2)}) collective-permute-start(f32[2688,16]{0,1:T(8,128)S(1)} %add.156), channel_id=1, source_target_pairs={{0,8},{2,10},{4,12},{6,14},{8,0},{10,2},{12,4},{14,6},{1,9},{3,11}... | collective-permute-start | bytes 516104 | tf_op jit(solution)/shard_map/ppermute | solution.py:19
  (11 other events, 428.7 us)
Sparse Core Ops, SparseCore 0:
  10.8 58.7 all-gather.2
  71.1 14.1 all-gather.4

commit v4 on v3

--- a/solution.py
+++ b/solution.py
@@ -31,6 +31,58 @@
             parts = jax.tree.map(jnp.add, parts, got)
             stride += 1
     return parts
+
+
+def tree_spread(block, levels):
+    count = 2 * levels
+    climbed = []
+    held = block
+    for step in range(1, levels):
+        held = lax.ppermute(held, "ctx", [(c - 2, c) for c in range(2 * step, count)])
+        climbed.append(held)
+    crossed = [lax.ppermute(block, "ctx", [(c - 1, c) for c in range(1, count, 2)])]
+    for step in range(1, levels):
+        crossed.append(
+            lax.ppermute(climbed[step - 1], "ctx", [(c ^ 1, c) for c in range(2 * step, count)])
+        )
+    return climbed + crossed
+
+
+def tree_slots(ctx_index, levels):
+    partner = jnp.bitwise_xor(ctx_index, 1)
+    owners, valid = [], []
+    for step in range(1, levels):
+        owners.append(ctx_index - 2 * step)
+        valid.append(ctx_index >= 2 * step)
+    owners.append(ctx_index - 1)
+    valid.append(ctx_index % 2 == 1)
+    for step in range(1, levels):
+        owners.append(partner - 2 * step)
+        valid.append(ctx_index >= 2 * step)
+    return owners, valid
+
+
+def tree_return(slot_parts, levels):
+    count = 2 * levels
+    climbed = slot_parts[: levels - 1]
+    crossed = slot_parts[levels - 1 :]
+    back = [lax.ppermute(crossed[0], "ctx", [(c, c - 1) for c in range(1, count, 2)])]
+    for step in range(1, levels):
+        back.append(
+            lax.ppermute(crossed[step], "ctx", [(c, c ^ 1) for c in range(2 * step, count)])
+        )
+    total = back[0].astype(jnp.float32)
+    carry = None
+    for step in range(levels - 1, 0, -1):
+        acc = climbed[step - 1].astype(jnp.float32) + back[step].astype(jnp.float32)
+        if carry is not None:
+            acc = acc + carry.astype(jnp.float32)
+        carry = lax.ppermute(
+            acc.astype(jnp.bfloat16), "ctx", [(c, c - 2) for c in range(2 * step, count)]
+        )
+    if carry is not None:
+        total = total + carry.astype(jnp.float32)
+    return total
 
 
 def shifted(block, axis, distance):
@@ -85,18 +137,34 @@
     starts = jnp.cumsum(counts) - counts
     tok_start = jnp.sum(seg_table * starts[None, :], 1).astype(jnp.int32)
     token_coefficient = jnp.sum(seg_table * coef[None, :], 1)
-    halo_blocks = min(WINDOW // tok_rows, lax.axis_size("ctx") - 1)
-    key_blocks = []
-    value_blocks = []
-    for distance in range(halo_blocks, 0, -1):
-        key_blocks.append(shifted(own_keys, "ctx", distance))
-        value_blocks.append(shifted(values, "ctx", distance))
+    ctx_size = lax.axis_size("ctx")
+    halo_blocks = min(WINDOW // tok_rows, ctx_size - 1)
+    use_tree = halo_blocks == ctx_size - 1 and ctx_size % 2 == 0 and ctx_size >= 4
+    levels = ctx_size // 2
+    row_iota = jnp.arange(tok_rows, dtype=jnp.int32)
+    if use_tree:
+        key_blocks = tree_spread(own_keys, levels)
+        value_blocks = tree_spread(values, levels)
+        owners, valid = tree_slots(ctx_index, levels)
+        far = jnp.int32(1 << 30)
+        upos = jnp.concatenate(
+            [jnp.where(ok, owner * tok_rows + row_iota, far) for owner, ok in zip(owners, valid)]
+            + [ctx_index * tok_rows + row_iota],
+            0,
+        )
+    else:
+        key_blocks = []
+        value_blocks = []
+        for distance in range(halo_blocks, 0, -1):
+            key_blocks.append(shifted(own_keys, "ctx", distance))
+            value_blocks.append(shifted(values, "ctx", distance))
     all_keys = jnp.concatenate(key_blocks + [own_keys], 0)
     all_keys, own_values = lax.optimization_barrier((all_keys, values))
     all_values = jnp.concatenate(value_blocks + [own_values], 0)
     span = all_keys.shape[0]
-    tpos = ctx_index * tok_rows + jnp.arange(tok_rows, dtype=jnp.int32)
-    upos = ctx_index * tok_rows - halo_blocks * tok_rows + jnp.arange(span, dtype=jnp.int32)
+    tpos = ctx_index * tok_rows + row_iota
+    if not use_tree:
+        upos = ctx_index * tok_rows - halo_blocks * tok_rows + jnp.arange(span, dtype=jnp.int32)
     allowed = (
         (upos[None, :] <= tpos[:, None])
         & (upos[None, :] > tpos[:, None] - WINDOW)
@@ -131,13 +199,20 @@
     ).reshape(span, width_kv)
     key_total = key_parts[halo_blocks * tok_rows :]
     value_total = value_parts[halo_blocks * tok_rows :]
-    for distance in range(1, halo_blocks + 1):
-        block_start = (halo_blocks - distance) * tok_rows
-        send_keys = key_parts[block_start : block_start + tok_rows].astype(jnp.bfloat16)
-        send_values = value_parts[block_start : block_start + tok_rows].astype(jnp.bfloat16)
-        back_keys, back_values = shifted((send_keys, send_values), "ctx", -distance)
-        key_total = key_total + back_keys.astype(jnp.float32)
-        value_total = value_total + back_values.astype(jnp.float32)
+    if use_tree:
+        slot_rows = lambda parts: [
+            parts[k * tok_rows : (k + 1) * tok_rows].astype(jnp.bfloat16) for k in range(halo_blocks)
+        ]
+        key_total = key_total + tree_return(slot_rows(key_parts), levels)
+        value_total = value_total + tree_return(slot_rows(value_parts), levels)
+    else:
+        for distance in range(1, halo_blocks + 1):
+            block_start = (halo_blocks - distance) * tok_rows
+            send_keys = key_parts[block_start : block_start + tok_rows].astype(jnp.bfloat16)
+            send_values = value_parts[block_start : block_start + tok_rows].astype(jnp.bfloat16)
+            back_keys, back_values = shifted((send_keys, send_values), "ctx", -distance)
+            key_total = key_total + back_keys.astype(jnp.float32)
+            value_total = value_total + back_values.astype(jnp.float32)
     key_grad = key_total.astype(jnp.bfloat16)
     value_gradient = value_total.astype(jnp.bfloat16)
     rank_middle = jnp.einsum(

time: 316 us -> 283 us (0.90)
  waiting for transfers between devices: 141 us -> 98.2 us
  other arithmetic: 7.78 us -> 20.7 us
  local copies, waits for them, and re-layouts: 32.6 us -> 29 us
    ppermute x15, waiting for transfers between devices: 44.8 us -> 5.44 us  [from_partner(): lax.ppermute(shard, axis, [(i, i ^ 1 << stride) for i in range(lax.axis_s...]
    ppermute x28, starting transfers between devices: 68.7 us -> 51 us  [the longest x6 24.2 us: tree_spread(): lax.ppermute(held, 'ctx', [(c - 2, c) for c in range(2 * step, count)])]
    ppermute x15, starting transfers between devices: 19.6 us -> 35.1 us  [from_partner(): lax.ppermute(shard, axis, [(i, i ^ 1 << stride) for i in range(lax.axis_s...]
    convert_element_type x0 -> x9, other arithmetic: none -> 9.51 us  [the longest x6 6.03 us: tree_return(): acc.astype(jnp.bfloat16)]
    add x14, other arithmetic: 2.36 us -> 6.83 us  [butterfly_sum(): parts = jax.tree.map(jnp.add, parts, got)]
    unnamed x44 -> x54, local copies, waits for them, and re-layouts: 9.34 us -> 5.7 us
    ppermute x28, waiting for transfers between devices: 35.7 us -> 32.3 us  [the longest x6 27.7 us: tree_return(): lax.ppermute(acc.astype(jnp.bfloat16), 'ctx', [(c, c - 2) for c in range(...]
  transfers between devices with their start and end apart: 45 -> 45, of which waited for: 20 -> 9; matrix products, arithmetic and copies ran while one was open for 18% -> 17% of each run, Pallas kernels for 0% -> 0%
where the time goes in v4:
time: 283 us; the launch traced here: 282 us
  waiting for transfers between devices  98.2 us (35%)
  starting transfers between devices  86.2 us (30%)
  matrix products  32.8 us (12%)
  local copies, waits for them, and re-layouts  29 us (10%)
  other arithmetic  20.7 us (7%)
  between operations  15 us (5%)
    all_gather x1, waiting for transfers between devices, shards(): rows_half = lax.all_gather(own_half, 'ctx', axis=0, tiled=True)  60.4 us
    ppermute x15, starting transfers between devices, from_partner(): lax.ppermute(shard, axis, [(i, i ^ 1 << stride) for i in range(lax.axis_s...  35.1 us
    ppermute x6, waiting for transfers between devices, tree_return(): lax.ppermute(acc.astype(jnp.bfloat16), 'ctx', [(c, c - 2) for c in range(...  27.7 us
    ppermute x6, starting transfers between devices, tree_spread(): lax.ppermute(held, 'ctx', [(c - 2, c) for c in range(2 * step, count)])  24.2 us
    convert_element_type x4, local copies, waits for them, and re-layouts, shards(): parts[k * tok_rows:(k + 1) * tok_rows].astype(jnp.bfloat16)  7.16 us
    add x14, other arithmetic, butterfly_sum(): parts = jax.tree.map(jnp.add, parts, got)  6.83 us
    ppermute x2, starting transfers between devices, tree_spread(): lax.ppermute(block, 'ctx', [(c - 1, c) for c in range(1, count, 2)])  6.83 us
    ppermute x6, starting transfers between devices, tree_return(): lax.ppermute(acc.astype(jnp.bfloat16), 'ctx', [(c, c - 2) for c in range(...  6.8 us
  transfers between devices with their start and end apart: 45, of which 9 were waited for; matrix products, arithmetic and copies ran while one was open for 17% of the time, Pallas kernels for 0%

profile of v4, /device:TPU:0, one launch (start us, length us, event | category | flops | bytes accessed | tf_op | source)
XLA Modules:
  0.0 281.8 jit_solution(15011084256623611525)
XLA Ops:
  7.3 1.8 constant_dynamic-slice_fusion
  9.2 60.4 %all-gather.3.cloned.1.call-done = bf16[2688,512]{1,0:T(8,128)(2,1)} async-done(((bf16[336,512]{1,0:T(8,128)(2,1)}), bf16[2688,512]{1,0:T(8,128)(2,1)}) %all-gather.3.cloned.1.call-update) | async-done | bytes 2752528 | tf_op jit(solution)/shard_map/all_gather | solution.py:116
  69.6 3.5 %collective-permute-start.3 = (bf16[128,1024]{1,0:T(8,128)(2,1)}, bf16[128,1024]{1,0:T(8,128)(2,1)S(1)}, u32[]{:S(2)}, u32[]{:S(2)}) collective-permute-start(bf16[128,1024]{1,0:T(8,128)(2,1)} %bitcast.3), channel_id=1, source_target_pairs={{0,4},{2,6},{4,8},{6,10},{8,12},{10,14},{1,5},{3,7},{5,9},{7,11},{... | collective-permute-start | bytes 786440 | tf_op jit(solution)/shard_map/ppermute | solution.py:41
  73.2 3.2 %collective-permute-start.6 = (bf16[128,1024]{1,0:T(8,128)(2,1)}, bf16[128,1024]{1,0:T(8,128)(2,1)}, u32[]{:S(2)}, u32[]{:S(2)}) collective-permute-start(bf16[128,1024]{1,0:T(8,128)(2,1)} %bitcast.3), channel_id=1, source_target_pairs={{0,2},{4,6},{8,10},{12,14},{1,3},{5,7},{9,11},{13,15},{16,18},{20,... | collective-permute-start | bytes 786440 | tf_op jit(solution)/shard_map/ppermute | solution.py:43
  76.6 2.0 collective-permute-start.10
  82.6 1.5 collective-permute-done.1
  84.1 1.6 collective-permute-start.2
  87.1 3.2 %collective-permute-done.12 = f32[8]{0:T(128)S(1)} collective-permute-done((f32[8]{0:T(128)S(1)}, f32[8]{0:T(128)S(1)}, u32[]{:S(2)}, u32[]{:S(2)}) %collective-permute-start.12) | collective-permute-done | bytes 64 | tf_op jit(solution)/shard_map/ppermute | solution.py:19
  97.6 4.2 %convolution_bitcast_fusion.1 = f32[128,1024]{0,1:T(8,128)S(1)} fusion(bf16[2688,1024]{1,0:T(8,128)(2,1)} %all-gather.5.cloned.1.call-done, bf16[1,128,2688]{2,1,0:T(8,128)(2,1)S(1)} %copy-done), kind=kOutput, calls=%fused_computation.26 | convolution fusion | flops 704643072 | bytes 6717440 | tf_op jit(solution)/shard_map/dot_general | solution.py:122
  102.8 2.0 copy.71
  104.7 3.2 %copy.60 = bf16[1024,8,128,1]{0,2,3,1:T(8,128)(2,1)S(1)} copy(bf16[1024,8,128,1]{2,1,0,3:T(8,128)(2,1)} %bitcast.120) | data formatting | bytes 4194304 | tf_op jit(solution)/shard_map/reshape | solution.py:176
  108.0 5.7 %fusion.35 = (f32[8,2,128]{2,1,0:T(2,128)S(1)}, f32[8,2,128,1024]{2,3,1,0:T(8,128)}) fusion(pred[128,1024]{0,1:T(8,128)(4,1)S(1)} %compare_and_fusion, bf16[1024,8,128,1]{0,2,3,1:T(8,128)(2,1)S(1)} %copy.60, bf16[128,8,2,128]{0,3,2,1:T(8,128)(2,1)S(1)} %bitcast.124), kind=kOutput, calls=%fused_computation.104 | convolution fusion | flops 547357696 | bytes 11149312 | tf_op jit(solution)/shard_map/sub | solution.py:183
  113.7 5.0 %fusion.36 = (bf16[1024,8,128]{0,2,1:T(8,128)(2,1)S(1)}, f32[1024,8,128]{0,2,1:T(8,128)S(1)}) fusion(bf16[128,8,2,128]{3,2,1,0:T(2,128)(2,1)} %reshape_squeeze.7, f32[128]{0:T(128)S(1)} %get-tuple-element.20, f32[8,2,128,1024]{2,3,1,0:T(8,128)} %get-tuple-element.38, f32[8,2,128]{2,1,0:T(2,128)S(1)} %get-tuple-element.37), kind=kOutput, calls=%fused_computation.105 | convolution fusion | flops 544210944 | bytes 15213056 | tf_op jit(solution)/shard_map/jgtl,tjgd->ljd/dot_general | solution.py:197
  119.8 18.0 %collective-permute-start.21 = (bf16[128,1024]{0,1:T(8,128)(2,1)S(1)}, bf16[128,1024]{0,1:T(8,128)(2,1)S(1)}, u32[]{:S(2)}, u32[]{:S(2)}) collective-permute-start(bf16[128,1024]{0,1:T(8,128)(2,1)S(1)} %copy-done.7), channel_id=1, source_target_pairs={{0,4},{2,6},{4,8},{6,10},{8,12},{10,14},{1,5},{3,7},{5,9},{7,11},{... | collective-permute-start | bytes 786440 | tf_op jit(solution)/shard_map/ppermute | solution.py:41
  140.0 2.6 collective-permute-done.21
  144.3 3.7 %collective-permute-start.24 = (bf16[128,1024]{0,1:T(8,128)(2,1)S(1)}, bf16[128,1024]{0,1:T(8,128)(2,1)S(1)}, u32[]{:S(2)}, u32[]{:S(2)}) collective-permute-start(bf16[128,1024]{0,1:T(8,128)(2,1)S(1)} %copy-done.7), channel_id=1, source_target_pairs={{0,2},{4,6},{8,10},{12,14},{1,3},{5,7},{9,11},{13,15},{16,18},{20,... | collective-permute-start | bytes 786440 | tf_op jit(solution)/shard_map/ppermute | solution.py:43
  154.4 1.9 collective-permute-done.14
  156.3 27.4 %collective-permute-done.20 = bf16[128,1024]{0,1:T(8,128)(2,1)S(1)} collective-permute-done((bf16[128,1024]{0,1:T(8,128)(2,1)S(1)}, bf16[128,1024]{0,1:T(8,128)(2,1)S(1)}, u32[]{:S(2)}, u32[]{:S(2)}) %collective-permute-start.20) | collective-permute-done | bytes 262176 | tf_op jit(solution)/shard_map/ppermute | solution.py:80
  184.1 1.9 fusion.1
  186.1 1.7 fusion.3
  187.9 3.5 %fusion.37 = (bf16[1024,8,128]{0,2,1:T(8,128)(2,1)S(1)}, f32[1024,8,128]{0,2,1:T(8,128)}) fusion(bf16[8,2,128,1024]{2,3,1,0:T(8,128)(2,1)S(1)} %fusion.3, bf16[128,8,2,128]{0,3,2,1:T(8,128)(2,1)S(1)} %bitcast.125), kind=kOutput, calls=%fused_computation.106 | convolution fusion | flops 537919488 | bytes 11010048 | tf_op jit(solution)/shard_map/jgtl,tjgd->ljd/dot_general | solution.py:193
  191.3 1.4 fusion.33
  192.8 1.8 copy.51
  194.6 1.3 collective-permute-start.31
  195.9 1.8 copy.49
  197.7 1.4 collective-permute-start.30
  199.3 1.8 bitcast_convert_fusion
  201.1 2.0 copy.52
  203.1 2.4 convolution_multiply_fusion
  205.5 1.9 add_convert_fusion.3
  207.4 1.4 collective-permute-start.32
  210.3 2.0 copy.50
  212.3 1.8 copy.47
  214.1 1.4 collective-permute-start.29
  215.5 1.8 copy.46
  217.3 1.4 collective-permute-start.28
  219.5 3.4 %collective-permute-start.40 = (f32[16,1024]{1,0:T(8,128)S(1)}, f32[16,1024]{1,0:T(8,128)S(1)}, u32[]{:S(2)}, u32[]{:S(2)}) collective-permute-start(f32[16,1024]{1,0:T(8,128)S(1)} %add.215), channel_id=1, source_target_pairs={{0,2},{2,0},{4,6},{6,4},{8,10},{10,8},{12,14},{14,12},{1,3},{3,1},... | collective-permute-start | bytes 196616 | tf_op jit(solution)/shard_map/ppermute | solution.py:19
  224.0 2.0 add_convert_fusion.2
  226.0 1.4 collective-permute-start.33
  227.3 5.3 %fusion.11 = bf16[1,128,2688]{2,1,0:T(8,128)(2,1)} fusion(f32[128,2688]{1,0:T(8,128)S(1)} %copy-done.3, bf16[128,1024]{0,1:T(8,128)(2,1)S(1)} %fusion.26, bf16[2688,1024]{1,0:T(8,128)(2,1)} %all-gather.5.cloned.1.call-done), kind=kOutput, calls=%fused_computation.19 | convolution fusion | flops 705331200 | bytes 7831552 | tf_op jit(solution)/shard_map/tk,dk->td/dot_general | solution.py:222
  232.7 10.9 %collective-permute-start.41 = (f32[16,1024]{1,0:T(8,128)S(1)}, f32[16,1024]{1,0:T(8,128)}, u32[]{:S(2)}, u32[]{:S(2)}) collective-permute-start(f32[16,1024]{1,0:T(8,128)S(1)} %add.216), channel_id=1, source_target_pairs={{0,4},{2,6},{4,0},{6,2},{8,12},{10,14},{12,8},{14,10},{1,5},{3,7},... | collective-permute-start | bytes 196616 | tf_op jit(solution)/shard_map/ppermute | solution.py:19
  247.4 9.9 %collective-permute-start.42 = (f32[16,1024]{1,0:T(8,128)S(1)}, f32[16,1024]{1,0:T(8,128)}, u32[]{:S(2)}, u32[]{:S(2)}) collective-permute-start(f32[16,1024]{1,0:T(8,128)S(1)} %add.217), channel_id=1, source_target_pairs={{0,8},{2,10},{4,12},{6,14},{8,0},{10,2},{12,4},{14,6},{1,9},{3,11}... | collective-permute-start | bytes 196616 | tf_op jit(solution)/shard_map/ppermute | solution.py:19
  258.4 2.9 %collective-permute-start.38 = (f32[2688,16]{0,1:T(8,128)S(1)}, f32[2688,16]{0,1:T(8,128)}, u32[]{:S(2)}, u32[]{:S(2)}) collective-permute-start(f32[2688,16]{0,1:T(8,128)S(1)} %add.213), channel_id=1, source_target_pairs={{0,8},{2,10},{4,12},{6,14},{8,0},{10,2},{12,4},{14,6},{1,9},{3,11}... | collective-permute-start | bytes 516104 | tf_op jit(solution)/shard_map/ppermute | solution.py:19
  261.3 1.8 add_convert_fusion.1
  264.4 3.0 %convolution_convert_fusion = bf16[8,128,2,128]{3,1,2,0:T(8,128)(2,1)S(1)} fusion(bf16[1024,8,128,1]{0,2,3,1:T(8,128)(2,1)S(1)} %copy.60, bf16[8,2,128,1024]{2,3,1,0:T(8,128)(2,1)} %copy-done.1), kind=kOutput, calls=%fused_computation.24 | convolution fusion | flops 537133056 | bytes 6815744 | tf_op jit(solution)/shard_map/jgtl,ljd->tjgd/dot_general | solution.py:190
  269.7 1.5 add.218
  271.2 1.6 add.214
  273.2 1.8 fusion.30
  (173 shorter events, 37.7 us)
Async XLA Ops:
  7.2 71.5 %copy-start = (bf16[1,128,2688]{2,1,0:T(8,128)(2,1)S(1)}, bf16[1,128,2688]{2,1,0:T(8,128)(2,1)}, u32[]{:S(2)}) copy-start(bf16[1,128,2688]{2,1,0:T(8,128)(2,1)} %param.10) | copy-start | bytes 2064388
  7.2 71.5 %copy-start.12 = (bf16[2688,16]{0,1:T(8,128)(2,1)S(1)}, bf16[2688,16]{0,1:T(8,128)(2,1)}, u32[]{:S(2)}) copy-start(bf16[2688,16]{0,1:T(8,128)(2,1)} %param.14) | copy-start | bytes 258052
  7.2 62.4 %all-gather.3.cloned.1.call-start = ((), (), s32[]{:S(2)}) async-start(), calls=%async_computation | async-start | bytes 3096576 | tf_op jit(solution)/shard_map/all_gather | solution.py:116
  9.1 69.9 %copy-start.9 = (bf16[1,128,2048]{2,1,0:T(8,128)(2,1)S(1)}, bf16[1,128,2048]{2,1,0:T(8,128)(2,1)}, u32[]{:S(2)}) copy-start(bf16[1,128,2048]{2,1,0:T(8,128)(2,1)} %param.16) | copy-start | bytes 1572868
  9.1 88.4 %all-gather.5.cloned.1.call-start = ((), (), s32[]{:S(2)}) async-start(), calls=%async_computation.1 | async-start | bytes 8257536 | tf_op jit(solution)/shard_map/all_gather | solution.py:117
  69.6 20.8 %collective-permute-start.3 = (bf16[128,1024]{1,0:T(8,128)(2,1)}, bf16[128,1024]{1,0:T(8,128)(2,1)S(1)}, u32[]{:S(2)}, u32[]{:S(2)}) collective-permute-start(bf16[128,1024]{1,0:T(8,128)(2,1)} %bitcast.3), channel_id=1, source_target_pairs={{0,4},{2,6},{4,8},{6,10},{8,12},{10,14},{1,5},{3,7},{5,9},{7,11},{... | collective-permute-start | bytes 786440 | tf_op jit(solution)/shard_map/ppermute | solution.py:41
  73.2 22.3 %collective-permute-start.6 = (bf16[128,1024]{1,0:T(8,128)(2,1)}, bf16[128,1024]{1,0:T(8,128)(2,1)}, u32[]{:S(2)}, u32[]{:S(2)}) collective-permute-start(bf16[128,1024]{1,0:T(8,128)(2,1)} %bitcast.3), channel_id=1, source_target_pairs={{0,2},{4,6},{8,10},{12,14},{1,3},{5,7},{9,11},{13,15},{16,18},{20,... | collective-permute-start | bytes 786440 | tf_op jit(solution)/shard_map/ppermute | solution.py:43
  76.5 4.0 %collective-permute-start = (f32[8]{0:T(128)S(1)}, f32[8]{0:T(128)S(1)}, u32[]{:S(2)}, u32[]{:S(2)}) collective-permute-start(f32[8]{0:T(128)S(1)} %get-tuple-element.21), channel_id=1, source_target_pairs={{0,2},{2,0},{4,6},{6,4},{8,10},{10,8},{12,14},{14,12},{1,3},{3,1},... | collective-permute-start | bytes 104 | tf_op jit(solution)/shard_map/ppermute | solution.py:19
  76.6 5.0 %collective-permute-start.10 = (f32[8]{0:T(128)S(1)}, f32[8]{0:T(128)S(1)}, u32[]{:S(2)}, u32[]{:S(2)}) collective-permute-start(f32[8]{0:T(128)S(1)} %get-tuple-element.22), channel_id=1, source_target_pairs={{0,2},{2,0},{4,6},{6,4},{8,10},{10,8},{12,14},{14,12},{1,3},{3,1},... | collective-permute-start | bytes 104 | tf_op jit(solution)/shard_map/ppermute | solution.py:19
  80.5 3.6 %collective-permute-start.1 = (f32[8]{0:T(128)S(1)}, f32[8]{0:T(128)S(1)}, u32[]{:S(2)}, u32[]{:S(2)}) collective-permute-start(f32[8]{0:T(128)S(1)} %add.187), channel_id=1, source_target_pairs={{0,4},{2,6},{4,0},{6,2},{8,12},{10,14},{12,8},{14,10},{1,5},{3,7},... | collective-permute-start | bytes 104 | tf_op jit(solution)/shard_map/ppermute | solution.py:19
  81.6 4.2 %collective-permute-start.11 = (f32[8]{0:T(128)S(1)}, f32[8]{0:T(128)S(1)}, u32[]{:S(2)}, u32[]{:S(2)}) collective-permute-start(f32[8]{0:T(128)S(1)} %add.192), channel_id=1, source_target_pairs={{0,4},{2,6},{4,0},{6,2},{8,12},{10,14},{12,8},{14,10},{1,5},{3,7},... | collective-permute-start | bytes 104 | tf_op jit(solution)/shard_map/ppermute | solution.py:19
  84.1 6.1 %collective-permute-start.2 = (f32[8]{0:T(128)S(1)}, f32[8]{0:T(128)S(1)}, u32[]{:S(2)}, u32[]{:S(2)}) collective-permute-start(f32[8]{0:T(128)S(1)} %add.188), channel_id=1, source_target_pairs={{0,8},{2,10},{4,12},{6,14},{8,0},{10,2},{12,4},{14,6},{1,9},{3,11}... | collective-permute-start | bytes 104 | tf_op jit(solution)/shard_map/ppermute | solution.py:19
  85.8 4.4 %collective-permute-start.12 = (f32[8]{0:T(128)S(1)}, f32[8]{0:T(128)S(1)}, u32[]{:S(2)}, u32[]{:S(2)}) collective-permute-start(f32[8]{0:T(128)S(1)} %add.193), channel_id=1, source_target_pairs={{0,8},{2,10},{4,12},{6,14},{8,0},{10,2},{12,4},{14,6},{1,9},{3,11}... | collective-permute-start | bytes 104 | tf_op jit(solution)/shard_map/ppermute | solution.py:19
  90.2 1.1 collective-permute-start.13
  90.4 1.0 collective-permute-start.4
  91.5 3.3 %collective-permute-start.5 = (bf16[128,1024]{1,0:T(8,128)(2,1)S(1)}, bf16[128,1024]{1,0:T(8,128)(2,1)S(1)}, u32[]{:S(2)}, u32[]{:S(2)}) collective-permute-start(bf16[128,1024]{1,0:T(8,128)(2,1)S(1)} %collective-permute-done.4), channel_id=1, source_target_pairs={{8,12},{10,14},{9,13},{11,15},{24,28},{26,30},{25,29},{27,31}} | collective-permute-start | bytes 786440 | tf_op jit(solution)/shard_map/ppermute | solution.py:41
  93.3 3.1 %collective-permute-start.7 = (bf16[128,1024]{1,0:T(8,128)(2,1)}, bf16[128,1024]{1,0:T(8,128)(2,1)S(1)}, u32[]{:S(2)}, u32[]{:S(2)}) collective-permute-start(bf16[128,1024]{1,0:T(8,128)(2,1)} %copy-done.14), channel_id=1, source_target_pairs={{6,4},{4,6},{10,8},{8,10},{14,12},{12,14},{7,5},{5,7},{11,9},{9,11... | collective-permute-start | bytes 786440 | tf_op jit(solution)/shard_map/ppermute | solution.py:46
  94.0 2.5 collective-permute-start.8
  94.8 1.8 collective-permute-start.9
  119.1 19.4 %collective-permute-start.17 = (bf16[128,1024]{0,1:T(8,128)(2,1)S(1)}, bf16[128,1024]{0,1:T(8,128)(2,1)S(1)}, u32[]{:S(2)}, u32[]{:S(2)}) collective-permute-start(bf16[128,1024]{0,1:T(8,128)(2,1)S(1)} %bitcast.133), channel_id=1, source_target_pairs={{12,14},{14,12},{13,15},{15,13},{28,30},{30,28},{29,31},{31,29}} | collective-permute-start | bytes 786440 | tf_op jit(solution)/shard_map/ppermute | solution.py:72
  119.8 22.8 %collective-permute-start.21 = (bf16[128,1024]{0,1:T(8,128)(2,1)S(1)}, bf16[128,1024]{0,1:T(8,128)(2,1)S(1)}, u32[]{:S(2)}, u32[]{:S(2)}) collective-permute-start(bf16[128,1024]{0,1:T(8,128)(2,1)S(1)} %copy-done.7), channel_id=1, source_target_pairs={{0,4},{2,6},{4,8},{6,10},{8,12},{10,14},{1,5},{3,7},{5,9},{7,11},{... | collective-permute-start | bytes 786440 | tf_op jit(solution)/shard_map/ppermute | solution.py:41
  137.8 5.5 %collective-permute-start.16 = (bf16[128,1024]{0,1:T(8,128)(2,1)S(1)}, bf16[128,1024]{0,1:T(8,128)(2,1)S(1)}, u32[]{:S(2)}, u32[]{:S(2)}) collective-permute-start(bf16[128,1024]{0,1:T(8,128)(2,1)S(1)} %bitcast.132), channel_id=1, source_target_pairs={{8,10},{10,8},{12,14},{14,12},{9,11},{11,9},{13,15},{15,13},{24,26... | collective-permute-start | bytes 786440 | tf_op jit(solution)/shard_map/ppermute | solution.py:72
  138.6 4.7 %collective-permute-start.18 = (bf16[128,1024]{0,1:T(8,128)(2,1)S(1)}, bf16[128,1024]{0,1:T(8,128)(2,1)S(1)}, u32[]{:S(2)}, u32[]{:S(2)}) collective-permute-start(bf16[128,1024]{0,1:T(8,128)(2,1)S(1)} %fusion.21), channel_id=1, source_target_pairs={{12,8},{14,10},{13,9},{15,11},{28,24},{30,26},{29,25},{31,27}} | collective-permute-start | bytes 786440 | tf_op jit(solution)/shard_map/ppermute | solution.py:80
  139.3 10.9 %collective-permute-start.15 = (bf16[128,1024]{0,1:T(8,128)(2,1)S(1)}, bf16[128,1024]{0,1:T(8,128)(2,1)S(1)}, u32[]{:S(2)}, u32[]{:S(2)}) collective-permute-start(bf16[128,1024]{0,1:T(8,128)(2,1)S(1)} %bitcast.131), channel_id=1, source_target_pairs={{4,6},{6,4},{8,10},{10,8},{12,14},{14,12},{5,7},{7,5},{9,11},{11,9... | collective-permute-start | bytes 786440 | tf_op jit(solution)/shard_map/ppermute | solution.py:72
  142.6 6.8 %collective-permute-start.22 = (bf16[128,1024]{0,1:T(8,128)(2,1)S(1)}, bf16[128,1024]{0,1:T(8,128)(2,1)S(1)}, u32[]{:S(2)}, u32[]{:S(2)}) collective-permute-start(bf16[128,1024]{0,1:T(8,128)(2,1)S(1)} %collective-permute-done.21), channel_id=1, source_target_pairs={{4,8},{6,10},{8,12},{10,14},{5,9},{7,11},{9,13},{11,15},{20,24},{2... | collective-permute-start | bytes 786440 | tf_op jit(solution)/shard_map/ppermute | solution.py:41
  143.5 7.4 %collective-permute-start.19 = (bf16[128,1024]{0,1:T(8,128)(2,1)S(1)}, bf16[128,1024]{0,1:T(8,128)(2,1)S(1)}, u32[]{:S(2)}, u32[]{:S(2)}) collective-permute-start(bf16[128,1024]{0,1:T(8,128)(2,1)S(1)} %fusion.23), channel_id=1, source_target_pairs={{8,4},{10,6},{12,8},{14,10},{9,5},{11,7},{13,9},{15,11},{24,20},{2... | collective-permute-start | bytes 786440 | tf_op jit(solution)/shard_map/ppermute | solution.py:80
  144.3 8.8 %collective-permute-start.24 = (bf16[128,1024]{0,1:T(8,128)(2,1)S(1)}, bf16[128,1024]{0,1:T(8,128)(2,1)S(1)}, u32[]{:S(2)}, u32[]{:S(2)}) collective-permute-start(bf16[128,1024]{0,1:T(8,128)(2,1)S(1)} %copy-done.7), channel_id=1, source_target_pairs={{0,2},{4,6},{8,10},{12,14},{1,3},{5,7},{9,11},{13,15},{16,18},{20,... | collective-permute-start | bytes 786440 | tf_op jit(solution)/shard_map/ppermute | solution.py:43
  148.0 8.3 %collective-permute-start.14 = (bf16[128,1024]{0,1:T(8,128)(2,1)S(1)}, bf16[128,1024]{0,1:T(8,128)(2,1)S(1)}, u32[]{:S(2)}, u32[]{:S(2)}) collective-permute-start(bf16[128,1024]{0,1:T(8,128)(2,1)S(1)} %bitcast.130), channel_id=1, source_target_pairs={{2,0},{6,4},{10,8},{14,12},{3,1},{7,5},{11,9},{15,13},{18,16},{22,... | collective-permute-start | bytes 786440 | tf_op jit(solution)/shard_map/ppermute | solution.py:69
  149.4 2.3 collective-permute-start.23
  150.2 4.0 %collective-permute-start.25 = (bf16[128,1024]{0,1:T(8,128)(2,1)S(1)}, bf16[128,1024]{0,1:T(8,128)(2,1)S(1)}, u32[]{:S(2)}, u32[]{:S(2)}) collective-permute-start(bf16[128,1024]{0,1:T(8,128)(2,1)S(1)} %collective-permute-done.21), channel_id=1, source_target_pairs={{6,4},{4,6},{10,8},{8,10},{14,12},{12,14},{7,5},{5,7},{11,9},{9,11... | collective-permute-start | bytes 786440 | tf_op jit(solution)/shard_map/ppermute | solution.py:46
  150.9 3.4 %collective-permute-start.26 = (bf16[128,1024]{0,1:T(8,128)(2,1)S(1)}, bf16[128,1024]{0,1:T(8,128)(2,1)S(1)}, u32[]{:S(2)}, u32[]{:S(2)}) collective-permute-start(bf16[128,1024]{0,1:T(8,128)(2,1)S(1)} %collective-permute-done.22), channel_id=1, source_target_pairs={{10,8},{8,10},{14,12},{12,14},{11,9},{9,11},{15,13},{13,15},{26,24... | collective-permute-start | bytes 786440 | tf_op jit(solution)/shard_map/ppermute | solution.py:46
  151.7 32.0 %collective-permute-start.20 = (bf16[128,1024]{0,1:T(8,128)(2,1)S(1)}, bf16[128,1024]{0,1:T(8,128)(2,1)S(1)}, u32[]{:S(2)}, u32[]{:S(2)}) collective-permute-start(bf16[128,1024]{0,1:T(8,128)(2,1)S(1)} %fusion.25), channel_id=1, source_target_pairs={{4,0},{6,2},{8,4},{10,6},{12,8},{14,10},{5,1},{7,3},{9,5},{11,7},{... | collective-permute-start | bytes 786440 | tf_op jit(solution)/shard_map/ppermute | solution.py:80
  153.1 30.8 %collective-permute-start.27 = (bf16[128,1024]{0,1:T(8,128)(2,1)S(1)}, bf16[128,1024]{0,1:T(8,128)(2,1)S(1)}, u32[]{:S(2)}, u32[]{:S(2)}) collective-permute-start(bf16[128,1024]{0,1:T(8,128)(2,1)S(1)} %collective-permute-done.23), channel_id=1, source_target_pairs={{14,12},{12,14},{15,13},{13,15},{30,28},{28,30},{31,29},{29,31}} | collective-permute-start | bytes 786440 | tf_op jit(solution)/shard_map/ppermute | solution.py:46
  194.6 11.0 %collective-permute-start.31 = (bf16[128,1024]{1,0:T(8,128)(2,1)}, bf16[128,1024]{1,0:T(8,128)(2,1)}, u32[]{:S(2)}, u32[]{:S(2)}) collective-permute-start(bf16[128,1024]{1,0:T(8,128)(2,1)} %copy.51), channel_id=1, source_target_pairs={{12,14},{14,12},{13,15},{15,13},{28,30},{30,28},{29,31},{31,29}} | collective-permute-start | bytes 786440 | tf_op jit(solution)/shard_map/ppermute | solution.py:72
  197.7 26.2 %collective-permute-start.30 = (bf16[128,1024]{1,0:T(8,128)(2,1)}, bf16[128,1024]{1,0:T(8,128)(2,1)}, u32[]{:S(2)}, u32[]{:S(2)}) collective-permute-start(bf16[128,1024]{1,0:T(8,128)(2,1)} %copy.49), channel_id=1, source_target_pairs={{8,10},{10,8},{12,14},{14,12},{9,11},{11,9},{13,15},{15,13},{24,26... | collective-permute-start | bytes 786440 | tf_op jit(solution)/shard_map/ppermute | solution.py:72
  207.4 16.6 %collective-permute-start.32 = (bf16[128,1024]{1,0:T(8,128)(2,1)}, bf16[128,1024]{1,0:T(8,128)(2,1)}, u32[]{:S(2)}, u32[]{:S(2)}) collective-permute-start(bf16[128,1024]{1,0:T(8,128)(2,1)} %add_convert_fusion.3), channel_id=1, source_target_pairs={{12,8},{14,10},{13,9},{15,11},{28,24},{30,26},{29,25},{31,27}} | collective-permute-start | bytes 786440 | tf_op jit(solution)/shard_map/ppermute | solution.py:80
  208.9 10.6 %collective-permute-start.35 = (f32[2688,16]{0,1:T(8,128)S(1)}, f32[2688,16]{0,1:T(8,128)}, u32[]{:S(2)}, u32[]{:S(2)}) collective-permute-start(f32[2688,16]{0,1:T(8,128)S(1)} %fusion.12), channel_id=1, source_target_pairs={{0,1},{1,0},{2,3},{3,2},{4,5},{5,4},{6,7},{7,6},{8,9},{9,8},{10,11... | collective-permute-start | bytes 516104 | tf_op jit(solution)/shard_map/ppermute | solution.py:19
  208.9 8.3 %collective-permute-start.39 = (f32[16,1024]{1,0:T(8,128)S(1)}, f32[16,1024]{1,0:T(8,128)}, u32[]{:S(2)}, u32[]{:S(2)}) collective-permute-start(f32[16,1024]{1,0:T(8,128)S(1)} %convolution_multiply_fusion.3), channel_id=1, source_target_pairs={{0,1},{1,0},{2,3},{3,2},{4,5},{5,4},{6,7},{7,6},{8,9},{9,8},{10,11... | collective-permute-start | bytes 196616 | tf_op jit(solution)/shard_map/ppermute | solution.py:19
  214.1 47.2 %collective-permute-start.29 = (bf16[128,1024]{1,0:T(8,128)(2,1)}, bf16[128,1024]{1,0:T(8,128)(2,1)}, u32[]{:S(2)}, u32[]{:S(2)}) collective-permute-start(bf16[128,1024]{1,0:T(8,128)(2,1)} %copy.47), channel_id=1, source_target_pairs={{4,6},{6,4},{8,10},{10,8},{12,14},{14,12},{5,7},{7,5},{9,11},{11,9... | collective-permute-start | bytes 786440 | tf_op jit(solution)/shard_map/ppermute | solution.py:72
  217.3 55.6 %collective-permute-start.28 = (bf16[128,1024]{1,0:T(8,128)(2,1)}, bf16[128,1024]{1,0:T(8,128)(2,1)}, u32[]{:S(2)}, u32[]{:S(2)}) collective-permute-start(bf16[128,1024]{1,0:T(8,128)(2,1)} %copy.46), channel_id=1, source_target_pairs={{2,0},{6,4},{10,8},{14,12},{3,1},{7,5},{11,9},{15,13},{18,16},{22,... | collective-permute-start | bytes 786440 | tf_op jit(solution)/shard_map/ppermute | solution.py:69
  219.5 13.1 %collective-permute-start.40 = (f32[16,1024]{1,0:T(8,128)S(1)}, f32[16,1024]{1,0:T(8,128)S(1)}, u32[]{:S(2)}, u32[]{:S(2)}) collective-permute-start(f32[16,1024]{1,0:T(8,128)S(1)} %add.215), channel_id=1, source_target_pairs={{0,2},{2,0},{4,6},{6,4},{8,10},{10,8},{12,14},{14,12},{1,3},{3,1},... | collective-permute-start | bytes 196616 | tf_op jit(solution)/shard_map/ppermute | solution.py:19
  223.9 19.7 %collective-permute-start.36 = (f32[2688,16]{0,1:T(8,128)S(1)}, f32[2688,16]{0,1:T(8,128)S(1)}, u32[]{:S(2)}, u32[]{:S(2)}) collective-permute-start(f32[2688,16]{0,1:T(8,128)S(1)} %add.211), channel_id=1, source_target_pairs={{0,2},{2,0},{4,6},{6,4},{8,10},{10,8},{12,14},{14,12},{1,3},{3,1},... | collective-permute-start | bytes 516104 | tf_op jit(solution)/shard_map/ppermute | solution.py:19
  226.0 35.3 %collective-permute-start.33 = (bf16[128,1024]{1,0:T(8,128)(2,1)}, bf16[128,1024]{1,0:T(8,128)(2,1)}, u32[]{:S(2)}, u32[]{:S(2)}) collective-permute-start(bf16[128,1024]{1,0:T(8,128)(2,1)} %add_convert_fusion.2), channel_id=1, source_target_pairs={{8,4},{10,6},{12,8},{14,10},{9,5},{11,7},{13,9},{15,11},{24,20},{2... | collective-permute-start | bytes 786440 | tf_op jit(solution)/shard_map/ppermute | solution.py:80
  232.7 13.8 %collective-permute-start.41 = (f32[16,1024]{1,0:T(8,128)S(1)}, f32[16,1024]{1,0:T(8,128)}, u32[]{:S(2)}, u32[]{:S(2)}) collective-permute-start(f32[16,1024]{1,0:T(8,128)S(1)} %add.216), channel_id=1, source_target_pairs={{0,4},{2,6},{4,0},{6,2},{8,12},{10,14},{12,8},{14,10},{1,5},{3,7},... | collective-permute-start | bytes 196616 | tf_op jit(solution)/shard_map/ppermute | solution.py:19
  243.6 13.7 %collective-permute-start.37 = (f32[2688,16]{0,1:T(8,128)S(1)}, f32[2688,16]{0,1:T(8,128)}, u32[]{:S(2)}, u32[]{:S(2)}) collective-permute-start(f32[2688,16]{0,1:T(8,128)S(1)} %add.212), channel_id=1, source_target_pairs={{0,4},{2,6},{4,0},{6,2},{8,12},{10,14},{12,8},{14,10},{1,5},{3,7},... | collective-permute-start | bytes 516104 | tf_op jit(solution)/shard_map/ppermute | solution.py:19
  247.4 22.3 %collective-permute-start.42 = (f32[16,1024]{1,0:T(8,128)S(1)}, f32[16,1024]{1,0:T(8,128)}, u32[]{:S(2)}, u32[]{:S(2)}) collective-permute-start(f32[16,1024]{1,0:T(8,128)S(1)} %add.217), channel_id=1, source_target_pairs={{0,8},{2,10},{4,12},{6,14},{8,0},{10,2},{12,4},{14,6},{1,9},{3,11}... | collective-permute-start | bytes 196616 | tf_op jit(solution)/shard_map/ppermute | solution.py:19
  258.4 12.9 %collective-permute-start.38 = (f32[2688,16]{0,1:T(8,128)S(1)}, f32[2688,16]{0,1:T(8,128)}, u32[]{:S(2)}, u32[]{:S(2)}) collective-permute-start(f32[2688,16]{0,1:T(8,128)S(1)} %add.213), channel_id=1, source_target_pairs={{0,8},{2,10},{4,12},{6,14},{8,0},{10,2},{12,4},{14,6},{1,9},{3,11}... | collective-permute-start | bytes 516104 | tf_op jit(solution)/shard_map/ppermute | solution.py:19
  263.1 10.1 %collective-permute-start.34 = (bf16[128,1024]{1,0:T(8,128)(2,1)}, bf16[128,1024]{1,0:T(8,128)(2,1)}, u32[]{:S(2)}, u32[]{:S(2)}) collective-permute-start(bf16[128,1024]{1,0:T(8,128)(2,1)} %add_convert_fusion.1), channel_id=1, source_target_pairs={{4,0},{6,2},{8,4},{10,6},{12,8},{14,10},{5,1},{7,3},{9,5},{11,7},{... | collective-permute-start | bytes 786440 | tf_op jit(solution)/shard_map/ppermute | solution.py:80
  (16 other events, 373.2 us)
Sparse Core Ops, SparseCore 0:
  10.8 58.7 all-gather.2
  71.1 14.1 all-gather.4

commit v5 on v4

--- a/solution.py
+++ b/solution.py
@@ -129,7 +129,8 @@
     log_gap = policy_logprob[0] - reference_logprob[0]
     part_diff = jnp.sum(seg_table * log_gap[:, None], 0)
     part_count = jnp.sum(seg_table, 0)
-    own_diff, counts = butterfly_sum((part_diff, part_count), ("ctx",))
+    both_sums = butterfly_sum(jnp.concatenate([part_diff, part_count], 0), ("ctx",))
+    own_diff, counts = both_sums[:SEGS], both_sums[SEGS:]
     other_diff = from_partner(own_diff, "pair", 0)
     direction = 1.0 - 2.0 * pair_index.astype(jnp.float32)
     margin = DPO_BETA * (direction * (own_diff - other_diff))
@@ -203,8 +204,10 @@
         slot_rows = lambda parts: [
             parts[k * tok_rows : (k + 1) * tok_rows].astype(jnp.bfloat16) for k in range(halo_blocks)
         ]
-        key_total = key_total + tree_return(slot_rows(key_parts), levels)
-        value_total = value_total + tree_return(slot_rows(value_parts), levels)
+        joined = jnp.concatenate([key_parts, value_parts], 1)
+        returned = tree_return(slot_rows(joined), levels)
+        key_total = key_total + returned[:, :width_kv]
+        value_total = value_total + returned[:, width_kv:]
     else:
         for distance in range(1, halo_blocks + 1):
             block_start = (halo_blocks - distance) * tok_rows
@@ -229,7 +232,11 @@
     down_factor = ADAPTER_SCALE * jnp.einsum(
         "td,tr->dr", hidden_rows, rank_middle, preferred_element_type=jnp.float32
     )
-    down_gradient, up_gradient = butterfly_sum((down_factor, up_factor), ("pair", "ctx"))
+    down_size = down_factor.size
+    flat = jnp.concatenate([down_factor.reshape(-1), up_factor.reshape(-1)], 0)
+    flat = butterfly_sum(flat.reshape(-1, HEAD_SIZE), ("pair", "ctx")).reshape(-1)
+    down_gradient = flat[:down_size].reshape(down_factor.shape)
+    up_gradient = flat[down_size:].reshape(up_factor.shape)
     return (input_grad[None], query_grad[None], key_grad[None], down_gradient, up_gradient)
 
 

time: 283 us -> 299 us (1.057)
  waiting for transfers between devices: 98.2 us -> 144 us
  starting transfers between devices: 86.2 us -> 54.4 us
  other arithmetic: 20.7 us -> 9.33 us
  local copies, waits for them, and re-layouts: 29 us -> 37.9 us
  matrix products: 32.8 us -> 37.6 us
    ppermute x6 -> x3, waiting for transfers between devices: 27.7 us -> 57.5 us  [tree_return(): lax.ppermute(acc.astype(jnp.bfloat16), 'ctx', [(c, c - 2) for c in range(...]
    ppermute x15 -> x8, starting transfers between devices: 35.1 us -> 9.14 us  [from_partner(): lax.ppermute(shard, axis, [(i, i ^ 1 << stride) for i in range(lax.axis_s...]
    ppermute x15 -> x8, waiting for transfers between devices: 5.44 us -> 18.2 us  [from_partner(): lax.ppermute(shard, axis, [(i, i ^ 1 << stride) for i in range(lax.axis_s...]
    convert_element_type x7 -> x0, local copies, waits for them, and re-layouts: 12.5 us -> none  [the longest x4 7.16 us: shards(): parts[k * tok_rows:(k + 1) * tok_rows].astype(jnp.bfloat16)]
    reshape x0 -> x5, local copies, waits for them, and re-layouts: none -> 10.7 us  [the longest x1 4.61 us: shards(): key_parts = jnp.einsum('jgtl,tjgd->ljd', score_grad, query_rows, preferre...]
    unnamed x54 -> x50, local copies, waits for them, and re-layouts: 5.7 us -> 14.4 us
    ppermute x2 -> x1, waiting for transfers between devices: 1.86 us -> 7.88 us  [tree_return(): lax.ppermute(crossed[0], 'ctx', [(c, c - 1) for c in range(1, count, 2)])]
    add x14 -> x7, other arithmetic: 6.83 us -> 1.87 us  [butterfly_sum(): parts = jax.tree.map(jnp.add, parts, got)]
  transfers between devices with their start and end apart: 45 -> 31, of which waited for: 9 -> 11; matrix products, arithmetic and copies ran while one was open for 17% -> 18% of each run, Pallas kernels for 0% -> 0%
where the time goes in v5:
time: 299 us; the launch traced here: 298 us
  waiting for transfers between devices  144 us (48%)
  starting transfers between devices  54.4 us (18%)
  local copies, waits for them, and re-layouts  37.9 us (13%)
  matrix products  37.6 us (13%)
  between operations  14.9 us (5%)
  other arithmetic  9.33 us (3%)
    all_gather x1, waiting for transfers between devices, shards(): rows_half = lax.all_gather(own_half, 'ctx', axis=0, tiled=True)  60.4 us
    ppermute x3, waiting for transfers between devices, tree_return(): lax.ppermute(acc.astype(jnp.bfloat16), 'ctx', [(c, c - 2) for c in range(...  57.5 us
    ppermute x6, starting transfers between devices, tree_spread(): lax.ppermute(held, 'ctx', [(c - 2, c) for c in range(2 * step, count)])  26.6 us
    ppermute x8, waiting for transfers between devices, from_partner(): lax.ppermute(shard, axis, [(i, i ^ 1 << stride) for i in range(lax.axis_s...  18.2 us
    unnamed x50, local copies, waits for them, and re-layouts  14.4 us
    ppermute x8, starting transfers between devices, from_partner(): lax.ppermute(shard, axis, [(i, i ^ 1 << stride) for i in range(lax.axis_s...  9.14 us
    ppermute x1, waiting for transfers between devices, tree_return(): lax.ppermute(crossed[0], 'ctx', [(c, c - 1) for c in range(1, count, 2)])  7.88 us
    ppermute x2, starting transfers between devices, tree_spread(): lax.ppermute(block, 'ctx', [(c - 1, c) for c in range(1, count, 2)])  7.56 us
  transfers between devices with their start and end apart: 31, of which 11 were waited for; matrix products, arithmetic and copies ran while one was open for 18% of the time, Pallas kernels for 0%

profile of v5, /device:TPU:0, one launch (start us, length us, event | category | flops | bytes accessed | tf_op | source)
XLA Modules:
  0.0 298.1 jit_solution(16142563103868533421)
XLA Ops:
  7.3 1.8 constant_dynamic-slice_fusion
  9.2 60.4 %all-gather.3.cloned.1.call-done = bf16[2688,512]{1,0:T(8,128)(2,1)} async-done(((bf16[336,512]{1,0:T(8,128)(2,1)}), bf16[2688,512]{1,0:T(8,128)(2,1)}) %all-gather.3.cloned.1.call-update) | async-done | bytes 2752528 | tf_op jit(solution)/shard_map/all_gather | solution.py:116
  69.6 3.5 %collective-permute-start.3 = (bf16[128,1024]{1,0:T(8,128)(2,1)}, bf16[128,1024]{1,0:T(8,128)(2,1)S(1)}, u32[]{:S(2)}, u32[]{:S(2)}) collective-permute-start(bf16[128,1024]{1,0:T(8,128)(2,1)} %bitcast.4), channel_id=1, source_target_pairs={{0,4},{2,6},{4,8},{6,10},{8,12},{10,14},{1,5},{3,7},{5,9},{7,11},{... | collective-permute-start | bytes 786440 | tf_op jit(solution)/shard_map/ppermute | solution.py:41
  73.2 3.2 %collective-permute-start.6 = (bf16[128,1024]{1,0:T(8,128)(2,1)}, bf16[128,1024]{1,0:T(8,128)(2,1)}, u32[]{:S(2)}, u32[]{:S(2)}) collective-permute-start(bf16[128,1024]{1,0:T(8,128)(2,1)} %bitcast.4), channel_id=1, source_target_pairs={{0,2},{4,6},{8,10},{12,14},{1,3},{5,7},{9,11},{13,15},{16,18},{20,... | collective-permute-start | bytes 786440 | tf_op jit(solution)/shard_map/ppermute | solution.py:43
  77.4 2.7 collective-permute-done
  80.2 1.4 collective-permute-start.1
  81.6 1.2 reshape_squeeze.7
  83.8 2.1 collective-permute-start.2
  85.8 2.4 collective-permute-done.2
  89.6 1.4 collective-permute-start.5
  93.5 1.4 collective-permute-start.9
  97.0 4.2 %convolution_bitcast_fusion = f32[128,1024]{0,1:T(8,128)S(1)} fusion(bf16[2688,1024]{1,0:T(8,128)(2,1)} %all-gather.5.cloned.1.call-done, bf16[1,128,2688]{2,1,0:T(8,128)(2,1)S(1)} %copy-done), kind=kOutput, calls=%fused_computation.24 | convolution fusion | flops 704643072 | bytes 6717440 | tf_op jit(solution)/shard_map/dot_general | solution.py:122
  102.2 18.3 %collective-permute-start.11 = (bf16[128,1024]{0,1:T(8,128)(2,1)}, bf16[128,1024]{0,1:T(8,128)(2,1)}, u32[]{:S(2)}, u32[]{:S(2)}) collective-permute-start(bf16[128,1024]{0,1:T(8,128)(2,1)} %fusion.14), channel_id=1, source_target_pairs={{0,4},{2,6},{4,8},{6,10},{8,12},{10,14},{1,5},{3,7},{5,9},{7,11},{... | collective-permute-start | bytes 786440 | tf_op jit(solution)/shard_map/ppermute | solution.py:41
  122.4 4.4 %collective-permute-start.14 = (bf16[128,1024]{0,1:T(8,128)(2,1)}, bf16[128,1024]{0,1:T(8,128)(2,1)}, u32[]{:S(2)}, u32[]{:S(2)}) collective-permute-start(bf16[128,1024]{0,1:T(8,128)(2,1)} %fusion.14), channel_id=1, source_target_pairs={{0,2},{4,6},{8,10},{12,14},{1,3},{5,7},{9,11},{13,15},{16,18},{20,... | collective-permute-start | bytes 786440 | tf_op jit(solution)/shard_map/ppermute | solution.py:43
  126.7 2.0 copy.83
  128.7 3.2 %copy.74 = bf16[1024,8,128,1]{0,2,3,1:T(8,128)(2,1)S(1)} copy(bf16[1024,8,128,1]{2,1,0,3:T(8,128)(2,1)} %bitcast.105) | data formatting | bytes 4194304 | tf_op jit(solution)/shard_map/reshape | solution.py:177
  132.0 1.4 collective-permute-start.12
  133.4 5.7 %fusion.32 = (f32[8,2,128]{2,1,0:T(2,128)S(1)}, f32[8,2,128,1024]{2,3,1,0:T(8,128)}) fusion(pred[128,1024]{0,1:T(8,128)(4,1)S(1)} %compare_and_fusion, bf16[1024,8,128,1]{0,2,3,1:T(8,128)(2,1)S(1)} %copy.74, bf16[128,8,2,128]{0,3,2,1:T(8,128)(2,1)S(1)} %bitcast.112), kind=kOutput, calls=%fused_computation.105 | convolution fusion | flops 547357696 | bytes 11149312 | tf_op jit(solution)/shard_map/sub | solution.py:184
  139.1 1.4 collective-permute-start.13
  140.5 6.9 %fusion.5 = f32[8,1024,128,1]{1,2,3,0:T(8,128)} fusion(f32[128]{0:T(128)S(1)} %get-tuple-element.25, bf16[128,8,2,128]{3,2,1,0:T(2,128)(2,1)} %reshape_squeeze.7, f32[8,2,128,1024]{2,3,1,0:T(8,128)} %get-tuple-element.39, f32[8,2,128]{2,1,0:T(2,128)S(1)} %get-tuple-element.38), kind=kOutput, calls=%fused_computation.10 | convolution fusion | flops 543162368 | bytes 13115904 | tf_op jit(solution)/shard_map/jgtl,tjgd->ljd/dot_general | solution.py:198
  147.4 3.3 %copy.59 = bf16[1024,1024]{1,0:T(8,128)(2,1)S(1)} copy(f32[1024,1024]{0,1:T(8,128)} %bitcast.108) | data formatting | bytes 6291456 | tf_op jit(solution)/shard_map/reshape | solution.py:200
  150.8 1.1 constant_dynamic-update-slice_fusion.16
  157.6 1.0 constant_dynamic-update-slice_fusion.9
  158.6 5.1 %fusion.1 = (f32[8,2,128]{2,1,0:T(2,128)S(1)}, f32[8,1024,128,2]{2,1,3,0:T(8,128)S(1)}) fusion(f32[128]{0:T(128)S(1)} %get-tuple-element.25, f32[8,2,128,1024]{2,3,1,0:T(8,128)} %get-tuple-element.39, f32[8,2,128]{2,1,0:T(2,128)S(1)} %get-tuple-element.38, bf16[1024,8,128,1]{0,2,3,1:T(8,128)(2,1)S(1)} %bitcast.119, bf16[128,8,2,128]{3,2,1,0:T(2,128)(2,1)S(1)} %copy-done.7), kind=kOutput, calls=%fused_computation.3 | convolution fusion | flops 545257472 | bytes 19415552 | tf_op jit(solution)/shard_map/tjgd,ljd->jgtl/dot_general | solution.py:186
  164.5 1.7 fusion.3
  166.3 3.5 %fusion.33 = f32[8,1024,128,1]{1,2,3,0:T(8,128)} fusion(bf16[8,2,128,1024]{2,3,1,0:T(8,128)(2,1)S(1)} %fusion.3, bf16[128,8,2,128]{0,3,2,1:T(8,128)(2,1)S(1)} %bitcast.113), kind=kOutput, calls=%fused_computation.106 | convolution fusion | flops 536870912 | bytes 8912896 | tf_op jit(solution)/shard_map/jgtl,tjgd->ljd/dot_general | solution.py:194
  169.8 4.6 %copy.58 = bf16[1024,1024]{1,0:T(8,128)(2,1)} copy(f32[1024,1024]{0,1:T(8,128)} %bitcast.103) | data formatting | bytes 6291456 | tf_op jit(solution)/shard_map/reshape | solution.py:196
  174.4 1.5 maximum_convert_fusion.5
  179.8 1.3 collective-permute-start.18
  182.1 1.3 collective-permute-start.24
  183.4 1.1 slice.77
  184.7 1.1 slice.79
  186.0 7.9 %collective-permute-done.18 = bf16[128,2048]{1,0:T(8,128)(2,1)} collective-permute-done((bf16[128,2048]{1,0:T(8,128)(2,1)S(1)}, bf16[128,2048]{1,0:T(8,128)(2,1)}, u32[]{:S(2)}, u32[]{:S(2)}) %collective-permute-start.18) | collective-permute-done | bytes 524320 | tf_op jit(solution)/shard_map/ppermute | solution.py:69
  193.9 57.5 %collective-permute-done.24 = bf16[128,2048]{1,0:T(8,128)(2,1)S(1)} collective-permute-done((bf16[128,2048]{1,0:T(8,128)(2,1)}, bf16[128,2048]{1,0:T(8,128)(2,1)S(1)}, u32[]{:S(2)}, u32[]{:S(2)}) %collective-permute-start.24) | collective-permute-done | bytes 524320 | tf_op jit(solution)/shard_map/ppermute | solution.py:80
  251.4 1.2 convert_add_fusion
  254.0 1.6 copy.64
  255.5 1.7 reshape.186
  257.4 1.5 collective-permute-done.25
  259.6 3.8 %convolution_convert_fusion = bf16[8,128,2,128]{3,1,2,0:T(8,128)(2,1)} fusion(bf16[1024,8,128,1]{0,2,3,1:T(8,128)(2,1)S(1)} %copy-done.4, bf16[8,2,128,1024]{2,3,1,0:T(8,128)(2,1)} %copy-done.2), kind=kOutput, calls=%fused_computation.22 | convolution fusion | flops 537133056 | bytes 6815744 | tf_op jit(solution)/shard_map/jgtl,ljd->tjgd/dot_general | solution.py:191
  263.4 2.0 copy.65
  265.5 2.3 collective-permute-done.26
  268.7 2.4 collective-permute-start.27
  271.1 1.2 convolution_multiply_fusion
  272.3 4.0 %collective-permute-done.27 = f32[464,128]{1,0:T(8,128)S(1)} collective-permute-done((f32[464,128]{1,0:T(8,128)S(1)}, f32[464,128]{1,0:T(8,128)S(1)}, u32[]{:S(2)}, u32[]{:S(2)}) %collective-permute-start.27) | collective-permute-done | bytes 237600 | tf_op jit(solution)/shard_map/ppermute | solution.py:19
  276.4 3.3 %collective-permute-start.28 = (f32[464,128]{1,0:T(8,128)S(1)}, f32[464,128]{1,0:T(8,128)S(1)}, u32[]{:S(2)}, u32[]{:S(2)}) collective-permute-start(f32[464,128]{1,0:T(8,128)S(1)} %add.165), channel_id=1, source_target_pairs={{0,8},{2,10},{4,12},{6,14},{8,0},{10,2},{12,4},{14,6},{1,9},{3,11}... | collective-permute-start | bytes 712712 | tf_op jit(solution)/shard_map/ppermute | solution.py:19
  279.6 5.4 %fusion.11 = bf16[1,128,2688]{2,1,0:T(8,128)(2,1)} fusion(f32[128,2688]{1,0:T(8,128)S(1)} %convolution_multiply_fusion, bf16[128,1024]{1,0:T(8,128)(2,1)S(1)} %get-tuple-element.33, bf16[2688,1024]{1,0:T(8,128)(2,1)} %all-gather.5.cloned.1.call-done), kind=kOutput, calls=%fused_computation.19 | convolution fusion | flops 705331200 | bytes 7831552 | tf_op jit(solution)/shard_map/tk,dk->td/dot_general | solution.py:225
  285.0 4.1 %collective-permute-done.28 = f32[464,128]{1,0:T(8,128)S(1)} collective-permute-done((f32[464,128]{1,0:T(8,128)S(1)}, f32[464,128]{1,0:T(8,128)S(1)}, u32[]{:S(2)}, u32[]{:S(2)}) %collective-permute-start.28) | collective-permute-done | bytes 237600 | tf_op jit(solution)/shard_map/ppermute | solution.py:19
  289.5 1.1 copy.66
  (132 shorter events, 27.0 us)
Async XLA Ops:
  7.2 69.6 %copy-start = (bf16[1,128,2688]{2,1,0:T(8,128)(2,1)S(1)}, bf16[1,128,2688]{2,1,0:T(8,128)(2,1)}, u32[]{:S(2)}) copy-start(bf16[1,128,2688]{2,1,0:T(8,128)(2,1)} %param.10) | copy-start | bytes 2064388
  7.2 69.2 %copy-start.12 = (f32[1,128]{1,0:T(1,128)S(1)}, f32[1,128]{1,0:T(1,128)}, u32[]{:S(2)}) copy-start(f32[1,128]{1,0:T(1,128)} %param.17) | copy-start | bytes 1540
  7.2 69.2 %copy-start.13 = (f32[1,128]{1,0:T(1,128)S(1)}, f32[1,128]{1,0:T(1,128)}, u32[]{:S(2)}) copy-start(f32[1,128]{1,0:T(1,128)} %param.18) | copy-start | bytes 1540
  7.2 69.2 %copy-start.11 = (s32[1,128]{1,0:T(1,128)S(1)}, s32[1,128]{1,0:T(1,128)}, u32[]{:S(2)}) copy-start(s32[1,128]{1,0:T(1,128)} %param.19) | copy-start | bytes 1540
  7.2 69.6 %copy-start.8 = (bf16[2688,16]{0,1:T(8,128)(2,1)S(1)}, bf16[2688,16]{0,1:T(8,128)(2,1)}, u32[]{:S(2)}) copy-start(bf16[2688,16]{0,1:T(8,128)(2,1)} %param.14) | copy-start | bytes 258052
  7.2 62.4 %all-gather.3.cloned.1.call-start = ((), (), s32[]{:S(2)}) async-start(), calls=%async_computation | async-start | bytes 3096576 | tf_op jit(solution)/shard_map/all_gather | solution.py:116
  9.1 68.0 %copy-start.5 = (bf16[1,128,2048]{2,1,0:T(8,128)(2,1)S(1)}, bf16[1,128,2048]{2,1,0:T(8,128)(2,1)}, u32[]{:S(2)}) copy-start(bf16[1,128,2048]{2,1,0:T(8,128)(2,1)} %param.11) | copy-start | bytes 1572868
  9.1 87.8 %all-gather.5.cloned.1.call-start = ((), (), s32[]{:S(2)}) async-start(), calls=%async_computation.1 | async-start | bytes 8257536 | tf_op jit(solution)/shard_map/all_gather | solution.py:117
  69.6 12.0 %copy-start.6 = (bf16[1,128,2048]{2,1,0:T(8,128)(2,1)S(1)}, bf16[1,128,2048]{2,1,0:T(8,128)(2,1)}, u32[]{:S(2)}) copy-start(bf16[1,128,2048]{2,1,0:T(8,128)(2,1)} %param.16) | copy-start | bytes 1572868
  69.6 18.9 %collective-permute-start.3 = (bf16[128,1024]{1,0:T(8,128)(2,1)}, bf16[128,1024]{1,0:T(8,128)(2,1)S(1)}, u32[]{:S(2)}, u32[]{:S(2)}) collective-permute-start(bf16[128,1024]{1,0:T(8,128)(2,1)} %bitcast.4), channel_id=1, source_target_pairs={{0,4},{2,6},{4,8},{6,10},{8,12},{10,14},{1,5},{3,7},{5,9},{7,11},{... | collective-permute-start | bytes 786440 | tf_op jit(solution)/shard_map/ppermute | solution.py:41
  73.2 22.7 %collective-permute-start.6 = (bf16[128,1024]{1,0:T(8,128)(2,1)}, bf16[128,1024]{1,0:T(8,128)(2,1)}, u32[]{:S(2)}, u32[]{:S(2)}) collective-permute-start(bf16[128,1024]{1,0:T(8,128)(2,1)} %bitcast.4), channel_id=1, source_target_pairs={{0,2},{4,6},{8,10},{12,14},{1,3},{5,7},{9,11},{13,15},{16,18},{20,... | collective-permute-start | bytes 786440 | tf_op jit(solution)/shard_map/ppermute | solution.py:43
  76.6 3.5 %collective-permute-start = (f32[16]{0:T(128)S(1)}, f32[16]{0:T(128)S(1)}, u32[]{:S(2)}, u32[]{:S(2)}) collective-permute-start(f32[16]{0:T(128)S(1)} %pad_maximum_fusion.1), channel_id=1, source_target_pairs={{0,2},{2,0},{4,6},{6,4},{8,10},{10,8},{12,14},{14,12},{1,3},{3,1},... | collective-permute-start | bytes 200 | tf_op jit(solution)/shard_map/ppermute | solution.py:19
  80.2 3.5 %collective-permute-start.1 = (f32[16]{0:T(128)S(1)}, f32[16]{0:T(128)S(1)}, u32[]{:S(2)}, u32[]{:S(2)}) collective-permute-start(f32[16]{0:T(128)S(1)} %fusion.57), channel_id=1, source_target_pairs={{0,4},{2,6},{4,0},{6,2},{8,12},{10,14},{12,8},{14,10},{1,5},{3,7},... | collective-permute-start | bytes 200 | tf_op jit(solution)/shard_map/ppermute | solution.py:19
  83.8 4.4 %collective-permute-start.2 = (f32[16]{0:T(128)S(1)}, f32[16]{0:T(128)S(1)}, u32[]{:S(2)}, u32[]{:S(2)}) collective-permute-start(f32[16]{0:T(128)S(1)} %add.149), channel_id=1, source_target_pairs={{0,8},{2,10},{4,12},{6,14},{8,0},{10,2},{12,4},{14,6},{1,9},{3,11}... | collective-permute-start | bytes 200 | tf_op jit(solution)/shard_map/ppermute | solution.py:19
  88.3 1.1 collective-permute-start.10
  88.5 2.5 copy-start.9
  88.5 1.1 collective-permute-start.4
  89.6 4.0 %collective-permute-start.5 = (bf16[128,1024]{1,0:T(8,128)(2,1)S(1)}, bf16[128,1024]{1,0:T(8,128)(2,1)}, u32[]{:S(2)}, u32[]{:S(2)}) collective-permute-start(bf16[128,1024]{1,0:T(8,128)(2,1)S(1)} %collective-permute-done.4), channel_id=1, source_target_pairs={{8,12},{10,14},{9,13},{11,15},{24,28},{26,30},{25,29},{27,31}} | collective-permute-start | bytes 786440 | tf_op jit(solution)/shard_map/ppermute | solution.py:41
  92.1 4.7 %collective-permute-start.7 = (bf16[128,1024]{1,0:T(8,128)(2,1)}, bf16[128,1024]{1,0:T(8,128)(2,1)S(1)}, u32[]{:S(2)}, u32[]{:S(2)}) collective-permute-start(bf16[128,1024]{1,0:T(8,128)(2,1)} %copy-done.9), channel_id=1, source_target_pairs={{6,4},{4,6},{10,8},{8,10},{14,12},{12,14},{7,5},{5,7},{11,9},{9,11... | collective-permute-start | bytes 786440 | tf_op jit(solution)/shard_map/ppermute | solution.py:46
  92.8 4.1 %collective-permute-start.8 = (bf16[128,1024]{1,0:T(8,128)(2,1)S(1)}, bf16[128,1024]{1,0:T(8,128)(2,1)S(1)}, u32[]{:S(2)}, u32[]{:S(2)}) collective-permute-start(bf16[128,1024]{1,0:T(8,128)(2,1)S(1)} %collective-permute-done.4), channel_id=1, source_target_pairs={{10,8},{8,10},{14,12},{12,14},{11,9},{9,11},{15,13},{13,15},{26,24... | collective-permute-start | bytes 786440 | tf_op jit(solution)/shard_map/ppermute | solution.py:46
  93.5 26.9 %collective-permute-start.9 = (bf16[128,1024]{1,0:T(8,128)(2,1)}, bf16[128,1024]{1,0:T(8,128)(2,1)}, u32[]{:S(2)}, u32[]{:S(2)}) collective-permute-start(bf16[128,1024]{1,0:T(8,128)(2,1)} %collective-permute-done.5), channel_id=1, source_target_pairs={{14,12},{12,14},{15,13},{13,15},{30,28},{28,30},{31,29},{29,31}} | collective-permute-start | bytes 786440 | tf_op jit(solution)/shard_map/ppermute | solution.py:46
  96.9 4.2 %copy-start.10 = (bf16[16,1024]{1,0:T(8,128)(2,1)S(1)}, bf16[16,1024]{1,0:T(8,128)(2,1)}, u32[]{:S(2)}) copy-start(bf16[16,1024]{1,0:T(8,128)(2,1)} %param.15) | copy-start | bytes 98308
  102.2 29.8 %collective-permute-start.11 = (bf16[128,1024]{0,1:T(8,128)(2,1)}, bf16[128,1024]{0,1:T(8,128)(2,1)}, u32[]{:S(2)}, u32[]{:S(2)}) collective-permute-start(bf16[128,1024]{0,1:T(8,128)(2,1)} %fusion.14), channel_id=1, source_target_pairs={{0,4},{2,6},{4,8},{6,10},{8,12},{10,14},{1,5},{3,7},{5,9},{7,11},{... | collective-permute-start | bytes 786440 | tf_op jit(solution)/shard_map/ppermute | solution.py:41
  122.4 33.8 %collective-permute-start.14 = (bf16[128,1024]{0,1:T(8,128)(2,1)}, bf16[128,1024]{0,1:T(8,128)(2,1)}, u32[]{:S(2)}, u32[]{:S(2)}) collective-permute-start(bf16[128,1024]{0,1:T(8,128)(2,1)} %fusion.14), channel_id=1, source_target_pairs={{0,2},{4,6},{8,10},{12,14},{1,3},{5,7},{9,11},{13,15},{16,18},{20,... | collective-permute-start | bytes 786440 | tf_op jit(solution)/shard_map/ppermute | solution.py:43
  132.0 7.1 %copy-start.3 = (bf16[1024,8,128,1]{0,2,3,1:T(8,128)(2,1)}, bf16[1024,8,128,1]{0,2,3,1:T(8,128)(2,1)S(1)}, u32[]{:S(2)}) copy-start(bf16[1024,8,128,1]{0,2,3,1:T(8,128)(2,1)S(1)} %copy.74) | copy-start | bytes 6291460
  132.0 7.1 %collective-permute-start.12 = (bf16[128,1024]{0,1:T(8,128)(2,1)}, bf16[128,1024]{0,1:T(8,128)(2,1)}, u32[]{:S(2)}, u32[]{:S(2)}) collective-permute-start(bf16[128,1024]{0,1:T(8,128)(2,1)} %collective-permute-done.11), channel_id=1, source_target_pairs={{4,8},{6,10},{8,12},{10,14},{5,9},{7,11},{9,13},{11,15},{20,24},{2... | collective-permute-start | bytes 786440 | tf_op jit(solution)/shard_map/ppermute | solution.py:41
  139.1 15.2 %collective-permute-start.13 = (bf16[128,1024]{0,1:T(8,128)(2,1)}, bf16[128,1024]{0,1:T(8,128)(2,1)}, u32[]{:S(2)}, u32[]{:S(2)}) collective-permute-start(bf16[128,1024]{0,1:T(8,128)(2,1)} %collective-permute-done.12), channel_id=1, source_target_pairs={{8,12},{10,14},{9,13},{11,15},{24,28},{26,30},{25,29},{27,31}} | collective-permute-start | bytes 786440 | tf_op jit(solution)/shard_map/ppermute | solution.py:41
  150.8 7.8 %copy-start.7 = (bf16[128,8,2,128]{3,2,1,0:T(2,128)(2,1)S(1)}, bf16[128,8,2,128]{3,2,1,0:T(2,128)(2,1)}, u32[]{:S(2)}) copy-start(bf16[128,8,2,128]{3,2,1,0:T(2,128)(2,1)} %reshape_squeeze.7) | copy-start | bytes 1572868
  151.9 5.4 %collective-permute-start.15 = (bf16[128,1024]{0,1:T(8,128)(2,1)}, bf16[128,1024]{0,1:T(8,128)(2,1)S(1)}, u32[]{:S(2)}, u32[]{:S(2)}) collective-permute-start(bf16[128,1024]{0,1:T(8,128)(2,1)} %collective-permute-done.11), channel_id=1, source_target_pairs={{6,4},{4,6},{10,8},{8,10},{14,12},{12,14},{7,5},{5,7},{11,9},{9,11... | collective-permute-start | bytes 786440 | tf_op jit(solution)/shard_map/ppermute | solution.py:46
  152.6 4.8 %collective-permute-start.16 = (bf16[128,1024]{0,1:T(8,128)(2,1)}, bf16[128,1024]{0,1:T(8,128)(2,1)S(1)}, u32[]{:S(2)}, u32[]{:S(2)}) collective-permute-start(bf16[128,1024]{0,1:T(8,128)(2,1)} %collective-permute-done.12), channel_id=1, source_target_pairs={{10,8},{8,10},{14,12},{12,14},{11,9},{9,11},{15,13},{13,15},{26,24... | collective-permute-start | bytes 786440 | tf_op jit(solution)/shard_map/ppermute | solution.py:46
  154.3 3.2 %collective-permute-start.17 = (bf16[128,1024]{0,1:T(8,128)(2,1)}, bf16[128,1024]{0,1:T(8,128)(2,1)S(1)}, u32[]{:S(2)}, u32[]{:S(2)}) collective-permute-start(bf16[128,1024]{0,1:T(8,128)(2,1)} %collective-permute-done.13), channel_id=1, source_target_pairs={{14,12},{12,14},{15,13},{13,15},{30,28},{28,30},{31,29},{29,31}} | collective-permute-start | bytes 786440 | tf_op jit(solution)/shard_map/ppermute | solution.py:46
  158.6 5.1 %slice-start = ((s8[8388608]{0:T(1024)(128)(4,1)}), s8[4194304]{0:T(1024)(128)(4,1)S(1)}, s32[]{:S(2)}) async-start(s8[8388608]{0:T(1024)(128)(4,1)} %bitcast.106), calls=%async_computation.2 | async-start | bytes 8388608
  158.6 5.9 %slice-start.1 = ((s8[8388608]{0:T(1024)(128)(4,1)}), s8[4194304]{0:T(1024)(128)(4,1)S(1)}, s32[]{:S(2)}) async-start(s8[8388608]{0:T(1024)(128)(4,1)} %bitcast.106), calls=%async_computation.3 | async-start | bytes 8388608
  166.3 3.5 %copy-start.2 = (bf16[8,2,128,1024]{2,3,1,0:T(8,128)(2,1)}, bf16[8,2,128,1024]{2,3,1,0:T(8,128)(2,1)S(1)}, u32[]{:S(2)}) copy-start(bf16[8,2,128,1024]{2,3,1,0:T(8,128)(2,1)S(1)} %fusion.3) | copy-start | bytes 12582916
  174.4 2.9 copy-start.1
  175.9 1.4 collective-permute-start.21
  176.6 2.3 collective-permute-start.20
  177.4 1.4 collective-permute-start.22
  178.1 3.0 collective-permute-start.19
  179.1 2.0 collective-permute-start.23
  179.8 14.1 %collective-permute-start.18 = (bf16[128,2048]{1,0:T(8,128)(2,1)S(1)}, bf16[128,2048]{1,0:T(8,128)(2,1)}, u32[]{:S(2)}, u32[]{:S(2)}) collective-permute-start(bf16[128,2048]{1,0:T(8,128)(2,1)S(1)} %get-tuple-element.28), channel_id=1, source_target_pairs={{2,0},{6,4},{10,8},{14,12},{3,1},{7,5},{11,9},{15,13},{18,16},{22,... | collective-permute-start | bytes 1572872 | tf_op jit(solution)/shard_map/ppermute | solution.py:69
  182.1 69.2 %collective-permute-start.24 = (bf16[128,2048]{1,0:T(8,128)(2,1)}, bf16[128,2048]{1,0:T(8,128)(2,1)S(1)}, u32[]{:S(2)}, u32[]{:S(2)}) collective-permute-start(bf16[128,2048]{1,0:T(8,128)(2,1)} %add_convert_fusion), channel_id=1, source_target_pairs={{4,0},{6,2},{8,4},{10,6},{12,8},{14,10},{5,1},{7,3},{9,5},{11,7},{... | collective-permute-start | bytes 1572872 | tf_op jit(solution)/shard_map/ppermute | solution.py:80
  254.0 5.6 %copy-start.4 = (bf16[1024,8,128,1]{0,2,3,1:T(8,128)(2,1)S(1)}, bf16[1024,8,128,1]{0,2,3,1:T(8,128)(2,1)}, u32[]{:S(2)}) copy-start(bf16[1024,8,128,1]{0,2,3,1:T(8,128)(2,1)} %copy-done.3) | copy-start | bytes 6291460
  257.3 1.6 collective-permute-start.25
  259.6 8.1 %collective-permute-start.26 = (f32[464,128]{1,0:T(8,128)}, f32[464,128]{1,0:T(8,128)}, u32[]{:S(2)}, u32[]{:S(2)}) collective-permute-start(f32[464,128]{1,0:T(8,128)} %fusion.30), channel_id=1, source_target_pairs={{0,2},{2,0},{4,6},{6,4},{8,10},{10,8},{12,14},{14,12},{1,3},{3,1},... | collective-permute-start | bytes 712712 | tf_op jit(solution)/shard_map/ppermute | solution.py:19
  268.7 7.6 %collective-permute-start.27 = (f32[464,128]{1,0:T(8,128)S(1)}, f32[464,128]{1,0:T(8,128)S(1)}, u32[]{:S(2)}, u32[]{:S(2)}) collective-permute-start(f32[464,128]{1,0:T(8,128)S(1)} %fusion.56), channel_id=1, source_target_pairs={{0,4},{2,6},{4,0},{6,2},{8,12},{10,14},{12,8},{14,10},{1,5},{3,7},... | collective-permute-start | bytes 712712 | tf_op jit(solution)/shard_map/ppermute | solution.py:19
  276.4 12.7 %collective-permute-start.28 = (f32[464,128]{1,0:T(8,128)S(1)}, f32[464,128]{1,0:T(8,128)S(1)}, u32[]{:S(2)}, u32[]{:S(2)}) collective-permute-start(f32[464,128]{1,0:T(8,128)S(1)} %add.165), channel_id=1, source_target_pairs={{0,8},{2,10},{4,12},{6,14},{8,0},{10,2},{12,4},{14,6},{1,9},{3,11}... | collective-permute-start | bytes 712712 | tf_op jit(solution)/shard_map/ppermute | solution.py:19
Sparse Core Ops, SparseCore 0:
  10.8 58.7 all-gather.2
  71.1 14.1 all-gather.4

commit v6 on v5

--- a/solution.py
+++ b/solution.py
@@ -204,10 +204,8 @@
         slot_rows = lambda parts: [
             parts[k * tok_rows : (k + 1) * tok_rows].astype(jnp.bfloat16) for k in range(halo_blocks)
         ]
-        joined = jnp.concatenate([key_parts, value_parts], 1)
-        returned = tree_return(slot_rows(joined), levels)
-        key_total = key_total + returned[:, :width_kv]
-        value_total = value_total + returned[:, width_kv:]
+        key_total = key_total + tree_return(slot_rows(key_parts), levels)
+        value_total = value_total + tree_return(slot_rows(value_parts), levels)
     else:
         for distance in range(1, halo_blocks + 1):
             block_start = (halo_blocks - distance) * tok_rows

time: 299 us -> 282 us (0.943)
  waiting for transfers between devices: 144 us -> 109 us
  starting transfers between devices: 54.4 us -> 88.7 us
  local copies, waits for them, and re-layouts: 37.9 us -> 25.4 us
  matrix products: 37.6 us -> 28.6 us
  other arithmetic: 9.33 us -> 14.2 us
    ppermute x3 -> x6, waiting for transfers between devices: 57.5 us -> 21.7 us  [tree_return(): lax.ppermute(acc.astype(jnp.bfloat16), 'ctx', [(c, c - 2) for c in range(...]
    ppermute x8, starting transfers between devices: 9.14 us -> 37.2 us  [from_partner(): lax.ppermute(shard, axis, [(i, i ^ 1 << stride) for i in range(lax.axis_s...]
    reshape x2 -> x0, local copies, waits for them, and re-layouts: 7.95 us -> none  [the longest x1 4.61 us: shards(): key_parts = jnp.einsum('jgtl,tjgd->ljd', score_grad, query_rows, preferre...]
    ppermute x1 -> x2, waiting for transfers between devices: 7.88 us -> 0.01 us  [tree_return(): lax.ppermute(crossed[0], 'ctx', [(c, c - 1) for c in range(1, count, 2)])]
    unnamed x50 -> x56, local copies, waits for them, and re-layouts: 14.4 us -> 6.93 us
    convert_element_type x0 -> x7, local copies, waits for them, and re-layouts: none -> 5.82 us  [the longest x4 4.43 us: shards(): parts[k * tok_rows:(k + 1) * tok_rows].astype(jnp.bfloat16)]
    ppermute x8, waiting for transfers between devices: 18.2 us -> 23.8 us  [from_partner(): lax.ppermute(shard, axis, [(i, i ^ 1 << stride) for i in range(lax.axis_s...]
    ppermute x3 -> x6, starting transfers between devices: 2.08 us -> 6.29 us  [tree_return(): lax.ppermute(crossed[step], 'ctx', [(c, c ^ 1) for c in range(2 * step, c...]
  transfers between devices with their start and end apart: 31 -> 38, of which waited for: 11 -> 11; matrix products, arithmetic and copies ran while one was open for 18% -> 14% of each run, Pallas kernels for 0% -> 0%
where the time goes in v6:
time: 282 us; the launch traced here: 281 us
  waiting for transfers between devices  109 us (39%)
  starting transfers between devices  88.7 us (31%)
  matrix products  28.6 us (10%)
  local copies, waits for them, and re-layouts  25.4 us (9%)
  between operations  15 us (5%)
  other arithmetic  14.2 us (5%)
    all_gather x1, waiting for transfers between devices, shards(): rows_half = lax.all_gather(own_half, 'ctx', axis=0, tiled=True)  60.4 us
    ppermute x8, starting transfers between devices, from_partner(): lax.ppermute(shard, axis, [(i, i ^ 1 << stride) for i in range(lax.axis_s...  37.2 us
    ppermute x6, starting transfers between devices, tree_spread(): lax.ppermute(held, 'ctx', [(c - 2, c) for c in range(2 * step, count)])  25.7 us
    ppermute x8, waiting for transfers between devices, from_partner(): lax.ppermute(shard, axis, [(i, i ^ 1 << stride) for i in range(lax.axis_s...  23.8 us
    ppermute x6, waiting for transfers between devices, tree_return(): lax.ppermute(acc.astype(jnp.bfloat16), 'ctx', [(c, c - 2) for c in range(...  21.7 us
    unnamed x56, local copies, waits for them, and re-layouts  6.93 us
    ppermute x2, starting transfers between devices, tree_spread(): lax.ppermute(block, 'ctx', [(c - 1, c) for c in range(1, count, 2)])  6.52 us
    ppermute x6, starting transfers between devices, tree_return(): lax.ppermute(crossed[step], 'ctx', [(c, c ^ 1) for c in range(2 * step, c...  6.29 us
  transfers between devices with their start and end apart: 38, of which 11 were waited for; matrix products, arithmetic and copies ran while one was open for 14% of the time, Pallas kernels for 0%

profile of v6, /device:TPU:0, one launch (start us, length us, event | category | flops | bytes accessed | tf_op | source)
XLA Modules:
  0.0 280.7 jit_solution(14576800294788585194)
XLA Ops:
  7.3 1.8 constant_dynamic-slice_fusion
  9.2 60.4 %all-gather.3.cloned.1.call-done = bf16[2688,512]{1,0:T(8,128)(2,1)} async-done(((bf16[336,512]{1,0:T(8,128)(2,1)}), bf16[2688,512]{1,0:T(8,128)(2,1)}) %all-gather.3.cloned.1.call-update) | async-done | bytes 2752528 | tf_op jit(solution)/shard_map/all_gather | solution.py:116
  69.6 3.5 %collective-permute-start.3 = (bf16[128,1024]{1,0:T(8,128)(2,1)}, bf16[128,1024]{1,0:T(8,128)(2,1)S(1)}, u32[]{:S(2)}, u32[]{:S(2)}) collective-permute-start(bf16[128,1024]{1,0:T(8,128)(2,1)} %bitcast.4), channel_id=1, source_target_pairs={{0,4},{2,6},{4,8},{6,10},{8,12},{10,14},{1,5},{3,7},{5,9},{7,11},{... | collective-permute-start | bytes 786440 | tf_op jit(solution)/shard_map/ppermute | solution.py:41
  73.2 3.2 %collective-permute-start.6 = (bf16[128,1024]{1,0:T(8,128)(2,1)}, bf16[128,1024]{1,0:T(8,128)(2,1)}, u32[]{:S(2)}, u32[]{:S(2)}) collective-permute-start(bf16[128,1024]{1,0:T(8,128)(2,1)} %bitcast.4), channel_id=1, source_target_pairs={{0,2},{4,6},{8,10},{12,14},{1,3},{5,7},{9,11},{13,15},{16,18},{20,... | collective-permute-start | bytes 786440 | tf_op jit(solution)/shard_map/ppermute | solution.py:43
  76.6 1.2 reshape_squeeze.7
  78.2 1.9 collective-permute-done
  80.2 1.4 collective-permute-start.1
  81.9 1.9 collective-permute-done.1
  83.7 2.1 collective-permute-start.2
  85.8 2.3 collective-permute-done.2
  95.7 4.2 %convolution_bitcast_fusion.1 = f32[128,1024]{0,1:T(8,128)S(1)} fusion(bf16[2688,1024]{1,0:T(8,128)(2,1)} %all-gather.5.cloned.1.call-done, bf16[1,128,2688]{2,1,0:T(8,128)(2,1)S(1)} %copy-done), kind=kOutput, calls=%fused_computation.26 | convolution fusion | flops 704643072 | bytes 6717440 | tf_op jit(solution)/shard_map/dot_general | solution.py:122
  100.8 2.0 copy.95
  102.8 3.2 %copy.84 = bf16[1024,8,128,1]{0,2,3,1:T(8,128)(2,1)S(1)} copy(bf16[1024,8,128,1]{2,1,0,3:T(8,128)(2,1)} %bitcast.130) | data formatting | bytes 4194304 | tf_op jit(solution)/shard_map/reshape | solution.py:177
  106.1 5.7 %fusion.38 = (f32[8,2,128]{2,1,0:T(2,128)S(1)}, f32[8,2,128,1024]{2,3,1,0:T(8,128)}) fusion(pred[128,1024]{0,1:T(8,128)(4,1)S(1)} %compare_and_fusion, bf16[1024,8,128,1]{0,2,3,1:T(8,128)(2,1)S(1)} %copy.84, bf16[128,8,2,128]{0,3,2,1:T(8,128)(2,1)S(1)} %bitcast.134), kind=kOutput, calls=%fused_computation.110 | convolution fusion | flops 547357696 | bytes 11149312 | tf_op jit(solution)/shard_map/sub | solution.py:184
  111.8 5.0 %fusion.39 = (bf16[1024,8,128]{0,2,1:T(8,128)(2,1)S(1)}, f32[1024,8,128]{0,2,1:T(8,128)S(1)}) fusion(bf16[128,8,2,128]{3,2,1,0:T(2,128)(2,1)} %reshape_squeeze.7, f32[128]{0:T(128)S(1)} %get-tuple-element.25, f32[8,2,128,1024]{2,3,1,0:T(8,128)} %get-tuple-element.47, f32[8,2,128]{2,1,0:T(2,128)S(1)} %get-tuple-element.46), kind=kOutput, calls=%fused_computation.111 | convolution fusion | flops 544210944 | bytes 15213056 | tf_op jit(solution)/shard_map/jgtl,tjgd->ljd/dot_general | solution.py:198
  118.1 19.5 %collective-permute-start.18 = (bf16[128,1024]{0,1:T(8,128)(2,1)S(1)}, bf16[128,1024]{0,1:T(8,128)(2,1)S(1)}, u32[]{:S(2)}, u32[]{:S(2)}) collective-permute-start(bf16[128,1024]{0,1:T(8,128)(2,1)S(1)} %copy-done.6), channel_id=1, source_target_pairs={{0,4},{2,6},{4,8},{6,10},{8,12},{10,14},{1,5},{3,7},{5,9},{7,11},{... | collective-permute-start | bytes 786440 | tf_op jit(solution)/shard_map/ppermute | solution.py:41
  139.8 2.7 collective-permute-done.18
  144.0 3.3 %collective-permute-start.21 = (bf16[128,1024]{0,1:T(8,128)(2,1)S(1)}, bf16[128,1024]{0,1:T(8,128)(2,1)S(1)}, u32[]{:S(2)}, u32[]{:S(2)}) collective-permute-start(bf16[128,1024]{0,1:T(8,128)(2,1)S(1)} %copy-done.6), channel_id=1, source_target_pairs={{0,2},{4,6},{8,10},{12,14},{1,3},{5,7},{9,11},{13,15},{16,18},{20,... | collective-permute-start | bytes 786440 | tf_op jit(solution)/shard_map/ppermute | solution.py:43
  147.4 1.3 collective-permute-start.11
  151.1 1.3 collective-permute-start.17
  153.9 1.9 fusion.1
  155.9 1.7 fusion.3
  158.6 3.5 %fusion.40 = (bf16[1024,8,128]{0,2,1:T(8,128)(2,1)S(1)}, f32[1024,8,128]{0,2,1:T(8,128)}) fusion(bf16[8,2,128,1024]{2,3,1,0:T(8,128)(2,1)S(1)} %fusion.3, bf16[128,8,2,128]{0,3,2,1:T(8,128)(2,1)S(1)} %bitcast.135), kind=kOutput, calls=%fused_computation.112 | convolution fusion | flops 537919488 | bytes 11010048 | tf_op jit(solution)/shard_map/jgtl,tjgd->ljd/dot_general | solution.py:194
  162.1 20.0 %collective-permute-done.17 = bf16[128,1024]{0,1:T(8,128)(2,1)S(1)} collective-permute-done((bf16[128,1024]{0,1:T(8,128)(2,1)S(1)}, bf16[128,1024]{0,1:T(8,128)(2,1)S(1)}, u32[]{:S(2)}, u32[]{:S(2)}) %collective-permute-start.17) | collective-permute-done | bytes 262176 | tf_op jit(solution)/shard_map/ppermute | solution.py:80
  182.6 1.3 fusion.35
  183.9 1.0 copy.74
  185.7 1.4 collective-permute-start.28
  188.0 1.4 collective-permute-start.27
  192.2 1.9 add_convert_fusion.3
  194.0 1.4 collective-permute-start.29
  196.3 1.0 copy.77
  197.3 1.1 slice.126
  199.1 1.8 copy.69
  200.9 1.4 collective-permute-start.26
  203.2 1.3 collective-permute-start.25
  205.4 2.7 collective-permute-start.33
  208.2 1.1 add_convert_fusion.2
  210.0 9.1 %collective-permute-done.33 = f32[464,128]{1,0:T(8,128)S(1)} collective-permute-done((f32[464,128]{1,0:T(8,128)S(1)}, f32[464,128]{1,0:T(8,128)S(1)}, u32[]{:S(2)}, u32[]{:S(2)}) %collective-permute-start.33) | collective-permute-done | bytes 237600 | tf_op jit(solution)/shard_map/ppermute | solution.py:19
  220.0 12.1 %collective-permute-start.34 = (f32[464,128]{1,0:T(8,128)S(1)}, f32[464,128]{1,0:T(8,128)S(1)}, u32[]{:S(2)}, u32[]{:S(2)}) collective-permute-start(f32[464,128]{1,0:T(8,128)S(1)} %fusion.63), channel_id=1, source_target_pairs={{0,4},{2,6},{4,0},{6,2},{8,12},{10,14},{12,8},{14,10},{1,5},{3,7},... | collective-permute-start | bytes 712712 | tf_op jit(solution)/shard_map/ppermute | solution.py:19
  232.5 5.5 %collective-permute-done.34 = f32[464,128]{1,0:T(8,128)S(1)} collective-permute-done((f32[464,128]{1,0:T(8,128)S(1)}, f32[464,128]{1,0:T(8,128)S(1)}, u32[]{:S(2)}, u32[]{:S(2)}) %collective-permute-start.34) | collective-permute-done | bytes 237600 | tf_op jit(solution)/shard_map/ppermute | solution.py:19
  238.1 18.9 %collective-permute-start.35 = (f32[464,128]{1,0:T(8,128)S(1)}, f32[464,128]{1,0:T(8,128)S(1)}, u32[]{:S(2)}, u32[]{:S(2)}) collective-permute-start(f32[464,128]{1,0:T(8,128)S(1)} %add.189), channel_id=1, source_target_pairs={{0,8},{2,10},{4,12},{6,14},{8,0},{10,2},{12,4},{14,6},{1,9},{3,11}... | collective-permute-start | bytes 712712 | tf_op jit(solution)/shard_map/ppermute | solution.py:19
  257.0 1.8 add_convert_fusion.1
  258.7 1.3 collective-permute-start.31
  260.0 5.4 %fusion.11 = bf16[1,128,2688]{2,1,0:T(8,128)(2,1)} fusion(f32[128,2688]{1,0:T(8,128)S(1)} %convolution_multiply_fusion, bf16[128,1024]{0,1:T(8,128)(2,1)S(1)} %fusion.27, bf16[2688,1024]{1,0:T(8,128)(2,1)} %all-gather.5.cloned.1.call-done), kind=kOutput, calls=%fused_computation.19 | convolution fusion | flops 705331200 | bytes 7831552 | tf_op jit(solution)/shard_map/tk,dk->td/dot_general | solution.py:223
  265.4 2.8 %collective-permute-done.35 = f32[464,128]{1,0:T(8,128)S(1)} collective-permute-done((f32[464,128]{1,0:T(8,128)S(1)}, f32[464,128]{1,0:T(8,128)S(1)}, u32[]{:S(2)}, u32[]{:S(2)}) %collective-permute-start.35) | collective-permute-done | bytes 237600 | tf_op jit(solution)/shard_map/ppermute | solution.py:19
  268.7 1.1 copy.78
  270.4 1.7 collective-permute-done.31
  272.1 1.8 fusion.31
  (162 shorter events, 30.5 us)
Async XLA Ops:
  7.2 70.7 %copy-start = (bf16[1,128,2688]{2,1,0:T(8,128)(2,1)S(1)}, bf16[1,128,2688]{2,1,0:T(8,128)(2,1)}, u32[]{:S(2)}) copy-start(bf16[1,128,2688]{2,1,0:T(8,128)(2,1)} %param.10) | copy-start | bytes 2064388
  7.2 69.2 %copy-start.17 = (f32[1,128]{1,0:T(1,128)S(1)}, f32[1,128]{1,0:T(1,128)}, u32[]{:S(2)}) copy-start(f32[1,128]{1,0:T(1,128)} %param.17) | copy-start | bytes 1540
  7.2 69.2 %copy-start.18 = (f32[1,128]{1,0:T(1,128)S(1)}, f32[1,128]{1,0:T(1,128)}, u32[]{:S(2)}) copy-start(f32[1,128]{1,0:T(1,128)} %param.18) | copy-start | bytes 1540
  7.2 69.1 %copy-start.16 = (s32[1,128]{1,0:T(1,128)S(1)}, s32[1,128]{1,0:T(1,128)}, u32[]{:S(2)}) copy-start(s32[1,128]{1,0:T(1,128)} %param.19) | copy-start | bytes 1540
  7.2 69.4 %copy-start.9 = (bf16[1,128,2048]{2,1,0:T(8,128)(2,1)S(1)}, bf16[1,128,2048]{2,1,0:T(8,128)(2,1)}, u32[]{:S(2)}) copy-start(bf16[1,128,2048]{2,1,0:T(8,128)(2,1)} %param.16) | copy-start | bytes 1572868
  7.2 62.4 %all-gather.3.cloned.1.call-start = ((), (), s32[]{:S(2)}) async-start(), calls=%async_computation | async-start | bytes 3096576 | tf_op jit(solution)/shard_map/all_gather | solution.py:116
  9.1 68.8 %copy-start.12 = (bf16[2688,16]{0,1:T(8,128)(2,1)S(1)}, bf16[2688,16]{0,1:T(8,128)(2,1)}, u32[]{:S(2)}) copy-start(bf16[2688,16]{0,1:T(8,128)(2,1)} %param.14) | copy-start | bytes 258052
  9.1 86.5 %all-gather.5.cloned.1.call-start = ((), (), s32[]{:S(2)}) async-start(), calls=%async_computation.1 | async-start | bytes 8257536 | tf_op jit(solution)/shard_map/all_gather | solution.py:117
  69.6 12.0 %copy-start.10 = (bf16[1,128,2048]{2,1,0:T(8,128)(2,1)S(1)}, bf16[1,128,2048]{2,1,0:T(8,128)(2,1)}, u32[]{:S(2)}) copy-start(bf16[1,128,2048]{2,1,0:T(8,128)(2,1)} %param.11) | copy-start | bytes 1572868
  69.6 18.8 %collective-permute-start.3 = (bf16[128,1024]{1,0:T(8,128)(2,1)}, bf16[128,1024]{1,0:T(8,128)(2,1)S(1)}, u32[]{:S(2)}, u32[]{:S(2)}) collective-permute-start(bf16[128,1024]{1,0:T(8,128)(2,1)} %bitcast.4), channel_id=1, source_target_pairs={{0,4},{2,6},{4,8},{6,10},{8,12},{10,14},{1,5},{3,7},{5,9},{7,11},{... | collective-permute-start | bytes 786440 | tf_op jit(solution)/shard_map/ppermute | solution.py:41
  73.2 20.4 %collective-permute-start.6 = (bf16[128,1024]{1,0:T(8,128)(2,1)}, bf16[128,1024]{1,0:T(8,128)(2,1)}, u32[]{:S(2)}, u32[]{:S(2)}) collective-permute-start(bf16[128,1024]{1,0:T(8,128)(2,1)} %bitcast.4), channel_id=1, source_target_pairs={{0,2},{4,6},{8,10},{12,14},{1,3},{5,7},{9,11},{13,15},{16,18},{20,... | collective-permute-start | bytes 786440 | tf_op jit(solution)/shard_map/ppermute | solution.py:43
  76.6 3.5 %collective-permute-start = (f32[16]{0:T(128)S(1)}, f32[16]{0:T(128)S(1)}, u32[]{:S(2)}, u32[]{:S(2)}) collective-permute-start(f32[16]{0:T(128)S(1)} %pad_maximum_fusion), channel_id=1, source_target_pairs={{0,2},{2,0},{4,6},{6,4},{8,10},{10,8},{12,14},{14,12},{1,3},{3,1},... | collective-permute-start | bytes 200 | tf_op jit(solution)/shard_map/ppermute | solution.py:19
  80.2 3.5 %collective-permute-start.1 = (f32[16]{0:T(128)S(1)}, f32[16]{0:T(128)S(1)}, u32[]{:S(2)}, u32[]{:S(2)}) collective-permute-start(f32[16]{0:T(128)S(1)} %fusion.64), channel_id=1, source_target_pairs={{0,4},{2,6},{4,0},{6,2},{8,12},{10,14},{12,8},{14,10},{1,5},{3,7},... | collective-permute-start | bytes 200 | tf_op jit(solution)/shard_map/ppermute | solution.py:19
  81.9 24.2 %copy-start.3 = (bf16[1,128,2048]{1,2,0:T(8,128)(2,1)}, bf16[1,128,2048]{1,2,0:T(8,128)(2,1)S(1)}, u32[]{:S(2)}) copy-start(bf16[1,128,2048]{1,2,0:T(8,128)(2,1)S(1)} %copy.94) | copy-start | bytes 1572868
  83.7 4.4 %collective-permute-start.2 = (f32[16]{0:T(128)S(1)}, f32[16]{0:T(128)S(1)}, u32[]{:S(2)}, u32[]{:S(2)}) collective-permute-start(f32[16]{0:T(128)S(1)} %add.167), channel_id=1, source_target_pairs={{0,8},{2,10},{4,12},{6,14},{8,0},{10,2},{12,4},{14,6},{1,9},{3,11}... | collective-permute-start | bytes 200 | tf_op jit(solution)/shard_map/ppermute | solution.py:19
  88.3 1.1 collective-permute-start.10
  88.5 1.1 collective-permute-start.4
  89.6 3.3 %collective-permute-start.5 = (bf16[128,1024]{1,0:T(8,128)(2,1)S(1)}, bf16[128,1024]{1,0:T(8,128)(2,1)S(1)}, u32[]{:S(2)}, u32[]{:S(2)}) collective-permute-start(bf16[128,1024]{1,0:T(8,128)(2,1)S(1)} %collective-permute-done.4), channel_id=1, source_target_pairs={{8,12},{10,14},{9,13},{11,15},{24,28},{26,30},{25,29},{27,31}} | collective-permute-start | bytes 786440 | tf_op jit(solution)/shard_map/ppermute | solution.py:41
  91.4 3.1 %collective-permute-start.7 = (bf16[128,1024]{1,0:T(8,128)(2,1)}, bf16[128,1024]{1,0:T(8,128)(2,1)S(1)}, u32[]{:S(2)}, u32[]{:S(2)}) collective-permute-start(bf16[128,1024]{1,0:T(8,128)(2,1)} %copy-done.14), channel_id=1, source_target_pairs={{6,4},{4,6},{10,8},{8,10},{14,12},{12,14},{7,5},{5,7},{11,9},{9,11... | collective-permute-start | bytes 786440 | tf_op jit(solution)/shard_map/ppermute | solution.py:46
  92.1 2.5 collective-permute-start.8
  92.8 1.8 collective-permute-start.9
  116.8 37.1 %copy-start.1 = (f32[8,2,128,1024]{2,3,1,0:T(8,128)S(1)}, f32[8,2,128,1024]{2,3,1,0:T(8,128)}, u32[]{:S(2)}) copy-start(f32[8,2,128,1024]{2,3,1,0:T(8,128)} %get-tuple-element.47) | copy-start | bytes 25165828
  117.3 21.0 %collective-permute-start.14 = (bf16[128,1024]{0,1:T(8,128)(2,1)S(1)}, bf16[128,1024]{0,1:T(8,128)(2,1)S(1)}, u32[]{:S(2)}, u32[]{:S(2)}) collective-permute-start(bf16[128,1024]{0,1:T(8,128)(2,1)S(1)} %bitcast.146), channel_id=1, source_target_pairs={{12,14},{14,12},{13,15},{15,13},{28,30},{30,28},{29,31},{31,29}} | collective-permute-start | bytes 786440 | tf_op jit(solution)/shard_map/ppermute | solution.py:72
  118.1 24.4 %collective-permute-start.18 = (bf16[128,1024]{0,1:T(8,128)(2,1)S(1)}, bf16[128,1024]{0,1:T(8,128)(2,1)S(1)}, u32[]{:S(2)}, u32[]{:S(2)}) collective-permute-start(bf16[128,1024]{0,1:T(8,128)(2,1)S(1)} %copy-done.6), channel_id=1, source_target_pairs={{0,4},{2,6},{4,8},{6,10},{8,12},{10,14},{1,5},{3,7},{5,9},{7,11},{... | collective-permute-start | bytes 786440 | tf_op jit(solution)/shard_map/ppermute | solution.py:41
  137.6 5.5 %collective-permute-start.13 = (bf16[128,1024]{0,1:T(8,128)(2,1)S(1)}, bf16[128,1024]{0,1:T(8,128)(2,1)S(1)}, u32[]{:S(2)}, u32[]{:S(2)}) collective-permute-start(bf16[128,1024]{0,1:T(8,128)(2,1)S(1)} %bitcast.145), channel_id=1, source_target_pairs={{8,10},{10,8},{12,14},{14,12},{9,11},{11,9},{13,15},{15,13},{24,26... | collective-permute-start | bytes 786440 | tf_op jit(solution)/shard_map/ppermute | solution.py:72
  138.4 4.7 %collective-permute-start.15 = (bf16[128,1024]{0,1:T(8,128)(2,1)S(1)}, bf16[128,1024]{0,1:T(8,128)(2,1)S(1)}, u32[]{:S(2)}, u32[]{:S(2)}) collective-permute-start(bf16[128,1024]{0,1:T(8,128)(2,1)S(1)} %fusion.22), channel_id=1, source_target_pairs={{12,8},{14,10},{13,9},{15,11},{28,24},{30,26},{29,25},{31,27}} | collective-permute-start | bytes 786440 | tf_op jit(solution)/shard_map/ppermute | solution.py:80
  139.1 10.5 %collective-permute-start.12 = (bf16[128,1024]{0,1:T(8,128)(2,1)S(1)}, bf16[128,1024]{0,1:T(8,128)(2,1)S(1)}, u32[]{:S(2)}, u32[]{:S(2)}) collective-permute-start(bf16[128,1024]{0,1:T(8,128)(2,1)S(1)} %bitcast.144), channel_id=1, source_target_pairs={{4,6},{6,4},{8,10},{10,8},{12,14},{14,12},{5,7},{7,5},{9,11},{11,9... | collective-permute-start | bytes 786440 | tf_op jit(solution)/shard_map/ppermute | solution.py:72
  142.5 6.3 %collective-permute-start.19 = (bf16[128,1024]{0,1:T(8,128)(2,1)S(1)}, bf16[128,1024]{0,1:T(8,128)(2,1)S(1)}, u32[]{:S(2)}, u32[]{:S(2)}) collective-permute-start(bf16[128,1024]{0,1:T(8,128)(2,1)S(1)} %collective-permute-done.18), channel_id=1, source_target_pairs={{4,8},{6,10},{8,12},{10,14},{5,9},{7,11},{9,13},{11,15},{20,24},{2... | collective-permute-start | bytes 786440 | tf_op jit(solution)/shard_map/ppermute | solution.py:41
  143.3 7.0 %collective-permute-start.16 = (bf16[128,1024]{0,1:T(8,128)(2,1)S(1)}, bf16[128,1024]{0,1:T(8,128)(2,1)S(1)}, u32[]{:S(2)}, u32[]{:S(2)}) collective-permute-start(bf16[128,1024]{0,1:T(8,128)(2,1)S(1)} %fusion.24), channel_id=1, source_target_pairs={{8,4},{10,6},{12,8},{14,10},{9,5},{11,7},{13,9},{15,11},{24,20},{2... | collective-permute-start | bytes 786440 | tf_op jit(solution)/shard_map/ppermute | solution.py:80
  144.0 8.5 %collective-permute-start.21 = (bf16[128,1024]{0,1:T(8,128)(2,1)S(1)}, bf16[128,1024]{0,1:T(8,128)(2,1)S(1)}, u32[]{:S(2)}, u32[]{:S(2)}) collective-permute-start(bf16[128,1024]{0,1:T(8,128)(2,1)S(1)} %copy-done.6), channel_id=1, source_target_pairs={{0,2},{4,6},{8,10},{12,14},{1,3},{5,7},{9,11},{13,15},{16,18},{20,... | collective-permute-start | bytes 786440 | tf_op jit(solution)/shard_map/ppermute | solution.py:43
  147.4 14.7 %collective-permute-start.11 = (bf16[128,1024]{0,1:T(8,128)(2,1)S(1)}, bf16[128,1024]{0,1:T(8,128)(2,1)S(1)}, u32[]{:S(2)}, u32[]{:S(2)}) collective-permute-start(bf16[128,1024]{0,1:T(8,128)(2,1)S(1)} %bitcast.143), channel_id=1, source_target_pairs={{2,0},{6,4},{10,8},{14,12},{3,1},{7,5},{11,9},{15,13},{18,16},{22,... | collective-permute-start | bytes 786440 | tf_op jit(solution)/shard_map/ppermute | solution.py:69
  148.8 2.3 collective-permute-start.20
  149.6 3.9 %collective-permute-start.22 = (bf16[128,1024]{0,1:T(8,128)(2,1)S(1)}, bf16[128,1024]{0,1:T(8,128)(2,1)S(1)}, u32[]{:S(2)}, u32[]{:S(2)}) collective-permute-start(bf16[128,1024]{0,1:T(8,128)(2,1)S(1)} %collective-permute-done.18), channel_id=1, source_target_pairs={{6,4},{4,6},{10,8},{8,10},{14,12},{12,14},{7,5},{5,7},{11,9},{9,11... | collective-permute-start | bytes 786440 | tf_op jit(solution)/shard_map/ppermute | solution.py:46
  150.3 3.3 %collective-permute-start.23 = (bf16[128,1024]{0,1:T(8,128)(2,1)S(1)}, bf16[128,1024]{0,1:T(8,128)(2,1)S(1)}, u32[]{:S(2)}, u32[]{:S(2)}) collective-permute-start(bf16[128,1024]{0,1:T(8,128)(2,1)S(1)} %collective-permute-done.19), channel_id=1, source_target_pairs={{10,8},{8,10},{14,12},{12,14},{11,9},{9,11},{15,13},{13,15},{26,24... | collective-permute-start | bytes 786440 | tf_op jit(solution)/shard_map/ppermute | solution.py:46
  151.1 31.0 %collective-permute-start.17 = (bf16[128,1024]{0,1:T(8,128)(2,1)S(1)}, bf16[128,1024]{0,1:T(8,128)(2,1)S(1)}, u32[]{:S(2)}, u32[]{:S(2)}) collective-permute-start(bf16[128,1024]{0,1:T(8,128)(2,1)S(1)} %fusion.26), channel_id=1, source_target_pairs={{4,0},{6,2},{8,4},{10,6},{12,8},{14,10},{5,1},{7,3},{9,5},{11,7},{... | collective-permute-start | bytes 786440 | tf_op jit(solution)/shard_map/ppermute | solution.py:80
  152.5 1.2 collective-permute-start.24
  185.7 6.4 %collective-permute-start.28 = (bf16[128,1024]{1,0:T(8,128)(2,1)}, bf16[128,1024]{1,0:T(8,128)(2,1)}, u32[]{:S(2)}, u32[]{:S(2)}) collective-permute-start(bf16[128,1024]{1,0:T(8,128)(2,1)} %copy.73), channel_id=1, source_target_pairs={{12,14},{14,12},{13,15},{15,13},{28,30},{30,28},{29,31},{31,29}} | collective-permute-start | bytes 786440 | tf_op jit(solution)/shard_map/ppermute | solution.py:72
  188.0 20.2 %collective-permute-start.27 = (bf16[128,1024]{1,0:T(8,128)(2,1)}, bf16[128,1024]{1,0:T(8,128)(2,1)}, u32[]{:S(2)}, u32[]{:S(2)}) collective-permute-start(bf16[128,1024]{1,0:T(8,128)(2,1)} %copy.71), channel_id=1, source_target_pairs={{8,10},{10,8},{12,14},{14,12},{9,11},{11,9},{13,15},{15,13},{24,26... | collective-permute-start | bytes 786440 | tf_op jit(solution)/shard_map/ppermute | solution.py:72
  191.2 13.3 %collective-permute-start.32 = (f32[464,128]{1,0:T(8,128)}, f32[464,128]{1,0:T(8,128)}, u32[]{:S(2)}, u32[]{:S(2)}) collective-permute-start(f32[464,128]{1,0:T(8,128)} %maximum_bitcast_fusion), channel_id=1, source_target_pairs={{0,1},{1,0},{2,3},{3,2},{4,5},{5,4},{6,7},{7,6},{8,9},{9,8},{10,11... | collective-permute-start | bytes 712712 | tf_op jit(solution)/shard_map/ppermute | solution.py:19
  194.0 14.1 %collective-permute-start.29 = (bf16[128,1024]{1,0:T(8,128)(2,1)}, bf16[128,1024]{1,0:T(8,128)(2,1)}, u32[]{:S(2)}, u32[]{:S(2)}) collective-permute-start(bf16[128,1024]{1,0:T(8,128)(2,1)} %add_convert_fusion.3), channel_id=1, source_target_pairs={{12,8},{14,10},{13,9},{15,11},{28,24},{30,26},{29,25},{31,27}} | collective-permute-start | bytes 786440 | tf_op jit(solution)/shard_map/ppermute | solution.py:80
  199.1 33.1 %copy-start.13 = (bf16[2688,16]{0,1:T(8,128)(2,1)S(1)}, bf16[2688,16]{0,1:T(8,128)(2,1)}, u32[]{:S(2)}) copy-start(bf16[2688,16]{0,1:T(8,128)(2,1)} %param.14) | copy-start | bytes 258052
  200.9 56.1 %collective-permute-start.26 = (bf16[128,1024]{1,0:T(8,128)(2,1)}, bf16[128,1024]{1,0:T(8,128)(2,1)}, u32[]{:S(2)}, u32[]{:S(2)}) collective-permute-start(bf16[128,1024]{1,0:T(8,128)(2,1)} %copy.69), channel_id=1, source_target_pairs={{4,6},{6,4},{8,10},{10,8},{12,14},{14,12},{5,7},{7,5},{9,11},{11,9... | collective-permute-start | bytes 786440 | tf_op jit(solution)/shard_map/ppermute | solution.py:72
  203.2 67.3 %collective-permute-start.25 = (bf16[128,1024]{1,0:T(8,128)(2,1)}, bf16[128,1024]{1,0:T(8,128)(2,1)S(1)}, u32[]{:S(2)}, u32[]{:S(2)}) collective-permute-start(bf16[128,1024]{1,0:T(8,128)(2,1)} %copy.68), channel_id=1, source_target_pairs={{2,0},{6,4},{10,8},{14,12},{3,1},{7,5},{11,9},{15,13},{18,16},{22,... | collective-permute-start | bytes 786440 | tf_op jit(solution)/shard_map/ppermute | solution.py:69
  205.4 13.6 %collective-permute-start.33 = (f32[464,128]{1,0:T(8,128)S(1)}, f32[464,128]{1,0:T(8,128)S(1)}, u32[]{:S(2)}, u32[]{:S(2)}) collective-permute-start(f32[464,128]{1,0:T(8,128)S(1)} %fusion.34), channel_id=1, source_target_pairs={{0,2},{2,0},{4,6},{6,4},{8,10},{10,8},{12,14},{14,12},{1,3},{3,1},... | collective-permute-start | bytes 712712 | tf_op jit(solution)/shard_map/ppermute | solution.py:19
  209.3 47.7 %collective-permute-start.30 = (bf16[128,1024]{1,0:T(8,128)(2,1)S(1)}, bf16[128,1024]{1,0:T(8,128)(2,1)S(1)}, u32[]{:S(2)}, u32[]{:S(2)}) collective-permute-start(bf16[128,1024]{1,0:T(8,128)(2,1)S(1)} %add_convert_fusion.2), channel_id=1, source_target_pairs={{8,4},{10,6},{12,8},{14,10},{9,5},{11,7},{13,9},{15,11},{24,20},{2... | collective-permute-start | bytes 786440 | tf_op jit(solution)/shard_map/ppermute | solution.py:80
  220.0 18.0 %collective-permute-start.34 = (f32[464,128]{1,0:T(8,128)S(1)}, f32[464,128]{1,0:T(8,128)S(1)}, u32[]{:S(2)}, u32[]{:S(2)}) collective-permute-start(f32[464,128]{1,0:T(8,128)S(1)} %fusion.63), channel_id=1, source_target_pairs={{0,4},{2,6},{4,0},{6,2},{8,12},{10,14},{12,8},{14,10},{1,5},{3,7},... | collective-permute-start | bytes 712712 | tf_op jit(solution)/shard_map/ppermute | solution.py:19
  238.1 30.2 %collective-permute-start.35 = (f32[464,128]{1,0:T(8,128)S(1)}, f32[464,128]{1,0:T(8,128)S(1)}, u32[]{:S(2)}, u32[]{:S(2)}) collective-permute-start(f32[464,128]{1,0:T(8,128)S(1)} %add.189), channel_id=1, source_target_pairs={{0,8},{2,10},{4,12},{6,14},{8,0},{10,2},{12,4},{14,6},{1,9},{3,11}... | collective-permute-start | bytes 712712 | tf_op jit(solution)/shard_map/ppermute | solution.py:19
  258.7 13.4 %collective-permute-start.31 = (bf16[128,1024]{1,0:T(8,128)(2,1)}, bf16[128,1024]{1,0:T(8,128)(2,1)}, u32[]{:S(2)}, u32[]{:S(2)}) collective-permute-start(bf16[128,1024]{1,0:T(8,128)(2,1)} %add_convert_fusion.1), channel_id=1, source_target_pairs={{4,0},{6,2},{8,4},{10,6},{12,8},{14,10},{5,1},{7,3},{9,5},{11,7},{... | collective-permute-start | bytes 786440 | tf_op jit(solution)/shard_map/ppermute | solution.py:80
  (9 other events, 24.6 us)
Sparse Core Ops, SparseCore 0:
  10.8 58.7 all-gather.2
  71.1 14.1 all-gather.4

commit v7 on v6

--- a/solution.py
+++ b/solution.py
@@ -46,6 +46,40 @@
             lax.ppermute(climbed[step - 1], "ctx", [(c ^ 1, c) for c in range(2 * step, count)])
         )
     return climbed + crossed
+
+
+def tree_gather(block, ctx_index, levels):
+    count = 2 * levels
+    partner = jnp.bitwise_xor(ctx_index, 1)
+    got = [block]
+    owners = [ctx_index]
+    valid = [ctx_index >= 0]
+    up, down = block, block
+    ups, downs = [], []
+    for step in range(1, levels):
+        up = lax.ppermute(up, "ctx", [(c - 2, c) for c in range(2 * step, count)])
+        down = lax.ppermute(down, "ctx", [(c + 2, c) for c in range(0, count - 2 * step)])
+        ups.append(up)
+        downs.append(down)
+        got += [up, down]
+        owners += [ctx_index - 2 * step, ctx_index + 2 * step]
+        valid += [ctx_index >= 2 * step, ctx_index < count - 2 * step]
+    got.append(lax.ppermute(block, "ctx", [(c ^ 1, c) for c in range(count)]))
+    owners.append(partner)
+    valid.append(ctx_index >= 0)
+    for step in range(1, levels):
+        got.append(lax.ppermute(ups[step - 1], "ctx", [(c ^ 1, c) for c in range(2 * step, count)]))
+        got.append(
+            lax.ppermute(downs[step - 1], "ctx", [(c ^ 1, c) for c in range(0, count - 2 * step)])
+        )
+        owners += [partner - 2 * step, partner + 2 * step]
+        valid += [ctx_index >= 2 * step, ctx_index < count - 2 * step]
+    rows = block.shape[0]
+    whole = jnp.zeros(((count + 1) * rows,) + block.shape[1:], block.dtype)
+    for piece, owner, ok in zip(got, owners, valid):
+        place = jnp.where(ok, owner, count) * rows
+        whole = lax.dynamic_update_slice_in_dim(whole, piece, place, 0)
+    return whole[: count * rows]
 
 
 def tree_slots(ctx_index, levels):
@@ -113,7 +147,11 @@
     ctx_index = lax.axis_index("ctx")
     half_cols = width_kv // 2
     own_half = lax.dynamic_slice_in_dim(value_projection, pair_index * half_cols, half_cols, 1)
-    rows_half = lax.all_gather(own_half, "ctx", axis=0, tiled=True)
+    ctx_count = lax.axis_size("ctx")
+    if ctx_count % 2 == 0 and 4 <= ctx_count <= 8:
+        rows_half = tree_gather(own_half, ctx_index, ctx_count // 2)
+    else:
+        rows_half = lax.all_gather(own_half, "ctx", axis=0, tiled=True)
     full_weight = lax.all_gather(rows_half, "pair", axis=1, tiled=True)
     rank_projection = jnp.dot(hidden_rows, adapter_down, preferred_element_type=jnp.float32).astype(
         jnp.bfloat16

time: 282 us -> 279 us (0.989)
  waiting for transfers between devices: 109 us -> 68.8 us
  starting transfers between devices: 88.7 us -> 110 us
  local copies, waits for them, and re-layouts: 25.4 us -> 40.5 us
    all_gather x1 -> x0, waiting for transfers between devices: 60.4 us -> none  [shards(): rows_half = lax.all_gather(own_half, 'ctx', axis=0, tiled=True)]
    ppermute x0 -> x13, waiting for transfers between devices: none -> 22.4 us  [the longest x3 11.8 us: tree_gather(): lax.ppermute(down, 'ctx', [(c + 2, c) for c in range(0, count - 2 * step)])]
    ppermute x0 -> x13, starting transfers between devices: none -> 21.9 us  [the longest x3 8.2 us: tree_gather(): lax.ppermute(downs[step - 1], 'ctx', [(c ^ 1, c) for c in range(0, count...]
    dynamic_update_slice x0 -> x14, local copies, waits for them, and re-layouts: none -> 10.7 us  [tree_gather(): whole = lax.dynamic_update_slice_in_dim(whole, piece, place, 0)]
    slice x0 -> x1, local copies, waits for them, and re-layouts: none -> 3.59 us  [tree_gather(): return whole[:count * rows]]
    unnamed x56 -> x58, local copies, waits for them, and re-layouts: 6.93 us -> 6.93 us
  transfers between devices with their start and end apart: 38 -> 50, of which waited for: 11 -> 16; matrix products, arithmetic and copies ran while one was open for 14% -> 18% of each run, Pallas kernels for 0% -> 0%
where the time goes in v7:
time: 279 us; the launch traced here: 277 us
  starting transfers between devices  110 us (39%)
  waiting for transfers between devices  68.8 us (25%)
  local copies, waits for them, and re-layouts  40.5 us (15%)
  matrix products  28.7 us (10%)
  between operations  15.1 us (5%)
  other arithmetic  14.2 us (5%)
    ppermute x8, starting transfers between devices, from_partner(): lax.ppermute(shard, axis, [(i, i ^ 1 << stride) for i in range(lax.axis_s...  38.4 us
    ppermute x6, starting transfers between devices, tree_spread(): lax.ppermute(held, 'ctx', [(c - 2, c) for c in range(2 * step, count)])  23.7 us
    ppermute x8, waiting for transfers between devices, from_partner(): lax.ppermute(shard, axis, [(i, i ^ 1 << stride) for i in range(lax.axis_s...  21.9 us
    ppermute x6, waiting for transfers between devices, tree_return(): lax.ppermute(acc.astype(jnp.bfloat16), 'ctx', [(c, c - 2) for c in range(...  21.7 us
    ppermute x3, waiting for transfers between devices, tree_gather(): lax.ppermute(down, 'ctx', [(c + 2, c) for c in range(0, count - 2 * step)])  11.8 us
    dynamic_update_slice x14, local copies, waits for them, and re-layouts, tree_gather(): whole = lax.dynamic_update_slice_in_dim(whole, piece, place, 0)  10.7 us
    ppermute x3, starting transfers between devices, tree_gather(): lax.ppermute(downs[step - 1], 'ctx', [(c ^ 1, c) for c in range(0, count...  8.2 us
    ppermute x2, starting transfers between devices, tree_spread(): lax.ppermute(block, 'ctx', [(c - 1, c) for c in range(1, count, 2)])  7.12 us
  transfers between devices with their start and end apart: 50, of which 16 were waited for; matrix products, arithmetic and copies ran while one was open for 18% of the time, Pallas kernels for 0%

profile of v7, /device:TPU:0, one launch (start us, length us, event | category | flops | bytes accessed | tf_op | source)
XLA Modules:
  0.0 277.4 jit_solution(11138782290476178601)
XLA Ops:
  7.2 1.8 broadcast_in_dim.54
  9.9 4.9 %collective-permute-start.10 = (bf16[336,512]{1,0:T(8,128)(2,1)S(1)}, bf16[336,512]{1,0:T(8,128)(2,1)S(1)}, u32[]{:S(2)}, u32[]{:S(2)}) collective-permute-start(bf16[336,512]{1,0:T(8,128)(2,1)S(1)} %get-tuple-element.29), channel_id=1, source_target_pairs={{0,4},{2,6},{4,8},{6,10},{8,12},{10,14},{1,5},{3,7},{5,9},{7,11},{... | collective-permute-start | bytes 1032200 | tf_op jit(solution)/shard_map/ppermute | solution.py:60
  16.1 6.0 %collective-permute-done.10 = bf16[336,512]{1,0:T(8,128)(2,1)S(1)} collective-permute-done((bf16[336,512]{1,0:T(8,128)(2,1)S(1)}, bf16[336,512]{1,0:T(8,128)(2,1)S(1)}, u32[]{:S(2)}, u32[]{:S(2)}) %collective-permute-start.10) | collective-permute-done | bytes 344096 | tf_op jit(solution)/shard_map/ppermute | solution.py:60
  22.7 3.5 %collective-permute-done.11 = bf16[336,512]{1,0:T(8,128)(2,1)S(1)} collective-permute-done((bf16[336,512]{1,0:T(8,128)(2,1)S(1)}, bf16[336,512]{1,0:T(8,128)(2,1)S(1)}, u32[]{:S(2)}, u32[]{:S(2)}) %collective-permute-start.11) | collective-permute-done | bytes 344096 | tf_op jit(solution)/shard_map/ppermute | solution.py:61
  27.5 1.6 collective-permute-start.16
  29.8 2.4 collective-permute-start.18
  34.4 2.5 collective-permute-done.13
  41.1 5.8 %collective-permute-done.15 = bf16[336,512]{1,0:T(8,128)(2,1)S(1)} collective-permute-done((bf16[336,512]{1,0:T(8,128)(2,1)S(1)}, bf16[336,512]{1,0:T(8,128)(2,1)S(1)}, u32[]{:S(2)}, u32[]{:S(2)}) %collective-permute-start.15) | collective-permute-done | bytes 344096 | tf_op jit(solution)/shard_map/ppermute | solution.py:61
  46.9 3.0 %collective-permute-start.20 = (bf16[336,512]{1,0:T(8,128)(2,1)S(1)}, bf16[336,512]{1,0:T(8,128)(2,1)S(1)}, u32[]{:S(2)}, u32[]{:S(2)}) collective-permute-start(bf16[336,512]{1,0:T(8,128)(2,1)S(1)} %collective-permute-done.13), channel_id=1, source_target_pairs={{2,0},{0,2},{6,4},{4,6},{3,1},{1,3},{7,5},{5,7},{18,16},{16,18},{2... | collective-permute-start | bytes 1032200 | tf_op jit(solution)/shard_map/ppermute | solution.py:73
  52.2 2.8 %collective-permute-start.22 = (bf16[336,512]{1,0:T(8,128)(2,1)S(1)}, bf16[336,512]{1,0:T(8,128)(2,1)S(1)}, u32[]{:S(2)}, u32[]{:S(2)}) collective-permute-start(bf16[336,512]{1,0:T(8,128)(2,1)S(1)} %collective-permute-done.15), channel_id=1, source_target_pairs={{2,0},{0,2},{3,1},{1,3},{18,16},{16,18},{19,17},{17,19}} | collective-permute-start | bytes 1032200 | tf_op jit(solution)/shard_map/ppermute | solution.py:73
  57.3 1.5 collective-permute-done.20
  60.3 3.1 %collective-permute-done.22 = bf16[336,512]{1,0:T(8,128)(2,1)S(1)} collective-permute-done((bf16[336,512]{1,0:T(8,128)(2,1)S(1)}, bf16[336,512]{1,0:T(8,128)(2,1)S(1)}, u32[]{:S(2)}, u32[]{:S(2)}) %collective-permute-start.22) | collective-permute-done | bytes 344096 | tf_op jit(solution)/shard_map/ppermute | solution.py:73
  64.2 3.6 %slice.122 = bf16[2688,512]{1,0:T(8,128)(2,1)} slice(bf16[3024,512]{1,0:T(8,128)(2,1)} %constant_dynamic-update-slice_fusion.24), slice={[0:2688], [0:512]} | slice | bytes 5505024 | tf_op jit(solution)/shard_map/slice | solution.py:82
  67.8 1.4 collective-permute-start.3
  69.3 3.8 %collective-permute-start.6 = (bf16[128,1024]{1,0:T(8,128)(2,1)}, bf16[128,1024]{1,0:T(8,128)(2,1)}, u32[]{:S(2)}, u32[]{:S(2)}) collective-permute-start(bf16[128,1024]{1,0:T(8,128)(2,1)} %bitcast.4), channel_id=1, source_target_pairs={{0,2},{4,6},{8,10},{12,14},{1,3},{5,7},{9,11},{13,15},{16,18},{20,... | collective-permute-start | bytes 786440 | tf_op jit(solution)/shard_map/ppermute | solution.py:43
  75.3 1.6 collective-permute-done
  76.9 2.3 collective-permute-start.1
  80.8 2.3 collective-permute-start.2
  83.1 2.2 collective-permute-done.2
  92.7 4.9 %fusion.15 = bf16[128,1024]{0,1:T(8,128)(2,1)} fusion(f32[128,1024]{0,1:T(8,128)S(1)} %convolution_multiply_fusion.2, bf16[2688,1024]{1,0:T(8,128)(2,1)} %all-gather.2.cloned.1.call-done, bf16[1,128,2688]{2,1,0:T(8,128)(2,1)S(1)} %copy-done), kind=kOutput, calls=%fused_computation.28 | convolution fusion | flops 704905216 | bytes 6979584 | tf_op jit(solution)/shard_map/dot_general | solution.py:160
  97.6 2.0 copy.95
  99.6 3.3 %copy.84 = bf16[1024,8,128,1]{0,2,3,1:T(8,128)(2,1)S(1)} copy(bf16[1024,8,128,1]{2,1,0,3:T(8,128)(2,1)} %bitcast.134) | data formatting | bytes 4194304 | tf_op jit(solution)/shard_map/reshape | solution.py:215
  102.9 5.7 %fusion.38 = (f32[8,2,128]{2,1,0:T(2,128)S(1)}, f32[8,2,128,1024]{2,3,1,0:T(8,128)}) fusion(pred[128,1024]{0,1:T(8,128)(4,1)S(1)} %compare_and_fusion, bf16[1024,8,128,1]{0,2,3,1:T(8,128)(2,1)S(1)} %copy.84, bf16[128,8,2,128]{0,3,2,1:T(8,128)(2,1)S(1)} %bitcast.138), kind=kOutput, calls=%fused_computation.124 | convolution fusion | flops 547357696 | bytes 11149312 | tf_op jit(solution)/shard_map/sub | solution.py:222
  108.6 5.0 %fusion.39 = (bf16[1024,8,128]{0,2,1:T(8,128)(2,1)S(1)}, f32[1024,8,128]{0,2,1:T(8,128)S(1)}) fusion(bf16[128,8,2,128]{3,2,1,0:T(2,128)(2,1)} %reshape_squeeze.7, f32[128]{0:T(128)S(1)} %get-tuple-element.25, f32[8,2,128,1024]{2,3,1,0:T(8,128)} %get-tuple-element.49, f32[8,2,128]{2,1,0:T(2,128)S(1)} %get-tuple-element.48), kind=kOutput, calls=%fused_computation.125 | convolution fusion | flops 544210944 | bytes 15213056 | tf_op jit(solution)/shard_map/jgtl,tjgd->ljd/dot_general | solution.py:236
  114.9 19.4 %collective-permute-start.31 = (bf16[128,1024]{0,1:T(8,128)(2,1)S(1)}, bf16[128,1024]{0,1:T(8,128)(2,1)S(1)}, u32[]{:S(2)}, u32[]{:S(2)}) collective-permute-start(bf16[128,1024]{0,1:T(8,128)(2,1)S(1)} %copy-done.5), channel_id=1, source_target_pairs={{0,4},{2,6},{4,8},{6,10},{8,12},{10,14},{1,5},{3,7},{5,9},{7,11},{... | collective-permute-start | bytes 786440 | tf_op jit(solution)/shard_map/ppermute | solution.py:41
  136.5 2.7 collective-permute-done.31
  140.8 3.3 %collective-permute-start.34 = (bf16[128,1024]{0,1:T(8,128)(2,1)S(1)}, bf16[128,1024]{0,1:T(8,128)(2,1)S(1)}, u32[]{:S(2)}, u32[]{:S(2)}) collective-permute-start(bf16[128,1024]{0,1:T(8,128)(2,1)S(1)} %copy-done.5), channel_id=1, source_target_pairs={{0,2},{4,6},{8,10},{12,14},{1,3},{5,7},{9,11},{13,15},{16,18},{20,... | collective-permute-start | bytes 786440 | tf_op jit(solution)/shard_map/ppermute | solution.py:43
  144.3 1.4 collective-permute-start.24
  150.7 1.9 fusion.1
  152.7 1.7 fusion.3
  155.4 3.5 %fusion.40 = (bf16[1024,8,128]{0,2,1:T(8,128)(2,1)S(1)}, f32[1024,8,128]{0,2,1:T(8,128)}) fusion(bf16[8,2,128,1024]{2,3,1,0:T(8,128)(2,1)S(1)} %fusion.3, bf16[128,8,2,128]{0,3,2,1:T(8,128)(2,1)S(1)} %bitcast.139), kind=kOutput, calls=%fused_computation.126 | convolution fusion | flops 537919488 | bytes 11010048 | tf_op jit(solution)/shard_map/jgtl,tjgd->ljd/dot_general | solution.py:232
  158.9 20.0 %collective-permute-done.30 = bf16[128,1024]{0,1:T(8,128)(2,1)S(1)} collective-permute-done((bf16[128,1024]{0,1:T(8,128)(2,1)S(1)}, bf16[128,1024]{0,1:T(8,128)(2,1)S(1)}, u32[]{:S(2)}, u32[]{:S(2)}) %collective-permute-start.30) | collective-permute-done | bytes 262176 | tf_op jit(solution)/shard_map/ppermute | solution.py:114
  182.5 1.4 collective-permute-start.41
  184.8 1.4 collective-permute-start.40
  188.9 1.9 add_convert_fusion.3
  190.8 1.4 collective-permute-start.42
  195.7 1.8 copy.69
  197.6 1.4 collective-permute-start.39
  202.1 2.7 collective-permute-start.46
  206.6 9.1 %collective-permute-done.46 = f32[464,128]{1,0:T(8,128)S(1)} collective-permute-done((f32[464,128]{1,0:T(8,128)S(1)}, f32[464,128]{1,0:T(8,128)S(1)}, u32[]{:S(2)}, u32[]{:S(2)}) %collective-permute-start.46) | collective-permute-done | bytes 237600 | tf_op jit(solution)/shard_map/ppermute | solution.py:19
  216.7 12.1 %collective-permute-start.47 = (f32[464,128]{1,0:T(8,128)S(1)}, f32[464,128]{1,0:T(8,128)S(1)}, u32[]{:S(2)}, u32[]{:S(2)}) collective-permute-start(f32[464,128]{1,0:T(8,128)S(1)} %fusion.63), channel_id=1, source_target_pairs={{0,4},{2,6},{4,0},{6,2},{8,12},{10,14},{12,8},{14,10},{1,5},{3,7},... | collective-permute-start | bytes 712712 | tf_op jit(solution)/shard_map/ppermute | solution.py:19
  229.2 5.5 %collective-permute-done.47 = f32[464,128]{1,0:T(8,128)S(1)} collective-permute-done((f32[464,128]{1,0:T(8,128)S(1)}, f32[464,128]{1,0:T(8,128)S(1)}, u32[]{:S(2)}, u32[]{:S(2)}) %collective-permute-start.47) | collective-permute-done | bytes 237600 | tf_op jit(solution)/shard_map/ppermute | solution.py:19
  234.7 19.0 %collective-permute-start.48 = (f32[464,128]{1,0:T(8,128)S(1)}, f32[464,128]{1,0:T(8,128)S(1)}, u32[]{:S(2)}, u32[]{:S(2)}) collective-permute-start(f32[464,128]{1,0:T(8,128)S(1)} %add.269), channel_id=1, source_target_pairs={{0,8},{2,10},{4,12},{6,14},{8,0},{10,2},{12,4},{14,6},{1,9},{3,11}... | collective-permute-start | bytes 712712 | tf_op jit(solution)/shard_map/ppermute | solution.py:19
  253.7 1.8 add_convert_fusion.1
  256.7 5.4 %fusion.11 = bf16[1,128,2688]{2,1,0:T(8,128)(2,1)} fusion(f32[128,2688]{1,0:T(8,128)S(1)} %convolution_multiply_fusion, bf16[128,1024]{0,1:T(8,128)(2,1)S(1)} %fusion.27, bf16[2688,1024]{1,0:T(8,128)(2,1)} %all-gather.2.cloned.1.call-done), kind=kOutput, calls=%fused_computation.19 | convolution fusion | flops 705331200 | bytes 7831552 | tf_op jit(solution)/shard_map/tk,dk->td/dot_general | solution.py:261
  262.1 2.8 %collective-permute-done.48 = f32[464,128]{1,0:T(8,128)S(1)} collective-permute-done((f32[464,128]{1,0:T(8,128)S(1)}, f32[464,128]{1,0:T(8,128)S(1)}, u32[]{:S(2)}, u32[]{:S(2)}) %collective-permute-start.48) | collective-permute-done | bytes 237600 | tf_op jit(solution)/shard_map/ppermute | solution.py:19
  267.1 1.7 collective-permute-done.44
  268.8 1.8 fusion.31
  (202 shorter events, 60.5 us)
Async XLA Ops:
  7.2 85.5 %all-gather.2.cloned.1.call-start = ((), (), s32[]{:S(2)}) async-start(), calls=%async_computation | async-start | bytes 8257536 | tf_op jit(solution)/shard_map/all_gather | solution.py:155
  9.9 12.2 %collective-permute-start.10 = (bf16[336,512]{1,0:T(8,128)(2,1)S(1)}, bf16[336,512]{1,0:T(8,128)(2,1)S(1)}, u32[]{:S(2)}, u32[]{:S(2)}) collective-permute-start(bf16[336,512]{1,0:T(8,128)(2,1)S(1)} %get-tuple-element.29), channel_id=1, source_target_pairs={{0,4},{2,6},{4,8},{6,10},{8,12},{10,14},{1,5},{3,7},{5,9},{7,11},{... | collective-permute-start | bytes 1032200 | tf_op jit(solution)/shard_map/ppermute | solution.py:60
  14.8 11.4 %collective-permute-start.11 = (bf16[336,512]{1,0:T(8,128)(2,1)S(1)}, bf16[336,512]{1,0:T(8,128)(2,1)S(1)}, u32[]{:S(2)}, u32[]{:S(2)}) collective-permute-start(bf16[336,512]{1,0:T(8,128)(2,1)S(1)} %get-tuple-element.29), channel_id=1, source_target_pairs={{4,0},{6,2},{8,4},{10,6},{12,8},{14,10},{5,1},{7,3},{9,5},{11,7},{... | collective-permute-start | bytes 1032200 | tf_op jit(solution)/shard_map/ppermute | solution.py:61
  22.1 10.9 %collective-permute-start.12 = (bf16[336,512]{1,0:T(8,128)(2,1)S(1)}, bf16[336,512]{1,0:T(8,128)(2,1)S(1)}, u32[]{:S(2)}, u32[]{:S(2)}) collective-permute-start(bf16[336,512]{1,0:T(8,128)(2,1)S(1)} %collective-permute-done.10), channel_id=1, source_target_pairs={{4,8},{6,10},{8,12},{10,14},{5,9},{7,11},{9,13},{11,15},{20,24},{2... | collective-permute-start | bytes 1032200 | tf_op jit(solution)/shard_map/ppermute | solution.py:60
  26.2 10.7 %collective-permute-start.13 = (bf16[336,512]{1,0:T(8,128)(2,1)S(1)}, bf16[336,512]{1,0:T(8,128)(2,1)S(1)}, u32[]{:S(2)}, u32[]{:S(2)}) collective-permute-start(bf16[336,512]{1,0:T(8,128)(2,1)S(1)} %collective-permute-done.11), channel_id=1, source_target_pairs={{4,0},{6,2},{8,4},{10,6},{5,1},{7,3},{9,5},{11,7},{20,16},{22,18},... | collective-permute-start | bytes 1032200 | tf_op jit(solution)/shard_map/ppermute | solution.py:61
  27.5 23.3 %collective-permute-start.16 = (bf16[336,512]{1,0:T(8,128)(2,1)S(1)}, bf16[336,512]{1,0:T(8,128)(2,1)S(1)}, u32[]{:S(2)}, u32[]{:S(2)}) collective-permute-start(bf16[336,512]{1,0:T(8,128)(2,1)S(1)} %get-tuple-element.29), channel_id=1, source_target_pairs={{2,0},{0,2},{6,4},{4,6},{10,8},{8,10},{14,12},{12,14},{3,1},{1,3},... | collective-permute-start | bytes 1032200 | tf_op jit(solution)/shard_map/ppermute | solution.py:67
  29.1 23.1 %collective-permute-start.17 = (bf16[336,512]{1,0:T(8,128)(2,1)S(1)}, bf16[336,512]{1,0:T(8,128)(2,1)S(1)}, u32[]{:S(2)}, u32[]{:S(2)}) collective-permute-start(bf16[336,512]{1,0:T(8,128)(2,1)S(1)} %collective-permute-done.10), channel_id=1, source_target_pairs={{6,4},{4,6},{10,8},{8,10},{14,12},{12,14},{7,5},{5,7},{11,9},{9,11... | collective-permute-start | bytes 1032200 | tf_op jit(solution)/shard_map/ppermute | solution.py:71
  29.8 26.0 %collective-permute-start.18 = (bf16[336,512]{1,0:T(8,128)(2,1)S(1)}, bf16[336,512]{1,0:T(8,128)(2,1)S(1)}, u32[]{:S(2)}, u32[]{:S(2)}) collective-permute-start(bf16[336,512]{1,0:T(8,128)(2,1)S(1)} %collective-permute-done.11), channel_id=1, source_target_pairs={{2,0},{0,2},{6,4},{4,6},{10,8},{8,10},{3,1},{1,3},{7,5},{5,7},{11,... | collective-permute-start | bytes 1032200 | tf_op jit(solution)/shard_map/ppermute | solution.py:73
  32.9 6.7 %collective-permute-start.14 = (bf16[336,512]{1,0:T(8,128)(2,1)S(1)}, bf16[336,512]{1,0:T(8,128)(2,1)S(1)}, u32[]{:S(2)}, u32[]{:S(2)}) collective-permute-start(bf16[336,512]{1,0:T(8,128)(2,1)S(1)} %collective-permute-done.12), channel_id=1, source_target_pairs={{8,12},{10,14},{9,13},{11,15},{24,28},{26,30},{25,29},{27,31}} | collective-permute-start | bytes 1032200 | tf_op jit(solution)/shard_map/ppermute | solution.py:60
  36.9 10.1 %collective-permute-start.15 = (bf16[336,512]{1,0:T(8,128)(2,1)S(1)}, bf16[336,512]{1,0:T(8,128)(2,1)S(1)}, u32[]{:S(2)}, u32[]{:S(2)}) collective-permute-start(bf16[336,512]{1,0:T(8,128)(2,1)S(1)} %collective-permute-done.13), channel_id=1, source_target_pairs={{4,0},{6,2},{5,1},{7,3},{20,16},{22,18},{21,17},{23,19}} | collective-permute-start | bytes 1032200 | tf_op jit(solution)/shard_map/ppermute | solution.py:61
  39.7 16.9 %collective-permute-start.19 = (bf16[336,512]{1,0:T(8,128)(2,1)S(1)}, bf16[336,512]{1,0:T(8,128)(2,1)S(1)}, u32[]{:S(2)}, u32[]{:S(2)}) collective-permute-start(bf16[336,512]{1,0:T(8,128)(2,1)S(1)} %collective-permute-done.12), channel_id=1, source_target_pairs={{10,8},{8,10},{14,12},{12,14},{11,9},{9,11},{15,13},{13,15},{26,24... | collective-permute-start | bytes 1032200 | tf_op jit(solution)/shard_map/ppermute | solution.py:71
  46.9 11.9 %collective-permute-start.20 = (bf16[336,512]{1,0:T(8,128)(2,1)S(1)}, bf16[336,512]{1,0:T(8,128)(2,1)S(1)}, u32[]{:S(2)}, u32[]{:S(2)}) collective-permute-start(bf16[336,512]{1,0:T(8,128)(2,1)S(1)} %collective-permute-done.13), channel_id=1, source_target_pairs={{2,0},{0,2},{6,4},{4,6},{3,1},{1,3},{7,5},{5,7},{18,16},{16,18},{2... | collective-permute-start | bytes 1032200 | tf_op jit(solution)/shard_map/ppermute | solution.py:73
  50.8 8.8 %collective-permute-start.21 = (bf16[336,512]{1,0:T(8,128)(2,1)S(1)}, bf16[336,512]{1,0:T(8,128)(2,1)S(1)}, u32[]{:S(2)}, u32[]{:S(2)}) collective-permute-start(bf16[336,512]{1,0:T(8,128)(2,1)S(1)} %collective-permute-done.14), channel_id=1, source_target_pairs={{14,12},{12,14},{15,13},{13,15},{30,28},{28,30},{31,29},{29,31}} | collective-permute-start | bytes 1032200 | tf_op jit(solution)/shard_map/ppermute | solution.py:71
  52.2 11.2 %collective-permute-start.22 = (bf16[336,512]{1,0:T(8,128)(2,1)S(1)}, bf16[336,512]{1,0:T(8,128)(2,1)S(1)}, u32[]{:S(2)}, u32[]{:S(2)}) collective-permute-start(bf16[336,512]{1,0:T(8,128)(2,1)S(1)} %collective-permute-done.15), channel_id=1, source_target_pairs={{2,0},{0,2},{3,1},{1,3},{18,16},{16,18},{19,17},{17,19}} | collective-permute-start | bytes 1032200 | tf_op jit(solution)/shard_map/ppermute | solution.py:73
  67.8 17.7 %collective-permute-start.3 = (bf16[128,1024]{1,0:T(8,128)(2,1)}, bf16[128,1024]{1,0:T(8,128)(2,1)S(1)}, u32[]{:S(2)}, u32[]{:S(2)}) collective-permute-start(bf16[128,1024]{1,0:T(8,128)(2,1)} %bitcast.4), channel_id=1, source_target_pairs={{0,4},{2,6},{4,8},{6,10},{8,12},{10,14},{1,5},{3,7},{5,9},{7,11},{... | collective-permute-start | bytes 786440 | tf_op jit(solution)/shard_map/ppermute | solution.py:41
  69.3 21.3 %collective-permute-start.6 = (bf16[128,1024]{1,0:T(8,128)(2,1)}, bf16[128,1024]{1,0:T(8,128)(2,1)}, u32[]{:S(2)}, u32[]{:S(2)}) collective-permute-start(bf16[128,1024]{1,0:T(8,128)(2,1)} %bitcast.4), channel_id=1, source_target_pairs={{0,2},{4,6},{8,10},{12,14},{1,3},{5,7},{9,11},{13,15},{16,18},{20,... | collective-permute-start | bytes 786440 | tf_op jit(solution)/shard_map/ppermute | solution.py:43
  73.3 3.5 %collective-permute-start = (f32[16]{0:T(128)S(1)}, f32[16]{0:T(128)S(1)}, u32[]{:S(2)}, u32[]{:S(2)}) collective-permute-start(f32[16]{0:T(128)S(1)} %pad_maximum_fusion), channel_id=1, source_target_pairs={{0,2},{2,0},{4,6},{6,4},{8,10},{10,8},{12,14},{14,12},{1,3},{3,1},... | collective-permute-start | bytes 200 | tf_op jit(solution)/shard_map/ppermute | solution.py:19
  76.9 3.9 %collective-permute-start.1 = (f32[16]{0:T(128)S(1)}, f32[16]{0:T(128)S(1)}, u32[]{:S(2)}, u32[]{:S(2)}) collective-permute-start(f32[16]{0:T(128)S(1)} %fusion.64), channel_id=1, source_target_pairs={{0,4},{2,6},{4,0},{6,2},{8,12},{10,14},{12,8},{14,10},{1,5},{3,7},... | collective-permute-start | bytes 200 | tf_op jit(solution)/shard_map/ppermute | solution.py:19
  80.8 4.4 %collective-permute-start.2 = (f32[16]{0:T(128)S(1)}, f32[16]{0:T(128)S(1)}, u32[]{:S(2)}, u32[]{:S(2)}) collective-permute-start(f32[16]{0:T(128)S(1)} %add.227), channel_id=1, source_target_pairs={{0,8},{2,10},{4,12},{6,14},{8,0},{10,2},{12,4},{14,6},{1,9},{3,11}... | collective-permute-start | bytes 200 | tf_op jit(solution)/shard_map/ppermute | solution.py:19
  85.3 1.1 collective-permute-start.23
  86.6 3.3 %collective-permute-start.5 = (bf16[128,1024]{1,0:T(8,128)(2,1)S(1)}, bf16[128,1024]{1,0:T(8,128)(2,1)S(1)}, u32[]{:S(2)}, u32[]{:S(2)}) collective-permute-start(bf16[128,1024]{1,0:T(8,128)(2,1)S(1)} %collective-permute-done.4), channel_id=1, source_target_pairs={{8,12},{10,14},{9,13},{11,15},{24,28},{26,30},{25,29},{27,31}} | collective-permute-start | bytes 786440 | tf_op jit(solution)/shard_map/ppermute | solution.py:41
  88.5 3.1 %collective-permute-start.7 = (bf16[128,1024]{1,0:T(8,128)(2,1)}, bf16[128,1024]{1,0:T(8,128)(2,1)S(1)}, u32[]{:S(2)}, u32[]{:S(2)}) collective-permute-start(bf16[128,1024]{1,0:T(8,128)(2,1)} %copy-done.14), channel_id=1, source_target_pairs={{6,4},{4,6},{10,8},{8,10},{14,12},{12,14},{7,5},{5,7},{11,9},{9,11... | collective-permute-start | bytes 786440 | tf_op jit(solution)/shard_map/ppermute | solution.py:46
  89.2 2.5 collective-permute-start.8
  89.9 1.8 collective-permute-start.9
  114.1 20.9 %collective-permute-start.27 = (bf16[128,1024]{0,1:T(8,128)(2,1)S(1)}, bf16[128,1024]{0,1:T(8,128)(2,1)S(1)}, u32[]{:S(2)}, u32[]{:S(2)}) collective-permute-start(bf16[128,1024]{0,1:T(8,128)(2,1)S(1)} %bitcast.150), channel_id=1, source_target_pairs={{12,14},{14,12},{13,15},{15,13},{28,30},{30,28},{29,31},{31,29}} | collective-permute-start | bytes 786440 | tf_op jit(solution)/shard_map/ppermute | solution.py:106
  114.9 24.2 %collective-permute-start.31 = (bf16[128,1024]{0,1:T(8,128)(2,1)S(1)}, bf16[128,1024]{0,1:T(8,128)(2,1)S(1)}, u32[]{:S(2)}, u32[]{:S(2)}) collective-permute-start(bf16[128,1024]{0,1:T(8,128)(2,1)S(1)} %copy-done.5), channel_id=1, source_target_pairs={{0,4},{2,6},{4,8},{6,10},{8,12},{10,14},{1,5},{3,7},{5,9},{7,11},{... | collective-permute-start | bytes 786440 | tf_op jit(solution)/shard_map/ppermute | solution.py:41
  134.3 5.7 %collective-permute-start.26 = (bf16[128,1024]{0,1:T(8,128)(2,1)S(1)}, bf16[128,1024]{0,1:T(8,128)(2,1)S(1)}, u32[]{:S(2)}, u32[]{:S(2)}) collective-permute-start(bf16[128,1024]{0,1:T(8,128)(2,1)S(1)} %bitcast.149), channel_id=1, source_target_pairs={{8,10},{10,8},{12,14},{14,12},{9,11},{11,9},{13,15},{15,13},{24,26... | collective-permute-start | bytes 786440 | tf_op jit(solution)/shard_map/ppermute | solution.py:106
  135.1 4.9 %collective-permute-start.28 = (bf16[128,1024]{0,1:T(8,128)(2,1)S(1)}, bf16[128,1024]{0,1:T(8,128)(2,1)S(1)}, u32[]{:S(2)}, u32[]{:S(2)}) collective-permute-start(bf16[128,1024]{0,1:T(8,128)(2,1)S(1)} %fusion.22), channel_id=1, source_target_pairs={{12,8},{14,10},{13,9},{15,11},{28,24},{30,26},{29,25},{31,27}} | collective-permute-start | bytes 786440 | tf_op jit(solution)/shard_map/ppermute | solution.py:114
  135.8 10.8 %collective-permute-start.25 = (bf16[128,1024]{0,1:T(8,128)(2,1)S(1)}, bf16[128,1024]{0,1:T(8,128)(2,1)S(1)}, u32[]{:S(2)}, u32[]{:S(2)}) collective-permute-start(bf16[128,1024]{0,1:T(8,128)(2,1)S(1)} %bitcast.148), channel_id=1, source_target_pairs={{4,6},{6,4},{8,10},{10,8},{12,14},{14,12},{5,7},{7,5},{9,11},{11,9... | collective-permute-start | bytes 786440 | tf_op jit(solution)/shard_map/ppermute | solution.py:106
  139.2 6.6 %collective-permute-start.32 = (bf16[128,1024]{0,1:T(8,128)(2,1)S(1)}, bf16[128,1024]{0,1:T(8,128)(2,1)S(1)}, u32[]{:S(2)}, u32[]{:S(2)}) collective-permute-start(bf16[128,1024]{0,1:T(8,128)(2,1)S(1)} %collective-permute-done.31), channel_id=1, source_target_pairs={{4,8},{6,10},{8,12},{10,14},{5,9},{7,11},{9,13},{11,15},{20,24},{2... | collective-permute-start | bytes 786440 | tf_op jit(solution)/shard_map/ppermute | solution.py:41
  140.2 7.1 %collective-permute-start.29 = (bf16[128,1024]{0,1:T(8,128)(2,1)S(1)}, bf16[128,1024]{0,1:T(8,128)(2,1)S(1)}, u32[]{:S(2)}, u32[]{:S(2)}) collective-permute-start(bf16[128,1024]{0,1:T(8,128)(2,1)S(1)} %fusion.24), channel_id=1, source_target_pairs={{8,4},{10,6},{12,8},{14,10},{9,5},{11,7},{13,9},{15,11},{24,20},{2... | collective-permute-start | bytes 786440 | tf_op jit(solution)/shard_map/ppermute | solution.py:114
  140.8 8.7 %collective-permute-start.34 = (bf16[128,1024]{0,1:T(8,128)(2,1)S(1)}, bf16[128,1024]{0,1:T(8,128)(2,1)S(1)}, u32[]{:S(2)}, u32[]{:S(2)}) collective-permute-start(bf16[128,1024]{0,1:T(8,128)(2,1)S(1)} %copy-done.5), channel_id=1, source_target_pairs={{0,2},{4,6},{8,10},{12,14},{1,3},{5,7},{9,11},{13,15},{16,18},{20,... | collective-permute-start | bytes 786440 | tf_op jit(solution)/shard_map/ppermute | solution.py:43
  144.3 14.6 %collective-permute-start.24 = (bf16[128,1024]{0,1:T(8,128)(2,1)S(1)}, bf16[128,1024]{0,1:T(8,128)(2,1)S(1)}, u32[]{:S(2)}, u32[]{:S(2)}) collective-permute-start(bf16[128,1024]{0,1:T(8,128)(2,1)S(1)} %bitcast.147), channel_id=1, source_target_pairs={{2,0},{6,4},{10,8},{14,12},{3,1},{7,5},{11,9},{15,13},{18,16},{22,... | collective-permute-start | bytes 786440 | tf_op jit(solution)/shard_map/ppermute | solution.py:103
  145.8 2.3 collective-permute-start.33
  146.6 3.7 %collective-permute-start.35 = (bf16[128,1024]{0,1:T(8,128)(2,1)S(1)}, bf16[128,1024]{0,1:T(8,128)(2,1)S(1)}, u32[]{:S(2)}, u32[]{:S(2)}) collective-permute-start(bf16[128,1024]{0,1:T(8,128)(2,1)S(1)} %collective-permute-done.31), channel_id=1, source_target_pairs={{6,4},{4,6},{10,8},{8,10},{14,12},{12,14},{7,5},{5,7},{11,9},{9,11... | collective-permute-start | bytes 786440 | tf_op jit(solution)/shard_map/ppermute | solution.py:46
  147.3 3.1 %collective-permute-start.36 = (bf16[128,1024]{0,1:T(8,128)(2,1)S(1)}, bf16[128,1024]{0,1:T(8,128)(2,1)S(1)}, u32[]{:S(2)}, u32[]{:S(2)}) collective-permute-start(bf16[128,1024]{0,1:T(8,128)(2,1)S(1)} %collective-permute-done.32), channel_id=1, source_target_pairs={{10,8},{8,10},{14,12},{12,14},{11,9},{9,11},{15,13},{13,15},{26,24... | collective-permute-start | bytes 786440 | tf_op jit(solution)/shard_map/ppermute | solution.py:46
  148.1 30.8 %collective-permute-start.30 = (bf16[128,1024]{0,1:T(8,128)(2,1)S(1)}, bf16[128,1024]{0,1:T(8,128)(2,1)S(1)}, u32[]{:S(2)}, u32[]{:S(2)}) collective-permute-start(bf16[128,1024]{0,1:T(8,128)(2,1)S(1)} %fusion.26), channel_id=1, source_target_pairs={{4,0},{6,2},{8,4},{10,6},{12,8},{14,10},{5,1},{7,3},{9,5},{11,7},{... | collective-permute-start | bytes 786440 | tf_op jit(solution)/shard_map/ppermute | solution.py:114
  182.5 6.3 %collective-permute-start.41 = (bf16[128,1024]{1,0:T(8,128)(2,1)}, bf16[128,1024]{1,0:T(8,128)(2,1)}, u32[]{:S(2)}, u32[]{:S(2)}) collective-permute-start(bf16[128,1024]{1,0:T(8,128)(2,1)} %copy.73), channel_id=1, source_target_pairs={{12,14},{14,12},{13,15},{15,13},{28,30},{30,28},{29,31},{31,29}} | collective-permute-start | bytes 786440 | tf_op jit(solution)/shard_map/ppermute | solution.py:106
  184.8 20.1 %collective-permute-start.40 = (bf16[128,1024]{1,0:T(8,128)(2,1)}, bf16[128,1024]{1,0:T(8,128)(2,1)}, u32[]{:S(2)}, u32[]{:S(2)}) collective-permute-start(bf16[128,1024]{1,0:T(8,128)(2,1)} %copy.71), channel_id=1, source_target_pairs={{8,10},{10,8},{12,14},{14,12},{9,11},{11,9},{13,15},{15,13},{24,26... | collective-permute-start | bytes 786440 | tf_op jit(solution)/shard_map/ppermute | solution.py:106
  187.9 13.2 %collective-permute-start.45 = (f32[464,128]{1,0:T(8,128)}, f32[464,128]{1,0:T(8,128)}, u32[]{:S(2)}, u32[]{:S(2)}) collective-permute-start(f32[464,128]{1,0:T(8,128)} %maximum_bitcast_fusion), channel_id=1, source_target_pairs={{0,1},{1,0},{2,3},{3,2},{4,5},{5,4},{6,7},{7,6},{8,9},{9,8},{10,11... | collective-permute-start | bytes 712712 | tf_op jit(solution)/shard_map/ppermute | solution.py:19
  190.8 14.1 %collective-permute-start.42 = (bf16[128,1024]{1,0:T(8,128)(2,1)}, bf16[128,1024]{1,0:T(8,128)(2,1)}, u32[]{:S(2)}, u32[]{:S(2)}) collective-permute-start(bf16[128,1024]{1,0:T(8,128)(2,1)} %add_convert_fusion.3), channel_id=1, source_target_pairs={{12,8},{14,10},{13,9},{15,11},{28,24},{30,26},{29,25},{31,27}} | collective-permute-start | bytes 786440 | tf_op jit(solution)/shard_map/ppermute | solution.py:114
  197.6 56.1 %collective-permute-start.39 = (bf16[128,1024]{1,0:T(8,128)(2,1)}, bf16[128,1024]{1,0:T(8,128)(2,1)}, u32[]{:S(2)}, u32[]{:S(2)}) collective-permute-start(bf16[128,1024]{1,0:T(8,128)(2,1)} %copy.69), channel_id=1, source_target_pairs={{4,6},{6,4},{8,10},{10,8},{12,14},{14,12},{5,7},{7,5},{9,11},{11,9... | collective-permute-start | bytes 786440 | tf_op jit(solution)/shard_map/ppermute | solution.py:106
  199.8 67.3 %collective-permute-start.38 = (bf16[128,1024]{1,0:T(8,128)(2,1)}, bf16[128,1024]{1,0:T(8,128)(2,1)S(1)}, u32[]{:S(2)}, u32[]{:S(2)}) collective-permute-start(bf16[128,1024]{1,0:T(8,128)(2,1)} %copy.68), channel_id=1, source_target_pairs={{2,0},{6,4},{10,8},{14,12},{3,1},{7,5},{11,9},{15,13},{18,16},{22,... | collective-permute-start | bytes 786440 | tf_op jit(solution)/shard_map/ppermute | solution.py:103
  202.1 13.6 %collective-permute-start.46 = (f32[464,128]{1,0:T(8,128)S(1)}, f32[464,128]{1,0:T(8,128)S(1)}, u32[]{:S(2)}, u32[]{:S(2)}) collective-permute-start(f32[464,128]{1,0:T(8,128)S(1)} %fusion.34), channel_id=1, source_target_pairs={{0,2},{2,0},{4,6},{6,4},{8,10},{10,8},{12,14},{14,12},{1,3},{3,1},... | collective-permute-start | bytes 712712 | tf_op jit(solution)/shard_map/ppermute | solution.py:19
  206.0 47.7 %collective-permute-start.43 = (bf16[128,1024]{1,0:T(8,128)(2,1)S(1)}, bf16[128,1024]{1,0:T(8,128)(2,1)S(1)}, u32[]{:S(2)}, u32[]{:S(2)}) collective-permute-start(bf16[128,1024]{1,0:T(8,128)(2,1)S(1)} %add_convert_fusion.2), channel_id=1, source_target_pairs={{8,4},{10,6},{12,8},{14,10},{9,5},{11,7},{13,9},{15,11},{24,20},{2... | collective-permute-start | bytes 786440 | tf_op jit(solution)/shard_map/ppermute | solution.py:114
  216.7 18.0 %collective-permute-start.47 = (f32[464,128]{1,0:T(8,128)S(1)}, f32[464,128]{1,0:T(8,128)S(1)}, u32[]{:S(2)}, u32[]{:S(2)}) collective-permute-start(f32[464,128]{1,0:T(8,128)S(1)} %fusion.63), channel_id=1, source_target_pairs={{0,4},{2,6},{4,0},{6,2},{8,12},{10,14},{12,8},{14,10},{1,5},{3,7},... | collective-permute-start | bytes 712712 | tf_op jit(solution)/shard_map/ppermute | solution.py:19
  234.7 30.2 %collective-permute-start.48 = (f32[464,128]{1,0:T(8,128)S(1)}, f32[464,128]{1,0:T(8,128)S(1)}, u32[]{:S(2)}, u32[]{:S(2)}) collective-permute-start(f32[464,128]{1,0:T(8,128)S(1)} %add.269), channel_id=1, source_target_pairs={{0,8},{2,10},{4,12},{6,14},{8,0},{10,2},{12,4},{14,6},{1,9},{3,11}... | collective-permute-start | bytes 712712 | tf_op jit(solution)/shard_map/ppermute | solution.py:19
  255.4 13.3 %collective-permute-start.44 = (bf16[128,1024]{1,0:T(8,128)(2,1)}, bf16[128,1024]{1,0:T(8,128)(2,1)}, u32[]{:S(2)}, u32[]{:S(2)}) collective-permute-start(bf16[128,1024]{1,0:T(8,128)(2,1)} %add_convert_fusion.1), channel_id=1, source_target_pairs={{4,0},{6,2},{8,4},{10,6},{12,8},{14,10},{5,1},{7,3},{9,5},{11,7},{... | collective-permute-start | bytes 786440 | tf_op jit(solution)/shard_map/ppermute | solution.py:114
  (22 other events, 237.9 us)
Sparse Core Ops, SparseCore 0:
  68.0 14.3 all-gather.1

commit v8 on v7

--- a/solution.py
+++ b/solution.py
@@ -36,10 +36,10 @@
 def tree_spread(block, levels):
     count = 2 * levels
     climbed = []
-    held = block
-    for step in range(1, levels):
-        held = lax.ppermute(held, "ctx", [(c - 2, c) for c in range(2 * step, count)])
-        climbed.append(held)
+    for step in range(1, levels):
+        climbed.append(
+            lax.ppermute(block, "ctx", [(c - 2 * step, c) for c in range(2 * step, count)])
+        )
     crossed = [lax.ppermute(block, "ctx", [(c - 1, c) for c in range(1, count, 2)])]
     for step in range(1, levels):
         crossed.append(
@@ -54,11 +54,10 @@
     got = [block]
     owners = [ctx_index]
     valid = [ctx_index >= 0]
-    up, down = block, block
     ups, downs = [], []
     for step in range(1, levels):
-        up = lax.ppermute(up, "ctx", [(c - 2, c) for c in range(2 * step, count)])
-        down = lax.ppermute(down, "ctx", [(c + 2, c) for c in range(0, count - 2 * step)])
+        up = lax.ppermute(block, "ctx", [(c - 2 * step, c) for c in range(2 * step, count)])
+        down = lax.ppermute(block, "ctx", [(c + 2 * step, c) for c in range(0, count - 2 * step)])
         ups.append(up)
         downs.append(down)
         got += [up, down]
@@ -106,16 +105,12 @@
             lax.ppermute(crossed[step], "ctx", [(c, c ^ 1) for c in range(2 * step, count)])
         )
     total = back[0].astype(jnp.float32)
-    carry = None
-    for step in range(levels - 1, 0, -1):
+    for step in range(1, levels):
         acc = climbed[step - 1].astype(jnp.float32) + back[step].astype(jnp.float32)
-        if carry is not None:
-            acc = acc + carry.astype(jnp.float32)
-        carry = lax.ppermute(
-            acc.astype(jnp.bfloat16), "ctx", [(c, c - 2) for c in range(2 * step, count)]
-        )
-    if carry is not None:
-        total = total + carry.astype(jnp.float32)
+        home = lax.ppermute(
+            acc.astype(jnp.bfloat16), "ctx", [(c, c - 2 * step) for c in range(2 * step, count)]
+        )
+        total = total + home.astype(jnp.float32)
     return total
 
 

time: 279 us -> 290 us (1.039)
  local copies, waits for them, and re-layouts: 40.5 us -> 47.8 us
  matrix products: 28.7 us -> 32.3 us
  starting transfers between devices: 110 us -> 113 us
    ppermute x18, starting transfers between devices: 39.8 us -> 64 us  [the longest x6 35.4 us: tree_spread(): lax.ppermute(block, 'ctx', [(c - 2 * step, c) for c in range(2 * step, co...]
    ppermute x8, starting transfers between devices: 38.4 us -> 15.3 us  [from_partner(): lax.ppermute(shard, axis, [(i, i ^ 1 << stride) for i in range(lax.axis_s...]
    ppermute x18, waiting for transfers between devices: 42.2 us -> 29.5 us  [the longest x6 15.1 us: tree_return(): lax.ppermute(acc.astype(jnp.bfloat16), 'ctx', [(c, c - 2 * step) for c in...]
    ppermute x8, waiting for transfers between devices: 21.9 us -> 30.8 us  [from_partner(): lax.ppermute(shard, axis, [(i, i ^ 1 << stride) for i in range(lax.axis_s...]
    ppermute x3, waiting for transfers between devices: 4.63 us -> 8.18 us  [tree_gather(): lax.ppermute(downs[step - 1], 'ctx', [(c ^ 1, c) for c in range(0, count...]
    unnamed x58 -> x54, local copies, waits for them, and re-layouts: 6.93 us -> 9.69 us
  transfers between devices with their start and end apart: 50 -> 50, of which waited for: 16 -> 12; matrix products, arithmetic and copies ran while one was open for 18% -> 16% of each run, Pallas kernels for 0% -> 0%
where the time goes in v8:
time: 290 us; the launch traced here: 288 us
  starting transfers between devices  113 us (39%)
  waiting for transfers between devices  68.6 us (24%)
  local copies, waits for them, and re-layouts  47.8 us (16%)
  matrix products  32.3 us (11%)
  between operations  15.1 us (5%)
  other arithmetic  11.6 us (4%)
    ppermute x6, starting transfers between devices, tree_spread(): lax.ppermute(block, 'ctx', [(c - 2 * step, c) for c in range(2 * step, co...  35.4 us
    ppermute x8, waiting for transfers between devices, from_partner(): lax.ppermute(shard, axis, [(i, i ^ 1 << stride) for i in range(lax.axis_s...  30.8 us
    ppermute x3, starting transfers between devices, tree_gather(): lax.ppermute(block, 'ctx', [(c - 2 * step, c) for c in range(2 * step, co...  17 us
    ppermute x8, starting transfers between devices, from_partner(): lax.ppermute(shard, axis, [(i, i ^ 1 << stride) for i in range(lax.axis_s...  15.3 us
    ppermute x6, waiting for transfers between devices, tree_return(): lax.ppermute(acc.astype(jnp.bfloat16), 'ctx', [(c, c - 2 * step) for c in...  15.1 us
    ppermute x3, waiting for transfers between devices, tree_gather(): lax.ppermute(block, 'ctx', [(c + 2 * step, c) for c in range(0, count - 2...  14 us
    dynamic_update_slice x14, local copies, waits for them, and re-layouts, tree_gather(): whole = lax.dynamic_update_slice_in_dim(whole, piece, place, 0)  10.6 us
    unnamed x54, local copies, waits for them, and re-layouts  9.69 us
  transfers between devices with their start and end apart: 50, of which 12 were waited for; matrix products, arithmetic and copies ran while one was open for 16% of the time, Pallas kernels for 0%

profile of v8, /device:TPU:0, one launch (start us, length us, event | category | flops | bytes accessed | tf_op | source)
XLA Modules:
  0.0 288.4 jit_solution(11512322111168417420)
XLA Ops:
  7.2 1.8 broadcast_in_dim.54
  9.9 4.9 %collective-permute-start.10 = (bf16[336,512]{1,0:T(8,128)(2,1)S(1)}, bf16[336,512]{1,0:T(8,128)(2,1)S(1)}, u32[]{:S(2)}, u32[]{:S(2)}) collective-permute-start(bf16[336,512]{1,0:T(8,128)(2,1)S(1)} %get-tuple-element.29), channel_id=1, source_target_pairs={{0,4},{2,6},{4,8},{6,10},{8,12},{10,14},{1,5},{3,7},{5,9},{7,11},{... | collective-permute-start | bytes 1032200 | tf_op jit(solution)/shard_map/ppermute | solution.py:59
  16.1 5.6 %collective-permute-start.12 = (bf16[336,512]{1,0:T(8,128)(2,1)S(1)}, bf16[336,512]{1,0:T(8,128)(2,1)S(1)}, u32[]{:S(2)}, u32[]{:S(2)}) collective-permute-start(bf16[336,512]{1,0:T(8,128)(2,1)S(1)} %get-tuple-element.29), channel_id=1, source_target_pairs={{0,8},{2,10},{4,12},{6,14},{1,9},{3,11},{5,13},{7,15},{16,24},{18,... | collective-permute-start | bytes 1032200 | tf_op jit(solution)/shard_map/ppermute | solution.py:59
  23.0 6.5 %collective-permute-start.14 = (bf16[336,512]{1,0:T(8,128)(2,1)S(1)}, bf16[336,512]{1,0:T(8,128)(2,1)S(1)}, u32[]{:S(2)}, u32[]{:S(2)}) collective-permute-start(bf16[336,512]{1,0:T(8,128)(2,1)S(1)} %get-tuple-element.29), channel_id=1, source_target_pairs={{0,12},{2,14},{1,13},{3,15},{16,28},{18,30},{17,29},{19,31}} | collective-permute-start | bytes 1032200 | tf_op jit(solution)/shard_map/ppermute | solution.py:59
  31.7 1.5 collective-permute-start.16
  35.3 14.0 %collective-permute-done.13 = bf16[336,512]{1,0:T(8,128)(2,1)S(1)} collective-permute-done((bf16[336,512]{1,0:T(8,128)(2,1)S(1)}, bf16[336,512]{1,0:T(8,128)(2,1)S(1)}, u32[]{:S(2)}, u32[]{:S(2)}) %collective-permute-start.13) | collective-permute-done | bytes 344096 | tf_op jit(solution)/shard_map/ppermute | solution.py:60
  49.3 3.4 %collective-permute-start.18 = (bf16[336,512]{1,0:T(8,128)(2,1)S(1)}, bf16[336,512]{1,0:T(8,128)(2,1)S(1)}, u32[]{:S(2)}, u32[]{:S(2)}) collective-permute-start(bf16[336,512]{1,0:T(8,128)(2,1)S(1)} %collective-permute-done.11), channel_id=1, source_target_pairs={{2,0},{0,2},{6,4},{4,6},{10,8},{8,10},{3,1},{1,3},{7,5},{5,7},{11,... | collective-permute-start | bytes 1032200 | tf_op jit(solution)/shard_map/ppermute | solution.py:72
  54.9 2.4 collective-permute-start.20
  59.6 3.4 %collective-permute-start.22 = (bf16[336,512]{1,0:T(8,128)(2,1)S(1)}, bf16[336,512]{1,0:T(8,128)(2,1)S(1)}, u32[]{:S(2)}, u32[]{:S(2)}) collective-permute-start(bf16[336,512]{1,0:T(8,128)(2,1)S(1)} %collective-permute-done.15), channel_id=1, source_target_pairs={{2,0},{0,2},{3,1},{1,3},{18,16},{16,18},{19,17},{17,19}} | collective-permute-start | bytes 1032200 | tf_op jit(solution)/shard_map/ppermute | solution.py:72
  65.3 4.3 %collective-permute-done.20 = bf16[336,512]{1,0:T(8,128)(2,1)S(1)} collective-permute-done((bf16[336,512]{1,0:T(8,128)(2,1)S(1)}, bf16[336,512]{1,0:T(8,128)(2,1)S(1)}, u32[]{:S(2)}, u32[]{:S(2)}) %collective-permute-start.20) | collective-permute-done | bytes 344096 | tf_op jit(solution)/shard_map/ppermute | solution.py:72
  71.1 3.9 %collective-permute-done.22 = bf16[336,512]{1,0:T(8,128)(2,1)S(1)} collective-permute-done((bf16[336,512]{1,0:T(8,128)(2,1)S(1)}, bf16[336,512]{1,0:T(8,128)(2,1)S(1)}, u32[]{:S(2)}, u32[]{:S(2)}) %collective-permute-start.22) | collective-permute-done | bytes 344096 | tf_op jit(solution)/shard_map/ppermute | solution.py:72
  75.7 3.6 %slice.122 = bf16[2688,512]{1,0:T(8,128)(2,1)} slice(bf16[3024,512]{1,0:T(8,128)(2,1)} %constant_dynamic-update-slice_fusion.24), slice={[0:2688], [0:512]} | slice | bytes 5505024 | tf_op jit(solution)/shard_map/slice | solution.py:81
  79.3 2.1 collective-permute-start.3
  81.5 3.2 %collective-permute-start.4 = (bf16[128,1024]{1,0:T(8,128)(2,1)}, bf16[128,1024]{1,0:T(8,128)(2,1)}, u32[]{:S(2)}, u32[]{:S(2)}) collective-permute-start(bf16[128,1024]{1,0:T(8,128)(2,1)} %bitcast.4), channel_id=1, source_target_pairs={{0,8},{2,10},{4,12},{6,14},{1,9},{3,11},{5,13},{7,15},{16,24},{18,... | collective-permute-start | bytes 786440 | tf_op jit(solution)/shard_map/ppermute | solution.py:41
  84.7 2.0 collective-permute-start.5
  86.7 4.1 %collective-permute-start.6 = (bf16[128,1024]{1,0:T(8,128)(2,1)}, bf16[128,1024]{1,0:T(8,128)(2,1)}, u32[]{:S(2)}, u32[]{:S(2)}) collective-permute-start(bf16[128,1024]{1,0:T(8,128)(2,1)} %bitcast.4), channel_id=1, source_target_pairs={{0,2},{4,6},{8,10},{12,14},{1,3},{5,7},{9,11},{13,15},{16,18},{20,... | collective-permute-start | bytes 786440 | tf_op jit(solution)/shard_map/ppermute | solution.py:43
  92.9 1.6 collective-permute-done
  95.6 2.5 collective-permute-done.1
  98.2 4.4 %collective-permute-done.2 = f32[16]{0:T(128)S(1)} collective-permute-done((f32[16]{0:T(128)S(1)}, f32[16]{0:T(128)S(1)}, u32[]{:S(2)}, u32[]{:S(2)}) %collective-permute-start.2) | collective-permute-done | bytes 96 | tf_op jit(solution)/shard_map/ppermute | solution.py:19
  111.9 4.9 %fusion.15 = bf16[128,1024]{0,1:T(8,128)(2,1)} fusion(f32[128,1024]{0,1:T(8,128)S(1)} %convolution_multiply_fusion.2, bf16[2688,1024]{1,0:T(8,128)(2,1)} %all-gather.2.cloned.1.call-done, bf16[1,128,2688]{2,1,0:T(8,128)(2,1)S(1)} %copy-done), kind=kOutput, calls=%fused_computation.28 | convolution fusion | flops 704905216 | bytes 6979584 | tf_op jit(solution)/shard_map/dot_general | solution.py:155
  116.8 2.0 copy.95
  118.8 3.3 %copy.84 = bf16[1024,8,128,1]{0,2,3,1:T(8,128)(2,1)S(1)} copy(bf16[1024,8,128,1]{2,1,0,3:T(8,128)(2,1)} %bitcast.134) | data formatting | bytes 4194304 | tf_op jit(solution)/shard_map/reshape | solution.py:210
  122.1 6.9 %fusion.36 = (f32[8,2,128]{2,1,0:T(2,128)S(1)}, f32[8,2,128,1024]{2,3,1,0:T(8,128)}) fusion(pred[128,1024]{0,1:T(8,128)(4,1)} %compare_and_fusion, bf16[1024,8,128,1]{0,2,3,1:T(8,128)(2,1)S(1)} %copy.84, bf16[128,8,2,128]{0,3,2,1:T(8,128)(2,1)S(1)} %bitcast.138), kind=kOutput, calls=%fused_computation.122 | convolution fusion | flops 547357696 | bytes 11149312 | tf_op jit(solution)/shard_map/sub | solution.py:217
  129.0 5.0 %fusion.37 = (bf16[1024,8,128]{0,2,1:T(8,128)(2,1)S(1)}, f32[1024,8,128]{0,2,1:T(8,128)S(1)}) fusion(bf16[128,8,2,128]{3,2,1,0:T(2,128)(2,1)} %reshape_squeeze.7, f32[128]{0:T(128)S(1)} %get-tuple-element.25, f32[8,2,128,1024]{2,3,1,0:T(8,128)} %get-tuple-element.49, f32[8,2,128]{2,1,0:T(2,128)S(1)} %get-tuple-element.48), kind=kOutput, calls=%fused_computation.123 | convolution fusion | flops 544210944 | bytes 15213056 | tf_op jit(solution)/shard_map/jgtl,tjgd->ljd/dot_general | solution.py:231
  136.1 8.2 %collective-permute-start.31 = (bf16[128,1024]{0,1:T(8,128)(2,1)S(1)}, bf16[128,1024]{0,1:T(8,128)(2,1)S(1)}, u32[]{:S(2)}, u32[]{:S(2)}) collective-permute-start(bf16[128,1024]{0,1:T(8,128)(2,1)S(1)} %copy-done.6), channel_id=1, source_target_pairs={{0,4},{2,6},{4,8},{6,10},{8,12},{10,14},{1,5},{3,7},{5,9},{7,11},{... | collective-permute-start | bytes 786440 | tf_op jit(solution)/shard_map/ppermute | solution.py:41
  144.3 18.3 %collective-permute-start.32 = (bf16[128,1024]{0,1:T(8,128)(2,1)S(1)}, bf16[128,1024]{0,1:T(8,128)(2,1)S(1)}, u32[]{:S(2)}, u32[]{:S(2)}) collective-permute-start(bf16[128,1024]{0,1:T(8,128)(2,1)S(1)} %copy-done.6), channel_id=1, source_target_pairs={{0,8},{2,10},{4,12},{6,14},{1,9},{3,11},{5,13},{7,15},{16,24},{18,... | collective-permute-start | bytes 786440 | tf_op jit(solution)/shard_map/ppermute | solution.py:41
  162.7 1.5 collective-permute-start.33
  165.1 3.5 %collective-permute-start.34 = (bf16[128,1024]{0,1:T(8,128)(2,1)S(1)}, bf16[128,1024]{0,1:T(8,128)(2,1)S(1)}, u32[]{:S(2)}, u32[]{:S(2)}) collective-permute-start(bf16[128,1024]{0,1:T(8,128)(2,1)S(1)} %copy-done.6), channel_id=1, source_target_pairs={{0,2},{4,6},{8,10},{12,14},{1,3},{5,7},{9,11},{13,15},{16,18},{20,... | collective-permute-start | bytes 786440 | tf_op jit(solution)/shard_map/ppermute | solution.py:43
  177.3 1.9 fusion.1
  179.2 1.7 fusion.3
  180.9 1.7 convolution_convert_fusion
  182.6 3.4 %fusion.38 = (bf16[1024,8,128]{0,2,1:T(8,128)(2,1)S(1)}, f32[1024,8,128]{0,2,1:T(8,128)}) fusion(bf16[8,2,128,1024]{2,3,1,0:T(8,128)(2,1)S(1)} %fusion.3, bf16[128,8,2,128]{0,3,2,1:T(8,128)(2,1)S(1)} %bitcast.139), kind=kOutput, calls=%fused_computation.124 | convolution fusion | flops 537919488 | bytes 11010048 | tf_op jit(solution)/shard_map/jgtl,tjgd->ljd/dot_general | solution.py:227
  186.0 15.1 %collective-permute-done.28 = bf16[128,1024]{0,1:T(8,128)(2,1)S(1)} collective-permute-done((bf16[128,1024]{0,1:T(8,128)(2,1)S(1)}, bf16[128,1024]{0,1:T(8,128)(2,1)S(1)}, u32[]{:S(2)}, u32[]{:S(2)}) %collective-permute-start.28) | collective-permute-done | bytes 262176 | tf_op jit(solution)/shard_map/ppermute | solution.py:110
  202.2 1.5 convolution_multiply_fusion
  203.9 2.1 copy.77
  206.0 1.9 slice.131
  207.9 2.0 copy.75
  212.3 1.8 copy.73
  222.7 1.4 collective-permute-start.39
  224.1 1.8 copy.68
  225.9 1.4 collective-permute-start.38
  228.3 2.7 collective-permute-start.46
  238.2 3.8 %collective-permute-done.46 = f32[464,128]{1,0:T(8,128)S(1)} collective-permute-done((f32[464,128]{1,0:T(8,128)S(1)}, f32[464,128]{1,0:T(8,128)S(1)}, u32[]{:S(2)}, u32[]{:S(2)}) %collective-permute-start.46) | collective-permute-done | bytes 237600 | tf_op jit(solution)/shard_map/ppermute | solution.py:19
  242.9 5.5 %collective-permute-start.47 = (f32[464,128]{1,0:T(8,128)S(1)}, f32[464,128]{1,0:T(8,128)S(1)}, u32[]{:S(2)}, u32[]{:S(2)}) collective-permute-start(f32[464,128]{1,0:T(8,128)S(1)} %fusion.61), channel_id=1, source_target_pairs={{0,4},{2,6},{4,0},{6,2},{8,12},{10,14},{12,8},{14,10},{1,5},{3,7},... | collective-permute-start | bytes 712712 | tf_op jit(solution)/shard_map/ppermute | solution.py:19
  248.4 5.3 %fusion.11 = bf16[1,128,2688]{2,1,0:T(8,128)(2,1)} fusion(f32[128,2688]{1,0:T(8,128)S(1)} %copy-done.2, bf16[128,1024]{0,1:T(8,128)(2,1)S(1)} %fusion.25, bf16[2688,1024]{1,0:T(8,128)(2,1)} %all-gather.2.cloned.1.call-done), kind=kOutput, calls=%fused_computation.19 | convolution fusion | flops 705331200 | bytes 7831552 | tf_op jit(solution)/shard_map/tk,dk->td/dot_general | solution.py:256
  253.8 9.3 %collective-permute-done.47 = f32[464,128]{1,0:T(8,128)S(1)} collective-permute-done((f32[464,128]{1,0:T(8,128)S(1)}, f32[464,128]{1,0:T(8,128)S(1)}, u32[]{:S(2)}, u32[]{:S(2)}) %collective-permute-start.47) | collective-permute-done | bytes 237600 | tf_op jit(solution)/shard_map/ppermute | solution.py:19
  263.1 7.0 %collective-permute-start.48 = (f32[464,128]{1,0:T(8,128)S(1)}, f32[464,128]{1,0:T(8,128)S(1)}, u32[]{:S(2)}, u32[]{:S(2)}) collective-permute-start(f32[464,128]{1,0:T(8,128)S(1)} %add.269), channel_id=1, source_target_pairs={{0,8},{2,10},{4,12},{6,14},{8,0},{10,2},{12,4},{14,6},{1,9},{3,11}... | collective-permute-start | bytes 712712 | tf_op jit(solution)/shard_map/ppermute | solution.py:19
  271.0 8.3 %collective-permute-done.48 = f32[464,128]{1,0:T(8,128)S(1)} collective-permute-done((f32[464,128]{1,0:T(8,128)S(1)}, f32[464,128]{1,0:T(8,128)S(1)}, u32[]{:S(2)}, u32[]{:S(2)}) %collective-permute-start.48) | collective-permute-done | bytes 237600 | tf_op jit(solution)/shard_map/ppermute | solution.py:19
  (198 shorter events, 64.9 us)
Async XLA Ops:
  7.2 104.7 %all-gather.2.cloned.1.call-start = ((), (), s32[]{:S(2)}) async-start(), calls=%async_computation | async-start | bytes 8257536 | tf_op jit(solution)/shard_map/all_gather | solution.py:150
  9.9 19.8 %collective-permute-start.10 = (bf16[336,512]{1,0:T(8,128)(2,1)S(1)}, bf16[336,512]{1,0:T(8,128)(2,1)S(1)}, u32[]{:S(2)}, u32[]{:S(2)}) collective-permute-start(bf16[336,512]{1,0:T(8,128)(2,1)S(1)} %get-tuple-element.29), channel_id=1, source_target_pairs={{0,4},{2,6},{4,8},{6,10},{8,12},{10,14},{1,5},{3,7},{5,9},{7,11},{... | collective-permute-start | bytes 1032200 | tf_op jit(solution)/shard_map/ppermute | solution.py:59
  14.8 16.9 %collective-permute-start.11 = (bf16[336,512]{1,0:T(8,128)(2,1)S(1)}, bf16[336,512]{1,0:T(8,128)(2,1)S(1)}, u32[]{:S(2)}, u32[]{:S(2)}) collective-permute-start(bf16[336,512]{1,0:T(8,128)(2,1)S(1)} %get-tuple-element.29), channel_id=1, source_target_pairs={{4,0},{6,2},{8,4},{10,6},{12,8},{14,10},{5,1},{7,3},{9,5},{11,7},{... | collective-permute-start | bytes 1032200 | tf_op jit(solution)/shard_map/ppermute | solution.py:60
  16.1 17.8 %collective-permute-start.12 = (bf16[336,512]{1,0:T(8,128)(2,1)S(1)}, bf16[336,512]{1,0:T(8,128)(2,1)S(1)}, u32[]{:S(2)}, u32[]{:S(2)}) collective-permute-start(bf16[336,512]{1,0:T(8,128)(2,1)S(1)} %get-tuple-element.29), channel_id=1, source_target_pairs={{0,8},{2,10},{4,12},{6,14},{1,9},{3,11},{5,13},{7,15},{16,24},{18,... | collective-permute-start | bytes 1032200 | tf_op jit(solution)/shard_map/ppermute | solution.py:59
  21.7 27.7 %collective-permute-start.13 = (bf16[336,512]{1,0:T(8,128)(2,1)S(1)}, bf16[336,512]{1,0:T(8,128)(2,1)S(1)}, u32[]{:S(2)}, u32[]{:S(2)}) collective-permute-start(bf16[336,512]{1,0:T(8,128)(2,1)S(1)} %get-tuple-element.29), channel_id=1, source_target_pairs={{8,0},{10,2},{12,4},{14,6},{9,1},{11,3},{13,5},{15,7},{24,16},{26,... | collective-permute-start | bytes 1032200 | tf_op jit(solution)/shard_map/ppermute | solution.py:60
  23.0 30.5 %collective-permute-start.14 = (bf16[336,512]{1,0:T(8,128)(2,1)S(1)}, bf16[336,512]{1,0:T(8,128)(2,1)S(1)}, u32[]{:S(2)}, u32[]{:S(2)}) collective-permute-start(bf16[336,512]{1,0:T(8,128)(2,1)S(1)} %get-tuple-element.29), channel_id=1, source_target_pairs={{0,12},{2,14},{1,13},{3,15},{16,28},{18,30},{17,29},{19,31}} | collective-permute-start | bytes 1032200 | tf_op jit(solution)/shard_map/ppermute | solution.py:59
  29.6 25.3 %collective-permute-start.15 = (bf16[336,512]{1,0:T(8,128)(2,1)S(1)}, bf16[336,512]{1,0:T(8,128)(2,1)S(1)}, u32[]{:S(2)}, u32[]{:S(2)}) collective-permute-start(bf16[336,512]{1,0:T(8,128)(2,1)S(1)} %get-tuple-element.29), channel_id=1, source_target_pairs={{12,0},{14,2},{13,1},{15,3},{28,16},{30,18},{29,17},{31,19}} | collective-permute-start | bytes 1032200 | tf_op jit(solution)/shard_map/ppermute | solution.py:60
  31.7 26.5 %collective-permute-start.16 = (bf16[336,512]{1,0:T(8,128)(2,1)S(1)}, bf16[336,512]{1,0:T(8,128)(2,1)S(1)}, u32[]{:S(2)}, u32[]{:S(2)}) collective-permute-start(bf16[336,512]{1,0:T(8,128)(2,1)S(1)} %get-tuple-element.29), channel_id=1, source_target_pairs={{2,0},{0,2},{6,4},{4,6},{10,8},{8,10},{14,12},{12,14},{3,1},{1,3},... | collective-permute-start | bytes 1032200 | tf_op jit(solution)/shard_map/ppermute | solution.py:66
  33.9 25.7 %collective-permute-start.17 = (bf16[336,512]{1,0:T(8,128)(2,1)S(1)}, bf16[336,512]{1,0:T(8,128)(2,1)S(1)}, u32[]{:S(2)}, u32[]{:S(2)}) collective-permute-start(bf16[336,512]{1,0:T(8,128)(2,1)S(1)} %collective-permute-done.10), channel_id=1, source_target_pairs={{6,4},{4,6},{10,8},{8,10},{14,12},{12,14},{7,5},{5,7},{11,9},{9,11... | collective-permute-start | bytes 1032200 | tf_op jit(solution)/shard_map/ppermute | solution.py:70
  49.3 14.4 %collective-permute-start.18 = (bf16[336,512]{1,0:T(8,128)(2,1)S(1)}, bf16[336,512]{1,0:T(8,128)(2,1)S(1)}, u32[]{:S(2)}, u32[]{:S(2)}) collective-permute-start(bf16[336,512]{1,0:T(8,128)(2,1)S(1)} %collective-permute-done.11), channel_id=1, source_target_pairs={{2,0},{0,2},{6,4},{4,6},{10,8},{8,10},{3,1},{1,3},{7,5},{5,7},{11,... | collective-permute-start | bytes 1032200 | tf_op jit(solution)/shard_map/ppermute | solution.py:72
  53.5 11.0 %collective-permute-start.19 = (bf16[336,512]{1,0:T(8,128)(2,1)S(1)}, bf16[336,512]{1,0:T(8,128)(2,1)S(1)}, u32[]{:S(2)}, u32[]{:S(2)}) collective-permute-start(bf16[336,512]{1,0:T(8,128)(2,1)S(1)} %collective-permute-done.12), channel_id=1, source_target_pairs={{10,8},{8,10},{14,12},{12,14},{11,9},{9,11},{15,13},{13,15},{26,24... | collective-permute-start | bytes 1032200 | tf_op jit(solution)/shard_map/ppermute | solution.py:70
  54.9 14.7 %collective-permute-start.20 = (bf16[336,512]{1,0:T(8,128)(2,1)S(1)}, bf16[336,512]{1,0:T(8,128)(2,1)S(1)}, u32[]{:S(2)}, u32[]{:S(2)}) collective-permute-start(bf16[336,512]{1,0:T(8,128)(2,1)S(1)} %collective-permute-done.13), channel_id=1, source_target_pairs={{2,0},{0,2},{6,4},{4,6},{3,1},{1,3},{7,5},{5,7},{18,16},{16,18},{2... | collective-permute-start | bytes 1032200 | tf_op jit(solution)/shard_map/ppermute | solution.py:72
  58.1 12.2 %collective-permute-start.21 = (bf16[336,512]{1,0:T(8,128)(2,1)S(1)}, bf16[336,512]{1,0:T(8,128)(2,1)S(1)}, u32[]{:S(2)}, u32[]{:S(2)}) collective-permute-start(bf16[336,512]{1,0:T(8,128)(2,1)S(1)} %collective-permute-done.14), channel_id=1, source_target_pairs={{14,12},{12,14},{15,13},{13,15},{30,28},{28,30},{31,29},{29,31}} | collective-permute-start | bytes 1032200 | tf_op jit(solution)/shard_map/ppermute | solution.py:70
  59.6 15.3 %collective-permute-start.22 = (bf16[336,512]{1,0:T(8,128)(2,1)S(1)}, bf16[336,512]{1,0:T(8,128)(2,1)S(1)}, u32[]{:S(2)}, u32[]{:S(2)}) collective-permute-start(bf16[336,512]{1,0:T(8,128)(2,1)S(1)} %collective-permute-done.15), channel_id=1, source_target_pairs={{2,0},{0,2},{3,1},{1,3},{18,16},{16,18},{19,17},{17,19}} | collective-permute-start | bytes 1032200 | tf_op jit(solution)/shard_map/ppermute | solution.py:72
  79.3 25.5 %collective-permute-start.3 = (bf16[128,1024]{1,0:T(8,128)(2,1)}, bf16[128,1024]{1,0:T(8,128)(2,1)}, u32[]{:S(2)}, u32[]{:S(2)}) collective-permute-start(bf16[128,1024]{1,0:T(8,128)(2,1)} %bitcast.4), channel_id=1, source_target_pairs={{0,4},{2,6},{4,8},{6,10},{8,12},{10,14},{1,5},{3,7},{5,9},{7,11},{... | collective-permute-start | bytes 786440 | tf_op jit(solution)/shard_map/ppermute | solution.py:41
  81.5 25.0 %collective-permute-start.4 = (bf16[128,1024]{1,0:T(8,128)(2,1)}, bf16[128,1024]{1,0:T(8,128)(2,1)}, u32[]{:S(2)}, u32[]{:S(2)}) collective-permute-start(bf16[128,1024]{1,0:T(8,128)(2,1)} %bitcast.4), channel_id=1, source_target_pairs={{0,8},{2,10},{4,12},{6,14},{1,9},{3,11},{5,13},{7,15},{16,24},{18,... | collective-permute-start | bytes 786440 | tf_op jit(solution)/shard_map/ppermute | solution.py:41
  84.7 23.5 %collective-permute-start.5 = (bf16[128,1024]{1,0:T(8,128)(2,1)}, bf16[128,1024]{1,0:T(8,128)(2,1)}, u32[]{:S(2)}, u32[]{:S(2)}) collective-permute-start(bf16[128,1024]{1,0:T(8,128)(2,1)} %bitcast.4), channel_id=1, source_target_pairs={{0,12},{2,14},{1,13},{3,15},{16,28},{18,30},{17,29},{19,31}} | collective-permute-start | bytes 786440 | tf_op jit(solution)/shard_map/ppermute | solution.py:41
  86.7 23.1 %collective-permute-start.6 = (bf16[128,1024]{1,0:T(8,128)(2,1)}, bf16[128,1024]{1,0:T(8,128)(2,1)}, u32[]{:S(2)}, u32[]{:S(2)}) collective-permute-start(bf16[128,1024]{1,0:T(8,128)(2,1)} %bitcast.4), channel_id=1, source_target_pairs={{0,2},{4,6},{8,10},{12,14},{1,3},{5,7},{9,11},{13,15},{16,18},{20,... | collective-permute-start | bytes 786440 | tf_op jit(solution)/shard_map/ppermute | solution.py:43
  91.0 3.5 %collective-permute-start = (f32[16]{0:T(128)S(1)}, f32[16]{0:T(128)S(1)}, u32[]{:S(2)}, u32[]{:S(2)}) collective-permute-start(f32[16]{0:T(128)S(1)} %pad_maximum_fusion), channel_id=1, source_target_pairs={{0,2},{2,0},{4,6},{6,4},{8,10},{10,8},{12,14},{14,12},{1,3},{3,1},... | collective-permute-start | bytes 200 | tf_op jit(solution)/shard_map/ppermute | solution.py:19
  94.6 3.5 %collective-permute-start.1 = (f32[16]{0:T(128)S(1)}, f32[16]{0:T(128)S(1)}, u32[]{:S(2)}, u32[]{:S(2)}) collective-permute-start(f32[16]{0:T(128)S(1)} %fusion.62), channel_id=1, source_target_pairs={{0,4},{2,6},{4,0},{6,2},{8,12},{10,14},{12,8},{14,10},{1,5},{3,7},... | collective-permute-start | bytes 200 | tf_op jit(solution)/shard_map/ppermute | solution.py:19
  98.1 4.4 %collective-permute-start.2 = (f32[16]{0:T(128)S(1)}, f32[16]{0:T(128)S(1)}, u32[]{:S(2)}, u32[]{:S(2)}) collective-permute-start(f32[16]{0:T(128)S(1)} %add.227), channel_id=1, source_target_pairs={{0,8},{2,10},{4,12},{6,14},{8,0},{10,2},{12,4},{14,6},{1,9},{3,11}... | collective-permute-start | bytes 200 | tf_op jit(solution)/shard_map/ppermute | solution.py:19
  105.8 5.0 %collective-permute-start.7 = (bf16[128,1024]{1,0:T(8,128)(2,1)}, bf16[128,1024]{1,0:T(8,128)(2,1)S(1)}, u32[]{:S(2)}, u32[]{:S(2)}) collective-permute-start(bf16[128,1024]{1,0:T(8,128)(2,1)} %collective-permute-done.3), channel_id=1, source_target_pairs={{6,4},{4,6},{10,8},{8,10},{14,12},{12,14},{7,5},{5,7},{11,9},{9,11... | collective-permute-start | bytes 786440 | tf_op jit(solution)/shard_map/ppermute | solution.py:46
  106.5 4.3 %collective-permute-start.8 = (bf16[128,1024]{1,0:T(8,128)(2,1)}, bf16[128,1024]{1,0:T(8,128)(2,1)S(1)}, u32[]{:S(2)}, u32[]{:S(2)}) collective-permute-start(bf16[128,1024]{1,0:T(8,128)(2,1)} %collective-permute-done.4), channel_id=1, source_target_pairs={{10,8},{8,10},{14,12},{12,14},{11,9},{9,11},{15,13},{13,15},{26,24... | collective-permute-start | bytes 786440 | tf_op jit(solution)/shard_map/ppermute | solution.py:46
  134.5 29.8 %collective-permute-start.29 = (bf16[128,1024]{0,1:T(8,128)(2,1)S(1)}, bf16[128,1024]{0,1:T(8,128)(2,1)S(1)}, u32[]{:S(2)}, u32[]{:S(2)}) collective-permute-start(bf16[128,1024]{0,1:T(8,128)(2,1)S(1)} %bitcast.150), channel_id=1, source_target_pairs={{12,14},{14,12},{13,15},{15,13},{28,30},{30,28},{29,31},{31,29}} | collective-permute-start | bytes 786440 | tf_op jit(solution)/shard_map/ppermute | solution.py:105
  135.3 29.8 %collective-permute-start.27 = (bf16[128,1024]{0,1:T(8,128)(2,1)S(1)}, bf16[128,1024]{0,1:T(8,128)(2,1)S(1)}, u32[]{:S(2)}, u32[]{:S(2)}) collective-permute-start(bf16[128,1024]{0,1:T(8,128)(2,1)S(1)} %bitcast.149), channel_id=1, source_target_pairs={{8,10},{10,8},{12,14},{14,12},{9,11},{11,9},{13,15},{15,13},{24,26... | collective-permute-start | bytes 786440 | tf_op jit(solution)/shard_map/ppermute | solution.py:105
  136.1 34.0 %collective-permute-start.31 = (bf16[128,1024]{0,1:T(8,128)(2,1)S(1)}, bf16[128,1024]{0,1:T(8,128)(2,1)S(1)}, u32[]{:S(2)}, u32[]{:S(2)}) collective-permute-start(bf16[128,1024]{0,1:T(8,128)(2,1)S(1)} %copy-done.6), channel_id=1, source_target_pairs={{0,4},{2,6},{4,8},{6,10},{8,12},{10,14},{1,5},{3,7},{5,9},{7,11},{... | collective-permute-start | bytes 786440 | tf_op jit(solution)/shard_map/ppermute | solution.py:41
  144.3 27.2 %collective-permute-start.32 = (bf16[128,1024]{0,1:T(8,128)(2,1)S(1)}, bf16[128,1024]{0,1:T(8,128)(2,1)S(1)}, u32[]{:S(2)}, u32[]{:S(2)}) collective-permute-start(bf16[128,1024]{0,1:T(8,128)(2,1)S(1)} %copy-done.6), channel_id=1, source_target_pairs={{0,8},{2,10},{4,12},{6,14},{1,9},{3,11},{5,13},{7,15},{16,24},{18,... | collective-permute-start | bytes 786440 | tf_op jit(solution)/shard_map/ppermute | solution.py:41
  162.7 10.0 %collective-permute-start.33 = (bf16[128,1024]{0,1:T(8,128)(2,1)S(1)}, bf16[128,1024]{0,1:T(8,128)(2,1)S(1)}, u32[]{:S(2)}, u32[]{:S(2)}) collective-permute-start(bf16[128,1024]{0,1:T(8,128)(2,1)S(1)} %copy-done.6), channel_id=1, source_target_pairs={{0,12},{2,14},{1,13},{3,15},{16,28},{18,30},{17,29},{19,31}} | collective-permute-start | bytes 786440 | tf_op jit(solution)/shard_map/ppermute | solution.py:41
  164.3 4.5 %collective-permute-start.25 = (bf16[128,1024]{0,1:T(8,128)(2,1)S(1)}, bf16[128,1024]{0,1:T(8,128)(2,1)S(1)}, u32[]{:S(2)}, u32[]{:S(2)}) collective-permute-start(bf16[128,1024]{0,1:T(8,128)(2,1)S(1)} %bitcast.148), channel_id=1, source_target_pairs={{4,6},{6,4},{8,10},{10,8},{12,14},{14,12},{5,7},{7,5},{9,11},{11,9... | collective-permute-start | bytes 786440 | tf_op jit(solution)/shard_map/ppermute | solution.py:105
  165.1 8.4 %collective-permute-start.34 = (bf16[128,1024]{0,1:T(8,128)(2,1)S(1)}, bf16[128,1024]{0,1:T(8,128)(2,1)S(1)}, u32[]{:S(2)}, u32[]{:S(2)}) collective-permute-start(bf16[128,1024]{0,1:T(8,128)(2,1)S(1)} %copy-done.6), channel_id=1, source_target_pairs={{0,2},{4,6},{8,10},{12,14},{1,3},{5,7},{9,11},{13,15},{16,18},{20,... | collective-permute-start | bytes 786440 | tf_op jit(solution)/shard_map/ppermute | solution.py:43
  168.7 17.3 %collective-permute-start.24 = (bf16[128,1024]{0,1:T(8,128)(2,1)S(1)}, bf16[128,1024]{0,1:T(8,128)(2,1)S(1)}, u32[]{:S(2)}, u32[]{:S(2)}) collective-permute-start(bf16[128,1024]{0,1:T(8,128)(2,1)S(1)} %bitcast.147), channel_id=1, source_target_pairs={{2,0},{6,4},{10,8},{14,12},{3,1},{7,5},{11,9},{15,13},{18,16},{22,... | collective-permute-start | bytes 786440 | tf_op jit(solution)/shard_map/ppermute | solution.py:102
  170.1 15.9 %collective-permute-start.30 = (bf16[128,1024]{0,1:T(8,128)(2,1)S(1)}, bf16[128,1024]{0,1:T(8,128)(2,1)S(1)}, u32[]{:S(2)}, u32[]{:S(2)}) collective-permute-start(bf16[128,1024]{0,1:T(8,128)(2,1)S(1)} %fusion.22), channel_id=1, source_target_pairs={{12,0},{14,2},{13,1},{15,3},{28,16},{30,18},{29,17},{31,19}} | collective-permute-start | bytes 786440 | tf_op jit(solution)/shard_map/ppermute | solution.py:110
  171.5 2.8 collective-permute-start.35
  172.7 3.0 %collective-permute-start.36 = (bf16[128,1024]{0,1:T(8,128)(2,1)S(1)}, bf16[128,1024]{0,1:T(8,128)(2,1)S(1)}, u32[]{:S(2)}, u32[]{:S(2)}) collective-permute-start(bf16[128,1024]{0,1:T(8,128)(2,1)S(1)} %collective-permute-done.32), channel_id=1, source_target_pairs={{10,8},{8,10},{14,12},{12,14},{11,9},{9,11},{15,13},{13,15},{26,24... | collective-permute-start | bytes 786440 | tf_op jit(solution)/shard_map/ppermute | solution.py:46
  173.5 3.6 %collective-permute-start.37 = (bf16[128,1024]{0,1:T(8,128)(2,1)S(1)}, bf16[128,1024]{0,1:T(8,128)(2,1)S(1)}, u32[]{:S(2)}, u32[]{:S(2)}) collective-permute-start(bf16[128,1024]{0,1:T(8,128)(2,1)S(1)} %collective-permute-done.33), channel_id=1, source_target_pairs={{14,12},{12,14},{15,13},{13,15},{30,28},{28,30},{31,29},{29,31}} | collective-permute-start | bytes 786440 | tf_op jit(solution)/shard_map/ppermute | solution.py:46
  174.3 26.8 %collective-permute-start.28 = (bf16[128,1024]{0,1:T(8,128)(2,1)S(1)}, bf16[128,1024]{0,1:T(8,128)(2,1)S(1)}, u32[]{:S(2)}, u32[]{:S(2)}) collective-permute-start(bf16[128,1024]{0,1:T(8,128)(2,1)S(1)} %fusion.23), channel_id=1, source_target_pairs={{8,0},{10,2},{12,4},{14,6},{9,1},{11,3},{13,5},{15,7},{24,16},{26,... | collective-permute-start | bytes 786440 | tf_op jit(solution)/shard_map/ppermute | solution.py:110
  175.7 25.4 %collective-permute-start.26 = (bf16[128,1024]{0,1:T(8,128)(2,1)S(1)}, bf16[128,1024]{0,1:T(8,128)(2,1)S(1)}, u32[]{:S(2)}, u32[]{:S(2)}) collective-permute-start(bf16[128,1024]{0,1:T(8,128)(2,1)S(1)} %fusion.24), channel_id=1, source_target_pairs={{4,0},{6,2},{8,4},{10,6},{12,8},{14,10},{5,1},{7,3},{9,5},{11,7},{... | collective-permute-start | bytes 786440 | tf_op jit(solution)/shard_map/ppermute | solution.py:110
  214.1 16.9 %collective-permute-start.43 = (bf16[128,1024]{1,0:T(8,128)(2,1)}, bf16[128,1024]{1,0:T(8,128)(2,1)}, u32[]{:S(2)}, u32[]{:S(2)}) collective-permute-start(bf16[128,1024]{1,0:T(8,128)(2,1)} %copy.73), channel_id=1, source_target_pairs={{12,14},{14,12},{13,15},{15,13},{28,30},{30,28},{29,31},{31,29}} | collective-permute-start | bytes 786440 | tf_op jit(solution)/shard_map/ppermute | solution.py:105
  217.5 16.0 %collective-permute-start.41 = (bf16[128,1024]{1,0:T(8,128)(2,1)}, bf16[128,1024]{1,0:T(8,128)(2,1)}, u32[]{:S(2)}, u32[]{:S(2)}) collective-permute-start(bf16[128,1024]{1,0:T(8,128)(2,1)} %copy.71), channel_id=1, source_target_pairs={{8,10},{10,8},{12,14},{14,12},{9,11},{11,9},{13,15},{15,13},{24,26... | collective-permute-start | bytes 786440 | tf_op jit(solution)/shard_map/ppermute | solution.py:105
  220.4 6.9 %collective-permute-start.45 = (f32[464,128]{1,0:T(8,128)}, f32[464,128]{1,0:T(8,128)}, u32[]{:S(2)}, u32[]{:S(2)}) collective-permute-start(f32[464,128]{1,0:T(8,128)} %maximum_bitcast_fusion), channel_id=1, source_target_pairs={{0,1},{1,0},{2,3},{3,2},{4,5},{5,4},{6,7},{7,6},{8,9},{9,8},{10,11... | collective-permute-start | bytes 712712 | tf_op jit(solution)/shard_map/ppermute | solution.py:19
  222.7 13.1 %collective-permute-start.39 = (bf16[128,1024]{1,0:T(8,128)(2,1)S(1)}, bf16[128,1024]{1,0:T(8,128)(2,1)}, u32[]{:S(2)}, u32[]{:S(2)}) collective-permute-start(bf16[128,1024]{1,0:T(8,128)(2,1)S(1)} %copy.69), channel_id=1, source_target_pairs={{4,6},{6,4},{8,10},{10,8},{12,14},{14,12},{5,7},{7,5},{9,11},{11,9... | collective-permute-start | bytes 786440 | tf_op jit(solution)/shard_map/ppermute | solution.py:105
  225.9 44.2 %collective-permute-start.38 = (bf16[128,1024]{1,0:T(8,128)(2,1)}, bf16[128,1024]{1,0:T(8,128)(2,1)S(1)}, u32[]{:S(2)}, u32[]{:S(2)}) collective-permute-start(bf16[128,1024]{1,0:T(8,128)(2,1)} %copy.68), channel_id=1, source_target_pairs={{2,0},{6,4},{10,8},{14,12},{3,1},{7,5},{11,9},{15,13},{18,16},{22,... | collective-permute-start | bytes 786440 | tf_op jit(solution)/shard_map/ppermute | solution.py:102
  228.3 13.6 %collective-permute-start.46 = (f32[464,128]{1,0:T(8,128)S(1)}, f32[464,128]{1,0:T(8,128)S(1)}, u32[]{:S(2)}, u32[]{:S(2)}) collective-permute-start(f32[464,128]{1,0:T(8,128)S(1)} %fusion.32), channel_id=1, source_target_pairs={{0,2},{2,0},{4,6},{6,4},{8,10},{10,8},{12,14},{14,12},{1,3},{3,1},... | collective-permute-start | bytes 712712 | tf_op jit(solution)/shard_map/ppermute | solution.py:19
  232.2 37.9 %collective-permute-start.44 = (bf16[128,1024]{1,0:T(8,128)(2,1)S(1)}, bf16[128,1024]{1,0:T(8,128)(2,1)S(1)}, u32[]{:S(2)}, u32[]{:S(2)}) collective-permute-start(bf16[128,1024]{1,0:T(8,128)(2,1)S(1)} %add_convert_fusion.1), channel_id=1, source_target_pairs={{12,0},{14,2},{13,1},{15,3},{28,16},{30,18},{29,17},{31,19}} | collective-permute-start | bytes 786440 | tf_op jit(solution)/shard_map/ppermute | solution.py:110
  234.5 35.6 %collective-permute-start.42 = (bf16[128,1024]{1,0:T(8,128)(2,1)S(1)}, bf16[128,1024]{1,0:T(8,128)(2,1)S(1)}, u32[]{:S(2)}, u32[]{:S(2)}) collective-permute-start(bf16[128,1024]{1,0:T(8,128)(2,1)S(1)} %add_convert_fusion.2), channel_id=1, source_target_pairs={{8,0},{10,2},{12,4},{14,6},{9,1},{11,3},{13,5},{15,7},{24,16},{26,... | collective-permute-start | bytes 786440 | tf_op jit(solution)/shard_map/ppermute | solution.py:110
  236.9 33.3 %collective-permute-start.40 = (bf16[128,1024]{1,0:T(8,128)(2,1)S(1)}, bf16[128,1024]{1,0:T(8,128)(2,1)S(1)}, u32[]{:S(2)}, u32[]{:S(2)}) collective-permute-start(bf16[128,1024]{1,0:T(8,128)(2,1)S(1)} %add_convert_fusion.3), channel_id=1, source_target_pairs={{4,0},{6,2},{8,4},{10,6},{12,8},{14,10},{5,1},{7,3},{9,5},{11,7},{... | collective-permute-start | bytes 786440 | tf_op jit(solution)/shard_map/ppermute | solution.py:110
  242.9 20.2 %collective-permute-start.47 = (f32[464,128]{1,0:T(8,128)S(1)}, f32[464,128]{1,0:T(8,128)S(1)}, u32[]{:S(2)}, u32[]{:S(2)}) collective-permute-start(f32[464,128]{1,0:T(8,128)S(1)} %fusion.61), channel_id=1, source_target_pairs={{0,4},{2,6},{4,0},{6,2},{8,12},{10,14},{12,8},{14,10},{1,5},{3,7},... | collective-permute-start | bytes 712712 | tf_op jit(solution)/shard_map/ppermute | solution.py:19
  263.1 16.2 %collective-permute-start.48 = (f32[464,128]{1,0:T(8,128)S(1)}, f32[464,128]{1,0:T(8,128)S(1)}, u32[]{:S(2)}, u32[]{:S(2)}) collective-permute-start(f32[464,128]{1,0:T(8,128)S(1)} %add.269), channel_id=1, source_target_pairs={{0,8},{2,10},{4,12},{6,14},{8,0},{10,2},{12,4},{14,6},{1,9},{3,11}... | collective-permute-start | bytes 712712 | tf_op jit(solution)/shard_map/ppermute | solution.py:19
  (20 other events, 331.3 us)
Sparse Core Ops, SparseCore 0:
  79.4 13.8 all-gather.1

commit v9 on v7

--- a/solution.py
+++ b/solution.py
@@ -152,7 +152,15 @@
         rows_half = tree_gather(own_half, ctx_index, ctx_count // 2)
     else:
         rows_half = lax.all_gather(own_half, "ctx", axis=0, tiled=True)
-    full_weight = lax.all_gather(rows_half, "pair", axis=1, tiled=True)
+    if lax.axis_size("pair") == 2:
+        other_half = from_partner(rows_half, "pair", 0)
+        full_weight = jnp.zeros((rows_half.shape[0], width_kv), rows_half.dtype)
+        full_weight = lax.dynamic_update_slice_in_dim(full_weight, rows_half, pair_index * half_cols, 1)
+        full_weight = lax.dynamic_update_slice_in_dim(
+            full_weight, other_half, (1 - pair_index) * half_cols, 1
+        )
+    else:
+        full_weight = lax.all_gather(rows_half, "pair", axis=1, tiled=True)
     rank_projection = jnp.dot(hidden_rows, adapter_down, preferred_element_type=jnp.float32).astype(
         jnp.bfloat16
     )

time: 279 us -> 277 us (level)
  between operations: 15.1 us -> 1.82 us
  local copies, waits for them, and re-layouts: 40.5 us -> 47.5 us
  waiting for transfers between devices: 68.8 us -> 75.7 us
  starting transfers between devices: 110 us -> 107 us
    ppermute x3, waiting for transfers between devices: 4.63 us -> 8.89 us  [tree_gather(): lax.ppermute(downs[step - 1], 'ctx', [(c ^ 1, c) for c in range(0, count...]
    dynamic_update_slice x0 -> x1, local copies, waits for them, and re-layouts: none -> 3.58 us  [shards(): lax.dynamic_update_slice_in_dim(full_weight, other_half, (1 - pair_index)...]
    ppermute x8 -> x9, starting transfers between devices: 38.4 us -> 34.9 us  [from_partner(): lax.ppermute(shard, axis, [(i, i ^ 1 << stride) for i in range(lax.axis_s...]
    ppermute x6, starting transfers between devices: 23.7 us -> 27 us  [tree_spread(): lax.ppermute(held, 'ctx', [(c - 2, c) for c in range(2 * step, count)])]
    broadcast_in_dim x0 -> x1, local copies, waits for them, and re-layouts: none -> 3.15 us  [shards(): full_weight = jnp.zeros((rows_half.shape[0], width_kv), rows_half.dtype)]
    ppermute x3, waiting for transfers between devices: 11.8 us -> 14.9 us  [tree_gather(): lax.ppermute(down, 'ctx', [(c + 2, c) for c in range(0, count - 2 * step)])]
    ppermute x8 -> x9, waiting for transfers between devices: 21.9 us -> 24 us  [from_partner(): lax.ppermute(shard, axis, [(i, i ^ 1 << stride) for i in range(lax.axis_s...]
    unnamed x58 -> x60, local copies, waits for them, and re-layouts: 6.93 us -> 6.94 us
  transfers between devices with their start and end apart: 50 -> 50, of which waited for: 16 -> 16; matrix products, arithmetic and copies ran while one was open for 18% -> 22% of each run, Pallas kernels for 0% -> 0%
where the time goes in v9:
time: 277 us; the launch traced here: 276 us
  starting transfers between devices  107 us (39%)
  waiting for transfers between devices  75.7 us (27%)
  local copies, waits for them, and re-layouts  47.5 us (17%)
  matrix products  29.5 us (11%)
  other arithmetic  14.8 us (5%)
    ppermute x9, starting transfers between devices, from_partner(): lax.ppermute(shard, axis, [(i, i ^ 1 << stride) for i in range(lax.axis_s...  34.9 us
    ppermute x6, starting transfers between devices, tree_spread(): lax.ppermute(held, 'ctx', [(c - 2, c) for c in range(2 * step, count)])  27 us
    ppermute x9, waiting for transfers between devices, from_partner(): lax.ppermute(shard, axis, [(i, i ^ 1 << stride) for i in range(lax.axis_s...  24 us
    ppermute x6, waiting for transfers between devices, tree_return(): lax.ppermute(acc.astype(jnp.bfloat16), 'ctx', [(c, c - 2) for c in range(...  21.7 us
    ppermute x3, waiting for transfers between devices, tree_gather(): lax.ppermute(down, 'ctx', [(c + 2, c) for c in range(0, count - 2 * step)])  14.9 us
    dynamic_update_slice x14, local copies, waits for them, and re-layouts, tree_gather(): whole = lax.dynamic_update_slice_in_dim(whole, piece, place, 0)  10.7 us
    ppermute x3, waiting for transfers between devices, tree_gather(): lax.ppermute(downs[step - 1], 'ctx', [(c ^ 1, c) for c in range(0, count...  8.89 us
    ppermute x3, starting transfers between devices, tree_gather(): lax.ppermute(downs[step - 1], 'ctx', [(c ^ 1, c) for c in range(0, count...  7.71 us
  transfers between devices with their start and end apart: 50, of which 16 were waited for; matrix products, arithmetic and copies ran while one was open for 22% of the time, Pallas kernels for 0%

profile of v9, /device:TPU:0, one launch (start us, length us, event | category | flops | bytes accessed | tf_op | source)
XLA Modules:
  0.0 275.9 jit_solution(9957655602330106144)
XLA Ops:
  0.7 5.8 %collective-permute-start.3 = (bf16[128,1024]{1,0:T(8,128)(2,1)}, bf16[128,1024]{1,0:T(8,128)(2,1)}, u32[]{:S(2)}, u32[]{:S(2)}) collective-permute-start(bf16[128,1024]{1,0:T(8,128)(2,1)} %bitcast.151), channel_id=1, source_target_pairs={{0,4},{2,6},{4,8},{6,10},{8,12},{10,14},{1,5},{3,7},{5,9},{7,11},{... | collective-permute-start | bytes 786440 | tf_op jit(solution)/shard_map/ppermute | solution.py:41
  6.5 4.1 %collective-permute-start.6 = (bf16[128,1024]{1,0:T(8,128)(2,1)}, bf16[128,1024]{1,0:T(8,128)(2,1)}, u32[]{:S(2)}, u32[]{:S(2)}) collective-permute-start(bf16[128,1024]{1,0:T(8,128)(2,1)} %bitcast.152), channel_id=1, source_target_pairs={{0,2},{4,6},{8,10},{12,14},{1,3},{5,7},{9,11},{13,15},{16,18},{20,... | collective-permute-start | bytes 786440 | tf_op jit(solution)/shard_map/ppermute | solution.py:43
  10.6 1.8 broadcast_in_dim.58
  13.2 2.8 %collective-permute-start.10 = (bf16[336,512]{1,0:T(8,128)(2,1)S(1)}, bf16[336,512]{1,0:T(8,128)(2,1)S(1)}, u32[]{:S(2)}, u32[]{:S(2)}) collective-permute-start(bf16[336,512]{1,0:T(8,128)(2,1)S(1)} %get-tuple-element.29), channel_id=1, source_target_pairs={{0,4},{2,6},{4,8},{6,10},{8,12},{10,14},{1,5},{3,7},{5,9},{7,11},{... | collective-permute-start | bytes 1032200 | tf_op jit(solution)/shard_map/ppermute | solution.py:60
  19.0 3.7 %collective-permute-done.10 = bf16[336,512]{1,0:T(8,128)(2,1)S(1)} collective-permute-done((bf16[336,512]{1,0:T(8,128)(2,1)S(1)}, bf16[336,512]{1,0:T(8,128)(2,1)S(1)}, u32[]{:S(2)}, u32[]{:S(2)}) %collective-permute-start.10) | collective-permute-done | bytes 344096 | tf_op jit(solution)/shard_map/ppermute | solution.py:60
  23.4 3.4 %collective-permute-done.11 = bf16[336,512]{1,0:T(8,128)(2,1)S(1)} collective-permute-done((bf16[336,512]{1,0:T(8,128)(2,1)S(1)}, bf16[336,512]{1,0:T(8,128)(2,1)S(1)}, u32[]{:S(2)}, u32[]{:S(2)}) %collective-permute-start.11) | collective-permute-done | bytes 344096 | tf_op jit(solution)/shard_map/ppermute | solution.py:61
  30.4 6.6 %collective-permute-done.13 = bf16[336,512]{1,0:T(8,128)(2,1)S(1)} collective-permute-done((bf16[336,512]{1,0:T(8,128)(2,1)S(1)}, bf16[336,512]{1,0:T(8,128)(2,1)S(1)}, u32[]{:S(2)}, u32[]{:S(2)}) %collective-permute-start.13) | collective-permute-done | bytes 344096 | tf_op jit(solution)/shard_map/ppermute | solution.py:61
  41.2 4.9 %collective-permute-done.15 = bf16[336,512]{1,0:T(8,128)(2,1)S(1)} collective-permute-done((bf16[336,512]{1,0:T(8,128)(2,1)S(1)}, bf16[336,512]{1,0:T(8,128)(2,1)S(1)}, u32[]{:S(2)}, u32[]{:S(2)}) %collective-permute-start.15) | collective-permute-done | bytes 344096 | tf_op jit(solution)/shard_map/ppermute | solution.py:61
  46.1 1.9 collective-permute-start.18
  50.2 3.9 %collective-permute-start.20 = (bf16[336,512]{1,0:T(8,128)(2,1)S(1)}, bf16[336,512]{1,0:T(8,128)(2,1)S(1)}, u32[]{:S(2)}, u32[]{:S(2)}) collective-permute-start(bf16[336,512]{1,0:T(8,128)(2,1)S(1)} %collective-permute-done.13), channel_id=1, source_target_pairs={{2,0},{0,2},{6,4},{4,6},{3,1},{1,3},{7,5},{5,7},{18,16},{16,18},{2... | collective-permute-start | bytes 1032200 | tf_op jit(solution)/shard_map/ppermute | solution.py:73
  54.9 4.0 %collective-permute-done.18 = bf16[336,512]{1,0:T(8,128)(2,1)S(1)} collective-permute-done((bf16[336,512]{1,0:T(8,128)(2,1)S(1)}, bf16[336,512]{1,0:T(8,128)(2,1)S(1)}, u32[]{:S(2)}, u32[]{:S(2)}) %collective-permute-start.18) | collective-permute-done | bytes 344096 | tf_op jit(solution)/shard_map/ppermute | solution.py:73
  60.3 1.9 collective-permute-start.22
  63.0 2.6 collective-permute-done.20
  67.1 2.3 collective-permute-done.22
  70.2 3.2 %broadcast_in_dim.57 = bf16[2688,1024]{1,0:T(8,128)(2,1)} broadcast(bf16[]{:T(256)} %constant.74.clone.1), dimensions={} | broadcast | bytes 5505026 | tf_op jit(solution)/shard_map/broadcast_in_dim | solution.py:157
  73.4 3.8 %fusion.35 = (bf16[2688,512]{1,0:T(8,128)(2,1)S(1)}, bf16[2688,1024]{1,0:T(8,128)(2,1)}) fusion(bf16[3024,512]{1,0:T(8,128)(2,1)} %constant_dynamic-update-slice_fusion.26, bf16[2688,1024]{1,0:T(8,128)(2,1)} %broadcast_in_dim.57, s32[]{:T(128)S(6)} %select_n.156), kind=kLoop, calls=%fused_computation.123 | loop fusion | bytes 8257540 | tf_op jit(solution)/shard_map/slice | solution.py:82
  78.6 2.0 copy.94
  80.7 3.5 %collective-permute-done.1 = f32[16]{0:T(128)S(1)} collective-permute-done((f32[16]{0:T(128)S(1)}, f32[16]{0:T(128)S(1)}, u32[]{:S(2)}, u32[]{:S(2)}) %collective-permute-start.1) | collective-permute-done | bytes 96 | tf_op jit(solution)/shard_map/ppermute | solution.py:19
  84.2 1.5 collective-permute-start.2
  85.7 2.9 %collective-permute-done.2 = f32[16]{0:T(128)S(1)} collective-permute-done((f32[16]{0:T(128)S(1)}, f32[16]{0:T(128)S(1)}, u32[]{:S(2)}, u32[]{:S(2)}) %collective-permute-start.2) | collective-permute-done | bytes 96 | tf_op jit(solution)/shard_map/ppermute | solution.py:19
  96.0 3.6 %constant_dynamic-update-slice_fusion.24 = bf16[2688,1024]{1,0:T(8,128)(2,1)} fusion(bf16[2688,1024]{1,0:T(8,128)(2,1)} %get-tuple-element.31, bf16[2688,512]{1,0:T(8,128)(2,1)} %collective-permute-done.23, s32[]{:T(128)S(6)} %select_n.185), kind=kLoop, calls=%fused_computation.84 | loop fusion | bytes 5505028 | tf_op jit(solution)/shard_map/dynamic_update_slice | solution.py:159
  99.6 4.9 %fusion.15 = bf16[128,1024]{0,1:T(8,128)(2,1)} fusion(f32[128,1024]{0,1:T(8,128)S(1)} %copy-done.2, bf16[2688,1024]{1,0:T(8,128)(2,1)} %constant_dynamic-update-slice_fusion.24, bf16[1,128,2688]{2,1,0:T(8,128)(2,1)S(1)} %copy-done), kind=kOutput, calls=%fused_computation.28 | convolution fusion | flops 704905216 | bytes 6979584 | tf_op jit(solution)/shard_map/dot_general | solution.py:168
  104.5 2.0 copy.95
  106.5 3.3 %copy.84 = bf16[1024,8,128,1]{0,2,3,1:T(8,128)(2,1)S(1)} copy(bf16[1024,8,128,1]{2,1,0,3:T(8,128)(2,1)} %bitcast.134) | data formatting | bytes 4194304 | tf_op jit(solution)/shard_map/reshape | solution.py:223
  109.8 5.7 %fusion.39 = (f32[8,2,128]{2,1,0:T(2,128)S(1)}, f32[8,2,128,1024]{2,3,1,0:T(8,128)}) fusion(pred[128,1024]{0,1:T(8,128)(4,1)S(1)} %copy-done.17, bf16[1024,8,128,1]{0,2,3,1:T(8,128)(2,1)S(1)} %copy.84, bf16[128,8,2,128]{0,3,2,1:T(8,128)(2,1)S(1)} %bitcast.138), kind=kOutput, calls=%fused_computation.127 | convolution fusion | flops 547357696 | bytes 11149312 | tf_op jit(solution)/shard_map/sub | solution.py:230
  115.5 5.0 %fusion.40 = (bf16[1024,8,128]{0,2,1:T(8,128)(2,1)S(1)}, f32[1024,8,128]{0,2,1:T(8,128)S(1)}) fusion(bf16[128,8,2,128]{3,2,1,0:T(2,128)(2,1)} %reshape_squeeze.7, f32[128]{0:T(128)S(1)} %get-tuple-element.25, f32[8,2,128,1024]{2,3,1,0:T(8,128)} %get-tuple-element.51, f32[8,2,128]{2,1,0:T(2,128)S(1)} %get-tuple-element.50), kind=kOutput, calls=%fused_computation.128 | convolution fusion | flops 544210944 | bytes 15213056 | tf_op jit(solution)/shard_map/jgtl,tjgd->ljd/dot_general | solution.py:244
  121.9 18.4 %collective-permute-start.32 = (bf16[128,1024]{0,1:T(8,128)(2,1)S(1)}, bf16[128,1024]{0,1:T(8,128)(2,1)S(1)}, u32[]{:S(2)}, u32[]{:S(2)}) collective-permute-start(bf16[128,1024]{0,1:T(8,128)(2,1)S(1)} %copy-done.6), channel_id=1, source_target_pairs={{0,4},{2,6},{4,8},{6,10},{8,12},{10,14},{1,5},{3,7},{5,9},{7,11},{... | collective-permute-start | bytes 786440 | tf_op jit(solution)/shard_map/ppermute | solution.py:41
  142.5 2.4 collective-permute-done.32
  146.4 3.4 %collective-permute-start.35 = (bf16[128,1024]{0,1:T(8,128)(2,1)S(1)}, bf16[128,1024]{0,1:T(8,128)(2,1)S(1)}, u32[]{:S(2)}, u32[]{:S(2)}) collective-permute-start(bf16[128,1024]{0,1:T(8,128)(2,1)S(1)} %copy-done.6), channel_id=1, source_target_pairs={{0,2},{4,6},{8,10},{12,14},{1,3},{5,7},{9,11},{13,15},{16,18},{20,... | collective-permute-start | bytes 786440 | tf_op jit(solution)/shard_map/ppermute | solution.py:43
  149.9 1.4 collective-permute-start.25
  156.5 1.9 fusion.1
  158.5 1.7 fusion.3
  161.2 3.5 %fusion.41 = (bf16[1024,8,128]{0,2,1:T(8,128)(2,1)S(1)}, f32[1024,8,128]{0,2,1:T(8,128)}) fusion(bf16[8,2,128,1024]{2,3,1,0:T(8,128)(2,1)S(1)} %fusion.3, bf16[128,8,2,128]{0,3,2,1:T(8,128)(2,1)S(1)} %bitcast.139), kind=kOutput, calls=%fused_computation.129 | convolution fusion | flops 537919488 | bytes 11010048 | tf_op jit(solution)/shard_map/jgtl,tjgd->ljd/dot_general | solution.py:240
  164.7 20.0 %collective-permute-done.31 = bf16[128,1024]{0,1:T(8,128)(2,1)S(1)} collective-permute-done((bf16[128,1024]{0,1:T(8,128)(2,1)S(1)}, bf16[128,1024]{0,1:T(8,128)(2,1)S(1)}, u32[]{:S(2)}, u32[]{:S(2)}) %collective-permute-start.31) | collective-permute-done | bytes 262176 | tf_op jit(solution)/shard_map/ppermute | solution.py:114
  190.5 1.4 collective-permute-start.41
  194.6 1.9 add_convert_fusion.3
  201.5 1.8 copy.69
  203.3 1.4 collective-permute-start.40
  207.8 2.7 collective-permute-start.47
  212.4 9.1 %collective-permute-done.47 = f32[464,128]{1,0:T(8,128)S(1)} collective-permute-done((f32[464,128]{1,0:T(8,128)S(1)}, f32[464,128]{1,0:T(8,128)S(1)}, u32[]{:S(2)}, u32[]{:S(2)}) %collective-permute-start.47) | collective-permute-done | bytes 237600 | tf_op jit(solution)/shard_map/ppermute | solution.py:19
  222.4 12.2 %collective-permute-start.48 = (f32[464,128]{1,0:T(8,128)S(1)}, f32[464,128]{1,0:T(8,128)S(1)}, u32[]{:S(2)}, u32[]{:S(2)}) collective-permute-start(f32[464,128]{1,0:T(8,128)S(1)} %fusion.64), channel_id=1, source_target_pairs={{0,4},{2,6},{4,0},{6,2},{8,12},{10,14},{12,8},{14,10},{1,5},{3,7},... | collective-permute-start | bytes 712712 | tf_op jit(solution)/shard_map/ppermute | solution.py:19
  234.9 5.5 %collective-permute-done.48 = f32[464,128]{1,0:T(8,128)S(1)} collective-permute-done((f32[464,128]{1,0:T(8,128)S(1)}, f32[464,128]{1,0:T(8,128)S(1)}, u32[]{:S(2)}, u32[]{:S(2)}) %collective-permute-start.48) | collective-permute-done | bytes 237600 | tf_op jit(solution)/shard_map/ppermute | solution.py:19
  240.5 18.5 %collective-permute-start.49 = (f32[464,128]{1,0:T(8,128)S(1)}, f32[464,128]{1,0:T(8,128)S(1)}, u32[]{:S(2)}, u32[]{:S(2)}) collective-permute-start(f32[464,128]{1,0:T(8,128)S(1)} %add.274), channel_id=1, source_target_pairs={{0,8},{2,10},{4,12},{6,14},{8,0},{10,2},{12,4},{14,6},{1,9},{3,11}... | collective-permute-start | bytes 712712 | tf_op jit(solution)/shard_map/ppermute | solution.py:19
  259.0 1.8 add_convert_fusion.1
  262.1 5.3 %fusion.11 = bf16[1,128,2688]{2,1,0:T(8,128)(2,1)} fusion(f32[128,2688]{1,0:T(8,128)S(1)} %convolution_multiply_fusion, bf16[128,1024]{0,1:T(8,128)(2,1)S(1)} %fusion.27, bf16[2688,1024]{1,0:T(8,128)(2,1)} %constant_dynamic-update-slice_fusion.24), kind=kOutput, calls=%fused_computation.19 | convolution fusion | flops 705331200 | bytes 7831552 | tf_op jit(solution)/shard_map/tk,dk->td/dot_general | solution.py:269
  267.4 2.9 %collective-permute-done.49 = f32[464,128]{1,0:T(8,128)S(1)} collective-permute-done((f32[464,128]{1,0:T(8,128)S(1)}, f32[464,128]{1,0:T(8,128)S(1)}, u32[]{:S(2)}, u32[]{:S(2)}) %collective-permute-start.49) | collective-permute-done | bytes 237600 | tf_op jit(solution)/shard_map/ppermute | solution.py:19
  272.5 1.7 collective-permute-done.45
  274.2 1.8 fusion.31
  (205 shorter events, 62.4 us)
Async XLA Ops:
  0.7 88.3 %collective-permute-start.3 = (bf16[128,1024]{1,0:T(8,128)(2,1)}, bf16[128,1024]{1,0:T(8,128)(2,1)}, u32[]{:S(2)}, u32[]{:S(2)}) collective-permute-start(bf16[128,1024]{1,0:T(8,128)(2,1)} %bitcast.151), channel_id=1, source_target_pairs={{0,4},{2,6},{4,8},{6,10},{8,12},{10,14},{1,5},{3,7},{5,9},{7,11},{... | collective-permute-start | bytes 786440 | tf_op jit(solution)/shard_map/ppermute | solution.py:41
  6.5 88.4 %collective-permute-start.6 = (bf16[128,1024]{1,0:T(8,128)(2,1)}, bf16[128,1024]{1,0:T(8,128)(2,1)}, u32[]{:S(2)}, u32[]{:S(2)}) collective-permute-start(bf16[128,1024]{1,0:T(8,128)(2,1)} %bitcast.152), channel_id=1, source_target_pairs={{0,2},{4,6},{8,10},{12,14},{1,3},{5,7},{9,11},{13,15},{16,18},{20,... | collective-permute-start | bytes 786440 | tf_op jit(solution)/shard_map/ppermute | solution.py:43
  13.2 9.5 %collective-permute-start.10 = (bf16[336,512]{1,0:T(8,128)(2,1)S(1)}, bf16[336,512]{1,0:T(8,128)(2,1)S(1)}, u32[]{:S(2)}, u32[]{:S(2)}) collective-permute-start(bf16[336,512]{1,0:T(8,128)(2,1)S(1)} %get-tuple-element.29), channel_id=1, source_target_pairs={{0,4},{2,6},{4,8},{6,10},{8,12},{10,14},{1,5},{3,7},{5,9},{7,11},{... | collective-permute-start | bytes 1032200 | tf_op jit(solution)/shard_map/ppermute | solution.py:60
  16.0 10.9 %collective-permute-start.11 = (bf16[336,512]{1,0:T(8,128)(2,1)S(1)}, bf16[336,512]{1,0:T(8,128)(2,1)S(1)}, u32[]{:S(2)}, u32[]{:S(2)}) collective-permute-start(bf16[336,512]{1,0:T(8,128)(2,1)S(1)} %get-tuple-element.29), channel_id=1, source_target_pairs={{4,0},{6,2},{8,4},{10,6},{12,8},{14,10},{5,1},{7,3},{9,5},{11,7},{... | collective-permute-start | bytes 1032200 | tf_op jit(solution)/shard_map/ppermute | solution.py:61
  17.3 31.5 %collective-permute-start.16 = (bf16[336,512]{1,0:T(8,128)(2,1)S(1)}, bf16[336,512]{1,0:T(8,128)(2,1)S(1)}, u32[]{:S(2)}, u32[]{:S(2)}) collective-permute-start(bf16[336,512]{1,0:T(8,128)(2,1)S(1)} %get-tuple-element.29), channel_id=1, source_target_pairs={{2,0},{0,2},{6,4},{4,6},{10,8},{8,10},{14,12},{12,14},{3,1},{1,3},... | collective-permute-start | bytes 1032200 | tf_op jit(solution)/shard_map/ppermute | solution.py:67
  22.7 6.2 %collective-permute-start.12 = (bf16[336,512]{1,0:T(8,128)(2,1)S(1)}, bf16[336,512]{1,0:T(8,128)(2,1)S(1)}, u32[]{:S(2)}, u32[]{:S(2)}) collective-permute-start(bf16[336,512]{1,0:T(8,128)(2,1)S(1)} %collective-permute-done.10), channel_id=1, source_target_pairs={{4,8},{6,10},{8,12},{10,14},{5,9},{7,11},{9,13},{11,15},{20,24},{2... | collective-permute-start | bytes 1032200 | tf_op jit(solution)/shard_map/ppermute | solution.py:60
  26.9 10.1 %collective-permute-start.13 = (bf16[336,512]{1,0:T(8,128)(2,1)S(1)}, bf16[336,512]{1,0:T(8,128)(2,1)S(1)}, u32[]{:S(2)}, u32[]{:S(2)}) collective-permute-start(bf16[336,512]{1,0:T(8,128)(2,1)S(1)} %collective-permute-done.11), channel_id=1, source_target_pairs={{4,0},{6,2},{8,4},{10,6},{5,1},{7,3},{9,5},{11,7},{20,16},{22,18},... | collective-permute-start | bytes 1032200 | tf_op jit(solution)/shard_map/ppermute | solution.py:61
  28.9 10.8 %collective-permute-start.14 = (bf16[336,512]{1,0:T(8,128)(2,1)S(1)}, bf16[336,512]{1,0:T(8,128)(2,1)S(1)}, u32[]{:S(2)}, u32[]{:S(2)}) collective-permute-start(bf16[336,512]{1,0:T(8,128)(2,1)S(1)} %collective-permute-done.12), channel_id=1, source_target_pairs={{8,12},{10,14},{9,13},{11,15},{24,28},{26,30},{25,29},{27,31}} | collective-permute-start | bytes 1032200 | tf_op jit(solution)/shard_map/ppermute | solution.py:60
  36.9 9.1 %collective-permute-start.15 = (bf16[336,512]{1,0:T(8,128)(2,1)S(1)}, bf16[336,512]{1,0:T(8,128)(2,1)S(1)}, u32[]{:S(2)}, u32[]{:S(2)}) collective-permute-start(bf16[336,512]{1,0:T(8,128)(2,1)S(1)} %collective-permute-done.13), channel_id=1, source_target_pairs={{4,0},{6,2},{5,1},{7,3},{20,16},{22,18},{21,17},{23,19}} | collective-permute-start | bytes 1032200 | tf_op jit(solution)/shard_map/ppermute | solution.py:61
  39.7 10.5 %collective-permute-start.17 = (bf16[336,512]{1,0:T(8,128)(2,1)S(1)}, bf16[336,512]{1,0:T(8,128)(2,1)S(1)}, u32[]{:S(2)}, u32[]{:S(2)}) collective-permute-start(bf16[336,512]{1,0:T(8,128)(2,1)S(1)} %collective-permute-done.10), channel_id=1, source_target_pairs={{6,4},{4,6},{10,8},{8,10},{14,12},{12,14},{7,5},{5,7},{11,9},{9,11... | collective-permute-start | bytes 1032200 | tf_op jit(solution)/shard_map/ppermute | solution.py:71
  46.1 12.8 %collective-permute-start.18 = (bf16[336,512]{1,0:T(8,128)(2,1)S(1)}, bf16[336,512]{1,0:T(8,128)(2,1)S(1)}, u32[]{:S(2)}, u32[]{:S(2)}) collective-permute-start(bf16[336,512]{1,0:T(8,128)(2,1)S(1)} %collective-permute-done.11), channel_id=1, source_target_pairs={{2,0},{0,2},{6,4},{4,6},{10,8},{8,10},{3,1},{1,3},{7,5},{5,7},{11,... | collective-permute-start | bytes 1032200 | tf_op jit(solution)/shard_map/ppermute | solution.py:73
  48.8 11.5 %collective-permute-start.19 = (bf16[336,512]{1,0:T(8,128)(2,1)S(1)}, bf16[336,512]{1,0:T(8,128)(2,1)S(1)}, u32[]{:S(2)}, u32[]{:S(2)}) collective-permute-start(bf16[336,512]{1,0:T(8,128)(2,1)S(1)} %collective-permute-done.12), channel_id=1, source_target_pairs={{10,8},{8,10},{14,12},{12,14},{11,9},{9,11},{15,13},{13,15},{26,24... | collective-permute-start | bytes 1032200 | tf_op jit(solution)/shard_map/ppermute | solution.py:71
  50.2 15.4 %collective-permute-start.20 = (bf16[336,512]{1,0:T(8,128)(2,1)S(1)}, bf16[336,512]{1,0:T(8,128)(2,1)S(1)}, u32[]{:S(2)}, u32[]{:S(2)}) collective-permute-start(bf16[336,512]{1,0:T(8,128)(2,1)S(1)} %collective-permute-done.13), channel_id=1, source_target_pairs={{2,0},{0,2},{6,4},{4,6},{3,1},{1,3},{7,5},{5,7},{18,16},{16,18},{2... | collective-permute-start | bytes 1032200 | tf_op jit(solution)/shard_map/ppermute | solution.py:73
  58.8 7.5 %collective-permute-start.21 = (bf16[336,512]{1,0:T(8,128)(2,1)S(1)}, bf16[336,512]{1,0:T(8,128)(2,1)S(1)}, u32[]{:S(2)}, u32[]{:S(2)}) collective-permute-start(bf16[336,512]{1,0:T(8,128)(2,1)S(1)} %collective-permute-done.14), channel_id=1, source_target_pairs={{14,12},{12,14},{15,13},{13,15},{30,28},{28,30},{31,29},{29,31}} | collective-permute-start | bytes 1032200 | tf_op jit(solution)/shard_map/ppermute | solution.py:71
  60.3 9.1 %collective-permute-start.22 = (bf16[336,512]{1,0:T(8,128)(2,1)S(1)}, bf16[336,512]{1,0:T(8,128)(2,1)S(1)}, u32[]{:S(2)}, u32[]{:S(2)}) collective-permute-start(bf16[336,512]{1,0:T(8,128)(2,1)S(1)} %collective-permute-done.15), channel_id=1, source_target_pairs={{2,0},{0,2},{3,1},{1,3},{18,16},{16,18},{19,17},{17,19}} | collective-permute-start | bytes 1032200 | tf_op jit(solution)/shard_map/ppermute | solution.py:73
  65.6 15.0 %collective-permute-start = (f32[16]{0:T(128)S(1)}, f32[16]{0:T(128)S(1)}, u32[]{:S(2)}, u32[]{:S(2)}) collective-permute-start(f32[16]{0:T(128)S(1)} %pad_maximum_fusion), channel_id=1, source_target_pairs={{0,2},{2,0},{4,6},{6,4},{8,10},{10,8},{12,14},{14,12},{1,3},{3,1},... | collective-permute-start | bytes 200 | tf_op jit(solution)/shard_map/ppermute | solution.py:19
  77.1 18.9 %collective-permute-start.23 = (bf16[2688,512]{1,0:T(8,128)(2,1)S(1)}, bf16[2688,512]{1,0:T(8,128)(2,1)}, u32[]{:S(2)}, u32[]{:S(2)}) collective-permute-start(bf16[2688,512]{1,0:T(8,128)(2,1)S(1)} %get-tuple-element.30), channel_id=1, source_target_pairs={{0,1},{1,0},{2,3},{3,2},{4,5},{5,4},{6,7},{7,6},{8,9},{9,8},{10,11... | collective-permute-start | bytes 8257544 | tf_op jit(solution)/shard_map/ppermute | solution.py:19
  80.7 3.5 %collective-permute-start.1 = (f32[16]{0:T(128)S(1)}, f32[16]{0:T(128)S(1)}, u32[]{:S(2)}, u32[]{:S(2)}) collective-permute-start(f32[16]{0:T(128)S(1)} %fusion.65), channel_id=1, source_target_pairs={{0,4},{2,6},{4,0},{6,2},{8,12},{10,14},{12,8},{14,10},{1,5},{3,7},... | collective-permute-start | bytes 200 | tf_op jit(solution)/shard_map/ppermute | solution.py:19
  84.2 4.4 %collective-permute-start.2 = (f32[16]{0:T(128)S(1)}, f32[16]{0:T(128)S(1)}, u32[]{:S(2)}, u32[]{:S(2)}) collective-permute-start(f32[16]{0:T(128)S(1)} %add.231), channel_id=1, source_target_pairs={{0,8},{2,10},{4,12},{6,14},{8,0},{10,2},{12,4},{14,6},{1,9},{3,11}... | collective-permute-start | bytes 200 | tf_op jit(solution)/shard_map/ppermute | solution.py:19
  90.1 3.9 %collective-permute-start.5 = (bf16[128,1024]{1,0:T(8,128)(2,1)S(1)}, bf16[128,1024]{1,0:T(8,128)(2,1)S(1)}, u32[]{:S(2)}, u32[]{:S(2)}) collective-permute-start(bf16[128,1024]{1,0:T(8,128)(2,1)S(1)} %collective-permute-done.4), channel_id=1, source_target_pairs={{8,12},{10,14},{9,13},{11,15},{24,28},{26,30},{25,29},{27,31}} | collective-permute-start | bytes 786440 | tf_op jit(solution)/shard_map/ppermute | solution.py:41
  92.6 3.3 %collective-permute-start.7 = (bf16[128,1024]{1,0:T(8,128)(2,1)}, bf16[128,1024]{1,0:T(8,128)(2,1)S(1)}, u32[]{:S(2)}, u32[]{:S(2)}) collective-permute-start(bf16[128,1024]{1,0:T(8,128)(2,1)} %collective-permute-done.3), channel_id=1, source_target_pairs={{6,4},{4,6},{10,8},{8,10},{14,12},{12,14},{7,5},{5,7},{11,9},{9,11... | collective-permute-start | bytes 786440 | tf_op jit(solution)/shard_map/ppermute | solution.py:46
  93.3 2.6 collective-permute-start.8
  94.0 2.0 collective-permute-start.9
  121.0 20.0 %collective-permute-start.28 = (bf16[128,1024]{0,1:T(8,128)(2,1)S(1)}, bf16[128,1024]{0,1:T(8,128)(2,1)S(1)}, u32[]{:S(2)}, u32[]{:S(2)}) collective-permute-start(bf16[128,1024]{0,1:T(8,128)(2,1)S(1)} %bitcast.150), channel_id=1, source_target_pairs={{12,14},{14,12},{13,15},{15,13},{28,30},{30,28},{29,31},{31,29}} | collective-permute-start | bytes 786440 | tf_op jit(solution)/shard_map/ppermute | solution.py:106
  121.9 23.0 %collective-permute-start.32 = (bf16[128,1024]{0,1:T(8,128)(2,1)S(1)}, bf16[128,1024]{0,1:T(8,128)(2,1)S(1)}, u32[]{:S(2)}, u32[]{:S(2)}) collective-permute-start(bf16[128,1024]{0,1:T(8,128)(2,1)S(1)} %copy-done.6), channel_id=1, source_target_pairs={{0,4},{2,6},{4,8},{6,10},{8,12},{10,14},{1,5},{3,7},{5,9},{7,11},{... | collective-permute-start | bytes 786440 | tf_op jit(solution)/shard_map/ppermute | solution.py:41
  140.3 5.2 %collective-permute-start.27 = (bf16[128,1024]{0,1:T(8,128)(2,1)S(1)}, bf16[128,1024]{0,1:T(8,128)(2,1)S(1)}, u32[]{:S(2)}, u32[]{:S(2)}) collective-permute-start(bf16[128,1024]{0,1:T(8,128)(2,1)S(1)} %bitcast.149), channel_id=1, source_target_pairs={{8,10},{10,8},{12,14},{14,12},{9,11},{11,9},{13,15},{15,13},{24,26... | collective-permute-start | bytes 786440 | tf_op jit(solution)/shard_map/ppermute | solution.py:106
  141.1 4.4 %collective-permute-start.29 = (bf16[128,1024]{0,1:T(8,128)(2,1)S(1)}, bf16[128,1024]{0,1:T(8,128)(2,1)S(1)}, u32[]{:S(2)}, u32[]{:S(2)}) collective-permute-start(bf16[128,1024]{0,1:T(8,128)(2,1)S(1)} %fusion.22), channel_id=1, source_target_pairs={{12,8},{14,10},{13,9},{15,11},{28,24},{30,26},{29,25},{31,27}} | collective-permute-start | bytes 786440 | tf_op jit(solution)/shard_map/ppermute | solution.py:114
  141.8 10.4 %collective-permute-start.26 = (bf16[128,1024]{0,1:T(8,128)(2,1)S(1)}, bf16[128,1024]{0,1:T(8,128)(2,1)S(1)}, u32[]{:S(2)}, u32[]{:S(2)}) collective-permute-start(bf16[128,1024]{0,1:T(8,128)(2,1)S(1)} %bitcast.148), channel_id=1, source_target_pairs={{4,6},{6,4},{8,10},{10,8},{12,14},{14,12},{5,7},{7,5},{9,11},{11,9... | collective-permute-start | bytes 786440 | tf_op jit(solution)/shard_map/ppermute | solution.py:106
  144.8 6.6 %collective-permute-start.33 = (bf16[128,1024]{0,1:T(8,128)(2,1)S(1)}, bf16[128,1024]{0,1:T(8,128)(2,1)S(1)}, u32[]{:S(2)}, u32[]{:S(2)}) collective-permute-start(bf16[128,1024]{0,1:T(8,128)(2,1)S(1)} %collective-permute-done.32), channel_id=1, source_target_pairs={{4,8},{6,10},{8,12},{10,14},{5,9},{7,11},{9,13},{11,15},{20,24},{2... | collective-permute-start | bytes 786440 | tf_op jit(solution)/shard_map/ppermute | solution.py:41
  145.7 7.2 %collective-permute-start.30 = (bf16[128,1024]{0,1:T(8,128)(2,1)S(1)}, bf16[128,1024]{0,1:T(8,128)(2,1)S(1)}, u32[]{:S(2)}, u32[]{:S(2)}) collective-permute-start(bf16[128,1024]{0,1:T(8,128)(2,1)S(1)} %fusion.24), channel_id=1, source_target_pairs={{8,4},{10,6},{12,8},{14,10},{9,5},{11,7},{13,9},{15,11},{24,20},{2... | collective-permute-start | bytes 786440 | tf_op jit(solution)/shard_map/ppermute | solution.py:114
  146.4 8.8 %collective-permute-start.35 = (bf16[128,1024]{0,1:T(8,128)(2,1)S(1)}, bf16[128,1024]{0,1:T(8,128)(2,1)S(1)}, u32[]{:S(2)}, u32[]{:S(2)}) collective-permute-start(bf16[128,1024]{0,1:T(8,128)(2,1)S(1)} %copy-done.6), channel_id=1, source_target_pairs={{0,2},{4,6},{8,10},{12,14},{1,3},{5,7},{9,11},{13,15},{16,18},{20,... | collective-permute-start | bytes 786440 | tf_op jit(solution)/shard_map/ppermute | solution.py:43
  149.9 14.8 %collective-permute-start.25 = (bf16[128,1024]{0,1:T(8,128)(2,1)S(1)}, bf16[128,1024]{0,1:T(8,128)(2,1)S(1)}, u32[]{:S(2)}, u32[]{:S(2)}) collective-permute-start(bf16[128,1024]{0,1:T(8,128)(2,1)S(1)} %bitcast.147), channel_id=1, source_target_pairs={{2,0},{6,4},{10,8},{14,12},{3,1},{7,5},{11,9},{15,13},{18,16},{22,... | collective-permute-start | bytes 786440 | tf_op jit(solution)/shard_map/ppermute | solution.py:103
  151.4 2.3 collective-permute-start.34
  152.2 3.9 %collective-permute-start.36 = (bf16[128,1024]{0,1:T(8,128)(2,1)S(1)}, bf16[128,1024]{0,1:T(8,128)(2,1)S(1)}, u32[]{:S(2)}, u32[]{:S(2)}) collective-permute-start(bf16[128,1024]{0,1:T(8,128)(2,1)S(1)} %collective-permute-done.32), channel_id=1, source_target_pairs={{6,4},{4,6},{10,8},{8,10},{14,12},{12,14},{7,5},{5,7},{11,9},{9,11... | collective-permute-start | bytes 786440 | tf_op jit(solution)/shard_map/ppermute | solution.py:46
  152.9 3.3 %collective-permute-start.37 = (bf16[128,1024]{0,1:T(8,128)(2,1)S(1)}, bf16[128,1024]{0,1:T(8,128)(2,1)S(1)}, u32[]{:S(2)}, u32[]{:S(2)}) collective-permute-start(bf16[128,1024]{0,1:T(8,128)(2,1)S(1)} %collective-permute-done.33), channel_id=1, source_target_pairs={{10,8},{8,10},{14,12},{12,14},{11,9},{9,11},{15,13},{13,15},{26,24... | collective-permute-start | bytes 786440 | tf_op jit(solution)/shard_map/ppermute | solution.py:46
  153.7 31.0 %collective-permute-start.31 = (bf16[128,1024]{0,1:T(8,128)(2,1)S(1)}, bf16[128,1024]{0,1:T(8,128)(2,1)S(1)}, u32[]{:S(2)}, u32[]{:S(2)}) collective-permute-start(bf16[128,1024]{0,1:T(8,128)(2,1)S(1)} %fusion.26), channel_id=1, source_target_pairs={{4,0},{6,2},{8,4},{10,6},{12,8},{14,10},{5,1},{7,3},{9,5},{11,7},{... | collective-permute-start | bytes 786440 | tf_op jit(solution)/shard_map/ppermute | solution.py:114
  155.1 1.2 collective-permute-start.38
  188.3 6.3 %collective-permute-start.42 = (bf16[128,1024]{1,0:T(8,128)(2,1)}, bf16[128,1024]{1,0:T(8,128)(2,1)}, u32[]{:S(2)}, u32[]{:S(2)}) collective-permute-start(bf16[128,1024]{1,0:T(8,128)(2,1)} %copy.73), channel_id=1, source_target_pairs={{12,14},{14,12},{13,15},{15,13},{28,30},{30,28},{29,31},{31,29}} | collective-permute-start | bytes 786440 | tf_op jit(solution)/shard_map/ppermute | solution.py:106
  190.5 20.1 %collective-permute-start.41 = (bf16[128,1024]{1,0:T(8,128)(2,1)}, bf16[128,1024]{1,0:T(8,128)(2,1)}, u32[]{:S(2)}, u32[]{:S(2)}) collective-permute-start(bf16[128,1024]{1,0:T(8,128)(2,1)} %copy.71), channel_id=1, source_target_pairs={{8,10},{10,8},{12,14},{14,12},{9,11},{11,9},{13,15},{15,13},{24,26... | collective-permute-start | bytes 786440 | tf_op jit(solution)/shard_map/ppermute | solution.py:106
  193.6 13.2 %collective-permute-start.46 = (f32[464,128]{1,0:T(8,128)}, f32[464,128]{1,0:T(8,128)}, u32[]{:S(2)}, u32[]{:S(2)}) collective-permute-start(f32[464,128]{1,0:T(8,128)} %maximum_bitcast_fusion), channel_id=1, source_target_pairs={{0,1},{1,0},{2,3},{3,2},{4,5},{5,4},{6,7},{7,6},{8,9},{9,8},{10,11... | collective-permute-start | bytes 712712 | tf_op jit(solution)/shard_map/ppermute | solution.py:19
  196.5 14.1 %collective-permute-start.43 = (bf16[128,1024]{1,0:T(8,128)(2,1)}, bf16[128,1024]{1,0:T(8,128)(2,1)}, u32[]{:S(2)}, u32[]{:S(2)}) collective-permute-start(bf16[128,1024]{1,0:T(8,128)(2,1)} %add_convert_fusion.3), channel_id=1, source_target_pairs={{12,8},{14,10},{13,9},{15,11},{28,24},{30,26},{29,25},{31,27}} | collective-permute-start | bytes 786440 | tf_op jit(solution)/shard_map/ppermute | solution.py:114
  203.3 55.7 %collective-permute-start.40 = (bf16[128,1024]{1,0:T(8,128)(2,1)}, bf16[128,1024]{1,0:T(8,128)(2,1)}, u32[]{:S(2)}, u32[]{:S(2)}) collective-permute-start(bf16[128,1024]{1,0:T(8,128)(2,1)} %copy.69), channel_id=1, source_target_pairs={{4,6},{6,4},{8,10},{10,8},{12,14},{14,12},{5,7},{7,5},{9,11},{11,9... | collective-permute-start | bytes 786440 | tf_op jit(solution)/shard_map/ppermute | solution.py:106
  205.5 66.9 %collective-permute-start.39 = (bf16[128,1024]{1,0:T(8,128)(2,1)}, bf16[128,1024]{1,0:T(8,128)(2,1)S(1)}, u32[]{:S(2)}, u32[]{:S(2)}) collective-permute-start(bf16[128,1024]{1,0:T(8,128)(2,1)} %copy.68), channel_id=1, source_target_pairs={{2,0},{6,4},{10,8},{14,12},{3,1},{7,5},{11,9},{15,13},{18,16},{22,... | collective-permute-start | bytes 786440 | tf_op jit(solution)/shard_map/ppermute | solution.py:103
  207.8 13.6 %collective-permute-start.47 = (f32[464,128]{1,0:T(8,128)S(1)}, f32[464,128]{1,0:T(8,128)S(1)}, u32[]{:S(2)}, u32[]{:S(2)}) collective-permute-start(f32[464,128]{1,0:T(8,128)S(1)} %fusion.34), channel_id=1, source_target_pairs={{0,2},{2,0},{4,6},{6,4},{8,10},{10,8},{12,14},{14,12},{1,3},{3,1},... | collective-permute-start | bytes 712712 | tf_op jit(solution)/shard_map/ppermute | solution.py:19
  211.7 47.4 %collective-permute-start.44 = (bf16[128,1024]{1,0:T(8,128)(2,1)S(1)}, bf16[128,1024]{1,0:T(8,128)(2,1)S(1)}, u32[]{:S(2)}, u32[]{:S(2)}) collective-permute-start(bf16[128,1024]{1,0:T(8,128)(2,1)S(1)} %add_convert_fusion.2), channel_id=1, source_target_pairs={{8,4},{10,6},{12,8},{14,10},{9,5},{11,7},{13,9},{15,11},{24,20},{2... | collective-permute-start | bytes 786440 | tf_op jit(solution)/shard_map/ppermute | solution.py:114
  222.4 18.0 %collective-permute-start.48 = (f32[464,128]{1,0:T(8,128)S(1)}, f32[464,128]{1,0:T(8,128)S(1)}, u32[]{:S(2)}, u32[]{:S(2)}) collective-permute-start(f32[464,128]{1,0:T(8,128)S(1)} %fusion.64), channel_id=1, source_target_pairs={{0,4},{2,6},{4,0},{6,2},{8,12},{10,14},{12,8},{14,10},{1,5},{3,7},... | collective-permute-start | bytes 712712 | tf_op jit(solution)/shard_map/ppermute | solution.py:19
  240.5 29.8 %collective-permute-start.49 = (f32[464,128]{1,0:T(8,128)S(1)}, f32[464,128]{1,0:T(8,128)S(1)}, u32[]{:S(2)}, u32[]{:S(2)}) collective-permute-start(f32[464,128]{1,0:T(8,128)S(1)} %add.274), channel_id=1, source_target_pairs={{0,8},{2,10},{4,12},{6,14},{8,0},{10,2},{12,4},{14,6},{1,9},{3,11}... | collective-permute-start | bytes 712712 | tf_op jit(solution)/shard_map/ppermute | solution.py:19
  260.8 13.4 %collective-permute-start.45 = (bf16[128,1024]{1,0:T(8,128)(2,1)}, bf16[128,1024]{1,0:T(8,128)(2,1)}, u32[]{:S(2)}, u32[]{:S(2)}) collective-permute-start(bf16[128,1024]{1,0:T(8,128)(2,1)} %add_convert_fusion.1), channel_id=1, source_target_pairs={{4,0},{6,2},{8,4},{10,6},{12,8},{14,10},{5,1},{7,3},{9,5},{11,7},{... | collective-permute-start | bytes 786440 | tf_op jit(solution)/shard_map/ppermute | solution.py:114
  (23 other events, 282.5 us)

commit v10 on v9

--- a/solution.py
+++ b/solution.py
@@ -190,8 +190,9 @@
     levels = ctx_size // 2
     row_iota = jnp.arange(tok_rows, dtype=jnp.int32)
     if use_tree:
-        key_blocks = tree_spread(own_keys, levels)
-        value_blocks = tree_spread(values, levels)
+        joined_blocks = tree_spread(jnp.concatenate([own_keys, values], 1), levels)
+        key_blocks = [block[:, :width_kv] for block in joined_blocks]
+        value_blocks = [block[:, width_kv:] for block in joined_blocks]
         owners, valid = tree_slots(ctx_index, levels)
         far = jnp.int32(1 << 30)
         upos = jnp.concatenate(

time: 277 us -> 281 us (1.014)
  starting transfers between devices: 107 us -> 78.6 us
  waiting for transfers between devices: 75.7 us -> 97.2 us
  matrix products: 29.5 us -> 33.8 us
  other arithmetic: 14.8 us -> 18.3 us
    ppermute x6 -> x3, starting transfers between devices: 27 us -> 3.47 us  [tree_spread(): lax.ppermute(held, 'ctx', [(c - 2, c) for c in range(2 * step, count)])]
    ppermute x6, waiting for transfers between devices: 21.7 us -> 44.6 us  [tree_return(): lax.ppermute(acc.astype(jnp.bfloat16), 'ctx', [(c, c - 2) for c in range(...]
    ppermute x2 -> x1, waiting for transfers between devices: 0.01 us -> 7 us  [tree_spread(): lax.ppermute(block, 'ctx', [(c - 1, c) for c in range(1, count, 2)])]
    ppermute x2 -> x1, starting transfers between devices: 7.57 us -> 2.82 us  [tree_spread(): lax.ppermute(block, 'ctx', [(c - 1, c) for c in range(1, count, 2)])]
    ppermute x9, starting transfers between devices: 34.9 us -> 30.4 us  [from_partner(): lax.ppermute(shard, axis, [(i, i ^ 1 << stride) for i in range(lax.axis_s...]
    ppermute x3, waiting for transfers between devices: 8.89 us -> 4.69 us  [tree_gather(): lax.ppermute(downs[step - 1], 'ctx', [(c ^ 1, c) for c in range(0, count...]
    convert_element_type x6, other arithmetic: 5.11 us -> 8.47 us  [tree_return(): acc.astype(jnp.bfloat16)]
    reshape x1 -> x0, local copies, waits for them, and re-layouts: 3.31 us -> none  [shards(): key_rows = all_keys.reshape(span, kv_heads, HEAD_SIZE)]
  transfers between devices with their start and end apart: 50 -> 43, of which waited for: 16 -> 13; matrix products, arithmetic and copies ran while one was open for 22% -> 26% of each run, Pallas kernels for 0% -> 0%
where the time goes in v10:
time: 281 us; the launch traced here: 279 us
  waiting for transfers between devices  97.2 us (35%)
  starting transfers between devices  78.6 us (28%)
  local copies, waits for them, and re-layouts  50.1 us (18%)
  matrix products  33.8 us (12%)
  other arithmetic  18.3 us (7%)
    ppermute x6, waiting for transfers between devices, tree_return(): lax.ppermute(acc.astype(jnp.bfloat16), 'ctx', [(c, c - 2) for c in range(...  44.6 us
    ppermute x9, starting transfers between devices, from_partner(): lax.ppermute(shard, axis, [(i, i ^ 1 << stride) for i in range(lax.axis_s...  30.4 us
    ppermute x9, waiting for transfers between devices, from_partner(): lax.ppermute(shard, axis, [(i, i ^ 1 << stride) for i in range(lax.axis_s...  23.1 us
    ppermute x3, waiting for transfers between devices, tree_gather(): lax.ppermute(down, 'ctx', [(c + 2, c) for c in range(0, count - 2 * step)])  11.8 us
    dynamic_update_slice x14, local copies, waits for them, and re-layouts, tree_gather(): whole = lax.dynamic_update_slice_in_dim(whole, piece, place, 0)  10.6 us
    unnamed x45, local copies, waits for them, and re-layouts  9.19 us
    convert_element_type x6, other arithmetic, tree_return(): acc.astype(jnp.bfloat16)  8.47 us
    ppermute x3, starting transfers between devices, tree_gather(): lax.ppermute(downs[step - 1], 'ctx', [(c ^ 1, c) for c in range(0, count...  8.22 us
  transfers between devices with their start and end apart: 43, of which 13 were waited for; matrix products, arithmetic and copies ran while one was open for 26% of the time, Pallas kernels for 0%

profile of v10, /device:TPU:0, one launch (start us, length us, event | category | flops | bytes accessed | tf_op | source)
XLA Modules:
  0.0 279.4 jit_solution(4126881655324719541)
XLA Ops:
  0.7 1.8 broadcast_in_dim.58
  3.3 4.9 %collective-permute-start.3 = (bf16[336,512]{1,0:T(8,128)(2,1)S(1)}, bf16[336,512]{1,0:T(8,128)(2,1)S(1)}, u32[]{:S(2)}, u32[]{:S(2)}) collective-permute-start(bf16[336,512]{1,0:T(8,128)(2,1)S(1)} %get-tuple-element.29), channel_id=1, source_target_pairs={{0,4},{2,6},{4,8},{6,10},{8,12},{10,14},{1,5},{3,7},{5,9},{7,11},{... | collective-permute-start | bytes 1032200 | tf_op jit(solution)/shard_map/ppermute | solution.py:60
  9.5 6.0 %collective-permute-done.3 = bf16[336,512]{1,0:T(8,128)(2,1)S(1)} collective-permute-done((bf16[336,512]{1,0:T(8,128)(2,1)S(1)}, bf16[336,512]{1,0:T(8,128)(2,1)S(1)}, u32[]{:S(2)}, u32[]{:S(2)}) %collective-permute-start.3) | collective-permute-done | bytes 344096 | tf_op jit(solution)/shard_map/ppermute | solution.py:60
  16.2 3.5 %collective-permute-done.4 = bf16[336,512]{1,0:T(8,128)(2,1)S(1)} collective-permute-done((bf16[336,512]{1,0:T(8,128)(2,1)S(1)}, bf16[336,512]{1,0:T(8,128)(2,1)S(1)}, u32[]{:S(2)}, u32[]{:S(2)}) %collective-permute-start.4) | collective-permute-done | bytes 344096 | tf_op jit(solution)/shard_map/ppermute | solution.py:61
  20.9 1.6 collective-permute-start.9
  23.2 2.4 collective-permute-start.11
  27.8 2.5 collective-permute-done.6
  34.5 5.8 %collective-permute-done.8 = bf16[336,512]{1,0:T(8,128)(2,1)S(1)} collective-permute-done((bf16[336,512]{1,0:T(8,128)(2,1)S(1)}, bf16[336,512]{1,0:T(8,128)(2,1)S(1)}, u32[]{:S(2)}, u32[]{:S(2)}) %collective-permute-start.8) | collective-permute-done | bytes 344096 | tf_op jit(solution)/shard_map/ppermute | solution.py:61
  40.4 3.0 %collective-permute-start.13 = (bf16[336,512]{1,0:T(8,128)(2,1)S(1)}, bf16[336,512]{1,0:T(8,128)(2,1)S(1)}, u32[]{:S(2)}, u32[]{:S(2)}) collective-permute-start(bf16[336,512]{1,0:T(8,128)(2,1)S(1)} %collective-permute-done.6), channel_id=1, source_target_pairs={{2,0},{0,2},{6,4},{4,6},{3,1},{1,3},{7,5},{5,7},{18,16},{16,18},{2... | collective-permute-start | bytes 1032200 | tf_op jit(solution)/shard_map/ppermute | solution.py:73
  45.6 2.8 collective-permute-start.15
  50.7 1.5 collective-permute-done.13
  53.7 3.1 %collective-permute-done.15 = bf16[336,512]{1,0:T(8,128)(2,1)S(1)} collective-permute-done((bf16[336,512]{1,0:T(8,128)(2,1)S(1)}, bf16[336,512]{1,0:T(8,128)(2,1)S(1)}, u32[]{:S(2)}, u32[]{:S(2)}) %collective-permute-start.15) | collective-permute-done | bytes 344096 | tf_op jit(solution)/shard_map/ppermute | solution.py:73
  57.6 3.2 %broadcast_in_dim.57 = bf16[2688,1024]{1,0:T(8,128)(2,1)} broadcast(bf16[]{:T(256)} %constant.74.clone.1), dimensions={} | broadcast | bytes 5505026 | tf_op jit(solution)/shard_map/broadcast_in_dim | solution.py:157
  60.8 3.8 %fusion.35 = (bf16[2688,512]{1,0:T(8,128)(2,1)S(1)}, bf16[2688,1024]{1,0:T(8,128)(2,1)}) fusion(bf16[3024,512]{1,0:T(8,128)(2,1)} %constant_dynamic-update-slice_fusion.12, bf16[2688,1024]{1,0:T(8,128)(2,1)} %broadcast_in_dim.57, s32[]{:T(128)S(6)} %select_n.156), kind=kLoop, calls=%fused_computation.124 | loop fusion | bytes 8257540 | tf_op jit(solution)/shard_map/slice | solution.py:82
  66.5 2.2 reshape_squeeze.7
  68.7 1.8 copy.57
  71.9 3.5 %constant_dynamic-update-slice_fusion.10 = bf16[2688,1024]{1,0:T(8,128)(2,1)} fusion(bf16[2688,1024]{1,0:T(8,128)(2,1)} %get-tuple-element.31, bf16[2688,512]{1,0:T(8,128)(2,1)} %collective-permute-done.16, s32[]{:T(128)S(6)} %select_n.185), kind=kLoop, calls=%fused_computation.85 | loop fusion | bytes 5505028 | tf_op jit(solution)/shard_map/dynamic_update_slice | solution.py:159
  75.5 4.3 %fusion.15 = bf16[128,1024]{0,1:T(8,128)(2,1)S(1)} fusion(f32[128,1024]{0,1:T(8,128)S(1)} %convolution_multiply_fusion.2, bf16[2688,1024]{1,0:T(8,128)(2,1)} %constant_dynamic-update-slice_fusion.10, bf16[1,128,2688]{2,1,0:T(8,128)(2,1)S(1)} %copy-done), kind=kOutput, calls=%fused_computation.28 | convolution fusion | flops 704905216 | bytes 6979584 | tf_op jit(solution)/shard_map/dot_general | solution.py:168
  82.0 2.3 collective-permute-start.1
  85.4 8.7 %collective-permute-done.1 = f32[16]{0:T(128)S(1)} collective-permute-done((f32[16]{0:T(128)S(1)}, f32[16]{0:T(128)S(1)}, u32[]{:S(2)}, u32[]{:S(2)}) %collective-permute-start.1) | collective-permute-done | bytes 96 | tf_op jit(solution)/shard_map/ppermute | solution.py:19
  94.0 2.3 collective-permute-start.2
  96.4 2.1 collective-permute-done.2
  98.5 1.5 collective-permute-start.18
  102.3 2.8 %collective-permute-start.20 = (bf16[128,2048]{0,1:T(8,128)(2,1)}, bf16[128,2048]{0,1:T(8,128)(2,1)S(1)}, u32[]{:S(2)}, u32[]{:S(2)}) collective-permute-start(bf16[128,2048]{0,1:T(8,128)(2,1)} %pad_maximum_fusion), channel_id=1, source_target_pairs={{0,2},{4,6},{8,10},{12,14},{1,3},{5,7},{9,11},{13,15},{16,18},{20,... | collective-permute-start | bytes 1572872 | tf_op jit(solution)/shard_map/ppermute | solution.py:43
  109.9 7.0 %collective-permute-done.20 = bf16[128,2048]{0,1:T(8,128)(2,1)S(1)} collective-permute-done((bf16[128,2048]{0,1:T(8,128)(2,1)}, bf16[128,2048]{0,1:T(8,128)(2,1)S(1)}, u32[]{:S(2)}, u32[]{:S(2)}) %collective-permute-start.20) | collective-permute-done | bytes 524320 | tf_op jit(solution)/shard_map/ppermute | solution.py:43
  119.0 7.7 %fusion.39 = (f32[8,2,128]{2,1,0:T(2,128)S(1)}, f32[8,2,128,1024]{2,3,1,0:T(8,128)}) fusion(pred[128,1024]{0,1:T(8,128)(4,1)S(1)} %compare_and_fusion, bf16[1024,8,128,1]{0,2,3,1:T(8,128)(2,1)S(1)} %bitcast.137, bf16[128,8,2,128]{0,3,2,1:T(8,128)(2,1)} %bitcast.142), kind=kOutput, calls=%fused_computation.128 | convolution fusion | flops 547357696 | bytes 11149312 | tf_op jit(solution)/shard_map/sub | solution.py:231
  126.7 7.1 %fusion.40 = (bf16[1024,8,128]{0,2,1:T(8,128)(2,1)S(1)}, f32[1024,8,128]{0,2,1:T(8,128)}) fusion(bf16[128,8,2,128]{3,2,1,0:T(2,128)(2,1)} %reshape_squeeze.7, f32[128]{0:T(128)S(1)} %get-tuple-element.25, f32[8,2,128,1024]{2,3,1,0:T(8,128)} %get-tuple-element.65, f32[8,2,128]{2,1,0:T(2,128)S(1)} %get-tuple-element.64), kind=kOutput, calls=%fused_computation.129 | convolution fusion | flops 544210944 | bytes 15213056 | tf_op jit(solution)/shard_map/jgtl,tjgd->ljd/dot_general | solution.py:245
  137.2 1.4 collective-permute-start.26
  140.0 1.9 fusion.1
  141.9 1.7 fusion.3
  144.7 3.5 %fusion.41 = (bf16[1024,8,128]{0,2,1:T(8,128)(2,1)S(1)}, f32[1024,8,128]{0,2,1:T(8,128)}) fusion(bf16[8,2,128,1024]{2,3,1,0:T(8,128)(2,1)S(1)} %fusion.3, bf16[128,8,2,128]{0,3,2,1:T(8,128)(2,1)S(1)} %bitcast.143), kind=kOutput, calls=%fused_computation.130 | convolution fusion | flops 537919488 | bytes 11010048 | tf_op jit(solution)/shard_map/jgtl,tjgd->ljd/dot_general | solution.py:241
  151.1 1.4 collective-permute-start.35
  152.6 1.8 fusion.24
  155.9 1.8 copy.71
  159.1 1.7 add_convert_fusion.3
  162.2 1.9 fusion.26
  164.1 1.5 collective-permute-start.31
  171.3 1.8 copy.69
  174.4 1.8 copy.68
  177.5 1.8 add_convert_fusion.2
  180.7 44.6 %collective-permute-done.31 = bf16[128,1024]{0,1:T(8,128)(2,1)} collective-permute-done((bf16[128,1024]{0,1:T(8,128)(2,1)}, bf16[128,1024]{0,1:T(8,128)(2,1)}, u32[]{:S(2)}, u32[]{:S(2)}) %collective-permute-start.31) | collective-permute-done | bytes 262176 | tf_op jit(solution)/shard_map/ppermute | solution.py:114
  232.9 3.4 %collective-permute-start.40 = (f32[464,128]{1,0:T(8,128)S(1)}, f32[464,128]{1,0:T(8,128)S(1)}, u32[]{:S(2)}, u32[]{:S(2)}) collective-permute-start(f32[464,128]{1,0:T(8,128)S(1)} %fusion.34), channel_id=1, source_target_pairs={{0,2},{2,0},{4,6},{6,4},{8,10},{10,8},{12,14},{14,12},{1,3},{3,1},... | collective-permute-start | bytes 712712 | tf_op jit(solution)/shard_map/ppermute | solution.py:19
  237.5 5.2 %collective-permute-done.40 = f32[464,128]{1,0:T(8,128)S(1)} collective-permute-done((f32[464,128]{1,0:T(8,128)S(1)}, f32[464,128]{1,0:T(8,128)S(1)}, u32[]{:S(2)}, u32[]{:S(2)}) %collective-permute-start.40) | collective-permute-done | bytes 237600 | tf_op jit(solution)/shard_map/ppermute | solution.py:19
  242.8 17.6 %collective-permute-start.41 = (f32[464,128]{1,0:T(8,128)S(1)}, f32[464,128]{1,0:T(8,128)S(1)}, u32[]{:S(2)}, u32[]{:S(2)}) collective-permute-start(f32[464,128]{1,0:T(8,128)S(1)} %fusion.64), channel_id=1, source_target_pairs={{0,4},{2,6},{4,0},{6,2},{8,12},{10,14},{12,8},{14,10},{1,5},{3,7},... | collective-permute-start | bytes 712712 | tf_op jit(solution)/shard_map/ppermute | solution.py:19
  260.4 5.3 %fusion.11 = bf16[1,128,2688]{2,1,0:T(8,128)(2,1)} fusion(f32[128,2688]{1,0:T(8,128)S(1)} %convolution_multiply_fusion, bf16[128,1024]{0,1:T(8,128)(2,1)S(1)} %fusion.27, bf16[2688,1024]{1,0:T(8,128)(2,1)} %constant_dynamic-update-slice_fusion.10), kind=kOutput, calls=%fused_computation.19 | convolution fusion | flops 705331200 | bytes 7831552 | tf_op jit(solution)/shard_map/tk,dk->td/dot_general | solution.py:270
  265.8 3.6 %collective-permute-start.42 = (f32[464,128]{1,0:T(8,128)S(1)}, f32[464,128]{1,0:T(8,128)S(1)}, u32[]{:S(2)}, u32[]{:S(2)}) collective-permute-start(f32[464,128]{1,0:T(8,128)S(1)} %add.274), channel_id=1, source_target_pairs={{0,8},{2,10},{4,12},{6,14},{8,0},{10,2},{12,4},{14,6},{1,9},{3,11}... | collective-permute-start | bytes 712712 | tf_op jit(solution)/shard_map/ppermute | solution.py:19
  269.3 1.8 fusion.31
  271.1 6.2 %collective-permute-done.42 = f32[464,128]{1,0:T(8,128)S(1)} collective-permute-done((f32[464,128]{1,0:T(8,128)S(1)}, f32[464,128]{1,0:T(8,128)S(1)}, u32[]{:S(2)}, u32[]{:S(2)}) %collective-permute-start.42) | collective-permute-done | bytes 237600 | tf_op jit(solution)/shard_map/ppermute | solution.py:19
  (176 shorter events, 67.2 us)
Async XLA Ops:
  0.6 69.9 %copy-start = (bf16[1,128,2688]{2,1,0:T(8,128)(2,1)S(1)}, bf16[1,128,2688]{2,1,0:T(8,128)(2,1)}, u32[]{:S(2)}) copy-start(bf16[1,128,2688]{2,1,0:T(8,128)(2,1)} %param.10) | copy-start | bytes 2064388
  3.3 12.2 %collective-permute-start.3 = (bf16[336,512]{1,0:T(8,128)(2,1)S(1)}, bf16[336,512]{1,0:T(8,128)(2,1)S(1)}, u32[]{:S(2)}, u32[]{:S(2)}) collective-permute-start(bf16[336,512]{1,0:T(8,128)(2,1)S(1)} %get-tuple-element.29), channel_id=1, source_target_pairs={{0,4},{2,6},{4,8},{6,10},{8,12},{10,14},{1,5},{3,7},{5,9},{7,11},{... | collective-permute-start | bytes 1032200 | tf_op jit(solution)/shard_map/ppermute | solution.py:60
  8.2 11.4 %collective-permute-start.4 = (bf16[336,512]{1,0:T(8,128)(2,1)S(1)}, bf16[336,512]{1,0:T(8,128)(2,1)S(1)}, u32[]{:S(2)}, u32[]{:S(2)}) collective-permute-start(bf16[336,512]{1,0:T(8,128)(2,1)S(1)} %get-tuple-element.29), channel_id=1, source_target_pairs={{4,0},{6,2},{8,4},{10,6},{12,8},{14,10},{5,1},{7,3},{9,5},{11,7},{... | collective-permute-start | bytes 1032200 | tf_op jit(solution)/shard_map/ppermute | solution.py:61
  15.5 10.9 %collective-permute-start.5 = (bf16[336,512]{1,0:T(8,128)(2,1)S(1)}, bf16[336,512]{1,0:T(8,128)(2,1)S(1)}, u32[]{:S(2)}, u32[]{:S(2)}) collective-permute-start(bf16[336,512]{1,0:T(8,128)(2,1)S(1)} %collective-permute-done.3), channel_id=1, source_target_pairs={{4,8},{6,10},{8,12},{10,14},{5,9},{7,11},{9,13},{11,15},{20,24},{2... | collective-permute-start | bytes 1032200 | tf_op jit(solution)/shard_map/ppermute | solution.py:60
  19.6 10.7 %collective-permute-start.6 = (bf16[336,512]{1,0:T(8,128)(2,1)S(1)}, bf16[336,512]{1,0:T(8,128)(2,1)S(1)}, u32[]{:S(2)}, u32[]{:S(2)}) collective-permute-start(bf16[336,512]{1,0:T(8,128)(2,1)S(1)} %collective-permute-done.4), channel_id=1, source_target_pairs={{4,0},{6,2},{8,4},{10,6},{5,1},{7,3},{9,5},{11,7},{20,16},{22,18},... | collective-permute-start | bytes 1032200 | tf_op jit(solution)/shard_map/ppermute | solution.py:61
  20.9 23.3 %collective-permute-start.9 = (bf16[336,512]{1,0:T(8,128)(2,1)S(1)}, bf16[336,512]{1,0:T(8,128)(2,1)S(1)}, u32[]{:S(2)}, u32[]{:S(2)}) collective-permute-start(bf16[336,512]{1,0:T(8,128)(2,1)S(1)} %get-tuple-element.29), channel_id=1, source_target_pairs={{2,0},{0,2},{6,4},{4,6},{10,8},{8,10},{14,12},{12,14},{3,1},{1,3},... | collective-permute-start | bytes 1032200 | tf_op jit(solution)/shard_map/ppermute | solution.py:67
  22.5 23.1 %collective-permute-start.10 = (bf16[336,512]{1,0:T(8,128)(2,1)S(1)}, bf16[336,512]{1,0:T(8,128)(2,1)S(1)}, u32[]{:S(2)}, u32[]{:S(2)}) collective-permute-start(bf16[336,512]{1,0:T(8,128)(2,1)S(1)} %collective-permute-done.3), channel_id=1, source_target_pairs={{6,4},{4,6},{10,8},{8,10},{14,12},{12,14},{7,5},{5,7},{11,9},{9,11... | collective-permute-start | bytes 1032200 | tf_op jit(solution)/shard_map/ppermute | solution.py:71
  23.2 26.0 %collective-permute-start.11 = (bf16[336,512]{1,0:T(8,128)(2,1)S(1)}, bf16[336,512]{1,0:T(8,128)(2,1)S(1)}, u32[]{:S(2)}, u32[]{:S(2)}) collective-permute-start(bf16[336,512]{1,0:T(8,128)(2,1)S(1)} %collective-permute-done.4), channel_id=1, source_target_pairs={{2,0},{0,2},{6,4},{4,6},{10,8},{8,10},{3,1},{1,3},{7,5},{5,7},{11,... | collective-permute-start | bytes 1032200 | tf_op jit(solution)/shard_map/ppermute | solution.py:73
  26.3 6.8 %collective-permute-start.7 = (bf16[336,512]{1,0:T(8,128)(2,1)S(1)}, bf16[336,512]{1,0:T(8,128)(2,1)S(1)}, u32[]{:S(2)}, u32[]{:S(2)}) collective-permute-start(bf16[336,512]{1,0:T(8,128)(2,1)S(1)} %collective-permute-done.5), channel_id=1, source_target_pairs={{8,12},{10,14},{9,13},{11,15},{24,28},{26,30},{25,29},{27,31}} | collective-permute-start | bytes 1032200 | tf_op jit(solution)/shard_map/ppermute | solution.py:60
  30.3 10.1 %collective-permute-start.8 = (bf16[336,512]{1,0:T(8,128)(2,1)S(1)}, bf16[336,512]{1,0:T(8,128)(2,1)S(1)}, u32[]{:S(2)}, u32[]{:S(2)}) collective-permute-start(bf16[336,512]{1,0:T(8,128)(2,1)S(1)} %collective-permute-done.6), channel_id=1, source_target_pairs={{4,0},{6,2},{5,1},{7,3},{20,16},{22,18},{21,17},{23,19}} | collective-permute-start | bytes 1032200 | tf_op jit(solution)/shard_map/ppermute | solution.py:61
  33.1 16.8 %collective-permute-start.12 = (bf16[336,512]{1,0:T(8,128)(2,1)S(1)}, bf16[336,512]{1,0:T(8,128)(2,1)S(1)}, u32[]{:S(2)}, u32[]{:S(2)}) collective-permute-start(bf16[336,512]{1,0:T(8,128)(2,1)S(1)} %collective-permute-done.5), channel_id=1, source_target_pairs={{10,8},{8,10},{14,12},{12,14},{11,9},{9,11},{15,13},{13,15},{26,24... | collective-permute-start | bytes 1032200 | tf_op jit(solution)/shard_map/ppermute | solution.py:71
  40.4 11.9 %collective-permute-start.13 = (bf16[336,512]{1,0:T(8,128)(2,1)S(1)}, bf16[336,512]{1,0:T(8,128)(2,1)S(1)}, u32[]{:S(2)}, u32[]{:S(2)}) collective-permute-start(bf16[336,512]{1,0:T(8,128)(2,1)S(1)} %collective-permute-done.6), channel_id=1, source_target_pairs={{2,0},{0,2},{6,4},{4,6},{3,1},{1,3},{7,5},{5,7},{18,16},{16,18},{2... | collective-permute-start | bytes 1032200 | tf_op jit(solution)/shard_map/ppermute | solution.py:73
  44.2 8.8 %collective-permute-start.14 = (bf16[336,512]{1,0:T(8,128)(2,1)S(1)}, bf16[336,512]{1,0:T(8,128)(2,1)S(1)}, u32[]{:S(2)}, u32[]{:S(2)}) collective-permute-start(bf16[336,512]{1,0:T(8,128)(2,1)S(1)} %collective-permute-done.7), channel_id=1, source_target_pairs={{14,12},{12,14},{15,13},{13,15},{30,28},{28,30},{31,29},{29,31}} | collective-permute-start | bytes 1032200 | tf_op jit(solution)/shard_map/ppermute | solution.py:71
  45.6 11.2 %collective-permute-start.15 = (bf16[336,512]{1,0:T(8,128)(2,1)S(1)}, bf16[336,512]{1,0:T(8,128)(2,1)S(1)}, u32[]{:S(2)}, u32[]{:S(2)}) collective-permute-start(bf16[336,512]{1,0:T(8,128)(2,1)S(1)} %collective-permute-done.8), channel_id=1, source_target_pairs={{2,0},{0,2},{3,1},{1,3},{18,16},{16,18},{19,17},{17,19}} | collective-permute-start | bytes 1032200 | tf_op jit(solution)/shard_map/ppermute | solution.py:73
  60.8 9.8 %copy-start.9 = (bf16[2688,16]{0,1:T(8,128)(2,1)S(1)}, bf16[2688,16]{0,1:T(8,128)(2,1)}, u32[]{:S(2)}) copy-start(bf16[2688,16]{0,1:T(8,128)(2,1)} %param.14) | copy-start | bytes 258052
  64.6 7.4 %collective-permute-start.16 = (bf16[2688,512]{1,0:T(8,128)(2,1)S(1)}, bf16[2688,512]{1,0:T(8,128)(2,1)}, u32[]{:S(2)}, u32[]{:S(2)}) collective-permute-start(bf16[2688,512]{1,0:T(8,128)(2,1)S(1)} %get-tuple-element.30), channel_id=1, source_target_pairs={{0,1},{1,0},{2,3},{3,2},{4,5},{5,4},{6,7},{7,6},{8,9},{9,8},{10,11... | collective-permute-start | bytes 8257544 | tf_op jit(solution)/shard_map/ppermute | solution.py:19
  65.3 16.6 %collective-permute-start = (f32[16]{0:T(128)}, f32[16]{0:T(128)S(1)}, u32[]{:S(2)}, u32[]{:S(2)}) collective-permute-start(f32[16]{0:T(128)} %pad_maximum_fusion.1), channel_id=1, source_target_pairs={{0,2},{2,0},{4,6},{6,4},{8,10},{10,8},{12,14},{14,12},{1,3},{3,1},... | collective-permute-start | bytes 200 | tf_op jit(solution)/shard_map/ppermute | solution.py:19
  80.6 17.9 %collective-permute-start.17 = (bf16[128,2048]{0,1:T(8,128)(2,1)}, bf16[128,2048]{0,1:T(8,128)(2,1)S(1)}, u32[]{:S(2)}, u32[]{:S(2)}) collective-permute-start(bf16[128,2048]{0,1:T(8,128)(2,1)} %pad_maximum_fusion), channel_id=1, source_target_pairs={{0,4},{2,6},{4,8},{6,10},{8,12},{10,14},{1,5},{3,7},{5,9},{7,11},{... | collective-permute-start | bytes 1572872 | tf_op jit(solution)/shard_map/ppermute | solution.py:41
  82.0 12.0 %collective-permute-start.1 = (f32[16]{0:T(128)S(1)}, f32[16]{0:T(128)S(1)}, u32[]{:S(2)}, u32[]{:S(2)}) collective-permute-start(f32[16]{0:T(128)S(1)} %fusion.65), channel_id=1, source_target_pairs={{0,4},{2,6},{4,0},{6,2},{8,12},{10,14},{12,8},{14,10},{1,5},{3,7},... | collective-permute-start | bytes 200 | tf_op jit(solution)/shard_map/ppermute | solution.py:19
  94.0 4.4 %collective-permute-start.2 = (f32[16]{0:T(128)S(1)}, f32[16]{0:T(128)S(1)}, u32[]{:S(2)}, u32[]{:S(2)}) collective-permute-start(f32[16]{0:T(128)S(1)} %add.231), channel_id=1, source_target_pairs={{0,8},{2,10},{4,12},{6,14},{8,0},{10,2},{12,4},{14,6},{1,9},{3,11}... | collective-permute-start | bytes 200 | tf_op jit(solution)/shard_map/ppermute | solution.py:19
  98.5 2.8 %collective-permute-start.18 = (bf16[128,2048]{0,1:T(8,128)(2,1)S(1)}, bf16[128,2048]{0,1:T(8,128)(2,1)}, u32[]{:S(2)}, u32[]{:S(2)}) collective-permute-start(bf16[128,2048]{0,1:T(8,128)(2,1)S(1)} %collective-permute-done.17), channel_id=1, source_target_pairs={{4,8},{6,10},{8,12},{10,14},{5,9},{7,11},{9,13},{11,15},{20,24},{2... | collective-permute-start | bytes 1572872 | tf_op jit(solution)/shard_map/ppermute | solution.py:41
  100.0 1.1 collective-permute-start.24
  101.3 7.5 %collective-permute-start.19 = (bf16[128,2048]{0,1:T(8,128)(2,1)}, bf16[128,2048]{0,1:T(8,128)(2,1)S(1)}, u32[]{:S(2)}, u32[]{:S(2)}) collective-permute-start(bf16[128,2048]{0,1:T(8,128)(2,1)} %collective-permute-done.18), channel_id=1, source_target_pairs={{8,12},{10,14},{9,13},{11,15},{24,28},{26,30},{25,29},{27,31}} | collective-permute-start | bytes 1572872 | tf_op jit(solution)/shard_map/ppermute | solution.py:41
  102.3 14.6 %collective-permute-start.20 = (bf16[128,2048]{0,1:T(8,128)(2,1)}, bf16[128,2048]{0,1:T(8,128)(2,1)S(1)}, u32[]{:S(2)}, u32[]{:S(2)}) collective-permute-start(bf16[128,2048]{0,1:T(8,128)(2,1)} %pad_maximum_fusion), channel_id=1, source_target_pairs={{0,2},{4,6},{8,10},{12,14},{1,3},{5,7},{9,11},{13,15},{16,18},{20,... | collective-permute-start | bytes 1572872 | tf_op jit(solution)/shard_map/ppermute | solution.py:43
  106.2 10.9 %collective-permute-start.21 = (bf16[128,2048]{0,1:T(8,128)(2,1)}, bf16[128,2048]{0,1:T(8,128)(2,1)S(1)}, u32[]{:S(2)}, u32[]{:S(2)}) collective-permute-start(bf16[128,2048]{0,1:T(8,128)(2,1)} %copy-done.8), channel_id=1, source_target_pairs={{6,4},{4,6},{10,8},{8,10},{14,12},{12,14},{7,5},{5,7},{11,9},{9,11... | collective-permute-start | bytes 1572872 | tf_op jit(solution)/shard_map/ppermute | solution.py:46
  106.9 10.4 %collective-permute-start.22 = (bf16[128,2048]{0,1:T(8,128)(2,1)}, bf16[128,2048]{0,1:T(8,128)(2,1)S(1)}, u32[]{:S(2)}, u32[]{:S(2)}) collective-permute-start(bf16[128,2048]{0,1:T(8,128)(2,1)} %collective-permute-done.18), channel_id=1, source_target_pairs={{10,8},{8,10},{14,12},{12,14},{11,9},{9,11},{15,13},{13,15},{26,24... | collective-permute-start | bytes 1572872 | tf_op jit(solution)/shard_map/ppermute | solution.py:46
  108.8 8.6 %collective-permute-start.23 = (bf16[128,2048]{0,1:T(8,128)(2,1)S(1)}, bf16[128,2048]{0,1:T(8,128)(2,1)S(1)}, u32[]{:S(2)}, u32[]{:S(2)}) collective-permute-start(bf16[128,2048]{0,1:T(8,128)(2,1)S(1)} %collective-permute-done.19), channel_id=1, source_target_pairs={{14,12},{12,14},{15,13},{13,15},{30,28},{28,30},{31,29},{29,31}} | collective-permute-start | bytes 1572872 | tf_op jit(solution)/shard_map/ppermute | solution.py:46
  126.7 13.2 %copy-start.1 = (f32[8,2,128,1024]{2,3,1,0:T(8,128)S(1)}, f32[8,2,128,1024]{2,3,1,0:T(8,128)}, u32[]{:S(2)}) copy-start(f32[8,2,128,1024]{2,3,1,0:T(8,128)} %get-tuple-element.65) | copy-start | bytes 25165828
  135.0 13.2 %collective-permute-start.28 = (bf16[128,1024]{0,1:T(8,128)(2,1)S(1)}, bf16[128,1024]{0,1:T(8,128)(2,1)S(1)}, u32[]{:S(2)}, u32[]{:S(2)}) collective-permute-start(bf16[128,1024]{0,1:T(8,128)(2,1)S(1)} %bitcast.151), channel_id=1, source_target_pairs={{12,14},{14,12},{13,15},{15,13},{28,30},{30,28},{29,31},{31,29}} | collective-permute-start | bytes 786440 | tf_op jit(solution)/shard_map/ppermute | solution.py:106
  135.8 16.7 %collective-permute-start.27 = (bf16[128,1024]{0,1:T(8,128)(2,1)}, bf16[128,1024]{0,1:T(8,128)(2,1)}, u32[]{:S(2)}, u32[]{:S(2)}) collective-permute-start(bf16[128,1024]{0,1:T(8,128)(2,1)} %bitcast.19), channel_id=1, source_target_pairs={{8,10},{10,8},{12,14},{14,12},{9,11},{11,9},{13,15},{15,13},{24,26... | collective-permute-start | bytes 786440 | tf_op jit(solution)/shard_map/ppermute | solution.py:106
  137.2 25.0 %collective-permute-start.26 = (bf16[128,1024]{0,1:T(8,128)(2,1)}, bf16[128,1024]{0,1:T(8,128)(2,1)}, u32[]{:S(2)}, u32[]{:S(2)}) collective-permute-start(bf16[128,1024]{0,1:T(8,128)(2,1)} %bitcast.17), channel_id=1, source_target_pairs={{4,6},{6,4},{8,10},{10,8},{12,14},{14,12},{5,7},{7,5},{9,11},{11,9... | collective-permute-start | bytes 786440 | tf_op jit(solution)/shard_map/ppermute | solution.py:106
  138.6 42.2 %collective-permute-start.25 = (bf16[128,1024]{0,1:T(8,128)(2,1)}, bf16[128,1024]{0,1:T(8,128)(2,1)}, u32[]{:S(2)}, u32[]{:S(2)}) collective-permute-start(bf16[128,1024]{0,1:T(8,128)(2,1)} %bitcast.15), channel_id=1, source_target_pairs={{2,0},{6,4},{10,8},{14,12},{3,1},{7,5},{11,9},{15,13},{18,16},{22,... | collective-permute-start | bytes 786440 | tf_op jit(solution)/shard_map/ppermute | solution.py:103
  148.3 4.3 %collective-permute-start.29 = (bf16[128,1024]{0,1:T(8,128)(2,1)S(1)}, bf16[128,1024]{0,1:T(8,128)(2,1)S(1)}, u32[]{:S(2)}, u32[]{:S(2)}) collective-permute-start(bf16[128,1024]{0,1:T(8,128)(2,1)S(1)} %fusion.22), channel_id=1, source_target_pairs={{12,8},{14,10},{13,9},{15,11},{28,24},{30,26},{29,25},{31,27}} | collective-permute-start | bytes 786440 | tf_op jit(solution)/shard_map/ppermute | solution.py:114
  151.1 8.0 %collective-permute-start.35 = (bf16[128,1024]{1,0:T(8,128)(2,1)}, bf16[128,1024]{1,0:T(8,128)(2,1)}, u32[]{:S(2)}, u32[]{:S(2)}) collective-permute-start(bf16[128,1024]{1,0:T(8,128)(2,1)} %copy.73), channel_id=1, source_target_pairs={{12,14},{14,12},{13,15},{15,13},{28,30},{30,28},{29,31},{31,29}} | collective-permute-start | bytes 786440 | tf_op jit(solution)/shard_map/ppermute | solution.py:106
  154.3 7.9 %collective-permute-start.30 = (bf16[128,1024]{0,1:T(8,128)(2,1)}, bf16[128,1024]{0,1:T(8,128)(2,1)}, u32[]{:S(2)}, u32[]{:S(2)}) collective-permute-start(bf16[128,1024]{0,1:T(8,128)(2,1)} %fusion.24), channel_id=1, source_target_pairs={{8,4},{10,6},{12,8},{14,10},{9,5},{11,7},{13,9},{15,11},{24,20},{2... | collective-permute-start | bytes 786440 | tf_op jit(solution)/shard_map/ppermute | solution.py:114
  157.7 18.5 %collective-permute-start.34 = (bf16[128,1024]{1,0:T(8,128)(2,1)}, bf16[128,1024]{1,0:T(8,128)(2,1)}, u32[]{:S(2)}, u32[]{:S(2)}) collective-permute-start(bf16[128,1024]{1,0:T(8,128)(2,1)} %copy.71), channel_id=1, source_target_pairs={{8,10},{10,8},{12,14},{14,12},{9,11},{11,9},{13,15},{15,13},{24,26... | collective-permute-start | bytes 786440 | tf_op jit(solution)/shard_map/ppermute | solution.py:106
  160.8 16.7 %collective-permute-start.36 = (bf16[128,1024]{1,0:T(8,128)(2,1)}, bf16[128,1024]{1,0:T(8,128)(2,1)}, u32[]{:S(2)}, u32[]{:S(2)}) collective-permute-start(bf16[128,1024]{1,0:T(8,128)(2,1)} %add_convert_fusion.3), channel_id=1, source_target_pairs={{12,8},{14,10},{13,9},{15,11},{28,24},{30,26},{29,25},{31,27}} | collective-permute-start | bytes 786440 | tf_op jit(solution)/shard_map/ppermute | solution.py:114
  164.1 61.2 %collective-permute-start.31 = (bf16[128,1024]{0,1:T(8,128)(2,1)}, bf16[128,1024]{0,1:T(8,128)(2,1)}, u32[]{:S(2)}, u32[]{:S(2)}) collective-permute-start(bf16[128,1024]{0,1:T(8,128)(2,1)} %fusion.26), channel_id=1, source_target_pairs={{4,0},{6,2},{8,4},{10,6},{12,8},{14,10},{5,1},{7,3},{9,5},{11,7},{... | collective-permute-start | bytes 786440 | tf_op jit(solution)/shard_map/ppermute | solution.py:114
  169.9 56.6 %copy-start.11 = (bf16[16,1024]{1,0:T(8,128)(2,1)S(1)}, bf16[16,1024]{1,0:T(8,128)(2,1)}, u32[]{:S(2)}) copy-start(bf16[16,1024]{1,0:T(8,128)(2,1)} %param.15) | copy-start | bytes 98308
  173.1 56.4 %collective-permute-start.33 = (bf16[128,1024]{1,0:T(8,128)(2,1)}, bf16[128,1024]{1,0:T(8,128)(2,1)}, u32[]{:S(2)}, u32[]{:S(2)}) collective-permute-start(bf16[128,1024]{1,0:T(8,128)(2,1)} %copy.69), channel_id=1, source_target_pairs={{4,6},{6,4},{8,10},{10,8},{12,14},{14,12},{5,7},{7,5},{9,11},{11,9... | collective-permute-start | bytes 786440 | tf_op jit(solution)/shard_map/ppermute | solution.py:106
  176.2 93.1 %collective-permute-start.32 = (bf16[128,1024]{1,0:T(8,128)(2,1)}, bf16[128,1024]{1,0:T(8,128)(2,1)}, u32[]{:S(2)}, u32[]{:S(2)}) collective-permute-start(bf16[128,1024]{1,0:T(8,128)(2,1)} %copy.68), channel_id=1, source_target_pairs={{2,0},{6,4},{10,8},{14,12},{3,1},{7,5},{11,9},{15,13},{18,16},{22,... | collective-permute-start | bytes 786440 | tf_op jit(solution)/shard_map/ppermute | solution.py:103
  179.4 50.2 %collective-permute-start.37 = (bf16[128,1024]{1,0:T(8,128)(2,1)}, bf16[128,1024]{1,0:T(8,128)(2,1)}, u32[]{:S(2)}, u32[]{:S(2)}) collective-permute-start(bf16[128,1024]{1,0:T(8,128)(2,1)} %add_convert_fusion.2), channel_id=1, source_target_pairs={{8,4},{10,6},{12,8},{14,10},{9,5},{11,7},{13,9},{15,11},{24,20},{2... | collective-permute-start | bytes 786440 | tf_op jit(solution)/shard_map/ppermute | solution.py:114
  228.5 14.2 %copy-start.5 = (f32[2,8,8,128]{3,1,2,0:T(8,128)S(1)}, f32[2,8,8,128]{3,1,2,0:T(8,128)}, u32[]{:S(2)}) copy-start(f32[2,8,8,128]{3,1,2,0:T(8,128)} %copy.93) | copy-start | bytes 196612
  229.4 2.5 collective-permute-start.39
  230.7 38.6 %collective-permute-start.38 = (bf16[128,1024]{1,0:T(8,128)(2,1)S(1)}, bf16[128,1024]{1,0:T(8,128)(2,1)S(1)}, u32[]{:S(2)}, u32[]{:S(2)}) collective-permute-start(bf16[128,1024]{1,0:T(8,128)(2,1)S(1)} %add_convert_fusion.1), channel_id=1, source_target_pairs={{4,0},{6,2},{8,4},{10,6},{12,8},{14,10},{5,1},{7,3},{9,5},{11,7},{... | collective-permute-start | bytes 786440 | tf_op jit(solution)/shard_map/ppermute | solution.py:114
  232.9 9.8 %collective-permute-start.40 = (f32[464,128]{1,0:T(8,128)S(1)}, f32[464,128]{1,0:T(8,128)S(1)}, u32[]{:S(2)}, u32[]{:S(2)}) collective-permute-start(f32[464,128]{1,0:T(8,128)S(1)} %fusion.34), channel_id=1, source_target_pairs={{0,2},{2,0},{4,6},{6,4},{8,10},{10,8},{12,14},{14,12},{1,3},{3,1},... | collective-permute-start | bytes 712712 | tf_op jit(solution)/shard_map/ppermute | solution.py:19
  242.8 22.9 %collective-permute-start.41 = (f32[464,128]{1,0:T(8,128)S(1)}, f32[464,128]{1,0:T(8,128)S(1)}, u32[]{:S(2)}, u32[]{:S(2)}) collective-permute-start(f32[464,128]{1,0:T(8,128)S(1)} %fusion.64), channel_id=1, source_target_pairs={{0,4},{2,6},{4,0},{6,2},{8,12},{10,14},{12,8},{14,10},{1,5},{3,7},... | collective-permute-start | bytes 712712 | tf_op jit(solution)/shard_map/ppermute | solution.py:19
  265.8 11.5 %collective-permute-start.42 = (f32[464,128]{1,0:T(8,128)S(1)}, f32[464,128]{1,0:T(8,128)S(1)}, u32[]{:S(2)}, u32[]{:S(2)}) collective-permute-start(f32[464,128]{1,0:T(8,128)S(1)} %add.274), channel_id=1, source_target_pairs={{0,8},{2,10},{4,12},{6,14},{8,0},{10,2},{12,4},{14,6},{1,9},{3,11}... | collective-permute-start | bytes 712712 | tf_op jit(solution)/shard_map/ppermute | solution.py:19
  (12 other events, 49.1 us)

commit v11 on v9

--- a/solution.py
+++ b/solution.py
@@ -106,16 +106,12 @@
             lax.ppermute(crossed[step], "ctx", [(c, c ^ 1) for c in range(2 * step, count)])
         )
     total = back[0].astype(jnp.float32)
-    carry = None
-    for step in range(levels - 1, 0, -1):
+    for step in range(1, levels):
         acc = climbed[step - 1].astype(jnp.float32) + back[step].astype(jnp.float32)
-        if carry is not None:
-            acc = acc + carry.astype(jnp.float32)
-        carry = lax.ppermute(
-            acc.astype(jnp.bfloat16), "ctx", [(c, c - 2) for c in range(2 * step, count)]
-        )
-    if carry is not None:
-        total = total + carry.astype(jnp.float32)
+        home = lax.ppermute(
+            acc.astype(jnp.bfloat16), "ctx", [(c, c - 2 * step) for c in range(2 * step, count)]
+        )
+        total = total + home.astype(jnp.float32)
     return total
 
 

time: 277 us -> 290 us (1.047); the launches traced: 276 us -> 284 us
  local copies, waits for them, and re-layouts: 47.5 us -> 60.5 us
  starting transfers between devices: 107 us -> 95.5 us
  matrix products: 29.5 us -> 36.4 us
  waiting for transfers between devices: 75.7 us -> 70.4 us
  other arithmetic: 14.8 us -> 19.8 us
    ppermute x9, starting transfers between devices: 34.9 us -> 19 us  [from_partner(): lax.ppermute(shard, axis, [(i, i ^ 1 << stride) for i in range(lax.axis_s...]
    ppermute x9, waiting for transfers between devices: 24 us -> 18.1 us  [from_partner(): lax.ppermute(shard, axis, [(i, i ^ 1 << stride) for i in range(lax.axis_s...]
    unnamed x60 -> x66, local copies, waits for them, and re-layouts: 6.94 us -> 12 us
    ppermute x6, waiting for transfers between devices: 21.7 us -> 25.3 us  [tree_return(): lax.ppermute(acc.astype(jnp.bfloat16), 'ctx', [(c, c - 2 * step) for c in...]
    dot_general x1, matrix products: 1.93 us -> 5.08 us  [shards(): jnp.einsum('tjgd,ljd->jgtl', grad_rows, value_rows, preferred_element_typ...]
  transfers between devices with their start and end apart: 50 -> 50, of which waited for: 16 -> 14; matrix products, arithmetic and copies ran while one was open for 22% -> 31% of each run, Pallas kernels for 0% -> 0%
where the time goes in v11:
time: 290 us; the launch traced here: 284 us
  starting transfers between devices  95.5 us (33%)
  waiting for transfers between devices  70.4 us (24%)
  local copies, waits for them, and re-layouts  60.5 us (21%)
  matrix products  36.4 us (13%)
  other arithmetic  19.8 us (7%)
    ppermute x6, starting transfers between devices, tree_spread(): lax.ppermute(held, 'ctx', [(c - 2, c) for c in range(2 * step, count)])  27.8 us
    ppermute x6, waiting for transfers between devices, tree_return(): lax.ppermute(acc.astype(jnp.bfloat16), 'ctx', [(c, c - 2 * step) for c in...  25.3 us
    ppermute x9, starting transfers between devices, from_partner(): lax.ppermute(shard, axis, [(i, i ^ 1 << stride) for i in range(lax.axis_s...  19 us
    ppermute x9, waiting for transfers between devices, from_partner(): lax.ppermute(shard, axis, [(i, i ^ 1 << stride) for i in range(lax.axis_s...  18.1 us
    ppermute x3, waiting for transfers between devices, tree_gather(): lax.ppermute(down, 'ctx', [(c + 2, c) for c in range(0, count - 2 * step)])  14.8 us
    unnamed x66, local copies, waits for them, and re-layouts  12 us
    dynamic_update_slice x14, local copies, waits for them, and re-layouts, tree_gather(): whole = lax.dynamic_update_slice_in_dim(whole, piece, place, 0)  10.8 us
    ppermute x2, starting transfers between devices, tree_spread(): lax.ppermute(block, 'ctx', [(c - 1, c) for c in range(1, count, 2)])  9.38 us
  transfers between devices with their start and end apart: 50, of which 14 were waited for; matrix products, arithmetic and copies ran while one was open for 31% of the time, Pallas kernels for 0%

profile of v11, /device:TPU:0, one launch (start us, length us, event | category | flops | bytes accessed | tf_op | source)
XLA Modules:
  0.0 284.4 jit_solution(16108951200837122906)
XLA Ops:
  0.7 5.8 %collective-permute-start.3 = (bf16[128,1024]{1,0:T(8,128)(2,1)}, bf16[128,1024]{1,0:T(8,128)(2,1)}, u32[]{:S(2)}, u32[]{:S(2)}) collective-permute-start(bf16[128,1024]{1,0:T(8,128)(2,1)} %bitcast.153), channel_id=1, source_target_pairs={{0,4},{2,6},{4,8},{6,10},{8,12},{10,14},{1,5},{3,7},{5,9},{7,11},{... | collective-permute-start | bytes 786440 | tf_op jit(solution)/shard_map/ppermute | solution.py:41
  6.5 4.1 %collective-permute-start.6 = (bf16[128,1024]{1,0:T(8,128)(2,1)}, bf16[128,1024]{1,0:T(8,128)(2,1)}, u32[]{:S(2)}, u32[]{:S(2)}) collective-permute-start(bf16[128,1024]{1,0:T(8,128)(2,1)} %bitcast.154), channel_id=1, source_target_pairs={{0,2},{4,6},{8,10},{12,14},{1,3},{5,7},{9,11},{13,15},{16,18},{20,... | collective-permute-start | bytes 786440 | tf_op jit(solution)/shard_map/ppermute | solution.py:43
  10.6 1.8 broadcast_in_dim.58
  13.2 2.8 collective-permute-start.10
  19.5 3.2 %collective-permute-done.10 = bf16[336,512]{1,0:T(8,128)(2,1)S(1)} collective-permute-done((bf16[336,512]{1,0:T(8,128)(2,1)S(1)}, bf16[336,512]{1,0:T(8,128)(2,1)S(1)}, u32[]{:S(2)}, u32[]{:S(2)}) %collective-permute-start.10) | collective-permute-done | bytes 344096 | tf_op jit(solution)/shard_map/ppermute | solution.py:60
  23.4 3.4 %collective-permute-done.11 = bf16[336,512]{1,0:T(8,128)(2,1)S(1)} collective-permute-done((bf16[336,512]{1,0:T(8,128)(2,1)S(1)}, bf16[336,512]{1,0:T(8,128)(2,1)S(1)}, u32[]{:S(2)}, u32[]{:S(2)}) %collective-permute-start.11) | collective-permute-done | bytes 344096 | tf_op jit(solution)/shard_map/ppermute | solution.py:61
  30.4 6.5 %collective-permute-done.13 = bf16[336,512]{1,0:T(8,128)(2,1)S(1)} collective-permute-done((bf16[336,512]{1,0:T(8,128)(2,1)S(1)}, bf16[336,512]{1,0:T(8,128)(2,1)S(1)}, u32[]{:S(2)}, u32[]{:S(2)}) %collective-permute-start.13) | collective-permute-done | bytes 344096 | tf_op jit(solution)/shard_map/ppermute | solution.py:61
  41.2 4.8 %collective-permute-done.15 = bf16[336,512]{1,0:T(8,128)(2,1)S(1)} collective-permute-done((bf16[336,512]{1,0:T(8,128)(2,1)S(1)}, bf16[336,512]{1,0:T(8,128)(2,1)S(1)}, u32[]{:S(2)}, u32[]{:S(2)}) %collective-permute-start.15) | collective-permute-done | bytes 344096 | tf_op jit(solution)/shard_map/ppermute | solution.py:61
  46.1 1.9 collective-permute-start.18
  50.2 3.9 %collective-permute-start.20 = (bf16[336,512]{1,0:T(8,128)(2,1)S(1)}, bf16[336,512]{1,0:T(8,128)(2,1)S(1)}, u32[]{:S(2)}, u32[]{:S(2)}) collective-permute-start(bf16[336,512]{1,0:T(8,128)(2,1)S(1)} %collective-permute-done.13), channel_id=1, source_target_pairs={{2,0},{0,2},{6,4},{4,6},{3,1},{1,3},{7,5},{5,7},{18,16},{16,18},{2... | collective-permute-start | bytes 1032200 | tf_op jit(solution)/shard_map/ppermute | solution.py:73
  54.9 3.9 %collective-permute-done.18 = bf16[336,512]{1,0:T(8,128)(2,1)S(1)} collective-permute-done((bf16[336,512]{1,0:T(8,128)(2,1)S(1)}, bf16[336,512]{1,0:T(8,128)(2,1)S(1)}, u32[]{:S(2)}, u32[]{:S(2)}) %collective-permute-start.18) | collective-permute-done | bytes 344096 | tf_op jit(solution)/shard_map/ppermute | solution.py:73
  60.3 1.9 collective-permute-start.22
  63.0 2.6 collective-permute-done.20
  67.1 2.3 collective-permute-done.22
  70.2 3.2 %broadcast_in_dim.57 = bf16[2688,1024]{1,0:T(8,128)(2,1)} broadcast(bf16[]{:T(256)} %constant.74.clone.1), dimensions={} | broadcast | bytes 5505026 | tf_op jit(solution)/shard_map/broadcast_in_dim | solution.py:153
  73.4 3.8 %fusion.33 = (bf16[2688,512]{1,0:T(8,128)(2,1)S(1)}, bf16[2688,1024]{1,0:T(8,128)(2,1)}) fusion(bf16[3024,512]{1,0:T(8,128)(2,1)} %constant_dynamic-update-slice_fusion.26, bf16[2688,1024]{1,0:T(8,128)(2,1)} %broadcast_in_dim.57, s32[]{:T(128)S(6)} %select_n.156), kind=kLoop, calls=%fused_computation.121 | loop fusion | bytes 8257540 | tf_op jit(solution)/shard_map/slice | solution.py:82
  78.6 2.0 copy.94
  81.9 3.7 %collective-permute-done.1 = f32[16]{0:T(128)S(1)} collective-permute-done((f32[16]{0:T(128)}, f32[16]{0:T(128)S(1)}, u32[]{:S(2)}, u32[]{:S(2)}) %collective-permute-start.1) | collective-permute-done | bytes 96 | tf_op jit(solution)/shard_map/ppermute | solution.py:19
  87.8 2.8 collective-permute-done.2
  100.9 3.6 %constant_dynamic-update-slice_fusion.24 = bf16[2688,1024]{1,0:T(8,128)(2,1)} fusion(bf16[2688,1024]{1,0:T(8,128)(2,1)} %get-tuple-element.31, bf16[2688,512]{1,0:T(8,128)(2,1)} %collective-permute-done.23, s32[]{:T(128)S(6)} %select_n.185), kind=kLoop, calls=%fused_computation.82 | loop fusion | bytes 5505028 | tf_op jit(solution)/shard_map/dynamic_update_slice | solution.py:155
  104.5 4.9 %fusion.15 = bf16[128,1024]{0,1:T(8,128)(2,1)} fusion(f32[128,1024]{0,1:T(8,128)S(1)} %copy-done.3, bf16[2688,1024]{1,0:T(8,128)(2,1)} %constant_dynamic-update-slice_fusion.24, bf16[1,128,2688]{2,1,0:T(8,128)(2,1)S(1)} %copy-done), kind=kOutput, calls=%fused_computation.28 | convolution fusion | flops 704905216 | bytes 6979584 | tf_op jit(solution)/shard_map/dot_general | solution.py:164
  109.4 2.0 copy.95
  111.4 3.3 %copy.84 = bf16[1024,8,128,1]{0,2,3,1:T(8,128)(2,1)S(1)} copy(bf16[1024,8,128,1]{2,1,0,3:T(8,128)(2,1)} %bitcast.134) | data formatting | bytes 4194304 | tf_op jit(solution)/shard_map/reshape | solution.py:219
  114.7 5.7 %fusion.37 = (f32[8,2,128]{2,1,0:T(2,128)S(1)}, f32[8,2,128,1024]{2,3,1,0:T(8,128)}) fusion(pred[128,1024]{0,1:T(8,128)(4,1)S(1)} %copy-done.15, bf16[1024,8,128,1]{0,2,3,1:T(8,128)(2,1)S(1)} %copy.84, bf16[128,8,2,128]{0,3,2,1:T(8,128)(2,1)S(1)} %bitcast.140), kind=kOutput, calls=%fused_computation.125 | convolution fusion | flops 547357696 | bytes 11149312 | tf_op jit(solution)/shard_map/sub | solution.py:226
  120.4 5.0 %fusion.38 = (bf16[1024,8,128]{0,2,1:T(8,128)(2,1)S(1)}, f32[1024,8,128]{0,2,1:T(8,128)S(1)}) fusion(bf16[128,8,2,128]{3,2,1,0:T(2,128)(2,1)} %reshape_squeeze.7, f32[128]{0:T(128)S(1)} %get-tuple-element.25, f32[8,2,128,1024]{2,3,1,0:T(8,128)} %get-tuple-element.51, f32[8,2,128]{2,1,0:T(2,128)S(1)} %get-tuple-element.50), kind=kOutput, calls=%fused_computation.126 | convolution fusion | flops 544210944 | bytes 15213056 | tf_op jit(solution)/shard_map/jgtl,tjgd->ljd/dot_general | solution.py:240
  127.2 18.4 %collective-permute-start.32 = (bf16[128,1024]{0,1:T(8,128)(2,1)S(1)}, bf16[128,1024]{0,1:T(8,128)(2,1)}, u32[]{:S(2)}, u32[]{:S(2)}) collective-permute-start(bf16[128,1024]{0,1:T(8,128)(2,1)S(1)} %copy-done.6), channel_id=1, source_target_pairs={{0,4},{2,6},{4,8},{6,10},{8,12},{10,14},{1,5},{3,7},{5,9},{7,11},{... | collective-permute-start | bytes 786440 | tf_op jit(solution)/shard_map/ppermute | solution.py:41
  151.9 5.3 %collective-permute-start.35 = (bf16[128,1024]{0,1:T(8,128)(2,1)S(1)}, bf16[128,1024]{0,1:T(8,128)(2,1)}, u32[]{:S(2)}, u32[]{:S(2)}) collective-permute-start(bf16[128,1024]{0,1:T(8,128)(2,1)S(1)} %copy-done.6), channel_id=1, source_target_pairs={{0,2},{4,6},{8,10},{12,14},{1,3},{5,7},{9,11},{13,15},{16,18},{20,... | collective-permute-start | bytes 786440 | tf_op jit(solution)/shard_map/ppermute | solution.py:43
  160.2 15.6 %collective-permute-done.31 = bf16[128,1024]{0,1:T(8,128)(2,1)S(1)} collective-permute-done((bf16[128,1024]{0,1:T(8,128)(2,1)S(1)}, bf16[128,1024]{0,1:T(8,128)(2,1)S(1)}, u32[]{:S(2)}, u32[]{:S(2)}) %collective-permute-start.31) | collective-permute-done | bytes 262176 | tf_op jit(solution)/shard_map/ppermute | solution.py:111
  177.2 7.4 %collective-permute-done.29 = bf16[128,1024]{0,1:T(8,128)(2,1)S(1)} collective-permute-done((bf16[128,1024]{0,1:T(8,128)(2,1)S(1)}, bf16[128,1024]{0,1:T(8,128)(2,1)S(1)}, u32[]{:S(2)}, u32[]{:S(2)}) %collective-permute-start.29) | collective-permute-done | bytes 262176 | tf_op jit(solution)/shard_map/ppermute | solution.py:111
  190.1 5.8 %fusion.11 = bf16[1,128,2688]{2,1,0:T(8,128)(2,1)} fusion(f32[128,2688]{1,0:T(8,128)} %convolution_multiply_fusion, bf16[128,1024]{0,1:T(8,128)(2,1)S(1)} %fusion.25, bf16[2688,1024]{1,0:T(8,128)(2,1)} %constant_dynamic-update-slice_fusion.24), kind=kOutput, calls=%fused_computation.19 | convolution fusion | flops 705331200 | bytes 7831552 | tf_op jit(solution)/shard_map/tk,dk->td/dot_general | solution.py:265
  198.6 2.4 collective-permute-start.47
  204.2 3.1 %collective-permute-done.47 = f32[464,128]{1,0:T(8,128)S(1)} collective-permute-done((f32[464,128]{1,0:T(8,128)S(1)}, f32[464,128]{1,0:T(8,128)S(1)}, u32[]{:S(2)}, u32[]{:S(2)}) %collective-permute-start.47) | collective-permute-done | bytes 237600 | tf_op jit(solution)/shard_map/ppermute | solution.py:19
  207.4 6.2 %collective-permute-start.48 = (f32[464,128]{1,0:T(8,128)S(1)}, f32[464,128]{1,0:T(8,128)}, u32[]{:S(2)}, u32[]{:S(2)}) collective-permute-start(f32[464,128]{1,0:T(8,128)S(1)} %fusion.62), channel_id=1, source_target_pairs={{0,4},{2,6},{4,0},{6,2},{8,12},{10,14},{12,8},{14,10},{1,5},{3,7},... | collective-permute-start | bytes 712712 | tf_op jit(solution)/shard_map/ppermute | solution.py:19
  213.8 5.1 %fusion.1 = (f32[8,2,128]{2,1,0:T(2,128)S(1)}, f32[8,1024,128,2]{2,1,3,0:T(8,128)S(1)}) fusion(f32[128]{0:T(128)S(1)} %copy-done.18, f32[8,2,128,1024]{2,3,1,0:T(8,128)} %get-tuple-element.51, f32[8,2,128]{2,1,0:T(2,128)S(1)} %get-tuple-element.50, bf16[1024,8,128,1]{0,2,3,1:T(8,128)(2,1)S(1)} %bitcast.155, bf16[128,8,2,128]{3,2,1,0:T(2,128)(2,1)S(1)} %copy-done.9), kind=kOutput, calls=%fused_computation.3 | convolution fusion | flops 545257472 | bytes 19415552 | tf_op jit(solution)/shard_map/tjgd,ljd->jgtl/dot_general | solution.py:228
  219.7 1.7 fusion.3
  221.4 3.4 %fusion.39 = (bf16[1024,8,128]{0,2,1:T(8,128)(2,1)S(1)}, f32[1024,8,128]{0,2,1:T(8,128)}) fusion(bf16[8,2,128,1024]{2,3,1,0:T(8,128)(2,1)S(1)} %fusion.3, bf16[128,8,2,128]{0,3,2,1:T(8,128)(2,1)S(1)} %bitcast.141), kind=kOutput, calls=%fused_computation.127 | convolution fusion | flops 537919488 | bytes 11010048 | tf_op jit(solution)/shard_map/jgtl,tjgd->ljd/dot_general | solution.py:236
  226.2 1.8 copy.73
  230.3 1.8 copy.71
  237.8 1.8 copy.69
  240.9 1.8 copy.68
  245.1 8.7 %collective-permute-start.49 = (f32[464,128]{1,0:T(8,128)S(1)}, f32[464,128]{1,0:T(8,128)}, u32[]{:S(2)}, u32[]{:S(2)}) collective-permute-start(f32[464,128]{1,0:T(8,128)S(1)} %add.274), channel_id=1, source_target_pairs={{0,8},{2,10},{4,12},{6,14},{8,0},{10,2},{12,4},{14,6},{1,9},{3,11}... | collective-permute-start | bytes 712712 | tf_op jit(solution)/shard_map/ppermute | solution.py:19
  253.8 1.9 add_convert_fusion.1
  257.0 1.7 add_convert_fusion.2
  260.0 1.7 add_convert_fusion.3
  263.0 3.0 %convolution_convert_fusion = bf16[8,128,2,128]{3,1,2,0:T(8,128)(2,1)S(1)} fusion(bf16[1024,8,128,1]{0,2,3,1:T(8,128)(2,1)S(1)} %copy.84, bf16[8,2,128,1024]{2,3,1,0:T(8,128)(2,1)} %copy-done.2), kind=kOutput, calls=%fused_computation.24 | convolution fusion | flops 537133056 | bytes 6815744 | tf_op jit(solution)/shard_map/jgtl,ljd->tjgd/dot_general | solution.py:233
  268.4 8.5 %collective-permute-done.49 = f32[464,128]{1,0:T(8,128)} collective-permute-done((f32[464,128]{1,0:T(8,128)S(1)}, f32[464,128]{1,0:T(8,128)}, u32[]{:S(2)}, u32[]{:S(2)}) %collective-permute-start.49) | collective-permute-done | bytes 237600 | tf_op jit(solution)/shard_map/ppermute | solution.py:19
  280.0 2.3 collective-permute-done.43
  282.4 2.0 fusion.29
  (212 shorter events, 82.0 us)
Async XLA Ops:
  0.7 92.5 %collective-permute-start.3 = (bf16[128,1024]{1,0:T(8,128)(2,1)}, bf16[128,1024]{1,0:T(8,128)(2,1)}, u32[]{:S(2)}, u32[]{:S(2)}) collective-permute-start(bf16[128,1024]{1,0:T(8,128)(2,1)} %bitcast.153), channel_id=1, source_target_pairs={{0,4},{2,6},{4,8},{6,10},{8,12},{10,14},{1,5},{3,7},{5,9},{7,11},{... | collective-permute-start | bytes 786440 | tf_op jit(solution)/shard_map/ppermute | solution.py:41
  6.5 93.2 %collective-permute-start.6 = (bf16[128,1024]{1,0:T(8,128)(2,1)}, bf16[128,1024]{1,0:T(8,128)(2,1)}, u32[]{:S(2)}, u32[]{:S(2)}) collective-permute-start(bf16[128,1024]{1,0:T(8,128)(2,1)} %bitcast.154), channel_id=1, source_target_pairs={{0,2},{4,6},{8,10},{12,14},{1,3},{5,7},{9,11},{13,15},{16,18},{20,... | collective-permute-start | bytes 786440 | tf_op jit(solution)/shard_map/ppermute | solution.py:43
  13.2 9.5 %collective-permute-start.10 = (bf16[336,512]{1,0:T(8,128)(2,1)S(1)}, bf16[336,512]{1,0:T(8,128)(2,1)S(1)}, u32[]{:S(2)}, u32[]{:S(2)}) collective-permute-start(bf16[336,512]{1,0:T(8,128)(2,1)S(1)} %get-tuple-element.29), channel_id=1, source_target_pairs={{0,4},{2,6},{4,8},{6,10},{8,12},{10,14},{1,5},{3,7},{5,9},{7,11},{... | collective-permute-start | bytes 1032200 | tf_op jit(solution)/shard_map/ppermute | solution.py:60
  16.0 10.9 %collective-permute-start.11 = (bf16[336,512]{1,0:T(8,128)(2,1)S(1)}, bf16[336,512]{1,0:T(8,128)(2,1)S(1)}, u32[]{:S(2)}, u32[]{:S(2)}) collective-permute-start(bf16[336,512]{1,0:T(8,128)(2,1)S(1)} %get-tuple-element.29), channel_id=1, source_target_pairs={{4,0},{6,2},{8,4},{10,6},{12,8},{14,10},{5,1},{7,3},{9,5},{11,7},{... | collective-permute-start | bytes 1032200 | tf_op jit(solution)/shard_map/ppermute | solution.py:61
  17.3 31.4 %collective-permute-start.16 = (bf16[336,512]{1,0:T(8,128)(2,1)S(1)}, bf16[336,512]{1,0:T(8,128)(2,1)S(1)}, u32[]{:S(2)}, u32[]{:S(2)}) collective-permute-start(bf16[336,512]{1,0:T(8,128)(2,1)S(1)} %get-tuple-element.29), channel_id=1, source_target_pairs={{2,0},{0,2},{6,4},{4,6},{10,8},{8,10},{14,12},{12,14},{3,1},{1,3},... | collective-permute-start | bytes 1032200 | tf_op jit(solution)/shard_map/ppermute | solution.py:67
  22.7 6.2 %collective-permute-start.12 = (bf16[336,512]{1,0:T(8,128)(2,1)S(1)}, bf16[336,512]{1,0:T(8,128)(2,1)S(1)}, u32[]{:S(2)}, u32[]{:S(2)}) collective-permute-start(bf16[336,512]{1,0:T(8,128)(2,1)S(1)} %collective-permute-done.10), channel_id=1, source_target_pairs={{4,8},{6,10},{8,12},{10,14},{5,9},{7,11},{9,13},{11,15},{20,24},{2... | collective-permute-start | bytes 1032200 | tf_op jit(solution)/shard_map/ppermute | solution.py:60
  26.9 10.1 %collective-permute-start.13 = (bf16[336,512]{1,0:T(8,128)(2,1)S(1)}, bf16[336,512]{1,0:T(8,128)(2,1)S(1)}, u32[]{:S(2)}, u32[]{:S(2)}) collective-permute-start(bf16[336,512]{1,0:T(8,128)(2,1)S(1)} %collective-permute-done.11), channel_id=1, source_target_pairs={{4,0},{6,2},{8,4},{10,6},{5,1},{7,3},{9,5},{11,7},{20,16},{22,18},... | collective-permute-start | bytes 1032200 | tf_op jit(solution)/shard_map/ppermute | solution.py:61
  28.9 10.8 %collective-permute-start.14 = (bf16[336,512]{1,0:T(8,128)(2,1)S(1)}, bf16[336,512]{1,0:T(8,128)(2,1)S(1)}, u32[]{:S(2)}, u32[]{:S(2)}) collective-permute-start(bf16[336,512]{1,0:T(8,128)(2,1)S(1)} %collective-permute-done.12), channel_id=1, source_target_pairs={{8,12},{10,14},{9,13},{11,15},{24,28},{26,30},{25,29},{27,31}} | collective-permute-start | bytes 1032200 | tf_op jit(solution)/shard_map/ppermute | solution.py:60
  36.9 9.1 %collective-permute-start.15 = (bf16[336,512]{1,0:T(8,128)(2,1)S(1)}, bf16[336,512]{1,0:T(8,128)(2,1)S(1)}, u32[]{:S(2)}, u32[]{:S(2)}) collective-permute-start(bf16[336,512]{1,0:T(8,128)(2,1)S(1)} %collective-permute-done.13), channel_id=1, source_target_pairs={{4,0},{6,2},{5,1},{7,3},{20,16},{22,18},{21,17},{23,19}} | collective-permute-start | bytes 1032200 | tf_op jit(solution)/shard_map/ppermute | solution.py:61
  39.7 10.4 %collective-permute-start.17 = (bf16[336,512]{1,0:T(8,128)(2,1)S(1)}, bf16[336,512]{1,0:T(8,128)(2,1)S(1)}, u32[]{:S(2)}, u32[]{:S(2)}) collective-permute-start(bf16[336,512]{1,0:T(8,128)(2,1)S(1)} %collective-permute-done.10), channel_id=1, source_target_pairs={{6,4},{4,6},{10,8},{8,10},{14,12},{12,14},{7,5},{5,7},{11,9},{9,11... | collective-permute-start | bytes 1032200 | tf_op jit(solution)/shard_map/ppermute | solution.py:71
  46.1 12.8 %collective-permute-start.18 = (bf16[336,512]{1,0:T(8,128)(2,1)S(1)}, bf16[336,512]{1,0:T(8,128)(2,1)S(1)}, u32[]{:S(2)}, u32[]{:S(2)}) collective-permute-start(bf16[336,512]{1,0:T(8,128)(2,1)S(1)} %collective-permute-done.11), channel_id=1, source_target_pairs={{2,0},{0,2},{6,4},{4,6},{10,8},{8,10},{3,1},{1,3},{7,5},{5,7},{11,... | collective-permute-start | bytes 1032200 | tf_op jit(solution)/shard_map/ppermute | solution.py:73
  48.7 11.6 %collective-permute-start.19 = (bf16[336,512]{1,0:T(8,128)(2,1)S(1)}, bf16[336,512]{1,0:T(8,128)(2,1)S(1)}, u32[]{:S(2)}, u32[]{:S(2)}) collective-permute-start(bf16[336,512]{1,0:T(8,128)(2,1)S(1)} %collective-permute-done.12), channel_id=1, source_target_pairs={{10,8},{8,10},{14,12},{12,14},{11,9},{9,11},{15,13},{13,15},{26,24... | collective-permute-start | bytes 1032200 | tf_op jit(solution)/shard_map/ppermute | solution.py:71
  50.2 15.4 %collective-permute-start.20 = (bf16[336,512]{1,0:T(8,128)(2,1)S(1)}, bf16[336,512]{1,0:T(8,128)(2,1)S(1)}, u32[]{:S(2)}, u32[]{:S(2)}) collective-permute-start(bf16[336,512]{1,0:T(8,128)(2,1)S(1)} %collective-permute-done.13), channel_id=1, source_target_pairs={{2,0},{0,2},{6,4},{4,6},{3,1},{1,3},{7,5},{5,7},{18,16},{16,18},{2... | collective-permute-start | bytes 1032200 | tf_op jit(solution)/shard_map/ppermute | solution.py:73
  58.8 7.5 %collective-permute-start.21 = (bf16[336,512]{1,0:T(8,128)(2,1)S(1)}, bf16[336,512]{1,0:T(8,128)(2,1)S(1)}, u32[]{:S(2)}, u32[]{:S(2)}) collective-permute-start(bf16[336,512]{1,0:T(8,128)(2,1)S(1)} %collective-permute-done.14), channel_id=1, source_target_pairs={{14,12},{12,14},{15,13},{13,15},{30,28},{28,30},{31,29},{29,31}} | collective-permute-start | bytes 1032200 | tf_op jit(solution)/shard_map/ppermute | solution.py:71
  60.3 9.1 %collective-permute-start.22 = (bf16[336,512]{1,0:T(8,128)(2,1)S(1)}, bf16[336,512]{1,0:T(8,128)(2,1)S(1)}, u32[]{:S(2)}, u32[]{:S(2)}) collective-permute-start(bf16[336,512]{1,0:T(8,128)(2,1)S(1)} %collective-permute-done.15), channel_id=1, source_target_pairs={{2,0},{0,2},{3,1},{1,3},{18,16},{16,18},{19,17},{17,19}} | collective-permute-start | bytes 1032200 | tf_op jit(solution)/shard_map/ppermute | solution.py:73
  65.5 15.1 %collective-permute-start = (f32[16]{0:T(128)}, f32[16]{0:T(128)}, u32[]{:S(2)}, u32[]{:S(2)}) collective-permute-start(f32[16]{0:T(128)} %pad_maximum_fusion), channel_id=1, source_target_pairs={{0,2},{2,0},{4,6},{6,4},{8,10},{10,8},{12,14},{14,12},{1,3},{3,1},... | collective-permute-start | bytes 200 | tf_op jit(solution)/shard_map/ppermute | solution.py:19
  77.1 23.7 %collective-permute-start.23 = (bf16[2688,512]{1,0:T(8,128)(2,1)S(1)}, bf16[2688,512]{1,0:T(8,128)(2,1)}, u32[]{:S(2)}, u32[]{:S(2)}) collective-permute-start(bf16[2688,512]{1,0:T(8,128)(2,1)S(1)} %get-tuple-element.30), channel_id=1, source_target_pairs={{0,1},{1,0},{2,3},{3,2},{4,5},{5,4},{6,7},{7,6},{8,9},{9,8},{10,11... | collective-permute-start | bytes 8257544 | tf_op jit(solution)/shard_map/ppermute | solution.py:19
  81.9 3.7 %collective-permute-start.1 = (f32[16]{0:T(128)}, f32[16]{0:T(128)S(1)}, u32[]{:S(2)}, u32[]{:S(2)}) collective-permute-start(f32[16]{0:T(128)} %fusion.63), channel_id=1, source_target_pairs={{0,4},{2,6},{4,0},{6,2},{8,12},{10,14},{12,8},{14,10},{1,5},{3,7},... | collective-permute-start | bytes 200 | tf_op jit(solution)/shard_map/ppermute | solution.py:19
  86.2 4.4 %collective-permute-start.2 = (f32[16]{0:T(128)S(1)}, f32[16]{0:T(128)}, u32[]{:S(2)}, u32[]{:S(2)}) collective-permute-start(f32[16]{0:T(128)S(1)} %add.231), channel_id=1, source_target_pairs={{0,8},{2,10},{4,12},{6,14},{8,0},{10,2},{12,4},{14,6},{1,9},{3,11}... | collective-permute-start | bytes 200 | tf_op jit(solution)/shard_map/ppermute | solution.py:19
  91.9 2.2 collective-permute-start.24
  94.9 3.9 %collective-permute-start.5 = (bf16[128,1024]{1,0:T(8,128)(2,1)S(1)}, bf16[128,1024]{1,0:T(8,128)(2,1)S(1)}, u32[]{:S(2)}, u32[]{:S(2)}) collective-permute-start(bf16[128,1024]{1,0:T(8,128)(2,1)S(1)} %collective-permute-done.4), channel_id=1, source_target_pairs={{8,12},{10,14},{9,13},{11,15},{24,28},{26,30},{25,29},{27,31}} | collective-permute-start | bytes 786440 | tf_op jit(solution)/shard_map/ppermute | solution.py:41
  97.4 3.3 %collective-permute-start.7 = (bf16[128,1024]{1,0:T(8,128)(2,1)}, bf16[128,1024]{1,0:T(8,128)(2,1)S(1)}, u32[]{:S(2)}, u32[]{:S(2)}) collective-permute-start(bf16[128,1024]{1,0:T(8,128)(2,1)} %collective-permute-done.3), channel_id=1, source_target_pairs={{6,4},{4,6},{10,8},{8,10},{14,12},{12,14},{7,5},{5,7},{11,9},{9,11... | collective-permute-start | bytes 786440 | tf_op jit(solution)/shard_map/ppermute | solution.py:46
  98.1 2.6 collective-permute-start.8
  125.9 21.7 %collective-permute-start.30 = (bf16[128,1024]{0,1:T(8,128)(2,1)S(1)}, bf16[128,1024]{0,1:T(8,128)(2,1)S(1)}, u32[]{:S(2)}, u32[]{:S(2)}) collective-permute-start(bf16[128,1024]{0,1:T(8,128)(2,1)S(1)} %bitcast.152), channel_id=1, source_target_pairs={{12,14},{14,12},{13,15},{15,13},{28,30},{30,28},{29,31},{31,29}} | collective-permute-start | bytes 786440 | tf_op jit(solution)/shard_map/ppermute | solution.py:106
  126.6 22.4 %collective-permute-start.28 = (bf16[128,1024]{0,1:T(8,128)(2,1)S(1)}, bf16[128,1024]{0,1:T(8,128)(2,1)S(1)}, u32[]{:S(2)}, u32[]{:S(2)}) collective-permute-start(bf16[128,1024]{0,1:T(8,128)(2,1)S(1)} %bitcast.151), channel_id=1, source_target_pairs={{8,10},{10,8},{12,14},{14,12},{9,11},{11,9},{13,15},{15,13},{24,26... | collective-permute-start | bytes 786440 | tf_op jit(solution)/shard_map/ppermute | solution.py:106
  127.2 24.6 %collective-permute-start.32 = (bf16[128,1024]{0,1:T(8,128)(2,1)S(1)}, bf16[128,1024]{0,1:T(8,128)(2,1)}, u32[]{:S(2)}, u32[]{:S(2)}) collective-permute-start(bf16[128,1024]{0,1:T(8,128)(2,1)S(1)} %copy-done.6), channel_id=1, source_target_pairs={{0,4},{2,6},{4,8},{6,10},{8,12},{10,14},{1,5},{3,7},{5,9},{7,11},{... | collective-permute-start | bytes 786440 | tf_op jit(solution)/shard_map/ppermute | solution.py:41
  145.6 4.8 %collective-permute-start.26 = (bf16[128,1024]{0,1:T(8,128)(2,1)S(1)}, bf16[128,1024]{0,1:T(8,128)(2,1)S(1)}, u32[]{:S(2)}, u32[]{:S(2)}) collective-permute-start(bf16[128,1024]{0,1:T(8,128)(2,1)S(1)} %bitcast.150), channel_id=1, source_target_pairs={{4,6},{6,4},{8,10},{10,8},{12,14},{14,12},{5,7},{7,5},{9,11},{11,9... | collective-permute-start | bytes 786440 | tf_op jit(solution)/shard_map/ppermute | solution.py:106
  146.3 12.6 %collective-permute-start.25 = (bf16[128,1024]{0,1:T(8,128)(2,1)S(1)}, bf16[128,1024]{0,1:T(8,128)(2,1)S(1)}, u32[]{:S(2)}, u32[]{:S(2)}) collective-permute-start(bf16[128,1024]{0,1:T(8,128)(2,1)S(1)} %bitcast.149), channel_id=1, source_target_pairs={{2,0},{6,4},{10,8},{14,12},{3,1},{7,5},{11,9},{15,13},{18,16},{22,... | collective-permute-start | bytes 786440 | tf_op jit(solution)/shard_map/ppermute | solution.py:103
  147.7 28.1 %collective-permute-start.31 = (bf16[128,1024]{0,1:T(8,128)(2,1)S(1)}, bf16[128,1024]{0,1:T(8,128)(2,1)S(1)}, u32[]{:S(2)}, u32[]{:S(2)}) collective-permute-start(bf16[128,1024]{0,1:T(8,128)(2,1)S(1)} %fusion.22), channel_id=1, source_target_pairs={{12,0},{14,2},{13,1},{15,3},{28,16},{30,18},{29,17},{31,19}} | collective-permute-start | bytes 786440 | tf_op jit(solution)/shard_map/ppermute | solution.py:111
  149.1 35.4 %collective-permute-start.29 = (bf16[128,1024]{0,1:T(8,128)(2,1)S(1)}, bf16[128,1024]{0,1:T(8,128)(2,1)S(1)}, u32[]{:S(2)}, u32[]{:S(2)}) collective-permute-start(bf16[128,1024]{0,1:T(8,128)(2,1)S(1)} %fusion.23), channel_id=1, source_target_pairs={{8,0},{10,2},{12,4},{14,6},{9,1},{11,3},{13,5},{15,7},{24,16},{26,... | collective-permute-start | bytes 786440 | tf_op jit(solution)/shard_map/ppermute | solution.py:111
  150.5 34.0 %collective-permute-start.27 = (bf16[128,1024]{0,1:T(8,128)(2,1)S(1)}, bf16[128,1024]{0,1:T(8,128)(2,1)S(1)}, u32[]{:S(2)}, u32[]{:S(2)}) collective-permute-start(bf16[128,1024]{0,1:T(8,128)(2,1)S(1)} %fusion.24), channel_id=1, source_target_pairs={{4,0},{6,2},{8,4},{10,6},{12,8},{14,10},{5,1},{7,3},{9,5},{11,7},{... | collective-permute-start | bytes 786440 | tf_op jit(solution)/shard_map/ppermute | solution.py:111
  151.9 50.1 %collective-permute-start.35 = (bf16[128,1024]{0,1:T(8,128)(2,1)S(1)}, bf16[128,1024]{0,1:T(8,128)(2,1)}, u32[]{:S(2)}, u32[]{:S(2)}) collective-permute-start(bf16[128,1024]{0,1:T(8,128)(2,1)S(1)} %copy-done.6), channel_id=1, source_target_pairs={{0,2},{4,6},{8,10},{12,14},{1,3},{5,7},{9,11},{13,15},{16,18},{20,... | collective-permute-start | bytes 786440 | tf_op jit(solution)/shard_map/ppermute | solution.py:43
  158.8 37.1 %collective-permute-start.33 = (bf16[128,1024]{0,1:T(8,128)(2,1)}, bf16[128,1024]{0,1:T(8,128)(2,1)}, u32[]{:S(2)}, u32[]{:S(2)}) collective-permute-start(bf16[128,1024]{0,1:T(8,128)(2,1)} %collective-permute-done.32), channel_id=1, source_target_pairs={{4,8},{6,10},{8,12},{10,14},{5,9},{7,11},{9,13},{11,15},{20,24},{2... | collective-permute-start | bytes 786440 | tf_op jit(solution)/shard_map/ppermute | solution.py:41
  175.8 27.2 %collective-permute-start.36 = (bf16[128,1024]{0,1:T(8,128)(2,1)}, bf16[128,1024]{0,1:T(8,128)(2,1)}, u32[]{:S(2)}, u32[]{:S(2)}) collective-permute-start(bf16[128,1024]{0,1:T(8,128)(2,1)} %collective-permute-done.32), channel_id=1, source_target_pairs={{6,4},{4,6},{10,8},{8,10},{14,12},{12,14},{7,5},{5,7},{11,9},{9,11... | collective-permute-start | bytes 786440 | tf_op jit(solution)/shard_map/ppermute | solution.py:46
  190.1 8.5 %collective-permute-start.46 = (f32[464,128]{1,0:T(8,128)S(1)}, f32[464,128]{1,0:T(8,128)S(1)}, u32[]{:S(2)}, u32[]{:S(2)}) collective-permute-start(f32[464,128]{1,0:T(8,128)S(1)} %maximum_bitcast_fusion), channel_id=1, source_target_pairs={{0,1},{1,0},{2,3},{3,2},{4,5},{5,4},{6,7},{7,6},{8,9},{9,8},{10,11... | collective-permute-start | bytes 712712 | tf_op jit(solution)/shard_map/ppermute | solution.py:19
  196.0 5.0 %collective-permute-start.34 = (bf16[128,1024]{0,1:T(8,128)(2,1)}, bf16[128,1024]{0,1:T(8,128)(2,1)S(1)}, u32[]{:S(2)}, u32[]{:S(2)}) collective-permute-start(bf16[128,1024]{0,1:T(8,128)(2,1)} %collective-permute-done.33), channel_id=1, source_target_pairs={{8,12},{10,14},{9,13},{11,15},{24,28},{26,30},{25,29},{27,31}} | collective-permute-start | bytes 786440 | tf_op jit(solution)/shard_map/ppermute | solution.py:41
  196.8 7.3 %collective-permute-start.37 = (bf16[128,1024]{0,1:T(8,128)(2,1)}, bf16[128,1024]{0,1:T(8,128)(2,1)S(1)}, u32[]{:S(2)}, u32[]{:S(2)}) collective-permute-start(bf16[128,1024]{0,1:T(8,128)(2,1)} %collective-permute-done.33), channel_id=1, source_target_pairs={{10,8},{8,10},{14,12},{12,14},{11,9},{9,11},{15,13},{13,15},{26,24... | collective-permute-start | bytes 786440 | tf_op jit(solution)/shard_map/ppermute | solution.py:46
  198.6 8.7 %collective-permute-start.47 = (f32[464,128]{1,0:T(8,128)S(1)}, f32[464,128]{1,0:T(8,128)S(1)}, u32[]{:S(2)}, u32[]{:S(2)}) collective-permute-start(f32[464,128]{1,0:T(8,128)S(1)} %fusion.32), channel_id=1, source_target_pairs={{0,2},{2,0},{4,6},{6,4},{8,10},{10,8},{12,14},{14,12},{1,3},{3,1},... | collective-permute-start | bytes 712712 | tf_op jit(solution)/shard_map/ppermute | solution.py:19
  201.0 12.6 %collective-permute-start.38 = (bf16[128,1024]{0,1:T(8,128)(2,1)S(1)}, bf16[128,1024]{0,1:T(8,128)(2,1)S(1)}, u32[]{:S(2)}, u32[]{:S(2)}) collective-permute-start(bf16[128,1024]{0,1:T(8,128)(2,1)S(1)} %collective-permute-done.34), channel_id=1, source_target_pairs={{14,12},{12,14},{15,13},{13,15},{30,28},{28,30},{31,29},{29,31}} | collective-permute-start | bytes 786440 | tf_op jit(solution)/shard_map/ppermute | solution.py:46
  207.4 36.6 %collective-permute-start.48 = (f32[464,128]{1,0:T(8,128)S(1)}, f32[464,128]{1,0:T(8,128)}, u32[]{:S(2)}, u32[]{:S(2)}) collective-permute-start(f32[464,128]{1,0:T(8,128)S(1)} %fusion.62), channel_id=1, source_target_pairs={{0,4},{2,6},{4,0},{6,2},{8,12},{10,14},{12,8},{14,10},{1,5},{3,7},... | collective-permute-start | bytes 712712 | tf_op jit(solution)/shard_map/ppermute | solution.py:19
  228.1 25.7 %collective-permute-start.44 = (bf16[128,1024]{1,0:T(8,128)(2,1)}, bf16[128,1024]{1,0:T(8,128)(2,1)}, u32[]{:S(2)}, u32[]{:S(2)}) collective-permute-start(bf16[128,1024]{1,0:T(8,128)(2,1)} %copy.73), channel_id=1, source_target_pairs={{12,14},{14,12},{13,15},{15,13},{28,30},{30,28},{29,31},{31,29}} | collective-permute-start | bytes 786440 | tf_op jit(solution)/shard_map/ppermute | solution.py:106
  232.1 24.9 %collective-permute-start.42 = (bf16[128,1024]{1,0:T(8,128)(2,1)}, bf16[128,1024]{1,0:T(8,128)(2,1)}, u32[]{:S(2)}, u32[]{:S(2)}) collective-permute-start(bf16[128,1024]{1,0:T(8,128)(2,1)} %copy.71), channel_id=1, source_target_pairs={{8,10},{10,8},{12,14},{14,12},{9,11},{11,9},{13,15},{15,13},{24,26... | collective-permute-start | bytes 786440 | tf_op jit(solution)/shard_map/ppermute | solution.py:106
  239.6 20.5 %collective-permute-start.40 = (bf16[128,1024]{1,0:T(8,128)(2,1)}, bf16[128,1024]{1,0:T(8,128)(2,1)}, u32[]{:S(2)}, u32[]{:S(2)}) collective-permute-start(bf16[128,1024]{1,0:T(8,128)(2,1)} %copy.69), channel_id=1, source_target_pairs={{4,6},{6,4},{8,10},{10,8},{12,14},{14,12},{5,7},{7,5},{9,11},{11,9... | collective-permute-start | bytes 786440 | tf_op jit(solution)/shard_map/ppermute | solution.py:106
  242.7 37.3 %collective-permute-start.39 = (bf16[128,1024]{1,0:T(8,128)(2,1)}, bf16[128,1024]{1,0:T(8,128)(2,1)}, u32[]{:S(2)}, u32[]{:S(2)}) collective-permute-start(bf16[128,1024]{1,0:T(8,128)(2,1)} %copy.68), channel_id=1, source_target_pairs={{2,0},{6,4},{10,8},{14,12},{3,1},{7,5},{11,9},{15,13},{18,16},{22,... | collective-permute-start | bytes 786440 | tf_op jit(solution)/shard_map/ppermute | solution.py:103
  245.1 31.8 %collective-permute-start.49 = (f32[464,128]{1,0:T(8,128)S(1)}, f32[464,128]{1,0:T(8,128)}, u32[]{:S(2)}, u32[]{:S(2)}) collective-permute-start(f32[464,128]{1,0:T(8,128)S(1)} %add.274), channel_id=1, source_target_pairs={{0,8},{2,10},{4,12},{6,14},{8,0},{10,2},{12,4},{14,6},{1,9},{3,11}... | collective-permute-start | bytes 712712 | tf_op jit(solution)/shard_map/ppermute | solution.py:19
  255.7 24.3 %collective-permute-start.45 = (bf16[128,1024]{1,0:T(8,128)(2,1)}, bf16[128,1024]{1,0:T(8,128)(2,1)}, u32[]{:S(2)}, u32[]{:S(2)}) collective-permute-start(bf16[128,1024]{1,0:T(8,128)(2,1)} %add_convert_fusion.1), channel_id=1, source_target_pairs={{12,0},{14,2},{13,1},{15,3},{28,16},{30,18},{29,17},{31,19}} | collective-permute-start | bytes 786440 | tf_op jit(solution)/shard_map/ppermute | solution.py:111
  258.7 23.6 %collective-permute-start.43 = (bf16[128,1024]{1,0:T(8,128)(2,1)}, bf16[128,1024]{1,0:T(8,128)(2,1)S(1)}, u32[]{:S(2)}, u32[]{:S(2)}) collective-permute-start(bf16[128,1024]{1,0:T(8,128)(2,1)} %add_convert_fusion.2), channel_id=1, source_target_pairs={{8,0},{10,2},{12,4},{14,6},{9,1},{11,3},{13,5},{15,7},{24,16},{26,... | collective-permute-start | bytes 786440 | tf_op jit(solution)/shard_map/ppermute | solution.py:111
  261.7 20.6 %collective-permute-start.41 = (bf16[128,1024]{1,0:T(8,128)(2,1)}, bf16[128,1024]{1,0:T(8,128)(2,1)}, u32[]{:S(2)}, u32[]{:S(2)}) collective-permute-start(bf16[128,1024]{1,0:T(8,128)(2,1)} %add_convert_fusion.3), channel_id=1, source_target_pairs={{4,0},{6,2},{8,4},{10,6},{12,8},{14,10},{5,1},{7,3},{9,5},{11,7},{... | collective-permute-start | bytes 786440 | tf_op jit(solution)/shard_map/ppermute | solution.py:111
  (26 other events, 358.9 us)

commit v12 on v7

--- a/solution.py
+++ b/solution.py
@@ -152,14 +152,28 @@
         rows_half = tree_gather(own_half, ctx_index, ctx_count // 2)
     else:
         rows_half = lax.all_gather(own_half, "ctx", axis=0, tiled=True)
-    full_weight = lax.all_gather(rows_half, "pair", axis=1, tiled=True)
+    split_pair = lax.axis_size("pair") == 2
+    if split_pair:
+        other_half = from_partner(rows_half, "pair", 0)
+        mine_at = pair_index * half_cols
+        other_at = (1 - pair_index) * half_cols
+    else:
+        full_weight = lax.all_gather(rows_half, "pair", axis=1, tiled=True)
     rank_projection = jnp.dot(hidden_rows, adapter_down, preferred_element_type=jnp.float32).astype(
         jnp.bfloat16
     )
-    values = (
-        jnp.dot(hidden_rows, full_weight, preferred_element_type=jnp.float32)
-        + ADAPTER_SCALE * jnp.dot(rank_projection, adapter_up, preferred_element_type=jnp.float32)
-    ).astype(jnp.bfloat16)
+    low_up = ADAPTER_SCALE * jnp.dot(rank_projection, adapter_up, preferred_element_type=jnp.float32)
+    if split_pair:
+        mine_cols = jnp.dot(hidden_rows, rows_half, preferred_element_type=jnp.float32)
+        other_cols = jnp.dot(hidden_rows, other_half, preferred_element_type=jnp.float32)
+        values = jnp.zeros((tok_rows, width_kv), jnp.float32)
+        values = lax.dynamic_update_slice_in_dim(values, mine_cols, mine_at, 1)
+        values = lax.dynamic_update_slice_in_dim(values, other_cols, other_at, 1)
+        values = (values + low_up).astype(jnp.bfloat16)
+    else:
+        values = (
+            jnp.dot(hidden_rows, full_weight, preferred_element_type=jnp.float32) + low_up
+        ).astype(jnp.bfloat16)
     segment_labels = token_pair_index[0]
     seg_table = (segment_labels[:, None] == jnp.arange(SEGS, dtype=jnp.int32)[None, :]).astype(
         jnp.float32
@@ -257,8 +271,24 @@
     rank_middle = jnp.einsum(
         "sj,zj->sz", value_gradient, adapter_up, preferred_element_type=jnp.float32
     ).astype(jnp.bfloat16)
+    if split_pair:
+        projected = jnp.einsum(
+            "tk,dk->td",
+            lax.dynamic_slice_in_dim(value_gradient, mine_at, half_cols, 1),
+            rows_half,
+            preferred_element_type=jnp.float32,
+        ) + jnp.einsum(
+            "tk,dk->td",
+            lax.dynamic_slice_in_dim(value_gradient, other_at, half_cols, 1),
+            other_half,
+            preferred_element_type=jnp.float32,
+        )
+    else:
+        projected = jnp.einsum(
+            "tk,dk->td", value_gradient, full_weight, preferred_element_type=jnp.float32
+        )
     input_grad = (
-        jnp.einsum("tk,dk->td", value_gradient, full_weight, preferred_element_type=jnp.float32)
+        projected
         + ADAPTER_SCALE
         * jnp.einsum("pb,wb->pw", rank_middle, adapter_down, preferred_element_type=jnp.float32)
     ).astype(jnp.bfloat16)

time: 279 us -> 292 us (1.047)
  local copies, waits for them, and re-layouts: 40.5 us -> 62.6 us
  between operations: 15.1 us -> 1.78 us
  matrix products: 28.7 us -> 33 us
  starting transfers between devices: 110 us -> 106 us
    unnamed x58 -> x67, local copies, waits for them, and re-layouts: 6.93 us -> 15.4 us
    ppermute x3, waiting for transfers between devices: 4.63 us -> 8.86 us  [tree_gather(): lax.ppermute(downs[step - 1], 'ctx', [(c ^ 1, c) for c in range(0, count...]
    dot_general x0 -> x2, local copies, waits for them, and re-layouts: none -> 3.58 us  [the longest x1 1.8 us: shards(): jnp.dot(hidden_rows, other_half, preferred_element_type=jnp.float32)]
    dynamic_update_slice x0 -> x2, local copies, waits for them, and re-layouts: none -> 3.35 us  [the longest x1 1.68 us: shards(): values = lax.dynamic_update_slice_in_dim(values, mine_cols, mine_at, 1)]
    ppermute x3, waiting for transfers between devices: 11.8 us -> 14.8 us  [tree_gather(): lax.ppermute(down, 'ctx', [(c + 2, c) for c in range(0, count - 2 * step)])]
    ppermute x8 -> x9, waiting for transfers between devices: 21.9 us -> 19.9 us  [from_partner(): lax.ppermute(shard, axis, [(i, i ^ 1 << stride) for i in range(lax.axis_s...]
    dot_general x2 -> x4, matrix products: 10.3 us -> 11.8 us  [the longest x1 3.73 us: shards(): jnp.einsum('tk,dk->td', lax.dynamic_slice_in_dim(value_gradient, mine_at,...]
    ppermute x8 -> x9, starting transfers between devices: 38.4 us -> 37.1 us  [from_partner(): lax.ppermute(shard, axis, [(i, i ^ 1 << stride) for i in range(lax.axis_s...]
  transfers between devices with their start and end apart: 50 -> 50, of which waited for: 16 -> 16; matrix products, arithmetic and copies ran while one was open for 18% -> 27% of each run, Pallas kernels for 0% -> 0%
where the time goes in v12:
time: 292 us; the launch traced here: 290 us
  starting transfers between devices  106 us (36%)
  waiting for transfers between devices  71.3 us (24%)
  local copies, waits for them, and re-layouts  62.6 us (21%)
  matrix products  33 us (11%)
  other arithmetic  15.2 us (5%)
    ppermute x9, starting transfers between devices, from_partner(): lax.ppermute(shard, axis, [(i, i ^ 1 << stride) for i in range(lax.axis_s...  37.1 us
    ppermute x6, starting transfers between devices, tree_spread(): lax.ppermute(held, 'ctx', [(c - 2, c) for c in range(2 * step, count)])  25.1 us
    ppermute x6, waiting for transfers between devices, tree_return(): lax.ppermute(acc.astype(jnp.bfloat16), 'ctx', [(c, c - 2) for c in range(...  21.8 us
    ppermute x9, waiting for transfers between devices, from_partner(): lax.ppermute(shard, axis, [(i, i ^ 1 << stride) for i in range(lax.axis_s...  19.9 us
    unnamed x67, local copies, waits for them, and re-layouts  15.4 us
    ppermute x3, waiting for transfers between devices, tree_gather(): lax.ppermute(down, 'ctx', [(c + 2, c) for c in range(0, count - 2 * step)])  14.8 us
    dynamic_update_slice x14, local copies, waits for them, and re-layouts, tree_gather(): whole = lax.dynamic_update_slice_in_dim(whole, piece, place, 0)  10.8 us
    ppermute x3, waiting for transfers between devices, tree_gather(): lax.ppermute(downs[step - 1], 'ctx', [(c ^ 1, c) for c in range(0, count...  8.86 us
  transfers between devices with their start and end apart: 50, of which 16 were waited for; matrix products, arithmetic and copies ran while one was open for 27% of the time, Pallas kernels for 0%

profile of v12, /device:TPU:0, one launch (start us, length us, event | category | flops | bytes accessed | tf_op | source)
XLA Modules:
  0.0 290.1 jit_solution(6155604555685779398)
XLA Ops:
  0.7 5.8 %collective-permute-start.3 = (bf16[128,1024]{1,0:T(8,128)(2,1)}, bf16[128,1024]{1,0:T(8,128)(2,1)}, u32[]{:S(2)}, u32[]{:S(2)}) collective-permute-start(bf16[128,1024]{1,0:T(8,128)(2,1)} %bitcast.151), channel_id=1, source_target_pairs={{0,4},{2,6},{4,8},{6,10},{8,12},{10,14},{1,5},{3,7},{5,9},{7,11},{... | collective-permute-start | bytes 786440 | tf_op jit(solution)/shard_map/ppermute | solution.py:41
  6.5 4.1 %collective-permute-start.6 = (bf16[128,1024]{1,0:T(8,128)(2,1)}, bf16[128,1024]{1,0:T(8,128)(2,1)}, u32[]{:S(2)}, u32[]{:S(2)}) collective-permute-start(bf16[128,1024]{1,0:T(8,128)(2,1)} %bitcast.152), channel_id=1, source_target_pairs={{0,2},{4,6},{8,10},{12,14},{1,3},{5,7},{9,11},{13,15},{16,18},{20,... | collective-permute-start | bytes 786440 | tf_op jit(solution)/shard_map/ppermute | solution.py:43
  10.5 1.8 broadcast_in_dim.58
  13.1 2.8 collective-permute-start.10
  19.0 3.7 %collective-permute-done.10 = bf16[336,512]{1,0:T(8,128)(2,1)S(1)} collective-permute-done((bf16[336,512]{1,0:T(8,128)(2,1)S(1)}, bf16[336,512]{1,0:T(8,128)(2,1)S(1)}, u32[]{:S(2)}, u32[]{:S(2)}) %collective-permute-start.10) | collective-permute-done | bytes 344096 | tf_op jit(solution)/shard_map/ppermute | solution.py:60
  23.4 3.4 %collective-permute-done.11 = bf16[336,512]{1,0:T(8,128)(2,1)S(1)} collective-permute-done((bf16[336,512]{1,0:T(8,128)(2,1)S(1)}, bf16[336,512]{1,0:T(8,128)(2,1)S(1)}, u32[]{:S(2)}, u32[]{:S(2)}) %collective-permute-start.11) | collective-permute-done | bytes 344096 | tf_op jit(solution)/shard_map/ppermute | solution.py:61
  30.4 6.5 %collective-permute-done.13 = bf16[336,512]{1,0:T(8,128)(2,1)S(1)} collective-permute-done((bf16[336,512]{1,0:T(8,128)(2,1)S(1)}, bf16[336,512]{1,0:T(8,128)(2,1)S(1)}, u32[]{:S(2)}, u32[]{:S(2)}) %collective-permute-start.13) | collective-permute-done | bytes 344096 | tf_op jit(solution)/shard_map/ppermute | solution.py:61
  41.1 4.9 %collective-permute-done.15 = bf16[336,512]{1,0:T(8,128)(2,1)S(1)} collective-permute-done((bf16[336,512]{1,0:T(8,128)(2,1)S(1)}, bf16[336,512]{1,0:T(8,128)(2,1)S(1)}, u32[]{:S(2)}, u32[]{:S(2)}) %collective-permute-start.15) | collective-permute-done | bytes 344096 | tf_op jit(solution)/shard_map/ppermute | solution.py:61
  46.0 1.9 collective-permute-start.18
  50.2 3.9 %collective-permute-start.20 = (bf16[336,512]{1,0:T(8,128)(2,1)S(1)}, bf16[336,512]{1,0:T(8,128)(2,1)S(1)}, u32[]{:S(2)}, u32[]{:S(2)}) collective-permute-start(bf16[336,512]{1,0:T(8,128)(2,1)S(1)} %collective-permute-done.13), channel_id=1, source_target_pairs={{2,0},{0,2},{6,4},{4,6},{3,1},{1,3},{7,5},{5,7},{18,16},{16,18},{2... | collective-permute-start | bytes 1032200 | tf_op jit(solution)/shard_map/ppermute | solution.py:73
  54.8 4.0 %collective-permute-done.18 = bf16[336,512]{1,0:T(8,128)(2,1)S(1)} collective-permute-done((bf16[336,512]{1,0:T(8,128)(2,1)S(1)}, bf16[336,512]{1,0:T(8,128)(2,1)S(1)}, u32[]{:S(2)}, u32[]{:S(2)}) %collective-permute-start.18) | collective-permute-done | bytes 344096 | tf_op jit(solution)/shard_map/ppermute | solution.py:73
  60.3 1.9 collective-permute-start.22
  62.9 2.6 collective-permute-done.20
  67.0 2.3 collective-permute-done.22
  70.1 3.5 %slice.122 = bf16[2688,512]{1,0:T(8,128)(2,1)} slice(bf16[3024,512]{1,0:T(8,128)(2,1)} %constant_dynamic-update-slice_fusion.26), slice={[0:2688], [0:512]} | slice | bytes 5505024 | tf_op jit(solution)/shard_map/slice | solution.py:82
  73.9 2.1 copy.96
  76.1 3.5 %collective-permute-done.1 = f32[16]{0:T(128)S(1)} collective-permute-done((f32[16]{0:T(128)S(1)}, f32[16]{0:T(128)S(1)}, u32[]{:S(2)}, u32[]{:S(2)}) %collective-permute-start.1) | collective-permute-done | bytes 96 | tf_op jit(solution)/shard_map/ppermute | solution.py:19
  81.2 2.9 collective-permute-done.2
  96.8 3.4 %convolution_bitcast_fusion.2 = f32[128,512]{0,1:T(8,128)} fusion(bf16[1,128,2688]{2,1,0:T(8,128)(2,1)S(1)} %copy-done, bf16[3024,512]{1,0:T(8,128)(2,1)} %constant_dynamic-update-slice_fusion.26), kind=kOutput, calls=%fused_computation.32 | convolution fusion | flops 352321536 | bytes 3702784 | tf_op jit(solution)/shard_map/dot_general | solution.py:167
  100.2 1.8 copy.59
  104.5 1.7 convolution_bitcast_fusion.1
  106.2 1.8 copy.60
  109.7 2.0 fusion.18
  111.7 3.6 %copy.97 = bf16[128,8,8,128]{3,2,1,0:T(8,128)(2,1)} copy(bf16[128,8,8,128]{3,1,2,0:T(8,128)(2,1)} %bitcast.51) | data formatting | bytes 4194304
  115.3 3.3 %copy.86 = bf16[1024,8,128,1]{0,2,3,1:T(8,128)(2,1)S(1)} copy(bf16[1024,8,128,1]{2,1,0,3:T(8,128)(2,1)} %bitcast.131) | data formatting | bytes 4194304 | tf_op jit(solution)/shard_map/reshape | solution.py:229
  118.6 5.8 %fusion.48 = (f32[8,2,128]{2,1,0:T(2,128)S(1)}, f32[8,2,128,1024]{2,3,1,0:T(8,128)}) fusion(pred[128,1024]{0,1:T(8,128)(4,1)S(1)} %copy-done.18, bf16[1024,8,128,1]{0,2,3,1:T(8,128)(2,1)S(1)} %copy.86, bf16[128,8,2,128]{0,3,2,1:T(8,128)(2,1)S(1)} %bitcast.138), kind=kOutput, calls=%fused_computation.137 | convolution fusion | flops 547357696 | bytes 11149312 | tf_op jit(solution)/shard_map/sub | solution.py:236
  124.4 5.0 %fusion.49 = (bf16[1024,8,128]{0,2,1:T(8,128)(2,1)S(1)}, f32[1024,8,128]{0,2,1:T(8,128)S(1)}) fusion(bf16[128,8,2,128]{3,2,1,0:T(2,128)(2,1)} %reshape_squeeze.7, f32[128]{0:T(128)S(1)} %get-tuple-element.25, f32[8,2,128,1024]{2,3,1,0:T(8,128)} %get-tuple-element.49, f32[8,2,128]{2,1,0:T(2,128)S(1)} %get-tuple-element.48), kind=kOutput, calls=%fused_computation.138 | convolution fusion | flops 544210944 | bytes 15213056 | tf_op jit(solution)/shard_map/jgtl,tjgd->ljd/dot_general | solution.py:250
  130.7 16.5 %collective-permute-start.32 = (bf16[128,1024]{1,0:T(8,128)(2,1)S(1)}, bf16[128,1024]{1,0:T(8,128)(2,1)S(1)}, u32[]{:S(2)}, u32[]{:S(2)}) collective-permute-start(bf16[128,1024]{1,0:T(8,128)(2,1)S(1)} %copy-done.10), channel_id=1, source_target_pairs={{0,4},{2,6},{4,8},{6,10},{8,12},{10,14},{1,5},{3,7},{5,9},{7,11},{... | collective-permute-start | bytes 786440 | tf_op jit(solution)/shard_map/ppermute | solution.py:41
  149.5 2.2 collective-permute-done.32
  153.2 3.5 %collective-permute-start.35 = (bf16[128,1024]{1,0:T(8,128)(2,1)S(1)}, bf16[128,1024]{1,0:T(8,128)(2,1)S(1)}, u32[]{:S(2)}, u32[]{:S(2)}) collective-permute-start(bf16[128,1024]{1,0:T(8,128)(2,1)S(1)} %copy-done.10), channel_id=1, source_target_pairs={{0,2},{4,6},{8,10},{12,14},{1,3},{5,7},{9,11},{13,15},{16,18},{20,... | collective-permute-start | bytes 786440 | tf_op jit(solution)/shard_map/ppermute | solution.py:43
  168.0 3.6 %fusion.50 = (bf16[1024,8,128]{0,2,1:T(8,128)(2,1)S(1)}, f32[1024,8,128]{0,2,1:T(8,128)}) fusion(bf16[8,2,128,1024]{2,3,1,0:T(8,128)(2,1)S(1)} %fusion.3, bf16[128,8,2,128]{0,3,2,1:T(8,128)(2,1)S(1)} %bitcast.139), kind=kOutput, calls=%fused_computation.139 | convolution fusion | flops 537919488 | bytes 11010048 | tf_op jit(solution)/shard_map/jgtl,tjgd->ljd/dot_general | solution.py:246
  171.6 18.7 %collective-permute-done.31 = bf16[128,1024]{0,1:T(8,128)(2,1)S(1)} collective-permute-done((bf16[128,1024]{0,1:T(8,128)(2,1)S(1)}, bf16[128,1024]{0,1:T(8,128)(2,1)S(1)}, u32[]{:S(2)}, u32[]{:S(2)}) %collective-permute-start.31) | collective-permute-done | bytes 262176 | tf_op jit(solution)/shard_map/ppermute | solution.py:114
  196.7 1.8 copy.74
  199.8 1.8 copy.72
  203.0 1.8 copy.71
  207.8 2.5 copy.79
  210.3 2.4 reshape.220
  214.3 3.0 %fusion.35 = f32[128,2688]{1,0:T(8,128)} fusion(bf16[2688,512]{1,0:T(8,128)(2,1)S(1)} %copy-done.2, bf16[128,1024]{0,1:T(8,128)(2,1)} %copy-done.4, s32[]{:T(128)S(6)} %select_n.187), kind=kOutput, calls=%fused_computation.64 | convolution fusion | flops 352321536 | bytes 4259844 | tf_op jit(solution)/shard_map/tk,dk->td/dot_general | solution.py:280
  218.6 1.8 add_convert_fusion.3
  224.9 3.4 %collective-permute-start.47 = (f32[464,128]{1,0:T(8,128)S(1)}, f32[464,128]{1,0:T(8,128)S(1)}, u32[]{:S(2)}, u32[]{:S(2)}) collective-permute-start(f32[464,128]{1,0:T(8,128)S(1)} %fusion.42), channel_id=1, source_target_pairs={{0,2},{2,0},{4,6},{6,4},{8,10},{10,8},{12,14},{14,12},{1,3},{3,1},... | collective-permute-start | bytes 712712 | tf_op jit(solution)/shard_map/ppermute | solution.py:19
  230.1 4.7 %collective-permute-done.47 = f32[464,128]{1,0:T(8,128)S(1)} collective-permute-done((f32[464,128]{1,0:T(8,128)S(1)}, f32[464,128]{1,0:T(8,128)S(1)}, u32[]{:S(2)}, u32[]{:S(2)}) %collective-permute-start.47) | collective-permute-done | bytes 237600 | tf_op jit(solution)/shard_map/ppermute | solution.py:19
  235.7 11.1 %collective-permute-start.48 = (f32[464,128]{1,0:T(8,128)S(1)}, f32[464,128]{1,0:T(8,128)S(1)}, u32[]{:S(2)}, u32[]{:S(2)}) collective-permute-start(f32[464,128]{1,0:T(8,128)S(1)} %fusion.71), channel_id=1, source_target_pairs={{0,4},{2,6},{4,0},{6,2},{8,12},{10,14},{12,8},{14,10},{1,5},{3,7},... | collective-permute-start | bytes 712712 | tf_op jit(solution)/shard_map/ppermute | solution.py:19
  247.2 5.5 %collective-permute-done.48 = f32[464,128]{1,0:T(8,128)S(1)} collective-permute-done((f32[464,128]{1,0:T(8,128)S(1)}, f32[464,128]{1,0:T(8,128)S(1)}, u32[]{:S(2)}, u32[]{:S(2)}) %collective-permute-start.48) | collective-permute-done | bytes 237600 | tf_op jit(solution)/shard_map/ppermute | solution.py:19
  252.7 21.1 %collective-permute-start.49 = (f32[464,128]{1,0:T(8,128)S(1)}, f32[464,128]{1,0:T(8,128)S(1)}, u32[]{:S(2)}, u32[]{:S(2)}) collective-permute-start(f32[464,128]{1,0:T(8,128)S(1)} %add.280), channel_id=1, source_target_pairs={{0,8},{2,10},{4,12},{6,14},{8,0},{10,2},{12,4},{14,6},{1,9},{3,11}... | collective-permute-start | bytes 712712 | tf_op jit(solution)/shard_map/ppermute | solution.py:19
  276.2 3.7 %fusion.12 = bf16[1,128,2688]{2,1,0:T(8,128)(2,1)} fusion(f32[128,2688]{1,0:T(8,128)S(1)} %convolution_multiply_fusion, f32[128,2688]{1,0:T(8,128)S(1)} %copy-done.3, bf16[128,1024]{0,1:T(8,128)(2,1)S(1)} %copy-done.5, s32[]{:T(128)S(6)} %select_n.158, bf16[3024,512]{1,0:T(8,128)(2,1)} %constant_dynamic-update-slice_fusion.26), kind=kOutput, calls=%fused_computation.20 | convolution fusion | flops 353353728 | bytes 6324228 | tf_op jit(solution)/shard_map/tk,dk->td/dot_general | solution.py:275
  279.9 3.2 %collective-permute-done.49 = f32[464,128]{1,0:T(8,128)S(1)} collective-permute-done((f32[464,128]{1,0:T(8,128)S(1)}, f32[464,128]{1,0:T(8,128)S(1)}, u32[]{:S(2)}, u32[]{:S(2)}) %collective-permute-start.49) | collective-permute-done | bytes 237600 | tf_op jit(solution)/shard_map/ppermute | solution.py:19
  285.3 3.1 %collective-permute-done.45 = bf16[128,1024]{1,0:T(8,128)(2,1)S(1)} collective-permute-done((bf16[128,1024]{1,0:T(8,128)(2,1)S(1)}, bf16[128,1024]{1,0:T(8,128)(2,1)S(1)}, u32[]{:S(2)}, u32[]{:S(2)}) %collective-permute-start.45) | collective-permute-done | bytes 262176 | tf_op jit(solution)/shard_map/ppermute | solution.py:114
  288.3 1.8 fusion.34
  (218 shorter events, 81.6 us)
Async XLA Ops:
  0.7 83.7 %collective-permute-start.3 = (bf16[128,1024]{1,0:T(8,128)(2,1)}, bf16[128,1024]{1,0:T(8,128)(2,1)}, u32[]{:S(2)}, u32[]{:S(2)}) collective-permute-start(bf16[128,1024]{1,0:T(8,128)(2,1)} %bitcast.151), channel_id=1, source_target_pairs={{0,4},{2,6},{4,8},{6,10},{8,12},{10,14},{1,5},{3,7},{5,9},{7,11},{... | collective-permute-start | bytes 786440 | tf_op jit(solution)/shard_map/ppermute | solution.py:41
  6.5 85.7 %collective-permute-start.6 = (bf16[128,1024]{1,0:T(8,128)(2,1)}, bf16[128,1024]{1,0:T(8,128)(2,1)}, u32[]{:S(2)}, u32[]{:S(2)}) collective-permute-start(bf16[128,1024]{1,0:T(8,128)(2,1)} %bitcast.152), channel_id=1, source_target_pairs={{0,2},{4,6},{8,10},{12,14},{1,3},{5,7},{9,11},{13,15},{16,18},{20,... | collective-permute-start | bytes 786440 | tf_op jit(solution)/shard_map/ppermute | solution.py:43
  13.1 9.6 %collective-permute-start.10 = (bf16[336,512]{1,0:T(8,128)(2,1)S(1)}, bf16[336,512]{1,0:T(8,128)(2,1)S(1)}, u32[]{:S(2)}, u32[]{:S(2)}) collective-permute-start(bf16[336,512]{1,0:T(8,128)(2,1)S(1)} %get-tuple-element.29), channel_id=1, source_target_pairs={{0,4},{2,6},{4,8},{6,10},{8,12},{10,14},{1,5},{3,7},{5,9},{7,11},{... | collective-permute-start | bytes 1032200 | tf_op jit(solution)/shard_map/ppermute | solution.py:60
  16.0 10.9 %collective-permute-start.11 = (bf16[336,512]{1,0:T(8,128)(2,1)S(1)}, bf16[336,512]{1,0:T(8,128)(2,1)S(1)}, u32[]{:S(2)}, u32[]{:S(2)}) collective-permute-start(bf16[336,512]{1,0:T(8,128)(2,1)S(1)} %get-tuple-element.29), channel_id=1, source_target_pairs={{4,0},{6,2},{8,4},{10,6},{12,8},{14,10},{5,1},{7,3},{9,5},{11,7},{... | collective-permute-start | bytes 1032200 | tf_op jit(solution)/shard_map/ppermute | solution.py:61
  17.3 31.4 %collective-permute-start.16 = (bf16[336,512]{1,0:T(8,128)(2,1)S(1)}, bf16[336,512]{1,0:T(8,128)(2,1)S(1)}, u32[]{:S(2)}, u32[]{:S(2)}) collective-permute-start(bf16[336,512]{1,0:T(8,128)(2,1)S(1)} %get-tuple-element.29), channel_id=1, source_target_pairs={{2,0},{0,2},{6,4},{4,6},{10,8},{8,10},{14,12},{12,14},{3,1},{1,3},... | collective-permute-start | bytes 1032200 | tf_op jit(solution)/shard_map/ppermute | solution.py:67
  22.7 6.3 %collective-permute-start.12 = (bf16[336,512]{1,0:T(8,128)(2,1)S(1)}, bf16[336,512]{1,0:T(8,128)(2,1)S(1)}, u32[]{:S(2)}, u32[]{:S(2)}) collective-permute-start(bf16[336,512]{1,0:T(8,128)(2,1)S(1)} %collective-permute-done.10), channel_id=1, source_target_pairs={{4,8},{6,10},{8,12},{10,14},{5,9},{7,11},{9,13},{11,15},{20,24},{2... | collective-permute-start | bytes 1032200 | tf_op jit(solution)/shard_map/ppermute | solution.py:60
  26.8 10.0 %collective-permute-start.13 = (bf16[336,512]{1,0:T(8,128)(2,1)S(1)}, bf16[336,512]{1,0:T(8,128)(2,1)S(1)}, u32[]{:S(2)}, u32[]{:S(2)}) collective-permute-start(bf16[336,512]{1,0:T(8,128)(2,1)S(1)} %collective-permute-done.11), channel_id=1, source_target_pairs={{4,0},{6,2},{8,4},{10,6},{5,1},{7,3},{9,5},{11,7},{20,16},{22,18},... | collective-permute-start | bytes 1032200 | tf_op jit(solution)/shard_map/ppermute | solution.py:61
  29.0 10.7 %collective-permute-start.14 = (bf16[336,512]{1,0:T(8,128)(2,1)S(1)}, bf16[336,512]{1,0:T(8,128)(2,1)S(1)}, u32[]{:S(2)}, u32[]{:S(2)}) collective-permute-start(bf16[336,512]{1,0:T(8,128)(2,1)S(1)} %collective-permute-done.12), channel_id=1, source_target_pairs={{8,12},{10,14},{9,13},{11,15},{24,28},{26,30},{25,29},{27,31}} | collective-permute-start | bytes 1032200 | tf_op jit(solution)/shard_map/ppermute | solution.py:60
  36.9 9.1 %collective-permute-start.15 = (bf16[336,512]{1,0:T(8,128)(2,1)S(1)}, bf16[336,512]{1,0:T(8,128)(2,1)S(1)}, u32[]{:S(2)}, u32[]{:S(2)}) collective-permute-start(bf16[336,512]{1,0:T(8,128)(2,1)S(1)} %collective-permute-done.13), channel_id=1, source_target_pairs={{4,0},{6,2},{5,1},{7,3},{20,16},{22,18},{21,17},{23,19}} | collective-permute-start | bytes 1032200 | tf_op jit(solution)/shard_map/ppermute | solution.py:61
  39.7 10.5 %collective-permute-start.17 = (bf16[336,512]{1,0:T(8,128)(2,1)S(1)}, bf16[336,512]{1,0:T(8,128)(2,1)S(1)}, u32[]{:S(2)}, u32[]{:S(2)}) collective-permute-start(bf16[336,512]{1,0:T(8,128)(2,1)S(1)} %collective-permute-done.10), channel_id=1, source_target_pairs={{6,4},{4,6},{10,8},{8,10},{14,12},{12,14},{7,5},{5,7},{11,9},{9,11... | collective-permute-start | bytes 1032200 | tf_op jit(solution)/shard_map/ppermute | solution.py:71
  46.0 12.8 %collective-permute-start.18 = (bf16[336,512]{1,0:T(8,128)(2,1)S(1)}, bf16[336,512]{1,0:T(8,128)(2,1)S(1)}, u32[]{:S(2)}, u32[]{:S(2)}) collective-permute-start(bf16[336,512]{1,0:T(8,128)(2,1)S(1)} %collective-permute-done.11), channel_id=1, source_target_pairs={{2,0},{0,2},{6,4},{4,6},{10,8},{8,10},{3,1},{1,3},{7,5},{5,7},{11,... | collective-permute-start | bytes 1032200 | tf_op jit(solution)/shard_map/ppermute | solution.py:73
  48.7 11.6 %collective-permute-start.19 = (bf16[336,512]{1,0:T(8,128)(2,1)S(1)}, bf16[336,512]{1,0:T(8,128)(2,1)S(1)}, u32[]{:S(2)}, u32[]{:S(2)}) collective-permute-start(bf16[336,512]{1,0:T(8,128)(2,1)S(1)} %collective-permute-done.12), channel_id=1, source_target_pairs={{10,8},{8,10},{14,12},{12,14},{11,9},{9,11},{15,13},{13,15},{26,24... | collective-permute-start | bytes 1032200 | tf_op jit(solution)/shard_map/ppermute | solution.py:71
  50.2 15.4 %collective-permute-start.20 = (bf16[336,512]{1,0:T(8,128)(2,1)S(1)}, bf16[336,512]{1,0:T(8,128)(2,1)S(1)}, u32[]{:S(2)}, u32[]{:S(2)}) collective-permute-start(bf16[336,512]{1,0:T(8,128)(2,1)S(1)} %collective-permute-done.13), channel_id=1, source_target_pairs={{2,0},{0,2},{6,4},{4,6},{3,1},{1,3},{7,5},{5,7},{18,16},{16,18},{2... | collective-permute-start | bytes 1032200 | tf_op jit(solution)/shard_map/ppermute | solution.py:73
  58.8 7.5 %collective-permute-start.21 = (bf16[336,512]{1,0:T(8,128)(2,1)S(1)}, bf16[336,512]{1,0:T(8,128)(2,1)S(1)}, u32[]{:S(2)}, u32[]{:S(2)}) collective-permute-start(bf16[336,512]{1,0:T(8,128)(2,1)S(1)} %collective-permute-done.14), channel_id=1, source_target_pairs={{14,12},{12,14},{15,13},{13,15},{30,28},{28,30},{31,29},{29,31}} | collective-permute-start | bytes 1032200 | tf_op jit(solution)/shard_map/ppermute | solution.py:71
  60.3 9.1 %collective-permute-start.22 = (bf16[336,512]{1,0:T(8,128)(2,1)S(1)}, bf16[336,512]{1,0:T(8,128)(2,1)S(1)}, u32[]{:S(2)}, u32[]{:S(2)}) collective-permute-start(bf16[336,512]{1,0:T(8,128)(2,1)S(1)} %collective-permute-done.15), channel_id=1, source_target_pairs={{2,0},{0,2},{3,1},{1,3},{18,16},{16,18},{19,17},{17,19}} | collective-permute-start | bytes 1032200 | tf_op jit(solution)/shard_map/ppermute | solution.py:73
  65.5 10.5 %collective-permute-start = (f32[16]{0:T(128)S(1)}, f32[16]{0:T(128)S(1)}, u32[]{:S(2)}, u32[]{:S(2)}) collective-permute-start(f32[16]{0:T(128)S(1)} %pad_maximum_fusion), channel_id=1, source_target_pairs={{0,2},{2,0},{4,6},{6,4},{8,10},{10,8},{12,14},{14,12},{1,3},{3,1},... | collective-permute-start | bytes 200 | tf_op jit(solution)/shard_map/ppermute | solution.py:19
  73.7 30.9 %collective-permute-start.23 = (bf16[2688,512]{1,0:T(8,128)(2,1)}, bf16[2688,512]{1,0:T(8,128)(2,1)S(1)}, u32[]{:S(2)}, u32[]{:S(2)}) collective-permute-start(bf16[2688,512]{1,0:T(8,128)(2,1)} %slice.122), channel_id=1, source_target_pairs={{0,1},{1,0},{2,3},{3,2},{4,5},{5,4},{6,7},{7,6},{8,9},{9,8},{10,11... | collective-permute-start | bytes 8257544 | tf_op jit(solution)/shard_map/ppermute | solution.py:19
  76.1 3.5 %collective-permute-start.1 = (f32[16]{0:T(128)S(1)}, f32[16]{0:T(128)S(1)}, u32[]{:S(2)}, u32[]{:S(2)}) collective-permute-start(f32[16]{0:T(128)S(1)} %fusion.72), channel_id=1, source_target_pairs={{0,4},{2,6},{4,0},{6,2},{8,12},{10,14},{12,8},{14,10},{1,5},{3,7},... | collective-permute-start | bytes 200 | tf_op jit(solution)/shard_map/ppermute | solution.py:19
  79.7 4.4 %collective-permute-start.2 = (f32[16]{0:T(128)S(1)}, f32[16]{0:T(128)S(1)}, u32[]{:S(2)}, u32[]{:S(2)}) collective-permute-start(f32[16]{0:T(128)S(1)} %add.236), channel_id=1, source_target_pairs={{0,8},{2,10},{4,12},{6,14},{8,0},{10,2},{12,4},{14,6},{1,9},{3,11}... | collective-permute-start | bytes 200 | tf_op jit(solution)/shard_map/ppermute | solution.py:19
  84.2 1.1 collective-permute-start.24
  85.5 5.3 %collective-permute-start.5 = (bf16[128,1024]{1,0:T(8,128)(2,1)S(1)}, bf16[128,1024]{1,0:T(8,128)(2,1)S(1)}, u32[]{:S(2)}, u32[]{:S(2)}) collective-permute-start(bf16[128,1024]{1,0:T(8,128)(2,1)S(1)} %collective-permute-done.4), channel_id=1, source_target_pairs={{8,12},{10,14},{9,13},{11,15},{24,28},{26,30},{25,29},{27,31}} | collective-permute-start | bytes 786440 | tf_op jit(solution)/shard_map/ppermute | solution.py:41
  88.7 5.1 %collective-permute-start.7 = (bf16[128,1024]{1,0:T(8,128)(2,1)}, bf16[128,1024]{1,0:T(8,128)(2,1)S(1)}, u32[]{:S(2)}, u32[]{:S(2)}) collective-permute-start(bf16[128,1024]{1,0:T(8,128)(2,1)} %collective-permute-done.3), channel_id=1, source_target_pairs={{6,4},{4,6},{10,8},{8,10},{14,12},{12,14},{7,5},{5,7},{11,9},{9,11... | collective-permute-start | bytes 786440 | tf_op jit(solution)/shard_map/ppermute | solution.py:46
  89.4 5.2 %collective-permute-start.8 = (bf16[128,1024]{1,0:T(8,128)(2,1)S(1)}, bf16[128,1024]{1,0:T(8,128)(2,1)S(1)}, u32[]{:S(2)}, u32[]{:S(2)}) collective-permute-start(bf16[128,1024]{1,0:T(8,128)(2,1)S(1)} %collective-permute-done.4), channel_id=1, source_target_pairs={{10,8},{8,10},{14,12},{12,14},{11,9},{9,11},{15,13},{13,15},{26,24... | collective-permute-start | bytes 786440 | tf_op jit(solution)/shard_map/ppermute | solution.py:46
  90.8 4.6 %collective-permute-start.9 = (bf16[128,1024]{1,0:T(8,128)(2,1)S(1)}, bf16[128,1024]{1,0:T(8,128)(2,1)S(1)}, u32[]{:S(2)}, u32[]{:S(2)}) collective-permute-start(bf16[128,1024]{1,0:T(8,128)(2,1)S(1)} %collective-permute-done.5), channel_id=1, source_target_pairs={{14,12},{12,14},{15,13},{13,15},{30,28},{28,30},{31,29},{29,31}} | collective-permute-start | bytes 786440 | tf_op jit(solution)/shard_map/ppermute | solution.py:46
  129.9 18.0 %collective-permute-start.28 = (bf16[128,1024]{0,1:T(8,128)(2,1)S(1)}, bf16[128,1024]{0,1:T(8,128)(2,1)S(1)}, u32[]{:S(2)}, u32[]{:S(2)}) collective-permute-start(bf16[128,1024]{0,1:T(8,128)(2,1)S(1)} %bitcast.150), channel_id=1, source_target_pairs={{12,14},{14,12},{13,15},{15,13},{28,30},{30,28},{29,31},{31,29}} | collective-permute-start | bytes 786440 | tf_op jit(solution)/shard_map/ppermute | solution.py:106
  130.7 21.0 %collective-permute-start.32 = (bf16[128,1024]{1,0:T(8,128)(2,1)S(1)}, bf16[128,1024]{1,0:T(8,128)(2,1)S(1)}, u32[]{:S(2)}, u32[]{:S(2)}) collective-permute-start(bf16[128,1024]{1,0:T(8,128)(2,1)S(1)} %copy-done.10), channel_id=1, source_target_pairs={{0,4},{2,6},{4,8},{6,10},{8,12},{10,14},{1,5},{3,7},{5,9},{7,11},{... | collective-permute-start | bytes 786440 | tf_op jit(solution)/shard_map/ppermute | solution.py:41
  147.2 5.2 %collective-permute-start.27 = (bf16[128,1024]{0,1:T(8,128)(2,1)S(1)}, bf16[128,1024]{0,1:T(8,128)(2,1)S(1)}, u32[]{:S(2)}, u32[]{:S(2)}) collective-permute-start(bf16[128,1024]{0,1:T(8,128)(2,1)S(1)} %bitcast.149), channel_id=1, source_target_pairs={{8,10},{10,8},{12,14},{14,12},{9,11},{11,9},{13,15},{15,13},{24,26... | collective-permute-start | bytes 786440 | tf_op jit(solution)/shard_map/ppermute | solution.py:106
  148.0 4.4 %collective-permute-start.29 = (bf16[128,1024]{0,1:T(8,128)(2,1)S(1)}, bf16[128,1024]{0,1:T(8,128)(2,1)S(1)}, u32[]{:S(2)}, u32[]{:S(2)}) collective-permute-start(bf16[128,1024]{0,1:T(8,128)(2,1)S(1)} %fusion.26), channel_id=1, source_target_pairs={{12,8},{14,10},{13,9},{15,11},{28,24},{30,26},{29,25},{31,27}} | collective-permute-start | bytes 786440 | tf_op jit(solution)/shard_map/ppermute | solution.py:114
  148.6 10.2 %collective-permute-start.26 = (bf16[128,1024]{0,1:T(8,128)(2,1)S(1)}, bf16[128,1024]{0,1:T(8,128)(2,1)S(1)}, u32[]{:S(2)}, u32[]{:S(2)}) collective-permute-start(bf16[128,1024]{0,1:T(8,128)(2,1)S(1)} %bitcast.148), channel_id=1, source_target_pairs={{4,6},{6,4},{8,10},{10,8},{12,14},{14,12},{5,7},{7,5},{9,11},{11,9... | collective-permute-start | bytes 786440 | tf_op jit(solution)/shard_map/ppermute | solution.py:106
  151.7 6.4 %collective-permute-start.33 = (bf16[128,1024]{1,0:T(8,128)(2,1)S(1)}, bf16[128,1024]{1,0:T(8,128)(2,1)S(1)}, u32[]{:S(2)}, u32[]{:S(2)}) collective-permute-start(bf16[128,1024]{1,0:T(8,128)(2,1)S(1)} %collective-permute-done.32), channel_id=1, source_target_pairs={{4,8},{6,10},{8,12},{10,14},{5,9},{7,11},{9,13},{11,15},{20,24},{2... | collective-permute-start | bytes 786440 | tf_op jit(solution)/shard_map/ppermute | solution.py:41
  152.5 7.0 %collective-permute-start.30 = (bf16[128,1024]{0,1:T(8,128)(2,1)S(1)}, bf16[128,1024]{0,1:T(8,128)(2,1)S(1)}, u32[]{:S(2)}, u32[]{:S(2)}) collective-permute-start(bf16[128,1024]{0,1:T(8,128)(2,1)S(1)} %fusion.28), channel_id=1, source_target_pairs={{8,4},{10,6},{12,8},{14,10},{9,5},{11,7},{13,9},{15,11},{24,20},{2... | collective-permute-start | bytes 786440 | tf_op jit(solution)/shard_map/ppermute | solution.py:114
  153.2 8.8 %collective-permute-start.35 = (bf16[128,1024]{1,0:T(8,128)(2,1)S(1)}, bf16[128,1024]{1,0:T(8,128)(2,1)S(1)}, u32[]{:S(2)}, u32[]{:S(2)}) collective-permute-start(bf16[128,1024]{1,0:T(8,128)(2,1)S(1)} %copy-done.10), channel_id=1, source_target_pairs={{0,2},{4,6},{8,10},{12,14},{1,3},{5,7},{9,11},{13,15},{16,18},{20,... | collective-permute-start | bytes 786440 | tf_op jit(solution)/shard_map/ppermute | solution.py:43
  156.8 14.8 %collective-permute-start.25 = (bf16[128,1024]{0,1:T(8,128)(2,1)S(1)}, bf16[128,1024]{0,1:T(8,128)(2,1)S(1)}, u32[]{:S(2)}, u32[]{:S(2)}) collective-permute-start(bf16[128,1024]{0,1:T(8,128)(2,1)S(1)} %bitcast.147), channel_id=1, source_target_pairs={{2,0},{6,4},{10,8},{14,12},{3,1},{7,5},{11,9},{15,13},{18,16},{22,... | collective-permute-start | bytes 786440 | tf_op jit(solution)/shard_map/ppermute | solution.py:103
  158.1 2.2 collective-permute-start.34
  158.8 3.9 %collective-permute-start.36 = (bf16[128,1024]{1,0:T(8,128)(2,1)S(1)}, bf16[128,1024]{1,0:T(8,128)(2,1)S(1)}, u32[]{:S(2)}, u32[]{:S(2)}) collective-permute-start(bf16[128,1024]{1,0:T(8,128)(2,1)S(1)} %collective-permute-done.32), channel_id=1, source_target_pairs={{6,4},{4,6},{10,8},{8,10},{14,12},{12,14},{7,5},{5,7},{11,9},{9,11... | collective-permute-start | bytes 786440 | tf_op jit(solution)/shard_map/ppermute | solution.py:46
  159.5 3.2 %collective-permute-start.37 = (bf16[128,1024]{1,0:T(8,128)(2,1)S(1)}, bf16[128,1024]{1,0:T(8,128)(2,1)S(1)}, u32[]{:S(2)}, u32[]{:S(2)}) collective-permute-start(bf16[128,1024]{1,0:T(8,128)(2,1)S(1)} %collective-permute-done.33), channel_id=1, source_target_pairs={{10,8},{8,10},{14,12},{12,14},{11,9},{9,11},{15,13},{13,15},{26,24... | collective-permute-start | bytes 786440 | tf_op jit(solution)/shard_map/ppermute | solution.py:46
  160.4 29.9 %collective-permute-start.31 = (bf16[128,1024]{0,1:T(8,128)(2,1)S(1)}, bf16[128,1024]{0,1:T(8,128)(2,1)S(1)}, u32[]{:S(2)}, u32[]{:S(2)}) collective-permute-start(bf16[128,1024]{0,1:T(8,128)(2,1)S(1)} %fusion.30), channel_id=1, source_target_pairs={{4,0},{6,2},{8,4},{10,6},{12,8},{14,10},{5,1},{7,3},{9,5},{11,7},{... | collective-permute-start | bytes 786440 | tf_op jit(solution)/shard_map/ppermute | solution.py:114
  195.2 23.4 %collective-permute-start.42 = (bf16[128,1024]{1,0:T(8,128)(2,1)}, bf16[128,1024]{1,0:T(8,128)(2,1)}, u32[]{:S(2)}, u32[]{:S(2)}) collective-permute-start(bf16[128,1024]{1,0:T(8,128)(2,1)} %copy.76), channel_id=1, source_target_pairs={{12,14},{14,12},{13,15},{15,13},{28,30},{30,28},{29,31},{31,29}} | collective-permute-start | bytes 786440 | tf_op jit(solution)/shard_map/ppermute | solution.py:106
  198.5 29.8 %collective-permute-start.41 = (bf16[128,1024]{1,0:T(8,128)(2,1)}, bf16[128,1024]{1,0:T(8,128)(2,1)}, u32[]{:S(2)}, u32[]{:S(2)}) collective-permute-start(bf16[128,1024]{1,0:T(8,128)(2,1)} %copy.74), channel_id=1, source_target_pairs={{8,10},{10,8},{12,14},{14,12},{9,11},{11,9},{13,15},{15,13},{24,26... | collective-permute-start | bytes 786440 | tf_op jit(solution)/shard_map/ppermute | solution.py:106
  201.6 72.2 %collective-permute-start.40 = (bf16[128,1024]{1,0:T(8,128)(2,1)}, bf16[128,1024]{1,0:T(8,128)(2,1)}, u32[]{:S(2)}, u32[]{:S(2)}) collective-permute-start(bf16[128,1024]{1,0:T(8,128)(2,1)} %copy.72), channel_id=1, source_target_pairs={{4,6},{6,4},{8,10},{10,8},{12,14},{14,12},{5,7},{7,5},{9,11},{11,9... | collective-permute-start | bytes 786440 | tf_op jit(solution)/shard_map/ppermute | solution.py:106
  204.8 80.5 %collective-permute-start.39 = (bf16[128,1024]{1,0:T(8,128)(2,1)}, bf16[128,1024]{1,0:T(8,128)(2,1)}, u32[]{:S(2)}, u32[]{:S(2)}) collective-permute-start(bf16[128,1024]{1,0:T(8,128)(2,1)} %copy.71), channel_id=1, source_target_pairs={{2,0},{6,4},{10,8},{14,12},{3,1},{7,5},{11,9},{15,13},{18,16},{22,... | collective-permute-start | bytes 786440 | tf_op jit(solution)/shard_map/ppermute | solution.py:103
  214.3 9.4 %collective-permute-start.46 = (f32[464,128]{1,0:T(8,128)}, f32[464,128]{1,0:T(8,128)}, u32[]{:S(2)}, u32[]{:S(2)}) collective-permute-start(f32[464,128]{1,0:T(8,128)} %maximum_bitcast_fusion), channel_id=1, source_target_pairs={{0,1},{1,0},{2,3},{3,2},{4,5},{5,4},{6,7},{7,6},{8,9},{9,8},{10,11... | collective-permute-start | bytes 712712 | tf_op jit(solution)/shard_map/ppermute | solution.py:19
  220.4 7.9 %collective-permute-start.43 = (bf16[128,1024]{1,0:T(8,128)(2,1)}, bf16[128,1024]{1,0:T(8,128)(2,1)S(1)}, u32[]{:S(2)}, u32[]{:S(2)}) collective-permute-start(bf16[128,1024]{1,0:T(8,128)(2,1)} %add_convert_fusion.3), channel_id=1, source_target_pairs={{12,8},{14,10},{13,9},{15,11},{28,24},{30,26},{29,25},{31,27}} | collective-permute-start | bytes 786440 | tf_op jit(solution)/shard_map/ppermute | solution.py:114
  224.9 9.9 %collective-permute-start.47 = (f32[464,128]{1,0:T(8,128)S(1)}, f32[464,128]{1,0:T(8,128)S(1)}, u32[]{:S(2)}, u32[]{:S(2)}) collective-permute-start(f32[464,128]{1,0:T(8,128)S(1)} %fusion.42), channel_id=1, source_target_pairs={{0,2},{2,0},{4,6},{6,4},{8,10},{10,8},{12,14},{14,12},{1,3},{3,1},... | collective-permute-start | bytes 712712 | tf_op jit(solution)/shard_map/ppermute | solution.py:19
  229.4 44.4 %collective-permute-start.44 = (bf16[128,1024]{1,0:T(8,128)(2,1)S(1)}, bf16[128,1024]{1,0:T(8,128)(2,1)S(1)}, u32[]{:S(2)}, u32[]{:S(2)}) collective-permute-start(bf16[128,1024]{1,0:T(8,128)(2,1)S(1)} %add_convert_fusion.2), channel_id=1, source_target_pairs={{8,4},{10,6},{12,8},{14,10},{9,5},{11,7},{13,9},{15,11},{24,20},{2... | collective-permute-start | bytes 786440 | tf_op jit(solution)/shard_map/ppermute | solution.py:114
  235.7 16.9 %collective-permute-start.48 = (f32[464,128]{1,0:T(8,128)S(1)}, f32[464,128]{1,0:T(8,128)S(1)}, u32[]{:S(2)}, u32[]{:S(2)}) collective-permute-start(f32[464,128]{1,0:T(8,128)S(1)} %fusion.71), channel_id=1, source_target_pairs={{0,4},{2,6},{4,0},{6,2},{8,12},{10,14},{12,8},{14,10},{1,5},{3,7},... | collective-permute-start | bytes 712712 | tf_op jit(solution)/shard_map/ppermute | solution.py:19
  252.7 30.4 %collective-permute-start.49 = (f32[464,128]{1,0:T(8,128)S(1)}, f32[464,128]{1,0:T(8,128)S(1)}, u32[]{:S(2)}, u32[]{:S(2)}) collective-permute-start(f32[464,128]{1,0:T(8,128)S(1)} %add.280), channel_id=1, source_target_pairs={{0,8},{2,10},{4,12},{6,14},{8,0},{10,2},{12,4},{14,6},{1,9},{3,11}... | collective-permute-start | bytes 712712 | tf_op jit(solution)/shard_map/ppermute | solution.py:19
  274.9 13.5 %collective-permute-start.45 = (bf16[128,1024]{1,0:T(8,128)(2,1)S(1)}, bf16[128,1024]{1,0:T(8,128)(2,1)S(1)}, u32[]{:S(2)}, u32[]{:S(2)}) collective-permute-start(bf16[128,1024]{1,0:T(8,128)(2,1)S(1)} %add_convert_fusion.1), channel_id=1, source_target_pairs={{4,0},{6,2},{8,4},{10,6},{12,8},{14,10},{5,1},{7,3},{9,5},{11,7},{... | collective-permute-start | bytes 786440 | tf_op jit(solution)/shard_map/ppermute | solution.py:114
  (26 other events, 399.3 us)

commit v13 on v9

--- a/solution.py
+++ b/solution.py
@@ -68,10 +68,10 @@
     owners.append(partner)
     valid.append(ctx_index >= 0)
     for step in range(1, levels):
-        got.append(lax.ppermute(ups[step - 1], "ctx", [(c ^ 1, c) for c in range(2 * step, count)]))
-        got.append(
-            lax.ppermute(downs[step - 1], "ctx", [(c ^ 1, c) for c in range(0, count - 2 * step)])
-        )
+        both = lax.ppermute(
+            jnp.concatenate([ups[step - 1], downs[step - 1]], 0), "ctx", [(c ^ 1, c) for c in range(count)]
+        )
+        got += [both[: block.shape[0]], both[block.shape[0] :]]
         owners += [partner - 2 * step, partner + 2 * step]
         valid += [ctx_index >= 2 * step, ctx_index < count - 2 * step]
     rows = block.shape[0]

time: 277 us -> 289 us (1.043)
  starting transfers between devices: 107 us -> 114 us
  waiting for transfers between devices: 75.7 us -> 79.6 us
    ppermute x6 -> x3, waiting for transfers between devices: 8.9 us -> 23.6 us  [tree_gather(): lax.ppermute(jnp.concatenate([ups[step - 1], downs[step - 1]], 0), 'ctx',...]
    ppermute x9, starting transfers between devices: 34.9 us -> 43.8 us  [from_partner(): lax.ppermute(shard, axis, [(i, i ^ 1 << stride) for i in range(lax.axis_s...]
    ppermute x6 -> x3, starting transfers between devices: 9.73 us -> 3.67 us  [tree_gather(): lax.ppermute(jnp.concatenate([ups[step - 1], downs[step - 1]], 0), 'ctx',...]
    ppermute x3, waiting for transfers between devices: 14.9 us -> 9.81 us  [tree_gather(): lax.ppermute(down, 'ctx', [(c + 2, c) for c in range(0, count - 2 * step)])]
    ppermute x9, waiting for transfers between devices: 24 us -> 20.2 us  [from_partner(): lax.ppermute(shard, axis, [(i, i ^ 1 << stride) for i in range(lax.axis_s...]
    ppermute x3, waiting for transfers between devices: 3.73 us -> 0.01 us  [tree_gather(): up = lax.ppermute(up, 'ctx', [(c - 2, c) for c in range(2 * step, count)])]
    unnamed x60 -> x58, local copies, waits for them, and re-layouts: 6.94 us -> 6.94 us
  transfers between devices with their start and end apart: 50 -> 47, of which waited for: 16 -> 14; matrix products, arithmetic and copies ran while one was open for 22% -> 21% of each run, Pallas kernels for 0% -> 0%
where the time goes in v13:
time: 289 us; the launch traced here: 288 us
  starting transfers between devices  114 us (39%)
  waiting for transfers between devices  79.6 us (28%)
  local copies, waits for them, and re-layouts  48.2 us (17%)
  matrix products  29.5 us (10%)
  other arithmetic  14.9 us (5%)
    ppermute x9, starting transfers between devices, from_partner(): lax.ppermute(shard, axis, [(i, i ^ 1 << stride) for i in range(lax.axis_s...  43.8 us
    ppermute x6, starting transfers between devices, tree_spread(): lax.ppermute(held, 'ctx', [(c - 2, c) for c in range(2 * step, count)])  28.6 us
    ppermute x3, waiting for transfers between devices, tree_gather(): lax.ppermute(jnp.concatenate([ups[step - 1], downs[step - 1]], 0), 'ctx',...  23.6 us
    ppermute x6, waiting for transfers between devices, tree_return(): lax.ppermute(acc.astype(jnp.bfloat16), 'ctx', [(c, c - 2) for c in range(...  23.3 us
    ppermute x9, waiting for transfers between devices, from_partner(): lax.ppermute(shard, axis, [(i, i ^ 1 << stride) for i in range(lax.axis_s...  20.2 us
    dynamic_update_slice x14, local copies, waits for them, and re-layouts, tree_gather(): whole = lax.dynamic_update_slice_in_dim(whole, piece, place, 0)  10.6 us
    ppermute x3, waiting for transfers between devices, tree_gather(): lax.ppermute(down, 'ctx', [(c + 2, c) for c in range(0, count - 2 * step)])  9.81 us
    unnamed x58, local copies, waits for them, and re-layouts  6.94 us
  transfers between devices with their start and end apart: 47, of which 14 were waited for; matrix products, arithmetic and copies ran while one was open for 21% of the time, Pallas kernels for 0%

profile of v13, /device:TPU:0, one launch (start us, length us, event | category | flops | bytes accessed | tf_op | source)
XLA Modules:
  0.0 287.7 jit_solution(12075926262089186523)
XLA Ops:
  0.7 1.8 broadcast_in_dim.58
  3.3 4.9 %collective-permute-start.10 = (bf16[336,512]{1,0:T(8,128)(2,1)S(1)}, bf16[336,512]{1,0:T(8,128)(2,1)S(1)}, u32[]{:S(2)}, u32[]{:S(2)}) collective-permute-start(bf16[336,512]{1,0:T(8,128)(2,1)S(1)} %get-tuple-element.29), channel_id=1, source_target_pairs={{0,4},{2,6},{4,8},{6,10},{8,12},{10,14},{1,5},{3,7},{5,9},{7,11},{... | collective-permute-start | bytes 1032200 | tf_op jit(solution)/shard_map/ppermute | solution.py:60
  9.5 1.6 collective-permute-start.16
  11.1 5.2 %collective-permute-start.3 = (bf16[128,1024]{1,0:T(8,128)(2,1)}, bf16[128,1024]{1,0:T(8,128)(2,1)}, u32[]{:S(2)}, u32[]{:S(2)}) collective-permute-start(bf16[128,1024]{1,0:T(8,128)(2,1)} %bitcast.4), channel_id=1, source_target_pairs={{0,4},{2,6},{4,8},{6,10},{8,12},{10,14},{1,5},{3,7},{5,9},{7,11},{... | collective-permute-start | bytes 786440 | tf_op jit(solution)/shard_map/ppermute | solution.py:41
  21.0 1.6 collective-permute-start.17
  24.8 6.2 %collective-permute-done.13 = bf16[336,512]{1,0:T(8,128)(2,1)S(1)} collective-permute-done((bf16[336,512]{1,0:T(8,128)(2,1)S(1)}, bf16[336,512]{1,0:T(8,128)(2,1)S(1)}, u32[]{:S(2)}, u32[]{:S(2)}) %collective-permute-start.13) | collective-permute-done | bytes 344096 | tf_op jit(solution)/shard_map/ppermute | solution.py:61
  33.8 3.4 %collective-permute-start.6 = (bf16[128,1024]{1,0:T(8,128)(2,1)}, bf16[128,1024]{1,0:T(8,128)(2,1)}, u32[]{:S(2)}, u32[]{:S(2)}) collective-permute-start(bf16[128,1024]{1,0:T(8,128)(2,1)} %bitcast.4), channel_id=1, source_target_pairs={{0,2},{4,6},{8,10},{12,14},{1,3},{5,7},{9,11},{13,15},{16,18},{20,... | collective-permute-start | bytes 786440 | tf_op jit(solution)/shard_map/ppermute | solution.py:43
  38.0 2.6 collective-permute-done.15
  41.7 1.7 collective-permute-start.18
  46.2 13.9 %collective-permute-done.18 = bf16[672,512]{1,0:T(8,128)(2,1)S(1)} collective-permute-done((bf16[672,512]{1,0:T(8,128)(2,1)S(1)}, bf16[672,512]{1,0:T(8,128)(2,1)S(1)}, u32[]{:S(2)}, u32[]{:S(2)}) %collective-permute-start.18) | collective-permute-done | bytes 688160 | tf_op jit(solution)/shard_map/ppermute | solution.py:71
  61.6 9.6 %collective-permute-done.19 = bf16[672,512]{1,0:T(8,128)(2,1)S(1)} collective-permute-done((bf16[672,512]{1,0:T(8,128)(2,1)S(1)}, bf16[672,512]{1,0:T(8,128)(2,1)S(1)}, u32[]{:S(2)}, u32[]{:S(2)}) %collective-permute-start.19) | collective-permute-done | bytes 688160 | tf_op jit(solution)/shard_map/ppermute | solution.py:71
  72.7 3.2 %broadcast_in_dim.57 = bf16[2688,1024]{1,0:T(8,128)(2,1)} broadcast(bf16[]{:T(256)} %constant.74.clone.1), dimensions={} | broadcast | bytes 5505026 | tf_op jit(solution)/shard_map/broadcast_in_dim | solution.py:157
  75.9 3.8 %fusion.35 = (bf16[2688,512]{1,0:T(8,128)(2,1)S(1)}, bf16[2688,1024]{1,0:T(8,128)(2,1)}) fusion(bf16[3024,512]{1,0:T(8,128)(2,1)} %slice_dynamic-update-slice_fusion, bf16[2688,1024]{1,0:T(8,128)(2,1)} %broadcast_in_dim.57, s32[]{:T(128)S(6)} %select_n.156), kind=kLoop, calls=%fused_computation.126 | loop fusion | bytes 8257540 | tf_op jit(solution)/shard_map/slice | solution.py:82
  81.1 2.0 copy.94
  83.2 2.5 collective-permute-start.1
  85.7 1.5 collective-permute-done.1
  87.2 7.7 %collective-permute-start.2 = (f32[16]{0:T(128)S(1)}, f32[16]{0:T(128)S(1)}, u32[]{:S(2)}, u32[]{:S(2)}) collective-permute-start(f32[16]{0:T(128)S(1)} %add.231), channel_id=1, source_target_pairs={{0,8},{2,10},{4,12},{6,14},{8,0},{10,2},{12,4},{14,6},{1,9},{3,11}... | collective-permute-start | bytes 200 | tf_op jit(solution)/shard_map/ppermute | solution.py:19
  94.9 1.5 collective-permute-done.2
  104.6 3.5 %constant_dynamic-update-slice_fusion.24 = bf16[2688,1024]{1,0:T(8,128)(2,1)} fusion(bf16[2688,1024]{1,0:T(8,128)(2,1)} %get-tuple-element.31, bf16[2688,512]{1,0:T(8,128)(2,1)} %collective-permute-done.20, s32[]{:T(128)S(6)} %select_n.185), kind=kLoop, calls=%fused_computation.93 | loop fusion | bytes 5505028 | tf_op jit(solution)/shard_map/dynamic_update_slice | solution.py:159
  108.1 4.9 %fusion.15 = bf16[128,1024]{0,1:T(8,128)(2,1)} fusion(f32[128,1024]{0,1:T(8,128)S(1)} %copy-done.2, bf16[2688,1024]{1,0:T(8,128)(2,1)} %constant_dynamic-update-slice_fusion.24, bf16[1,128,2688]{2,1,0:T(8,128)(2,1)S(1)} %copy-done), kind=kOutput, calls=%fused_computation.28 | convolution fusion | flops 704905216 | bytes 6979584 | tf_op jit(solution)/shard_map/dot_general | solution.py:168
  113.0 2.0 copy.95
  115.0 3.3 %copy.84 = bf16[1024,8,128,1]{0,2,3,1:T(8,128)(2,1)S(1)} copy(bf16[1024,8,128,1]{2,1,0,3:T(8,128)(2,1)} %bitcast.134) | data formatting | bytes 4194304 | tf_op jit(solution)/shard_map/reshape | solution.py:223
  118.3 5.7 %fusion.39 = (f32[8,2,128]{2,1,0:T(2,128)S(1)}, f32[8,2,128,1024]{2,3,1,0:T(8,128)}) fusion(pred[128,1024]{0,1:T(8,128)(4,1)S(1)} %copy-done.16, bf16[1024,8,128,1]{0,2,3,1:T(8,128)(2,1)S(1)} %copy.84, bf16[128,8,2,128]{0,3,2,1:T(8,128)(2,1)S(1)} %bitcast.138), kind=kOutput, calls=%fused_computation.130 | convolution fusion | flops 547357696 | bytes 11149312 | tf_op jit(solution)/shard_map/sub | solution.py:230
  124.1 5.0 %fusion.40 = (bf16[1024,8,128]{0,2,1:T(8,128)(2,1)S(1)}, f32[1024,8,128]{0,2,1:T(8,128)S(1)}) fusion(bf16[128,8,2,128]{3,2,1,0:T(2,128)(2,1)} %reshape_squeeze.7, f32[128]{0:T(128)S(1)} %get-tuple-element.25, f32[8,2,128,1024]{2,3,1,0:T(8,128)} %get-tuple-element.51, f32[8,2,128]{2,1,0:T(2,128)S(1)} %get-tuple-element.50), kind=kOutput, calls=%fused_computation.131 | convolution fusion | flops 544210944 | bytes 15213056 | tf_op jit(solution)/shard_map/jgtl,tjgd->ljd/dot_general | solution.py:244
  130.6 20.6 %collective-permute-start.29 = (bf16[128,1024]{0,1:T(8,128)(2,1)S(1)}, bf16[128,1024]{0,1:T(8,128)(2,1)S(1)}, u32[]{:S(2)}, u32[]{:S(2)}) collective-permute-start(bf16[128,1024]{0,1:T(8,128)(2,1)S(1)} %copy-done.6), channel_id=1, source_target_pairs={{0,4},{2,6},{4,8},{6,10},{8,12},{10,14},{1,5},{3,7},{5,9},{7,11},{... | collective-permute-start | bytes 786440 | tf_op jit(solution)/shard_map/ppermute | solution.py:41
  153.4 2.7 collective-permute-done.29
  157.6 3.3 %collective-permute-start.32 = (bf16[128,1024]{0,1:T(8,128)(2,1)S(1)}, bf16[128,1024]{0,1:T(8,128)(2,1)S(1)}, u32[]{:S(2)}, u32[]{:S(2)}) collective-permute-start(bf16[128,1024]{0,1:T(8,128)(2,1)S(1)} %copy-done.6), channel_id=1, source_target_pairs={{0,2},{4,6},{8,10},{12,14},{1,3},{5,7},{9,11},{13,15},{16,18},{20,... | collective-permute-start | bytes 786440 | tf_op jit(solution)/shard_map/ppermute | solution.py:43
  161.0 1.4 collective-permute-start.22
  167.5 1.9 fusion.1
  169.4 1.7 fusion.3
  172.1 3.5 %fusion.41 = (bf16[1024,8,128]{0,2,1:T(8,128)(2,1)S(1)}, f32[1024,8,128]{0,2,1:T(8,128)}) fusion(bf16[8,2,128,1024]{2,3,1,0:T(8,128)(2,1)S(1)} %fusion.3, bf16[128,8,2,128]{0,3,2,1:T(8,128)(2,1)S(1)} %bitcast.139), kind=kOutput, calls=%fused_computation.132 | convolution fusion | flops 537919488 | bytes 11010048 | tf_op jit(solution)/shard_map/jgtl,tjgd->ljd/dot_general | solution.py:240
  175.6 21.6 %collective-permute-done.28 = bf16[128,1024]{0,1:T(8,128)(2,1)S(1)} collective-permute-done((bf16[128,1024]{0,1:T(8,128)(2,1)S(1)}, bf16[128,1024]{0,1:T(8,128)(2,1)S(1)}, u32[]{:S(2)}, u32[]{:S(2)}) %collective-permute-start.28) | collective-permute-done | bytes 262176 | tf_op jit(solution)/shard_map/ppermute | solution.py:114
  200.8 1.4 collective-permute-start.39
  203.0 1.4 collective-permute-start.38
  207.2 1.9 add_convert_fusion.3
  209.0 1.4 collective-permute-start.40
  214.0 1.8 copy.69
  215.8 1.4 collective-permute-start.37
  220.3 2.7 collective-permute-start.44
  224.9 9.1 %collective-permute-done.44 = f32[464,128]{1,0:T(8,128)S(1)} collective-permute-done((f32[464,128]{1,0:T(8,128)S(1)}, f32[464,128]{1,0:T(8,128)S(1)}, u32[]{:S(2)}, u32[]{:S(2)}) %collective-permute-start.44) | collective-permute-done | bytes 237600 | tf_op jit(solution)/shard_map/ppermute | solution.py:19
  234.9 11.6 %collective-permute-start.45 = (f32[464,128]{1,0:T(8,128)S(1)}, f32[464,128]{1,0:T(8,128)S(1)}, u32[]{:S(2)}, u32[]{:S(2)}) collective-permute-start(f32[464,128]{1,0:T(8,128)S(1)} %fusion.64), channel_id=1, source_target_pairs={{0,4},{2,6},{4,0},{6,2},{8,12},{10,14},{12,8},{14,10},{1,5},{3,7},... | collective-permute-start | bytes 712712 | tf_op jit(solution)/shard_map/ppermute | solution.py:19
  246.9 5.4 %collective-permute-done.45 = f32[464,128]{1,0:T(8,128)S(1)} collective-permute-done((f32[464,128]{1,0:T(8,128)S(1)}, f32[464,128]{1,0:T(8,128)S(1)}, u32[]{:S(2)}, u32[]{:S(2)}) %collective-permute-start.45) | collective-permute-done | bytes 237600 | tf_op jit(solution)/shard_map/ppermute | solution.py:19
  252.4 18.9 %collective-permute-start.46 = (f32[464,128]{1,0:T(8,128)S(1)}, f32[464,128]{1,0:T(8,128)S(1)}, u32[]{:S(2)}, u32[]{:S(2)}) collective-permute-start(f32[464,128]{1,0:T(8,128)S(1)} %add.274), channel_id=1, source_target_pairs={{0,8},{2,10},{4,12},{6,14},{8,0},{10,2},{12,4},{14,6},{1,9},{3,11}... | collective-permute-start | bytes 712712 | tf_op jit(solution)/shard_map/ppermute | solution.py:19
  271.3 1.8 add_convert_fusion.1
  274.3 5.3 %fusion.11 = bf16[1,128,2688]{2,1,0:T(8,128)(2,1)} fusion(f32[128,2688]{1,0:T(8,128)S(1)} %convolution_multiply_fusion, bf16[128,1024]{0,1:T(8,128)(2,1)S(1)} %fusion.27, bf16[2688,1024]{1,0:T(8,128)(2,1)} %constant_dynamic-update-slice_fusion.24), kind=kOutput, calls=%fused_computation.19 | convolution fusion | flops 705331200 | bytes 7831552 | tf_op jit(solution)/shard_map/tk,dk->td/dot_general | solution.py:269
  279.7 2.4 collective-permute-done.46
  284.3 1.6 collective-permute-done.42
  285.9 1.8 fusion.31
  (200 shorter events, 60.1 us)
Async XLA Ops:
  0.6 79.0 %copy-start = (bf16[1,128,2688]{2,1,0:T(8,128)(2,1)S(1)}, bf16[1,128,2688]{2,1,0:T(8,128)(2,1)}, u32[]{:S(2)}) copy-start(bf16[1,128,2688]{2,1,0:T(8,128)(2,1)} %param.10) | copy-start | bytes 2064388
  3.3 14.7 %collective-permute-start.10 = (bf16[336,512]{1,0:T(8,128)(2,1)S(1)}, bf16[336,512]{1,0:T(8,128)(2,1)S(1)}, u32[]{:S(2)}, u32[]{:S(2)}) collective-permute-start(bf16[336,512]{1,0:T(8,128)(2,1)S(1)} %get-tuple-element.29), channel_id=1, source_target_pairs={{0,4},{2,6},{4,8},{6,10},{8,12},{10,14},{1,5},{3,7},{5,9},{7,11},{... | collective-permute-start | bytes 1032200 | tf_op jit(solution)/shard_map/ppermute | solution.py:60
  8.2 11.4 %collective-permute-start.11 = (bf16[336,512]{1,0:T(8,128)(2,1)S(1)}, bf16[336,512]{1,0:T(8,128)(2,1)S(1)}, u32[]{:S(2)}, u32[]{:S(2)}) collective-permute-start(bf16[336,512]{1,0:T(8,128)(2,1)S(1)} %get-tuple-element.29), channel_id=1, source_target_pairs={{4,0},{6,2},{8,4},{10,6},{12,8},{14,10},{5,1},{7,3},{9,5},{11,7},{... | collective-permute-start | bytes 1032200 | tf_op jit(solution)/shard_map/ppermute | solution.py:61
  9.5 32.2 %collective-permute-start.16 = (bf16[336,512]{1,0:T(8,128)(2,1)S(1)}, bf16[336,512]{1,0:T(8,128)(2,1)S(1)}, u32[]{:S(2)}, u32[]{:S(2)}) collective-permute-start(bf16[336,512]{1,0:T(8,128)(2,1)S(1)} %get-tuple-element.29), channel_id=1, source_target_pairs={{2,0},{0,2},{6,4},{4,6},{10,8},{8,10},{14,12},{12,14},{3,1},{1,3},... | collective-permute-start | bytes 1032200 | tf_op jit(solution)/shard_map/ppermute | solution.py:67
  11.1 85.6 %collective-permute-start.3 = (bf16[128,1024]{1,0:T(8,128)(2,1)}, bf16[128,1024]{1,0:T(8,128)(2,1)}, u32[]{:S(2)}, u32[]{:S(2)}) collective-permute-start(bf16[128,1024]{1,0:T(8,128)(2,1)} %bitcast.4), channel_id=1, source_target_pairs={{0,4},{2,6},{4,8},{6,10},{8,12},{10,14},{1,5},{3,7},{5,9},{7,11},{... | collective-permute-start | bytes 786440 | tf_op jit(solution)/shard_map/ppermute | solution.py:41
  18.0 6.1 %collective-permute-start.12 = (bf16[336,512]{1,0:T(8,128)(2,1)S(1)}, bf16[336,512]{1,0:T(8,128)(2,1)S(1)}, u32[]{:S(2)}, u32[]{:S(2)}) collective-permute-start(bf16[336,512]{1,0:T(8,128)(2,1)S(1)} %collective-permute-done.10), channel_id=1, source_target_pairs={{4,8},{6,10},{8,12},{10,14},{5,9},{7,11},{9,13},{11,15},{20,24},{2... | collective-permute-start | bytes 1032200 | tf_op jit(solution)/shard_map/ppermute | solution.py:60
  19.7 11.3 %collective-permute-start.13 = (bf16[336,512]{1,0:T(8,128)(2,1)S(1)}, bf16[336,512]{1,0:T(8,128)(2,1)S(1)}, u32[]{:S(2)}, u32[]{:S(2)}) collective-permute-start(bf16[336,512]{1,0:T(8,128)(2,1)S(1)} %collective-permute-done.11), channel_id=1, source_target_pairs={{4,0},{6,2},{8,4},{10,6},{5,1},{7,3},{9,5},{11,7},{20,16},{22,18},... | collective-permute-start | bytes 1032200 | tf_op jit(solution)/shard_map/ppermute | solution.py:61
  21.0 23.2 %collective-permute-start.17 = (bf16[672,512]{1,0:T(8,128)(2,1)S(1)}, bf16[672,512]{1,0:T(8,128)(2,1)S(1)}, u32[]{:S(2)}, u32[]{:S(2)}) collective-permute-start(bf16[672,512]{1,0:T(8,128)(2,1)S(1)} %pad_maximum_fusion), channel_id=1, source_target_pairs={{2,0},{0,2},{6,4},{4,6},{10,8},{8,10},{14,12},{12,14},{3,1},{1,3},... | collective-permute-start | bytes 2064392 | tf_op jit(solution)/shard_map/ppermute | solution.py:71
  24.1 9.8 %collective-permute-start.14 = (bf16[336,512]{1,0:T(8,128)(2,1)S(1)}, bf16[336,512]{1,0:T(8,128)(2,1)S(1)}, u32[]{:S(2)}, u32[]{:S(2)}) collective-permute-start(bf16[336,512]{1,0:T(8,128)(2,1)S(1)} %collective-permute-done.12), channel_id=1, source_target_pairs={{8,12},{10,14},{9,13},{11,15},{24,28},{26,30},{25,29},{27,31}} | collective-permute-start | bytes 1032200 | tf_op jit(solution)/shard_map/ppermute | solution.py:60
  31.0 9.6 %collective-permute-start.15 = (bf16[336,512]{1,0:T(8,128)(2,1)S(1)}, bf16[336,512]{1,0:T(8,128)(2,1)S(1)}, u32[]{:S(2)}, u32[]{:S(2)}) collective-permute-start(bf16[336,512]{1,0:T(8,128)(2,1)S(1)} %collective-permute-done.13), channel_id=1, source_target_pairs={{4,0},{6,2},{5,1},{7,3},{20,16},{22,18},{21,17},{23,19}} | collective-permute-start | bytes 1032200 | tf_op jit(solution)/shard_map/ppermute | solution.py:61
  33.8 68.6 %collective-permute-start.6 = (bf16[128,1024]{1,0:T(8,128)(2,1)}, bf16[128,1024]{1,0:T(8,128)(2,1)}, u32[]{:S(2)}, u32[]{:S(2)}) collective-permute-start(bf16[128,1024]{1,0:T(8,128)(2,1)} %bitcast.4), channel_id=1, source_target_pairs={{0,2},{4,6},{8,10},{12,14},{1,3},{5,7},{9,11},{13,15},{16,18},{20,... | collective-permute-start | bytes 786440 | tf_op jit(solution)/shard_map/ppermute | solution.py:43
  40.6 42.5 %collective-permute-start = (f32[16]{0:T(128)S(1)}, f32[16]{0:T(128)S(1)}, u32[]{:S(2)}, u32[]{:S(2)}) collective-permute-start(f32[16]{0:T(128)S(1)} %pad_maximum_fusion.3), channel_id=1, source_target_pairs={{0,2},{2,0},{4,6},{6,4},{8,10},{10,8},{12,14},{14,12},{1,3},{3,1},... | collective-permute-start | bytes 200 | tf_op jit(solution)/shard_map/ppermute | solution.py:19
  41.7 18.4 %collective-permute-start.18 = (bf16[672,512]{1,0:T(8,128)(2,1)S(1)}, bf16[672,512]{1,0:T(8,128)(2,1)S(1)}, u32[]{:S(2)}, u32[]{:S(2)}) collective-permute-start(bf16[672,512]{1,0:T(8,128)(2,1)S(1)} %pad_maximum_fusion.1), channel_id=1, source_target_pairs={{2,0},{0,2},{6,4},{4,6},{10,8},{8,10},{14,12},{12,14},{3,1},{1,3},... | collective-permute-start | bytes 2064392 | tf_op jit(solution)/shard_map/ppermute | solution.py:71
  44.2 27.0 %collective-permute-start.19 = (bf16[672,512]{1,0:T(8,128)(2,1)S(1)}, bf16[672,512]{1,0:T(8,128)(2,1)S(1)}, u32[]{:S(2)}, u32[]{:S(2)}) collective-permute-start(bf16[672,512]{1,0:T(8,128)(2,1)S(1)} %pad_maximum_fusion.2), channel_id=1, source_target_pairs={{2,0},{0,2},{6,4},{4,6},{10,8},{8,10},{14,12},{12,14},{3,1},{1,3},... | collective-permute-start | bytes 2064392 | tf_op jit(solution)/shard_map/ppermute | solution.py:71
  79.6 25.0 %collective-permute-start.20 = (bf16[2688,512]{1,0:T(8,128)(2,1)S(1)}, bf16[2688,512]{1,0:T(8,128)(2,1)}, u32[]{:S(2)}, u32[]{:S(2)}) collective-permute-start(bf16[2688,512]{1,0:T(8,128)(2,1)S(1)} %get-tuple-element.30), channel_id=1, source_target_pairs={{0,1},{1,0},{2,3},{3,2},{4,5},{5,4},{6,7},{7,6},{8,9},{9,8},{10,11... | collective-permute-start | bytes 8257544 | tf_op jit(solution)/shard_map/ppermute | solution.py:19
  83.2 4.0 %collective-permute-start.1 = (f32[16]{0:T(128)S(1)}, f32[16]{0:T(128)S(1)}, u32[]{:S(2)}, u32[]{:S(2)}) collective-permute-start(f32[16]{0:T(128)S(1)} %fusion.65), channel_id=1, source_target_pairs={{0,4},{2,6},{4,0},{6,2},{8,12},{10,14},{12,8},{14,10},{1,5},{3,7},... | collective-permute-start | bytes 200 | tf_op jit(solution)/shard_map/ppermute | solution.py:19
  87.2 9.2 %collective-permute-start.2 = (f32[16]{0:T(128)S(1)}, f32[16]{0:T(128)S(1)}, u32[]{:S(2)}, u32[]{:S(2)}) collective-permute-start(f32[16]{0:T(128)S(1)} %add.231), channel_id=1, source_target_pairs={{0,8},{2,10},{4,12},{6,14},{8,0},{10,2},{12,4},{14,6},{1,9},{3,11}... | collective-permute-start | bytes 200 | tf_op jit(solution)/shard_map/ppermute | solution.py:19
  96.5 1.1 collective-permute-start.21
  96.7 1.1 collective-permute-start.4
  97.8 3.9 %collective-permute-start.5 = (bf16[128,1024]{1,0:T(8,128)(2,1)S(1)}, bf16[128,1024]{1,0:T(8,128)(2,1)S(1)}, u32[]{:S(2)}, u32[]{:S(2)}) collective-permute-start(bf16[128,1024]{1,0:T(8,128)(2,1)S(1)} %collective-permute-done.4), channel_id=1, source_target_pairs={{8,12},{10,14},{9,13},{11,15},{24,28},{26,30},{25,29},{27,31}} | collective-permute-start | bytes 786440 | tf_op jit(solution)/shard_map/ppermute | solution.py:41
  100.3 3.1 %collective-permute-start.7 = (bf16[128,1024]{1,0:T(8,128)(2,1)}, bf16[128,1024]{1,0:T(8,128)(2,1)S(1)}, u32[]{:S(2)}, u32[]{:S(2)}) collective-permute-start(bf16[128,1024]{1,0:T(8,128)(2,1)} %collective-permute-done.3), channel_id=1, source_target_pairs={{6,4},{4,6},{10,8},{8,10},{14,12},{12,14},{7,5},{5,7},{11,9},{9,11... | collective-permute-start | bytes 786440 | tf_op jit(solution)/shard_map/ppermute | solution.py:46
  101.0 2.5 collective-permute-start.8
  101.7 1.8 collective-permute-start.9
  129.6 22.3 %collective-permute-start.25 = (bf16[128,1024]{0,1:T(8,128)(2,1)S(1)}, bf16[128,1024]{0,1:T(8,128)(2,1)S(1)}, u32[]{:S(2)}, u32[]{:S(2)}) collective-permute-start(bf16[128,1024]{0,1:T(8,128)(2,1)S(1)} %bitcast.150), channel_id=1, source_target_pairs={{12,14},{14,12},{13,15},{15,13},{28,30},{30,28},{29,31},{31,29}} | collective-permute-start | bytes 786440 | tf_op jit(solution)/shard_map/ppermute | solution.py:106
  130.6 25.5 %collective-permute-start.29 = (bf16[128,1024]{0,1:T(8,128)(2,1)S(1)}, bf16[128,1024]{0,1:T(8,128)(2,1)S(1)}, u32[]{:S(2)}, u32[]{:S(2)}) collective-permute-start(bf16[128,1024]{0,1:T(8,128)(2,1)S(1)} %copy-done.6), channel_id=1, source_target_pairs={{0,4},{2,6},{4,8},{6,10},{8,12},{10,14},{1,5},{3,7},{5,9},{7,11},{... | collective-permute-start | bytes 786440 | tf_op jit(solution)/shard_map/ppermute | solution.py:41
  151.2 5.6 %collective-permute-start.24 = (bf16[128,1024]{0,1:T(8,128)(2,1)S(1)}, bf16[128,1024]{0,1:T(8,128)(2,1)S(1)}, u32[]{:S(2)}, u32[]{:S(2)}) collective-permute-start(bf16[128,1024]{0,1:T(8,128)(2,1)S(1)} %bitcast.149), channel_id=1, source_target_pairs={{8,10},{10,8},{12,14},{14,12},{9,11},{11,9},{13,15},{15,13},{24,26... | collective-permute-start | bytes 786440 | tf_op jit(solution)/shard_map/ppermute | solution.py:106
  152.0 4.8 %collective-permute-start.26 = (bf16[128,1024]{0,1:T(8,128)(2,1)S(1)}, bf16[128,1024]{0,1:T(8,128)(2,1)S(1)}, u32[]{:S(2)}, u32[]{:S(2)}) collective-permute-start(bf16[128,1024]{0,1:T(8,128)(2,1)S(1)} %fusion.22), channel_id=1, source_target_pairs={{12,8},{14,10},{13,9},{15,11},{28,24},{30,26},{29,25},{31,27}} | collective-permute-start | bytes 786440 | tf_op jit(solution)/shard_map/ppermute | solution.py:114
  152.7 10.6 %collective-permute-start.23 = (bf16[128,1024]{0,1:T(8,128)(2,1)S(1)}, bf16[128,1024]{0,1:T(8,128)(2,1)S(1)}, u32[]{:S(2)}, u32[]{:S(2)}) collective-permute-start(bf16[128,1024]{0,1:T(8,128)(2,1)S(1)} %bitcast.148), channel_id=1, source_target_pairs={{4,6},{6,4},{8,10},{10,8},{12,14},{14,12},{5,7},{7,5},{9,11},{11,9... | collective-permute-start | bytes 786440 | tf_op jit(solution)/shard_map/ppermute | solution.py:106
  156.1 6.4 %collective-permute-start.30 = (bf16[128,1024]{0,1:T(8,128)(2,1)S(1)}, bf16[128,1024]{0,1:T(8,128)(2,1)S(1)}, u32[]{:S(2)}, u32[]{:S(2)}) collective-permute-start(bf16[128,1024]{0,1:T(8,128)(2,1)S(1)} %collective-permute-done.29), channel_id=1, source_target_pairs={{4,8},{6,10},{8,12},{10,14},{5,9},{7,11},{9,13},{11,15},{20,24},{2... | collective-permute-start | bytes 786440 | tf_op jit(solution)/shard_map/ppermute | solution.py:41
  156.9 7.1 %collective-permute-start.27 = (bf16[128,1024]{0,1:T(8,128)(2,1)S(1)}, bf16[128,1024]{0,1:T(8,128)(2,1)S(1)}, u32[]{:S(2)}, u32[]{:S(2)}) collective-permute-start(bf16[128,1024]{0,1:T(8,128)(2,1)S(1)} %fusion.24), channel_id=1, source_target_pairs={{8,4},{10,6},{12,8},{14,10},{9,5},{11,7},{13,9},{15,11},{24,20},{2... | collective-permute-start | bytes 786440 | tf_op jit(solution)/shard_map/ppermute | solution.py:114
  157.6 8.7 %collective-permute-start.32 = (bf16[128,1024]{0,1:T(8,128)(2,1)S(1)}, bf16[128,1024]{0,1:T(8,128)(2,1)S(1)}, u32[]{:S(2)}, u32[]{:S(2)}) collective-permute-start(bf16[128,1024]{0,1:T(8,128)(2,1)S(1)} %copy-done.6), channel_id=1, source_target_pairs={{0,2},{4,6},{8,10},{12,14},{1,3},{5,7},{9,11},{13,15},{16,18},{20,... | collective-permute-start | bytes 786440 | tf_op jit(solution)/shard_map/ppermute | solution.py:43
  161.0 14.6 %collective-permute-start.22 = (bf16[128,1024]{0,1:T(8,128)(2,1)S(1)}, bf16[128,1024]{0,1:T(8,128)(2,1)S(1)}, u32[]{:S(2)}, u32[]{:S(2)}) collective-permute-start(bf16[128,1024]{0,1:T(8,128)(2,1)S(1)} %bitcast.147), channel_id=1, source_target_pairs={{2,0},{6,4},{10,8},{14,12},{3,1},{7,5},{11,9},{15,13},{18,16},{22,... | collective-permute-start | bytes 786440 | tf_op jit(solution)/shard_map/ppermute | solution.py:103
  162.6 2.3 collective-permute-start.31
  163.3 3.7 %collective-permute-start.33 = (bf16[128,1024]{0,1:T(8,128)(2,1)S(1)}, bf16[128,1024]{0,1:T(8,128)(2,1)S(1)}, u32[]{:S(2)}, u32[]{:S(2)}) collective-permute-start(bf16[128,1024]{0,1:T(8,128)(2,1)S(1)} %collective-permute-done.29), channel_id=1, source_target_pairs={{6,4},{4,6},{10,8},{8,10},{14,12},{12,14},{7,5},{5,7},{11,9},{9,11... | collective-permute-start | bytes 786440 | tf_op jit(solution)/shard_map/ppermute | solution.py:46
  164.0 3.1 %collective-permute-start.34 = (bf16[128,1024]{0,1:T(8,128)(2,1)S(1)}, bf16[128,1024]{0,1:T(8,128)(2,1)S(1)}, u32[]{:S(2)}, u32[]{:S(2)}) collective-permute-start(bf16[128,1024]{0,1:T(8,128)(2,1)S(1)} %collective-permute-done.30), channel_id=1, source_target_pairs={{10,8},{8,10},{14,12},{12,14},{11,9},{9,11},{15,13},{13,15},{26,24... | collective-permute-start | bytes 786440 | tf_op jit(solution)/shard_map/ppermute | solution.py:46
  164.9 32.4 %collective-permute-start.28 = (bf16[128,1024]{0,1:T(8,128)(2,1)S(1)}, bf16[128,1024]{0,1:T(8,128)(2,1)S(1)}, u32[]{:S(2)}, u32[]{:S(2)}) collective-permute-start(bf16[128,1024]{0,1:T(8,128)(2,1)S(1)} %fusion.26), channel_id=1, source_target_pairs={{4,0},{6,2},{8,4},{10,6},{12,8},{14,10},{5,1},{7,3},{9,5},{11,7},{... | collective-permute-start | bytes 786440 | tf_op jit(solution)/shard_map/ppermute | solution.py:114
  166.3 1.0 collective-permute-start.35
  200.8 6.4 %collective-permute-start.39 = (bf16[128,1024]{1,0:T(8,128)(2,1)}, bf16[128,1024]{1,0:T(8,128)(2,1)}, u32[]{:S(2)}, u32[]{:S(2)}) collective-permute-start(bf16[128,1024]{1,0:T(8,128)(2,1)} %copy.73), channel_id=1, source_target_pairs={{12,14},{14,12},{13,15},{15,13},{28,30},{30,28},{29,31},{31,29}} | collective-permute-start | bytes 786440 | tf_op jit(solution)/shard_map/ppermute | solution.py:106
  203.0 20.0 %collective-permute-start.38 = (bf16[128,1024]{1,0:T(8,128)(2,1)}, bf16[128,1024]{1,0:T(8,128)(2,1)}, u32[]{:S(2)}, u32[]{:S(2)}) collective-permute-start(bf16[128,1024]{1,0:T(8,128)(2,1)} %copy.71), channel_id=1, source_target_pairs={{8,10},{10,8},{12,14},{14,12},{9,11},{11,9},{13,15},{15,13},{24,26... | collective-permute-start | bytes 786440 | tf_op jit(solution)/shard_map/ppermute | solution.py:106
  206.2 13.2 %collective-permute-start.43 = (f32[464,128]{1,0:T(8,128)}, f32[464,128]{1,0:T(8,128)}, u32[]{:S(2)}, u32[]{:S(2)}) collective-permute-start(f32[464,128]{1,0:T(8,128)} %maximum_bitcast_fusion), channel_id=1, source_target_pairs={{0,1},{1,0},{2,3},{3,2},{4,5},{5,4},{6,7},{7,6},{8,9},{9,8},{10,11... | collective-permute-start | bytes 712712 | tf_op jit(solution)/shard_map/ppermute | solution.py:19
  209.0 14.0 %collective-permute-start.40 = (bf16[128,1024]{1,0:T(8,128)(2,1)}, bf16[128,1024]{1,0:T(8,128)(2,1)}, u32[]{:S(2)}, u32[]{:S(2)}) collective-permute-start(bf16[128,1024]{1,0:T(8,128)(2,1)} %add_convert_fusion.3), channel_id=1, source_target_pairs={{12,8},{14,10},{13,9},{15,11},{28,24},{30,26},{29,25},{31,27}} | collective-permute-start | bytes 786440 | tf_op jit(solution)/shard_map/ppermute | solution.py:114
  215.8 55.4 %collective-permute-start.37 = (bf16[128,1024]{1,0:T(8,128)(2,1)}, bf16[128,1024]{1,0:T(8,128)(2,1)}, u32[]{:S(2)}, u32[]{:S(2)}) collective-permute-start(bf16[128,1024]{1,0:T(8,128)(2,1)} %copy.69), channel_id=1, source_target_pairs={{4,6},{6,4},{8,10},{10,8},{12,14},{14,12},{5,7},{7,5},{9,11},{11,9... | collective-permute-start | bytes 786440 | tf_op jit(solution)/shard_map/ppermute | solution.py:106
  218.1 66.2 %collective-permute-start.36 = (bf16[128,1024]{1,0:T(8,128)(2,1)}, bf16[128,1024]{1,0:T(8,128)(2,1)S(1)}, u32[]{:S(2)}, u32[]{:S(2)}) collective-permute-start(bf16[128,1024]{1,0:T(8,128)(2,1)} %copy.68), channel_id=1, source_target_pairs={{2,0},{6,4},{10,8},{14,12},{3,1},{7,5},{11,9},{15,13},{18,16},{22,... | collective-permute-start | bytes 786440 | tf_op jit(solution)/shard_map/ppermute | solution.py:103
  220.3 13.6 %collective-permute-start.44 = (f32[464,128]{1,0:T(8,128)S(1)}, f32[464,128]{1,0:T(8,128)S(1)}, u32[]{:S(2)}, u32[]{:S(2)}) collective-permute-start(f32[464,128]{1,0:T(8,128)S(1)} %fusion.34), channel_id=1, source_target_pairs={{0,2},{2,0},{4,6},{6,4},{8,10},{10,8},{12,14},{14,12},{1,3},{3,1},... | collective-permute-start | bytes 712712 | tf_op jit(solution)/shard_map/ppermute | solution.py:19
  224.2 47.1 %collective-permute-start.41 = (bf16[128,1024]{1,0:T(8,128)(2,1)S(1)}, bf16[128,1024]{1,0:T(8,128)(2,1)S(1)}, u32[]{:S(2)}, u32[]{:S(2)}) collective-permute-start(bf16[128,1024]{1,0:T(8,128)(2,1)S(1)} %add_convert_fusion.2), channel_id=1, source_target_pairs={{8,4},{10,6},{12,8},{14,10},{9,5},{11,7},{13,9},{15,11},{24,20},{2... | collective-permute-start | bytes 786440 | tf_op jit(solution)/shard_map/ppermute | solution.py:114
  234.9 17.4 %collective-permute-start.45 = (f32[464,128]{1,0:T(8,128)S(1)}, f32[464,128]{1,0:T(8,128)S(1)}, u32[]{:S(2)}, u32[]{:S(2)}) collective-permute-start(f32[464,128]{1,0:T(8,128)S(1)} %fusion.64), channel_id=1, source_target_pairs={{0,4},{2,6},{4,0},{6,2},{8,12},{10,14},{12,8},{14,10},{1,5},{3,7},... | collective-permute-start | bytes 712712 | tf_op jit(solution)/shard_map/ppermute | solution.py:19
  252.4 29.7 %collective-permute-start.46 = (f32[464,128]{1,0:T(8,128)S(1)}, f32[464,128]{1,0:T(8,128)S(1)}, u32[]{:S(2)}, u32[]{:S(2)}) collective-permute-start(f32[464,128]{1,0:T(8,128)S(1)} %add.274), channel_id=1, source_target_pairs={{0,8},{2,10},{4,12},{6,14},{8,0},{10,2},{12,4},{14,6},{1,9},{3,11}... | collective-permute-start | bytes 712712 | tf_op jit(solution)/shard_map/ppermute | solution.py:19
  273.0 12.9 %collective-permute-start.42 = (bf16[128,1024]{1,0:T(8,128)(2,1)}, bf16[128,1024]{1,0:T(8,128)(2,1)}, u32[]{:S(2)}, u32[]{:S(2)}) collective-permute-start(bf16[128,1024]{1,0:T(8,128)(2,1)} %add_convert_fusion.1), channel_id=1, source_target_pairs={{4,0},{6,2},{8,4},{10,6},{12,8},{14,10},{5,1},{7,3},{9,5},{11,7},{... | collective-permute-start | bytes 786440 | tf_op jit(solution)/shard_map/ppermute | solution.py:114
  (19 other events, 185.4 us)

commit v14 on v9

--- a/solution.py
+++ b/solution.py
@@ -278,7 +278,7 @@
     )
     down_size = down_factor.size
     flat = jnp.concatenate([down_factor.reshape(-1), up_factor.reshape(-1)], 0)
-    flat = butterfly_sum(flat.reshape(-1, HEAD_SIZE), ("pair", "ctx")).reshape(-1)
+    flat = butterfly_sum(flat.reshape(-1, HEAD_SIZE), ("ctx", "pair")).reshape(-1)
     down_gradient = flat[:down_size].reshape(down_factor.shape)
     up_gradient = flat[down_size:].reshape(up_factor.shape)
     return (input_grad[None], query_grad[None], key_grad[None], down_gradient, up_gradient)

time: 277 us -> 269 us (0.971)
  waiting for transfers between devices: 75.7 us -> 67.1 us
    ppermute x9, waiting for transfers between devices: 24 us -> 15.1 us  [from_partner(): lax.ppermute(shard, axis, [(i, i ^ 1 << stride) for i in range(lax.axis_s...]
  transfers between devices with their start and end apart: 50 -> 50, of which waited for: 16 -> 15; matrix products, arithmetic and copies ran while one was open for 22% -> 23% of each run, Pallas kernels for 0% -> 0%
where the time goes in v14:
time: 269 us; the launch traced here: 267 us
  starting transfers between devices  107 us (40%)
  waiting for transfers between devices  67.1 us (25%)
  local copies, waits for them, and re-layouts  47.5 us (18%)
  matrix products  29.5 us (11%)
  other arithmetic  14.8 us (6%)
    ppermute x9, starting transfers between devices, from_partner(): lax.ppermute(shard, axis, [(i, i ^ 1 << stride) for i in range(lax.axis_s...  34.9 us
    ppermute x6, starting transfers between devices, tree_spread(): lax.ppermute(held, 'ctx', [(c - 2, c) for c in range(2 * step, count)])  27 us
    ppermute x6, waiting for transfers between devices, tree_return(): lax.ppermute(acc.astype(jnp.bfloat16), 'ctx', [(c, c - 2) for c in range(...  22 us
    ppermute x9, waiting for transfers between devices, from_partner(): lax.ppermute(shard, axis, [(i, i ^ 1 << stride) for i in range(lax.axis_s...  15.1 us
    ppermute x3, waiting for transfers between devices, tree_gather(): lax.ppermute(down, 'ctx', [(c + 2, c) for c in range(0, count - 2 * step)])  14.9 us
    dynamic_update_slice x14, local copies, waits for them, and re-layouts, tree_gather(): whole = lax.dynamic_update_slice_in_dim(whole, piece, place, 0)  10.7 us
    ppermute x3, waiting for transfers between devices, tree_gather(): lax.ppermute(downs[step - 1], 'ctx', [(c ^ 1, c) for c in range(0, count...  8.89 us
    ppermute x3, starting transfers between devices, tree_gather(): lax.ppermute(downs[step - 1], 'ctx', [(c ^ 1, c) for c in range(0, count...  7.71 us
  transfers between devices with their start and end apart: 50, of which 15 were waited for; matrix products, arithmetic and copies ran while one was open for 23% of the time, Pallas kernels for 0%

profile of v14, /device:TPU:0, one launch (start us, length us, event | category | flops | bytes accessed | tf_op | source)
XLA Modules:
  0.0 267.4 jit_solution(9253459224346172477)
XLA Ops:
  0.7 5.8 %collective-permute-start.3 = (bf16[128,1024]{1,0:T(8,128)(2,1)}, bf16[128,1024]{1,0:T(8,128)(2,1)}, u32[]{:S(2)}, u32[]{:S(2)}) collective-permute-start(bf16[128,1024]{1,0:T(8,128)(2,1)} %bitcast.151), channel_id=1, source_target_pairs={{0,4},{2,6},{4,8},{6,10},{8,12},{10,14},{1,5},{3,7},{5,9},{7,11},{... | collective-permute-start | bytes 786440 | tf_op jit(solution)/shard_map/ppermute | solution.py:41
  6.5 4.1 %collective-permute-start.6 = (bf16[128,1024]{1,0:T(8,128)(2,1)}, bf16[128,1024]{1,0:T(8,128)(2,1)}, u32[]{:S(2)}, u32[]{:S(2)}) collective-permute-start(bf16[128,1024]{1,0:T(8,128)(2,1)} %bitcast.152), channel_id=1, source_target_pairs={{0,2},{4,6},{8,10},{12,14},{1,3},{5,7},{9,11},{13,15},{16,18},{20,... | collective-permute-start | bytes 786440 | tf_op jit(solution)/shard_map/ppermute | solution.py:43
  10.6 1.8 broadcast_in_dim.58
  13.2 2.8 %collective-permute-start.10 = (bf16[336,512]{1,0:T(8,128)(2,1)S(1)}, bf16[336,512]{1,0:T(8,128)(2,1)S(1)}, u32[]{:S(2)}, u32[]{:S(2)}) collective-permute-start(bf16[336,512]{1,0:T(8,128)(2,1)S(1)} %get-tuple-element.29), channel_id=1, source_target_pairs={{0,4},{2,6},{4,8},{6,10},{8,12},{10,14},{1,5},{3,7},{5,9},{7,11},{... | collective-permute-start | bytes 1032200 | tf_op jit(solution)/shard_map/ppermute | solution.py:60
  19.0 3.7 %collective-permute-done.10 = bf16[336,512]{1,0:T(8,128)(2,1)S(1)} collective-permute-done((bf16[336,512]{1,0:T(8,128)(2,1)S(1)}, bf16[336,512]{1,0:T(8,128)(2,1)S(1)}, u32[]{:S(2)}, u32[]{:S(2)}) %collective-permute-start.10) | collective-permute-done | bytes 344096 | tf_op jit(solution)/shard_map/ppermute | solution.py:60
  23.4 3.4 %collective-permute-done.11 = bf16[336,512]{1,0:T(8,128)(2,1)S(1)} collective-permute-done((bf16[336,512]{1,0:T(8,128)(2,1)S(1)}, bf16[336,512]{1,0:T(8,128)(2,1)S(1)}, u32[]{:S(2)}, u32[]{:S(2)}) %collective-permute-start.11) | collective-permute-done | bytes 344096 | tf_op jit(solution)/shard_map/ppermute | solution.py:61
  30.4 6.6 %collective-permute-done.13 = bf16[336,512]{1,0:T(8,128)(2,1)S(1)} collective-permute-done((bf16[336,512]{1,0:T(8,128)(2,1)S(1)}, bf16[336,512]{1,0:T(8,128)(2,1)S(1)}, u32[]{:S(2)}, u32[]{:S(2)}) %collective-permute-start.13) | collective-permute-done | bytes 344096 | tf_op jit(solution)/shard_map/ppermute | solution.py:61
  41.2 4.9 %collective-permute-done.15 = bf16[336,512]{1,0:T(8,128)(2,1)S(1)} collective-permute-done((bf16[336,512]{1,0:T(8,128)(2,1)S(1)}, bf16[336,512]{1,0:T(8,128)(2,1)S(1)}, u32[]{:S(2)}, u32[]{:S(2)}) %collective-permute-start.15) | collective-permute-done | bytes 344096 | tf_op jit(solution)/shard_map/ppermute | solution.py:61
  46.1 1.9 collective-permute-start.18
  50.2 3.9 %collective-permute-start.20 = (bf16[336,512]{1,0:T(8,128)(2,1)S(1)}, bf16[336,512]{1,0:T(8,128)(2,1)S(1)}, u32[]{:S(2)}, u32[]{:S(2)}) collective-permute-start(bf16[336,512]{1,0:T(8,128)(2,1)S(1)} %collective-permute-done.13), channel_id=1, source_target_pairs={{2,0},{0,2},{6,4},{4,6},{3,1},{1,3},{7,5},{5,7},{18,16},{16,18},{2... | collective-permute-start | bytes 1032200 | tf_op jit(solution)/shard_map/ppermute | solution.py:73
  54.9 4.0 %collective-permute-done.18 = bf16[336,512]{1,0:T(8,128)(2,1)S(1)} collective-permute-done((bf16[336,512]{1,0:T(8,128)(2,1)S(1)}, bf16[336,512]{1,0:T(8,128)(2,1)S(1)}, u32[]{:S(2)}, u32[]{:S(2)}) %collective-permute-start.18) | collective-permute-done | bytes 344096 | tf_op jit(solution)/shard_map/ppermute | solution.py:73
  60.3 1.9 collective-permute-start.22
  63.0 2.6 collective-permute-done.20
  67.1 2.3 collective-permute-done.22
  70.2 3.2 %broadcast_in_dim.57 = bf16[2688,1024]{1,0:T(8,128)(2,1)} broadcast(bf16[]{:T(256)} %constant.74.clone.1), dimensions={} | broadcast | bytes 5505026 | tf_op jit(solution)/shard_map/broadcast_in_dim | solution.py:157
  73.4 3.8 %fusion.35 = (bf16[2688,512]{1,0:T(8,128)(2,1)S(1)}, bf16[2688,1024]{1,0:T(8,128)(2,1)}) fusion(bf16[3024,512]{1,0:T(8,128)(2,1)} %constant_dynamic-update-slice_fusion.26, bf16[2688,1024]{1,0:T(8,128)(2,1)} %broadcast_in_dim.57, s32[]{:T(128)S(6)} %select_n.156), kind=kLoop, calls=%fused_computation.123 | loop fusion | bytes 8257540 | tf_op jit(solution)/shard_map/slice | solution.py:82
  78.6 2.0 copy.94
  80.7 3.5 %collective-permute-done.1 = f32[16]{0:T(128)S(1)} collective-permute-done((f32[16]{0:T(128)S(1)}, f32[16]{0:T(128)S(1)}, u32[]{:S(2)}, u32[]{:S(2)}) %collective-permute-start.1) | collective-permute-done | bytes 96 | tf_op jit(solution)/shard_map/ppermute | solution.py:19
  84.2 1.5 collective-permute-start.2
  85.7 2.9 %collective-permute-done.2 = f32[16]{0:T(128)S(1)} collective-permute-done((f32[16]{0:T(128)S(1)}, f32[16]{0:T(128)S(1)}, u32[]{:S(2)}, u32[]{:S(2)}) %collective-permute-start.2) | collective-permute-done | bytes 96 | tf_op jit(solution)/shard_map/ppermute | solution.py:19
  96.0 3.6 %constant_dynamic-update-slice_fusion.24 = bf16[2688,1024]{1,0:T(8,128)(2,1)} fusion(bf16[2688,1024]{1,0:T(8,128)(2,1)} %get-tuple-element.31, bf16[2688,512]{1,0:T(8,128)(2,1)} %collective-permute-done.23, s32[]{:T(128)S(6)} %select_n.185), kind=kLoop, calls=%fused_computation.84 | loop fusion | bytes 5505028 | tf_op jit(solution)/shard_map/dynamic_update_slice | solution.py:159
  99.6 4.9 %fusion.15 = bf16[128,1024]{0,1:T(8,128)(2,1)} fusion(f32[128,1024]{0,1:T(8,128)S(1)} %copy-done.2, bf16[2688,1024]{1,0:T(8,128)(2,1)} %constant_dynamic-update-slice_fusion.24, bf16[1,128,2688]{2,1,0:T(8,128)(2,1)S(1)} %copy-done), kind=kOutput, calls=%fused_computation.28 | convolution fusion | flops 704905216 | bytes 6979584 | tf_op jit(solution)/shard_map/dot_general | solution.py:168
  104.5 2.0 copy.95
  106.5 3.3 %copy.84 = bf16[1024,8,128,1]{0,2,3,1:T(8,128)(2,1)S(1)} copy(bf16[1024,8,128,1]{2,1,0,3:T(8,128)(2,1)} %bitcast.134) | data formatting | bytes 4194304 | tf_op jit(solution)/shard_map/reshape | solution.py:223
  109.8 5.7 %fusion.39 = (f32[8,2,128]{2,1,0:T(2,128)S(1)}, f32[8,2,128,1024]{2,3,1,0:T(8,128)}) fusion(pred[128,1024]{0,1:T(8,128)(4,1)S(1)} %copy-done.17, bf16[1024,8,128,1]{0,2,3,1:T(8,128)(2,1)S(1)} %copy.84, bf16[128,8,2,128]{0,3,2,1:T(8,128)(2,1)S(1)} %bitcast.138), kind=kOutput, calls=%fused_computation.127 | convolution fusion | flops 547357696 | bytes 11149312 | tf_op jit(solution)/shard_map/sub | solution.py:230
  115.5 5.0 %fusion.40 = (bf16[1024,8,128]{0,2,1:T(8,128)(2,1)S(1)}, f32[1024,8,128]{0,2,1:T(8,128)S(1)}) fusion(bf16[128,8,2,128]{3,2,1,0:T(2,128)(2,1)} %reshape_squeeze.7, f32[128]{0:T(128)S(1)} %get-tuple-element.25, f32[8,2,128,1024]{2,3,1,0:T(8,128)} %get-tuple-element.51, f32[8,2,128]{2,1,0:T(2,128)S(1)} %get-tuple-element.50), kind=kOutput, calls=%fused_computation.128 | convolution fusion | flops 544210944 | bytes 15213056 | tf_op jit(solution)/shard_map/jgtl,tjgd->ljd/dot_general | solution.py:244
  121.9 18.4 %collective-permute-start.32 = (bf16[128,1024]{0,1:T(8,128)(2,1)S(1)}, bf16[128,1024]{0,1:T(8,128)(2,1)S(1)}, u32[]{:S(2)}, u32[]{:S(2)}) collective-permute-start(bf16[128,1024]{0,1:T(8,128)(2,1)S(1)} %copy-done.6), channel_id=1, source_target_pairs={{0,4},{2,6},{4,8},{6,10},{8,12},{10,14},{1,5},{3,7},{5,9},{7,11},{... | collective-permute-start | bytes 786440 | tf_op jit(solution)/shard_map/ppermute | solution.py:41
  142.5 2.4 collective-permute-done.32
  146.4 3.4 %collective-permute-start.35 = (bf16[128,1024]{0,1:T(8,128)(2,1)S(1)}, bf16[128,1024]{0,1:T(8,128)(2,1)S(1)}, u32[]{:S(2)}, u32[]{:S(2)}) collective-permute-start(bf16[128,1024]{0,1:T(8,128)(2,1)S(1)} %copy-done.6), channel_id=1, source_target_pairs={{0,2},{4,6},{8,10},{12,14},{1,3},{5,7},{9,11},{13,15},{16,18},{20,... | collective-permute-start | bytes 786440 | tf_op jit(solution)/shard_map/ppermute | solution.py:43
  149.9 1.4 collective-permute-start.25
  156.5 1.9 fusion.1
  158.5 1.7 fusion.3
  161.2 3.5 %fusion.41 = (bf16[1024,8,128]{0,2,1:T(8,128)(2,1)S(1)}, f32[1024,8,128]{0,2,1:T(8,128)}) fusion(bf16[8,2,128,1024]{2,3,1,0:T(8,128)(2,1)S(1)} %fusion.3, bf16[128,8,2,128]{0,3,2,1:T(8,128)(2,1)S(1)} %bitcast.139), kind=kOutput, calls=%fused_computation.129 | convolution fusion | flops 537919488 | bytes 11010048 | tf_op jit(solution)/shard_map/jgtl,tjgd->ljd/dot_general | solution.py:240
  164.7 20.0 %collective-permute-done.31 = bf16[128,1024]{0,1:T(8,128)(2,1)S(1)} collective-permute-done((bf16[128,1024]{0,1:T(8,128)(2,1)S(1)}, bf16[128,1024]{0,1:T(8,128)(2,1)S(1)}, u32[]{:S(2)}, u32[]{:S(2)}) %collective-permute-start.31) | collective-permute-done | bytes 262176 | tf_op jit(solution)/shard_map/ppermute | solution.py:114
  188.3 1.4 collective-permute-start.42
  190.5 1.4 collective-permute-start.41
  194.6 1.9 add_convert_fusion.3
  196.5 1.4 collective-permute-start.43
  201.5 1.8 copy.69
  203.3 1.4 collective-permute-start.40
  207.8 11.1 %collective-permute-start.47 = (f32[464,128]{1,0:T(8,128)S(1)}, f32[464,128]{1,0:T(8,128)S(1)}, u32[]{:S(2)}, u32[]{:S(2)}) collective-permute-start(f32[464,128]{1,0:T(8,128)S(1)} %fusion.34), channel_id=1, source_target_pairs={{0,4},{2,6},{4,0},{6,2},{8,12},{10,14},{12,8},{14,10},{1,5},{3,7},... | collective-permute-start | bytes 712712 | tf_op jit(solution)/shard_map/ppermute | solution.py:19
  220.7 2.3 collective-permute-done.47
  224.0 22.2 %collective-permute-start.48 = (f32[464,128]{1,0:T(8,128)S(1)}, f32[464,128]{1,0:T(8,128)S(1)}, u32[]{:S(2)}, u32[]{:S(2)}) collective-permute-start(f32[464,128]{1,0:T(8,128)S(1)} %fusion.64), channel_id=1, source_target_pairs={{0,8},{2,10},{4,12},{6,14},{8,0},{10,2},{12,4},{14,6},{1,9},{3,11}... | collective-permute-start | bytes 712712 | tf_op jit(solution)/shard_map/ppermute | solution.py:19
  246.6 6.3 %collective-permute-done.48 = f32[464,128]{1,0:T(8,128)S(1)} collective-permute-done((f32[464,128]{1,0:T(8,128)S(1)}, f32[464,128]{1,0:T(8,128)S(1)}, u32[]{:S(2)}, u32[]{:S(2)}) %collective-permute-start.48) | collective-permute-done | bytes 237600 | tf_op jit(solution)/shard_map/ppermute | solution.py:19
  253.0 1.8 add_convert_fusion.1
  256.0 5.4 %fusion.11 = bf16[1,128,2688]{2,1,0:T(8,128)(2,1)} fusion(f32[128,2688]{1,0:T(8,128)S(1)} %convolution_multiply_fusion, bf16[128,1024]{0,1:T(8,128)(2,1)S(1)} %fusion.27, bf16[2688,1024]{1,0:T(8,128)(2,1)} %constant_dynamic-update-slice_fusion.24), kind=kOutput, calls=%fused_computation.19 | convolution fusion | flops 705331200 | bytes 7831552 | tf_op jit(solution)/shard_map/tk,dk->td/dot_general | solution.py:269
  263.6 2.1 collective-permute-done.45
  265.6 1.8 fusion.31
  (205 shorter events, 59.8 us)
Async XLA Ops:
  0.7 88.3 %collective-permute-start.3 = (bf16[128,1024]{1,0:T(8,128)(2,1)}, bf16[128,1024]{1,0:T(8,128)(2,1)}, u32[]{:S(2)}, u32[]{:S(2)}) collective-permute-start(bf16[128,1024]{1,0:T(8,128)(2,1)} %bitcast.151), channel_id=1, source_target_pairs={{0,4},{2,6},{4,8},{6,10},{8,12},{10,14},{1,5},{3,7},{5,9},{7,11},{... | collective-permute-start | bytes 786440 | tf_op jit(solution)/shard_map/ppermute | solution.py:41
  6.5 88.4 %collective-permute-start.6 = (bf16[128,1024]{1,0:T(8,128)(2,1)}, bf16[128,1024]{1,0:T(8,128)(2,1)}, u32[]{:S(2)}, u32[]{:S(2)}) collective-permute-start(bf16[128,1024]{1,0:T(8,128)(2,1)} %bitcast.152), channel_id=1, source_target_pairs={{0,2},{4,6},{8,10},{12,14},{1,3},{5,7},{9,11},{13,15},{16,18},{20,... | collective-permute-start | bytes 786440 | tf_op jit(solution)/shard_map/ppermute | solution.py:43
  13.2 9.5 %collective-permute-start.10 = (bf16[336,512]{1,0:T(8,128)(2,1)S(1)}, bf16[336,512]{1,0:T(8,128)(2,1)S(1)}, u32[]{:S(2)}, u32[]{:S(2)}) collective-permute-start(bf16[336,512]{1,0:T(8,128)(2,1)S(1)} %get-tuple-element.29), channel_id=1, source_target_pairs={{0,4},{2,6},{4,8},{6,10},{8,12},{10,14},{1,5},{3,7},{5,9},{7,11},{... | collective-permute-start | bytes 1032200 | tf_op jit(solution)/shard_map/ppermute | solution.py:60
  16.0 10.9 %collective-permute-start.11 = (bf16[336,512]{1,0:T(8,128)(2,1)S(1)}, bf16[336,512]{1,0:T(8,128)(2,1)S(1)}, u32[]{:S(2)}, u32[]{:S(2)}) collective-permute-start(bf16[336,512]{1,0:T(8,128)(2,1)S(1)} %get-tuple-element.29), channel_id=1, source_target_pairs={{4,0},{6,2},{8,4},{10,6},{12,8},{14,10},{5,1},{7,3},{9,5},{11,7},{... | collective-permute-start | bytes 1032200 | tf_op jit(solution)/shard_map/ppermute | solution.py:61
  17.3 31.5 %collective-permute-start.16 = (bf16[336,512]{1,0:T(8,128)(2,1)S(1)}, bf16[336,512]{1,0:T(8,128)(2,1)S(1)}, u32[]{:S(2)}, u32[]{:S(2)}) collective-permute-start(bf16[336,512]{1,0:T(8,128)(2,1)S(1)} %get-tuple-element.29), channel_id=1, source_target_pairs={{2,0},{0,2},{6,4},{4,6},{10,8},{8,10},{14,12},{12,14},{3,1},{1,3},... | collective-permute-start | bytes 1032200 | tf_op jit(solution)/shard_map/ppermute | solution.py:67
  22.7 6.2 %collective-permute-start.12 = (bf16[336,512]{1,0:T(8,128)(2,1)S(1)}, bf16[336,512]{1,0:T(8,128)(2,1)S(1)}, u32[]{:S(2)}, u32[]{:S(2)}) collective-permute-start(bf16[336,512]{1,0:T(8,128)(2,1)S(1)} %collective-permute-done.10), channel_id=1, source_target_pairs={{4,8},{6,10},{8,12},{10,14},{5,9},{7,11},{9,13},{11,15},{20,24},{2... | collective-permute-start | bytes 1032200 | tf_op jit(solution)/shard_map/ppermute | solution.py:60
  26.9 10.1 %collective-permute-start.13 = (bf16[336,512]{1,0:T(8,128)(2,1)S(1)}, bf16[336,512]{1,0:T(8,128)(2,1)S(1)}, u32[]{:S(2)}, u32[]{:S(2)}) collective-permute-start(bf16[336,512]{1,0:T(8,128)(2,1)S(1)} %collective-permute-done.11), channel_id=1, source_target_pairs={{4,0},{6,2},{8,4},{10,6},{5,1},{7,3},{9,5},{11,7},{20,16},{22,18},... | collective-permute-start | bytes 1032200 | tf_op jit(solution)/shard_map/ppermute | solution.py:61
  28.9 10.8 %collective-permute-start.14 = (bf16[336,512]{1,0:T(8,128)(2,1)S(1)}, bf16[336,512]{1,0:T(8,128)(2,1)S(1)}, u32[]{:S(2)}, u32[]{:S(2)}) collective-permute-start(bf16[336,512]{1,0:T(8,128)(2,1)S(1)} %collective-permute-done.12), channel_id=1, source_target_pairs={{8,12},{10,14},{9,13},{11,15},{24,28},{26,30},{25,29},{27,31}} | collective-permute-start | bytes 1032200 | tf_op jit(solution)/shard_map/ppermute | solution.py:60
  36.9 9.1 %collective-permute-start.15 = (bf16[336,512]{1,0:T(8,128)(2,1)S(1)}, bf16[336,512]{1,0:T(8,128)(2,1)S(1)}, u32[]{:S(2)}, u32[]{:S(2)}) collective-permute-start(bf16[336,512]{1,0:T(8,128)(2,1)S(1)} %collective-permute-done.13), channel_id=1, source_target_pairs={{4,0},{6,2},{5,1},{7,3},{20,16},{22,18},{21,17},{23,19}} | collective-permute-start | bytes 1032200 | tf_op jit(solution)/shard_map/ppermute | solution.py:61
  39.7 10.5 %collective-permute-start.17 = (bf16[336,512]{1,0:T(8,128)(2,1)S(1)}, bf16[336,512]{1,0:T(8,128)(2,1)S(1)}, u32[]{:S(2)}, u32[]{:S(2)}) collective-permute-start(bf16[336,512]{1,0:T(8,128)(2,1)S(1)} %collective-permute-done.10), channel_id=1, source_target_pairs={{6,4},{4,6},{10,8},{8,10},{14,12},{12,14},{7,5},{5,7},{11,9},{9,11... | collective-permute-start | bytes 1032200 | tf_op jit(solution)/shard_map/ppermute | solution.py:71
  46.1 12.8 %collective-permute-start.18 = (bf16[336,512]{1,0:T(8,128)(2,1)S(1)}, bf16[336,512]{1,0:T(8,128)(2,1)S(1)}, u32[]{:S(2)}, u32[]{:S(2)}) collective-permute-start(bf16[336,512]{1,0:T(8,128)(2,1)S(1)} %collective-permute-done.11), channel_id=1, source_target_pairs={{2,0},{0,2},{6,4},{4,6},{10,8},{8,10},{3,1},{1,3},{7,5},{5,7},{11,... | collective-permute-start | bytes 1032200 | tf_op jit(solution)/shard_map/ppermute | solution.py:73
  48.8 11.5 %collective-permute-start.19 = (bf16[336,512]{1,0:T(8,128)(2,1)S(1)}, bf16[336,512]{1,0:T(8,128)(2,1)S(1)}, u32[]{:S(2)}, u32[]{:S(2)}) collective-permute-start(bf16[336,512]{1,0:T(8,128)(2,1)S(1)} %collective-permute-done.12), channel_id=1, source_target_pairs={{10,8},{8,10},{14,12},{12,14},{11,9},{9,11},{15,13},{13,15},{26,24... | collective-permute-start | bytes 1032200 | tf_op jit(solution)/shard_map/ppermute | solution.py:71
  50.2 15.4 %collective-permute-start.20 = (bf16[336,512]{1,0:T(8,128)(2,1)S(1)}, bf16[336,512]{1,0:T(8,128)(2,1)S(1)}, u32[]{:S(2)}, u32[]{:S(2)}) collective-permute-start(bf16[336,512]{1,0:T(8,128)(2,1)S(1)} %collective-permute-done.13), channel_id=1, source_target_pairs={{2,0},{0,2},{6,4},{4,6},{3,1},{1,3},{7,5},{5,7},{18,16},{16,18},{2... | collective-permute-start | bytes 1032200 | tf_op jit(solution)/shard_map/ppermute | solution.py:73
  58.8 7.5 %collective-permute-start.21 = (bf16[336,512]{1,0:T(8,128)(2,1)S(1)}, bf16[336,512]{1,0:T(8,128)(2,1)S(1)}, u32[]{:S(2)}, u32[]{:S(2)}) collective-permute-start(bf16[336,512]{1,0:T(8,128)(2,1)S(1)} %collective-permute-done.14), channel_id=1, source_target_pairs={{14,12},{12,14},{15,13},{13,15},{30,28},{28,30},{31,29},{29,31}} | collective-permute-start | bytes 1032200 | tf_op jit(solution)/shard_map/ppermute | solution.py:71
  60.3 9.1 %collective-permute-start.22 = (bf16[336,512]{1,0:T(8,128)(2,1)S(1)}, bf16[336,512]{1,0:T(8,128)(2,1)S(1)}, u32[]{:S(2)}, u32[]{:S(2)}) collective-permute-start(bf16[336,512]{1,0:T(8,128)(2,1)S(1)} %collective-permute-done.15), channel_id=1, source_target_pairs={{2,0},{0,2},{3,1},{1,3},{18,16},{16,18},{19,17},{17,19}} | collective-permute-start | bytes 1032200 | tf_op jit(solution)/shard_map/ppermute | solution.py:73
  65.6 15.0 %collective-permute-start = (f32[16]{0:T(128)S(1)}, f32[16]{0:T(128)S(1)}, u32[]{:S(2)}, u32[]{:S(2)}) collective-permute-start(f32[16]{0:T(128)S(1)} %pad_maximum_fusion), channel_id=1, source_target_pairs={{0,2},{2,0},{4,6},{6,4},{8,10},{10,8},{12,14},{14,12},{1,3},{3,1},... | collective-permute-start | bytes 200 | tf_op jit(solution)/shard_map/ppermute | solution.py:19
  77.1 18.9 %collective-permute-start.23 = (bf16[2688,512]{1,0:T(8,128)(2,1)S(1)}, bf16[2688,512]{1,0:T(8,128)(2,1)}, u32[]{:S(2)}, u32[]{:S(2)}) collective-permute-start(bf16[2688,512]{1,0:T(8,128)(2,1)S(1)} %get-tuple-element.30), channel_id=1, source_target_pairs={{0,1},{1,0},{2,3},{3,2},{4,5},{5,4},{6,7},{7,6},{8,9},{9,8},{10,11... | collective-permute-start | bytes 8257544 | tf_op jit(solution)/shard_map/ppermute | solution.py:19
  80.7 3.5 %collective-permute-start.1 = (f32[16]{0:T(128)S(1)}, f32[16]{0:T(128)S(1)}, u32[]{:S(2)}, u32[]{:S(2)}) collective-permute-start(f32[16]{0:T(128)S(1)} %fusion.65), channel_id=1, source_target_pairs={{0,4},{2,6},{4,0},{6,2},{8,12},{10,14},{12,8},{14,10},{1,5},{3,7},... | collective-permute-start | bytes 200 | tf_op jit(solution)/shard_map/ppermute | solution.py:19
  84.2 4.4 %collective-permute-start.2 = (f32[16]{0:T(128)S(1)}, f32[16]{0:T(128)S(1)}, u32[]{:S(2)}, u32[]{:S(2)}) collective-permute-start(f32[16]{0:T(128)S(1)} %add.231), channel_id=1, source_target_pairs={{0,8},{2,10},{4,12},{6,14},{8,0},{10,2},{12,4},{14,6},{1,9},{3,11}... | collective-permute-start | bytes 200 | tf_op jit(solution)/shard_map/ppermute | solution.py:19
  90.1 3.9 %collective-permute-start.5 = (bf16[128,1024]{1,0:T(8,128)(2,1)S(1)}, bf16[128,1024]{1,0:T(8,128)(2,1)S(1)}, u32[]{:S(2)}, u32[]{:S(2)}) collective-permute-start(bf16[128,1024]{1,0:T(8,128)(2,1)S(1)} %collective-permute-done.4), channel_id=1, source_target_pairs={{8,12},{10,14},{9,13},{11,15},{24,28},{26,30},{25,29},{27,31}} | collective-permute-start | bytes 786440 | tf_op jit(solution)/shard_map/ppermute | solution.py:41
  92.6 3.3 %collective-permute-start.7 = (bf16[128,1024]{1,0:T(8,128)(2,1)}, bf16[128,1024]{1,0:T(8,128)(2,1)S(1)}, u32[]{:S(2)}, u32[]{:S(2)}) collective-permute-start(bf16[128,1024]{1,0:T(8,128)(2,1)} %collective-permute-done.3), channel_id=1, source_target_pairs={{6,4},{4,6},{10,8},{8,10},{14,12},{12,14},{7,5},{5,7},{11,9},{9,11... | collective-permute-start | bytes 786440 | tf_op jit(solution)/shard_map/ppermute | solution.py:46
  93.3 2.6 collective-permute-start.8
  94.0 2.0 collective-permute-start.9
  121.0 20.0 %collective-permute-start.28 = (bf16[128,1024]{0,1:T(8,128)(2,1)S(1)}, bf16[128,1024]{0,1:T(8,128)(2,1)S(1)}, u32[]{:S(2)}, u32[]{:S(2)}) collective-permute-start(bf16[128,1024]{0,1:T(8,128)(2,1)S(1)} %bitcast.150), channel_id=1, source_target_pairs={{12,14},{14,12},{13,15},{15,13},{28,30},{30,28},{29,31},{31,29}} | collective-permute-start | bytes 786440 | tf_op jit(solution)/shard_map/ppermute | solution.py:106
  121.9 23.0 %collective-permute-start.32 = (bf16[128,1024]{0,1:T(8,128)(2,1)S(1)}, bf16[128,1024]{0,1:T(8,128)(2,1)S(1)}, u32[]{:S(2)}, u32[]{:S(2)}) collective-permute-start(bf16[128,1024]{0,1:T(8,128)(2,1)S(1)} %copy-done.6), channel_id=1, source_target_pairs={{0,4},{2,6},{4,8},{6,10},{8,12},{10,14},{1,5},{3,7},{5,9},{7,11},{... | collective-permute-start | bytes 786440 | tf_op jit(solution)/shard_map/ppermute | solution.py:41
  140.3 5.2 %collective-permute-start.27 = (bf16[128,1024]{0,1:T(8,128)(2,1)S(1)}, bf16[128,1024]{0,1:T(8,128)(2,1)S(1)}, u32[]{:S(2)}, u32[]{:S(2)}) collective-permute-start(bf16[128,1024]{0,1:T(8,128)(2,1)S(1)} %bitcast.149), channel_id=1, source_target_pairs={{8,10},{10,8},{12,14},{14,12},{9,11},{11,9},{13,15},{15,13},{24,26... | collective-permute-start | bytes 786440 | tf_op jit(solution)/shard_map/ppermute | solution.py:106
  141.1 4.4 %collective-permute-start.29 = (bf16[128,1024]{0,1:T(8,128)(2,1)S(1)}, bf16[128,1024]{0,1:T(8,128)(2,1)S(1)}, u32[]{:S(2)}, u32[]{:S(2)}) collective-permute-start(bf16[128,1024]{0,1:T(8,128)(2,1)S(1)} %fusion.22), channel_id=1, source_target_pairs={{12,8},{14,10},{13,9},{15,11},{28,24},{30,26},{29,25},{31,27}} | collective-permute-start | bytes 786440 | tf_op jit(solution)/shard_map/ppermute | solution.py:114
  141.8 10.4 %collective-permute-start.26 = (bf16[128,1024]{0,1:T(8,128)(2,1)S(1)}, bf16[128,1024]{0,1:T(8,128)(2,1)S(1)}, u32[]{:S(2)}, u32[]{:S(2)}) collective-permute-start(bf16[128,1024]{0,1:T(8,128)(2,1)S(1)} %bitcast.148), channel_id=1, source_target_pairs={{4,6},{6,4},{8,10},{10,8},{12,14},{14,12},{5,7},{7,5},{9,11},{11,9... | collective-permute-start | bytes 786440 | tf_op jit(solution)/shard_map/ppermute | solution.py:106
  144.8 6.6 %collective-permute-start.33 = (bf16[128,1024]{0,1:T(8,128)(2,1)S(1)}, bf16[128,1024]{0,1:T(8,128)(2,1)S(1)}, u32[]{:S(2)}, u32[]{:S(2)}) collective-permute-start(bf16[128,1024]{0,1:T(8,128)(2,1)S(1)} %collective-permute-done.32), channel_id=1, source_target_pairs={{4,8},{6,10},{8,12},{10,14},{5,9},{7,11},{9,13},{11,15},{20,24},{2... | collective-permute-start | bytes 786440 | tf_op jit(solution)/shard_map/ppermute | solution.py:41
  145.7 7.2 %collective-permute-start.30 = (bf16[128,1024]{0,1:T(8,128)(2,1)S(1)}, bf16[128,1024]{0,1:T(8,128)(2,1)S(1)}, u32[]{:S(2)}, u32[]{:S(2)}) collective-permute-start(bf16[128,1024]{0,1:T(8,128)(2,1)S(1)} %fusion.24), channel_id=1, source_target_pairs={{8,4},{10,6},{12,8},{14,10},{9,5},{11,7},{13,9},{15,11},{24,20},{2... | collective-permute-start | bytes 786440 | tf_op jit(solution)/shard_map/ppermute | solution.py:114
  146.4 8.8 %collective-permute-start.35 = (bf16[128,1024]{0,1:T(8,128)(2,1)S(1)}, bf16[128,1024]{0,1:T(8,128)(2,1)S(1)}, u32[]{:S(2)}, u32[]{:S(2)}) collective-permute-start(bf16[128,1024]{0,1:T(8,128)(2,1)S(1)} %copy-done.6), channel_id=1, source_target_pairs={{0,2},{4,6},{8,10},{12,14},{1,3},{5,7},{9,11},{13,15},{16,18},{20,... | collective-permute-start | bytes 786440 | tf_op jit(solution)/shard_map/ppermute | solution.py:43
  149.9 14.8 %collective-permute-start.25 = (bf16[128,1024]{0,1:T(8,128)(2,1)S(1)}, bf16[128,1024]{0,1:T(8,128)(2,1)S(1)}, u32[]{:S(2)}, u32[]{:S(2)}) collective-permute-start(bf16[128,1024]{0,1:T(8,128)(2,1)S(1)} %bitcast.147), channel_id=1, source_target_pairs={{2,0},{6,4},{10,8},{14,12},{3,1},{7,5},{11,9},{15,13},{18,16},{22,... | collective-permute-start | bytes 786440 | tf_op jit(solution)/shard_map/ppermute | solution.py:103
  151.4 2.3 collective-permute-start.34
  152.2 3.9 %collective-permute-start.36 = (bf16[128,1024]{0,1:T(8,128)(2,1)S(1)}, bf16[128,1024]{0,1:T(8,128)(2,1)S(1)}, u32[]{:S(2)}, u32[]{:S(2)}) collective-permute-start(bf16[128,1024]{0,1:T(8,128)(2,1)S(1)} %collective-permute-done.32), channel_id=1, source_target_pairs={{6,4},{4,6},{10,8},{8,10},{14,12},{12,14},{7,5},{5,7},{11,9},{9,11... | collective-permute-start | bytes 786440 | tf_op jit(solution)/shard_map/ppermute | solution.py:46
  152.9 3.3 %collective-permute-start.37 = (bf16[128,1024]{0,1:T(8,128)(2,1)S(1)}, bf16[128,1024]{0,1:T(8,128)(2,1)S(1)}, u32[]{:S(2)}, u32[]{:S(2)}) collective-permute-start(bf16[128,1024]{0,1:T(8,128)(2,1)S(1)} %collective-permute-done.33), channel_id=1, source_target_pairs={{10,8},{8,10},{14,12},{12,14},{11,9},{9,11},{15,13},{13,15},{26,24... | collective-permute-start | bytes 786440 | tf_op jit(solution)/shard_map/ppermute | solution.py:46
  153.7 31.0 %collective-permute-start.31 = (bf16[128,1024]{0,1:T(8,128)(2,1)S(1)}, bf16[128,1024]{0,1:T(8,128)(2,1)S(1)}, u32[]{:S(2)}, u32[]{:S(2)}) collective-permute-start(bf16[128,1024]{0,1:T(8,128)(2,1)S(1)} %fusion.26), channel_id=1, source_target_pairs={{4,0},{6,2},{8,4},{10,6},{12,8},{14,10},{5,1},{7,3},{9,5},{11,7},{... | collective-permute-start | bytes 786440 | tf_op jit(solution)/shard_map/ppermute | solution.py:114
  155.1 1.2 collective-permute-start.38
  188.3 6.4 %collective-permute-start.42 = (bf16[128,1024]{1,0:T(8,128)(2,1)}, bf16[128,1024]{1,0:T(8,128)(2,1)}, u32[]{:S(2)}, u32[]{:S(2)}) collective-permute-start(bf16[128,1024]{1,0:T(8,128)(2,1)} %copy.73), channel_id=1, source_target_pairs={{12,14},{14,12},{13,15},{15,13},{28,30},{30,28},{29,31},{31,29}} | collective-permute-start | bytes 786440 | tf_op jit(solution)/shard_map/ppermute | solution.py:106
  190.5 28.4 %collective-permute-start.41 = (bf16[128,1024]{1,0:T(8,128)(2,1)}, bf16[128,1024]{1,0:T(8,128)(2,1)}, u32[]{:S(2)}, u32[]{:S(2)}) collective-permute-start(bf16[128,1024]{1,0:T(8,128)(2,1)} %copy.71), channel_id=1, source_target_pairs={{8,10},{10,8},{12,14},{14,12},{9,11},{11,9},{13,15},{15,13},{24,26... | collective-permute-start | bytes 786440 | tf_op jit(solution)/shard_map/ppermute | solution.py:106
  193.6 13.2 %collective-permute-start.46 = (f32[464,128]{1,0:T(8,128)}, f32[464,128]{1,0:T(8,128)}, u32[]{:S(2)}, u32[]{:S(2)}) collective-permute-start(f32[464,128]{1,0:T(8,128)} %maximum_bitcast_fusion), channel_id=1, source_target_pairs={{0,2},{2,0},{4,6},{6,4},{8,10},{10,8},{12,14},{14,12},{1,3},{3,1},... | collective-permute-start | bytes 712712 | tf_op jit(solution)/shard_map/ppermute | solution.py:19
  196.5 22.4 %collective-permute-start.43 = (bf16[128,1024]{1,0:T(8,128)(2,1)}, bf16[128,1024]{1,0:T(8,128)(2,1)}, u32[]{:S(2)}, u32[]{:S(2)}) collective-permute-start(bf16[128,1024]{1,0:T(8,128)(2,1)} %add_convert_fusion.3), channel_id=1, source_target_pairs={{12,8},{14,10},{13,9},{15,11},{28,24},{30,26},{29,25},{31,27}} | collective-permute-start | bytes 786440 | tf_op jit(solution)/shard_map/ppermute | solution.py:114
  203.3 49.6 %collective-permute-start.40 = (bf16[128,1024]{1,0:T(8,128)(2,1)}, bf16[128,1024]{1,0:T(8,128)(2,1)}, u32[]{:S(2)}, u32[]{:S(2)}) collective-permute-start(bf16[128,1024]{1,0:T(8,128)(2,1)} %copy.69), channel_id=1, source_target_pairs={{4,6},{6,4},{8,10},{10,8},{12,14},{14,12},{5,7},{7,5},{9,11},{11,9... | collective-permute-start | bytes 786440 | tf_op jit(solution)/shard_map/ppermute | solution.py:106
  205.5 58.0 %collective-permute-start.39 = (bf16[128,1024]{1,0:T(8,128)(2,1)}, bf16[128,1024]{1,0:T(8,128)(2,1)S(1)}, u32[]{:S(2)}, u32[]{:S(2)}) collective-permute-start(bf16[128,1024]{1,0:T(8,128)(2,1)} %copy.68), channel_id=1, source_target_pairs={{2,0},{6,4},{10,8},{14,12},{3,1},{7,5},{11,9},{15,13},{18,16},{22,... | collective-permute-start | bytes 786440 | tf_op jit(solution)/shard_map/ppermute | solution.py:103
  207.8 15.1 %collective-permute-start.47 = (f32[464,128]{1,0:T(8,128)S(1)}, f32[464,128]{1,0:T(8,128)S(1)}, u32[]{:S(2)}, u32[]{:S(2)}) collective-permute-start(f32[464,128]{1,0:T(8,128)S(1)} %fusion.34), channel_id=1, source_target_pairs={{0,4},{2,6},{4,0},{6,2},{8,12},{10,14},{12,8},{14,10},{1,5},{3,7},... | collective-permute-start | bytes 712712 | tf_op jit(solution)/shard_map/ppermute | solution.py:19
  220.0 32.9 %collective-permute-start.44 = (bf16[128,1024]{1,0:T(8,128)(2,1)S(1)}, bf16[128,1024]{1,0:T(8,128)(2,1)S(1)}, u32[]{:S(2)}, u32[]{:S(2)}) collective-permute-start(bf16[128,1024]{1,0:T(8,128)(2,1)S(1)} %add_convert_fusion.2), channel_id=1, source_target_pairs={{8,4},{10,6},{12,8},{14,10},{9,5},{11,7},{13,9},{15,11},{24,20},{2... | collective-permute-start | bytes 786440 | tf_op jit(solution)/shard_map/ppermute | solution.py:114
  224.0 28.9 %collective-permute-start.48 = (f32[464,128]{1,0:T(8,128)S(1)}, f32[464,128]{1,0:T(8,128)S(1)}, u32[]{:S(2)}, u32[]{:S(2)}) collective-permute-start(f32[464,128]{1,0:T(8,128)S(1)} %fusion.64), channel_id=1, source_target_pairs={{0,8},{2,10},{4,12},{6,14},{8,0},{10,2},{12,4},{14,6},{1,9},{3,11}... | collective-permute-start | bytes 712712 | tf_op jit(solution)/shard_map/ppermute | solution.py:19
  252.9 8.5 %collective-permute-start.49 = (f32[464,128]{1,0:T(8,128)S(1)}, f32[464,128]{1,0:T(8,128)S(1)}, u32[]{:S(2)}, u32[]{:S(2)}) collective-permute-start(f32[464,128]{1,0:T(8,128)S(1)} %add.274), channel_id=1, source_target_pairs={{0,1},{1,0},{2,3},{3,2},{4,5},{5,4},{6,7},{7,6},{8,9},{9,8},{10,11... | collective-permute-start | bytes 712712 | tf_op jit(solution)/shard_map/ppermute | solution.py:19
  254.7 10.9 %collective-permute-start.45 = (bf16[128,1024]{1,0:T(8,128)(2,1)}, bf16[128,1024]{1,0:T(8,128)(2,1)}, u32[]{:S(2)}, u32[]{:S(2)}) collective-permute-start(bf16[128,1024]{1,0:T(8,128)(2,1)} %add_convert_fusion.1), channel_id=1, source_target_pairs={{4,0},{6,2},{8,4},{10,6},{12,8},{14,10},{5,1},{7,3},{9,5},{11,7},{... | collective-permute-start | bytes 786440 | tf_op jit(solution)/shard_map/ppermute | solution.py:114
  (23 other events, 294.1 us)

commit v15 on v14

--- a/solution.py
+++ b/solution.py
@@ -19,17 +19,16 @@
     return lax.ppermute(shard, axis, [(i, i ^ 1 << stride) for i in range(lax.axis_size(axis))])
 
 
-def butterfly_sum(parts, axes):
+def butterfly_sum(parts, axes, far_first=False):
     for axis in axes:
         size = lax.axis_size(axis)
         if size & (size - 1):
             parts = lax.psum(parts, axis)
             continue
-        stride = 0
-        while 1 << stride < size:
+        strides = list(range(size.bit_length() - 1))
+        for stride in reversed(strides) if far_first else strides:
             got = from_partner(parts, axis, stride)
             parts = jax.tree.map(jnp.add, parts, got)
-            stride += 1
     return parts
 
 
@@ -278,7 +277,7 @@
     )
     down_size = down_factor.size
     flat = jnp.concatenate([down_factor.reshape(-1), up_factor.reshape(-1)], 0)
-    flat = butterfly_sum(flat.reshape(-1, HEAD_SIZE), ("ctx", "pair")).reshape(-1)
+    flat = butterfly_sum(flat.reshape(-1, HEAD_SIZE), ("ctx", "pair"), far_first=True).reshape(-1)
     down_gradient = flat[:down_size].reshape(down_factor.shape)
     up_gradient = flat[down_size:].reshape(up_factor.shape)
     return (input_grad[None], query_grad[None], key_grad[None], down_gradient, up_gradient)

time: 269 us -> 264 us (0.981)
  starting transfers between devices: 107 us -> 104 us
where the time goes in v15:
time: 264 us; the launch traced here: 263 us
  starting transfers between devices  104 us (39%)
  waiting for transfers between devices  64.9 us (25%)
  local copies, waits for them, and re-layouts  47.5 us (18%)
  matrix products  29.5 us (11%)
  other arithmetic  14.8 us (6%)
    ppermute x9, starting transfers between devices, from_partner(): lax.ppermute(shard, axis, [(i, i ^ 1 << stride) for i in range(lax.axis_s...  32.4 us
    ppermute x6, starting transfers between devices, tree_spread(): lax.ppermute(held, 'ctx', [(c - 2, c) for c in range(2 * step, count)])  27 us
    ppermute x6, waiting for transfers between devices, tree_return(): lax.ppermute(acc.astype(jnp.bfloat16), 'ctx', [(c, c - 2) for c in range(...  22.3 us
    ppermute x3, waiting for transfers between devices, tree_gather(): lax.ppermute(down, 'ctx', [(c + 2, c) for c in range(0, count - 2 * step)])  14.9 us
    ppermute x9, waiting for transfers between devices, from_partner(): lax.ppermute(shard, axis, [(i, i ^ 1 << stride) for i in range(lax.axis_s...  12.6 us
    dynamic_update_slice x14, local copies, waits for them, and re-layouts, tree_gather(): whole = lax.dynamic_update_slice_in_dim(whole, piece, place, 0)  10.7 us
    ppermute x3, waiting for transfers between devices, tree_gather(): lax.ppermute(downs[step - 1], 'ctx', [(c ^ 1, c) for c in range(0, count...  8.89 us
    ppermute x3, starting transfers between devices, tree_gather(): lax.ppermute(downs[step - 1], 'ctx', [(c ^ 1, c) for c in range(0, count...  7.71 us
  transfers between devices with their start and end apart: 50, of which 15 were waited for; matrix products, arithmetic and copies ran while one was open for 23% of the time, Pallas kernels for 0%

profile of v15, /device:TPU:0, one launch (start us, length us, event | category | flops | bytes accessed | tf_op | source)
XLA Modules:
  0.0 262.6 jit_solution(16154954162984456867)
XLA Ops:
  0.7 5.8 %collective-permute-start.3 = (bf16[128,1024]{1,0:T(8,128)(2,1)}, bf16[128,1024]{1,0:T(8,128)(2,1)}, u32[]{:S(2)}, u32[]{:S(2)}) collective-permute-start(bf16[128,1024]{1,0:T(8,128)(2,1)} %bitcast.151), channel_id=1, source_target_pairs={{0,4},{2,6},{4,8},{6,10},{8,12},{10,14},{1,5},{3,7},{5,9},{7,11},{... | collective-permute-start | bytes 786440 | tf_op jit(solution)/shard_map/ppermute | solution.py:40
  6.5 4.1 %collective-permute-start.6 = (bf16[128,1024]{1,0:T(8,128)(2,1)}, bf16[128,1024]{1,0:T(8,128)(2,1)}, u32[]{:S(2)}, u32[]{:S(2)}) collective-permute-start(bf16[128,1024]{1,0:T(8,128)(2,1)} %bitcast.152), channel_id=1, source_target_pairs={{0,2},{4,6},{8,10},{12,14},{1,3},{5,7},{9,11},{13,15},{16,18},{20,... | collective-permute-start | bytes 786440 | tf_op jit(solution)/shard_map/ppermute | solution.py:42
  10.6 1.8 broadcast_in_dim.58
  13.2 2.8 %collective-permute-start.10 = (bf16[336,512]{1,0:T(8,128)(2,1)S(1)}, bf16[336,512]{1,0:T(8,128)(2,1)S(1)}, u32[]{:S(2)}, u32[]{:S(2)}) collective-permute-start(bf16[336,512]{1,0:T(8,128)(2,1)S(1)} %get-tuple-element.29), channel_id=1, source_target_pairs={{0,4},{2,6},{4,8},{6,10},{8,12},{10,14},{1,5},{3,7},{5,9},{7,11},{... | collective-permute-start | bytes 1032200 | tf_op jit(solution)/shard_map/ppermute | solution.py:59
  19.0 3.7 %collective-permute-done.10 = bf16[336,512]{1,0:T(8,128)(2,1)S(1)} collective-permute-done((bf16[336,512]{1,0:T(8,128)(2,1)S(1)}, bf16[336,512]{1,0:T(8,128)(2,1)S(1)}, u32[]{:S(2)}, u32[]{:S(2)}) %collective-permute-start.10) | collective-permute-done | bytes 344096 | tf_op jit(solution)/shard_map/ppermute | solution.py:59
  23.4 3.4 %collective-permute-done.11 = bf16[336,512]{1,0:T(8,128)(2,1)S(1)} collective-permute-done((bf16[336,512]{1,0:T(8,128)(2,1)S(1)}, bf16[336,512]{1,0:T(8,128)(2,1)S(1)}, u32[]{:S(2)}, u32[]{:S(2)}) %collective-permute-start.11) | collective-permute-done | bytes 344096 | tf_op jit(solution)/shard_map/ppermute | solution.py:60
  30.4 6.6 %collective-permute-done.13 = bf16[336,512]{1,0:T(8,128)(2,1)S(1)} collective-permute-done((bf16[336,512]{1,0:T(8,128)(2,1)S(1)}, bf16[336,512]{1,0:T(8,128)(2,1)S(1)}, u32[]{:S(2)}, u32[]{:S(2)}) %collective-permute-start.13) | collective-permute-done | bytes 344096 | tf_op jit(solution)/shard_map/ppermute | solution.py:60
  41.2 4.9 %collective-permute-done.15 = bf16[336,512]{1,0:T(8,128)(2,1)S(1)} collective-permute-done((bf16[336,512]{1,0:T(8,128)(2,1)S(1)}, bf16[336,512]{1,0:T(8,128)(2,1)S(1)}, u32[]{:S(2)}, u32[]{:S(2)}) %collective-permute-start.15) | collective-permute-done | bytes 344096 | tf_op jit(solution)/shard_map/ppermute | solution.py:60
  46.1 1.9 collective-permute-start.18
  50.2 3.9 %collective-permute-start.20 = (bf16[336,512]{1,0:T(8,128)(2,1)S(1)}, bf16[336,512]{1,0:T(8,128)(2,1)S(1)}, u32[]{:S(2)}, u32[]{:S(2)}) collective-permute-start(bf16[336,512]{1,0:T(8,128)(2,1)S(1)} %collective-permute-done.13), channel_id=1, source_target_pairs={{2,0},{0,2},{6,4},{4,6},{3,1},{1,3},{7,5},{5,7},{18,16},{16,18},{2... | collective-permute-start | bytes 1032200 | tf_op jit(solution)/shard_map/ppermute | solution.py:72
  54.9 4.0 %collective-permute-done.18 = bf16[336,512]{1,0:T(8,128)(2,1)S(1)} collective-permute-done((bf16[336,512]{1,0:T(8,128)(2,1)S(1)}, bf16[336,512]{1,0:T(8,128)(2,1)S(1)}, u32[]{:S(2)}, u32[]{:S(2)}) %collective-permute-start.18) | collective-permute-done | bytes 344096 | tf_op jit(solution)/shard_map/ppermute | solution.py:72
  60.3 1.9 collective-permute-start.22
  63.0 2.6 collective-permute-done.20
  67.1 2.3 collective-permute-done.22
  70.2 3.2 %broadcast_in_dim.57 = bf16[2688,1024]{1,0:T(8,128)(2,1)} broadcast(bf16[]{:T(256)} %constant.74.clone.1), dimensions={} | broadcast | bytes 5505026 | tf_op jit(solution)/shard_map/broadcast_in_dim | solution.py:156
  73.4 3.8 %fusion.35 = (bf16[2688,512]{1,0:T(8,128)(2,1)S(1)}, bf16[2688,1024]{1,0:T(8,128)(2,1)}) fusion(bf16[3024,512]{1,0:T(8,128)(2,1)} %constant_dynamic-update-slice_fusion.26, bf16[2688,1024]{1,0:T(8,128)(2,1)} %broadcast_in_dim.57, s32[]{:T(128)S(6)} %select_n.156), kind=kLoop, calls=%fused_computation.123 | loop fusion | bytes 8257540 | tf_op jit(solution)/shard_map/slice | solution.py:81
  78.6 2.0 copy.94
  80.7 3.5 %collective-permute-done.1 = f32[16]{0:T(128)S(1)} collective-permute-done((f32[16]{0:T(128)S(1)}, f32[16]{0:T(128)S(1)}, u32[]{:S(2)}, u32[]{:S(2)}) %collective-permute-start.1) | collective-permute-done | bytes 96 | tf_op jit(solution)/shard_map/ppermute | solution.py:19
  84.2 1.5 collective-permute-start.2
  85.7 2.9 %collective-permute-done.2 = f32[16]{0:T(128)S(1)} collective-permute-done((f32[16]{0:T(128)S(1)}, f32[16]{0:T(128)S(1)}, u32[]{:S(2)}, u32[]{:S(2)}) %collective-permute-start.2) | collective-permute-done | bytes 96 | tf_op jit(solution)/shard_map/ppermute | solution.py:19
  96.0 3.6 %constant_dynamic-update-slice_fusion.24 = bf16[2688,1024]{1,0:T(8,128)(2,1)} fusion(bf16[2688,1024]{1,0:T(8,128)(2,1)} %get-tuple-element.31, bf16[2688,512]{1,0:T(8,128)(2,1)} %collective-permute-done.23, s32[]{:T(128)S(6)} %select_n.185), kind=kLoop, calls=%fused_computation.84 | loop fusion | bytes 5505028 | tf_op jit(solution)/shard_map/dynamic_update_slice | solution.py:158
  99.6 4.9 %fusion.15 = bf16[128,1024]{0,1:T(8,128)(2,1)} fusion(f32[128,1024]{0,1:T(8,128)S(1)} %copy-done.2, bf16[2688,1024]{1,0:T(8,128)(2,1)} %constant_dynamic-update-slice_fusion.24, bf16[1,128,2688]{2,1,0:T(8,128)(2,1)S(1)} %copy-done), kind=kOutput, calls=%fused_computation.28 | convolution fusion | flops 704905216 | bytes 6979584 | tf_op jit(solution)/shard_map/dot_general | solution.py:167
  104.5 2.0 copy.95
  106.5 3.3 %copy.84 = bf16[1024,8,128,1]{0,2,3,1:T(8,128)(2,1)S(1)} copy(bf16[1024,8,128,1]{2,1,0,3:T(8,128)(2,1)} %bitcast.134) | data formatting | bytes 4194304 | tf_op jit(solution)/shard_map/reshape | solution.py:222
  109.8 5.7 %fusion.39 = (f32[8,2,128]{2,1,0:T(2,128)S(1)}, f32[8,2,128,1024]{2,3,1,0:T(8,128)}) fusion(pred[128,1024]{0,1:T(8,128)(4,1)S(1)} %copy-done.17, bf16[1024,8,128,1]{0,2,3,1:T(8,128)(2,1)S(1)} %copy.84, bf16[128,8,2,128]{0,3,2,1:T(8,128)(2,1)S(1)} %bitcast.138), kind=kOutput, calls=%fused_computation.127 | convolution fusion | flops 547357696 | bytes 11149312 | tf_op jit(solution)/shard_map/sub | solution.py:229
  115.5 5.0 %fusion.40 = (bf16[1024,8,128]{0,2,1:T(8,128)(2,1)S(1)}, f32[1024,8,128]{0,2,1:T(8,128)S(1)}) fusion(bf16[128,8,2,128]{3,2,1,0:T(2,128)(2,1)} %reshape_squeeze.7, f32[128]{0:T(128)S(1)} %get-tuple-element.25, f32[8,2,128,1024]{2,3,1,0:T(8,128)} %get-tuple-element.51, f32[8,2,128]{2,1,0:T(2,128)S(1)} %get-tuple-element.50), kind=kOutput, calls=%fused_computation.128 | convolution fusion | flops 544210944 | bytes 15213056 | tf_op jit(solution)/shard_map/jgtl,tjgd->ljd/dot_general | solution.py:243
  121.9 18.4 %collective-permute-start.32 = (bf16[128,1024]{0,1:T(8,128)(2,1)S(1)}, bf16[128,1024]{0,1:T(8,128)(2,1)S(1)}, u32[]{:S(2)}, u32[]{:S(2)}) collective-permute-start(bf16[128,1024]{0,1:T(8,128)(2,1)S(1)} %copy-done.6), channel_id=1, source_target_pairs={{0,4},{2,6},{4,8},{6,10},{8,12},{10,14},{1,5},{3,7},{5,9},{7,11},{... | collective-permute-start | bytes 786440 | tf_op jit(solution)/shard_map/ppermute | solution.py:40
  142.5 2.4 collective-permute-done.32
  146.4 3.4 %collective-permute-start.35 = (bf16[128,1024]{0,1:T(8,128)(2,1)S(1)}, bf16[128,1024]{0,1:T(8,128)(2,1)S(1)}, u32[]{:S(2)}, u32[]{:S(2)}) collective-permute-start(bf16[128,1024]{0,1:T(8,128)(2,1)S(1)} %copy-done.6), channel_id=1, source_target_pairs={{0,2},{4,6},{8,10},{12,14},{1,3},{5,7},{9,11},{13,15},{16,18},{20,... | collective-permute-start | bytes 786440 | tf_op jit(solution)/shard_map/ppermute | solution.py:42
  149.9 1.4 collective-permute-start.25
  156.5 1.9 fusion.1
  158.5 1.7 fusion.3
  161.2 3.5 %fusion.41 = (bf16[1024,8,128]{0,2,1:T(8,128)(2,1)S(1)}, f32[1024,8,128]{0,2,1:T(8,128)}) fusion(bf16[8,2,128,1024]{2,3,1,0:T(8,128)(2,1)S(1)} %fusion.3, bf16[128,8,2,128]{0,3,2,1:T(8,128)(2,1)S(1)} %bitcast.139), kind=kOutput, calls=%fused_computation.129 | convolution fusion | flops 537919488 | bytes 11010048 | tf_op jit(solution)/shard_map/jgtl,tjgd->ljd/dot_general | solution.py:239
  164.7 20.0 %collective-permute-done.31 = bf16[128,1024]{0,1:T(8,128)(2,1)S(1)} collective-permute-done((bf16[128,1024]{0,1:T(8,128)(2,1)S(1)}, bf16[128,1024]{0,1:T(8,128)(2,1)S(1)}, u32[]{:S(2)}, u32[]{:S(2)}) %collective-permute-start.31) | collective-permute-done | bytes 262176 | tf_op jit(solution)/shard_map/ppermute | solution.py:113
  190.5 1.4 collective-permute-start.41
  193.6 18.1 %collective-permute-start.46 = (f32[464,128]{1,0:T(8,128)}, f32[464,128]{1,0:T(8,128)}, u32[]{:S(2)}, u32[]{:S(2)}) collective-permute-start(f32[464,128]{1,0:T(8,128)} %maximum_bitcast_fusion), channel_id=1, source_target_pairs={{0,8},{2,10},{4,12},{6,14},{8,0},{10,2},{12,4},{14,6},{1,9},{3,11}... | collective-permute-start | bytes 712712 | tf_op jit(solution)/shard_map/ppermute | solution.py:19
  212.7 1.9 add_convert_fusion.3
  214.6 1.4 collective-permute-start.43
  219.5 1.8 copy.69
  221.4 1.4 collective-permute-start.40
  225.9 10.0 %collective-permute-start.47 = (f32[464,128]{1,0:T(8,128)S(1)}, f32[464,128]{1,0:T(8,128)S(1)}, u32[]{:S(2)}, u32[]{:S(2)}) collective-permute-start(f32[464,128]{1,0:T(8,128)S(1)} %fusion.34), channel_id=1, source_target_pairs={{0,4},{2,6},{4,0},{6,2},{8,12},{10,14},{12,8},{14,10},{1,5},{3,7},... | collective-permute-start | bytes 712712 | tf_op jit(solution)/shard_map/ppermute | solution.py:19
  237.7 2.3 collective-permute-done.47
  241.0 2.7 %collective-permute-start.48 = (f32[464,128]{1,0:T(8,128)S(1)}, f32[464,128]{1,0:T(8,128)S(1)}, u32[]{:S(2)}, u32[]{:S(2)}) collective-permute-start(f32[464,128]{1,0:T(8,128)S(1)} %fusion.64), channel_id=1, source_target_pairs={{0,2},{2,0},{4,6},{6,4},{8,10},{10,8},{12,14},{14,12},{1,3},{3,1},... | collective-permute-start | bytes 712712 | tf_op jit(solution)/shard_map/ppermute | solution.py:19
  244.0 3.7 %collective-permute-done.48 = f32[464,128]{1,0:T(8,128)S(1)} collective-permute-done((f32[464,128]{1,0:T(8,128)S(1)}, f32[464,128]{1,0:T(8,128)S(1)}, u32[]{:S(2)}, u32[]{:S(2)}) %collective-permute-start.48) | collective-permute-done | bytes 237600 | tf_op jit(solution)/shard_map/ppermute | solution.py:19
  247.9 1.8 add_convert_fusion.1
  250.9 5.3 %fusion.11 = bf16[1,128,2688]{2,1,0:T(8,128)(2,1)} fusion(f32[128,2688]{1,0:T(8,128)S(1)} %convolution_multiply_fusion, bf16[128,1024]{0,1:T(8,128)(2,1)S(1)} %fusion.27, bf16[2688,1024]{1,0:T(8,128)(2,1)} %constant_dynamic-update-slice_fusion.24), kind=kOutput, calls=%fused_computation.19 | convolution fusion | flops 705331200 | bytes 7831552 | tf_op jit(solution)/shard_map/tk,dk->td/dot_general | solution.py:268
  258.5 2.3 collective-permute-done.45
  260.8 1.8 fusion.31
  (205 shorter events, 61.2 us)
Async XLA Ops:
  0.7 88.3 %collective-permute-start.3 = (bf16[128,1024]{1,0:T(8,128)(2,1)}, bf16[128,1024]{1,0:T(8,128)(2,1)}, u32[]{:S(2)}, u32[]{:S(2)}) collective-permute-start(bf16[128,1024]{1,0:T(8,128)(2,1)} %bitcast.151), channel_id=1, source_target_pairs={{0,4},{2,6},{4,8},{6,10},{8,12},{10,14},{1,5},{3,7},{5,9},{7,11},{... | collective-permute-start | bytes 786440 | tf_op jit(solution)/shard_map/ppermute | solution.py:40
  6.5 88.4 %collective-permute-start.6 = (bf16[128,1024]{1,0:T(8,128)(2,1)}, bf16[128,1024]{1,0:T(8,128)(2,1)}, u32[]{:S(2)}, u32[]{:S(2)}) collective-permute-start(bf16[128,1024]{1,0:T(8,128)(2,1)} %bitcast.152), channel_id=1, source_target_pairs={{0,2},{4,6},{8,10},{12,14},{1,3},{5,7},{9,11},{13,15},{16,18},{20,... | collective-permute-start | bytes 786440 | tf_op jit(solution)/shard_map/ppermute | solution.py:42
  13.2 9.5 %collective-permute-start.10 = (bf16[336,512]{1,0:T(8,128)(2,1)S(1)}, bf16[336,512]{1,0:T(8,128)(2,1)S(1)}, u32[]{:S(2)}, u32[]{:S(2)}) collective-permute-start(bf16[336,512]{1,0:T(8,128)(2,1)S(1)} %get-tuple-element.29), channel_id=1, source_target_pairs={{0,4},{2,6},{4,8},{6,10},{8,12},{10,14},{1,5},{3,7},{5,9},{7,11},{... | collective-permute-start | bytes 1032200 | tf_op jit(solution)/shard_map/ppermute | solution.py:59
  16.0 10.9 %collective-permute-start.11 = (bf16[336,512]{1,0:T(8,128)(2,1)S(1)}, bf16[336,512]{1,0:T(8,128)(2,1)S(1)}, u32[]{:S(2)}, u32[]{:S(2)}) collective-permute-start(bf16[336,512]{1,0:T(8,128)(2,1)S(1)} %get-tuple-element.29), channel_id=1, source_target_pairs={{4,0},{6,2},{8,4},{10,6},{12,8},{14,10},{5,1},{7,3},{9,5},{11,7},{... | collective-permute-start | bytes 1032200 | tf_op jit(solution)/shard_map/ppermute | solution.py:60
  17.3 31.5 %collective-permute-start.16 = (bf16[336,512]{1,0:T(8,128)(2,1)S(1)}, bf16[336,512]{1,0:T(8,128)(2,1)S(1)}, u32[]{:S(2)}, u32[]{:S(2)}) collective-permute-start(bf16[336,512]{1,0:T(8,128)(2,1)S(1)} %get-tuple-element.29), channel_id=1, source_target_pairs={{2,0},{0,2},{6,4},{4,6},{10,8},{8,10},{14,12},{12,14},{3,1},{1,3},... | collective-permute-start | bytes 1032200 | tf_op jit(solution)/shard_map/ppermute | solution.py:66
  22.7 6.2 %collective-permute-start.12 = (bf16[336,512]{1,0:T(8,128)(2,1)S(1)}, bf16[336,512]{1,0:T(8,128)(2,1)S(1)}, u32[]{:S(2)}, u32[]{:S(2)}) collective-permute-start(bf16[336,512]{1,0:T(8,128)(2,1)S(1)} %collective-permute-done.10), channel_id=1, source_target_pairs={{4,8},{6,10},{8,12},{10,14},{5,9},{7,11},{9,13},{11,15},{20,24},{2... | collective-permute-start | bytes 1032200 | tf_op jit(solution)/shard_map/ppermute | solution.py:59
  26.9 10.1 %collective-permute-start.13 = (bf16[336,512]{1,0:T(8,128)(2,1)S(1)}, bf16[336,512]{1,0:T(8,128)(2,1)S(1)}, u32[]{:S(2)}, u32[]{:S(2)}) collective-permute-start(bf16[336,512]{1,0:T(8,128)(2,1)S(1)} %collective-permute-done.11), channel_id=1, source_target_pairs={{4,0},{6,2},{8,4},{10,6},{5,1},{7,3},{9,5},{11,7},{20,16},{22,18},... | collective-permute-start | bytes 1032200 | tf_op jit(solution)/shard_map/ppermute | solution.py:60
  28.9 10.8 %collective-permute-start.14 = (bf16[336,512]{1,0:T(8,128)(2,1)S(1)}, bf16[336,512]{1,0:T(8,128)(2,1)S(1)}, u32[]{:S(2)}, u32[]{:S(2)}) collective-permute-start(bf16[336,512]{1,0:T(8,128)(2,1)S(1)} %collective-permute-done.12), channel_id=1, source_target_pairs={{8,12},{10,14},{9,13},{11,15},{24,28},{26,30},{25,29},{27,31}} | collective-permute-start | bytes 1032200 | tf_op jit(solution)/shard_map/ppermute | solution.py:59
  36.9 9.1 %collective-permute-start.15 = (bf16[336,512]{1,0:T(8,128)(2,1)S(1)}, bf16[336,512]{1,0:T(8,128)(2,1)S(1)}, u32[]{:S(2)}, u32[]{:S(2)}) collective-permute-start(bf16[336,512]{1,0:T(8,128)(2,1)S(1)} %collective-permute-done.13), channel_id=1, source_target_pairs={{4,0},{6,2},{5,1},{7,3},{20,16},{22,18},{21,17},{23,19}} | collective-permute-start | bytes 1032200 | tf_op jit(solution)/shard_map/ppermute | solution.py:60
  39.7 10.5 %collective-permute-start.17 = (bf16[336,512]{1,0:T(8,128)(2,1)S(1)}, bf16[336,512]{1,0:T(8,128)(2,1)S(1)}, u32[]{:S(2)}, u32[]{:S(2)}) collective-permute-start(bf16[336,512]{1,0:T(8,128)(2,1)S(1)} %collective-permute-done.10), channel_id=1, source_target_pairs={{6,4},{4,6},{10,8},{8,10},{14,12},{12,14},{7,5},{5,7},{11,9},{9,11... | collective-permute-start | bytes 1032200 | tf_op jit(solution)/shard_map/ppermute | solution.py:70
  46.1 12.8 %collective-permute-start.18 = (bf16[336,512]{1,0:T(8,128)(2,1)S(1)}, bf16[336,512]{1,0:T(8,128)(2,1)S(1)}, u32[]{:S(2)}, u32[]{:S(2)}) collective-permute-start(bf16[336,512]{1,0:T(8,128)(2,1)S(1)} %collective-permute-done.11), channel_id=1, source_target_pairs={{2,0},{0,2},{6,4},{4,6},{10,8},{8,10},{3,1},{1,3},{7,5},{5,7},{11,... | collective-permute-start | bytes 1032200 | tf_op jit(solution)/shard_map/ppermute | solution.py:72
  48.8 11.5 %collective-permute-start.19 = (bf16[336,512]{1,0:T(8,128)(2,1)S(1)}, bf16[336,512]{1,0:T(8,128)(2,1)S(1)}, u32[]{:S(2)}, u32[]{:S(2)}) collective-permute-start(bf16[336,512]{1,0:T(8,128)(2,1)S(1)} %collective-permute-done.12), channel_id=1, source_target_pairs={{10,8},{8,10},{14,12},{12,14},{11,9},{9,11},{15,13},{13,15},{26,24... | collective-permute-start | bytes 1032200 | tf_op jit(solution)/shard_map/ppermute | solution.py:70
  50.2 15.4 %collective-permute-start.20 = (bf16[336,512]{1,0:T(8,128)(2,1)S(1)}, bf16[336,512]{1,0:T(8,128)(2,1)S(1)}, u32[]{:S(2)}, u32[]{:S(2)}) collective-permute-start(bf16[336,512]{1,0:T(8,128)(2,1)S(1)} %collective-permute-done.13), channel_id=1, source_target_pairs={{2,0},{0,2},{6,4},{4,6},{3,1},{1,3},{7,5},{5,7},{18,16},{16,18},{2... | collective-permute-start | bytes 1032200 | tf_op jit(solution)/shard_map/ppermute | solution.py:72
  58.8 7.5 %collective-permute-start.21 = (bf16[336,512]{1,0:T(8,128)(2,1)S(1)}, bf16[336,512]{1,0:T(8,128)(2,1)S(1)}, u32[]{:S(2)}, u32[]{:S(2)}) collective-permute-start(bf16[336,512]{1,0:T(8,128)(2,1)S(1)} %collective-permute-done.14), channel_id=1, source_target_pairs={{14,12},{12,14},{15,13},{13,15},{30,28},{28,30},{31,29},{29,31}} | collective-permute-start | bytes 1032200 | tf_op jit(solution)/shard_map/ppermute | solution.py:70
  60.3 9.1 %collective-permute-start.22 = (bf16[336,512]{1,0:T(8,128)(2,1)S(1)}, bf16[336,512]{1,0:T(8,128)(2,1)S(1)}, u32[]{:S(2)}, u32[]{:S(2)}) collective-permute-start(bf16[336,512]{1,0:T(8,128)(2,1)S(1)} %collective-permute-done.15), channel_id=1, source_target_pairs={{2,0},{0,2},{3,1},{1,3},{18,16},{16,18},{19,17},{17,19}} | collective-permute-start | bytes 1032200 | tf_op jit(solution)/shard_map/ppermute | solution.py:72
  65.6 15.0 %collective-permute-start = (f32[16]{0:T(128)S(1)}, f32[16]{0:T(128)S(1)}, u32[]{:S(2)}, u32[]{:S(2)}) collective-permute-start(f32[16]{0:T(128)S(1)} %pad_maximum_fusion), channel_id=1, source_target_pairs={{0,2},{2,0},{4,6},{6,4},{8,10},{10,8},{12,14},{14,12},{1,3},{3,1},... | collective-permute-start | bytes 200 | tf_op jit(solution)/shard_map/ppermute | solution.py:19
  77.1 18.9 %collective-permute-start.23 = (bf16[2688,512]{1,0:T(8,128)(2,1)S(1)}, bf16[2688,512]{1,0:T(8,128)(2,1)}, u32[]{:S(2)}, u32[]{:S(2)}) collective-permute-start(bf16[2688,512]{1,0:T(8,128)(2,1)S(1)} %get-tuple-element.30), channel_id=1, source_target_pairs={{0,1},{1,0},{2,3},{3,2},{4,5},{5,4},{6,7},{7,6},{8,9},{9,8},{10,11... | collective-permute-start | bytes 8257544 | tf_op jit(solution)/shard_map/ppermute | solution.py:19
  80.7 3.5 %collective-permute-start.1 = (f32[16]{0:T(128)S(1)}, f32[16]{0:T(128)S(1)}, u32[]{:S(2)}, u32[]{:S(2)}) collective-permute-start(f32[16]{0:T(128)S(1)} %fusion.65), channel_id=1, source_target_pairs={{0,4},{2,6},{4,0},{6,2},{8,12},{10,14},{12,8},{14,10},{1,5},{3,7},... | collective-permute-start | bytes 200 | tf_op jit(solution)/shard_map/ppermute | solution.py:19
  84.2 4.4 %collective-permute-start.2 = (f32[16]{0:T(128)S(1)}, f32[16]{0:T(128)S(1)}, u32[]{:S(2)}, u32[]{:S(2)}) collective-permute-start(f32[16]{0:T(128)S(1)} %add.231), channel_id=1, source_target_pairs={{0,8},{2,10},{4,12},{6,14},{8,0},{10,2},{12,4},{14,6},{1,9},{3,11}... | collective-permute-start | bytes 200 | tf_op jit(solution)/shard_map/ppermute | solution.py:19
  90.1 3.9 %collective-permute-start.5 = (bf16[128,1024]{1,0:T(8,128)(2,1)S(1)}, bf16[128,1024]{1,0:T(8,128)(2,1)S(1)}, u32[]{:S(2)}, u32[]{:S(2)}) collective-permute-start(bf16[128,1024]{1,0:T(8,128)(2,1)S(1)} %collective-permute-done.4), channel_id=1, source_target_pairs={{8,12},{10,14},{9,13},{11,15},{24,28},{26,30},{25,29},{27,31}} | collective-permute-start | bytes 786440 | tf_op jit(solution)/shard_map/ppermute | solution.py:40
  92.6 3.3 %collective-permute-start.7 = (bf16[128,1024]{1,0:T(8,128)(2,1)}, bf16[128,1024]{1,0:T(8,128)(2,1)S(1)}, u32[]{:S(2)}, u32[]{:S(2)}) collective-permute-start(bf16[128,1024]{1,0:T(8,128)(2,1)} %collective-permute-done.3), channel_id=1, source_target_pairs={{6,4},{4,6},{10,8},{8,10},{14,12},{12,14},{7,5},{5,7},{11,9},{9,11... | collective-permute-start | bytes 786440 | tf_op jit(solution)/shard_map/ppermute | solution.py:45
  93.3 2.6 %collective-permute-start.8 = (bf16[128,1024]{1,0:T(8,128)(2,1)S(1)}, bf16[128,1024]{1,0:T(8,128)(2,1)S(1)}, u32[]{:S(2)}, u32[]{:S(2)}) collective-permute-start(bf16[128,1024]{1,0:T(8,128)(2,1)S(1)} %collective-permute-done.4), channel_id=1, source_target_pairs={{10,8},{8,10},{14,12},{12,14},{11,9},{9,11},{15,13},{13,15},{26,24... | collective-permute-start | bytes 786440 | tf_op jit(solution)/shard_map/ppermute | solution.py:45
  94.0 2.0 collective-permute-start.9
  121.0 20.0 %collective-permute-start.28 = (bf16[128,1024]{0,1:T(8,128)(2,1)S(1)}, bf16[128,1024]{0,1:T(8,128)(2,1)S(1)}, u32[]{:S(2)}, u32[]{:S(2)}) collective-permute-start(bf16[128,1024]{0,1:T(8,128)(2,1)S(1)} %bitcast.150), channel_id=1, source_target_pairs={{12,14},{14,12},{13,15},{15,13},{28,30},{30,28},{29,31},{31,29}} | collective-permute-start | bytes 786440 | tf_op jit(solution)/shard_map/ppermute | solution.py:105
  121.9 23.0 %collective-permute-start.32 = (bf16[128,1024]{0,1:T(8,128)(2,1)S(1)}, bf16[128,1024]{0,1:T(8,128)(2,1)S(1)}, u32[]{:S(2)}, u32[]{:S(2)}) collective-permute-start(bf16[128,1024]{0,1:T(8,128)(2,1)S(1)} %copy-done.6), channel_id=1, source_target_pairs={{0,4},{2,6},{4,8},{6,10},{8,12},{10,14},{1,5},{3,7},{5,9},{7,11},{... | collective-permute-start | bytes 786440 | tf_op jit(solution)/shard_map/ppermute | solution.py:40
  140.3 5.2 %collective-permute-start.27 = (bf16[128,1024]{0,1:T(8,128)(2,1)S(1)}, bf16[128,1024]{0,1:T(8,128)(2,1)S(1)}, u32[]{:S(2)}, u32[]{:S(2)}) collective-permute-start(bf16[128,1024]{0,1:T(8,128)(2,1)S(1)} %bitcast.149), channel_id=1, source_target_pairs={{8,10},{10,8},{12,14},{14,12},{9,11},{11,9},{13,15},{15,13},{24,26... | collective-permute-start | bytes 786440 | tf_op jit(solution)/shard_map/ppermute | solution.py:105
  141.1 4.4 %collective-permute-start.29 = (bf16[128,1024]{0,1:T(8,128)(2,1)S(1)}, bf16[128,1024]{0,1:T(8,128)(2,1)S(1)}, u32[]{:S(2)}, u32[]{:S(2)}) collective-permute-start(bf16[128,1024]{0,1:T(8,128)(2,1)S(1)} %fusion.22), channel_id=1, source_target_pairs={{12,8},{14,10},{13,9},{15,11},{28,24},{30,26},{29,25},{31,27}} | collective-permute-start | bytes 786440 | tf_op jit(solution)/shard_map/ppermute | solution.py:113
  141.8 10.4 %collective-permute-start.26 = (bf16[128,1024]{0,1:T(8,128)(2,1)S(1)}, bf16[128,1024]{0,1:T(8,128)(2,1)S(1)}, u32[]{:S(2)}, u32[]{:S(2)}) collective-permute-start(bf16[128,1024]{0,1:T(8,128)(2,1)S(1)} %bitcast.148), channel_id=1, source_target_pairs={{4,6},{6,4},{8,10},{10,8},{12,14},{14,12},{5,7},{7,5},{9,11},{11,9... | collective-permute-start | bytes 786440 | tf_op jit(solution)/shard_map/ppermute | solution.py:105
  144.8 6.6 %collective-permute-start.33 = (bf16[128,1024]{0,1:T(8,128)(2,1)S(1)}, bf16[128,1024]{0,1:T(8,128)(2,1)S(1)}, u32[]{:S(2)}, u32[]{:S(2)}) collective-permute-start(bf16[128,1024]{0,1:T(8,128)(2,1)S(1)} %collective-permute-done.32), channel_id=1, source_target_pairs={{4,8},{6,10},{8,12},{10,14},{5,9},{7,11},{9,13},{11,15},{20,24},{2... | collective-permute-start | bytes 786440 | tf_op jit(solution)/shard_map/ppermute | solution.py:40
  145.7 7.2 %collective-permute-start.30 = (bf16[128,1024]{0,1:T(8,128)(2,1)S(1)}, bf16[128,1024]{0,1:T(8,128)(2,1)S(1)}, u32[]{:S(2)}, u32[]{:S(2)}) collective-permute-start(bf16[128,1024]{0,1:T(8,128)(2,1)S(1)} %fusion.24), channel_id=1, source_target_pairs={{8,4},{10,6},{12,8},{14,10},{9,5},{11,7},{13,9},{15,11},{24,20},{2... | collective-permute-start | bytes 786440 | tf_op jit(solution)/shard_map/ppermute | solution.py:113
  146.4 8.8 %collective-permute-start.35 = (bf16[128,1024]{0,1:T(8,128)(2,1)S(1)}, bf16[128,1024]{0,1:T(8,128)(2,1)S(1)}, u32[]{:S(2)}, u32[]{:S(2)}) collective-permute-start(bf16[128,1024]{0,1:T(8,128)(2,1)S(1)} %copy-done.6), channel_id=1, source_target_pairs={{0,2},{4,6},{8,10},{12,14},{1,3},{5,7},{9,11},{13,15},{16,18},{20,... | collective-permute-start | bytes 786440 | tf_op jit(solution)/shard_map/ppermute | solution.py:42
  149.9 14.8 %collective-permute-start.25 = (bf16[128,1024]{0,1:T(8,128)(2,1)S(1)}, bf16[128,1024]{0,1:T(8,128)(2,1)S(1)}, u32[]{:S(2)}, u32[]{:S(2)}) collective-permute-start(bf16[128,1024]{0,1:T(8,128)(2,1)S(1)} %bitcast.147), channel_id=1, source_target_pairs={{2,0},{6,4},{10,8},{14,12},{3,1},{7,5},{11,9},{15,13},{18,16},{22,... | collective-permute-start | bytes 786440 | tf_op jit(solution)/shard_map/ppermute | solution.py:102
  151.4 2.3 collective-permute-start.34
  152.2 3.9 %collective-permute-start.36 = (bf16[128,1024]{0,1:T(8,128)(2,1)S(1)}, bf16[128,1024]{0,1:T(8,128)(2,1)S(1)}, u32[]{:S(2)}, u32[]{:S(2)}) collective-permute-start(bf16[128,1024]{0,1:T(8,128)(2,1)S(1)} %collective-permute-done.32), channel_id=1, source_target_pairs={{6,4},{4,6},{10,8},{8,10},{14,12},{12,14},{7,5},{5,7},{11,9},{9,11... | collective-permute-start | bytes 786440 | tf_op jit(solution)/shard_map/ppermute | solution.py:45
  152.9 3.3 %collective-permute-start.37 = (bf16[128,1024]{0,1:T(8,128)(2,1)S(1)}, bf16[128,1024]{0,1:T(8,128)(2,1)S(1)}, u32[]{:S(2)}, u32[]{:S(2)}) collective-permute-start(bf16[128,1024]{0,1:T(8,128)(2,1)S(1)} %collective-permute-done.33), channel_id=1, source_target_pairs={{10,8},{8,10},{14,12},{12,14},{11,9},{9,11},{15,13},{13,15},{26,24... | collective-permute-start | bytes 786440 | tf_op jit(solution)/shard_map/ppermute | solution.py:45
  153.7 31.0 %collective-permute-start.31 = (bf16[128,1024]{0,1:T(8,128)(2,1)S(1)}, bf16[128,1024]{0,1:T(8,128)(2,1)S(1)}, u32[]{:S(2)}, u32[]{:S(2)}) collective-permute-start(bf16[128,1024]{0,1:T(8,128)(2,1)S(1)} %fusion.26), channel_id=1, source_target_pairs={{4,0},{6,2},{8,4},{10,6},{12,8},{14,10},{5,1},{7,3},{9,5},{11,7},{... | collective-permute-start | bytes 786440 | tf_op jit(solution)/shard_map/ppermute | solution.py:113
  155.1 1.2 collective-permute-start.38
  188.3 24.4 %collective-permute-start.42 = (bf16[128,1024]{1,0:T(8,128)(2,1)}, bf16[128,1024]{1,0:T(8,128)(2,1)}, u32[]{:S(2)}, u32[]{:S(2)}) collective-permute-start(bf16[128,1024]{1,0:T(8,128)(2,1)} %copy.73), channel_id=1, source_target_pairs={{12,14},{14,12},{13,15},{15,13},{28,30},{30,28},{29,31},{31,29}} | collective-permute-start | bytes 786440 | tf_op jit(solution)/shard_map/ppermute | solution.py:105
  190.5 45.4 %collective-permute-start.41 = (bf16[128,1024]{1,0:T(8,128)(2,1)}, bf16[128,1024]{1,0:T(8,128)(2,1)}, u32[]{:S(2)}, u32[]{:S(2)}) collective-permute-start(bf16[128,1024]{1,0:T(8,128)(2,1)} %copy.71), channel_id=1, source_target_pairs={{8,10},{10,8},{12,14},{14,12},{9,11},{11,9},{13,15},{15,13},{24,26... | collective-permute-start | bytes 786440 | tf_op jit(solution)/shard_map/ppermute | solution.py:105
  193.6 31.3 %collective-permute-start.46 = (f32[464,128]{1,0:T(8,128)}, f32[464,128]{1,0:T(8,128)}, u32[]{:S(2)}, u32[]{:S(2)}) collective-permute-start(f32[464,128]{1,0:T(8,128)} %maximum_bitcast_fusion), channel_id=1, source_target_pairs={{0,8},{2,10},{4,12},{6,14},{8,0},{10,2},{12,4},{14,6},{1,9},{3,11}... | collective-permute-start | bytes 712712 | tf_op jit(solution)/shard_map/ppermute | solution.py:19
  214.6 21.3 %collective-permute-start.43 = (bf16[128,1024]{1,0:T(8,128)(2,1)}, bf16[128,1024]{1,0:T(8,128)(2,1)}, u32[]{:S(2)}, u32[]{:S(2)}) collective-permute-start(bf16[128,1024]{1,0:T(8,128)(2,1)} %add_convert_fusion.3), channel_id=1, source_target_pairs={{12,8},{14,10},{13,9},{15,11},{28,24},{30,26},{29,25},{31,27}} | collective-permute-start | bytes 786440 | tf_op jit(solution)/shard_map/ppermute | solution.py:113
  221.4 26.5 %collective-permute-start.40 = (bf16[128,1024]{1,0:T(8,128)(2,1)}, bf16[128,1024]{1,0:T(8,128)(2,1)}, u32[]{:S(2)}, u32[]{:S(2)}) collective-permute-start(bf16[128,1024]{1,0:T(8,128)(2,1)} %copy.69), channel_id=1, source_target_pairs={{4,6},{6,4},{8,10},{10,8},{12,14},{14,12},{5,7},{7,5},{9,11},{11,9... | collective-permute-start | bytes 786440 | tf_op jit(solution)/shard_map/ppermute | solution.py:105
  223.6 34.9 %collective-permute-start.39 = (bf16[128,1024]{1,0:T(8,128)(2,1)}, bf16[128,1024]{1,0:T(8,128)(2,1)S(1)}, u32[]{:S(2)}, u32[]{:S(2)}) collective-permute-start(bf16[128,1024]{1,0:T(8,128)(2,1)} %copy.68), channel_id=1, source_target_pairs={{2,0},{6,4},{10,8},{14,12},{3,1},{7,5},{11,9},{15,13},{18,16},{22,... | collective-permute-start | bytes 786440 | tf_op jit(solution)/shard_map/ppermute | solution.py:102
  225.9 14.1 %collective-permute-start.47 = (f32[464,128]{1,0:T(8,128)S(1)}, f32[464,128]{1,0:T(8,128)S(1)}, u32[]{:S(2)}, u32[]{:S(2)}) collective-permute-start(f32[464,128]{1,0:T(8,128)S(1)} %fusion.34), channel_id=1, source_target_pairs={{0,4},{2,6},{4,0},{6,2},{8,12},{10,14},{12,8},{14,10},{1,5},{3,7},... | collective-permute-start | bytes 712712 | tf_op jit(solution)/shard_map/ppermute | solution.py:19
  237.0 10.9 %collective-permute-start.44 = (bf16[128,1024]{1,0:T(8,128)(2,1)S(1)}, bf16[128,1024]{1,0:T(8,128)(2,1)S(1)}, u32[]{:S(2)}, u32[]{:S(2)}) collective-permute-start(bf16[128,1024]{1,0:T(8,128)(2,1)S(1)} %add_convert_fusion.2), channel_id=1, source_target_pairs={{8,4},{10,6},{12,8},{14,10},{9,5},{11,7},{13,9},{15,11},{24,20},{2... | collective-permute-start | bytes 786440 | tf_op jit(solution)/shard_map/ppermute | solution.py:113
  241.0 6.8 %collective-permute-start.48 = (f32[464,128]{1,0:T(8,128)S(1)}, f32[464,128]{1,0:T(8,128)S(1)}, u32[]{:S(2)}, u32[]{:S(2)}) collective-permute-start(f32[464,128]{1,0:T(8,128)S(1)} %fusion.64), channel_id=1, source_target_pairs={{0,2},{2,0},{4,6},{6,4},{8,10},{10,8},{12,14},{14,12},{1,3},{3,1},... | collective-permute-start | bytes 712712 | tf_op jit(solution)/shard_map/ppermute | solution.py:19
  247.8 8.5 %collective-permute-start.49 = (f32[464,128]{1,0:T(8,128)S(1)}, f32[464,128]{1,0:T(8,128)S(1)}, u32[]{:S(2)}, u32[]{:S(2)}) collective-permute-start(f32[464,128]{1,0:T(8,128)S(1)} %add.274), channel_id=1, source_target_pairs={{0,1},{1,0},{2,3},{3,2},{4,5},{5,4},{6,7},{7,6},{8,9},{9,8},{10,11... | collective-permute-start | bytes 712712 | tf_op jit(solution)/shard_map/ppermute | solution.py:19
  249.7 11.2 %collective-permute-start.45 = (bf16[128,1024]{1,0:T(8,128)(2,1)}, bf16[128,1024]{1,0:T(8,128)(2,1)}, u32[]{:S(2)}, u32[]{:S(2)}) collective-permute-start(bf16[128,1024]{1,0:T(8,128)(2,1)} %add_convert_fusion.1), channel_id=1, source_target_pairs={{4,0},{6,2},{8,4},{10,6},{12,8},{14,10},{5,1},{7,3},{9,5},{11,7},{... | collective-permute-start | bytes 786440 | tf_op jit(solution)/shard_map/ppermute | solution.py:113
  (23 other events, 291.6 us)

commit v16 on v15

--- a/solution.py
+++ b/solution.py
@@ -174,7 +174,7 @@
     log_gap = policy_logprob[0] - reference_logprob[0]
     part_diff = jnp.sum(seg_table * log_gap[:, None], 0)
     part_count = jnp.sum(seg_table, 0)
-    both_sums = butterfly_sum(jnp.concatenate([part_diff, part_count], 0), ("ctx",))
+    both_sums = butterfly_sum(jnp.concatenate([part_diff, part_count], 0), ("ctx",), far_first=True)
     own_diff, counts = both_sums[:SEGS], both_sums[SEGS:]
     other_diff = from_partner(own_diff, "pair", 0)
     direction = 1.0 - 2.0 * pair_index.astype(jnp.float32)

time: 264 us -> 263 us (level)
  transfers between devices with their start and end apart: 50 -> 50, of which waited for: 15 -> 14; matrix products, arithmetic and copies ran while one was open for 23% -> 23% of each run, Pallas kernels for 0% -> 0%
where the time goes in v16:
time: 263 us; the launch traced here: 261 us
  starting transfers between devices  104 us (40%)
  waiting for transfers between devices  63.9 us (24%)
  local copies, waits for them, and re-layouts  47.5 us (18%)
  matrix products  29.5 us (11%)
  other arithmetic  14.8 us (6%)
    ppermute x9, starting transfers between devices, from_partner(): lax.ppermute(shard, axis, [(i, i ^ 1 << stride) for i in range(lax.axis_s...  34.6 us
    ppermute x6, starting transfers between devices, tree_spread(): lax.ppermute(held, 'ctx', [(c - 2, c) for c in range(2 * step, count)])  25.5 us
    ppermute x6, waiting for transfers between devices, tree_return(): lax.ppermute(acc.astype(jnp.bfloat16), 'ctx', [(c, c - 2) for c in range(...  23.6 us
    ppermute x3, waiting for transfers between devices, tree_gather(): lax.ppermute(down, 'ctx', [(c + 2, c) for c in range(0, count - 2 * step)])  14.9 us
    ppermute x9, waiting for transfers between devices, from_partner(): lax.ppermute(shard, axis, [(i, i ^ 1 << stride) for i in range(lax.axis_s...  12.6 us
    dynamic_update_slice x14, local copies, waits for them, and re-layouts, tree_gather(): whole = lax.dynamic_update_slice_in_dim(whole, piece, place, 0)  10.7 us
    ppermute x3, starting transfers between devices, tree_gather(): lax.ppermute(downs[step - 1], 'ctx', [(c ^ 1, c) for c in range(0, count...  7.71 us
    unnamed x60, local copies, waits for them, and re-layouts  6.94 us
  transfers between devices with their start and end apart: 50, of which 14 were waited for; matrix products, arithmetic and copies ran while one was open for 23% of the time, Pallas kernels for 0%

profile of v16, /device:TPU:0, one launch (start us, length us, event | category | flops | bytes accessed | tf_op | source)
XLA Modules:
  0.0 261.2 jit_solution(7275876019625859896)
XLA Ops:
  0.7 5.8 %collective-permute-start.3 = (bf16[128,1024]{1,0:T(8,128)(2,1)}, bf16[128,1024]{1,0:T(8,128)(2,1)}, u32[]{:S(2)}, u32[]{:S(2)}) collective-permute-start(bf16[128,1024]{1,0:T(8,128)(2,1)} %bitcast.151), channel_id=1, source_target_pairs={{0,4},{2,6},{4,8},{6,10},{8,12},{10,14},{1,5},{3,7},{5,9},{7,11},{... | collective-permute-start | bytes 786440 | tf_op jit(solution)/shard_map/ppermute | solution.py:40
  6.5 4.1 %collective-permute-start.6 = (bf16[128,1024]{1,0:T(8,128)(2,1)}, bf16[128,1024]{1,0:T(8,128)(2,1)}, u32[]{:S(2)}, u32[]{:S(2)}) collective-permute-start(bf16[128,1024]{1,0:T(8,128)(2,1)} %bitcast.152), channel_id=1, source_target_pairs={{0,2},{4,6},{8,10},{12,14},{1,3},{5,7},{9,11},{13,15},{16,18},{20,... | collective-permute-start | bytes 786440 | tf_op jit(solution)/shard_map/ppermute | solution.py:42
  10.6 1.8 broadcast_in_dim.58
  13.2 2.8 %collective-permute-start.10 = (bf16[336,512]{1,0:T(8,128)(2,1)S(1)}, bf16[336,512]{1,0:T(8,128)(2,1)S(1)}, u32[]{:S(2)}, u32[]{:S(2)}) collective-permute-start(bf16[336,512]{1,0:T(8,128)(2,1)S(1)} %get-tuple-element.29), channel_id=1, source_target_pairs={{0,4},{2,6},{4,8},{6,10},{8,12},{10,14},{1,5},{3,7},{5,9},{7,11},{... | collective-permute-start | bytes 1032200 | tf_op jit(solution)/shard_map/ppermute | solution.py:59
  19.0 3.7 %collective-permute-done.10 = bf16[336,512]{1,0:T(8,128)(2,1)S(1)} collective-permute-done((bf16[336,512]{1,0:T(8,128)(2,1)S(1)}, bf16[336,512]{1,0:T(8,128)(2,1)S(1)}, u32[]{:S(2)}, u32[]{:S(2)}) %collective-permute-start.10) | collective-permute-done | bytes 344096 | tf_op jit(solution)/shard_map/ppermute | solution.py:59
  23.4 3.4 %collective-permute-done.11 = bf16[336,512]{1,0:T(8,128)(2,1)S(1)} collective-permute-done((bf16[336,512]{1,0:T(8,128)(2,1)S(1)}, bf16[336,512]{1,0:T(8,128)(2,1)S(1)}, u32[]{:S(2)}, u32[]{:S(2)}) %collective-permute-start.11) | collective-permute-done | bytes 344096 | tf_op jit(solution)/shard_map/ppermute | solution.py:60
  30.4 6.6 %collective-permute-done.13 = bf16[336,512]{1,0:T(8,128)(2,1)S(1)} collective-permute-done((bf16[336,512]{1,0:T(8,128)(2,1)S(1)}, bf16[336,512]{1,0:T(8,128)(2,1)S(1)}, u32[]{:S(2)}, u32[]{:S(2)}) %collective-permute-start.13) | collective-permute-done | bytes 344096 | tf_op jit(solution)/shard_map/ppermute | solution.py:60
  41.2 4.9 %collective-permute-done.15 = bf16[336,512]{1,0:T(8,128)(2,1)S(1)} collective-permute-done((bf16[336,512]{1,0:T(8,128)(2,1)S(1)}, bf16[336,512]{1,0:T(8,128)(2,1)S(1)}, u32[]{:S(2)}, u32[]{:S(2)}) %collective-permute-start.15) | collective-permute-done | bytes 344096 | tf_op jit(solution)/shard_map/ppermute | solution.py:60
  46.1 1.9 collective-permute-start.18
  50.2 3.9 %collective-permute-start.20 = (bf16[336,512]{1,0:T(8,128)(2,1)S(1)}, bf16[336,512]{1,0:T(8,128)(2,1)S(1)}, u32[]{:S(2)}, u32[]{:S(2)}) collective-permute-start(bf16[336,512]{1,0:T(8,128)(2,1)S(1)} %collective-permute-done.13), channel_id=1, source_target_pairs={{2,0},{0,2},{6,4},{4,6},{3,1},{1,3},{7,5},{5,7},{18,16},{16,18},{2... | collective-permute-start | bytes 1032200 | tf_op jit(solution)/shard_map/ppermute | solution.py:72
  54.9 4.0 %collective-permute-done.18 = bf16[336,512]{1,0:T(8,128)(2,1)S(1)} collective-permute-done((bf16[336,512]{1,0:T(8,128)(2,1)S(1)}, bf16[336,512]{1,0:T(8,128)(2,1)S(1)}, u32[]{:S(2)}, u32[]{:S(2)}) %collective-permute-start.18) | collective-permute-done | bytes 344096 | tf_op jit(solution)/shard_map/ppermute | solution.py:72
  60.3 1.9 collective-permute-start.22
  63.0 2.6 collective-permute-done.20
  65.6 3.4 %collective-permute-start = (f32[16]{0:T(128)S(1)}, f32[16]{0:T(128)S(1)}, u32[]{:S(2)}, u32[]{:S(2)}) collective-permute-start(f32[16]{0:T(128)S(1)} %pad_maximum_fusion), channel_id=1, source_target_pairs={{0,8},{2,10},{4,12},{6,14},{8,0},{10,2},{12,4},{14,6},{1,9},{3,11}... | collective-permute-start | bytes 200 | tf_op jit(solution)/shard_map/ppermute | solution.py:19
  71.2 3.2 %broadcast_in_dim.57 = bf16[2688,1024]{1,0:T(8,128)(2,1)} broadcast(bf16[]{:T(256)} %constant.74.clone.1), dimensions={} | broadcast | bytes 5505026 | tf_op jit(solution)/shard_map/broadcast_in_dim | solution.py:156
  74.4 3.8 %fusion.35 = (bf16[2688,512]{1,0:T(8,128)(2,1)S(1)}, bf16[2688,1024]{1,0:T(8,128)(2,1)}) fusion(bf16[3024,512]{1,0:T(8,128)(2,1)} %constant_dynamic-update-slice_fusion.26, bf16[2688,1024]{1,0:T(8,128)(2,1)} %broadcast_in_dim.57, s32[]{:T(128)S(6)} %select_n.156), kind=kLoop, calls=%fused_computation.123 | loop fusion | bytes 8257540 | tf_op jit(solution)/shard_map/slice | solution.py:81
  79.6 2.0 copy.94
  81.7 3.5 %collective-permute-done.1 = f32[16]{0:T(128)S(1)} collective-permute-done((f32[16]{0:T(128)S(1)}, f32[16]{0:T(128)S(1)}, u32[]{:S(2)}, u32[]{:S(2)}) %collective-permute-start.1) | collective-permute-done | bytes 96 | tf_op jit(solution)/shard_map/ppermute | solution.py:19
  85.8 3.0 %collective-permute-done.2 = f32[16]{0:T(128)S(1)} collective-permute-done((f32[16]{0:T(128)S(1)}, f32[16]{0:T(128)S(1)}, u32[]{:S(2)}, u32[]{:S(2)}) %collective-permute-start.2) | collective-permute-done | bytes 96 | tf_op jit(solution)/shard_map/ppermute | solution.py:19
  96.1 3.6 %constant_dynamic-update-slice_fusion.24 = bf16[2688,1024]{1,0:T(8,128)(2,1)} fusion(bf16[2688,1024]{1,0:T(8,128)(2,1)} %get-tuple-element.31, bf16[2688,512]{1,0:T(8,128)(2,1)} %collective-permute-done.23, s32[]{:T(128)S(6)} %select_n.185), kind=kLoop, calls=%fused_computation.84 | loop fusion | bytes 5505028 | tf_op jit(solution)/shard_map/dynamic_update_slice | solution.py:158
  99.7 4.9 %fusion.15 = bf16[128,1024]{0,1:T(8,128)(2,1)} fusion(f32[128,1024]{0,1:T(8,128)S(1)} %copy-done.2, bf16[2688,1024]{1,0:T(8,128)(2,1)} %constant_dynamic-update-slice_fusion.24, bf16[1,128,2688]{2,1,0:T(8,128)(2,1)S(1)} %copy-done), kind=kOutput, calls=%fused_computation.28 | convolution fusion | flops 704905216 | bytes 6979584 | tf_op jit(solution)/shard_map/dot_general | solution.py:167
  104.6 2.0 copy.95
  106.6 3.3 %copy.84 = bf16[1024,8,128,1]{0,2,3,1:T(8,128)(2,1)S(1)} copy(bf16[1024,8,128,1]{2,1,0,3:T(8,128)(2,1)} %bitcast.134) | data formatting | bytes 4194304 | tf_op jit(solution)/shard_map/reshape | solution.py:222
  109.9 5.7 %fusion.39 = (f32[8,2,128]{2,1,0:T(2,128)S(1)}, f32[8,2,128,1024]{2,3,1,0:T(8,128)}) fusion(pred[128,1024]{0,1:T(8,128)(4,1)S(1)} %copy-done.17, bf16[1024,8,128,1]{0,2,3,1:T(8,128)(2,1)S(1)} %copy.84, bf16[128,8,2,128]{0,3,2,1:T(8,128)(2,1)S(1)} %bitcast.138), kind=kOutput, calls=%fused_computation.127 | convolution fusion | flops 547357696 | bytes 11149312 | tf_op jit(solution)/shard_map/sub | solution.py:229
  115.6 5.0 %fusion.40 = (bf16[1024,8,128]{0,2,1:T(8,128)(2,1)S(1)}, f32[1024,8,128]{0,2,1:T(8,128)S(1)}) fusion(bf16[128,8,2,128]{3,2,1,0:T(2,128)(2,1)} %reshape_squeeze.7, f32[128]{0:T(128)S(1)} %get-tuple-element.25, f32[8,2,128,1024]{2,3,1,0:T(8,128)} %get-tuple-element.51, f32[8,2,128]{2,1,0:T(2,128)S(1)} %get-tuple-element.50), kind=kOutput, calls=%fused_computation.128 | convolution fusion | flops 544210944 | bytes 15213056 | tf_op jit(solution)/shard_map/jgtl,tjgd->ljd/dot_general | solution.py:243
  122.0 16.9 %collective-permute-start.32 = (bf16[128,1024]{0,1:T(8,128)(2,1)S(1)}, bf16[128,1024]{0,1:T(8,128)(2,1)S(1)}, u32[]{:S(2)}, u32[]{:S(2)}) collective-permute-start(bf16[128,1024]{0,1:T(8,128)(2,1)S(1)} %copy-done.6), channel_id=1, source_target_pairs={{0,4},{2,6},{4,8},{6,10},{8,12},{10,14},{1,5},{3,7},{5,9},{7,11},{... | collective-permute-start | bytes 786440 | tf_op jit(solution)/shard_map/ppermute | solution.py:40
  141.1 2.4 collective-permute-done.32
  144.9 2.4 collective-permute-start.35
  147.5 1.4 collective-permute-start.25
  154.1 1.9 fusion.1
  156.1 1.7 fusion.3
  158.8 3.5 %fusion.41 = (bf16[1024,8,128]{0,2,1:T(8,128)(2,1)S(1)}, f32[1024,8,128]{0,2,1:T(8,128)}) fusion(bf16[8,2,128,1024]{2,3,1,0:T(8,128)(2,1)S(1)} %fusion.3, bf16[128,8,2,128]{0,3,2,1:T(8,128)(2,1)S(1)} %bitcast.139), kind=kOutput, calls=%fused_computation.129 | convolution fusion | flops 537919488 | bytes 11010048 | tf_op jit(solution)/shard_map/jgtl,tjgd->ljd/dot_general | solution.py:239
  162.3 21.2 %collective-permute-done.31 = bf16[128,1024]{0,1:T(8,128)(2,1)S(1)} collective-permute-done((bf16[128,1024]{0,1:T(8,128)(2,1)S(1)}, bf16[128,1024]{0,1:T(8,128)(2,1)S(1)}, u32[]{:S(2)}, u32[]{:S(2)}) %collective-permute-start.31) | collective-permute-done | bytes 262176 | tf_op jit(solution)/shard_map/ppermute | solution.py:113
  187.1 1.4 collective-permute-start.42
  189.3 1.4 collective-permute-start.41
  192.5 17.9 %collective-permute-start.46 = (f32[464,128]{1,0:T(8,128)}, f32[464,128]{1,0:T(8,128)}, u32[]{:S(2)}, u32[]{:S(2)}) collective-permute-start(f32[464,128]{1,0:T(8,128)} %maximum_bitcast_fusion), channel_id=1, source_target_pairs={{0,8},{2,10},{4,12},{6,14},{8,0},{10,2},{12,4},{14,6},{1,9},{3,11}... | collective-permute-start | bytes 712712 | tf_op jit(solution)/shard_map/ppermute | solution.py:19
  211.3 1.9 add_convert_fusion.3
  213.2 1.4 collective-permute-start.43
  218.2 1.8 copy.69
  220.0 1.4 collective-permute-start.40
  224.5 10.0 %collective-permute-start.47 = (f32[464,128]{1,0:T(8,128)S(1)}, f32[464,128]{1,0:T(8,128)S(1)}, u32[]{:S(2)}, u32[]{:S(2)}) collective-permute-start(f32[464,128]{1,0:T(8,128)S(1)} %fusion.34), channel_id=1, source_target_pairs={{0,4},{2,6},{4,0},{6,2},{8,12},{10,14},{12,8},{14,10},{1,5},{3,7},... | collective-permute-start | bytes 712712 | tf_op jit(solution)/shard_map/ppermute | solution.py:19
  236.3 2.3 collective-permute-done.47
  239.6 2.7 %collective-permute-start.48 = (f32[464,128]{1,0:T(8,128)S(1)}, f32[464,128]{1,0:T(8,128)S(1)}, u32[]{:S(2)}, u32[]{:S(2)}) collective-permute-start(f32[464,128]{1,0:T(8,128)S(1)} %fusion.64), channel_id=1, source_target_pairs={{0,2},{2,0},{4,6},{6,4},{8,10},{10,8},{12,14},{14,12},{1,3},{3,1},... | collective-permute-start | bytes 712712 | tf_op jit(solution)/shard_map/ppermute | solution.py:19
  242.7 3.7 %collective-permute-done.48 = f32[464,128]{1,0:T(8,128)S(1)} collective-permute-done((f32[464,128]{1,0:T(8,128)S(1)}, f32[464,128]{1,0:T(8,128)S(1)}, u32[]{:S(2)}, u32[]{:S(2)}) %collective-permute-start.48) | collective-permute-done | bytes 237600 | tf_op jit(solution)/shard_map/ppermute | solution.py:19
  246.5 1.8 add_convert_fusion.1
  249.6 5.3 %fusion.11 = bf16[1,128,2688]{2,1,0:T(8,128)(2,1)} fusion(f32[128,2688]{1,0:T(8,128)S(1)} %convolution_multiply_fusion, bf16[128,1024]{0,1:T(8,128)(2,1)S(1)} %fusion.27, bf16[2688,1024]{1,0:T(8,128)(2,1)} %constant_dynamic-update-slice_fusion.24), kind=kOutput, calls=%fused_computation.19 | convolution fusion | flops 705331200 | bytes 7831552 | tf_op jit(solution)/shard_map/tk,dk->td/dot_general | solution.py:268
  257.1 2.3 collective-permute-done.45
  259.5 1.8 fusion.31
  (205 shorter events, 60.3 us)
Async XLA Ops:
  0.7 88.4 %collective-permute-start.3 = (bf16[128,1024]{1,0:T(8,128)(2,1)}, bf16[128,1024]{1,0:T(8,128)(2,1)}, u32[]{:S(2)}, u32[]{:S(2)}) collective-permute-start(bf16[128,1024]{1,0:T(8,128)(2,1)} %bitcast.151), channel_id=1, source_target_pairs={{0,4},{2,6},{4,8},{6,10},{8,12},{10,14},{1,5},{3,7},{5,9},{7,11},{... | collective-permute-start | bytes 786440 | tf_op jit(solution)/shard_map/ppermute | solution.py:40
  6.5 88.5 %collective-permute-start.6 = (bf16[128,1024]{1,0:T(8,128)(2,1)}, bf16[128,1024]{1,0:T(8,128)(2,1)}, u32[]{:S(2)}, u32[]{:S(2)}) collective-permute-start(bf16[128,1024]{1,0:T(8,128)(2,1)} %bitcast.152), channel_id=1, source_target_pairs={{0,2},{4,6},{8,10},{12,14},{1,3},{5,7},{9,11},{13,15},{16,18},{20,... | collective-permute-start | bytes 786440 | tf_op jit(solution)/shard_map/ppermute | solution.py:42
  13.2 9.5 %collective-permute-start.10 = (bf16[336,512]{1,0:T(8,128)(2,1)S(1)}, bf16[336,512]{1,0:T(8,128)(2,1)S(1)}, u32[]{:S(2)}, u32[]{:S(2)}) collective-permute-start(bf16[336,512]{1,0:T(8,128)(2,1)S(1)} %get-tuple-element.29), channel_id=1, source_target_pairs={{0,4},{2,6},{4,8},{6,10},{8,12},{10,14},{1,5},{3,7},{5,9},{7,11},{... | collective-permute-start | bytes 1032200 | tf_op jit(solution)/shard_map/ppermute | solution.py:59
  16.0 10.9 %collective-permute-start.11 = (bf16[336,512]{1,0:T(8,128)(2,1)S(1)}, bf16[336,512]{1,0:T(8,128)(2,1)S(1)}, u32[]{:S(2)}, u32[]{:S(2)}) collective-permute-start(bf16[336,512]{1,0:T(8,128)(2,1)S(1)} %get-tuple-element.29), channel_id=1, source_target_pairs={{4,0},{6,2},{8,4},{10,6},{12,8},{14,10},{5,1},{7,3},{9,5},{11,7},{... | collective-permute-start | bytes 1032200 | tf_op jit(solution)/shard_map/ppermute | solution.py:60
  17.3 31.5 %collective-permute-start.16 = (bf16[336,512]{1,0:T(8,128)(2,1)S(1)}, bf16[336,512]{1,0:T(8,128)(2,1)S(1)}, u32[]{:S(2)}, u32[]{:S(2)}) collective-permute-start(bf16[336,512]{1,0:T(8,128)(2,1)S(1)} %get-tuple-element.29), channel_id=1, source_target_pairs={{2,0},{0,2},{6,4},{4,6},{10,8},{8,10},{14,12},{12,14},{3,1},{1,3},... | collective-permute-start | bytes 1032200 | tf_op jit(solution)/shard_map/ppermute | solution.py:66
  22.7 6.2 %collective-permute-start.12 = (bf16[336,512]{1,0:T(8,128)(2,1)S(1)}, bf16[336,512]{1,0:T(8,128)(2,1)S(1)}, u32[]{:S(2)}, u32[]{:S(2)}) collective-permute-start(bf16[336,512]{1,0:T(8,128)(2,1)S(1)} %collective-permute-done.10), channel_id=1, source_target_pairs={{4,8},{6,10},{8,12},{10,14},{5,9},{7,11},{9,13},{11,15},{20,24},{2... | collective-permute-start | bytes 1032200 | tf_op jit(solution)/shard_map/ppermute | solution.py:59
  26.9 10.1 %collective-permute-start.13 = (bf16[336,512]{1,0:T(8,128)(2,1)S(1)}, bf16[336,512]{1,0:T(8,128)(2,1)S(1)}, u32[]{:S(2)}, u32[]{:S(2)}) collective-permute-start(bf16[336,512]{1,0:T(8,128)(2,1)S(1)} %collective-permute-done.11), channel_id=1, source_target_pairs={{4,0},{6,2},{8,4},{10,6},{5,1},{7,3},{9,5},{11,7},{20,16},{22,18},... | collective-permute-start | bytes 1032200 | tf_op jit(solution)/shard_map/ppermute | solution.py:60
  28.9 10.8 %collective-permute-start.14 = (bf16[336,512]{1,0:T(8,128)(2,1)S(1)}, bf16[336,512]{1,0:T(8,128)(2,1)S(1)}, u32[]{:S(2)}, u32[]{:S(2)}) collective-permute-start(bf16[336,512]{1,0:T(8,128)(2,1)S(1)} %collective-permute-done.12), channel_id=1, source_target_pairs={{8,12},{10,14},{9,13},{11,15},{24,28},{26,30},{25,29},{27,31}} | collective-permute-start | bytes 1032200 | tf_op jit(solution)/shard_map/ppermute | solution.py:59
  36.9 9.1 %collective-permute-start.15 = (bf16[336,512]{1,0:T(8,128)(2,1)S(1)}, bf16[336,512]{1,0:T(8,128)(2,1)S(1)}, u32[]{:S(2)}, u32[]{:S(2)}) collective-permute-start(bf16[336,512]{1,0:T(8,128)(2,1)S(1)} %collective-permute-done.13), channel_id=1, source_target_pairs={{4,0},{6,2},{5,1},{7,3},{20,16},{22,18},{21,17},{23,19}} | collective-permute-start | bytes 1032200 | tf_op jit(solution)/shard_map/ppermute | solution.py:60
  39.7 10.5 %collective-permute-start.17 = (bf16[336,512]{1,0:T(8,128)(2,1)S(1)}, bf16[336,512]{1,0:T(8,128)(2,1)S(1)}, u32[]{:S(2)}, u32[]{:S(2)}) collective-permute-start(bf16[336,512]{1,0:T(8,128)(2,1)S(1)} %collective-permute-done.10), channel_id=1, source_target_pairs={{6,4},{4,6},{10,8},{8,10},{14,12},{12,14},{7,5},{5,7},{11,9},{9,11... | collective-permute-start | bytes 1032200 | tf_op jit(solution)/shard_map/ppermute | solution.py:70
  46.1 12.8 %collective-permute-start.18 = (bf16[336,512]{1,0:T(8,128)(2,1)S(1)}, bf16[336,512]{1,0:T(8,128)(2,1)S(1)}, u32[]{:S(2)}, u32[]{:S(2)}) collective-permute-start(bf16[336,512]{1,0:T(8,128)(2,1)S(1)} %collective-permute-done.11), channel_id=1, source_target_pairs={{2,0},{0,2},{6,4},{4,6},{10,8},{8,10},{3,1},{1,3},{7,5},{5,7},{11,... | collective-permute-start | bytes 1032200 | tf_op jit(solution)/shard_map/ppermute | solution.py:72
  48.8 11.5 %collective-permute-start.19 = (bf16[336,512]{1,0:T(8,128)(2,1)S(1)}, bf16[336,512]{1,0:T(8,128)(2,1)S(1)}, u32[]{:S(2)}, u32[]{:S(2)}) collective-permute-start(bf16[336,512]{1,0:T(8,128)(2,1)S(1)} %collective-permute-done.12), channel_id=1, source_target_pairs={{10,8},{8,10},{14,12},{12,14},{11,9},{9,11},{15,13},{13,15},{26,24... | collective-permute-start | bytes 1032200 | tf_op jit(solution)/shard_map/ppermute | solution.py:70
  50.2 15.4 %collective-permute-start.20 = (bf16[336,512]{1,0:T(8,128)(2,1)S(1)}, bf16[336,512]{1,0:T(8,128)(2,1)S(1)}, u32[]{:S(2)}, u32[]{:S(2)}) collective-permute-start(bf16[336,512]{1,0:T(8,128)(2,1)S(1)} %collective-permute-done.13), channel_id=1, source_target_pairs={{2,0},{0,2},{6,4},{4,6},{3,1},{1,3},{7,5},{5,7},{18,16},{16,18},{2... | collective-permute-start | bytes 1032200 | tf_op jit(solution)/shard_map/ppermute | solution.py:72
  58.8 10.9 %collective-permute-start.21 = (bf16[336,512]{1,0:T(8,128)(2,1)S(1)}, bf16[336,512]{1,0:T(8,128)(2,1)S(1)}, u32[]{:S(2)}, u32[]{:S(2)}) collective-permute-start(bf16[336,512]{1,0:T(8,128)(2,1)S(1)} %collective-permute-done.14), channel_id=1, source_target_pairs={{14,12},{12,14},{15,13},{13,15},{30,28},{28,30},{31,29},{29,31}} | collective-permute-start | bytes 1032200 | tf_op jit(solution)/shard_map/ppermute | solution.py:70
  60.3 10.1 %collective-permute-start.22 = (bf16[336,512]{1,0:T(8,128)(2,1)S(1)}, bf16[336,512]{1,0:T(8,128)(2,1)S(1)}, u32[]{:S(2)}, u32[]{:S(2)}) collective-permute-start(bf16[336,512]{1,0:T(8,128)(2,1)S(1)} %collective-permute-done.15), channel_id=1, source_target_pairs={{2,0},{0,2},{3,1},{1,3},{18,16},{16,18},{19,17},{17,19}} | collective-permute-start | bytes 1032200 | tf_op jit(solution)/shard_map/ppermute | solution.py:72
  65.6 16.0 %collective-permute-start = (f32[16]{0:T(128)S(1)}, f32[16]{0:T(128)S(1)}, u32[]{:S(2)}, u32[]{:S(2)}) collective-permute-start(f32[16]{0:T(128)S(1)} %pad_maximum_fusion), channel_id=1, source_target_pairs={{0,8},{2,10},{4,12},{6,14},{8,0},{10,2},{12,4},{14,6},{1,9},{3,11}... | collective-permute-start | bytes 200 | tf_op jit(solution)/shard_map/ppermute | solution.py:19
  78.1 18.0 %collective-permute-start.23 = (bf16[2688,512]{1,0:T(8,128)(2,1)S(1)}, bf16[2688,512]{1,0:T(8,128)(2,1)}, u32[]{:S(2)}, u32[]{:S(2)}) collective-permute-start(bf16[2688,512]{1,0:T(8,128)(2,1)S(1)} %get-tuple-element.30), channel_id=1, source_target_pairs={{0,1},{1,0},{2,3},{3,2},{4,5},{5,4},{6,7},{7,6},{8,9},{9,8},{10,11... | collective-permute-start | bytes 8257544 | tf_op jit(solution)/shard_map/ppermute | solution.py:19
  81.7 3.5 %collective-permute-start.1 = (f32[16]{0:T(128)S(1)}, f32[16]{0:T(128)S(1)}, u32[]{:S(2)}, u32[]{:S(2)}) collective-permute-start(f32[16]{0:T(128)S(1)} %fusion.65), channel_id=1, source_target_pairs={{0,4},{2,6},{4,0},{6,2},{8,12},{10,14},{12,8},{14,10},{1,5},{3,7},... | collective-permute-start | bytes 200 | tf_op jit(solution)/shard_map/ppermute | solution.py:19
  85.2 3.5 %collective-permute-start.2 = (f32[16]{0:T(128)S(1)}, f32[16]{0:T(128)S(1)}, u32[]{:S(2)}, u32[]{:S(2)}) collective-permute-start(f32[16]{0:T(128)S(1)} %add.231), channel_id=1, source_target_pairs={{0,2},{2,0},{4,6},{6,4},{8,10},{10,8},{12,14},{14,12},{1,3},{3,1},... | collective-permute-start | bytes 200 | tf_op jit(solution)/shard_map/ppermute | solution.py:19
  90.2 3.9 %collective-permute-start.5 = (bf16[128,1024]{1,0:T(8,128)(2,1)S(1)}, bf16[128,1024]{1,0:T(8,128)(2,1)S(1)}, u32[]{:S(2)}, u32[]{:S(2)}) collective-permute-start(bf16[128,1024]{1,0:T(8,128)(2,1)S(1)} %collective-permute-done.4), channel_id=1, source_target_pairs={{8,12},{10,14},{9,13},{11,15},{24,28},{26,30},{25,29},{27,31}} | collective-permute-start | bytes 786440 | tf_op jit(solution)/shard_map/ppermute | solution.py:40
  92.7 3.3 %collective-permute-start.7 = (bf16[128,1024]{1,0:T(8,128)(2,1)}, bf16[128,1024]{1,0:T(8,128)(2,1)S(1)}, u32[]{:S(2)}, u32[]{:S(2)}) collective-permute-start(bf16[128,1024]{1,0:T(8,128)(2,1)} %collective-permute-done.3), channel_id=1, source_target_pairs={{6,4},{4,6},{10,8},{8,10},{14,12},{12,14},{7,5},{5,7},{11,9},{9,11... | collective-permute-start | bytes 786440 | tf_op jit(solution)/shard_map/ppermute | solution.py:45
  93.4 2.6 %collective-permute-start.8 = (bf16[128,1024]{1,0:T(8,128)(2,1)S(1)}, bf16[128,1024]{1,0:T(8,128)(2,1)S(1)}, u32[]{:S(2)}, u32[]{:S(2)}) collective-permute-start(bf16[128,1024]{1,0:T(8,128)(2,1)S(1)} %collective-permute-done.4), channel_id=1, source_target_pairs={{10,8},{8,10},{14,12},{12,14},{11,9},{9,11},{15,13},{13,15},{26,24... | collective-permute-start | bytes 786440 | tf_op jit(solution)/shard_map/ppermute | solution.py:45
  94.1 2.0 collective-permute-start.9
  121.1 18.4 %collective-permute-start.28 = (bf16[128,1024]{0,1:T(8,128)(2,1)S(1)}, bf16[128,1024]{0,1:T(8,128)(2,1)S(1)}, u32[]{:S(2)}, u32[]{:S(2)}) collective-permute-start(bf16[128,1024]{0,1:T(8,128)(2,1)S(1)} %bitcast.150), channel_id=1, source_target_pairs={{12,14},{14,12},{13,15},{15,13},{28,30},{30,28},{29,31},{31,29}} | collective-permute-start | bytes 786440 | tf_op jit(solution)/shard_map/ppermute | solution.py:105
  122.0 21.5 %collective-permute-start.32 = (bf16[128,1024]{0,1:T(8,128)(2,1)S(1)}, bf16[128,1024]{0,1:T(8,128)(2,1)S(1)}, u32[]{:S(2)}, u32[]{:S(2)}) collective-permute-start(bf16[128,1024]{0,1:T(8,128)(2,1)S(1)} %copy-done.6), channel_id=1, source_target_pairs={{0,4},{2,6},{4,8},{6,10},{8,12},{10,14},{1,5},{3,7},{5,9},{7,11},{... | collective-permute-start | bytes 786440 | tf_op jit(solution)/shard_map/ppermute | solution.py:40
  138.9 5.2 %collective-permute-start.27 = (bf16[128,1024]{0,1:T(8,128)(2,1)S(1)}, bf16[128,1024]{0,1:T(8,128)(2,1)S(1)}, u32[]{:S(2)}, u32[]{:S(2)}) collective-permute-start(bf16[128,1024]{0,1:T(8,128)(2,1)S(1)} %bitcast.149), channel_id=1, source_target_pairs={{8,10},{10,8},{12,14},{14,12},{9,11},{11,9},{13,15},{15,13},{24,26... | collective-permute-start | bytes 786440 | tf_op jit(solution)/shard_map/ppermute | solution.py:105
  139.7 4.4 %collective-permute-start.29 = (bf16[128,1024]{0,1:T(8,128)(2,1)S(1)}, bf16[128,1024]{0,1:T(8,128)(2,1)S(1)}, u32[]{:S(2)}, u32[]{:S(2)}) collective-permute-start(bf16[128,1024]{0,1:T(8,128)(2,1)S(1)} %fusion.22), channel_id=1, source_target_pairs={{12,8},{14,10},{13,9},{15,11},{28,24},{30,26},{29,25},{31,27}} | collective-permute-start | bytes 786440 | tf_op jit(solution)/shard_map/ppermute | solution.py:113
  140.4 9.4 %collective-permute-start.26 = (bf16[128,1024]{0,1:T(8,128)(2,1)S(1)}, bf16[128,1024]{0,1:T(8,128)(2,1)S(1)}, u32[]{:S(2)}, u32[]{:S(2)}) collective-permute-start(bf16[128,1024]{0,1:T(8,128)(2,1)S(1)} %bitcast.148), channel_id=1, source_target_pairs={{4,6},{6,4},{8,10},{10,8},{12,14},{14,12},{5,7},{7,5},{9,11},{11,9... | collective-permute-start | bytes 786440 | tf_op jit(solution)/shard_map/ppermute | solution.py:105
  143.4 5.5 %collective-permute-start.33 = (bf16[128,1024]{0,1:T(8,128)(2,1)S(1)}, bf16[128,1024]{0,1:T(8,128)(2,1)S(1)}, u32[]{:S(2)}, u32[]{:S(2)}) collective-permute-start(bf16[128,1024]{0,1:T(8,128)(2,1)S(1)} %collective-permute-done.32), channel_id=1, source_target_pairs={{4,8},{6,10},{8,12},{10,14},{5,9},{7,11},{9,13},{11,15},{20,24},{2... | collective-permute-start | bytes 786440 | tf_op jit(solution)/shard_map/ppermute | solution.py:40
  144.3 6.2 %collective-permute-start.30 = (bf16[128,1024]{0,1:T(8,128)(2,1)S(1)}, bf16[128,1024]{0,1:T(8,128)(2,1)S(1)}, u32[]{:S(2)}, u32[]{:S(2)}) collective-permute-start(bf16[128,1024]{0,1:T(8,128)(2,1)S(1)} %fusion.24), channel_id=1, source_target_pairs={{8,4},{10,6},{12,8},{14,10},{9,5},{11,7},{13,9},{15,11},{24,20},{2... | collective-permute-start | bytes 786440 | tf_op jit(solution)/shard_map/ppermute | solution.py:113
  144.9 7.8 %collective-permute-start.35 = (bf16[128,1024]{0,1:T(8,128)(2,1)S(1)}, bf16[128,1024]{0,1:T(8,128)(2,1)S(1)}, u32[]{:S(2)}, u32[]{:S(2)}) collective-permute-start(bf16[128,1024]{0,1:T(8,128)(2,1)S(1)} %copy-done.6), channel_id=1, source_target_pairs={{0,2},{4,6},{8,10},{12,14},{1,3},{5,7},{9,11},{13,15},{16,18},{20,... | collective-permute-start | bytes 786440 | tf_op jit(solution)/shard_map/ppermute | solution.py:42
  147.5 14.8 %collective-permute-start.25 = (bf16[128,1024]{0,1:T(8,128)(2,1)S(1)}, bf16[128,1024]{0,1:T(8,128)(2,1)S(1)}, u32[]{:S(2)}, u32[]{:S(2)}) collective-permute-start(bf16[128,1024]{0,1:T(8,128)(2,1)S(1)} %bitcast.147), channel_id=1, source_target_pairs={{2,0},{6,4},{10,8},{14,12},{3,1},{7,5},{11,9},{15,13},{18,16},{22,... | collective-permute-start | bytes 786440 | tf_op jit(solution)/shard_map/ppermute | solution.py:102
  149.0 2.3 collective-permute-start.34
  149.8 3.9 %collective-permute-start.36 = (bf16[128,1024]{0,1:T(8,128)(2,1)S(1)}, bf16[128,1024]{0,1:T(8,128)(2,1)S(1)}, u32[]{:S(2)}, u32[]{:S(2)}) collective-permute-start(bf16[128,1024]{0,1:T(8,128)(2,1)S(1)} %collective-permute-done.32), channel_id=1, source_target_pairs={{6,4},{4,6},{10,8},{8,10},{14,12},{12,14},{7,5},{5,7},{11,9},{9,11... | collective-permute-start | bytes 786440 | tf_op jit(solution)/shard_map/ppermute | solution.py:45
  150.5 3.3 %collective-permute-start.37 = (bf16[128,1024]{0,1:T(8,128)(2,1)S(1)}, bf16[128,1024]{0,1:T(8,128)(2,1)S(1)}, u32[]{:S(2)}, u32[]{:S(2)}) collective-permute-start(bf16[128,1024]{0,1:T(8,128)(2,1)S(1)} %collective-permute-done.33), channel_id=1, source_target_pairs={{10,8},{8,10},{14,12},{12,14},{11,9},{9,11},{15,13},{13,15},{26,24... | collective-permute-start | bytes 786440 | tf_op jit(solution)/shard_map/ppermute | solution.py:45
  151.3 32.2 %collective-permute-start.31 = (bf16[128,1024]{0,1:T(8,128)(2,1)S(1)}, bf16[128,1024]{0,1:T(8,128)(2,1)S(1)}, u32[]{:S(2)}, u32[]{:S(2)}) collective-permute-start(bf16[128,1024]{0,1:T(8,128)(2,1)S(1)} %fusion.26), channel_id=1, source_target_pairs={{4,0},{6,2},{8,4},{10,6},{12,8},{14,10},{5,1},{7,3},{9,5},{11,7},{... | collective-permute-start | bytes 786440 | tf_op jit(solution)/shard_map/ppermute | solution.py:113
  152.7 1.2 collective-permute-start.38
  187.1 24.2 %collective-permute-start.42 = (bf16[128,1024]{1,0:T(8,128)(2,1)}, bf16[128,1024]{1,0:T(8,128)(2,1)}, u32[]{:S(2)}, u32[]{:S(2)}) collective-permute-start(bf16[128,1024]{1,0:T(8,128)(2,1)} %copy.73), channel_id=1, source_target_pairs={{12,14},{14,12},{13,15},{15,13},{28,30},{30,28},{29,31},{31,29}} | collective-permute-start | bytes 786440 | tf_op jit(solution)/shard_map/ppermute | solution.py:105
  189.3 45.2 %collective-permute-start.41 = (bf16[128,1024]{1,0:T(8,128)(2,1)}, bf16[128,1024]{1,0:T(8,128)(2,1)}, u32[]{:S(2)}, u32[]{:S(2)}) collective-permute-start(bf16[128,1024]{1,0:T(8,128)(2,1)} %copy.71), channel_id=1, source_target_pairs={{8,10},{10,8},{12,14},{14,12},{9,11},{11,9},{13,15},{15,13},{24,26... | collective-permute-start | bytes 786440 | tf_op jit(solution)/shard_map/ppermute | solution.py:105
  192.5 31.1 %collective-permute-start.46 = (f32[464,128]{1,0:T(8,128)}, f32[464,128]{1,0:T(8,128)}, u32[]{:S(2)}, u32[]{:S(2)}) collective-permute-start(f32[464,128]{1,0:T(8,128)} %maximum_bitcast_fusion), channel_id=1, source_target_pairs={{0,8},{2,10},{4,12},{6,14},{8,0},{10,2},{12,4},{14,6},{1,9},{3,11}... | collective-permute-start | bytes 712712 | tf_op jit(solution)/shard_map/ppermute | solution.py:19
  213.2 21.3 %collective-permute-start.43 = (bf16[128,1024]{1,0:T(8,128)(2,1)}, bf16[128,1024]{1,0:T(8,128)(2,1)}, u32[]{:S(2)}, u32[]{:S(2)}) collective-permute-start(bf16[128,1024]{1,0:T(8,128)(2,1)} %add_convert_fusion.3), channel_id=1, source_target_pairs={{12,8},{14,10},{13,9},{15,11},{28,24},{30,26},{29,25},{31,27}} | collective-permute-start | bytes 786440 | tf_op jit(solution)/shard_map/ppermute | solution.py:113
  220.0 26.5 %collective-permute-start.40 = (bf16[128,1024]{1,0:T(8,128)(2,1)}, bf16[128,1024]{1,0:T(8,128)(2,1)}, u32[]{:S(2)}, u32[]{:S(2)}) collective-permute-start(bf16[128,1024]{1,0:T(8,128)(2,1)} %copy.69), channel_id=1, source_target_pairs={{4,6},{6,4},{8,10},{10,8},{12,14},{14,12},{5,7},{7,5},{9,11},{11,9... | collective-permute-start | bytes 786440 | tf_op jit(solution)/shard_map/ppermute | solution.py:105
  222.2 34.9 %collective-permute-start.39 = (bf16[128,1024]{1,0:T(8,128)(2,1)}, bf16[128,1024]{1,0:T(8,128)(2,1)S(1)}, u32[]{:S(2)}, u32[]{:S(2)}) collective-permute-start(bf16[128,1024]{1,0:T(8,128)(2,1)} %copy.68), channel_id=1, source_target_pairs={{2,0},{6,4},{10,8},{14,12},{3,1},{7,5},{11,9},{15,13},{18,16},{22,... | collective-permute-start | bytes 786440 | tf_op jit(solution)/shard_map/ppermute | solution.py:102
  224.5 14.1 %collective-permute-start.47 = (f32[464,128]{1,0:T(8,128)S(1)}, f32[464,128]{1,0:T(8,128)S(1)}, u32[]{:S(2)}, u32[]{:S(2)}) collective-permute-start(f32[464,128]{1,0:T(8,128)S(1)} %fusion.34), channel_id=1, source_target_pairs={{0,4},{2,6},{4,0},{6,2},{8,12},{10,14},{12,8},{14,10},{1,5},{3,7},... | collective-permute-start | bytes 712712 | tf_op jit(solution)/shard_map/ppermute | solution.py:19
  235.7 10.9 %collective-permute-start.44 = (bf16[128,1024]{1,0:T(8,128)(2,1)S(1)}, bf16[128,1024]{1,0:T(8,128)(2,1)S(1)}, u32[]{:S(2)}, u32[]{:S(2)}) collective-permute-start(bf16[128,1024]{1,0:T(8,128)(2,1)S(1)} %add_convert_fusion.2), channel_id=1, source_target_pairs={{8,4},{10,6},{12,8},{14,10},{9,5},{11,7},{13,9},{15,11},{24,20},{2... | collective-permute-start | bytes 786440 | tf_op jit(solution)/shard_map/ppermute | solution.py:113
  239.6 6.8 %collective-permute-start.48 = (f32[464,128]{1,0:T(8,128)S(1)}, f32[464,128]{1,0:T(8,128)S(1)}, u32[]{:S(2)}, u32[]{:S(2)}) collective-permute-start(f32[464,128]{1,0:T(8,128)S(1)} %fusion.64), channel_id=1, source_target_pairs={{0,2},{2,0},{4,6},{6,4},{8,10},{10,8},{12,14},{14,12},{1,3},{3,1},... | collective-permute-start | bytes 712712 | tf_op jit(solution)/shard_map/ppermute | solution.py:19
  246.4 8.5 %collective-permute-start.49 = (f32[464,128]{1,0:T(8,128)S(1)}, f32[464,128]{1,0:T(8,128)S(1)}, u32[]{:S(2)}, u32[]{:S(2)}) collective-permute-start(f32[464,128]{1,0:T(8,128)S(1)} %add.274), channel_id=1, source_target_pairs={{0,1},{1,0},{2,3},{3,2},{4,5},{5,4},{6,7},{7,6},{8,9},{9,8},{10,11... | collective-permute-start | bytes 712712 | tf_op jit(solution)/shard_map/ppermute | solution.py:19
  248.3 11.2 %collective-permute-start.45 = (bf16[128,1024]{1,0:T(8,128)(2,1)}, bf16[128,1024]{1,0:T(8,128)(2,1)}, u32[]{:S(2)}, u32[]{:S(2)}) collective-permute-start(bf16[128,1024]{1,0:T(8,128)(2,1)} %add_convert_fusion.1), channel_id=1, source_target_pairs={{4,0},{6,2},{8,4},{10,6},{12,8},{14,10},{5,1},{7,3},{9,5},{11,7},{... | collective-permute-start | bytes 786440 | tf_op jit(solution)/shard_map/ppermute | solution.py:113
  (23 other events, 289.9 us)

commit v17 on v16

--- a/solution.py
+++ b/solution.py
@@ -50,9 +50,9 @@
 def tree_gather(block, ctx_index, levels):
     count = 2 * levels
     partner = jnp.bitwise_xor(ctx_index, 1)
-    got = [block]
-    owners = [ctx_index]
-    valid = [ctx_index >= 0]
+    got = [block, lax.ppermute(block, "ctx", [(c ^ 1, c) for c in range(count)])]
+    owners = [ctx_index, partner]
+    valid = [ctx_index >= 0, ctx_index >= 0]
     up, down = block, block
     ups, downs = [], []
     for step in range(1, levels):
@@ -63,9 +63,6 @@
         got += [up, down]
         owners += [ctx_index - 2 * step, ctx_index + 2 * step]
         valid += [ctx_index >= 2 * step, ctx_index < count - 2 * step]
-    got.append(lax.ppermute(block, "ctx", [(c ^ 1, c) for c in range(count)]))
-    owners.append(partner)
-    valid.append(ctx_index >= 0)
     for step in range(1, levels):
         got.append(lax.ppermute(ups[step - 1], "ctx", [(c ^ 1, c) for c in range(2 * step, count)]))
         got.append(

time: 263 us -> 260 us (0.989)
    ppermute x9, starting transfers between devices: 34.6 us -> 31.7 us  [from_partner(): lax.ppermute(shard, axis, [(i, i ^ 1 << stride) for i in range(lax.axis_s...]
  transfers between devices with their start and end apart: 50 -> 50, of which waited for: 14 -> 14; matrix products, arithmetic and copies ran while one was open for 23% -> 24% of each run, Pallas kernels for 0% -> 0%
where the time goes in v17:
time: 260 us; the launch traced here: 258 us
  starting transfers between devices  102 us (39%)
  waiting for transfers between devices  61.9 us (24%)
  local copies, waits for them, and re-layouts  47.5 us (18%)
  matrix products  29.5 us (11%)
  other arithmetic  14.8 us (6%)
    ppermute x9, starting transfers between devices, from_partner(): lax.ppermute(shard, axis, [(i, i ^ 1 << stride) for i in range(lax.axis_s...  31.7 us
    ppermute x6, starting transfers between devices, tree_spread(): lax.ppermute(held, 'ctx', [(c - 2, c) for c in range(2 * step, count)])  26.3 us
    ppermute x6, waiting for transfers between devices, tree_return(): lax.ppermute(acc.astype(jnp.bfloat16), 'ctx', [(c, c - 2) for c in range(...  23 us
    ppermute x3, waiting for transfers between devices, tree_gather(): lax.ppermute(down, 'ctx', [(c + 2, c) for c in range(0, count - 2 * step)])  14.8 us
    ppermute x9, waiting for transfers between devices, from_partner(): lax.ppermute(shard, axis, [(i, i ^ 1 << stride) for i in range(lax.axis_s...  12.2 us
    dynamic_update_slice x14, local copies, waits for them, and re-layouts, tree_gather(): whole = lax.dynamic_update_slice_in_dim(whole, piece, place, 0)  10.7 us
    ppermute x3, starting transfers between devices, tree_gather(): lax.ppermute(downs[step - 1], 'ctx', [(c ^ 1, c) for c in range(0, count...  8.24 us
    unnamed x60, local copies, waits for them, and re-layouts  6.94 us
  transfers between devices with their start and end apart: 50, of which 14 were waited for; matrix products, arithmetic and copies ran while one was open for 24% of the time, Pallas kernels for 0%

profile of v17, /device:TPU:0, one launch (start us, length us, event | category | flops | bytes accessed | tf_op | source)
XLA Modules:
  0.0 258.1 jit_solution(1169830148806569385)
XLA Ops:
  0.7 5.8 %collective-permute-start.3 = (bf16[128,1024]{1,0:T(8,128)(2,1)}, bf16[128,1024]{1,0:T(8,128)(2,1)}, u32[]{:S(2)}, u32[]{:S(2)}) collective-permute-start(bf16[128,1024]{1,0:T(8,128)(2,1)} %bitcast.151), channel_id=1, source_target_pairs={{0,4},{2,6},{4,8},{6,10},{8,12},{10,14},{1,5},{3,7},{5,9},{7,11},{... | collective-permute-start | bytes 786440 | tf_op jit(solution)/shard_map/ppermute | solution.py:40
  6.5 4.1 %collective-permute-start.6 = (bf16[128,1024]{1,0:T(8,128)(2,1)}, bf16[128,1024]{1,0:T(8,128)(2,1)}, u32[]{:S(2)}, u32[]{:S(2)}) collective-permute-start(bf16[128,1024]{1,0:T(8,128)(2,1)} %bitcast.152), channel_id=1, source_target_pairs={{0,2},{4,6},{8,10},{12,14},{1,3},{5,7},{9,11},{13,15},{16,18},{20,... | collective-permute-start | bytes 786440 | tf_op jit(solution)/shard_map/ppermute | solution.py:42
  10.6 1.8 broadcast_in_dim.58
  13.2 2.8 %collective-permute-start.11 = (bf16[336,512]{1,0:T(8,128)(2,1)S(1)}, bf16[336,512]{1,0:T(8,128)(2,1)S(1)}, u32[]{:S(2)}, u32[]{:S(2)}) collective-permute-start(bf16[336,512]{1,0:T(8,128)(2,1)S(1)} %get-tuple-element.29), channel_id=1, source_target_pairs={{0,4},{2,6},{4,8},{6,10},{8,12},{10,14},{1,5},{3,7},{5,9},{7,11},{... | collective-permute-start | bytes 1032200 | tf_op jit(solution)/shard_map/ppermute | solution.py:59
  16.0 1.3 collective-permute-start.12
  18.9 3.8 %collective-permute-done.11 = bf16[336,512]{1,0:T(8,128)(2,1)S(1)} collective-permute-done((bf16[336,512]{1,0:T(8,128)(2,1)S(1)}, bf16[336,512]{1,0:T(8,128)(2,1)S(1)}, u32[]{:S(2)}, u32[]{:S(2)}) %collective-permute-start.11) | collective-permute-done | bytes 344096 | tf_op jit(solution)/shard_map/ppermute | solution.py:59
  24.1 2.7 %collective-permute-done.12 = bf16[336,512]{1,0:T(8,128)(2,1)S(1)} collective-permute-done((bf16[336,512]{1,0:T(8,128)(2,1)S(1)}, bf16[336,512]{1,0:T(8,128)(2,1)S(1)}, u32[]{:S(2)}, u32[]{:S(2)}) %collective-permute-start.12) | collective-permute-done | bytes 344096 | tf_op jit(solution)/shard_map/ppermute | solution.py:60
  31.1 8.9 %collective-permute-done.14 = bf16[336,512]{1,0:T(8,128)(2,1)S(1)} collective-permute-done((bf16[336,512]{1,0:T(8,128)(2,1)S(1)}, bf16[336,512]{1,0:T(8,128)(2,1)S(1)}, u32[]{:S(2)}, u32[]{:S(2)}) %collective-permute-start.14) | collective-permute-done | bytes 344096 | tf_op jit(solution)/shard_map/ppermute | solution.py:60
  42.8 2.5 collective-permute-start.18
  46.1 3.1 %collective-permute-done.16 = bf16[336,512]{1,0:T(8,128)(2,1)S(1)} collective-permute-done((bf16[336,512]{1,0:T(8,128)(2,1)S(1)}, bf16[336,512]{1,0:T(8,128)(2,1)S(1)}, u32[]{:S(2)}, u32[]{:S(2)}) %collective-permute-start.16) | collective-permute-done | bytes 344096 | tf_op jit(solution)/shard_map/ppermute | solution.py:60
  50.6 2.4 collective-permute-start.20
  55.3 3.4 %collective-permute-start.22 = (bf16[336,512]{1,0:T(8,128)(2,1)S(1)}, bf16[336,512]{1,0:T(8,128)(2,1)S(1)}, u32[]{:S(2)}, u32[]{:S(2)}) collective-permute-start(bf16[336,512]{1,0:T(8,128)(2,1)S(1)} %collective-permute-done.16), channel_id=1, source_target_pairs={{2,0},{0,2},{3,1},{1,3},{18,16},{16,18},{19,17},{17,19}} | collective-permute-start | bytes 1032200 | tf_op jit(solution)/shard_map/ppermute | solution.py:69
  59.4 3.6 %collective-permute-done.20 = bf16[336,512]{1,0:T(8,128)(2,1)S(1)} collective-permute-done((bf16[336,512]{1,0:T(8,128)(2,1)S(1)}, bf16[336,512]{1,0:T(8,128)(2,1)S(1)}, u32[]{:S(2)}, u32[]{:S(2)}) %collective-permute-start.20) | collective-permute-done | bytes 344096 | tf_op jit(solution)/shard_map/ppermute | solution.py:69
  64.5 2.2 collective-permute-done.22
  67.5 3.2 %broadcast_in_dim.57 = bf16[2688,1024]{1,0:T(8,128)(2,1)} broadcast(bf16[]{:T(256)} %constant.74.clone.1), dimensions={} | broadcast | bytes 5505026 | tf_op jit(solution)/shard_map/broadcast_in_dim | solution.py:153
  70.6 3.8 %fusion.35 = (bf16[2688,512]{1,0:T(8,128)(2,1)S(1)}, bf16[2688,1024]{1,0:T(8,128)(2,1)}) fusion(bf16[3024,512]{1,0:T(8,128)(2,1)} %constant_dynamic-update-slice_fusion.26, bf16[2688,1024]{1,0:T(8,128)(2,1)} %broadcast_in_dim.57, s32[]{:T(128)S(6)} %select_n.156), kind=kLoop, calls=%fused_computation.123 | loop fusion | bytes 8257540 | tf_op jit(solution)/shard_map/slice | solution.py:78
  75.8 2.0 copy.94
  78.0 3.5 %collective-permute-done.1 = f32[16]{0:T(128)S(1)} collective-permute-done((f32[16]{0:T(128)S(1)}, f32[16]{0:T(128)S(1)}, u32[]{:S(2)}, u32[]{:S(2)}) %collective-permute-start.1) | collective-permute-done | bytes 96 | tf_op jit(solution)/shard_map/ppermute | solution.py:19
  82.5 2.5 collective-permute-done.2
  92.4 3.6 %constant_dynamic-update-slice_fusion.24 = bf16[2688,1024]{1,0:T(8,128)(2,1)} fusion(bf16[2688,1024]{1,0:T(8,128)(2,1)} %get-tuple-element.31, bf16[2688,512]{1,0:T(8,128)(2,1)} %collective-permute-done.23, s32[]{:T(128)S(6)} %select_n.185), kind=kLoop, calls=%fused_computation.84 | loop fusion | bytes 5505028 | tf_op jit(solution)/shard_map/dynamic_update_slice | solution.py:155
  96.0 4.9 %fusion.15 = bf16[128,1024]{0,1:T(8,128)(2,1)} fusion(f32[128,1024]{0,1:T(8,128)S(1)} %copy-done.2, bf16[2688,1024]{1,0:T(8,128)(2,1)} %constant_dynamic-update-slice_fusion.24, bf16[1,128,2688]{2,1,0:T(8,128)(2,1)S(1)} %copy-done), kind=kOutput, calls=%fused_computation.28 | convolution fusion | flops 704905216 | bytes 6979584 | tf_op jit(solution)/shard_map/dot_general | solution.py:164
  100.9 2.0 copy.95
  102.9 3.3 %copy.84 = bf16[1024,8,128,1]{0,2,3,1:T(8,128)(2,1)S(1)} copy(bf16[1024,8,128,1]{2,1,0,3:T(8,128)(2,1)} %bitcast.134) | data formatting | bytes 4194304 | tf_op jit(solution)/shard_map/reshape | solution.py:219
  106.2 5.7 %fusion.39 = (f32[8,2,128]{2,1,0:T(2,128)S(1)}, f32[8,2,128,1024]{2,3,1,0:T(8,128)}) fusion(pred[128,1024]{0,1:T(8,128)(4,1)S(1)} %copy-done.17, bf16[1024,8,128,1]{0,2,3,1:T(8,128)(2,1)S(1)} %copy.84, bf16[128,8,2,128]{0,3,2,1:T(8,128)(2,1)S(1)} %bitcast.138), kind=kOutput, calls=%fused_computation.127 | convolution fusion | flops 547357696 | bytes 11149312 | tf_op jit(solution)/shard_map/sub | solution.py:226
  111.9 5.0 %fusion.40 = (bf16[1024,8,128]{0,2,1:T(8,128)(2,1)S(1)}, f32[1024,8,128]{0,2,1:T(8,128)S(1)}) fusion(bf16[128,8,2,128]{3,2,1,0:T(2,128)(2,1)} %reshape_squeeze.7, f32[128]{0:T(128)S(1)} %get-tuple-element.25, f32[8,2,128,1024]{2,3,1,0:T(8,128)} %get-tuple-element.51, f32[8,2,128]{2,1,0:T(2,128)S(1)} %get-tuple-element.50), kind=kOutput, calls=%fused_computation.128 | convolution fusion | flops 544210944 | bytes 15213056 | tf_op jit(solution)/shard_map/jgtl,tjgd->ljd/dot_general | solution.py:240
  118.2 17.7 %collective-permute-start.32 = (bf16[128,1024]{0,1:T(8,128)(2,1)S(1)}, bf16[128,1024]{0,1:T(8,128)(2,1)S(1)}, u32[]{:S(2)}, u32[]{:S(2)}) collective-permute-start(bf16[128,1024]{0,1:T(8,128)(2,1)S(1)} %copy-done.6), channel_id=1, source_target_pairs={{0,4},{2,6},{4,8},{6,10},{8,12},{10,14},{1,5},{3,7},{5,9},{7,11},{... | collective-permute-start | bytes 786440 | tf_op jit(solution)/shard_map/ppermute | solution.py:40
  138.1 2.4 collective-permute-done.32
  142.0 2.8 %collective-permute-start.35 = (bf16[128,1024]{0,1:T(8,128)(2,1)S(1)}, bf16[128,1024]{0,1:T(8,128)(2,1)S(1)}, u32[]{:S(2)}, u32[]{:S(2)}) collective-permute-start(bf16[128,1024]{0,1:T(8,128)(2,1)S(1)} %copy-done.6), channel_id=1, source_target_pairs={{0,2},{4,6},{8,10},{12,14},{1,3},{5,7},{9,11},{13,15},{16,18},{20,... | collective-permute-start | bytes 786440 | tf_op jit(solution)/shard_map/ppermute | solution.py:42
  144.9 1.4 collective-permute-start.25
  151.5 1.9 fusion.1
  153.5 1.7 fusion.3
  156.2 3.5 %fusion.41 = (bf16[1024,8,128]{0,2,1:T(8,128)(2,1)S(1)}, f32[1024,8,128]{0,2,1:T(8,128)}) fusion(bf16[8,2,128,1024]{2,3,1,0:T(8,128)(2,1)S(1)} %fusion.3, bf16[128,8,2,128]{0,3,2,1:T(8,128)(2,1)S(1)} %bitcast.139), kind=kOutput, calls=%fused_computation.129 | convolution fusion | flops 537919488 | bytes 11010048 | tf_op jit(solution)/shard_map/jgtl,tjgd->ljd/dot_general | solution.py:236
  159.7 20.6 %collective-permute-done.31 = bf16[128,1024]{0,1:T(8,128)(2,1)S(1)} collective-permute-done((bf16[128,1024]{0,1:T(8,128)(2,1)S(1)}, bf16[128,1024]{0,1:T(8,128)(2,1)S(1)}, u32[]{:S(2)}, u32[]{:S(2)}) %collective-permute-start.31) | collective-permute-done | bytes 262176 | tf_op jit(solution)/shard_map/ppermute | solution.py:110
  183.9 1.4 collective-permute-start.42
  186.1 1.4 collective-permute-start.41
  189.2 18.0 %collective-permute-start.46 = (f32[464,128]{1,0:T(8,128)}, f32[464,128]{1,0:T(8,128)}, u32[]{:S(2)}, u32[]{:S(2)}) collective-permute-start(f32[464,128]{1,0:T(8,128)} %maximum_bitcast_fusion), channel_id=1, source_target_pairs={{0,8},{2,10},{4,12},{6,14},{8,0},{10,2},{12,4},{14,6},{1,9},{3,11}... | collective-permute-start | bytes 712712 | tf_op jit(solution)/shard_map/ppermute | solution.py:19
  208.2 1.9 add_convert_fusion.3
  210.1 1.4 collective-permute-start.43
  215.1 1.8 copy.69
  216.9 1.4 collective-permute-start.40
  221.4 9.9 %collective-permute-start.47 = (f32[464,128]{1,0:T(8,128)S(1)}, f32[464,128]{1,0:T(8,128)S(1)}, u32[]{:S(2)}, u32[]{:S(2)}) collective-permute-start(f32[464,128]{1,0:T(8,128)S(1)} %fusion.34), channel_id=1, source_target_pairs={{0,4},{2,6},{4,0},{6,2},{8,12},{10,14},{12,8},{14,10},{1,5},{3,7},... | collective-permute-start | bytes 712712 | tf_op jit(solution)/shard_map/ppermute | solution.py:19
  233.2 2.3 collective-permute-done.47
  236.4 2.7 %collective-permute-start.48 = (f32[464,128]{1,0:T(8,128)S(1)}, f32[464,128]{1,0:T(8,128)S(1)}, u32[]{:S(2)}, u32[]{:S(2)}) collective-permute-start(f32[464,128]{1,0:T(8,128)S(1)} %fusion.64), channel_id=1, source_target_pairs={{0,2},{2,0},{4,6},{6,4},{8,10},{10,8},{12,14},{14,12},{1,3},{3,1},... | collective-permute-start | bytes 712712 | tf_op jit(solution)/shard_map/ppermute | solution.py:19
  239.5 3.7 %collective-permute-done.48 = f32[464,128]{1,0:T(8,128)S(1)} collective-permute-done((f32[464,128]{1,0:T(8,128)S(1)}, f32[464,128]{1,0:T(8,128)S(1)}, u32[]{:S(2)}, u32[]{:S(2)}) %collective-permute-start.48) | collective-permute-done | bytes 237600 | tf_op jit(solution)/shard_map/ppermute | solution.py:19
  243.4 1.8 add_convert_fusion.1
  246.4 5.4 %fusion.11 = bf16[1,128,2688]{2,1,0:T(8,128)(2,1)} fusion(f32[128,2688]{1,0:T(8,128)S(1)} %convolution_multiply_fusion, bf16[128,1024]{0,1:T(8,128)(2,1)S(1)} %fusion.27, bf16[2688,1024]{1,0:T(8,128)(2,1)} %constant_dynamic-update-slice_fusion.24), kind=kOutput, calls=%fused_computation.19 | convolution fusion | flops 705331200 | bytes 7831552 | tf_op jit(solution)/shard_map/tk,dk->td/dot_general | solution.py:265
  253.9 2.3 collective-permute-done.45
  256.3 1.8 fusion.31
  (205 shorter events, 59.4 us)
Async XLA Ops:
  0.7 84.6 %collective-permute-start.3 = (bf16[128,1024]{1,0:T(8,128)(2,1)}, bf16[128,1024]{1,0:T(8,128)(2,1)}, u32[]{:S(2)}, u32[]{:S(2)}) collective-permute-start(bf16[128,1024]{1,0:T(8,128)(2,1)} %bitcast.151), channel_id=1, source_target_pairs={{0,4},{2,6},{4,8},{6,10},{8,12},{10,14},{1,5},{3,7},{5,9},{7,11},{... | collective-permute-start | bytes 786440 | tf_op jit(solution)/shard_map/ppermute | solution.py:40
  6.5 84.8 %collective-permute-start.6 = (bf16[128,1024]{1,0:T(8,128)(2,1)}, bf16[128,1024]{1,0:T(8,128)(2,1)}, u32[]{:S(2)}, u32[]{:S(2)}) collective-permute-start(bf16[128,1024]{1,0:T(8,128)(2,1)} %bitcast.152), channel_id=1, source_target_pairs={{0,2},{4,6},{8,10},{12,14},{1,3},{5,7},{9,11},{13,15},{16,18},{20,... | collective-permute-start | bytes 786440 | tf_op jit(solution)/shard_map/ppermute | solution.py:42
  13.2 10.2 %collective-permute-start.10 = (bf16[336,512]{1,0:T(8,128)(2,1)S(1)}, bf16[336,512]{1,0:T(8,128)(2,1)S(1)}, u32[]{:S(2)}, u32[]{:S(2)}) collective-permute-start(bf16[336,512]{1,0:T(8,128)(2,1)S(1)} %get-tuple-element.29), channel_id=1, source_target_pairs={{2,0},{0,2},{6,4},{4,6},{10,8},{8,10},{14,12},{12,14},{3,1},{1,3},... | collective-permute-start | bytes 1032200 | tf_op jit(solution)/shard_map/ppermute | solution.py:53
  13.2 9.5 %collective-permute-start.11 = (bf16[336,512]{1,0:T(8,128)(2,1)S(1)}, bf16[336,512]{1,0:T(8,128)(2,1)S(1)}, u32[]{:S(2)}, u32[]{:S(2)}) collective-permute-start(bf16[336,512]{1,0:T(8,128)(2,1)S(1)} %get-tuple-element.29), channel_id=1, source_target_pairs={{0,4},{2,6},{4,8},{6,10},{8,12},{10,14},{1,5},{3,7},{5,9},{7,11},{... | collective-permute-start | bytes 1032200 | tf_op jit(solution)/shard_map/ppermute | solution.py:59
  16.0 10.9 %collective-permute-start.12 = (bf16[336,512]{1,0:T(8,128)(2,1)S(1)}, bf16[336,512]{1,0:T(8,128)(2,1)S(1)}, u32[]{:S(2)}, u32[]{:S(2)}) collective-permute-start(bf16[336,512]{1,0:T(8,128)(2,1)S(1)} %get-tuple-element.29), channel_id=1, source_target_pairs={{4,0},{6,2},{8,4},{10,6},{12,8},{14,10},{5,1},{7,3},{9,5},{11,7},{... | collective-permute-start | bytes 1032200 | tf_op jit(solution)/shard_map/ppermute | solution.py:60
  22.7 6.9 %collective-permute-start.13 = (bf16[336,512]{1,0:T(8,128)(2,1)S(1)}, bf16[336,512]{1,0:T(8,128)(2,1)S(1)}, u32[]{:S(2)}, u32[]{:S(2)}) collective-permute-start(bf16[336,512]{1,0:T(8,128)(2,1)S(1)} %collective-permute-done.11), channel_id=1, source_target_pairs={{4,8},{6,10},{8,12},{10,14},{5,9},{7,11},{9,13},{11,15},{20,24},{2... | collective-permute-start | bytes 1032200 | tf_op jit(solution)/shard_map/ppermute | solution.py:59
  23.4 27.2 %collective-permute-start.17 = (bf16[336,512]{1,0:T(8,128)(2,1)S(1)}, bf16[336,512]{1,0:T(8,128)(2,1)S(1)}, u32[]{:S(2)}, u32[]{:S(2)}) collective-permute-start(bf16[336,512]{1,0:T(8,128)(2,1)S(1)} %collective-permute-done.11), channel_id=1, source_target_pairs={{6,4},{4,6},{10,8},{8,10},{14,12},{12,14},{7,5},{5,7},{11,9},{9,11... | collective-permute-start | bytes 1032200 | tf_op jit(solution)/shard_map/ppermute | solution.py:67
  26.9 13.2 %collective-permute-start.14 = (bf16[336,512]{1,0:T(8,128)(2,1)S(1)}, bf16[336,512]{1,0:T(8,128)(2,1)S(1)}, u32[]{:S(2)}, u32[]{:S(2)}) collective-permute-start(bf16[336,512]{1,0:T(8,128)(2,1)S(1)} %collective-permute-done.12), channel_id=1, source_target_pairs={{4,0},{6,2},{8,4},{10,6},{5,1},{7,3},{9,5},{11,7},{20,16},{22,18},... | collective-permute-start | bytes 1032200 | tf_op jit(solution)/shard_map/ppermute | solution.py:60
  29.7 13.2 %collective-permute-start.15 = (bf16[336,512]{1,0:T(8,128)(2,1)S(1)}, bf16[336,512]{1,0:T(8,128)(2,1)S(1)}, u32[]{:S(2)}, u32[]{:S(2)}) collective-permute-start(bf16[336,512]{1,0:T(8,128)(2,1)S(1)} %collective-permute-done.13), channel_id=1, source_target_pairs={{8,12},{10,14},{9,13},{11,15},{24,28},{26,30},{25,29},{27,31}} | collective-permute-start | bytes 1032200 | tf_op jit(solution)/shard_map/ppermute | solution.py:59
  40.0 9.1 %collective-permute-start.16 = (bf16[336,512]{1,0:T(8,128)(2,1)S(1)}, bf16[336,512]{1,0:T(8,128)(2,1)S(1)}, u32[]{:S(2)}, u32[]{:S(2)}) collective-permute-start(bf16[336,512]{1,0:T(8,128)(2,1)S(1)} %collective-permute-done.14), channel_id=1, source_target_pairs={{4,0},{6,2},{5,1},{7,3},{20,16},{22,18},{21,17},{23,19}} | collective-permute-start | bytes 1032200 | tf_op jit(solution)/shard_map/ppermute | solution.py:60
  42.8 11.0 %collective-permute-start.18 = (bf16[336,512]{1,0:T(8,128)(2,1)S(1)}, bf16[336,512]{1,0:T(8,128)(2,1)S(1)}, u32[]{:S(2)}, u32[]{:S(2)}) collective-permute-start(bf16[336,512]{1,0:T(8,128)(2,1)S(1)} %collective-permute-done.12), channel_id=1, source_target_pairs={{2,0},{0,2},{6,4},{4,6},{10,8},{8,10},{3,1},{1,3},{7,5},{5,7},{11,... | collective-permute-start | bytes 1032200 | tf_op jit(solution)/shard_map/ppermute | solution.py:69
  49.2 6.2 %collective-permute-start.19 = (bf16[336,512]{1,0:T(8,128)(2,1)S(1)}, bf16[336,512]{1,0:T(8,128)(2,1)S(1)}, u32[]{:S(2)}, u32[]{:S(2)}) collective-permute-start(bf16[336,512]{1,0:T(8,128)(2,1)S(1)} %collective-permute-done.13), channel_id=1, source_target_pairs={{10,8},{8,10},{14,12},{12,14},{11,9},{9,11},{15,13},{13,15},{26,24... | collective-permute-start | bytes 1032200 | tf_op jit(solution)/shard_map/ppermute | solution.py:67
  50.6 12.4 %collective-permute-start.20 = (bf16[336,512]{1,0:T(8,128)(2,1)S(1)}, bf16[336,512]{1,0:T(8,128)(2,1)S(1)}, u32[]{:S(2)}, u32[]{:S(2)}) collective-permute-start(bf16[336,512]{1,0:T(8,128)(2,1)S(1)} %collective-permute-done.14), channel_id=1, source_target_pairs={{2,0},{0,2},{6,4},{4,6},{3,1},{1,3},{7,5},{5,7},{18,16},{16,18},{2... | collective-permute-start | bytes 1032200 | tf_op jit(solution)/shard_map/ppermute | solution.py:69
  53.8 10.0 %collective-permute-start.21 = (bf16[336,512]{1,0:T(8,128)(2,1)S(1)}, bf16[336,512]{1,0:T(8,128)(2,1)S(1)}, u32[]{:S(2)}, u32[]{:S(2)}) collective-permute-start(bf16[336,512]{1,0:T(8,128)(2,1)S(1)} %collective-permute-done.15), channel_id=1, source_target_pairs={{14,12},{12,14},{15,13},{13,15},{30,28},{28,30},{31,29},{29,31}} | collective-permute-start | bytes 1032200 | tf_op jit(solution)/shard_map/ppermute | solution.py:67
  55.3 11.4 %collective-permute-start.22 = (bf16[336,512]{1,0:T(8,128)(2,1)S(1)}, bf16[336,512]{1,0:T(8,128)(2,1)S(1)}, u32[]{:S(2)}, u32[]{:S(2)}) collective-permute-start(bf16[336,512]{1,0:T(8,128)(2,1)S(1)} %collective-permute-done.16), channel_id=1, source_target_pairs={{2,0},{0,2},{3,1},{1,3},{18,16},{16,18},{19,17},{17,19}} | collective-permute-start | bytes 1032200 | tf_op jit(solution)/shard_map/ppermute | solution.py:69
  63.0 14.9 %collective-permute-start = (f32[16]{0:T(128)S(1)}, f32[16]{0:T(128)S(1)}, u32[]{:S(2)}, u32[]{:S(2)}) collective-permute-start(f32[16]{0:T(128)S(1)} %pad_maximum_fusion), channel_id=1, source_target_pairs={{0,8},{2,10},{4,12},{6,14},{8,0},{10,2},{12,4},{14,6},{1,9},{3,11}... | collective-permute-start | bytes 200 | tf_op jit(solution)/shard_map/ppermute | solution.py:19
  74.4 18.0 %collective-permute-start.23 = (bf16[2688,512]{1,0:T(8,128)(2,1)S(1)}, bf16[2688,512]{1,0:T(8,128)(2,1)}, u32[]{:S(2)}, u32[]{:S(2)}) collective-permute-start(bf16[2688,512]{1,0:T(8,128)(2,1)S(1)} %get-tuple-element.30), channel_id=1, source_target_pairs={{0,1},{1,0},{2,3},{3,2},{4,5},{5,4},{6,7},{7,6},{8,9},{9,8},{10,11... | collective-permute-start | bytes 8257544 | tf_op jit(solution)/shard_map/ppermute | solution.py:19
  78.0 3.5 %collective-permute-start.1 = (f32[16]{0:T(128)S(1)}, f32[16]{0:T(128)S(1)}, u32[]{:S(2)}, u32[]{:S(2)}) collective-permute-start(f32[16]{0:T(128)S(1)} %fusion.65), channel_id=1, source_target_pairs={{0,4},{2,6},{4,0},{6,2},{8,12},{10,14},{12,8},{14,10},{1,5},{3,7},... | collective-permute-start | bytes 200 | tf_op jit(solution)/shard_map/ppermute | solution.py:19
  81.5 3.5 %collective-permute-start.2 = (f32[16]{0:T(128)S(1)}, f32[16]{0:T(128)S(1)}, u32[]{:S(2)}, u32[]{:S(2)}) collective-permute-start(f32[16]{0:T(128)S(1)} %add.231), channel_id=1, source_target_pairs={{0,2},{2,0},{4,6},{6,4},{8,10},{10,8},{12,14},{14,12},{1,3},{3,1},... | collective-permute-start | bytes 200 | tf_op jit(solution)/shard_map/ppermute | solution.py:19
  86.4 3.9 %collective-permute-start.5 = (bf16[128,1024]{1,0:T(8,128)(2,1)S(1)}, bf16[128,1024]{1,0:T(8,128)(2,1)S(1)}, u32[]{:S(2)}, u32[]{:S(2)}) collective-permute-start(bf16[128,1024]{1,0:T(8,128)(2,1)S(1)} %collective-permute-done.4), channel_id=1, source_target_pairs={{8,12},{10,14},{9,13},{11,15},{24,28},{26,30},{25,29},{27,31}} | collective-permute-start | bytes 786440 | tf_op jit(solution)/shard_map/ppermute | solution.py:40
  88.9 3.3 %collective-permute-start.7 = (bf16[128,1024]{1,0:T(8,128)(2,1)}, bf16[128,1024]{1,0:T(8,128)(2,1)S(1)}, u32[]{:S(2)}, u32[]{:S(2)}) collective-permute-start(bf16[128,1024]{1,0:T(8,128)(2,1)} %collective-permute-done.3), channel_id=1, source_target_pairs={{6,4},{4,6},{10,8},{8,10},{14,12},{12,14},{7,5},{5,7},{11,9},{9,11... | collective-permute-start | bytes 786440 | tf_op jit(solution)/shard_map/ppermute | solution.py:45
  89.6 2.6 %collective-permute-start.8 = (bf16[128,1024]{1,0:T(8,128)(2,1)S(1)}, bf16[128,1024]{1,0:T(8,128)(2,1)S(1)}, u32[]{:S(2)}, u32[]{:S(2)}) collective-permute-start(bf16[128,1024]{1,0:T(8,128)(2,1)S(1)} %collective-permute-done.4), channel_id=1, source_target_pairs={{10,8},{8,10},{14,12},{12,14},{11,9},{9,11},{15,13},{13,15},{26,24... | collective-permute-start | bytes 786440 | tf_op jit(solution)/shard_map/ppermute | solution.py:45
  90.4 2.0 collective-permute-start.9
  117.4 19.2 %collective-permute-start.28 = (bf16[128,1024]{0,1:T(8,128)(2,1)S(1)}, bf16[128,1024]{0,1:T(8,128)(2,1)S(1)}, u32[]{:S(2)}, u32[]{:S(2)}) collective-permute-start(bf16[128,1024]{0,1:T(8,128)(2,1)S(1)} %bitcast.150), channel_id=1, source_target_pairs={{12,14},{14,12},{13,15},{15,13},{28,30},{30,28},{29,31},{31,29}} | collective-permute-start | bytes 786440 | tf_op jit(solution)/shard_map/ppermute | solution.py:102
  118.2 22.2 %collective-permute-start.32 = (bf16[128,1024]{0,1:T(8,128)(2,1)S(1)}, bf16[128,1024]{0,1:T(8,128)(2,1)S(1)}, u32[]{:S(2)}, u32[]{:S(2)}) collective-permute-start(bf16[128,1024]{0,1:T(8,128)(2,1)S(1)} %copy-done.6), channel_id=1, source_target_pairs={{0,4},{2,6},{4,8},{6,10},{8,12},{10,14},{1,5},{3,7},{5,9},{7,11},{... | collective-permute-start | bytes 786440 | tf_op jit(solution)/shard_map/ppermute | solution.py:40
  135.9 5.2 %collective-permute-start.27 = (bf16[128,1024]{0,1:T(8,128)(2,1)S(1)}, bf16[128,1024]{0,1:T(8,128)(2,1)S(1)}, u32[]{:S(2)}, u32[]{:S(2)}) collective-permute-start(bf16[128,1024]{0,1:T(8,128)(2,1)S(1)} %bitcast.149), channel_id=1, source_target_pairs={{8,10},{10,8},{12,14},{14,12},{9,11},{11,9},{13,15},{15,13},{24,26... | collective-permute-start | bytes 786440 | tf_op jit(solution)/shard_map/ppermute | solution.py:102
  136.7 4.4 %collective-permute-start.29 = (bf16[128,1024]{0,1:T(8,128)(2,1)S(1)}, bf16[128,1024]{0,1:T(8,128)(2,1)S(1)}, u32[]{:S(2)}, u32[]{:S(2)}) collective-permute-start(bf16[128,1024]{0,1:T(8,128)(2,1)S(1)} %fusion.22), channel_id=1, source_target_pairs={{12,8},{14,10},{13,9},{15,11},{28,24},{30,26},{29,25},{31,27}} | collective-permute-start | bytes 786440 | tf_op jit(solution)/shard_map/ppermute | solution.py:110
  137.4 9.8 %collective-permute-start.26 = (bf16[128,1024]{0,1:T(8,128)(2,1)S(1)}, bf16[128,1024]{0,1:T(8,128)(2,1)S(1)}, u32[]{:S(2)}, u32[]{:S(2)}) collective-permute-start(bf16[128,1024]{0,1:T(8,128)(2,1)S(1)} %bitcast.148), channel_id=1, source_target_pairs={{4,6},{6,4},{8,10},{10,8},{12,14},{14,12},{5,7},{7,5},{9,11},{11,9... | collective-permute-start | bytes 786440 | tf_op jit(solution)/shard_map/ppermute | solution.py:102
  140.5 5.9 %collective-permute-start.33 = (bf16[128,1024]{0,1:T(8,128)(2,1)S(1)}, bf16[128,1024]{0,1:T(8,128)(2,1)S(1)}, u32[]{:S(2)}, u32[]{:S(2)}) collective-permute-start(bf16[128,1024]{0,1:T(8,128)(2,1)S(1)} %collective-permute-done.32), channel_id=1, source_target_pairs={{4,8},{6,10},{8,12},{10,14},{5,9},{7,11},{9,13},{11,15},{20,24},{2... | collective-permute-start | bytes 786440 | tf_op jit(solution)/shard_map/ppermute | solution.py:40
  141.3 6.6 %collective-permute-start.30 = (bf16[128,1024]{0,1:T(8,128)(2,1)S(1)}, bf16[128,1024]{0,1:T(8,128)(2,1)S(1)}, u32[]{:S(2)}, u32[]{:S(2)}) collective-permute-start(bf16[128,1024]{0,1:T(8,128)(2,1)S(1)} %fusion.24), channel_id=1, source_target_pairs={{8,4},{10,6},{12,8},{14,10},{9,5},{11,7},{13,9},{15,11},{24,20},{2... | collective-permute-start | bytes 786440 | tf_op jit(solution)/shard_map/ppermute | solution.py:110
  142.0 8.1 %collective-permute-start.35 = (bf16[128,1024]{0,1:T(8,128)(2,1)S(1)}, bf16[128,1024]{0,1:T(8,128)(2,1)S(1)}, u32[]{:S(2)}, u32[]{:S(2)}) collective-permute-start(bf16[128,1024]{0,1:T(8,128)(2,1)S(1)} %copy-done.6), channel_id=1, source_target_pairs={{0,2},{4,6},{8,10},{12,14},{1,3},{5,7},{9,11},{13,15},{16,18},{20,... | collective-permute-start | bytes 786440 | tf_op jit(solution)/shard_map/ppermute | solution.py:42
  144.9 14.8 %collective-permute-start.25 = (bf16[128,1024]{0,1:T(8,128)(2,1)S(1)}, bf16[128,1024]{0,1:T(8,128)(2,1)S(1)}, u32[]{:S(2)}, u32[]{:S(2)}) collective-permute-start(bf16[128,1024]{0,1:T(8,128)(2,1)S(1)} %bitcast.147), channel_id=1, source_target_pairs={{2,0},{6,4},{10,8},{14,12},{3,1},{7,5},{11,9},{15,13},{18,16},{22,... | collective-permute-start | bytes 786440 | tf_op jit(solution)/shard_map/ppermute | solution.py:99
  146.4 2.3 collective-permute-start.34
  147.2 3.9 %collective-permute-start.36 = (bf16[128,1024]{0,1:T(8,128)(2,1)S(1)}, bf16[128,1024]{0,1:T(8,128)(2,1)S(1)}, u32[]{:S(2)}, u32[]{:S(2)}) collective-permute-start(bf16[128,1024]{0,1:T(8,128)(2,1)S(1)} %collective-permute-done.32), channel_id=1, source_target_pairs={{6,4},{4,6},{10,8},{8,10},{14,12},{12,14},{7,5},{5,7},{11,9},{9,11... | collective-permute-start | bytes 786440 | tf_op jit(solution)/shard_map/ppermute | solution.py:45
  147.9 3.3 %collective-permute-start.37 = (bf16[128,1024]{0,1:T(8,128)(2,1)S(1)}, bf16[128,1024]{0,1:T(8,128)(2,1)S(1)}, u32[]{:S(2)}, u32[]{:S(2)}) collective-permute-start(bf16[128,1024]{0,1:T(8,128)(2,1)S(1)} %collective-permute-done.33), channel_id=1, source_target_pairs={{10,8},{8,10},{14,12},{12,14},{11,9},{9,11},{15,13},{13,15},{26,24... | collective-permute-start | bytes 786440 | tf_op jit(solution)/shard_map/ppermute | solution.py:45
  148.7 31.6 %collective-permute-start.31 = (bf16[128,1024]{0,1:T(8,128)(2,1)S(1)}, bf16[128,1024]{0,1:T(8,128)(2,1)S(1)}, u32[]{:S(2)}, u32[]{:S(2)}) collective-permute-start(bf16[128,1024]{0,1:T(8,128)(2,1)S(1)} %fusion.26), channel_id=1, source_target_pairs={{4,0},{6,2},{8,4},{10,6},{12,8},{14,10},{5,1},{7,3},{9,5},{11,7},{... | collective-permute-start | bytes 786440 | tf_op jit(solution)/shard_map/ppermute | solution.py:110
  150.1 1.2 collective-permute-start.38
  183.9 24.3 %collective-permute-start.42 = (bf16[128,1024]{1,0:T(8,128)(2,1)}, bf16[128,1024]{1,0:T(8,128)(2,1)}, u32[]{:S(2)}, u32[]{:S(2)}) collective-permute-start(bf16[128,1024]{1,0:T(8,128)(2,1)} %copy.73), channel_id=1, source_target_pairs={{12,14},{14,12},{13,15},{15,13},{28,30},{30,28},{29,31},{31,29}} | collective-permute-start | bytes 786440 | tf_op jit(solution)/shard_map/ppermute | solution.py:102
  186.1 45.2 %collective-permute-start.41 = (bf16[128,1024]{1,0:T(8,128)(2,1)}, bf16[128,1024]{1,0:T(8,128)(2,1)}, u32[]{:S(2)}, u32[]{:S(2)}) collective-permute-start(bf16[128,1024]{1,0:T(8,128)(2,1)} %copy.71), channel_id=1, source_target_pairs={{8,10},{10,8},{12,14},{14,12},{9,11},{11,9},{13,15},{15,13},{24,26... | collective-permute-start | bytes 786440 | tf_op jit(solution)/shard_map/ppermute | solution.py:102
  189.2 31.2 %collective-permute-start.46 = (f32[464,128]{1,0:T(8,128)}, f32[464,128]{1,0:T(8,128)}, u32[]{:S(2)}, u32[]{:S(2)}) collective-permute-start(f32[464,128]{1,0:T(8,128)} %maximum_bitcast_fusion), channel_id=1, source_target_pairs={{0,8},{2,10},{4,12},{6,14},{8,0},{10,2},{12,4},{14,6},{1,9},{3,11}... | collective-permute-start | bytes 712712 | tf_op jit(solution)/shard_map/ppermute | solution.py:19
  210.1 21.2 %collective-permute-start.43 = (bf16[128,1024]{1,0:T(8,128)(2,1)}, bf16[128,1024]{1,0:T(8,128)(2,1)}, u32[]{:S(2)}, u32[]{:S(2)}) collective-permute-start(bf16[128,1024]{1,0:T(8,128)(2,1)} %add_convert_fusion.3), channel_id=1, source_target_pairs={{12,8},{14,10},{13,9},{15,11},{28,24},{30,26},{29,25},{31,27}} | collective-permute-start | bytes 786440 | tf_op jit(solution)/shard_map/ppermute | solution.py:110
  216.9 26.4 %collective-permute-start.40 = (bf16[128,1024]{1,0:T(8,128)(2,1)}, bf16[128,1024]{1,0:T(8,128)(2,1)}, u32[]{:S(2)}, u32[]{:S(2)}) collective-permute-start(bf16[128,1024]{1,0:T(8,128)(2,1)} %copy.69), channel_id=1, source_target_pairs={{4,6},{6,4},{8,10},{10,8},{12,14},{14,12},{5,7},{7,5},{9,11},{11,9... | collective-permute-start | bytes 786440 | tf_op jit(solution)/shard_map/ppermute | solution.py:102
  219.2 34.8 %collective-permute-start.39 = (bf16[128,1024]{1,0:T(8,128)(2,1)}, bf16[128,1024]{1,0:T(8,128)(2,1)S(1)}, u32[]{:S(2)}, u32[]{:S(2)}) collective-permute-start(bf16[128,1024]{1,0:T(8,128)(2,1)} %copy.68), channel_id=1, source_target_pairs={{2,0},{6,4},{10,8},{14,12},{3,1},{7,5},{11,9},{15,13},{18,16},{22,... | collective-permute-start | bytes 786440 | tf_op jit(solution)/shard_map/ppermute | solution.py:99
  221.4 14.0 %collective-permute-start.47 = (f32[464,128]{1,0:T(8,128)S(1)}, f32[464,128]{1,0:T(8,128)S(1)}, u32[]{:S(2)}, u32[]{:S(2)}) collective-permute-start(f32[464,128]{1,0:T(8,128)S(1)} %fusion.34), channel_id=1, source_target_pairs={{0,4},{2,6},{4,0},{6,2},{8,12},{10,14},{12,8},{14,10},{1,5},{3,7},... | collective-permute-start | bytes 712712 | tf_op jit(solution)/shard_map/ppermute | solution.py:19
  232.5 10.9 %collective-permute-start.44 = (bf16[128,1024]{1,0:T(8,128)(2,1)S(1)}, bf16[128,1024]{1,0:T(8,128)(2,1)S(1)}, u32[]{:S(2)}, u32[]{:S(2)}) collective-permute-start(bf16[128,1024]{1,0:T(8,128)(2,1)S(1)} %add_convert_fusion.2), channel_id=1, source_target_pairs={{8,4},{10,6},{12,8},{14,10},{9,5},{11,7},{13,9},{15,11},{24,20},{2... | collective-permute-start | bytes 786440 | tf_op jit(solution)/shard_map/ppermute | solution.py:110
  236.4 6.8 %collective-permute-start.48 = (f32[464,128]{1,0:T(8,128)S(1)}, f32[464,128]{1,0:T(8,128)S(1)}, u32[]{:S(2)}, u32[]{:S(2)}) collective-permute-start(f32[464,128]{1,0:T(8,128)S(1)} %fusion.64), channel_id=1, source_target_pairs={{0,2},{2,0},{4,6},{6,4},{8,10},{10,8},{12,14},{14,12},{1,3},{3,1},... | collective-permute-start | bytes 712712 | tf_op jit(solution)/shard_map/ppermute | solution.py:19
  243.3 8.5 %collective-permute-start.49 = (f32[464,128]{1,0:T(8,128)S(1)}, f32[464,128]{1,0:T(8,128)S(1)}, u32[]{:S(2)}, u32[]{:S(2)}) collective-permute-start(f32[464,128]{1,0:T(8,128)S(1)} %add.274), channel_id=1, source_target_pairs={{0,1},{1,0},{2,3},{3,2},{4,5},{5,4},{6,7},{7,6},{8,9},{9,8},{10,11... | collective-permute-start | bytes 712712 | tf_op jit(solution)/shard_map/ppermute | solution.py:19
  245.1 11.2 %collective-permute-start.45 = (bf16[128,1024]{1,0:T(8,128)(2,1)}, bf16[128,1024]{1,0:T(8,128)(2,1)}, u32[]{:S(2)}, u32[]{:S(2)}) collective-permute-start(bf16[128,1024]{1,0:T(8,128)(2,1)} %add_convert_fusion.1), channel_id=1, source_target_pairs={{4,0},{6,2},{8,4},{10,6},{12,8},{14,10},{5,1},{7,3},{9,5},{11,7},{... | collective-permute-start | bytes 786440 | tf_op jit(solution)/shard_map/ppermute | solution.py:110
  (23 other events, 287.0 us)

commit v18 on v17

--- a/solution.py
+++ b/solution.py
@@ -34,12 +34,12 @@
 
 def tree_spread(block, levels):
     count = 2 * levels
+    crossed = [lax.ppermute(block, "ctx", [(c - 1, c) for c in range(1, count, 2)])]
     climbed = []
     held = block
     for step in range(1, levels):
         held = lax.ppermute(held, "ctx", [(c - 2, c) for c in range(2 * step, count)])
         climbed.append(held)
-    crossed = [lax.ppermute(block, "ctx", [(c - 1, c) for c in range(1, count, 2)])]
     for step in range(1, levels):
         crossed.append(
             lax.ppermute(climbed[step - 1], "ctx", [(c ^ 1, c) for c in range(2 * step, count)])

time: 260 us -> 260 us (level)
  no operation moved by 1% of the time
where the time goes in v18:
time: 260 us; the launch traced here: 258 us
  starting transfers between devices  102 us (39%)
  waiting for transfers between devices  61.9 us (24%)
  local copies, waits for them, and re-layouts  47.5 us (18%)
  matrix products  29.5 us (11%)
  other arithmetic  14.8 us (6%)
    ppermute x9, starting transfers between devices, from_partner(): lax.ppermute(shard, axis, [(i, i ^ 1 << stride) for i in range(lax.axis_s...  31.7 us
    ppermute x6, starting transfers between devices, tree_spread(): lax.ppermute(held, 'ctx', [(c - 2, c) for c in range(2 * step, count)])  26.3 us
    ppermute x6, waiting for transfers between devices, tree_return(): lax.ppermute(acc.astype(jnp.bfloat16), 'ctx', [(c, c - 2) for c in range(...  23 us
    ppermute x3, waiting for transfers between devices, tree_gather(): lax.ppermute(down, 'ctx', [(c + 2, c) for c in range(0, count - 2 * step)])  14.8 us
    ppermute x9, waiting for transfers between devices, from_partner(): lax.ppermute(shard, axis, [(i, i ^ 1 << stride) for i in range(lax.axis_s...  12.2 us
    dynamic_update_slice x14, local copies, waits for them, and re-layouts, tree_gather(): whole = lax.dynamic_update_slice_in_dim(whole, piece, place, 0)  10.7 us
    ppermute x3, starting transfers between devices, tree_gather(): lax.ppermute(downs[step - 1], 'ctx', [(c ^ 1, c) for c in range(0, count...  8.24 us
    unnamed x60, local copies, waits for them, and re-layouts  6.94 us
  transfers between devices with their start and end apart: 50, of which 14 were waited for; matrix products, arithmetic and copies ran while one was open for 24% of the time, Pallas kernels for 0%

profile of v18, /device:TPU:0, one launch (start us, length us, event | category | flops | bytes accessed | tf_op | source)
XLA Modules:
  0.0 258.1 jit_solution(1169830148806569385)
XLA Ops:
  0.7 5.8 %collective-permute-start.3 = (bf16[128,1024]{1,0:T(8,128)(2,1)}, bf16[128,1024]{1,0:T(8,128)(2,1)}, u32[]{:S(2)}, u32[]{:S(2)}) collective-permute-start(bf16[128,1024]{1,0:T(8,128)(2,1)} %bitcast.151), channel_id=1, source_target_pairs={{0,4},{2,6},{4,8},{6,10},{8,12},{10,14},{1,5},{3,7},{5,9},{7,11},{... | collective-permute-start | bytes 786440 | tf_op jit(solution)/shard_map/ppermute | solution.py:41
  6.5 4.1 %collective-permute-start.6 = (bf16[128,1024]{1,0:T(8,128)(2,1)}, bf16[128,1024]{1,0:T(8,128)(2,1)}, u32[]{:S(2)}, u32[]{:S(2)}) collective-permute-start(bf16[128,1024]{1,0:T(8,128)(2,1)} %bitcast.152), channel_id=1, source_target_pairs={{0,2},{4,6},{8,10},{12,14},{1,3},{5,7},{9,11},{13,15},{16,18},{20,... | collective-permute-start | bytes 786440 | tf_op jit(solution)/shard_map/ppermute | solution.py:37
  10.6 1.8 broadcast_in_dim.58
  13.2 2.8 %collective-permute-start.11 = (bf16[336,512]{1,0:T(8,128)(2,1)S(1)}, bf16[336,512]{1,0:T(8,128)(2,1)S(1)}, u32[]{:S(2)}, u32[]{:S(2)}) collective-permute-start(bf16[336,512]{1,0:T(8,128)(2,1)S(1)} %get-tuple-element.29), channel_id=1, source_target_pairs={{0,4},{2,6},{4,8},{6,10},{8,12},{10,14},{1,5},{3,7},{5,9},{7,11},{... | collective-permute-start | bytes 1032200 | tf_op jit(solution)/shard_map/ppermute | solution.py:59
  16.0 1.3 collective-permute-start.12
  18.9 3.8 %collective-permute-done.11 = bf16[336,512]{1,0:T(8,128)(2,1)S(1)} collective-permute-done((bf16[336,512]{1,0:T(8,128)(2,1)S(1)}, bf16[336,512]{1,0:T(8,128)(2,1)S(1)}, u32[]{:S(2)}, u32[]{:S(2)}) %collective-permute-start.11) | collective-permute-done | bytes 344096 | tf_op jit(solution)/shard_map/ppermute | solution.py:59
  24.1 2.7 %collective-permute-done.12 = bf16[336,512]{1,0:T(8,128)(2,1)S(1)} collective-permute-done((bf16[336,512]{1,0:T(8,128)(2,1)S(1)}, bf16[336,512]{1,0:T(8,128)(2,1)S(1)}, u32[]{:S(2)}, u32[]{:S(2)}) %collective-permute-start.12) | collective-permute-done | bytes 344096 | tf_op jit(solution)/shard_map/ppermute | solution.py:60
  31.1 8.9 %collective-permute-done.14 = bf16[336,512]{1,0:T(8,128)(2,1)S(1)} collective-permute-done((bf16[336,512]{1,0:T(8,128)(2,1)S(1)}, bf16[336,512]{1,0:T(8,128)(2,1)S(1)}, u32[]{:S(2)}, u32[]{:S(2)}) %collective-permute-start.14) | collective-permute-done | bytes 344096 | tf_op jit(solution)/shard_map/ppermute | solution.py:60
  42.8 2.5 collective-permute-start.18
  46.1 3.1 %collective-permute-done.16 = bf16[336,512]{1,0:T(8,128)(2,1)S(1)} collective-permute-done((bf16[336,512]{1,0:T(8,128)(2,1)S(1)}, bf16[336,512]{1,0:T(8,128)(2,1)S(1)}, u32[]{:S(2)}, u32[]{:S(2)}) %collective-permute-start.16) | collective-permute-done | bytes 344096 | tf_op jit(solution)/shard_map/ppermute | solution.py:60
  50.6 2.4 collective-permute-start.20
  55.3 3.4 %collective-permute-start.22 = (bf16[336,512]{1,0:T(8,128)(2,1)S(1)}, bf16[336,512]{1,0:T(8,128)(2,1)S(1)}, u32[]{:S(2)}, u32[]{:S(2)}) collective-permute-start(bf16[336,512]{1,0:T(8,128)(2,1)S(1)} %collective-permute-done.16), channel_id=1, source_target_pairs={{2,0},{0,2},{3,1},{1,3},{18,16},{16,18},{19,17},{17,19}} | collective-permute-start | bytes 1032200 | tf_op jit(solution)/shard_map/ppermute | solution.py:69
  59.4 3.6 %collective-permute-done.20 = bf16[336,512]{1,0:T(8,128)(2,1)S(1)} collective-permute-done((bf16[336,512]{1,0:T(8,128)(2,1)S(1)}, bf16[336,512]{1,0:T(8,128)(2,1)S(1)}, u32[]{:S(2)}, u32[]{:S(2)}) %collective-permute-start.20) | collective-permute-done | bytes 344096 | tf_op jit(solution)/shard_map/ppermute | solution.py:69
  64.5 2.2 collective-permute-done.22
  67.5 3.2 %broadcast_in_dim.57 = bf16[2688,1024]{1,0:T(8,128)(2,1)} broadcast(bf16[]{:T(256)} %constant.74.clone.1), dimensions={} | broadcast | bytes 5505026 | tf_op jit(solution)/shard_map/broadcast_in_dim | solution.py:153
  70.6 3.8 %fusion.35 = (bf16[2688,512]{1,0:T(8,128)(2,1)S(1)}, bf16[2688,1024]{1,0:T(8,128)(2,1)}) fusion(bf16[3024,512]{1,0:T(8,128)(2,1)} %constant_dynamic-update-slice_fusion.26, bf16[2688,1024]{1,0:T(8,128)(2,1)} %broadcast_in_dim.57, s32[]{:T(128)S(6)} %select_n.156), kind=kLoop, calls=%fused_computation.123 | loop fusion | bytes 8257540 | tf_op jit(solution)/shard_map/slice | solution.py:78
  75.8 2.0 copy.94
  78.0 3.5 %collective-permute-done.1 = f32[16]{0:T(128)S(1)} collective-permute-done((f32[16]{0:T(128)S(1)}, f32[16]{0:T(128)S(1)}, u32[]{:S(2)}, u32[]{:S(2)}) %collective-permute-start.1) | collective-permute-done | bytes 96 | tf_op jit(solution)/shard_map/ppermute | solution.py:19
  82.5 2.5 collective-permute-done.2
  92.4 3.6 %constant_dynamic-update-slice_fusion.24 = bf16[2688,1024]{1,0:T(8,128)(2,1)} fusion(bf16[2688,1024]{1,0:T(8,128)(2,1)} %get-tuple-element.31, bf16[2688,512]{1,0:T(8,128)(2,1)} %collective-permute-done.23, s32[]{:T(128)S(6)} %select_n.185), kind=kLoop, calls=%fused_computation.84 | loop fusion | bytes 5505028 | tf_op jit(solution)/shard_map/dynamic_update_slice | solution.py:155
  96.0 4.9 %fusion.15 = bf16[128,1024]{0,1:T(8,128)(2,1)} fusion(f32[128,1024]{0,1:T(8,128)S(1)} %copy-done.2, bf16[2688,1024]{1,0:T(8,128)(2,1)} %constant_dynamic-update-slice_fusion.24, bf16[1,128,2688]{2,1,0:T(8,128)(2,1)S(1)} %copy-done), kind=kOutput, calls=%fused_computation.28 | convolution fusion | flops 704905216 | bytes 6979584 | tf_op jit(solution)/shard_map/dot_general | solution.py:164
  100.9 2.0 copy.95
  102.9 3.3 %copy.84 = bf16[1024,8,128,1]{0,2,3,1:T(8,128)(2,1)S(1)} copy(bf16[1024,8,128,1]{2,1,0,3:T(8,128)(2,1)} %bitcast.134) | data formatting | bytes 4194304 | tf_op jit(solution)/shard_map/reshape | solution.py:219
  106.2 5.7 %fusion.39 = (f32[8,2,128]{2,1,0:T(2,128)S(1)}, f32[8,2,128,1024]{2,3,1,0:T(8,128)}) fusion(pred[128,1024]{0,1:T(8,128)(4,1)S(1)} %copy-done.17, bf16[1024,8,128,1]{0,2,3,1:T(8,128)(2,1)S(1)} %copy.84, bf16[128,8,2,128]{0,3,2,1:T(8,128)(2,1)S(1)} %bitcast.138), kind=kOutput, calls=%fused_computation.127 | convolution fusion | flops 547357696 | bytes 11149312 | tf_op jit(solution)/shard_map/sub | solution.py:226
  111.9 5.0 %fusion.40 = (bf16[1024,8,128]{0,2,1:T(8,128)(2,1)S(1)}, f32[1024,8,128]{0,2,1:T(8,128)S(1)}) fusion(bf16[128,8,2,128]{3,2,1,0:T(2,128)(2,1)} %reshape_squeeze.7, f32[128]{0:T(128)S(1)} %get-tuple-element.25, f32[8,2,128,1024]{2,3,1,0:T(8,128)} %get-tuple-element.51, f32[8,2,128]{2,1,0:T(2,128)S(1)} %get-tuple-element.50), kind=kOutput, calls=%fused_computation.128 | convolution fusion | flops 544210944 | bytes 15213056 | tf_op jit(solution)/shard_map/jgtl,tjgd->ljd/dot_general | solution.py:240
  118.2 17.7 %collective-permute-start.32 = (bf16[128,1024]{0,1:T(8,128)(2,1)S(1)}, bf16[128,1024]{0,1:T(8,128)(2,1)S(1)}, u32[]{:S(2)}, u32[]{:S(2)}) collective-permute-start(bf16[128,1024]{0,1:T(8,128)(2,1)S(1)} %copy-done.6), channel_id=1, source_target_pairs={{0,4},{2,6},{4,8},{6,10},{8,12},{10,14},{1,5},{3,7},{5,9},{7,11},{... | collective-permute-start | bytes 786440 | tf_op jit(solution)/shard_map/ppermute | solution.py:41
  138.1 2.4 collective-permute-done.32
  142.0 2.8 %collective-permute-start.35 = (bf16[128,1024]{0,1:T(8,128)(2,1)S(1)}, bf16[128,1024]{0,1:T(8,128)(2,1)S(1)}, u32[]{:S(2)}, u32[]{:S(2)}) collective-permute-start(bf16[128,1024]{0,1:T(8,128)(2,1)S(1)} %copy-done.6), channel_id=1, source_target_pairs={{0,2},{4,6},{8,10},{12,14},{1,3},{5,7},{9,11},{13,15},{16,18},{20,... | collective-permute-start | bytes 786440 | tf_op jit(solution)/shard_map/ppermute | solution.py:37
  144.9 1.4 collective-permute-start.25
  151.5 1.9 fusion.1
  153.5 1.7 fusion.3
  156.2 3.5 %fusion.41 = (bf16[1024,8,128]{0,2,1:T(8,128)(2,1)S(1)}, f32[1024,8,128]{0,2,1:T(8,128)}) fusion(bf16[8,2,128,1024]{2,3,1,0:T(8,128)(2,1)S(1)} %fusion.3, bf16[128,8,2,128]{0,3,2,1:T(8,128)(2,1)S(1)} %bitcast.139), kind=kOutput, calls=%fused_computation.129 | convolution fusion | flops 537919488 | bytes 11010048 | tf_op jit(solution)/shard_map/jgtl,tjgd->ljd/dot_general | solution.py:236
  159.7 20.6 %collective-permute-done.31 = bf16[128,1024]{0,1:T(8,128)(2,1)S(1)} collective-permute-done((bf16[128,1024]{0,1:T(8,128)(2,1)S(1)}, bf16[128,1024]{0,1:T(8,128)(2,1)S(1)}, u32[]{:S(2)}, u32[]{:S(2)}) %collective-permute-start.31) | collective-permute-done | bytes 262176 | tf_op jit(solution)/shard_map/ppermute | solution.py:110
  183.9 1.4 collective-permute-start.42
  186.1 1.4 collective-permute-start.41
  189.2 18.0 %collective-permute-start.46 = (f32[464,128]{1,0:T(8,128)}, f32[464,128]{1,0:T(8,128)}, u32[]{:S(2)}, u32[]{:S(2)}) collective-permute-start(f32[464,128]{1,0:T(8,128)} %maximum_bitcast_fusion), channel_id=1, source_target_pairs={{0,8},{2,10},{4,12},{6,14},{8,0},{10,2},{12,4},{14,6},{1,9},{3,11}... | collective-permute-start | bytes 712712 | tf_op jit(solution)/shard_map/ppermute | solution.py:19
  208.2 1.9 add_convert_fusion.3
  210.1 1.4 collective-permute-start.43
  215.1 1.8 copy.69
  216.9 1.4 collective-permute-start.40
  221.4 9.9 %collective-permute-start.47 = (f32[464,128]{1,0:T(8,128)S(1)}, f32[464,128]{1,0:T(8,128)S(1)}, u32[]{:S(2)}, u32[]{:S(2)}) collective-permute-start(f32[464,128]{1,0:T(8,128)S(1)} %fusion.34), channel_id=1, source_target_pairs={{0,4},{2,6},{4,0},{6,2},{8,12},{10,14},{12,8},{14,10},{1,5},{3,7},... | collective-permute-start | bytes 712712 | tf_op jit(solution)/shard_map/ppermute | solution.py:19
  233.2 2.3 collective-permute-done.47
  236.4 2.7 %collective-permute-start.48 = (f32[464,128]{1,0:T(8,128)S(1)}, f32[464,128]{1,0:T(8,128)S(1)}, u32[]{:S(2)}, u32[]{:S(2)}) collective-permute-start(f32[464,128]{1,0:T(8,128)S(1)} %fusion.64), channel_id=1, source_target_pairs={{0,2},{2,0},{4,6},{6,4},{8,10},{10,8},{12,14},{14,12},{1,3},{3,1},... | collective-permute-start | bytes 712712 | tf_op jit(solution)/shard_map/ppermute | solution.py:19
  239.5 3.7 %collective-permute-done.48 = f32[464,128]{1,0:T(8,128)S(1)} collective-permute-done((f32[464,128]{1,0:T(8,128)S(1)}, f32[464,128]{1,0:T(8,128)S(1)}, u32[]{:S(2)}, u32[]{:S(2)}) %collective-permute-start.48) | collective-permute-done | bytes 237600 | tf_op jit(solution)/shard_map/ppermute | solution.py:19
  243.4 1.8 add_convert_fusion.1
  246.4 5.4 %fusion.11 = bf16[1,128,2688]{2,1,0:T(8,128)(2,1)} fusion(f32[128,2688]{1,0:T(8,128)S(1)} %convolution_multiply_fusion, bf16[128,1024]{0,1:T(8,128)(2,1)S(1)} %fusion.27, bf16[2688,1024]{1,0:T(8,128)(2,1)} %constant_dynamic-update-slice_fusion.24), kind=kOutput, calls=%fused_computation.19 | convolution fusion | flops 705331200 | bytes 7831552 | tf_op jit(solution)/shard_map/tk,dk->td/dot_general | solution.py:265
  253.9 2.3 collective-permute-done.45
  256.3 1.8 fusion.31
  (205 shorter events, 59.4 us)
Async XLA Ops:
  0.7 84.6 %collective-permute-start.3 = (bf16[128,1024]{1,0:T(8,128)(2,1)}, bf16[128,1024]{1,0:T(8,128)(2,1)}, u32[]{:S(2)}, u32[]{:S(2)}) collective-permute-start(bf16[128,1024]{1,0:T(8,128)(2,1)} %bitcast.151), channel_id=1, source_target_pairs={{0,4},{2,6},{4,8},{6,10},{8,12},{10,14},{1,5},{3,7},{5,9},{7,11},{... | collective-permute-start | bytes 786440 | tf_op jit(solution)/shard_map/ppermute | solution.py:41
  6.5 84.8 %collective-permute-start.6 = (bf16[128,1024]{1,0:T(8,128)(2,1)}, bf16[128,1024]{1,0:T(8,128)(2,1)}, u32[]{:S(2)}, u32[]{:S(2)}) collective-permute-start(bf16[128,1024]{1,0:T(8,128)(2,1)} %bitcast.152), channel_id=1, source_target_pairs={{0,2},{4,6},{8,10},{12,14},{1,3},{5,7},{9,11},{13,15},{16,18},{20,... | collective-permute-start | bytes 786440 | tf_op jit(solution)/shard_map/ppermute | solution.py:37
  13.2 10.2 %collective-permute-start.10 = (bf16[336,512]{1,0:T(8,128)(2,1)S(1)}, bf16[336,512]{1,0:T(8,128)(2,1)S(1)}, u32[]{:S(2)}, u32[]{:S(2)}) collective-permute-start(bf16[336,512]{1,0:T(8,128)(2,1)S(1)} %get-tuple-element.29), channel_id=1, source_target_pairs={{2,0},{0,2},{6,4},{4,6},{10,8},{8,10},{14,12},{12,14},{3,1},{1,3},... | collective-permute-start | bytes 1032200 | tf_op jit(solution)/shard_map/ppermute | solution.py:53
  13.2 9.5 %collective-permute-start.11 = (bf16[336,512]{1,0:T(8,128)(2,1)S(1)}, bf16[336,512]{1,0:T(8,128)(2,1)S(1)}, u32[]{:S(2)}, u32[]{:S(2)}) collective-permute-start(bf16[336,512]{1,0:T(8,128)(2,1)S(1)} %get-tuple-element.29), channel_id=1, source_target_pairs={{0,4},{2,6},{4,8},{6,10},{8,12},{10,14},{1,5},{3,7},{5,9},{7,11},{... | collective-permute-start | bytes 1032200 | tf_op jit(solution)/shard_map/ppermute | solution.py:59
  16.0 10.9 %collective-permute-start.12 = (bf16[336,512]{1,0:T(8,128)(2,1)S(1)}, bf16[336,512]{1,0:T(8,128)(2,1)S(1)}, u32[]{:S(2)}, u32[]{:S(2)}) collective-permute-start(bf16[336,512]{1,0:T(8,128)(2,1)S(1)} %get-tuple-element.29), channel_id=1, source_target_pairs={{4,0},{6,2},{8,4},{10,6},{12,8},{14,10},{5,1},{7,3},{9,5},{11,7},{... | collective-permute-start | bytes 1032200 | tf_op jit(solution)/shard_map/ppermute | solution.py:60
  22.7 6.9 %collective-permute-start.13 = (bf16[336,512]{1,0:T(8,128)(2,1)S(1)}, bf16[336,512]{1,0:T(8,128)(2,1)S(1)}, u32[]{:S(2)}, u32[]{:S(2)}) collective-permute-start(bf16[336,512]{1,0:T(8,128)(2,1)S(1)} %collective-permute-done.11), channel_id=1, source_target_pairs={{4,8},{6,10},{8,12},{10,14},{5,9},{7,11},{9,13},{11,15},{20,24},{2... | collective-permute-start | bytes 1032200 | tf_op jit(solution)/shard_map/ppermute | solution.py:59
  23.4 27.2 %collective-permute-start.17 = (bf16[336,512]{1,0:T(8,128)(2,1)S(1)}, bf16[336,512]{1,0:T(8,128)(2,1)S(1)}, u32[]{:S(2)}, u32[]{:S(2)}) collective-permute-start(bf16[336,512]{1,0:T(8,128)(2,1)S(1)} %collective-permute-done.11), channel_id=1, source_target_pairs={{6,4},{4,6},{10,8},{8,10},{14,12},{12,14},{7,5},{5,7},{11,9},{9,11... | collective-permute-start | bytes 1032200 | tf_op jit(solution)/shard_map/ppermute | solution.py:67
  26.9 13.2 %collective-permute-start.14 = (bf16[336,512]{1,0:T(8,128)(2,1)S(1)}, bf16[336,512]{1,0:T(8,128)(2,1)S(1)}, u32[]{:S(2)}, u32[]{:S(2)}) collective-permute-start(bf16[336,512]{1,0:T(8,128)(2,1)S(1)} %collective-permute-done.12), channel_id=1, source_target_pairs={{4,0},{6,2},{8,4},{10,6},{5,1},{7,3},{9,5},{11,7},{20,16},{22,18},... | collective-permute-start | bytes 1032200 | tf_op jit(solution)/shard_map/ppermute | solution.py:60
  29.7 13.2 %collective-permute-start.15 = (bf16[336,512]{1,0:T(8,128)(2,1)S(1)}, bf16[336,512]{1,0:T(8,128)(2,1)S(1)}, u32[]{:S(2)}, u32[]{:S(2)}) collective-permute-start(bf16[336,512]{1,0:T(8,128)(2,1)S(1)} %collective-permute-done.13), channel_id=1, source_target_pairs={{8,12},{10,14},{9,13},{11,15},{24,28},{26,30},{25,29},{27,31}} | collective-permute-start | bytes 1032200 | tf_op jit(solution)/shard_map/ppermute | solution.py:59
  40.0 9.1 %collective-permute-start.16 = (bf16[336,512]{1,0:T(8,128)(2,1)S(1)}, bf16[336,512]{1,0:T(8,128)(2,1)S(1)}, u32[]{:S(2)}, u32[]{:S(2)}) collective-permute-start(bf16[336,512]{1,0:T(8,128)(2,1)S(1)} %collective-permute-done.14), channel_id=1, source_target_pairs={{4,0},{6,2},{5,1},{7,3},{20,16},{22,18},{21,17},{23,19}} | collective-permute-start | bytes 1032200 | tf_op jit(solution)/shard_map/ppermute | solution.py:60
  42.8 11.0 %collective-permute-start.18 = (bf16[336,512]{1,0:T(8,128)(2,1)S(1)}, bf16[336,512]{1,0:T(8,128)(2,1)S(1)}, u32[]{:S(2)}, u32[]{:S(2)}) collective-permute-start(bf16[336,512]{1,0:T(8,128)(2,1)S(1)} %collective-permute-done.12), channel_id=1, source_target_pairs={{2,0},{0,2},{6,4},{4,6},{10,8},{8,10},{3,1},{1,3},{7,5},{5,7},{11,... | collective-permute-start | bytes 1032200 | tf_op jit(solution)/shard_map/ppermute | solution.py:69
  49.2 6.2 %collective-permute-start.19 = (bf16[336,512]{1,0:T(8,128)(2,1)S(1)}, bf16[336,512]{1,0:T(8,128)(2,1)S(1)}, u32[]{:S(2)}, u32[]{:S(2)}) collective-permute-start(bf16[336,512]{1,0:T(8,128)(2,1)S(1)} %collective-permute-done.13), channel_id=1, source_target_pairs={{10,8},{8,10},{14,12},{12,14},{11,9},{9,11},{15,13},{13,15},{26,24... | collective-permute-start | bytes 1032200 | tf_op jit(solution)/shard_map/ppermute | solution.py:67
  50.6 12.4 %collective-permute-start.20 = (bf16[336,512]{1,0:T(8,128)(2,1)S(1)}, bf16[336,512]{1,0:T(8,128)(2,1)S(1)}, u32[]{:S(2)}, u32[]{:S(2)}) collective-permute-start(bf16[336,512]{1,0:T(8,128)(2,1)S(1)} %collective-permute-done.14), channel_id=1, source_target_pairs={{2,0},{0,2},{6,4},{4,6},{3,1},{1,3},{7,5},{5,7},{18,16},{16,18},{2... | collective-permute-start | bytes 1032200 | tf_op jit(solution)/shard_map/ppermute | solution.py:69
  53.8 10.0 %collective-permute-start.21 = (bf16[336,512]{1,0:T(8,128)(2,1)S(1)}, bf16[336,512]{1,0:T(8,128)(2,1)S(1)}, u32[]{:S(2)}, u32[]{:S(2)}) collective-permute-start(bf16[336,512]{1,0:T(8,128)(2,1)S(1)} %collective-permute-done.15), channel_id=1, source_target_pairs={{14,12},{12,14},{15,13},{13,15},{30,28},{28,30},{31,29},{29,31}} | collective-permute-start | bytes 1032200 | tf_op jit(solution)/shard_map/ppermute | solution.py:67
  55.3 11.4 %collective-permute-start.22 = (bf16[336,512]{1,0:T(8,128)(2,1)S(1)}, bf16[336,512]{1,0:T(8,128)(2,1)S(1)}, u32[]{:S(2)}, u32[]{:S(2)}) collective-permute-start(bf16[336,512]{1,0:T(8,128)(2,1)S(1)} %collective-permute-done.16), channel_id=1, source_target_pairs={{2,0},{0,2},{3,1},{1,3},{18,16},{16,18},{19,17},{17,19}} | collective-permute-start | bytes 1032200 | tf_op jit(solution)/shard_map/ppermute | solution.py:69
  63.0 14.9 %collective-permute-start = (f32[16]{0:T(128)S(1)}, f32[16]{0:T(128)S(1)}, u32[]{:S(2)}, u32[]{:S(2)}) collective-permute-start(f32[16]{0:T(128)S(1)} %pad_maximum_fusion), channel_id=1, source_target_pairs={{0,8},{2,10},{4,12},{6,14},{8,0},{10,2},{12,4},{14,6},{1,9},{3,11}... | collective-permute-start | bytes 200 | tf_op jit(solution)/shard_map/ppermute | solution.py:19
  74.4 18.0 %collective-permute-start.23 = (bf16[2688,512]{1,0:T(8,128)(2,1)S(1)}, bf16[2688,512]{1,0:T(8,128)(2,1)}, u32[]{:S(2)}, u32[]{:S(2)}) collective-permute-start(bf16[2688,512]{1,0:T(8,128)(2,1)S(1)} %get-tuple-element.30), channel_id=1, source_target_pairs={{0,1},{1,0},{2,3},{3,2},{4,5},{5,4},{6,7},{7,6},{8,9},{9,8},{10,11... | collective-permute-start | bytes 8257544 | tf_op jit(solution)/shard_map/ppermute | solution.py:19
  78.0 3.5 %collective-permute-start.1 = (f32[16]{0:T(128)S(1)}, f32[16]{0:T(128)S(1)}, u32[]{:S(2)}, u32[]{:S(2)}) collective-permute-start(f32[16]{0:T(128)S(1)} %fusion.65), channel_id=1, source_target_pairs={{0,4},{2,6},{4,0},{6,2},{8,12},{10,14},{12,8},{14,10},{1,5},{3,7},... | collective-permute-start | bytes 200 | tf_op jit(solution)/shard_map/ppermute | solution.py:19
  81.5 3.5 %collective-permute-start.2 = (f32[16]{0:T(128)S(1)}, f32[16]{0:T(128)S(1)}, u32[]{:S(2)}, u32[]{:S(2)}) collective-permute-start(f32[16]{0:T(128)S(1)} %add.231), channel_id=1, source_target_pairs={{0,2},{2,0},{4,6},{6,4},{8,10},{10,8},{12,14},{14,12},{1,3},{3,1},... | collective-permute-start | bytes 200 | tf_op jit(solution)/shard_map/ppermute | solution.py:19
  86.4 3.9 %collective-permute-start.5 = (bf16[128,1024]{1,0:T(8,128)(2,1)S(1)}, bf16[128,1024]{1,0:T(8,128)(2,1)S(1)}, u32[]{:S(2)}, u32[]{:S(2)}) collective-permute-start(bf16[128,1024]{1,0:T(8,128)(2,1)S(1)} %collective-permute-done.4), channel_id=1, source_target_pairs={{8,12},{10,14},{9,13},{11,15},{24,28},{26,30},{25,29},{27,31}} | collective-permute-start | bytes 786440 | tf_op jit(solution)/shard_map/ppermute | solution.py:41
  88.9 3.3 %collective-permute-start.7 = (bf16[128,1024]{1,0:T(8,128)(2,1)}, bf16[128,1024]{1,0:T(8,128)(2,1)S(1)}, u32[]{:S(2)}, u32[]{:S(2)}) collective-permute-start(bf16[128,1024]{1,0:T(8,128)(2,1)} %collective-permute-done.3), channel_id=1, source_target_pairs={{6,4},{4,6},{10,8},{8,10},{14,12},{12,14},{7,5},{5,7},{11,9},{9,11... | collective-permute-start | bytes 786440 | tf_op jit(solution)/shard_map/ppermute | solution.py:45
  89.6 2.6 %collective-permute-start.8 = (bf16[128,1024]{1,0:T(8,128)(2,1)S(1)}, bf16[128,1024]{1,0:T(8,128)(2,1)S(1)}, u32[]{:S(2)}, u32[]{:S(2)}) collective-permute-start(bf16[128,1024]{1,0:T(8,128)(2,1)S(1)} %collective-permute-done.4), channel_id=1, source_target_pairs={{10,8},{8,10},{14,12},{12,14},{11,9},{9,11},{15,13},{13,15},{26,24... | collective-permute-start | bytes 786440 | tf_op jit(solution)/shard_map/ppermute | solution.py:45
  90.4 2.0 collective-permute-start.9
  117.4 19.2 %collective-permute-start.28 = (bf16[128,1024]{0,1:T(8,128)(2,1)S(1)}, bf16[128,1024]{0,1:T(8,128)(2,1)S(1)}, u32[]{:S(2)}, u32[]{:S(2)}) collective-permute-start(bf16[128,1024]{0,1:T(8,128)(2,1)S(1)} %bitcast.150), channel_id=1, source_target_pairs={{12,14},{14,12},{13,15},{15,13},{28,30},{30,28},{29,31},{31,29}} | collective-permute-start | bytes 786440 | tf_op jit(solution)/shard_map/ppermute | solution.py:102
  118.2 22.2 %collective-permute-start.32 = (bf16[128,1024]{0,1:T(8,128)(2,1)S(1)}, bf16[128,1024]{0,1:T(8,128)(2,1)S(1)}, u32[]{:S(2)}, u32[]{:S(2)}) collective-permute-start(bf16[128,1024]{0,1:T(8,128)(2,1)S(1)} %copy-done.6), channel_id=1, source_target_pairs={{0,4},{2,6},{4,8},{6,10},{8,12},{10,14},{1,5},{3,7},{5,9},{7,11},{... | collective-permute-start | bytes 786440 | tf_op jit(solution)/shard_map/ppermute | solution.py:41
  135.9 5.2 %collective-permute-start.27 = (bf16[128,1024]{0,1:T(8,128)(2,1)S(1)}, bf16[128,1024]{0,1:T(8,128)(2,1)S(1)}, u32[]{:S(2)}, u32[]{:S(2)}) collective-permute-start(bf16[128,1024]{0,1:T(8,128)(2,1)S(1)} %bitcast.149), channel_id=1, source_target_pairs={{8,10},{10,8},{12,14},{14,12},{9,11},{11,9},{13,15},{15,13},{24,26... | collective-permute-start | bytes 786440 | tf_op jit(solution)/shard_map/ppermute | solution.py:102
  136.7 4.4 %collective-permute-start.29 = (bf16[128,1024]{0,1:T(8,128)(2,1)S(1)}, bf16[128,1024]{0,1:T(8,128)(2,1)S(1)}, u32[]{:S(2)}, u32[]{:S(2)}) collective-permute-start(bf16[128,1024]{0,1:T(8,128)(2,1)S(1)} %fusion.22), channel_id=1, source_target_pairs={{12,8},{14,10},{13,9},{15,11},{28,24},{30,26},{29,25},{31,27}} | collective-permute-start | bytes 786440 | tf_op jit(solution)/shard_map/ppermute | solution.py:110
  137.4 9.8 %collective-permute-start.26 = (bf16[128,1024]{0,1:T(8,128)(2,1)S(1)}, bf16[128,1024]{0,1:T(8,128)(2,1)S(1)}, u32[]{:S(2)}, u32[]{:S(2)}) collective-permute-start(bf16[128,1024]{0,1:T(8,128)(2,1)S(1)} %bitcast.148), channel_id=1, source_target_pairs={{4,6},{6,4},{8,10},{10,8},{12,14},{14,12},{5,7},{7,5},{9,11},{11,9... | collective-permute-start | bytes 786440 | tf_op jit(solution)/shard_map/ppermute | solution.py:102
  140.5 5.9 %collective-permute-start.33 = (bf16[128,1024]{0,1:T(8,128)(2,1)S(1)}, bf16[128,1024]{0,1:T(8,128)(2,1)S(1)}, u32[]{:S(2)}, u32[]{:S(2)}) collective-permute-start(bf16[128,1024]{0,1:T(8,128)(2,1)S(1)} %collective-permute-done.32), channel_id=1, source_target_pairs={{4,8},{6,10},{8,12},{10,14},{5,9},{7,11},{9,13},{11,15},{20,24},{2... | collective-permute-start | bytes 786440 | tf_op jit(solution)/shard_map/ppermute | solution.py:41
  141.3 6.6 %collective-permute-start.30 = (bf16[128,1024]{0,1:T(8,128)(2,1)S(1)}, bf16[128,1024]{0,1:T(8,128)(2,1)S(1)}, u32[]{:S(2)}, u32[]{:S(2)}) collective-permute-start(bf16[128,1024]{0,1:T(8,128)(2,1)S(1)} %fusion.24), channel_id=1, source_target_pairs={{8,4},{10,6},{12,8},{14,10},{9,5},{11,7},{13,9},{15,11},{24,20},{2... | collective-permute-start | bytes 786440 | tf_op jit(solution)/shard_map/ppermute | solution.py:110
  142.0 8.1 %collective-permute-start.35 = (bf16[128,1024]{0,1:T(8,128)(2,1)S(1)}, bf16[128,1024]{0,1:T(8,128)(2,1)S(1)}, u32[]{:S(2)}, u32[]{:S(2)}) collective-permute-start(bf16[128,1024]{0,1:T(8,128)(2,1)S(1)} %copy-done.6), channel_id=1, source_target_pairs={{0,2},{4,6},{8,10},{12,14},{1,3},{5,7},{9,11},{13,15},{16,18},{20,... | collective-permute-start | bytes 786440 | tf_op jit(solution)/shard_map/ppermute | solution.py:37
  144.9 14.8 %collective-permute-start.25 = (bf16[128,1024]{0,1:T(8,128)(2,1)S(1)}, bf16[128,1024]{0,1:T(8,128)(2,1)S(1)}, u32[]{:S(2)}, u32[]{:S(2)}) collective-permute-start(bf16[128,1024]{0,1:T(8,128)(2,1)S(1)} %bitcast.147), channel_id=1, source_target_pairs={{2,0},{6,4},{10,8},{14,12},{3,1},{7,5},{11,9},{15,13},{18,16},{22,... | collective-permute-start | bytes 786440 | tf_op jit(solution)/shard_map/ppermute | solution.py:99
  146.4 2.3 collective-permute-start.34
  147.2 3.9 %collective-permute-start.36 = (bf16[128,1024]{0,1:T(8,128)(2,1)S(1)}, bf16[128,1024]{0,1:T(8,128)(2,1)S(1)}, u32[]{:S(2)}, u32[]{:S(2)}) collective-permute-start(bf16[128,1024]{0,1:T(8,128)(2,1)S(1)} %collective-permute-done.32), channel_id=1, source_target_pairs={{6,4},{4,6},{10,8},{8,10},{14,12},{12,14},{7,5},{5,7},{11,9},{9,11... | collective-permute-start | bytes 786440 | tf_op jit(solution)/shard_map/ppermute | solution.py:45
  147.9 3.3 %collective-permute-start.37 = (bf16[128,1024]{0,1:T(8,128)(2,1)S(1)}, bf16[128,1024]{0,1:T(8,128)(2,1)S(1)}, u32[]{:S(2)}, u32[]{:S(2)}) collective-permute-start(bf16[128,1024]{0,1:T(8,128)(2,1)S(1)} %collective-permute-done.33), channel_id=1, source_target_pairs={{10,8},{8,10},{14,12},{12,14},{11,9},{9,11},{15,13},{13,15},{26,24... | collective-permute-start | bytes 786440 | tf_op jit(solution)/shard_map/ppermute | solution.py:45
  148.7 31.6 %collective-permute-start.31 = (bf16[128,1024]{0,1:T(8,128)(2,1)S(1)}, bf16[128,1024]{0,1:T(8,128)(2,1)S(1)}, u32[]{:S(2)}, u32[]{:S(2)}) collective-permute-start(bf16[128,1024]{0,1:T(8,128)(2,1)S(1)} %fusion.26), channel_id=1, source_target_pairs={{4,0},{6,2},{8,4},{10,6},{12,8},{14,10},{5,1},{7,3},{9,5},{11,7},{... | collective-permute-start | bytes 786440 | tf_op jit(solution)/shard_map/ppermute | solution.py:110
  150.1 1.2 collective-permute-start.38
  183.9 24.3 %collective-permute-start.42 = (bf16[128,1024]{1,0:T(8,128)(2,1)}, bf16[128,1024]{1,0:T(8,128)(2,1)}, u32[]{:S(2)}, u32[]{:S(2)}) collective-permute-start(bf16[128,1024]{1,0:T(8,128)(2,1)} %copy.73), channel_id=1, source_target_pairs={{12,14},{14,12},{13,15},{15,13},{28,30},{30,28},{29,31},{31,29}} | collective-permute-start | bytes 786440 | tf_op jit(solution)/shard_map/ppermute | solution.py:102
  186.1 45.2 %collective-permute-start.41 = (bf16[128,1024]{1,0:T(8,128)(2,1)}, bf16[128,1024]{1,0:T(8,128)(2,1)}, u32[]{:S(2)}, u32[]{:S(2)}) collective-permute-start(bf16[128,1024]{1,0:T(8,128)(2,1)} %copy.71), channel_id=1, source_target_pairs={{8,10},{10,8},{12,14},{14,12},{9,11},{11,9},{13,15},{15,13},{24,26... | collective-permute-start | bytes 786440 | tf_op jit(solution)/shard_map/ppermute | solution.py:102
  189.2 31.2 %collective-permute-start.46 = (f32[464,128]{1,0:T(8,128)}, f32[464,128]{1,0:T(8,128)}, u32[]{:S(2)}, u32[]{:S(2)}) collective-permute-start(f32[464,128]{1,0:T(8,128)} %maximum_bitcast_fusion), channel_id=1, source_target_pairs={{0,8},{2,10},{4,12},{6,14},{8,0},{10,2},{12,4},{14,6},{1,9},{3,11}... | collective-permute-start | bytes 712712 | tf_op jit(solution)/shard_map/ppermute | solution.py:19
  210.1 21.2 %collective-permute-start.43 = (bf16[128,1024]{1,0:T(8,128)(2,1)}, bf16[128,1024]{1,0:T(8,128)(2,1)}, u32[]{:S(2)}, u32[]{:S(2)}) collective-permute-start(bf16[128,1024]{1,0:T(8,128)(2,1)} %add_convert_fusion.3), channel_id=1, source_target_pairs={{12,8},{14,10},{13,9},{15,11},{28,24},{30,26},{29,25},{31,27}} | collective-permute-start | bytes 786440 | tf_op jit(solution)/shard_map/ppermute | solution.py:110
  216.9 26.4 %collective-permute-start.40 = (bf16[128,1024]{1,0:T(8,128)(2,1)}, bf16[128,1024]{1,0:T(8,128)(2,1)}, u32[]{:S(2)}, u32[]{:S(2)}) collective-permute-start(bf16[128,1024]{1,0:T(8,128)(2,1)} %copy.69), channel_id=1, source_target_pairs={{4,6},{6,4},{8,10},{10,8},{12,14},{14,12},{5,7},{7,5},{9,11},{11,9... | collective-permute-start | bytes 786440 | tf_op jit(solution)/shard_map/ppermute | solution.py:102
  219.2 34.8 %collective-permute-start.39 = (bf16[128,1024]{1,0:T(8,128)(2,1)}, bf16[128,1024]{1,0:T(8,128)(2,1)S(1)}, u32[]{:S(2)}, u32[]{:S(2)}) collective-permute-start(bf16[128,1024]{1,0:T(8,128)(2,1)} %copy.68), channel_id=1, source_target_pairs={{2,0},{6,4},{10,8},{14,12},{3,1},{7,5},{11,9},{15,13},{18,16},{22,... | collective-permute-start | bytes 786440 | tf_op jit(solution)/shard_map/ppermute | solution.py:99
  221.4 14.0 %collective-permute-start.47 = (f32[464,128]{1,0:T(8,128)S(1)}, f32[464,128]{1,0:T(8,128)S(1)}, u32[]{:S(2)}, u32[]{:S(2)}) collective-permute-start(f32[464,128]{1,0:T(8,128)S(1)} %fusion.34), channel_id=1, source_target_pairs={{0,4},{2,6},{4,0},{6,2},{8,12},{10,14},{12,8},{14,10},{1,5},{3,7},... | collective-permute-start | bytes 712712 | tf_op jit(solution)/shard_map/ppermute | solution.py:19
  232.5 10.9 %collective-permute-start.44 = (bf16[128,1024]{1,0:T(8,128)(2,1)S(1)}, bf16[128,1024]{1,0:T(8,128)(2,1)S(1)}, u32[]{:S(2)}, u32[]{:S(2)}) collective-permute-start(bf16[128,1024]{1,0:T(8,128)(2,1)S(1)} %add_convert_fusion.2), channel_id=1, source_target_pairs={{8,4},{10,6},{12,8},{14,10},{9,5},{11,7},{13,9},{15,11},{24,20},{2... | collective-permute-start | bytes 786440 | tf_op jit(solution)/shard_map/ppermute | solution.py:110
  236.4 6.8 %collective-permute-start.48 = (f32[464,128]{1,0:T(8,128)S(1)}, f32[464,128]{1,0:T(8,128)S(1)}, u32[]{:S(2)}, u32[]{:S(2)}) collective-permute-start(f32[464,128]{1,0:T(8,128)S(1)} %fusion.64), channel_id=1, source_target_pairs={{0,2},{2,0},{4,6},{6,4},{8,10},{10,8},{12,14},{14,12},{1,3},{3,1},... | collective-permute-start | bytes 712712 | tf_op jit(solution)/shard_map/ppermute | solution.py:19
  243.3 8.5 %collective-permute-start.49 = (f32[464,128]{1,0:T(8,128)S(1)}, f32[464,128]{1,0:T(8,128)S(1)}, u32[]{:S(2)}, u32[]{:S(2)}) collective-permute-start(f32[464,128]{1,0:T(8,128)S(1)} %add.274), channel_id=1, source_target_pairs={{0,1},{1,0},{2,3},{3,2},{4,5},{5,4},{6,7},{7,6},{8,9},{9,8},{10,11... | collective-permute-start | bytes 712712 | tf_op jit(solution)/shard_map/ppermute | solution.py:19
  245.1 11.2 %collective-permute-start.45 = (bf16[128,1024]{1,0:T(8,128)(2,1)}, bf16[128,1024]{1,0:T(8,128)(2,1)}, u32[]{:S(2)}, u32[]{:S(2)}) collective-permute-start(bf16[128,1024]{1,0:T(8,128)(2,1)} %add_convert_fusion.1), channel_id=1, source_target_pairs={{4,0},{6,2},{8,4},{10,6},{12,8},{14,10},{5,1},{7,3},{9,5},{11,7},{... | collective-permute-start | bytes 786440 | tf_op jit(solution)/shard_map/ppermute | solution.py:110
  (23 other events, 287.0 us)

commit v19 on v17

--- a/solution.py
+++ b/solution.py
@@ -96,12 +96,12 @@
     count = 2 * levels
     climbed = slot_parts[: levels - 1]
     crossed = slot_parts[levels - 1 :]
-    back = [lax.ppermute(crossed[0], "ctx", [(c, c - 1) for c in range(1, count, 2)])]
+    back = [None]
     for step in range(1, levels):
         back.append(
             lax.ppermute(crossed[step], "ctx", [(c, c ^ 1) for c in range(2 * step, count)])
         )
-    total = back[0].astype(jnp.float32)
+    total = None
     carry = None
     for step in range(levels - 1, 0, -1):
         acc = climbed[step - 1].astype(jnp.float32) + back[step].astype(jnp.float32)
@@ -110,6 +110,8 @@
         carry = lax.ppermute(
             acc.astype(jnp.bfloat16), "ctx", [(c, c - 2) for c in range(2 * step, count)]
         )
+    total = lax.ppermute(crossed[0], "ctx", [(c, c - 1) for c in range(1, count, 2)])
+    total = total.astype(jnp.float32)
     if carry is not None:
         total = total + carry.astype(jnp.float32)
     return total

time: 260 us -> 260 us (level)
  no operation moved by 1% of the time
where the time goes in v19:
time: 260 us; the launch traced here: 258 us
  starting transfers between devices  102 us (39%)
  waiting for transfers between devices  61.9 us (24%)
  local copies, waits for them, and re-layouts  47.5 us (18%)
  matrix products  29.5 us (11%)
  other arithmetic  14.8 us (6%)
    ppermute x9, starting transfers between devices, from_partner(): lax.ppermute(shard, axis, [(i, i ^ 1 << stride) for i in range(lax.axis_s...  31.7 us
    ppermute x6, starting transfers between devices, tree_spread(): lax.ppermute(held, 'ctx', [(c - 2, c) for c in range(2 * step, count)])  26.3 us
    ppermute x6, waiting for transfers between devices, tree_return(): lax.ppermute(acc.astype(jnp.bfloat16), 'ctx', [(c, c - 2) for c in range(...  23 us
    ppermute x3, waiting for transfers between devices, tree_gather(): lax.ppermute(down, 'ctx', [(c + 2, c) for c in range(0, count - 2 * step)])  14.8 us
    ppermute x9, waiting for transfers between devices, from_partner(): lax.ppermute(shard, axis, [(i, i ^ 1 << stride) for i in range(lax.axis_s...  12.2 us
    dynamic_update_slice x14, local copies, waits for them, and re-layouts, tree_gather(): whole = lax.dynamic_update_slice_in_dim(whole, piece, place, 0)  10.7 us
    ppermute x3, starting transfers between devices, tree_gather(): lax.ppermute(downs[step - 1], 'ctx', [(c ^ 1, c) for c in range(0, count...  8.24 us
    unnamed x60, local copies, waits for them, and re-layouts  6.94 us
  transfers between devices with their start and end apart: 50, of which 14 were waited for; matrix products, arithmetic and copies ran while one was open for 24% of the time, Pallas kernels for 0%

profile of v19, /device:TPU:0, one launch (start us, length us, event | category | flops | bytes accessed | tf_op | source)
XLA Modules:
  0.0 258.1 jit_solution(1169830148806569385)
XLA Ops:
  0.7 5.8 %collective-permute-start.3 = (bf16[128,1024]{1,0:T(8,128)(2,1)}, bf16[128,1024]{1,0:T(8,128)(2,1)}, u32[]{:S(2)}, u32[]{:S(2)}) collective-permute-start(bf16[128,1024]{1,0:T(8,128)(2,1)} %bitcast.151), channel_id=1, source_target_pairs={{0,4},{2,6},{4,8},{6,10},{8,12},{10,14},{1,5},{3,7},{5,9},{7,11},{... | collective-permute-start | bytes 786440 | tf_op jit(solution)/shard_map/ppermute | solution.py:40
  6.5 4.1 %collective-permute-start.6 = (bf16[128,1024]{1,0:T(8,128)(2,1)}, bf16[128,1024]{1,0:T(8,128)(2,1)}, u32[]{:S(2)}, u32[]{:S(2)}) collective-permute-start(bf16[128,1024]{1,0:T(8,128)(2,1)} %bitcast.152), channel_id=1, source_target_pairs={{0,2},{4,6},{8,10},{12,14},{1,3},{5,7},{9,11},{13,15},{16,18},{20,... | collective-permute-start | bytes 786440 | tf_op jit(solution)/shard_map/ppermute | solution.py:42
  10.6 1.8 broadcast_in_dim.58
  13.2 2.8 %collective-permute-start.11 = (bf16[336,512]{1,0:T(8,128)(2,1)S(1)}, bf16[336,512]{1,0:T(8,128)(2,1)S(1)}, u32[]{:S(2)}, u32[]{:S(2)}) collective-permute-start(bf16[336,512]{1,0:T(8,128)(2,1)S(1)} %get-tuple-element.29), channel_id=1, source_target_pairs={{0,4},{2,6},{4,8},{6,10},{8,12},{10,14},{1,5},{3,7},{5,9},{7,11},{... | collective-permute-start | bytes 1032200 | tf_op jit(solution)/shard_map/ppermute | solution.py:59
  16.0 1.3 collective-permute-start.12
  18.9 3.8 %collective-permute-done.11 = bf16[336,512]{1,0:T(8,128)(2,1)S(1)} collective-permute-done((bf16[336,512]{1,0:T(8,128)(2,1)S(1)}, bf16[336,512]{1,0:T(8,128)(2,1)S(1)}, u32[]{:S(2)}, u32[]{:S(2)}) %collective-permute-start.11) | collective-permute-done | bytes 344096 | tf_op jit(solution)/shard_map/ppermute | solution.py:59
  24.1 2.7 %collective-permute-done.12 = bf16[336,512]{1,0:T(8,128)(2,1)S(1)} collective-permute-done((bf16[336,512]{1,0:T(8,128)(2,1)S(1)}, bf16[336,512]{1,0:T(8,128)(2,1)S(1)}, u32[]{:S(2)}, u32[]{:S(2)}) %collective-permute-start.12) | collective-permute-done | bytes 344096 | tf_op jit(solution)/shard_map/ppermute | solution.py:60
  31.1 8.9 %collective-permute-done.14 = bf16[336,512]{1,0:T(8,128)(2,1)S(1)} collective-permute-done((bf16[336,512]{1,0:T(8,128)(2,1)S(1)}, bf16[336,512]{1,0:T(8,128)(2,1)S(1)}, u32[]{:S(2)}, u32[]{:S(2)}) %collective-permute-start.14) | collective-permute-done | bytes 344096 | tf_op jit(solution)/shard_map/ppermute | solution.py:60
  42.8 2.5 collective-permute-start.18
  46.1 3.1 %collective-permute-done.16 = bf16[336,512]{1,0:T(8,128)(2,1)S(1)} collective-permute-done((bf16[336,512]{1,0:T(8,128)(2,1)S(1)}, bf16[336,512]{1,0:T(8,128)(2,1)S(1)}, u32[]{:S(2)}, u32[]{:S(2)}) %collective-permute-start.16) | collective-permute-done | bytes 344096 | tf_op jit(solution)/shard_map/ppermute | solution.py:60
  50.6 2.4 collective-permute-start.20
  55.3 3.4 %collective-permute-start.22 = (bf16[336,512]{1,0:T(8,128)(2,1)S(1)}, bf16[336,512]{1,0:T(8,128)(2,1)S(1)}, u32[]{:S(2)}, u32[]{:S(2)}) collective-permute-start(bf16[336,512]{1,0:T(8,128)(2,1)S(1)} %collective-permute-done.16), channel_id=1, source_target_pairs={{2,0},{0,2},{3,1},{1,3},{18,16},{16,18},{19,17},{17,19}} | collective-permute-start | bytes 1032200 | tf_op jit(solution)/shard_map/ppermute | solution.py:69
  59.4 3.6 %collective-permute-done.20 = bf16[336,512]{1,0:T(8,128)(2,1)S(1)} collective-permute-done((bf16[336,512]{1,0:T(8,128)(2,1)S(1)}, bf16[336,512]{1,0:T(8,128)(2,1)S(1)}, u32[]{:S(2)}, u32[]{:S(2)}) %collective-permute-start.20) | collective-permute-done | bytes 344096 | tf_op jit(solution)/shard_map/ppermute | solution.py:69
  64.5 2.2 collective-permute-done.22
  67.5 3.2 %broadcast_in_dim.57 = bf16[2688,1024]{1,0:T(8,128)(2,1)} broadcast(bf16[]{:T(256)} %constant.74.clone.1), dimensions={} | broadcast | bytes 5505026 | tf_op jit(solution)/shard_map/broadcast_in_dim | solution.py:155
  70.6 3.8 %fusion.35 = (bf16[2688,512]{1,0:T(8,128)(2,1)S(1)}, bf16[2688,1024]{1,0:T(8,128)(2,1)}) fusion(bf16[3024,512]{1,0:T(8,128)(2,1)} %constant_dynamic-update-slice_fusion.26, bf16[2688,1024]{1,0:T(8,128)(2,1)} %broadcast_in_dim.57, s32[]{:T(128)S(6)} %select_n.156), kind=kLoop, calls=%fused_computation.123 | loop fusion | bytes 8257540 | tf_op jit(solution)/shard_map/slice | solution.py:78
  75.8 2.0 copy.94
  78.0 3.5 %collective-permute-done.1 = f32[16]{0:T(128)S(1)} collective-permute-done((f32[16]{0:T(128)S(1)}, f32[16]{0:T(128)S(1)}, u32[]{:S(2)}, u32[]{:S(2)}) %collective-permute-start.1) | collective-permute-done | bytes 96 | tf_op jit(solution)/shard_map/ppermute | solution.py:19
  82.5 2.5 collective-permute-done.2
  92.4 3.6 %constant_dynamic-update-slice_fusion.24 = bf16[2688,1024]{1,0:T(8,128)(2,1)} fusion(bf16[2688,1024]{1,0:T(8,128)(2,1)} %get-tuple-element.31, bf16[2688,512]{1,0:T(8,128)(2,1)} %collective-permute-done.23, s32[]{:T(128)S(6)} %select_n.185), kind=kLoop, calls=%fused_computation.84 | loop fusion | bytes 5505028 | tf_op jit(solution)/shard_map/dynamic_update_slice | solution.py:157
  96.0 4.9 %fusion.15 = bf16[128,1024]{0,1:T(8,128)(2,1)} fusion(f32[128,1024]{0,1:T(8,128)S(1)} %copy-done.2, bf16[2688,1024]{1,0:T(8,128)(2,1)} %constant_dynamic-update-slice_fusion.24, bf16[1,128,2688]{2,1,0:T(8,128)(2,1)S(1)} %copy-done), kind=kOutput, calls=%fused_computation.28 | convolution fusion | flops 704905216 | bytes 6979584 | tf_op jit(solution)/shard_map/dot_general | solution.py:166
  100.9 2.0 copy.95
  102.9 3.3 %copy.84 = bf16[1024,8,128,1]{0,2,3,1:T(8,128)(2,1)S(1)} copy(bf16[1024,8,128,1]{2,1,0,3:T(8,128)(2,1)} %bitcast.134) | data formatting | bytes 4194304 | tf_op jit(solution)/shard_map/reshape | solution.py:221
  106.2 5.7 %fusion.39 = (f32[8,2,128]{2,1,0:T(2,128)S(1)}, f32[8,2,128,1024]{2,3,1,0:T(8,128)}) fusion(pred[128,1024]{0,1:T(8,128)(4,1)S(1)} %copy-done.17, bf16[1024,8,128,1]{0,2,3,1:T(8,128)(2,1)S(1)} %copy.84, bf16[128,8,2,128]{0,3,2,1:T(8,128)(2,1)S(1)} %bitcast.138), kind=kOutput, calls=%fused_computation.127 | convolution fusion | flops 547357696 | bytes 11149312 | tf_op jit(solution)/shard_map/sub | solution.py:228
  111.9 5.0 %fusion.40 = (bf16[1024,8,128]{0,2,1:T(8,128)(2,1)S(1)}, f32[1024,8,128]{0,2,1:T(8,128)S(1)}) fusion(bf16[128,8,2,128]{3,2,1,0:T(2,128)(2,1)} %reshape_squeeze.7, f32[128]{0:T(128)S(1)} %get-tuple-element.25, f32[8,2,128,1024]{2,3,1,0:T(8,128)} %get-tuple-element.51, f32[8,2,128]{2,1,0:T(2,128)S(1)} %get-tuple-element.50), kind=kOutput, calls=%fused_computation.128 | convolution fusion | flops 544210944 | bytes 15213056 | tf_op jit(solution)/shard_map/jgtl,tjgd->ljd/dot_general | solution.py:242
  118.2 17.7 %collective-permute-start.32 = (bf16[128,1024]{0,1:T(8,128)(2,1)S(1)}, bf16[128,1024]{0,1:T(8,128)(2,1)S(1)}, u32[]{:S(2)}, u32[]{:S(2)}) collective-permute-start(bf16[128,1024]{0,1:T(8,128)(2,1)S(1)} %copy-done.6), channel_id=1, source_target_pairs={{0,4},{2,6},{4,8},{6,10},{8,12},{10,14},{1,5},{3,7},{5,9},{7,11},{... | collective-permute-start | bytes 786440 | tf_op jit(solution)/shard_map/ppermute | solution.py:40
  138.1 2.4 collective-permute-done.32
  142.0 2.8 %collective-permute-start.35 = (bf16[128,1024]{0,1:T(8,128)(2,1)S(1)}, bf16[128,1024]{0,1:T(8,128)(2,1)S(1)}, u32[]{:S(2)}, u32[]{:S(2)}) collective-permute-start(bf16[128,1024]{0,1:T(8,128)(2,1)S(1)} %copy-done.6), channel_id=1, source_target_pairs={{0,2},{4,6},{8,10},{12,14},{1,3},{5,7},{9,11},{13,15},{16,18},{20,... | collective-permute-start | bytes 786440 | tf_op jit(solution)/shard_map/ppermute | solution.py:42
  144.9 1.4 collective-permute-start.25
  151.5 1.9 fusion.1
  153.5 1.7 fusion.3
  156.2 3.5 %fusion.41 = (bf16[1024,8,128]{0,2,1:T(8,128)(2,1)S(1)}, f32[1024,8,128]{0,2,1:T(8,128)}) fusion(bf16[8,2,128,1024]{2,3,1,0:T(8,128)(2,1)S(1)} %fusion.3, bf16[128,8,2,128]{0,3,2,1:T(8,128)(2,1)S(1)} %bitcast.139), kind=kOutput, calls=%fused_computation.129 | convolution fusion | flops 537919488 | bytes 11010048 | tf_op jit(solution)/shard_map/jgtl,tjgd->ljd/dot_general | solution.py:238
  159.7 20.6 %collective-permute-done.31 = bf16[128,1024]{0,1:T(8,128)(2,1)S(1)} collective-permute-done((bf16[128,1024]{0,1:T(8,128)(2,1)S(1)}, bf16[128,1024]{0,1:T(8,128)(2,1)S(1)}, u32[]{:S(2)}, u32[]{:S(2)}) %collective-permute-start.31) | collective-permute-done | bytes 262176 | tf_op jit(solution)/shard_map/ppermute | solution.py:110
  183.9 1.4 collective-permute-start.42
  186.1 1.4 collective-permute-start.41
  189.2 18.0 %collective-permute-start.46 = (f32[464,128]{1,0:T(8,128)}, f32[464,128]{1,0:T(8,128)}, u32[]{:S(2)}, u32[]{:S(2)}) collective-permute-start(f32[464,128]{1,0:T(8,128)} %maximum_bitcast_fusion), channel_id=1, source_target_pairs={{0,8},{2,10},{4,12},{6,14},{8,0},{10,2},{12,4},{14,6},{1,9},{3,11}... | collective-permute-start | bytes 712712 | tf_op jit(solution)/shard_map/ppermute | solution.py:19
  208.2 1.9 add_convert_fusion.3
  210.1 1.4 collective-permute-start.43
  215.1 1.8 copy.69
  216.9 1.4 collective-permute-start.40
  221.4 9.9 %collective-permute-start.47 = (f32[464,128]{1,0:T(8,128)S(1)}, f32[464,128]{1,0:T(8,128)S(1)}, u32[]{:S(2)}, u32[]{:S(2)}) collective-permute-start(f32[464,128]{1,0:T(8,128)S(1)} %fusion.34), channel_id=1, source_target_pairs={{0,4},{2,6},{4,0},{6,2},{8,12},{10,14},{12,8},{14,10},{1,5},{3,7},... | collective-permute-start | bytes 712712 | tf_op jit(solution)/shard_map/ppermute | solution.py:19
  233.2 2.3 collective-permute-done.47
  236.4 2.7 %collective-permute-start.48 = (f32[464,128]{1,0:T(8,128)S(1)}, f32[464,128]{1,0:T(8,128)S(1)}, u32[]{:S(2)}, u32[]{:S(2)}) collective-permute-start(f32[464,128]{1,0:T(8,128)S(1)} %fusion.64), channel_id=1, source_target_pairs={{0,2},{2,0},{4,6},{6,4},{8,10},{10,8},{12,14},{14,12},{1,3},{3,1},... | collective-permute-start | bytes 712712 | tf_op jit(solution)/shard_map/ppermute | solution.py:19
  239.5 3.7 %collective-permute-done.48 = f32[464,128]{1,0:T(8,128)S(1)} collective-permute-done((f32[464,128]{1,0:T(8,128)S(1)}, f32[464,128]{1,0:T(8,128)S(1)}, u32[]{:S(2)}, u32[]{:S(2)}) %collective-permute-start.48) | collective-permute-done | bytes 237600 | tf_op jit(solution)/shard_map/ppermute | solution.py:19
  243.4 1.8 add_convert_fusion.1
  246.4 5.4 %fusion.11 = bf16[1,128,2688]{2,1,0:T(8,128)(2,1)} fusion(f32[128,2688]{1,0:T(8,128)S(1)} %convolution_multiply_fusion, bf16[128,1024]{0,1:T(8,128)(2,1)S(1)} %fusion.27, bf16[2688,1024]{1,0:T(8,128)(2,1)} %constant_dynamic-update-slice_fusion.24), kind=kOutput, calls=%fused_computation.19 | convolution fusion | flops 705331200 | bytes 7831552 | tf_op jit(solution)/shard_map/tk,dk->td/dot_general | solution.py:267
  253.9 2.3 collective-permute-done.45
  256.3 1.8 fusion.31
  (205 shorter events, 59.4 us)
Async XLA Ops:
  0.7 84.6 %collective-permute-start.3 = (bf16[128,1024]{1,0:T(8,128)(2,1)}, bf16[128,1024]{1,0:T(8,128)(2,1)}, u32[]{:S(2)}, u32[]{:S(2)}) collective-permute-start(bf16[128,1024]{1,0:T(8,128)(2,1)} %bitcast.151), channel_id=1, source_target_pairs={{0,4},{2,6},{4,8},{6,10},{8,12},{10,14},{1,5},{3,7},{5,9},{7,11},{... | collective-permute-start | bytes 786440 | tf_op jit(solution)/shard_map/ppermute | solution.py:40
  6.5 84.8 %collective-permute-start.6 = (bf16[128,1024]{1,0:T(8,128)(2,1)}, bf16[128,1024]{1,0:T(8,128)(2,1)}, u32[]{:S(2)}, u32[]{:S(2)}) collective-permute-start(bf16[128,1024]{1,0:T(8,128)(2,1)} %bitcast.152), channel_id=1, source_target_pairs={{0,2},{4,6},{8,10},{12,14},{1,3},{5,7},{9,11},{13,15},{16,18},{20,... | collective-permute-start | bytes 786440 | tf_op jit(solution)/shard_map/ppermute | solution.py:42
  13.2 10.2 %collective-permute-start.10 = (bf16[336,512]{1,0:T(8,128)(2,1)S(1)}, bf16[336,512]{1,0:T(8,128)(2,1)S(1)}, u32[]{:S(2)}, u32[]{:S(2)}) collective-permute-start(bf16[336,512]{1,0:T(8,128)(2,1)S(1)} %get-tuple-element.29), channel_id=1, source_target_pairs={{2,0},{0,2},{6,4},{4,6},{10,8},{8,10},{14,12},{12,14},{3,1},{1,3},... | collective-permute-start | bytes 1032200 | tf_op jit(solution)/shard_map/ppermute | solution.py:53
  13.2 9.5 %collective-permute-start.11 = (bf16[336,512]{1,0:T(8,128)(2,1)S(1)}, bf16[336,512]{1,0:T(8,128)(2,1)S(1)}, u32[]{:S(2)}, u32[]{:S(2)}) collective-permute-start(bf16[336,512]{1,0:T(8,128)(2,1)S(1)} %get-tuple-element.29), channel_id=1, source_target_pairs={{0,4},{2,6},{4,8},{6,10},{8,12},{10,14},{1,5},{3,7},{5,9},{7,11},{... | collective-permute-start | bytes 1032200 | tf_op jit(solution)/shard_map/ppermute | solution.py:59
  16.0 10.9 %collective-permute-start.12 = (bf16[336,512]{1,0:T(8,128)(2,1)S(1)}, bf16[336,512]{1,0:T(8,128)(2,1)S(1)}, u32[]{:S(2)}, u32[]{:S(2)}) collective-permute-start(bf16[336,512]{1,0:T(8,128)(2,1)S(1)} %get-tuple-element.29), channel_id=1, source_target_pairs={{4,0},{6,2},{8,4},{10,6},{12,8},{14,10},{5,1},{7,3},{9,5},{11,7},{... | collective-permute-start | bytes 1032200 | tf_op jit(solution)/shard_map/ppermute | solution.py:60
  22.7 6.9 %collective-permute-start.13 = (bf16[336,512]{1,0:T(8,128)(2,1)S(1)}, bf16[336,512]{1,0:T(8,128)(2,1)S(1)}, u32[]{:S(2)}, u32[]{:S(2)}) collective-permute-start(bf16[336,512]{1,0:T(8,128)(2,1)S(1)} %collective-permute-done.11), channel_id=1, source_target_pairs={{4,8},{6,10},{8,12},{10,14},{5,9},{7,11},{9,13},{11,15},{20,24},{2... | collective-permute-start | bytes 1032200 | tf_op jit(solution)/shard_map/ppermute | solution.py:59
  23.4 27.2 %collective-permute-start.17 = (bf16[336,512]{1,0:T(8,128)(2,1)S(1)}, bf16[336,512]{1,0:T(8,128)(2,1)S(1)}, u32[]{:S(2)}, u32[]{:S(2)}) collective-permute-start(bf16[336,512]{1,0:T(8,128)(2,1)S(1)} %collective-permute-done.11), channel_id=1, source_target_pairs={{6,4},{4,6},{10,8},{8,10},{14,12},{12,14},{7,5},{5,7},{11,9},{9,11... | collective-permute-start | bytes 1032200 | tf_op jit(solution)/shard_map/ppermute | solution.py:67
  26.9 13.2 %collective-permute-start.14 = (bf16[336,512]{1,0:T(8,128)(2,1)S(1)}, bf16[336,512]{1,0:T(8,128)(2,1)S(1)}, u32[]{:S(2)}, u32[]{:S(2)}) collective-permute-start(bf16[336,512]{1,0:T(8,128)(2,1)S(1)} %collective-permute-done.12), channel_id=1, source_target_pairs={{4,0},{6,2},{8,4},{10,6},{5,1},{7,3},{9,5},{11,7},{20,16},{22,18},... | collective-permute-start | bytes 1032200 | tf_op jit(solution)/shard_map/ppermute | solution.py:60
  29.7 13.2 %collective-permute-start.15 = (bf16[336,512]{1,0:T(8,128)(2,1)S(1)}, bf16[336,512]{1,0:T(8,128)(2,1)S(1)}, u32[]{:S(2)}, u32[]{:S(2)}) collective-permute-start(bf16[336,512]{1,0:T(8,128)(2,1)S(1)} %collective-permute-done.13), channel_id=1, source_target_pairs={{8,12},{10,14},{9,13},{11,15},{24,28},{26,30},{25,29},{27,31}} | collective-permute-start | bytes 1032200 | tf_op jit(solution)/shard_map/ppermute | solution.py:59
  40.0 9.1 %collective-permute-start.16 = (bf16[336,512]{1,0:T(8,128)(2,1)S(1)}, bf16[336,512]{1,0:T(8,128)(2,1)S(1)}, u32[]{:S(2)}, u32[]{:S(2)}) collective-permute-start(bf16[336,512]{1,0:T(8,128)(2,1)S(1)} %collective-permute-done.14), channel_id=1, source_target_pairs={{4,0},{6,2},{5,1},{7,3},{20,16},{22,18},{21,17},{23,19}} | collective-permute-start | bytes 1032200 | tf_op jit(solution)/shard_map/ppermute | solution.py:60
  42.8 11.0 %collective-permute-start.18 = (bf16[336,512]{1,0:T(8,128)(2,1)S(1)}, bf16[336,512]{1,0:T(8,128)(2,1)S(1)}, u32[]{:S(2)}, u32[]{:S(2)}) collective-permute-start(bf16[336,512]{1,0:T(8,128)(2,1)S(1)} %collective-permute-done.12), channel_id=1, source_target_pairs={{2,0},{0,2},{6,4},{4,6},{10,8},{8,10},{3,1},{1,3},{7,5},{5,7},{11,... | collective-permute-start | bytes 1032200 | tf_op jit(solution)/shard_map/ppermute | solution.py:69
  49.2 6.2 %collective-permute-start.19 = (bf16[336,512]{1,0:T(8,128)(2,1)S(1)}, bf16[336,512]{1,0:T(8,128)(2,1)S(1)}, u32[]{:S(2)}, u32[]{:S(2)}) collective-permute-start(bf16[336,512]{1,0:T(8,128)(2,1)S(1)} %collective-permute-done.13), channel_id=1, source_target_pairs={{10,8},{8,10},{14,12},{12,14},{11,9},{9,11},{15,13},{13,15},{26,24... | collective-permute-start | bytes 1032200 | tf_op jit(solution)/shard_map/ppermute | solution.py:67
  50.6 12.4 %collective-permute-start.20 = (bf16[336,512]{1,0:T(8,128)(2,1)S(1)}, bf16[336,512]{1,0:T(8,128)(2,1)S(1)}, u32[]{:S(2)}, u32[]{:S(2)}) collective-permute-start(bf16[336,512]{1,0:T(8,128)(2,1)S(1)} %collective-permute-done.14), channel_id=1, source_target_pairs={{2,0},{0,2},{6,4},{4,6},{3,1},{1,3},{7,5},{5,7},{18,16},{16,18},{2... | collective-permute-start | bytes 1032200 | tf_op jit(solution)/shard_map/ppermute | solution.py:69
  53.8 10.0 %collective-permute-start.21 = (bf16[336,512]{1,0:T(8,128)(2,1)S(1)}, bf16[336,512]{1,0:T(8,128)(2,1)S(1)}, u32[]{:S(2)}, u32[]{:S(2)}) collective-permute-start(bf16[336,512]{1,0:T(8,128)(2,1)S(1)} %collective-permute-done.15), channel_id=1, source_target_pairs={{14,12},{12,14},{15,13},{13,15},{30,28},{28,30},{31,29},{29,31}} | collective-permute-start | bytes 1032200 | tf_op jit(solution)/shard_map/ppermute | solution.py:67
  55.3 11.4 %collective-permute-start.22 = (bf16[336,512]{1,0:T(8,128)(2,1)S(1)}, bf16[336,512]{1,0:T(8,128)(2,1)S(1)}, u32[]{:S(2)}, u32[]{:S(2)}) collective-permute-start(bf16[336,512]{1,0:T(8,128)(2,1)S(1)} %collective-permute-done.16), channel_id=1, source_target_pairs={{2,0},{0,2},{3,1},{1,3},{18,16},{16,18},{19,17},{17,19}} | collective-permute-start | bytes 1032200 | tf_op jit(solution)/shard_map/ppermute | solution.py:69
  63.0 14.9 %collective-permute-start = (f32[16]{0:T(128)S(1)}, f32[16]{0:T(128)S(1)}, u32[]{:S(2)}, u32[]{:S(2)}) collective-permute-start(f32[16]{0:T(128)S(1)} %pad_maximum_fusion), channel_id=1, source_target_pairs={{0,8},{2,10},{4,12},{6,14},{8,0},{10,2},{12,4},{14,6},{1,9},{3,11}... | collective-permute-start | bytes 200 | tf_op jit(solution)/shard_map/ppermute | solution.py:19
  74.4 18.0 %collective-permute-start.23 = (bf16[2688,512]{1,0:T(8,128)(2,1)S(1)}, bf16[2688,512]{1,0:T(8,128)(2,1)}, u32[]{:S(2)}, u32[]{:S(2)}) collective-permute-start(bf16[2688,512]{1,0:T(8,128)(2,1)S(1)} %get-tuple-element.30), channel_id=1, source_target_pairs={{0,1},{1,0},{2,3},{3,2},{4,5},{5,4},{6,7},{7,6},{8,9},{9,8},{10,11... | collective-permute-start | bytes 8257544 | tf_op jit(solution)/shard_map/ppermute | solution.py:19
  78.0 3.5 %collective-permute-start.1 = (f32[16]{0:T(128)S(1)}, f32[16]{0:T(128)S(1)}, u32[]{:S(2)}, u32[]{:S(2)}) collective-permute-start(f32[16]{0:T(128)S(1)} %fusion.65), channel_id=1, source_target_pairs={{0,4},{2,6},{4,0},{6,2},{8,12},{10,14},{12,8},{14,10},{1,5},{3,7},... | collective-permute-start | bytes 200 | tf_op jit(solution)/shard_map/ppermute | solution.py:19
  81.5 3.5 %collective-permute-start.2 = (f32[16]{0:T(128)S(1)}, f32[16]{0:T(128)S(1)}, u32[]{:S(2)}, u32[]{:S(2)}) collective-permute-start(f32[16]{0:T(128)S(1)} %add.231), channel_id=1, source_target_pairs={{0,2},{2,0},{4,6},{6,4},{8,10},{10,8},{12,14},{14,12},{1,3},{3,1},... | collective-permute-start | bytes 200 | tf_op jit(solution)/shard_map/ppermute | solution.py:19
  86.4 3.9 %collective-permute-start.5 = (bf16[128,1024]{1,0:T(8,128)(2,1)S(1)}, bf16[128,1024]{1,0:T(8,128)(2,1)S(1)}, u32[]{:S(2)}, u32[]{:S(2)}) collective-permute-start(bf16[128,1024]{1,0:T(8,128)(2,1)S(1)} %collective-permute-done.4), channel_id=1, source_target_pairs={{8,12},{10,14},{9,13},{11,15},{24,28},{26,30},{25,29},{27,31}} | collective-permute-start | bytes 786440 | tf_op jit(solution)/shard_map/ppermute | solution.py:40
  88.9 3.3 %collective-permute-start.7 = (bf16[128,1024]{1,0:T(8,128)(2,1)}, bf16[128,1024]{1,0:T(8,128)(2,1)S(1)}, u32[]{:S(2)}, u32[]{:S(2)}) collective-permute-start(bf16[128,1024]{1,0:T(8,128)(2,1)} %collective-permute-done.3), channel_id=1, source_target_pairs={{6,4},{4,6},{10,8},{8,10},{14,12},{12,14},{7,5},{5,7},{11,9},{9,11... | collective-permute-start | bytes 786440 | tf_op jit(solution)/shard_map/ppermute | solution.py:45
  89.6 2.6 %collective-permute-start.8 = (bf16[128,1024]{1,0:T(8,128)(2,1)S(1)}, bf16[128,1024]{1,0:T(8,128)(2,1)S(1)}, u32[]{:S(2)}, u32[]{:S(2)}) collective-permute-start(bf16[128,1024]{1,0:T(8,128)(2,1)S(1)} %collective-permute-done.4), channel_id=1, source_target_pairs={{10,8},{8,10},{14,12},{12,14},{11,9},{9,11},{15,13},{13,15},{26,24... | collective-permute-start | bytes 786440 | tf_op jit(solution)/shard_map/ppermute | solution.py:45
  90.4 2.0 collective-permute-start.9
  117.4 19.2 %collective-permute-start.28 = (bf16[128,1024]{0,1:T(8,128)(2,1)S(1)}, bf16[128,1024]{0,1:T(8,128)(2,1)S(1)}, u32[]{:S(2)}, u32[]{:S(2)}) collective-permute-start(bf16[128,1024]{0,1:T(8,128)(2,1)S(1)} %bitcast.150), channel_id=1, source_target_pairs={{12,14},{14,12},{13,15},{15,13},{28,30},{30,28},{29,31},{31,29}} | collective-permute-start | bytes 786440 | tf_op jit(solution)/shard_map/ppermute | solution.py:102
  118.2 22.2 %collective-permute-start.32 = (bf16[128,1024]{0,1:T(8,128)(2,1)S(1)}, bf16[128,1024]{0,1:T(8,128)(2,1)S(1)}, u32[]{:S(2)}, u32[]{:S(2)}) collective-permute-start(bf16[128,1024]{0,1:T(8,128)(2,1)S(1)} %copy-done.6), channel_id=1, source_target_pairs={{0,4},{2,6},{4,8},{6,10},{8,12},{10,14},{1,5},{3,7},{5,9},{7,11},{... | collective-permute-start | bytes 786440 | tf_op jit(solution)/shard_map/ppermute | solution.py:40
  135.9 5.2 %collective-permute-start.27 = (bf16[128,1024]{0,1:T(8,128)(2,1)S(1)}, bf16[128,1024]{0,1:T(8,128)(2,1)S(1)}, u32[]{:S(2)}, u32[]{:S(2)}) collective-permute-start(bf16[128,1024]{0,1:T(8,128)(2,1)S(1)} %bitcast.149), channel_id=1, source_target_pairs={{8,10},{10,8},{12,14},{14,12},{9,11},{11,9},{13,15},{15,13},{24,26... | collective-permute-start | bytes 786440 | tf_op jit(solution)/shard_map/ppermute | solution.py:102
  136.7 4.4 %collective-permute-start.29 = (bf16[128,1024]{0,1:T(8,128)(2,1)S(1)}, bf16[128,1024]{0,1:T(8,128)(2,1)S(1)}, u32[]{:S(2)}, u32[]{:S(2)}) collective-permute-start(bf16[128,1024]{0,1:T(8,128)(2,1)S(1)} %fusion.22), channel_id=1, source_target_pairs={{12,8},{14,10},{13,9},{15,11},{28,24},{30,26},{29,25},{31,27}} | collective-permute-start | bytes 786440 | tf_op jit(solution)/shard_map/ppermute | solution.py:110
  137.4 9.8 %collective-permute-start.26 = (bf16[128,1024]{0,1:T(8,128)(2,1)S(1)}, bf16[128,1024]{0,1:T(8,128)(2,1)S(1)}, u32[]{:S(2)}, u32[]{:S(2)}) collective-permute-start(bf16[128,1024]{0,1:T(8,128)(2,1)S(1)} %bitcast.148), channel_id=1, source_target_pairs={{4,6},{6,4},{8,10},{10,8},{12,14},{14,12},{5,7},{7,5},{9,11},{11,9... | collective-permute-start | bytes 786440 | tf_op jit(solution)/shard_map/ppermute | solution.py:102
  140.5 5.9 %collective-permute-start.33 = (bf16[128,1024]{0,1:T(8,128)(2,1)S(1)}, bf16[128,1024]{0,1:T(8,128)(2,1)S(1)}, u32[]{:S(2)}, u32[]{:S(2)}) collective-permute-start(bf16[128,1024]{0,1:T(8,128)(2,1)S(1)} %collective-permute-done.32), channel_id=1, source_target_pairs={{4,8},{6,10},{8,12},{10,14},{5,9},{7,11},{9,13},{11,15},{20,24},{2... | collective-permute-start | bytes 786440 | tf_op jit(solution)/shard_map/ppermute | solution.py:40
  141.3 6.6 %collective-permute-start.30 = (bf16[128,1024]{0,1:T(8,128)(2,1)S(1)}, bf16[128,1024]{0,1:T(8,128)(2,1)S(1)}, u32[]{:S(2)}, u32[]{:S(2)}) collective-permute-start(bf16[128,1024]{0,1:T(8,128)(2,1)S(1)} %fusion.24), channel_id=1, source_target_pairs={{8,4},{10,6},{12,8},{14,10},{9,5},{11,7},{13,9},{15,11},{24,20},{2... | collective-permute-start | bytes 786440 | tf_op jit(solution)/shard_map/ppermute | solution.py:110
  142.0 8.1 %collective-permute-start.35 = (bf16[128,1024]{0,1:T(8,128)(2,1)S(1)}, bf16[128,1024]{0,1:T(8,128)(2,1)S(1)}, u32[]{:S(2)}, u32[]{:S(2)}) collective-permute-start(bf16[128,1024]{0,1:T(8,128)(2,1)S(1)} %copy-done.6), channel_id=1, source_target_pairs={{0,2},{4,6},{8,10},{12,14},{1,3},{5,7},{9,11},{13,15},{16,18},{20,... | collective-permute-start | bytes 786440 | tf_op jit(solution)/shard_map/ppermute | solution.py:42
  144.9 14.8 %collective-permute-start.25 = (bf16[128,1024]{0,1:T(8,128)(2,1)S(1)}, bf16[128,1024]{0,1:T(8,128)(2,1)S(1)}, u32[]{:S(2)}, u32[]{:S(2)}) collective-permute-start(bf16[128,1024]{0,1:T(8,128)(2,1)S(1)} %bitcast.147), channel_id=1, source_target_pairs={{2,0},{6,4},{10,8},{14,12},{3,1},{7,5},{11,9},{15,13},{18,16},{22,... | collective-permute-start | bytes 786440 | tf_op jit(solution)/shard_map/ppermute | solution.py:113
  146.4 2.3 collective-permute-start.34
  147.2 3.9 %collective-permute-start.36 = (bf16[128,1024]{0,1:T(8,128)(2,1)S(1)}, bf16[128,1024]{0,1:T(8,128)(2,1)S(1)}, u32[]{:S(2)}, u32[]{:S(2)}) collective-permute-start(bf16[128,1024]{0,1:T(8,128)(2,1)S(1)} %collective-permute-done.32), channel_id=1, source_target_pairs={{6,4},{4,6},{10,8},{8,10},{14,12},{12,14},{7,5},{5,7},{11,9},{9,11... | collective-permute-start | bytes 786440 | tf_op jit(solution)/shard_map/ppermute | solution.py:45
  147.9 3.3 %collective-permute-start.37 = (bf16[128,1024]{0,1:T(8,128)(2,1)S(1)}, bf16[128,1024]{0,1:T(8,128)(2,1)S(1)}, u32[]{:S(2)}, u32[]{:S(2)}) collective-permute-start(bf16[128,1024]{0,1:T(8,128)(2,1)S(1)} %collective-permute-done.33), channel_id=1, source_target_pairs={{10,8},{8,10},{14,12},{12,14},{11,9},{9,11},{15,13},{13,15},{26,24... | collective-permute-start | bytes 786440 | tf_op jit(solution)/shard_map/ppermute | solution.py:45
  148.7 31.6 %collective-permute-start.31 = (bf16[128,1024]{0,1:T(8,128)(2,1)S(1)}, bf16[128,1024]{0,1:T(8,128)(2,1)S(1)}, u32[]{:S(2)}, u32[]{:S(2)}) collective-permute-start(bf16[128,1024]{0,1:T(8,128)(2,1)S(1)} %fusion.26), channel_id=1, source_target_pairs={{4,0},{6,2},{8,4},{10,6},{12,8},{14,10},{5,1},{7,3},{9,5},{11,7},{... | collective-permute-start | bytes 786440 | tf_op jit(solution)/shard_map/ppermute | solution.py:110
  150.1 1.2 collective-permute-start.38
  183.9 24.3 %collective-permute-start.42 = (bf16[128,1024]{1,0:T(8,128)(2,1)}, bf16[128,1024]{1,0:T(8,128)(2,1)}, u32[]{:S(2)}, u32[]{:S(2)}) collective-permute-start(bf16[128,1024]{1,0:T(8,128)(2,1)} %copy.73), channel_id=1, source_target_pairs={{12,14},{14,12},{13,15},{15,13},{28,30},{30,28},{29,31},{31,29}} | collective-permute-start | bytes 786440 | tf_op jit(solution)/shard_map/ppermute | solution.py:102
  186.1 45.2 %collective-permute-start.41 = (bf16[128,1024]{1,0:T(8,128)(2,1)}, bf16[128,1024]{1,0:T(8,128)(2,1)}, u32[]{:S(2)}, u32[]{:S(2)}) collective-permute-start(bf16[128,1024]{1,0:T(8,128)(2,1)} %copy.71), channel_id=1, source_target_pairs={{8,10},{10,8},{12,14},{14,12},{9,11},{11,9},{13,15},{15,13},{24,26... | collective-permute-start | bytes 786440 | tf_op jit(solution)/shard_map/ppermute | solution.py:102
  189.2 31.2 %collective-permute-start.46 = (f32[464,128]{1,0:T(8,128)}, f32[464,128]{1,0:T(8,128)}, u32[]{:S(2)}, u32[]{:S(2)}) collective-permute-start(f32[464,128]{1,0:T(8,128)} %maximum_bitcast_fusion), channel_id=1, source_target_pairs={{0,8},{2,10},{4,12},{6,14},{8,0},{10,2},{12,4},{14,6},{1,9},{3,11}... | collective-permute-start | bytes 712712 | tf_op jit(solution)/shard_map/ppermute | solution.py:19
  210.1 21.2 %collective-permute-start.43 = (bf16[128,1024]{1,0:T(8,128)(2,1)}, bf16[128,1024]{1,0:T(8,128)(2,1)}, u32[]{:S(2)}, u32[]{:S(2)}) collective-permute-start(bf16[128,1024]{1,0:T(8,128)(2,1)} %add_convert_fusion.3), channel_id=1, source_target_pairs={{12,8},{14,10},{13,9},{15,11},{28,24},{30,26},{29,25},{31,27}} | collective-permute-start | bytes 786440 | tf_op jit(solution)/shard_map/ppermute | solution.py:110
  216.9 26.4 %collective-permute-start.40 = (bf16[128,1024]{1,0:T(8,128)(2,1)}, bf16[128,1024]{1,0:T(8,128)(2,1)}, u32[]{:S(2)}, u32[]{:S(2)}) collective-permute-start(bf16[128,1024]{1,0:T(8,128)(2,1)} %copy.69), channel_id=1, source_target_pairs={{4,6},{6,4},{8,10},{10,8},{12,14},{14,12},{5,7},{7,5},{9,11},{11,9... | collective-permute-start | bytes 786440 | tf_op jit(solution)/shard_map/ppermute | solution.py:102
  219.2 34.8 %collective-permute-start.39 = (bf16[128,1024]{1,0:T(8,128)(2,1)}, bf16[128,1024]{1,0:T(8,128)(2,1)S(1)}, u32[]{:S(2)}, u32[]{:S(2)}) collective-permute-start(bf16[128,1024]{1,0:T(8,128)(2,1)} %copy.68), channel_id=1, source_target_pairs={{2,0},{6,4},{10,8},{14,12},{3,1},{7,5},{11,9},{15,13},{18,16},{22,... | collective-permute-start | bytes 786440 | tf_op jit(solution)/shard_map/ppermute | solution.py:113
  221.4 14.0 %collective-permute-start.47 = (f32[464,128]{1,0:T(8,128)S(1)}, f32[464,128]{1,0:T(8,128)S(1)}, u32[]{:S(2)}, u32[]{:S(2)}) collective-permute-start(f32[464,128]{1,0:T(8,128)S(1)} %fusion.34), channel_id=1, source_target_pairs={{0,4},{2,6},{4,0},{6,2},{8,12},{10,14},{12,8},{14,10},{1,5},{3,7},... | collective-permute-start | bytes 712712 | tf_op jit(solution)/shard_map/ppermute | solution.py:19
  232.5 10.9 %collective-permute-start.44 = (bf16[128,1024]{1,0:T(8,128)(2,1)S(1)}, bf16[128,1024]{1,0:T(8,128)(2,1)S(1)}, u32[]{:S(2)}, u32[]{:S(2)}) collective-permute-start(bf16[128,1024]{1,0:T(8,128)(2,1)S(1)} %add_convert_fusion.2), channel_id=1, source_target_pairs={{8,4},{10,6},{12,8},{14,10},{9,5},{11,7},{13,9},{15,11},{24,20},{2... | collective-permute-start | bytes 786440 | tf_op jit(solution)/shard_map/ppermute | solution.py:110
  236.4 6.8 %collective-permute-start.48 = (f32[464,128]{1,0:T(8,128)S(1)}, f32[464,128]{1,0:T(8,128)S(1)}, u32[]{:S(2)}, u32[]{:S(2)}) collective-permute-start(f32[464,128]{1,0:T(8,128)S(1)} %fusion.64), channel_id=1, source_target_pairs={{0,2},{2,0},{4,6},{6,4},{8,10},{10,8},{12,14},{14,12},{1,3},{3,1},... | collective-permute-start | bytes 712712 | tf_op jit(solution)/shard_map/ppermute | solution.py:19
  243.3 8.5 %collective-permute-start.49 = (f32[464,128]{1,0:T(8,128)S(1)}, f32[464,128]{1,0:T(8,128)S(1)}, u32[]{:S(2)}, u32[]{:S(2)}) collective-permute-start(f32[464,128]{1,0:T(8,128)S(1)} %add.274), channel_id=1, source_target_pairs={{0,1},{1,0},{2,3},{3,2},{4,5},{5,4},{6,7},{7,6},{8,9},{9,8},{10,11... | collective-permute-start | bytes 712712 | tf_op jit(solution)/shard_map/ppermute | solution.py:19
  245.1 11.2 %collective-permute-start.45 = (bf16[128,1024]{1,0:T(8,128)(2,1)}, bf16[128,1024]{1,0:T(8,128)(2,1)}, u32[]{:S(2)}, u32[]{:S(2)}) collective-permute-start(bf16[128,1024]{1,0:T(8,128)(2,1)} %add_convert_fusion.1), channel_id=1, source_target_pairs={{4,0},{6,2},{8,4},{10,6},{12,8},{14,10},{5,1},{7,3},{9,5},{11,7},{... | collective-permute-start | bytes 786440 | tf_op jit(solution)/shard_map/ppermute | solution.py:110
  (23 other events, 287.0 us)
